TPU v7x, 32 devices: a whole 2x2x4 slice. The times are simulated.
32 devices in a mesh: gx: 4 (over y, x), gy: 2 (over core), gz: 4 (over z).
Axes of the slice: x: 2, y: 2, z: 4, core: 2. Of those that a mesh axis runs over, the one named last changes fastest.
Arguments:
- features: bfloat16 [8, 32, 65536], P('gz', 'gy', 'gx'), may hold values from -6 to 6
- depth_weight: bfloat16 [27, 64], replicated, may hold values from -1.25 to 1.25
- expand_weight: bfloat16 [64, 256], replicated, may hold values from -0.75 to 0.75
- project_weight: bfloat16 [256, 64], replicated, may hold values from -0.375 to 0.375
- spec_real: bfloat16 [32, 64, 64], replicated, may hold values from -2 to 2
- spec_imag: bfloat16 [32, 64, 64], replicated, may hold values from -2 to 2
- cotangent: bfloat16 [8, 32, 65536], P('gz', 'gy', 'gx'), may hold values from -6 to 6
Outputs:
- output: bfloat16 [8, 32, 65536], P('gz', 'gy', 'gx')
- grad_features: bfloat16 [8, 32, 65536], P('gz', 'gy', 'gx')
- grad_spec: float32 [2, 32, 64, 64], P(None, 'gx')
All inputs are finite; a program needn't handle non-finite values.
Results may differ from a plain program's by a relative error of at most 0.018.
Values may be sent and summed in bfloat16 or wider, within the bound.
No kernel may reach another device: no remote copies, remote signals or barrier semaphores. Data moves between devices by JAX's collectives and lax.ppermute only.
A program may use at most 64 MiB of HBM per device.

v0:
```python
import math

import jax
import jax.numpy as jnp
from jax import lax
from jax.sharding import PartitionSpec as P


def padded_2(value, sides, width, wrap):
    for axis, dim in sides:
        size, length = (lax.axis_size(axis), value.shape[dim])
        up = [(i, (i + 1) % size) for i in range(size if wrap else size - 1)]
        down = [(j, i) for i, j in up]
        last = lax.slice_in_dim(value, length - width, length, axis=dim)
        leading = lax.slice_in_dim(value, 0, width, axis=dim)
        before = lax.ppermute(last, axis, up)
        after = lax.ppermute(leading, axis, down)
        value = jnp.concatenate([before, value, after], axis=dim)
    return value


def gelu_parts(values):
    normal_cdf = 0.5 * (1.0 + jax.scipy.special.erf(values * (1.0 / math.sqrt(2.0))))
    density = jnp.exp(-0.5 * values * values) * (1.0 / math.sqrt(2.0 * math.pi))
    return (values * normal_cdf, normal_cdf + values * density)


def dft_tables(offset, cells, x_length, mode_count):
    position = offset + jnp.arange(cells, dtype=jnp.int32)
    frequency = jnp.arange(mode_count, dtype=jnp.int32)
    phase_int = position[:, None] * frequency[None, :] % x_length
    angles = phase_int.astype(jnp.float32) * (2.0 * math.pi / x_length)
    return (jnp.cos(angles).astype(jnp.bfloat16), (-jnp.sin(angles)).astype(jnp.bfloat16))


def scaled_table(table, mode_count, x_length):
    frequency = jnp.arange(mode_count, dtype=jnp.int32)
    mode_scale = jnp.where(frequency == 0, 1.0, 2.0).astype(jnp.float32) / x_length
    return (table.astype(jnp.float32) * mode_scale[None, :]).astype(jnp.bfloat16)


def block_weights(spec_real, spec_imag):
    upper_row = jnp.concatenate([spec_real, spec_imag], axis=2)
    lower_row = jnp.concatenate([-spec_imag, spec_real], axis=2)
    return jnp.concatenate([upper_row, lower_row], axis=1)


def spatial_rims(field_block, channels):
    x_wide = padded_2(field_block, (("gx", 2),), channels, True)
    return padded_2(x_wide, (("gy", 1), ("gz", 0)), 1, False)


def depthwise(padded, taps, flipped, x_cells, channels):
    planes = padded.shape[0] - 2
    y_cells = padded.shape[1] - 2
    running = jnp.zeros((planes, y_cells, x_cells * channels), jnp.float32)
    direction = -1 if flipped else 1
    for step_z in (-1, 0, 1):
        for step_y in (-1, 0, 1):
            for step_x in (-1, 0, 1):
                tap_gain = taps[(step_z + 1) * 9 + (step_y + 1) * 3 + (step_x + 1)].astype(
                    jnp.float32
                )
                z_offset = 1 + direction * step_z
                y_offset = 1 + direction * step_y
                x_offset = 1 + direction * step_x
                cut = padded[
                    z_offset : z_offset + planes,
                    y_offset : y_offset + y_cells,
                    x_offset * channels : (x_offset + x_cells) * channels,
                ]
                running = running + cut.astype(jnp.float32) * jnp.tile(tap_gain, x_cells)
    return running


def share_terms(field3, cos_table, sin_table):
    real_part = jnp.einsum("rxc,xk->krc", field3, cos_table, preferred_element_type=jnp.float32)
    imag_part = jnp.einsum("rxc,xk->krc", field3, sin_table, preferred_element_type=jnp.float32)
    return lax.psum_scatter(
        jnp.concatenate([real_part, imag_part], axis=2), "gx", scatter_dimension=0, tiled=True
    )


def share_inverse(modes_share, cos_table, sin_table, channels):
    segment = lax.all_gather(modes_share, "gx", axis=0, tiled=True)
    running = jnp.einsum(
        "krc,xk->rxc", segment[:, :, :channels], cos_table, preferred_element_type=jnp.float32
    )
    return running + jnp.einsum(
        "krc,xk->rxc", segment[:, :, channels:], sin_table, preferred_element_type=jnp.float32
    )


def split_gradients(dblock, channels):
    grad_real = dblock[:, :channels, :channels] + dblock[:, channels:, channels:]
    grad_imag = dblock[:, :channels, channels:] - dblock[:, channels:, :channels]
    return jnp.stack([grad_real, grad_imag])


def sum_gradients(local_grads):
    return lax.psum(local_grads.astype(jnp.bfloat16), ("gy", "gz")).astype(jnp.float32)


def per_device(
    features, depth_weight, expand_weight, project_weight, spec_real, spec_imag, cotangent
):
    planes, y_cells, merged = features.shape
    channels = depth_weight.shape[1]
    x_cells = merged // channels
    row_count = planes * y_cells
    mode_count = spec_real.shape[0]
    group_size = lax.axis_size("gx")
    x_length = x_cells * group_size
    x_start = lax.axis_index("gx") * x_cells
    cos_part, sin_part = dft_tables(x_start, x_cells, x_length, mode_count)
    cos_scaled = scaled_table(cos_part, mode_count, x_length)
    sin_scaled = scaled_table(sin_part, mode_count, x_length)
    blocks = block_weights(spec_real, spec_imag)
    padded = spatial_rims(features, channels)
    activation = depthwise(padded, depth_weight, False, x_cells, channels).astype(jnp.bfloat16)
    activation = activation.reshape(row_count * x_cells, channels)
    hidden_pre = jnp.dot(activation, expand_weight, preferred_element_type=jnp.float32)
    hidden, hidden_slope = gelu_parts(hidden_pre)
    local_branch = jnp.dot(
        hidden.astype(jnp.bfloat16), project_weight, preferred_element_type=jnp.float32
    )
    local_branch = local_branch.reshape(row_count, x_cells, channels)
    field3 = features.reshape(row_count, x_cells, channels)
    share_size = mode_count // group_size
    owned_blocks = lax.dynamic_slice_in_dim(
        blocks, lax.axis_index("gx") * share_size, share_size, 0
    )
    coeffs = share_terms(field3, cos_part, sin_part).astype(jnp.bfloat16)
    mixed_modes = jnp.einsum(
        "krc,kco->kro", coeffs, owned_blocks, preferred_element_type=jnp.float32
    ).astype(jnp.bfloat16)
    spectral = share_inverse(mixed_modes, cos_scaled, sin_scaled, channels)
    result, slopes = gelu_parts(local_branch + spectral)
    output = result.astype(jnp.bfloat16).reshape(planes, y_cells, merged)
    grad_pre = (
        cotangent.reshape(row_count, x_cells, channels).astype(jnp.float32) * slopes
    ).astype(jnp.bfloat16)
    hidden_grad = jnp.dot(
        grad_pre.reshape(row_count * x_cells, channels),
        project_weight.T,
        preferred_element_type=jnp.float32,
    )
    grad_hidden = (hidden_grad * hidden_slope).astype(jnp.bfloat16)
    grad_act = jnp.dot(grad_hidden, expand_weight.T, preferred_element_type=jnp.float32).astype(
        jnp.bfloat16
    )
    grad_act = grad_act.reshape(planes, y_cells, merged)
    dcoef = share_terms(grad_pre, cos_scaled, sin_scaled).astype(jnp.bfloat16)
    dmode = jnp.einsum(
        "kro,kco->krc", dcoef, owned_blocks, preferred_element_type=jnp.float32
    ).astype(jnp.bfloat16)
    spectral_grad = share_inverse(dmode, cos_part, sin_part, channels)
    dblock = jnp.einsum("krc,kro->kco", coeffs, dcoef, preferred_element_type=jnp.float32)
    grad_spec = sum_gradients(split_gradients(dblock, channels))
    padded_grad = spatial_rims(grad_act, channels)
    grad_local = depthwise(padded_grad, depth_weight, True, x_cells, channels)
    grad_features = (grad_local + spectral_grad.reshape(planes, y_cells, merged)).astype(
        jnp.bfloat16
    )
    return (output, grad_features, grad_spec)


def solution(mesh):
    placed = (P("gz", "gy", "gx"), P(), P(), P(), P(), P(), P("gz", "gy", "gx"))
    return jax.shard_map(
        per_device,
        mesh=mesh,
        in_specs=placed,
        out_specs=(P("gz", "gy", "gx"), P("gz", "gy", "gx"), P(None, "gx", None, None)),
        check_vma=False,
    )
```

profile of v0, /device:TPU:0, one launch (start us, length us, event | category | flops | bytes accessed | tf_op | source)
XLA Modules:
  0.0 243.0 jit_solution(9802269547435364776)
XLA Ops:
  8.0 3.9 %collective-permute-start.1 = (bf16[2,16,64]{2,1,0:T(8,128)(2,1)S(1)}, bf16[2,16,64]{2,1,0:T(8,128)(2,1)S(1)}, u32[]{:S(2)}, u32[]{:S(2)}) collective-permute-start(bf16[2,16,64]{2,1,0:T(8,128)(2,1)S(1)} %get-tuple-element.19), channel_id=1, source_target_pairs={{8,0},{16,8},{24,16},{0,24},{9,1},{17,9},{25,17},{1,25},{10,2},{18... | collective-permute-start | bytes 12296 | tf_op jit(solution)/shard_map/ppermute | solution.py:17
  11.9 3.0 %reshape.69 = bf16[32,256,64]{2,1,0:T(8,128)(2,1)S(1)} reshape(bf16[2,16,16384]{2,1,0:T(8,128)(2,1)} %param.7) | data formatting | bytes 2097152 | tf_op jit(solution)/shard_map/reshape | solution.py:128
  15.0 1.4 fusion.47
  16.3 1.3 fusion.50
  17.7 2.8 %concatenate.105 = bf16[2,16,16512]{2,1,0:T(8,128)(2,1)S(1)} concatenate(bf16[2,16,64]{2,1,0:T(8,128)(2,1)S(1)} %collective-permute-done, bf16[2,16,16384]{2,1,0:T(8,128)(2,1)} %param.7, bf16[2,16,64]{2,1,0:T(8,128)(2,1)S(1)} %collective-permute-done.1), dimensions={2} | concatenate | bytes 2113536 | tf_op jit(solution)/shard_map/concatenate | solution.py:18
  20.7 1.5 collective-permute-start.2
  22.2 1.3 collective-permute-start.3
  26.1 1.2 fusion.94
  27.3 4.4 %collective-permute-start.4 = (bf16[1,18,16512]{2,1,0:T(8,128)(2,1)}, bf16[1,18,16512]{2,1,0:T(8,128)(2,1)}, u32[]{:S(2)}, u32[]{:S(2)}) collective-permute-start(bf16[1,18,16512]{2,1,0:T(8,128)(2,1)} %get-tuple-element.7), channel_id=1, source_target_pairs={{0,1},{1,2},{2,3},{4,5},{5,6},{6,7},{8,9},{9,10},{10,11},{12,13},{... | collective-permute-start | bytes 1783304 | tf_op jit(solution)/shard_map/ppermute | solution.py:16
  31.7 1.5 collective-permute-start.5
  52.3 3.3 %reshape.101 = f32[32,256,64]{2,1,0:T(8,128)} reshape(bf16[2,16,16384]{2,1,0:T(8,128)(2,1)S(1)} %copy-done.13) | data formatting | bytes 3145728 | tf_op jit(solution)/shard_map/convert_element_type | solution.py:141
  55.6 3.9 %copy.44 = f32[32,256,64]{1,2,0:T(8,128)} copy(f32[32,256,64]{2,1,0:T(8,128)} %reshape.101) | data formatting | bytes 4194304 | tf_op jit(solution)/shard_map/convert_element_type | solution.py:141
  59.9 3.0 %maximum_maximum_fusion = (bf16[3,18,16512]{2,1,0:T(8,128)(2,1)S(1)}, bf16[3,18,16512]{2,1,0:T(8,128)(2,1)S(1)}) fusion(bf16[2,1,16512]{2,1,0:T(2,128)(2,1)S(1)} %collective-permute-done.3, bf16[2,16,16512]{2,1,0:T(8,128)(2,1)S(1)} %concatenate.105, bf16[2,1,16512]{2,1,0:T(2,128)(2,1)S(1)} %collective-permute-done.2, ...), kind=kLoop, calls=%fused_computation.12 | loop fusion | flops 14266368 | bytes 5944320 | tf_op jit(solution)/shard_map/concatenate | solution.py:18
  63.2 14.8 %add_convert_fusion.1 = bf16[2,16,16384]{2,1,0:T(8,128)(2,1)} fusion(bf16[2,16,16384]{2,1,0:T(8,128)(2,1)S(1)} %copy-done.3, bf16[2,16,16512]{2,1,0:T(8,128)(2,1)S(1)} %concatenate.105, bf16[2,1,16512]{2,1,0:T(2,128)(2,1)S(1)} %collective-permute-done.3, bf16[2,1,16512]{2,1,0:T(2,128)(2,1)S(1)} %collective-permute-done.2, ...), kind=kLoop, calls=%fused_computation.35 | loop fusion | flops 55050240 | bytes 23938048 | tf_op jit(solution)/shard_map/convert_element_type | solution.py:120
  78.0 3.0 %reshape.67 = bf16[8192,64]{1,0:T(8,128)(2,1)S(1)} reshape(bf16[2,16,16384]{2,1,0:T(8,128)(2,1)} %add_convert_fusion.1) | data formatting | bytes 2097152 | tf_op jit(solution)/shard_map/reshape | solution.py:121
  81.0 1.2 fusion.101
  82.3 3.3 %copy-done.2 = f32[8192,256]{1,0:T(8,128)} copy-done((f32[8192,256]{1,0:T(8,128)}, f32[8192,256]{1,0:T(8,128)S(1)}, u32[]{:S(2)}) %copy-start.2) | copy-done | bytes 8388632
  85.6 3.4 %fusion.5 = f32[8192,64]{0,1:T(8,128)} fusion(bf16[256,64]{0,1:T(8,128)(2,1)S(1)} %copy-done.44, f32[8192,256]{1,0:T(8,128)S(1)} %fusion.101), kind=kOutput, calls=%fused_computation.10 | convolution fusion | flops 278921216 | bytes 10518528 | tf_op jit(solution)/shard_map/dot_general | solution.py:124
  90.9 9.6 %all_gather.6 = bf16[32,32,128]{2,1,0:T(8,128)(2,1)S(1)} all-gather(bf16[8,32,128]{2,1,0:T(8,128)(2,1)S(1)} %convolution_convert_fusion.2), channel_id=1, replica_groups=mesh['gx'=4,'gy'=2,'gz'=4] {'gx'}, dimensions={0}, use_global_device_ids=true | all-gather | bytes 327680 | tf_op jit(solution)/shard_map/all_gather | solution.py:85
  101.2 2.5 %fusion.11 = (bf16[32,256,64]{1,2,0:T(8,128)(2,1)S(1)}, bf16[32,256,64]{1,2,0:T(8,128)(2,1)}) fusion(f32[32,256,64]{1,2,0:T(8,128)S(1)} %copy-done.5, f32[256,32,64]{0,2,1:T(8,128)S(1)} %fusion.29, bf16[32,32,64]{2,1,0:T(8,128)(2,1)S(1)} %get-tuple-element.25, f32[32]{0:T(128)S(1)} %fusion.66, s32[256]{0:T(256)S(1)} %iota_add_fusion, ...), kind=kOutput, calls=%fused_computation.29 | convolution fusion | flops 41050112 | bytes 8520832 | tf_op jit(solution)/shard_map/krc,xk->rxc/dot_general | solution.py:89
  104.5 7.8 %convolution_convert_fusion = bf16[8192,64]{0,1:T(8,128)(2,1)S(1)} fusion(bf16[64,256]{1,0:T(8,128)(2,1)S(1)} %copy-done, bf16[8192,64]{0,1:T(8,128)(2,1)S(1)} %bitcast.128, bf16[256,64]{0,1:T(8,128)(2,1)S(1)} %copy-done.45, f32[8192,256]{1,0:T(8,128)} %copy-done.2), kind=kOutput, calls=%fused_computation.3 | convolution fusion | flops 558366720 | bytes 10551296 | tf_op jit(solution)/shard_map/dot_general | solution.py:149
  112.4 1.8 copy.46
  114.2 2.8 %reshape.72 = bf16[2,16,16384]{2,1,0:T(8,128)(2,1)S(1)} reshape(bf16[8192,64]{1,0:T(8,128)(2,1)} %copy.46) | data formatting | bytes 2097152 | tf_op jit(solution)/shard_map/reshape | solution.py:152
  117.1 1.5 collective-permute-start.7
  119.1 1.6 collective-permute-done.7
  120.8 2.4 collective-permute-done.6
  123.1 1.1 concatenate.117
  124.5 1.3 collective-permute-start.9
  125.8 3.0 %collective-permute-start.8 = (bf16[2,1,16512]{2,1,0:T(2,128)(2,1)S(1)}, bf16[2,1,16512]{2,1,0:T(2,128)(2,1)S(1)}, u32[]{:S(2)}, u32[]{:S(2)}) collective-permute-start(bf16[2,1,16512]{2,1,0:T(2,128)(2,1)S(1)} %get-tuple-element.14), channel_id=1, source_target_pairs={{0,4},{1,5},{2,6},{3,7},{8,12},{9,13},{10,14},{11,15},{16,20},{17,... | collective-permute-start | bytes 198152 | tf_op jit(solution)/shard_map/ppermute | solution.py:16
  130.4 1.3 fusion.93
  131.7 1.3 collective-permute-start.10
  133.0 6.1 %collective-permute-start.11 = (bf16[1,18,16512]{2,1,0:T(8,128)(2,1)}, bf16[1,18,16512]{2,1,0:T(8,128)(2,1)}, u32[]{:S(2)}, u32[]{:S(2)}) collective-permute-start(bf16[1,18,16512]{2,1,0:T(8,128)(2,1)} %get-tuple-element.6), channel_id=1, source_target_pairs={{0,1},{1,2},{2,3},{4,5},{5,6},{6,7},{8,9},{9,10},{10,11},{12,13},{... | collective-permute-start | bytes 1783304 | tf_op jit(solution)/shard_map/ppermute | solution.py:16
  141.5 2.0 copy.43
  143.6 2.5 %reshape.70 = bf16[2,16,16384]{2,1,0:T(8,128)(2,1)} reshape(bf16[32,256,64]{2,1,0:T(8,128)(2,1)S(1)} %copy.43) | data formatting | bytes 2097152 | tf_op jit(solution)/shard_map/reshape | solution.py:139
  146.1 8.7 %collective-permute-done.10 = bf16[1,18,16512]{2,1,0:T(8,128)(2,1)} collective-permute-done((bf16[1,18,16512]{2,1,0:T(8,128)(2,1)}, bf16[1,18,16512]{2,1,0:T(8,128)(2,1)}, u32[]{:S(2)}, u32[]{:S(2)}) %collective-permute-start.10) | collective-permute-done | bytes 594464 | tf_op jit(solution)/shard_map/ppermute | solution.py:17
  154.8 1.2 collective-permute-done.11
  156.0 3.9 %pad_maximum_fusion.1 = (bf16[3,18,16512]{2,1,0:T(8,128)(2,1)S(1)}, bf16[3,18,16512]{2,1,0:T(8,128)(2,1)}) fusion(bf16[1,18,16512]{2,1,0:T(8,128)(2,1)} %collective-permute-done.10, bf16[2,1,16512]{2,1,0:T(2,128)(2,1)} %copy-done.11, bf16[2,16,16512]{2,1,0:T(8,128)(2,1)S(1)} %concatenate.117, bf16[2,1,16512]{2,1,0:T(2,128)(2,1)} %copy-done.12, ...), kind=kLoop, calls=%fused_computation.14 | loop fusion | flops 14266368 | bytes 5944320 | tf_op jit(solution)/shard_map/concatenate | solution.py:18
  159.9 5.4 %reduce-scatter.5.cloned.1.call-done = f32[8,32,128]{2,0,1:T(8,128)} async-done(((f32[32,32,128]{2,0,1:T(8,128)}), f32[8,32,128]{2,0,1:T(8,128)}) %reduce-scatter.5.cloned.1.call-update) | async-done | bytes 131088 | tf_op jit(solution)/shard_map/reduce_scatter | solution.py:79
  166.2 1.2 convolution_convert_fusion.1
  167.4 1.1 fusion.33
  168.5 9.2 %all_gather.7 = bf16[32,32,128]{2,1,0:T(8,128)(2,1)S(1)} all-gather(bf16[8,32,128]{2,1,0:T(8,128)(2,1)S(1)} %convolution_convert_fusion.1), channel_id=1, replica_groups=mesh['gx'=4,'gy'=2,'gz'=4] {'gx'}, dimensions={0}, use_global_device_ids=true | all-gather | bytes 327680 | tf_op jit(solution)/shard_map/all_gather | solution.py:85
  179.6 1.6 fusion.26
  181.2 2.0 add_bitcast_fusion
  183.2 3.8 %copy.50 = f32[32,256,64]{2,1,0:T(8,128)} copy(f32[32,256,64]{1,2,0:T(8,128)} %add_bitcast_fusion) | data formatting | bytes 4194304 | tf_op jit(solution)/shard_map/add | solution.py:89
  187.0 4.0 %reshape.73 = f32[2,16,16384]{2,1,0:T(8,128)} reshape(f32[32,256,64]{2,1,0:T(8,128)} %copy.50) | data formatting | bytes 4194304 | tf_op jit(solution)/shard_map/reshape | solution.py:162
  191.0 21.6 %add_convert_fusion = bf16[2,16,16384]{2,1,0:T(8,128)(2,1)} fusion(f32[2,16,16384]{2,1,0:T(8,128)} %reshape.73, bf16[2,16,16384]{2,1,0:T(8,128)(2,1)} %copy-done.4, bf16[2,16,16512]{2,1,0:T(8,128)(2,1)S(1)} %concatenate.117, bf16[2,1,16512]{2,1,0:T(2,128)(2,1)} %copy-done.12, bf16[2,1,16512]{2,1,0:T(2,128)(2,1)} %copy-done.11, ...), kind=kLoop, calls=%fused_computation.31 | loop fusion | flops 55574528 | bytes 26035200 | tf_op jit(solution)/shard_map/convert_element_type | solution.py:162
  212.5 22.1 %all-reduce.2.cloned.1.call-done = bf16[2,8,64,64]{3,2,1,0:T(8,128)(2,1)} async-done(((bf16[2,8,64,64]{3,2,1,0:T(8,128)(2,1)}), bf16[2,8,64,64]{3,2,1,0:T(8,128)(2,1)}) %all-reduce.2.cloned.1.call-update) | async-done | bytes 131088 | tf_op jit(solution)/shard_map/psum | solution.py:101
  234.7 1.8 convert_element_type.381
  (187 shorter events, 33.7 us)
Async XLA Ops:
  7.2 73.9 %copy-start = (bf16[64,256]{1,0:T(8,128)(2,1)S(1)}, bf16[64,256]{1,0:T(8,128)(2,1)}, u32[]{:S(2)}) copy-start(bf16[64,256]{1,0:T(8,128)(2,1)} %param.9) | copy-start | bytes 98308
  7.2 81.8 %reduce-scatter.3.cloned.1.call-start = ((), (), s32[]{:S(2)}) async-start(), calls=%async_computation.2 | async-start | bytes 655360 | tf_op jit(solution)/shard_map/reduce_scatter | solution.py:79
  8.0 9.7 %collective-permute-start.1 = (bf16[2,16,64]{2,1,0:T(8,128)(2,1)S(1)}, bf16[2,16,64]{2,1,0:T(8,128)(2,1)S(1)}, u32[]{:S(2)}, u32[]{:S(2)}) collective-permute-start(bf16[2,16,64]{2,1,0:T(8,128)(2,1)S(1)} %get-tuple-element.19), channel_id=1, source_target_pairs={{8,0},{16,8},{24,16},{0,24},{9,1},{17,9},{25,17},{1,25},{10,2},{18... | collective-permute-start | bytes 12296 | tf_op jit(solution)/shard_map/ppermute | solution.py:17
  11.9 5.8 %collective-permute-start = (bf16[2,16,64]{2,1,0:T(8,128)(2,1)S(1)}, bf16[2,16,64]{2,1,0:T(8,128)(2,1)S(1)}, u32[]{:S(2)}, u32[]{:S(2)}) collective-permute-start(bf16[2,16,64]{2,1,0:T(8,128)(2,1)S(1)} %get-tuple-element.20), channel_id=1, source_target_pairs={{0,8},{8,16},{16,24},{24,0},{1,9},{9,17},{17,25},{25,1},{2,10},{10... | collective-permute-start | bytes 12296 | tf_op jit(solution)/shard_map/ppermute | solution.py:16
  17.7 5.8 %copy-start.8 = (f32[32,32,64]{2,0,1:T(8,128)S(1)}, f32[32,32,64]{2,0,1:T(8,128)}, u32[]{:S(2)}) copy-start(f32[32,32,64]{2,0,1:T(8,128)} %fusion.47) | copy-start | bytes 786436
  17.7 5.8 %copy-start.9 = (f32[32,32,64]{2,0,1:T(8,128)S(1)}, f32[32,32,64]{2,0,1:T(8,128)}, u32[]{:S(2)}) copy-start(f32[32,32,64]{2,0,1:T(8,128)} %fusion.50) | copy-start | bytes 786436
  20.7 3.9 %collective-permute-start.2 = (bf16[2,1,16512]{2,1,0:T(2,128)(2,1)S(1)}, bf16[2,1,16512]{2,1,0:T(2,128)(2,1)S(1)}, u32[]{:S(2)}, u32[]{:S(2)}) collective-permute-start(bf16[2,1,16512]{2,1,0:T(2,128)(2,1)S(1)} %get-tuple-element.15), channel_id=1, source_target_pairs={{0,4},{1,5},{2,6},{3,7},{8,12},{9,13},{10,14},{11,15},{16,20},{17,... | collective-permute-start | bytes 198152 | tf_op jit(solution)/shard_map/ppermute | solution.py:16
  22.2 3.2 %collective-permute-start.3 = (bf16[2,1,16512]{2,1,0:T(2,128)(2,1)S(1)}, bf16[2,1,16512]{2,1,0:T(2,128)(2,1)S(1)}, u32[]{:S(2)}, u32[]{:S(2)}) collective-permute-start(bf16[2,1,16512]{2,1,0:T(2,128)(2,1)S(1)} %get-tuple-element.16), channel_id=1, source_target_pairs={{4,0},{5,1},{6,2},{7,3},{12,8},{13,9},{14,10},{15,11},{20,16},{21,... | collective-permute-start | bytes 198152 | tf_op jit(solution)/shard_map/ppermute | solution.py:17
  24.5 140.8 %reduce-scatter.5.cloned.1.call-start = ((), (), s32[]{:S(2)}) async-start(), calls=%async_computation.3 | async-start | bytes 655360 | tf_op jit(solution)/shard_map/reduce_scatter | solution.py:79
  26.0 7.1 %copy-start.43 = (bf16[27,64]{1,0:T(8,128)(2,1)S(1)}, bf16[27,64]{1,0:T(8,128)(2,1)}, u32[]{:S(2)}) copy-start(bf16[27,64]{1,0:T(8,128)(2,1)} %param.8) | copy-start | bytes 10372
  27.3 32.6 %collective-permute-start.4 = (bf16[1,18,16512]{2,1,0:T(8,128)(2,1)}, bf16[1,18,16512]{2,1,0:T(8,128)(2,1)}, u32[]{:S(2)}, u32[]{:S(2)}) collective-permute-start(bf16[1,18,16512]{2,1,0:T(8,128)(2,1)} %get-tuple-element.7), channel_id=1, source_target_pairs={{0,1},{1,2},{2,3},{4,5},{5,6},{6,7},{8,9},{9,10},{10,11},{12,13},{... | collective-permute-start | bytes 1783304 | tf_op jit(solution)/shard_map/ppermute | solution.py:16
  31.7 28.2 %collective-permute-start.5 = (bf16[1,18,16512]{2,1,0:T(8,128)(2,1)}, bf16[1,18,16512]{2,1,0:T(8,128)(2,1)}, u32[]{:S(2)}, u32[]{:S(2)}) collective-permute-start(bf16[1,18,16512]{2,1,0:T(8,128)(2,1)} %get-tuple-element.8), channel_id=1, source_target_pairs={{1,0},{2,1},{3,2},{5,4},{6,5},{7,6},{9,8},{10,9},{11,10},{13,12},{... | collective-permute-start | bytes 1783304 | tf_op jit(solution)/shard_map/ppermute | solution.py:17
  42.7 9.5 %copy-start.10 = (bf16[32,64,64]{2,1,0:T(8,128)(2,1)S(1)}, bf16[32,64,64]{2,1,0:T(8,128)(2,1)}, u32[]{:S(2)}) copy-start(bf16[32,64,64]{2,1,0:T(8,128)(2,1)} %param.12) | copy-start | bytes 786436
  44.9 7.4 %copy-start.13 = (bf16[2,16,16384]{2,1,0:T(8,128)(2,1)S(1)}, bf16[2,16,16384]{2,1,0:T(8,128)(2,1)}, u32[]{:S(2)}) copy-start(bf16[2,16,16384]{2,1,0:T(8,128)(2,1)} %param.13) | copy-start | bytes 3145732
  55.6 3.9 %copy-start.42 = (bf16[32,64,64]{2,1,0:T(8,128)(2,1)S(1)}, bf16[32,64,64]{2,1,0:T(8,128)(2,1)}, u32[]{:S(2)}) copy-start(bf16[32,64,64]{2,1,0:T(8,128)(2,1)} %param.11) | copy-start | bytes 786436
  59.6 30.5 %copy-start.6 = (bf16[8,128,128]{2,1,0:T(8,128)(2,1)}, bf16[8,128,128]{2,1,0:T(8,128)(2,1)S(1)}, u32[]{:S(2)}) copy-start(bf16[8,128,128]{2,1,0:T(8,128)(2,1)S(1)} %fusion.21) | copy-start | bytes 786436
  59.6 3.3 %copy-start.3 = (bf16[2,16,16384]{2,1,0:T(8,128)(2,1)S(1)}, bf16[2,16,16384]{2,1,0:T(8,128)(2,1)}, u32[]{:S(2)}) copy-start(bf16[2,16,16384]{2,1,0:T(8,128)(2,1)} %param.7) | copy-start | bytes 3145732
  59.6 3.3 %copy-start.15 = (f32[16384]{0:T(1024)S(1)}, f32[16384]{0:T(1024)}, u32[]{:S(2)}) copy-start(f32[16384]{0:T(1024)} %mul.548) | copy-start | bytes 196612
  59.6 3.3 %copy-start.16 = (f32[16384]{0:T(1024)S(1)}, f32[16384]{0:T(1024)}, u32[]{:S(2)}) copy-start(f32[16384]{0:T(1024)} %mul.617) | copy-start | bytes 196612
  59.6 3.3 %copy-start.17 = (f32[16384]{0:T(1024)S(1)}, f32[16384]{0:T(1024)}, u32[]{:S(2)}) copy-start(f32[16384]{0:T(1024)} %mul.614) | copy-start | bytes 196612
  59.7 3.3 %copy-start.18 = (f32[16384]{0:T(1024)S(1)}, f32[16384]{0:T(1024)}, u32[]{:S(2)}) copy-start(f32[16384]{0:T(1024)} %mul.611) | copy-start | bytes 196612
  59.7 3.3 %copy-start.19 = (f32[16384]{0:T(1024)S(1)}, f32[16384]{0:T(1024)}, u32[]{:S(2)}) copy-start(f32[16384]{0:T(1024)} %mul.608) | copy-start | bytes 196612
  59.7 3.3 %copy-start.20 = (f32[16384]{0:T(1024)S(1)}, f32[16384]{0:T(1024)}, u32[]{:S(2)}) copy-start(f32[16384]{0:T(1024)} %mul.605) | copy-start | bytes 196612
  59.7 3.3 %copy-start.21 = (f32[16384]{0:T(1024)S(1)}, f32[16384]{0:T(1024)}, u32[]{:S(2)}) copy-start(f32[16384]{0:T(1024)} %mul.602) | copy-start | bytes 196612
  59.7 3.3 %copy-start.22 = (f32[16384]{0:T(1024)S(1)}, f32[16384]{0:T(1024)}, u32[]{:S(2)}) copy-start(f32[16384]{0:T(1024)} %mul.599) | copy-start | bytes 196612
  59.7 3.3 %copy-start.23 = (f32[16384]{0:T(1024)S(1)}, f32[16384]{0:T(1024)}, u32[]{:S(2)}) copy-start(f32[16384]{0:T(1024)} %mul.596) | copy-start | bytes 196612
  59.7 3.3 %copy-start.24 = (f32[16384]{0:T(1024)S(1)}, f32[16384]{0:T(1024)}, u32[]{:S(2)}) copy-start(f32[16384]{0:T(1024)} %mul.593) | copy-start | bytes 196612
  59.7 3.3 %copy-start.25 = (f32[16384]{0:T(1024)S(1)}, f32[16384]{0:T(1024)}, u32[]{:S(2)}) copy-start(f32[16384]{0:T(1024)} %mul.590) | copy-start | bytes 196612
  59.7 3.3 %copy-start.26 = (f32[16384]{0:T(1024)S(1)}, f32[16384]{0:T(1024)}, u32[]{:S(2)}) copy-start(f32[16384]{0:T(1024)} %mul.587) | copy-start | bytes 196612
  59.7 3.3 %copy-start.27 = (f32[16384]{0:T(1024)S(1)}, f32[16384]{0:T(1024)}, u32[]{:S(2)}) copy-start(f32[16384]{0:T(1024)} %mul.584) | copy-start | bytes 196612
  59.8 3.3 %copy-start.28 = (f32[16384]{0:T(1024)S(1)}, f32[16384]{0:T(1024)}, u32[]{:S(2)}) copy-start(f32[16384]{0:T(1024)} %mul.581) | copy-start | bytes 196612
  59.8 3.3 %copy-start.29 = (f32[16384]{0:T(1024)S(1)}, f32[16384]{0:T(1024)}, u32[]{:S(2)}) copy-start(f32[16384]{0:T(1024)} %mul.578) | copy-start | bytes 196612
  59.8 3.3 %copy-start.30 = (f32[16384]{0:T(1024)S(1)}, f32[16384]{0:T(1024)}, u32[]{:S(2)}) copy-start(f32[16384]{0:T(1024)} %mul.575) | copy-start | bytes 196612
  59.8 3.3 %copy-start.31 = (f32[16384]{0:T(1024)S(1)}, f32[16384]{0:T(1024)}, u32[]{:S(2)}) copy-start(f32[16384]{0:T(1024)} %mul.572) | copy-start | bytes 196612
  59.8 3.3 %copy-start.32 = (f32[16384]{0:T(1024)S(1)}, f32[16384]{0:T(1024)}, u32[]{:S(2)}) copy-start(f32[16384]{0:T(1024)} %mul.569) | copy-start | bytes 196612
  59.8 3.3 %copy-start.33 = (f32[16384]{0:T(1024)S(1)}, f32[16384]{0:T(1024)}, u32[]{:S(2)}) copy-start(f32[16384]{0:T(1024)} %mul.566) | copy-start | bytes 196612
  81.0 4.6 %copy-start.44 = (bf16[256,64]{0,1:T(8,128)(2,1)S(1)}, bf16[256,64]{0,1:T(8,128)(2,1)}, u32[]{:S(2)}) copy-start(bf16[256,64]{0,1:T(8,128)(2,1)} %param.10) | copy-start | bytes 98308
  89.0 12.2 %copy-start.7 = (f32[8192,64]{0,1:T(8,128)S(1)}, f32[8192,64]{0,1:T(8,128)}, u32[]{:S(2)}) copy-start(f32[8192,64]{0,1:T(8,128)} %fusion.5) | copy-start | bytes 6291460
  90.7 10.5 %copy-start.5 = (f32[32,256,64]{1,2,0:T(8,128)S(1)}, f32[32,256,64]{1,2,0:T(8,128)}, u32[]{:S(2)}) copy-start(f32[32,256,64]{1,2,0:T(8,128)} %copy.44) | copy-start | bytes 6291460
  117.0 13.4 %copy-start.4 = (bf16[2,16,16384]{2,1,0:T(8,128)(2,1)}, bf16[2,16,16384]{2,1,0:T(8,128)(2,1)S(1)}, u32[]{:S(2)}) copy-start(bf16[2,16,16384]{2,1,0:T(8,128)(2,1)S(1)} %reshape.72) | copy-start | bytes 3145732
  117.1 3.7 %collective-permute-start.7 = (bf16[2,16,64]{2,1,0:T(8,128)(2,1)S(1)}, bf16[2,16,64]{2,1,0:T(8,128)(2,1)S(1)}, u32[]{:S(2)}, u32[]{:S(2)}) collective-permute-start(bf16[2,16,64]{2,1,0:T(8,128)(2,1)S(1)} %get-tuple-element.17), channel_id=1, source_target_pairs={{8,0},{16,8},{24,16},{0,24},{9,1},{17,9},{25,17},{1,25},{10,2},{18... | collective-permute-start | bytes 12296 | tf_op jit(solution)/shard_map/ppermute | solution.py:17
  118.6 4.5 %collective-permute-start.6 = (bf16[2,16,64]{2,1,0:T(8,128)(2,1)S(1)}, bf16[2,16,64]{2,1,0:T(8,128)(2,1)S(1)}, u32[]{:S(2)}, u32[]{:S(2)}) collective-permute-start(bf16[2,16,64]{2,1,0:T(8,128)(2,1)S(1)} %get-tuple-element.18), channel_id=1, source_target_pairs={{0,8},{8,16},{16,24},{24,0},{1,9},{9,17},{17,25},{25,1},{2,10},{10... | collective-permute-start | bytes 12296 | tf_op jit(solution)/shard_map/ppermute | solution.py:16
  124.5 4.4 %collective-permute-start.9 = (bf16[2,1,16512]{2,1,0:T(2,128)(2,1)S(1)}, bf16[2,1,16512]{2,1,0:T(2,128)(2,1)S(1)}, u32[]{:S(2)}, u32[]{:S(2)}) collective-permute-start(bf16[2,1,16512]{2,1,0:T(2,128)(2,1)S(1)} %get-tuple-element.13), channel_id=1, source_target_pairs={{4,0},{5,1},{6,2},{7,3},{12,8},{13,9},{14,10},{15,11},{20,16},{21,... | collective-permute-start | bytes 198152 | tf_op jit(solution)/shard_map/ppermute | solution.py:17
  125.8 4.0 %collective-permute-start.8 = (bf16[2,1,16512]{2,1,0:T(2,128)(2,1)S(1)}, bf16[2,1,16512]{2,1,0:T(2,128)(2,1)S(1)}, u32[]{:S(2)}, u32[]{:S(2)}) collective-permute-start(bf16[2,1,16512]{2,1,0:T(2,128)(2,1)S(1)} %get-tuple-element.14), channel_id=1, source_target_pairs={{0,4},{1,5},{2,6},{3,7},{8,12},{9,13},{10,14},{11,15},{16,20},{17,... | collective-permute-start | bytes 198152 | tf_op jit(solution)/shard_map/ppermute | solution.py:16
  131.7 23.0 %collective-permute-start.10 = (bf16[1,18,16512]{2,1,0:T(8,128)(2,1)}, bf16[1,18,16512]{2,1,0:T(8,128)(2,1)}, u32[]{:S(2)}, u32[]{:S(2)}) collective-permute-start(bf16[1,18,16512]{2,1,0:T(8,128)(2,1)} %get-tuple-element.5), channel_id=1, source_target_pairs={{1,0},{2,1},{3,2},{5,4},{6,5},{7,6},{9,8},{10,9},{11,10},{13,12},{... | collective-permute-start | bytes 1783304 | tf_op jit(solution)/shard_map/ppermute | solution.py:17
  133.0 22.9 %collective-permute-start.11 = (bf16[1,18,16512]{2,1,0:T(8,128)(2,1)}, bf16[1,18,16512]{2,1,0:T(8,128)(2,1)}, u32[]{:S(2)}, u32[]{:S(2)}) collective-permute-start(bf16[1,18,16512]{2,1,0:T(8,128)(2,1)} %get-tuple-element.6), channel_id=1, source_target_pairs={{0,1},{1,2},{2,3},{4,5},{5,6},{6,7},{8,9},{9,10},{10,11},{12,13},{... | collective-permute-start | bytes 1783304 | tf_op jit(solution)/shard_map/ppermute | solution.py:16
  141.5 93.2 %all-reduce.2.cloned.1.call-start = ((), (), s32[]{:S(2)}) async-start(), calls=%async_computation.4 | async-start | bytes 524288 | tf_op jit(solution)/shard_map/psum | solution.py:101
  191.0 45.5 %copy-start.1 = (bf16[64,256]{1,0:T(8,128)(2,1)S(1)}, bf16[64,256]{1,0:T(8,128)(2,1)}, u32[]{:S(2)}) copy-start(bf16[64,256]{1,0:T(8,128)(2,1)} %param.9) | copy-start | bytes 98308
  (13 other events, 34.5 us)
Sparse Core Ops, SparseCore 0:
  24.6 27.1 reduce-scatter.2
  141.6 23.6 reduce-scatter.4
  179.7 54.9 all-reduce.1
where the time goes:
time: 244 us; the launch traced here: 243 us
  local copies, waits for them, and re-layouts  62.6 us (26%)
  other arithmetic  51.6 us (21%)
  waiting for transfers between devices  43.3 us (18%)
  starting transfers between devices  26.4 us (11%)
  matrix products  25.6 us (10%)
  blocking collectives  18.8 us (8%)
  between operations  14.7 us (6%)
    psum x1, waiting for transfers between devices, sum_gradients(): lax.psum(local_grads.astype(jnp.bfloat16), ('gy', 'gz')).astype(jnp.float32)  22.1 us
    convert_element_type x1, other arithmetic, per_device(): (grad_local + spectral_grad.reshape(planes, y_cells, merged)).astype(jnp....  21.6 us
    all_gather x2, blocking collectives, share_inverse(): segment = lax.all_gather(modes_share, 'gx', axis=0, tiled=True)  18.8 us
    mul x27, local copies, waits for them, and re-layouts, depthwise(): running = running + cut.astype(jnp.float32) * jnp.tile(tap_gain, x_cells)  18.6 us
    ppermute x6, starting transfers between devices, padded_2(): before = lax.ppermute(last, axis, up)  15.6 us
    convert_element_type x1, other arithmetic, per_device(): depthwise(padded, depth_weight, False, x_cells, channels)  14.8 us
    ppermute x6, waiting for transfers between devices, padded_2(): after = lax.ppermute(leading, axis, down)  11.2 us
    ppermute x6, starting transfers between devices, padded_2(): after = lax.ppermute(leading, axis, down)  10.7 us
  transfers between devices with their start and end apart: 15, of which 8 were waited for; matrix products, arithmetic and copies ran while one was open for 43% of the time, Pallas kernels for 0%

commit v1 on v0

--- a/solution.py
+++ b/solution.py
@@ -1,8 +1,11 @@
+import functools
 import math
 
 import jax
 import jax.numpy as jnp
 from jax import lax
+from jax.experimental import pallas as pl
+from jax.experimental.pallas import tpu as pltpu
 from jax.sharding import PartitionSpec as P
 
 
@@ -46,31 +49,57 @@
 
 
 def spatial_rims(field_block, channels):
-    x_wide = padded_2(field_block, (("gx", 2),), channels, True)
+    x_wide = padded_2(field_block, (("gx", 2),), 2 * channels, True)
     return padded_2(x_wide, (("gy", 1), ("gz", 0)), 1, False)
 
 
-def depthwise(padded, taps, flipped, x_cells, channels):
+def stencil_kernel(chunk, x_pad, planes, y_cells, p_ref, w_ref, o_ref, s_ref):
+    s_ref[...] = p_ref[...].astype(jnp.float32)
+    width = chunk + 2 * x_pad
+    count = o_ref.shape[2] // chunk
+
+    def body(index, carry):
+        base = pl.multiple_of(index * chunk, chunk)
+        for plane in range(planes):
+            left = jnp.zeros((y_cells, chunk + x_pad), jnp.float32)
+            centre = jnp.zeros((y_cells, chunk), jnp.float32)
+            right = jnp.zeros((y_cells, chunk + x_pad), jnp.float32)
+            for step_z in range(3):
+                for step_y in range(3):
+                    window = s_ref[plane + step_z, pl.ds(step_y, y_cells), pl.ds(base, width)]
+                    tap = 9 * step_z + 3 * step_y
+                    left = left + window[:, : chunk + x_pad] * w_ref[tap : tap + 1, : chunk + x_pad]
+                    centre = centre + window[:, x_pad : x_pad + chunk] * w_ref[
+                        tap + 1 : tap + 2, :chunk
+                    ]
+                    right = right + window[:, x_pad:] * w_ref[tap + 2 : tap + 3, : chunk + x_pad]
+            shift = chunk + x_pad - x_pad // 2
+            total = (
+                centre
+                + pltpu.roll(left, shift, 1)[:, :chunk]
+                + pltpu.roll(right, shift, 1)[:, :chunk]
+            )
+            o_ref[plane, :, pl.ds(base, chunk)] = total.astype(o_ref.dtype)
+        return carry
+
+    lax.fori_loop(0, count, body, 0)
+
+
+def depthwise(padded, taps, flipped, x_cells, channels, out_dtype=jnp.float32):
     planes = padded.shape[0] - 2
     y_cells = padded.shape[1] - 2
-    running = jnp.zeros((planes, y_cells, x_cells * channels), jnp.float32)
-    direction = -1 if flipped else 1
-    for step_z in (-1, 0, 1):
-        for step_y in (-1, 0, 1):
-            for step_x in (-1, 0, 1):
-                tap_gain = taps[(step_z + 1) * 9 + (step_y + 1) * 3 + (step_x + 1)].astype(
-                    jnp.float32
-                )
-                z_offset = 1 + direction * step_z
-                y_offset = 1 + direction * step_y
-                x_offset = 1 + direction * step_x
-                cut = padded[
-                    z_offset : z_offset + planes,
-                    y_offset : y_offset + y_cells,
-                    x_offset * channels : (x_offset + x_cells) * channels,
-                ]
-                running = running + cut.astype(jnp.float32) * jnp.tile(tap_gain, x_cells)
-    return running
+    x_pad = 2 * channels
+    lanes = x_cells * channels
+    chunk = min(512, lanes)
+    if flipped:
+        taps = taps[::-1]
+    gains = jnp.tile(taps.astype(jnp.float32), (1, (chunk + x_pad) // channels))
+    kernel = functools.partial(stencil_kernel, chunk, x_pad, planes, y_cells)
+    return pl.pallas_call(
+        kernel,
+        out_shape=jax.ShapeDtypeStruct((planes, y_cells, lanes), out_dtype),
+        scratch_shapes=[pltpu.VMEM(padded.shape, jnp.float32)],
+    )(padded, gains)
 
 
 def share_terms(field3, cos_table, sin_table):
@@ -117,7 +146,7 @@
     sin_scaled = scaled_table(sin_part, mode_count, x_length)
     blocks = block_weights(spec_real, spec_imag)
     padded = spatial_rims(features, channels)
-    activation = depthwise(padded, depth_weight, False, x_cells, channels).astype(jnp.bfloat16)
+    activation = depthwise(padded, depth_weight, False, x_cells, channels, jnp.bfloat16)
     activation = activation.reshape(row_count * x_cells, channels)
     hidden_pre = jnp.dot(activation, expand_weight, preferred_element_type=jnp.float32)
     hidden, hidden_slope = gelu_parts(hidden_pre)

time: 244 us -> 248 us (1.016)
  other arithmetic: 51.6 us -> 18.7 us
  waiting for transfers between devices: 43.3 us -> 75.6 us
  Pallas kernels: 0 us -> 26.3 us
  local copies, waits for them, and re-layouts: 62.6 us -> 43.5 us
  matrix products: 25.6 us -> 20.2 us
  starting transfers between devices: 26.4 us -> 31.1 us
    psum x1, waiting for transfers between devices: 22.1 us -> 54.6 us  [sum_gradients(): lax.psum(local_grads.astype(jnp.bfloat16), ('gy', 'gz')).astype(jnp.float32)]
    pallas_call x0 -> x2, Pallas kernels: none -> 26.3 us  [depthwise(): pl.pallas_call(kernel, out_shape=jax.ShapeDtypeStruct((planes, y_cells, l...]
    convert_element_type x1, other arithmetic: 21.6 us -> 2.75 us  [per_device(): (grad_local + spectral_grad.reshape(planes, y_cells, merged)).astype(jnp....]
    mul x27 -> x0, local copies, waits for them, and re-layouts: 18.6 us -> none  [depthwise(): running = running + cut.astype(jnp.float32) * jnp.tile(tap_gain, x_cells)]
    convert_element_type x1 -> x0, other arithmetic: 14.8 us -> none  [per_device(): depthwise(padded, depth_weight, False, x_cells, channels)]
    ppermute x6, starting transfers between devices: 15.6 us -> 21.9 us  [padded_2(): before = lax.ppermute(last, axis, up)]
    reduce_scatter x2, waiting for transfers between devices: 5.44 us -> 0.02 us  [share_terms(): lax.psum_scatter(jnp.concatenate([real_part, imag_part], axis=2), 'gx', s...]
    ppermute x6, waiting for transfers between devices: 11.2 us -> 16.5 us  [padded_2(): after = lax.ppermute(leading, axis, down)]
  transfers between devices with their start and end apart: 15 -> 15, of which waited for: 8 -> 7; matrix products, arithmetic and copies ran while one was open for 43% -> 17% of each run, Pallas kernels for 0% -> 11%
where the time goes in v1:
time: 248 us; the launch traced here: 247 us
  waiting for transfers between devices  75.6 us (30%)
  local copies, waits for them, and re-layouts  43.5 us (18%)
  starting transfers between devices  31.1 us (13%)
  Pallas kernels  26.3 us (11%)
  matrix products  20.2 us (8%)
  other arithmetic  18.7 us (8%)
  blocking collectives  18 us (7%)
  between operations  14.1 us (6%)
    psum x1, waiting for transfers between devices, sum_gradients(): lax.psum(local_grads.astype(jnp.bfloat16), ('gy', 'gz')).astype(jnp.float32)  54.6 us
    pallas_call x2, Pallas kernels, depthwise(): pl.pallas_call(kernel, out_shape=jax.ShapeDtypeStruct((planes, y_cells, l...  26.3 us
    ppermute x6, starting transfers between devices, padded_2(): before = lax.ppermute(last, axis, up)  21.9 us
    all_gather x2, blocking collectives, share_inverse(): segment = lax.all_gather(modes_share, 'gx', axis=0, tiled=True)  18 us
    ppermute x6, waiting for transfers between devices, padded_2(): after = lax.ppermute(leading, axis, down)  16.5 us
    concatenate x4, other arithmetic, padded_2(): value = jnp.concatenate([before, value, after], axis=dim)  9.05 us
    ppermute x6, starting transfers between devices, padded_2(): after = lax.ppermute(leading, axis, down)  8.84 us
    dot_general x1, matrix products, per_device(): jnp.dot(grad_hidden, expand_weight.T, preferred_element_type=jnp.float32)  8.79 us
  transfers between devices with their start and end apart: 15, of which 7 were waited for; matrix products, arithmetic and copies ran while one was open for 17% of the time, Pallas kernels for 11%

profile of v1, /device:TPU:0, one launch (start us, length us, event | category | flops | bytes accessed | tf_op | source)
XLA Modules:
  0.0 247.3 jit_solution(1037208363197075402)
XLA Ops:
  7.9 2.9 %collective-permute-start = (bf16[2,16,128]{2,1,0:T(8,128)(2,1)S(1)}, bf16[2,16,128]{2,1,0:T(8,128)(2,1)S(1)}, u32[]{:S(2)}, u32[]{:S(2)}) collective-permute-start(bf16[2,16,128]{2,1,0:T(8,128)(2,1)S(1)} %get-tuple-element.16), channel_id=1, source_target_pairs={{0,8},{8,16},{16,24},{24,0},{1,9},{9,17},{17,25},{25,1},{2,10},{10... | collective-permute-start | bytes 24584 | tf_op jit(solution)/shard_map/ppermute | solution.py:19
  10.9 1.0 collective-permute-start.1
  11.8 3.0 %reshape.50 = bf16[32,256,64]{2,1,0:T(8,128)(2,1)S(1)} reshape(bf16[2,16,16384]{2,1,0:T(8,128)(2,1)} %param.7) | data formatting | bytes 2097152 | tf_op jit(solution)/shard_map/reshape | solution.py:157
  14.9 1.3 constant_dynamic-update-slice_fusion.1
  16.4 1.3 collective-permute-start.3
  17.7 3.0 %collective-permute-start.2 = (bf16[2,1,16640]{2,1,0:T(2,128)(2,1)S(1)}, bf16[2,1,16640]{2,1,0:T(2,128)(2,1)S(1)}, u32[]{:S(2)}, u32[]{:S(2)}) collective-permute-start(bf16[2,1,16640]{2,1,0:T(2,128)(2,1)S(1)} %get-tuple-element.11), channel_id=1, source_target_pairs={{0,4},{1,5},{2,6},{3,7},{8,12},{9,13},{10,14},{11,15},{16,20},{17,... | collective-permute-start | bytes 199688 | tf_op jit(solution)/shard_map/ppermute | solution.py:19
  22.4 1.3 fusion.86
  23.6 1.3 collective-permute-start.5
  24.9 5.5 %collective-permute-start.4 = (bf16[1,18,16640]{2,1,0:T(8,128)(2,1)}, bf16[1,18,16640]{2,1,0:T(8,128)(2,1)}, u32[]{:S(2)}, u32[]{:S(2)}) collective-permute-start(bf16[1,18,16640]{2,1,0:T(8,128)(2,1)} %get-tuple-element.7), channel_id=1, source_target_pairs={{0,1},{1,2},{2,3},{4,5},{5,6},{6,7},{8,9},{9,10},{10,11},{12,13},{... | collective-permute-start | bytes 1797128 | tf_op jit(solution)/shard_map/ppermute | solution.py:19
  31.0 1.0 pad_maximum_fusion.4
  32.1 4.3 %reshape.55 = f32[32,256,64]{2,1,0:T(8,128)} reshape(bf16[2,16,16384]{2,1,0:T(8,128)(2,1)} %param.13) | data formatting | bytes 3145728 | tf_op jit(solution)/shard_map/convert_element_type | solution.py:170
  36.3 3.9 %copy.46 = f32[32,256,64]{1,2,0:T(8,128)} copy(f32[32,256,64]{2,1,0:T(8,128)} %reshape.55) | data formatting | bytes 4194304 | tf_op jit(solution)/shard_map/convert_element_type | solution.py:170
  41.3 4.9 %collective-permute-done.5 = bf16[1,18,16640]{2,1,0:T(8,128)(2,1)} collective-permute-done((bf16[1,18,16640]{2,1,0:T(8,128)(2,1)}, bf16[1,18,16640]{2,1,0:T(8,128)(2,1)}, u32[]{:S(2)}, u32[]{:S(2)}) %collective-permute-start.5) | collective-permute-done | bytes 599072 | tf_op jit(solution)/shard_map/ppermute | solution.py:20
  46.2 1.2 collective-permute-done.4
  47.4 3.2 %pad_maximum_fusion.p_ref = bf16[4,18,16640]{2,1,0:T(8,128)(2,1)} fusion(bf16[1,18,16640]{2,1,0:T(8,128)(2,1)} %collective-permute-done.5, bf16[2,1,16640]{2,1,0:T(2,128)(2,1)S(1)} %copy-done.8, bf16[2,16,16640]{2,1,0:T(8,128)(2,1)S(1)} %constant_dynamic-update-slice_fusion, bf16[2,1,16640]{2,1,0:T(2,128)(2,1)S(1)} %copy-done.10, ...), kind=kLoop, calls=%fused_computation.11 | loop fusion | flops 11980800 | bytes 4792320 | tf_op jit(solution)/shard_map/concatenate | solution.py:21
  50.6 13.0 %shard_map.94 = bf16[2,16,16384]{2,1,0:T(8,128)(2,1)} custom-call(bf16[4,18,16640]{2,1,0:T(8,128)(2,1)} %pad_maximum_fusion.p_ref, f32[27,640]{1,0:T(8,128)} %tile.9.w_ref), custom_call_target="tpu_custom_call" | custom-call | tf_op jit(solution)/shard_map/pallas_call | solution.py:98
  63.6 3.0 %reshape.48 = bf16[8192,64]{1,0:T(8,128)(2,1)S(1)} reshape(bf16[2,16,16384]{2,1,0:T(8,128)(2,1)} %shard_map.94) | data formatting | bytes 2097152 | tf_op jit(solution)/shard_map/reshape | solution.py:150
  66.7 1.2 fusion.93
  67.9 3.3 %copy-done.2 = f32[8192,256]{1,0:T(8,128)} copy-done((f32[8192,256]{1,0:T(8,128)}, f32[8192,256]{1,0:T(8,128)S(1)}, u32[]{:S(2)}) %copy-start.2) | copy-done | bytes 8388632
  71.2 2.8 %fusion.5 = f32[8192,64]{0,1:T(8,128)S(1)} fusion(bf16[256,64]{0,1:T(8,128)(2,1)S(1)} %copy-done.13, f32[8192,256]{1,0:T(8,128)S(1)} %fusion.93), kind=kOutput, calls=%fused_computation.10 | convolution fusion | flops 278921216 | bytes 10518528 | tf_op jit(solution)/shard_map/dot_general | solution.py:153
  75.1 9.8 %all_gather.6 = bf16[32,32,128]{2,1,0:T(8,128)(2,1)S(1)} all-gather(bf16[8,32,128]{2,1,0:T(8,128)(2,1)S(1)} %convolution_convert_fusion.2), channel_id=1, replica_groups=mesh['gx'=4,'gy'=2,'gz'=4] {'gx'}, dimensions={0}, use_global_device_ids=true | all-gather | bytes 327680 | tf_op jit(solution)/shard_map/all_gather | solution.py:114
  85.7 2.6 %fusion.11 = (bf16[32,256,64]{1,2,0:T(8,128)(2,1)S(1)}, bf16[32,256,64]{1,2,0:T(8,128)(2,1)}) fusion(f32[32,256,64]{1,2,0:T(8,128)S(1)} %copy-done.3, f32[256,32,64]{0,2,1:T(8,128)S(1)} %fusion.21, bf16[32,32,64]{2,1,0:T(8,128)(2,1)S(1)} %get-tuple-element.21, f32[32]{0:T(128)S(1)} %fusion.58, s32[256]{0:T(256)S(1)} %iota_add_fusion, ...), kind=kOutput, calls=%fused_computation.19 | convolution fusion | flops 41050112 | bytes 8520832 | tf_op jit(solution)/shard_map/krc,xk->rxc/dot_general | solution.py:118
  89.0 8.8 %convolution_convert_fusion = bf16[8192,64]{0,1:T(8,128)(2,1)} fusion(bf16[64,256]{1,0:T(8,128)(2,1)S(1)} %copy-done, bf16[8192,64]{0,1:T(8,128)(2,1)S(1)} %bitcast.47, bf16[256,64]{0,1:T(8,128)(2,1)S(1)} %copy-done.14, f32[8192,256]{1,0:T(8,128)} %copy-done.2), kind=kOutput, calls=%fused_computation.3 | convolution fusion | flops 558366720 | bytes 10551296 | tf_op jit(solution)/shard_map/dot_general | solution.py:178
  97.8 2.0 copy.48
  99.9 2.5 %reshape.53 = bf16[2,16,16384]{2,1,0:T(8,128)(2,1)} reshape(bf16[8192,64]{1,0:T(8,128)(2,1)S(1)} %copy.48) | data formatting | bytes 2097152 | tf_op jit(solution)/shard_map/reshape | solution.py:181
  103.2 2.8 %collective-permute-start.7 = (bf16[2,16,128]{2,1,0:T(8,128)(2,1)S(1)}, bf16[2,16,128]{2,1,0:T(8,128)(2,1)S(1)}, u32[]{:S(2)}, u32[]{:S(2)}) collective-permute-start(bf16[2,16,128]{2,1,0:T(8,128)(2,1)S(1)} %get-tuple-element.13), channel_id=1, source_target_pairs={{8,0},{16,8},{24,16},{0,24},{9,1},{17,9},{25,17},{1,25},{10,2},{18... | collective-permute-start | bytes 24584 | tf_op jit(solution)/shard_map/ppermute | solution.py:20
  106.0 1.6 collective-permute-done.6
  107.6 1.3 constant_dynamic-update-slice_fusion.4
  108.9 1.0 copy-done.4
  110.8 1.3 collective-permute-start.9
  112.1 4.3 %collective-permute-start.8 = (bf16[2,1,16640]{2,1,0:T(2,128)(2,1)}, bf16[2,1,16640]{2,1,0:T(2,128)(2,1)}, u32[]{:S(2)}, u32[]{:S(2)}) collective-permute-start(bf16[2,1,16640]{2,1,0:T(2,128)(2,1)} %get-tuple-element.9), channel_id=1, source_target_pairs={{0,4},{1,5},{2,6},{3,7},{8,12},{9,13},{10,14},{11,15},{16,20},{17,... | collective-permute-start | bytes 199688 | tf_op jit(solution)/shard_map/ppermute | solution.py:19
  117.2 2.0 copy.45
  119.2 2.5 %reshape.51 = bf16[2,16,16384]{2,1,0:T(8,128)(2,1)} reshape(bf16[32,256,64]{2,1,0:T(8,128)(2,1)S(1)} %copy.45) | data formatting | bytes 2097152 | tf_op jit(solution)/shard_map/reshape | solution.py:168
  121.7 1.9 pad_maximum_fusion.3
  123.6 1.3 fusion.85
  124.9 1.3 collective-permute-start.11
  126.2 5.9 %collective-permute-start.10 = (bf16[1,18,16640]{2,1,0:T(8,128)(2,1)}, bf16[1,18,16640]{2,1,0:T(8,128)(2,1)}, u32[]{:S(2)}, u32[]{:S(2)}) collective-permute-start(bf16[1,18,16640]{2,1,0:T(8,128)(2,1)} %get-tuple-element.5), channel_id=1, source_target_pairs={{0,1},{1,2},{2,3},{4,5},{5,6},{6,7},{8,9},{9,10},{10,11},{12,13},{... | collective-permute-start | bytes 1797128 | tf_op jit(solution)/shard_map/ppermute | solution.py:19
  133.4 1.0 pad_maximum_fusion.5
  134.7 11.6 %collective-permute-done.11 = bf16[1,18,16640]{2,1,0:T(8,128)(2,1)} collective-permute-done((bf16[1,18,16640]{2,1,0:T(8,128)(2,1)}, bf16[1,18,16640]{2,1,0:T(8,128)(2,1)}, u32[]{:S(2)}, u32[]{:S(2)}) %collective-permute-start.11) | collective-permute-done | bytes 599072 | tf_op jit(solution)/shard_map/ppermute | solution.py:20
  146.3 1.2 collective-permute-done.10
  147.5 3.3 %pad_maximum_fusion.1.p_ref = bf16[4,18,16640]{2,1,0:T(8,128)(2,1)} fusion(bf16[1,18,16640]{2,1,0:T(8,128)(2,1)} %collective-permute-done.11, bf16[2,1,16640]{2,1,0:T(2,128)(2,1)} %collective-permute-done.9, bf16[2,16,16640]{2,1,0:T(8,128)(2,1)S(1)} %copy-done.5, bf16[2,1,16640]{2,1,0:T(2,128)(2,1)} %collective-permute-done.8, ...), kind=kLoop, calls=%fused_computation.12 | loop fusion | flops 11980800 | bytes 4792320 | tf_op jit(solution)/shard_map/concatenate | solution.py:21
  150.8 13.3 %shard_map.95 = f32[2,16,16384]{2,1,0:T(8,128)} custom-call(bf16[4,18,16640]{2,1,0:T(8,128)(2,1)} %pad_maximum_fusion.1.p_ref, f32[27,640]{1,0:T(8,128)} %tile.21.w_ref), custom_call_target="tpu_custom_call" | custom-call | tf_op jit(solution)/shard_map/pallas_call | solution.py:98
  165.5 8.2 %all_gather.7 = bf16[32,32,128]{2,1,0:T(8,128)(2,1)S(1)} all-gather(bf16[8,32,128]{2,1,0:T(8,128)(2,1)S(1)} %convolution_convert_fusion.1), channel_id=1, replica_groups=mesh['gx'=4,'gy'=2,'gz'=4] {'gx'}, dimensions={0}, use_global_device_ids=true | all-gather | bytes 327680 | tf_op jit(solution)/shard_map/all_gather | solution.py:114
  175.0 2.7 %copy.52 = f32[32,256,64]{2,1,0:T(8,128)} copy(f32[32,256,64]{1,2,0:T(8,128)S(1)} %add_bitcast_fusion) | data formatting | bytes 4194304 | tf_op jit(solution)/shard_map/add | solution.py:118
  177.7 2.9 %reshape.54 = f32[2,16,16384]{2,1,0:T(8,128)S(1)} reshape(f32[32,256,64]{2,1,0:T(8,128)} %copy.52) | data formatting | bytes 4194304 | tf_op jit(solution)/shard_map/reshape | solution.py:191
  181.6 2.7 %add_convert_fusion = bf16[2,16,16384]{2,1,0:T(8,128)(2,1)} fusion(f32[2,16,16384]{2,1,0:T(8,128)} %shard_map.95, f32[2,16,16384]{2,1,0:T(8,128)S(1)} %reshape.54), kind=kLoop, calls=%fused_computation.21 | loop fusion | flops 1048576 | bytes 5242880 | tf_op jit(solution)/shard_map/convert_element_type | solution.py:191
  184.4 54.6 %all-reduce.2.cloned.1.call-done = bf16[2,8,64,64]{3,2,1,0:T(8,128)(2,1)} async-done(((bf16[2,8,64,64]{3,2,1,0:T(8,128)(2,1)}), bf16[2,8,64,64]{3,2,1,0:T(8,128)(2,1)}) %all-reduce.2.cloned.1.call-update) | async-done | bytes 131088 | tf_op jit(solution)/shard_map/psum | solution.py:130
  239.0 1.8 convert_element_type.88
  (79 shorter events, 14.6 us)
Async XLA Ops:
  7.2 59.5 %copy-start = (bf16[64,256]{1,0:T(8,128)(2,1)S(1)}, bf16[64,256]{1,0:T(8,128)(2,1)}, u32[]{:S(2)}) copy-start(bf16[64,256]{1,0:T(8,128)(2,1)} %param.9) | copy-start | bytes 98308
  7.2 66.8 %reduce-scatter.3.cloned.1.call-start = ((), (), s32[]{:S(2)}) async-start(), calls=%async_computation.2 | async-start | bytes 655360 | tf_op jit(solution)/shard_map/reduce_scatter | solution.py:108
  7.9 6.9 %collective-permute-start = (bf16[2,16,128]{2,1,0:T(8,128)(2,1)S(1)}, bf16[2,16,128]{2,1,0:T(8,128)(2,1)S(1)}, u32[]{:S(2)}, u32[]{:S(2)}) collective-permute-start(bf16[2,16,128]{2,1,0:T(8,128)(2,1)S(1)} %get-tuple-element.16), channel_id=1, source_target_pairs={{0,8},{8,16},{16,24},{24,0},{1,9},{9,17},{17,25},{25,1},{2,10},{10... | collective-permute-start | bytes 24584 | tf_op jit(solution)/shard_map/ppermute | solution.py:19
  10.9 5.3 %collective-permute-start.1 = (bf16[2,16,128]{2,1,0:T(8,128)(2,1)S(1)}, bf16[2,16,128]{2,1,0:T(8,128)(2,1)S(1)}, u32[]{:S(2)}, u32[]{:S(2)}) collective-permute-start(bf16[2,16,128]{2,1,0:T(8,128)(2,1)S(1)} %get-tuple-element.15), channel_id=1, source_target_pairs={{8,0},{16,8},{24,16},{0,24},{9,1},{17,9},{25,17},{1,25},{10,2},{18... | collective-permute-start | bytes 24584 | tf_op jit(solution)/shard_map/ppermute | solution.py:20
  16.4 4.9 %collective-permute-start.3 = (bf16[2,1,16640]{2,1,0:T(2,128)(2,1)S(1)}, bf16[2,1,16640]{2,1,0:T(2,128)(2,1)S(1)}, u32[]{:S(2)}, u32[]{:S(2)}) collective-permute-start(bf16[2,1,16640]{2,1,0:T(2,128)(2,1)S(1)} %get-tuple-element.12), channel_id=1, source_target_pairs={{4,0},{5,1},{6,2},{7,3},{12,8},{13,9},{14,10},{15,11},{20,16},{21,... | collective-permute-start | bytes 199688 | tf_op jit(solution)/shard_map/ppermute | solution.py:20
  17.7 4.0 %collective-permute-start.2 = (bf16[2,1,16640]{2,1,0:T(2,128)(2,1)S(1)}, bf16[2,1,16640]{2,1,0:T(2,128)(2,1)S(1)}, u32[]{:S(2)}, u32[]{:S(2)}) collective-permute-start(bf16[2,1,16640]{2,1,0:T(2,128)(2,1)S(1)} %get-tuple-element.11), channel_id=1, source_target_pairs={{0,4},{1,5},{2,6},{3,7},{8,12},{9,13},{10,14},{11,15},{16,20},{17,... | collective-permute-start | bytes 199688 | tf_op jit(solution)/shard_map/ppermute | solution.py:19
  21.3 2.3 copy-start.7
  21.8 1.9 copy-start.9
  23.6 22.6 %collective-permute-start.5 = (bf16[1,18,16640]{2,1,0:T(8,128)(2,1)}, bf16[1,18,16640]{2,1,0:T(8,128)(2,1)}, u32[]{:S(2)}, u32[]{:S(2)}) collective-permute-start(bf16[1,18,16640]{2,1,0:T(8,128)(2,1)} %get-tuple-element.8), channel_id=1, source_target_pairs={{1,0},{2,1},{3,2},{5,4},{6,5},{7,6},{9,8},{10,9},{11,10},{13,12},{... | collective-permute-start | bytes 1797128 | tf_op jit(solution)/shard_map/ppermute | solution.py:20
  24.9 22.5 %collective-permute-start.4 = (bf16[1,18,16640]{2,1,0:T(8,128)(2,1)}, bf16[1,18,16640]{2,1,0:T(8,128)(2,1)}, u32[]{:S(2)}, u32[]{:S(2)}) collective-permute-start(bf16[1,18,16640]{2,1,0:T(8,128)(2,1)} %get-tuple-element.7), channel_id=1, source_target_pairs={{0,1},{1,2},{2,3},{4,5},{5,6},{6,7},{8,9},{9,10},{10,11},{12,13},{... | collective-permute-start | bytes 1797128 | tf_op jit(solution)/shard_map/ppermute | solution.py:19
  32.0 132.0 %reduce-scatter.5.cloned.1.call-start = ((), (), s32[]{:S(2)}) async-start(), calls=%async_computation.3 | async-start | bytes 655360 | tf_op jit(solution)/shard_map/reduce_scatter | solution.py:108
  36.3 3.9 %copy-start.6 = (bf16[32,64,64]{2,1,0:T(8,128)(2,1)S(1)}, bf16[32,64,64]{2,1,0:T(8,128)(2,1)}, u32[]{:S(2)}) copy-start(bf16[32,64,64]{2,1,0:T(8,128)(2,1)} %param.12) | copy-start | bytes 786436
  36.3 4.1 %copy-start.12 = (bf16[27,64]{1,0:T(8,128)(2,1)S(1)}, bf16[27,64]{1,0:T(8,128)(2,1)}, u32[]{:S(2)}) copy-start(bf16[27,64]{1,0:T(8,128)(2,1)} %param.8) | copy-start | bytes 10372
  36.3 4.9 %copy-start.11 = (bf16[32,64,64]{2,1,0:T(8,128)(2,1)S(1)}, bf16[32,64,64]{2,1,0:T(8,128)(2,1)}, u32[]{:S(2)}) copy-start(bf16[32,64,64]{2,1,0:T(8,128)(2,1)} %param.11) | copy-start | bytes 786436
  40.3 7.1 %copy-start.8 = (bf16[2,1,16640]{2,1,0:T(2,128)(2,1)S(1)}, bf16[2,1,16640]{2,1,0:T(2,128)(2,1)}, u32[]{:S(2)}) copy-start(bf16[2,1,16640]{2,1,0:T(2,128)(2,1)} %copy-done.7) | copy-start | bytes 199684
  40.3 7.1 %copy-start.10 = (bf16[2,1,16640]{2,1,0:T(2,128)(2,1)S(1)}, bf16[2,1,16640]{2,1,0:T(2,128)(2,1)}, u32[]{:S(2)}) copy-start(bf16[2,1,16640]{2,1,0:T(2,128)(2,1)} %copy-done.9) | copy-start | bytes 199684
  66.7 4.5 %copy-start.13 = (bf16[256,64]{0,1:T(8,128)(2,1)S(1)}, bf16[256,64]{0,1:T(8,128)(2,1)}, u32[]{:S(2)}) copy-start(bf16[256,64]{0,1:T(8,128)(2,1)} %param.10) | copy-start | bytes 98308
  67.9 3.3 %copy-start.2 = (f32[8192,256]{1,0:T(8,128)}, f32[8192,256]{1,0:T(8,128)S(1)}, u32[]{:S(2)}) copy-start(f32[8192,256]{1,0:T(8,128)S(1)} %fusion.93) | copy-start | bytes 25165828
  74.9 10.7 %copy-start.3 = (f32[32,256,64]{1,2,0:T(8,128)S(1)}, f32[32,256,64]{1,2,0:T(8,128)}, u32[]{:S(2)}) copy-start(f32[32,256,64]{1,2,0:T(8,128)} %copy.46) | copy-start | bytes 6291460
  88.3 0.8 copy-start.14
  103.1 4.5 %collective-permute-start.6 = (bf16[2,16,128]{2,1,0:T(8,128)(2,1)S(1)}, bf16[2,16,128]{2,1,0:T(8,128)(2,1)S(1)}, u32[]{:S(2)}, u32[]{:S(2)}) collective-permute-start(bf16[2,16,128]{2,1,0:T(8,128)(2,1)S(1)} %get-tuple-element.14), channel_id=1, source_target_pairs={{0,8},{8,16},{16,24},{24,0},{1,9},{9,17},{17,25},{25,1},{2,10},{10... | collective-permute-start | bytes 24584 | tf_op jit(solution)/shard_map/ppermute | solution.py:19
  103.2 5.7 %collective-permute-start.7 = (bf16[2,16,128]{2,1,0:T(8,128)(2,1)S(1)}, bf16[2,16,128]{2,1,0:T(8,128)(2,1)S(1)}, u32[]{:S(2)}, u32[]{:S(2)}) collective-permute-start(bf16[2,16,128]{2,1,0:T(8,128)(2,1)S(1)} %get-tuple-element.13), channel_id=1, source_target_pairs={{8,0},{16,8},{24,16},{0,24},{9,1},{17,9},{25,17},{1,25},{10,2},{18... | collective-permute-start | bytes 24584 | tf_op jit(solution)/shard_map/ppermute | solution.py:20
  108.9 1.0 copy-start.4
  110.8 10.9 %collective-permute-start.9 = (bf16[2,1,16640]{2,1,0:T(2,128)(2,1)}, bf16[2,1,16640]{2,1,0:T(2,128)(2,1)}, u32[]{:S(2)}, u32[]{:S(2)}) collective-permute-start(bf16[2,1,16640]{2,1,0:T(2,128)(2,1)} %get-tuple-element.10), channel_id=1, source_target_pairs={{4,0},{5,1},{6,2},{7,3},{12,8},{13,9},{14,10},{15,11},{20,16},{21,... | collective-permute-start | bytes 199688 | tf_op jit(solution)/shard_map/ppermute | solution.py:20
  112.1 9.6 %collective-permute-start.8 = (bf16[2,1,16640]{2,1,0:T(2,128)(2,1)}, bf16[2,1,16640]{2,1,0:T(2,128)(2,1)}, u32[]{:S(2)}, u32[]{:S(2)}) collective-permute-start(bf16[2,1,16640]{2,1,0:T(2,128)(2,1)} %get-tuple-element.9), channel_id=1, source_target_pairs={{0,4},{1,5},{2,6},{3,7},{8,12},{9,13},{10,14},{11,15},{16,20},{17,... | collective-permute-start | bytes 199688 | tf_op jit(solution)/shard_map/ppermute | solution.py:19
  124.9 21.4 %collective-permute-start.11 = (bf16[1,18,16640]{2,1,0:T(8,128)(2,1)}, bf16[1,18,16640]{2,1,0:T(8,128)(2,1)}, u32[]{:S(2)}, u32[]{:S(2)}) collective-permute-start(bf16[1,18,16640]{2,1,0:T(8,128)(2,1)} %get-tuple-element.6), channel_id=1, source_target_pairs={{1,0},{2,1},{3,2},{5,4},{6,5},{7,6},{9,8},{10,9},{11,10},{13,12},{... | collective-permute-start | bytes 1797128 | tf_op jit(solution)/shard_map/ppermute | solution.py:20
  126.2 21.3 %collective-permute-start.10 = (bf16[1,18,16640]{2,1,0:T(8,128)(2,1)}, bf16[1,18,16640]{2,1,0:T(8,128)(2,1)}, u32[]{:S(2)}, u32[]{:S(2)}) collective-permute-start(bf16[1,18,16640]{2,1,0:T(8,128)(2,1)} %get-tuple-element.5), channel_id=1, source_target_pairs={{0,1},{1,2},{2,3},{4,5},{5,6},{6,7},{8,9},{9,10},{10,11},{12,13},{... | collective-permute-start | bytes 1797128 | tf_op jit(solution)/shard_map/ppermute | solution.py:19
  132.7 14.7 %copy-start.5 = (bf16[2,16,16640]{2,1,0:T(8,128)(2,1)S(1)}, bf16[2,16,16640]{2,1,0:T(8,128)(2,1)}, u32[]{:S(2)}) copy-start(bf16[2,16,16640]{2,1,0:T(8,128)(2,1)} %copy-done.4) | copy-start | bytes 3194884
  134.4 104.6 %all-reduce.2.cloned.1.call-start = ((), (), s32[]{:S(2)}) async-start(), calls=%async_computation.4 | async-start | bytes 524288 | tf_op jit(solution)/shard_map/psum | solution.py:130
  181.6 59.2 %copy-start.1 = (bf16[64,256]{1,0:T(8,128)(2,1)S(1)}, bf16[64,256]{1,0:T(8,128)(2,1)}, u32[]{:S(2)}) copy-start(bf16[64,256]{1,0:T(8,128)(2,1)} %param.9) | copy-start | bytes 98308
Sparse Core Ops, SparseCore 0:
  32.1 24.5 reduce-scatter.2
  134.5 24.5 reduce-scatter.4
  181.7 57.1 all-reduce.1

commit v2 on v1

--- a/solution.py
+++ b/solution.py
@@ -28,18 +28,43 @@
     return (values * normal_cdf, normal_cdf + values * density)
 
 
-def dft_tables(offset, cells, x_length, mode_count):
+def dft_tables(offset, cells, x_length, frequency):
     position = offset + jnp.arange(cells, dtype=jnp.int32)
-    frequency = jnp.arange(mode_count, dtype=jnp.int32)
     phase_int = position[:, None] * frequency[None, :] % x_length
     angles = phase_int.astype(jnp.float32) * (2.0 * math.pi / x_length)
     return (jnp.cos(angles).astype(jnp.bfloat16), (-jnp.sin(angles)).astype(jnp.bfloat16))
 
 
-def scaled_table(table, mode_count, x_length):
-    frequency = jnp.arange(mode_count, dtype=jnp.int32)
+def scaled_table(table, frequency, x_length):
     mode_scale = jnp.where(frequency == 0, 1.0, 2.0).astype(jnp.float32) / x_length
     return (table.astype(jnp.float32) * mode_scale[None, :]).astype(jnp.bfloat16)
+
+
+def gathered_order(axis, share_size):
+    size = lax.axis_size(axis)
+    shifts = jnp.arange(size, dtype=jnp.int32)
+    sources = (lax.axis_index(axis) - shifts) % size
+    local = jnp.arange(share_size, dtype=jnp.int32)
+    return (sources[:, None] * share_size + local[None, :]).reshape(-1)
+
+
+def ring_gather(block, axis):
+    size = lax.axis_size(axis)
+    pieces = [block]
+    for shift in range(1, size):
+        pieces.append(lax.ppermute(block, axis, [(i, (i + shift) % size) for i in range(size)]))
+    return jnp.concatenate(pieces, axis=0)
+
+
+def butterfly_sum(value, axis):
+    size = lax.axis_size(axis)
+    if size & (size - 1):
+        return lax.psum(value, axis)
+    step = 1
+    while step < size:
+        value = value + lax.ppermute(value, axis, [(i, i ^ step) for i in range(size)])
+        step *= 2
+    return value
 
 
 def block_weights(spec_real, spec_imag):
@@ -111,7 +136,7 @@
 
 
 def share_inverse(modes_share, cos_table, sin_table, channels):
-    segment = lax.all_gather(modes_share, "gx", axis=0, tiled=True)
+    segment = ring_gather(modes_share, "gx")
     running = jnp.einsum(
         "krc,xk->rxc", segment[:, :, :channels], cos_table, preferred_element_type=jnp.float32
     )
@@ -127,7 +152,7 @@
 
 
 def sum_gradients(local_grads):
-    return lax.psum(local_grads.astype(jnp.bfloat16), ("gy", "gz")).astype(jnp.float32)
+    return butterfly_sum(butterfly_sum(local_grads, "gy"), "gz")
 
 
 def per_device(
@@ -141,9 +166,16 @@
     group_size = lax.axis_size("gx")
     x_length = x_cells * group_size
     x_start = lax.axis_index("gx") * x_cells
-    cos_part, sin_part = dft_tables(x_start, x_cells, x_length, mode_count)
-    cos_scaled = scaled_table(cos_part, mode_count, x_length)
-    sin_scaled = scaled_table(sin_part, mode_count, x_length)
+    share_size = mode_count // group_size
+    cos_part, sin_part = dft_tables(
+        x_start, x_cells, x_length, jnp.arange(mode_count, dtype=jnp.int32)
+    )
+    order = gathered_order("gx", share_size)
+    cos_order, sin_order = dft_tables(x_start, x_cells, x_length, order)
+    cos_scaled = scaled_table(cos_order, order, x_length)
+    sin_scaled = scaled_table(sin_order, order, x_length)
+    cos_fwd_scaled = scaled_table(cos_part, jnp.arange(mode_count, dtype=jnp.int32), x_length)
+    sin_fwd_scaled = scaled_table(sin_part, jnp.arange(mode_count, dtype=jnp.int32), x_length)
     blocks = block_weights(spec_real, spec_imag)
     padded = spatial_rims(features, channels)
     activation = depthwise(padded, depth_weight, False, x_cells, channels, jnp.bfloat16)
@@ -155,7 +187,6 @@
     )
     local_branch = local_branch.reshape(row_count, x_cells, channels)
     field3 = features.reshape(row_count, x_cells, channels)
-    share_size = mode_count // group_size
     owned_blocks = lax.dynamic_slice_in_dim(
         blocks, lax.axis_index("gx") * share_size, share_size, 0
     )
@@ -179,11 +210,11 @@
         jnp.bfloat16
     )
     grad_act = grad_act.reshape(planes, y_cells, merged)
-    dcoef = share_terms(grad_pre, cos_scaled, sin_scaled).astype(jnp.bfloat16)
+    dcoef = share_terms(grad_pre, cos_fwd_scaled, sin_fwd_scaled).astype(jnp.bfloat16)
     dmode = jnp.einsum(
         "kro,kco->krc", dcoef, owned_blocks, preferred_element_type=jnp.float32
     ).astype(jnp.bfloat16)
-    spectral_grad = share_inverse(dmode, cos_part, sin_part, channels)
+    spectral_grad = share_inverse(dmode, cos_order, sin_order, channels)
     dblock = jnp.einsum("krc,kro->kco", coeffs, dcoef, preferred_element_type=jnp.float32)
     grad_spec = sum_gradients(split_gradients(dblock, channels))
     padded_grad = spatial_rims(grad_act, channels)

time: 248 us -> 220 us (0.89); the launches traced: 247 us -> 216 us
  waiting for transfers between devices: 75.6 us -> 47.4 us
  blocking collectives: 18 us -> 0 us
  starting transfers between devices: 31.1 us -> 43.4 us
  matrix products: 20.2 us -> 25.9 us
  local copies, waits for them, and re-layouts: 43.5 us -> 40.1 us
    psum x1 -> x0, waiting for transfers between devices: 54.6 us -> none  [sum_gradients(): lax.psum(local_grads.astype(jnp.bfloat16), ('gy', 'gz')).astype(jnp.float32)]
    ppermute x0 -> x9, waiting for transfers between devices: none -> 25.7 us  [the longest x3 21.5 us: butterfly_sum(): lax.ppermute(value, axis, [(i, i ^ step) for i in range(size)])]
    all_gather x2 -> x0, blocking collectives: 18 us -> none  [share_inverse(): segment = lax.all_gather(modes_share, 'gx', axis=0, tiled=True)]
    ppermute x0 -> x9, starting transfers between devices: none -> 12.5 us  [the longest x3 6.36 us: butterfly_sum(): lax.ppermute(value, axis, [(i, i ^ step) for i in range(size)])]
    dot_general x1, matrix products: 1.23 us -> 4.5 us  [per_device(): jnp.dot(activation, expand_weight, preferred_element_type=jnp.float32)]
    add x0 -> x4, other arithmetic: none -> 2.92 us  [the longest x3 2.85 us: butterfly_sum(): value + lax.ppermute(value, axis, [(i, i ^ step) for i in range(size)])]
    unnamed x34 -> x30, local copies, waits for them, and re-layouts: 7.58 us -> 5.23 us
  transfers between devices with their start and end apart: 15 -> 23, of which waited for: 7 -> 10; matrix products, arithmetic and copies ran while one was open for 17% -> 25% of each run, Pallas kernels for 11% -> 12%
where the time goes in v2:
time: 220 us; the launch traced here: 216 us
  waiting for transfers between devices  47.4 us (22%)
  starting transfers between devices  43.4 us (20%)
  local copies, waits for them, and re-layouts  40.1 us (18%)
  Pallas kernels  26.2 us (12%)
  matrix products  25.9 us (12%)
  other arithmetic  18.7 us (8%)
  between operations  14.4 us (7%)
    pallas_call x2, Pallas kernels, depthwise(): pl.pallas_call(kernel, out_shape=jax.ShapeDtypeStruct((planes, y_cells, l...  26.2 us
    ppermute x6, starting transfers between devices, padded_2(): before = lax.ppermute(last, axis, up)  23.2 us
    ppermute x3, waiting for transfers between devices, butterfly_sum(): lax.ppermute(value, axis, [(i, i ^ step) for i in range(size)])  21.5 us
    ppermute x6, waiting for transfers between devices, padded_2(): after = lax.ppermute(leading, axis, down)  17.5 us
    concatenate x4, other arithmetic, padded_2(): value = jnp.concatenate([before, value, after], axis=dim)  8.99 us
    dot_general x1, matrix products, per_device(): jnp.dot(grad_hidden, expand_weight.T, preferred_element_type=jnp.float32)  8.79 us
    ppermute x6, starting transfers between devices, padded_2(): after = lax.ppermute(leading, axis, down)  7.52 us
    convert_element_type x2, local copies, waits for them, and re-layouts, per_device(): cotangent.reshape(row_count, x_cells, channels).astype(jnp.float32) * slopes  7.1 us
  transfers between devices with their start and end apart: 23, of which 10 were waited for; matrix products, arithmetic and copies ran while one was open for 25% of the time, Pallas kernels for 12%

profile of v2, /device:TPU:0, one launch (start us, length us, event | category | flops | bytes accessed | tf_op | source)
XLA Modules:
  0.0 216.1 jit_solution(14560766009410046266)
XLA Ops:
  7.9 2.9 %collective-permute-start = (bf16[2,16,128]{2,1,0:T(8,128)(2,1)S(1)}, bf16[2,16,128]{2,1,0:T(8,128)(2,1)S(1)}, u32[]{:S(2)}, u32[]{:S(2)}) collective-permute-start(bf16[2,16,128]{2,1,0:T(8,128)(2,1)S(1)} %get-tuple-element.16), channel_id=1, source_target_pairs={{0,8},{8,16},{16,24},{24,0},{1,9},{9,17},{17,25},{25,1},{2,10},{10... | collective-permute-start | bytes 24584 | tf_op jit(solution)/shard_map/ppermute | solution.py:19
  11.8 3.0 %reshape.93 = bf16[32,256,64]{2,1,0:T(8,128)(2,1)S(1)} reshape(bf16[2,16,16384]{2,1,0:T(8,128)(2,1)} %param.7) | data formatting | bytes 2097152 | tf_op jit(solution)/shard_map/reshape | solution.py:189
  16.4 1.3 collective-permute-start.3
  17.7 3.0 %collective-permute-start.2 = (bf16[2,1,16640]{2,1,0:T(2,128)(2,1)S(1)}, bf16[2,1,16640]{2,1,0:T(2,128)(2,1)S(1)}, u32[]{:S(2)}, u32[]{:S(2)}) collective-permute-start(bf16[2,1,16640]{2,1,0:T(2,128)(2,1)S(1)} %get-tuple-element.11), channel_id=1, source_target_pairs={{0,4},{1,5},{2,6},{3,7},{8,12},{9,13},{10,14},{11,15},{16,20},{17,... | collective-permute-start | bytes 199688 | tf_op jit(solution)/shard_map/ppermute | solution.py:19
  23.8 1.3 fusion.97
  25.1 1.3 collective-permute-start.5
  26.4 5.5 %collective-permute-start.4 = (bf16[1,18,16640]{2,1,0:T(8,128)(2,1)}, bf16[1,18,16640]{2,1,0:T(8,128)(2,1)}, u32[]{:S(2)}, u32[]{:S(2)}) collective-permute-start(bf16[1,18,16640]{2,1,0:T(8,128)(2,1)} %get-tuple-element.7), channel_id=1, source_target_pairs={{0,1},{1,2},{2,3},{4,5},{5,6},{6,7},{8,9},{9,10},{10,11},{12,13},{... | collective-permute-start | bytes 1797128 | tf_op jit(solution)/shard_map/ppermute | solution.py:19
  31.9 3.2 %reshape.98 = f32[32,256,64]{2,1,0:T(8,128)} reshape(bf16[2,16,16384]{2,1,0:T(8,128)(2,1)S(1)} %copy-done.8) | data formatting | bytes 3145728 | tf_op jit(solution)/shard_map/convert_element_type | solution.py:201
  35.1 3.9 %copy.30 = f32[32,256,64]{1,2,0:T(8,128)} copy(f32[32,256,64]{2,1,0:T(8,128)} %reshape.98) | data formatting | bytes 4194304 | tf_op jit(solution)/shard_map/convert_element_type | solution.py:201
  41.2 5.6 %collective-permute-done.5 = bf16[1,18,16640]{2,1,0:T(8,128)(2,1)S(1)} collective-permute-done((bf16[1,18,16640]{2,1,0:T(8,128)(2,1)}, bf16[1,18,16640]{2,1,0:T(8,128)(2,1)S(1)}, u32[]{:S(2)}, u32[]{:S(2)}) %collective-permute-start.5) | collective-permute-done | bytes 599072 | tf_op jit(solution)/shard_map/ppermute | solution.py:20
  46.8 1.3 collective-permute-done.4
  48.1 3.2 %pad_maximum_fusion.p_ref = bf16[4,18,16640]{2,1,0:T(8,128)(2,1)} fusion(bf16[1,18,16640]{2,1,0:T(8,128)(2,1)S(1)} %collective-permute-done.5, bf16[2,1,16640]{2,1,0:T(2,128)(2,1)} %copy-done.9, bf16[2,16,16640]{2,1,0:T(8,128)(2,1)S(1)} %constant_dynamic-update-slice_fusion, bf16[2,1,16640]{2,1,0:T(2,128)(2,1)} %copy-done.10, ...), kind=kLoop, calls=%fused_computation.11 | loop fusion | flops 11980800 | bytes 4792320 | tf_op jit(solution)/shard_map/concatenate | solution.py:21
  51.2 12.9 %shard_map.94 = bf16[2,16,16384]{2,1,0:T(8,128)(2,1)} custom-call(bf16[4,18,16640]{2,1,0:T(8,128)(2,1)} %pad_maximum_fusion.p_ref, f32[27,640]{1,0:T(8,128)} %tile.9.w_ref), custom_call_target="tpu_custom_call" | custom-call | tf_op jit(solution)/shard_map/pallas_call | solution.py:123
  64.1 3.0 %reshape.91 = bf16[8192,64]{1,0:T(8,128)(2,1)S(1)} reshape(bf16[2,16,16384]{2,1,0:T(8,128)(2,1)} %shard_map.94) | data formatting | bytes 2097152 | tf_op jit(solution)/shard_map/reshape | solution.py:182
  67.2 4.5 %fusion.104 = f32[8192,256]{1,0:T(8,128)} fusion(bf16[8192,64]{1,0:T(8,128)(2,1)S(1)} %reshape.91, bf16[64,256]{1,0:T(8,128)(2,1)S(1)} %copy-done), kind=kOutput, calls=%fused_computation.157 | convolution fusion | flops 268435456 | bytes 9469952 | tf_op jit(solution)/shard_map/dot_general | solution.py:183
  72.8 1.8 collective-permute-start.8
  75.0 1.5 collective-permute-start.6
  76.5 5.1 %fusion.5 = f32[8192,64]{0,1:T(8,128)S(1)} fusion(bf16[256,64]{0,1:T(8,128)(2,1)} %param.10, f32[8192,256]{1,0:T(8,128)} %fusion.104), kind=kOutput, calls=%fused_computation.10 | convolution fusion | flops 278921216 | bytes 10518528 | tf_op jit(solution)/shard_map/dot_general | solution.py:185
  83.2 2.7 %fusion.11 = (bf16[32,256,64]{1,2,0:T(8,128)(2,1)S(1)}, bf16[32,256,64]{1,2,0:T(8,128)(2,1)}) fusion(f32[32,256,64]{1,2,0:T(8,128)S(1)} %copy-done.2, f32[256,32,64]{0,2,1:T(8,128)S(1)} %fusion.20, bf16[32,32,64]{2,1,0:T(8,128)(2,1)S(1)} %get-tuple-element.21, f32[32]{0:T(128)S(1)} %get-tuple-element.23, s32[32]{0:T(128)S(1)} %add.119, ...), kind=kOutput, calls=%fused_computation.19 | convolution fusion | flops 41041920 | bytes 8520960 | tf_op jit(solution)/shard_map/krc,xk->rxc/dot_general | solution.py:140
  86.6 8.8 %convolution_convert_fusion = bf16[8192,64]{0,1:T(8,128)(2,1)} fusion(bf16[64,256]{1,0:T(8,128)(2,1)S(1)} %copy-done, bf16[8192,64]{0,1:T(8,128)(2,1)S(1)} %bitcast.53, bf16[256,64]{0,1:T(8,128)(2,1)S(1)} %copy-done.12, f32[8192,256]{1,0:T(8,128)} %fusion.104), kind=kOutput, calls=%fused_computation.3 | convolution fusion | flops 558366720 | bytes 10551296 | tf_op jit(solution)/shard_map/dot_general | solution.py:209
  95.4 2.0 copy.32
  97.5 2.5 %reshape.96 = bf16[2,16,16384]{2,1,0:T(8,128)(2,1)} reshape(bf16[8192,64]{1,0:T(8,128)(2,1)S(1)} %copy.32) | data formatting | bytes 2097152 | tf_op jit(solution)/shard_map/reshape | solution.py:212
  100.7 1.5 collective-permute-start.9
  102.2 1.4 collective-permute-start.10
  103.6 1.6 collective-permute-done.9
  105.2 1.3 constant_dynamic-update-slice_fusion.4
  108.5 1.3 collective-permute-start.12
  109.7 4.3 %collective-permute-start.11 = (bf16[2,1,16640]{2,1,0:T(2,128)(2,1)}, bf16[2,1,16640]{2,1,0:T(2,128)(2,1)}, u32[]{:S(2)}, u32[]{:S(2)}) collective-permute-start(bf16[2,1,16640]{2,1,0:T(2,128)(2,1)} %get-tuple-element.9), channel_id=1, source_target_pairs={{0,4},{1,5},{2,6},{3,7},{8,12},{9,13},{10,14},{11,15},{16,20},{17,... | collective-permute-start | bytes 199688 | tf_op jit(solution)/shard_map/ppermute | solution.py:19
  114.9 2.0 copy.29
  116.9 2.5 %reshape.94 = bf16[2,16,16384]{2,1,0:T(8,128)(2,1)} reshape(bf16[32,256,64]{2,1,0:T(8,128)(2,1)S(1)} %copy.29) | data formatting | bytes 2097152 | tf_op jit(solution)/shard_map/reshape | solution.py:199
  119.4 1.9 pad_maximum_fusion.3
  121.3 1.3 fusion.96
  122.6 1.3 collective-permute-start.14
  123.8 5.9 %collective-permute-start.13 = (bf16[1,18,16640]{2,1,0:T(8,128)(2,1)}, bf16[1,18,16640]{2,1,0:T(8,128)(2,1)}, u32[]{:S(2)}, u32[]{:S(2)}) collective-permute-start(bf16[1,18,16640]{2,1,0:T(8,128)(2,1)} %get-tuple-element.5), channel_id=1, source_target_pairs={{0,1},{1,2},{2,3},{4,5},{5,6},{6,7},{8,9},{9,10},{10,11},{12,13},{... | collective-permute-start | bytes 1797128 | tf_op jit(solution)/shard_map/ppermute | solution.py:19
  132.1 11.9 %collective-permute-done.14 = bf16[1,18,16640]{2,1,0:T(8,128)(2,1)} collective-permute-done((bf16[1,18,16640]{2,1,0:T(8,128)(2,1)}, bf16[1,18,16640]{2,1,0:T(8,128)(2,1)}, u32[]{:S(2)}, u32[]{:S(2)}) %collective-permute-start.14) | collective-permute-done | bytes 599072 | tf_op jit(solution)/shard_map/ppermute | solution.py:20
  145.1 3.3 %pad_maximum_fusion.1.p_ref = bf16[4,18,16640]{2,1,0:T(8,128)(2,1)} fusion(bf16[1,18,16640]{2,1,0:T(8,128)(2,1)} %collective-permute-done.14, bf16[2,1,16640]{2,1,0:T(2,128)(2,1)} %collective-permute-done.12, bf16[2,16,16640]{2,1,0:T(8,128)(2,1)S(1)} %copy-done.5, bf16[2,1,16640]{2,1,0:T(2,128)(2,1)} %collective-permute-done.11, ...), kind=kLoop, calls=%fused_computation.12 | loop fusion | flops 11980800 | bytes 4792320 | tf_op jit(solution)/shard_map/concatenate | solution.py:21
  148.4 13.3 %shard_map.95 = f32[2,16,16384]{2,1,0:T(8,128)} custom-call(bf16[4,18,16640]{2,1,0:T(8,128)(2,1)} %pad_maximum_fusion.1.p_ref, f32[27,640]{1,0:T(8,128)} %tile.21.w_ref), custom_call_target="tpu_custom_call" | custom-call | tf_op jit(solution)/shard_map/pallas_call | solution.py:123
  162.9 1.6 collective-permute-start.17
  165.9 1.3 collective-permute-done.17
  167.2 1.5 collective-permute-done.16
  168.8 1.3 collective-permute-done.15
  171.8 2.5 %collective-permute-start.19 = (f32[2,8,64,64]{3,2,1,0:T(8,128)}, f32[2,8,64,64]{3,2,1,0:T(8,128)}, u32[]{:S(2)}, u32[]{:S(2)}) collective-permute-start(f32[2,8,64,64]{3,2,1,0:T(8,128)} %fusion.95), channel_id=1, source_target_pairs={{0,1},{1,0},{2,3},{3,2},{4,5},{5,4},{6,7},{7,6},{8,9},{9,8},{10,11... | collective-permute-start | bytes 786440 | tf_op jit(solution)/shard_map/ppermute | solution.py:65
  174.9 2.7 %copy.36 = f32[32,256,64]{2,1,0:T(8,128)} copy(f32[32,256,64]{1,2,0:T(8,128)S(1)} %add_bitcast_fusion) | data formatting | bytes 4194304 | tf_op jit(solution)/shard_map/add | solution.py:143
  177.6 2.9 %reshape.97 = f32[2,16,16384]{2,1,0:T(8,128)S(1)} reshape(f32[32,256,64]{2,1,0:T(8,128)} %copy.36) | data formatting | bytes 4194304 | tf_op jit(solution)/shard_map/reshape | solution.py:222
  180.6 3.1 %collective-permute-done.19 = f32[2,8,64,64]{3,2,1,0:T(8,128)} collective-permute-done((f32[2,8,64,64]{3,2,1,0:T(8,128)}, f32[2,8,64,64]{3,2,1,0:T(8,128)}, u32[]{:S(2)}, u32[]{:S(2)}) %collective-permute-start.19) | collective-permute-done | bytes 262176 | tf_op jit(solution)/shard_map/ppermute | solution.py:65
  184.8 3.8 %collective-permute-start.20 = (f32[2,8,64,64]{3,2,1,0:T(8,128)S(1)}, f32[2,8,64,64]{3,2,1,0:T(8,128)S(1)}, u32[]{:S(2)}, u32[]{:S(2)}) collective-permute-start(f32[2,8,64,64]{3,2,1,0:T(8,128)S(1)} %fusion.117), channel_id=1, source_target_pairs={{0,2},{1,3},{2,0},{3,1},{4,6},{5,7},{6,4},{7,5},{8,10},{9,11},{10,... | collective-permute-start | bytes 786440 | tf_op jit(solution)/shard_map/ppermute | solution.py:65
  188.6 1.3 add_convert_fusion
  189.9 18.4 %collective-permute-done.20 = f32[2,8,64,64]{3,2,1,0:T(8,128)S(1)} collective-permute-done((f32[2,8,64,64]{3,2,1,0:T(8,128)S(1)}, f32[2,8,64,64]{3,2,1,0:T(8,128)S(1)}, u32[]{:S(2)}, u32[]{:S(2)}) %collective-permute-start.20) | collective-permute-done | bytes 262176 | tf_op jit(solution)/shard_map/ppermute | solution.py:65
  (95 shorter events, 26.0 us)
Async XLA Ops:
  7.2 60.0 %copy-start = (bf16[64,256]{1,0:T(8,128)(2,1)S(1)}, bf16[64,256]{1,0:T(8,128)(2,1)}, u32[]{:S(2)}) copy-start(bf16[64,256]{1,0:T(8,128)(2,1)} %param.9) | copy-start | bytes 98308
  7.2 64.5 %reduce-scatter.3.cloned.1.call-start = ((), (), s32[]{:S(2)}) async-start(), calls=%async_computation.2 | async-start | bytes 655360 | tf_op jit(solution)/shard_map/reduce_scatter | solution.py:133
  7.9 8.1 %collective-permute-start = (bf16[2,16,128]{2,1,0:T(8,128)(2,1)S(1)}, bf16[2,16,128]{2,1,0:T(8,128)(2,1)S(1)}, u32[]{:S(2)}, u32[]{:S(2)}) collective-permute-start(bf16[2,16,128]{2,1,0:T(8,128)(2,1)S(1)} %get-tuple-element.16), channel_id=1, source_target_pairs={{0,8},{8,16},{16,24},{24,0},{1,9},{9,17},{17,25},{25,1},{2,10},{10... | collective-permute-start | bytes 24584 | tf_op jit(solution)/shard_map/ppermute | solution.py:19
  10.9 5.3 %collective-permute-start.1 = (bf16[2,16,128]{2,1,0:T(8,128)(2,1)S(1)}, bf16[2,16,128]{2,1,0:T(8,128)(2,1)S(1)}, u32[]{:S(2)}, u32[]{:S(2)}) collective-permute-start(bf16[2,16,128]{2,1,0:T(8,128)(2,1)S(1)} %get-tuple-element.15), channel_id=1, source_target_pairs={{8,0},{16,8},{24,16},{0,24},{9,1},{17,9},{25,17},{1,25},{10,2},{18... | collective-permute-start | bytes 24584 | tf_op jit(solution)/shard_map/ppermute | solution.py:20
  14.9 1.2 copy-start.6
  16.4 5.4 %collective-permute-start.3 = (bf16[2,1,16640]{2,1,0:T(2,128)(2,1)S(1)}, bf16[2,1,16640]{2,1,0:T(2,128)(2,1)S(1)}, u32[]{:S(2)}, u32[]{:S(2)}) collective-permute-start(bf16[2,1,16640]{2,1,0:T(2,128)(2,1)S(1)} %get-tuple-element.12), channel_id=1, source_target_pairs={{4,0},{5,1},{6,2},{7,3},{12,8},{13,9},{14,10},{15,11},{20,16},{21,... | collective-permute-start | bytes 199688 | tf_op jit(solution)/shard_map/ppermute | solution.py:20
  17.7 4.1 %collective-permute-start.2 = (bf16[2,1,16640]{2,1,0:T(2,128)(2,1)S(1)}, bf16[2,1,16640]{2,1,0:T(2,128)(2,1)S(1)}, u32[]{:S(2)}, u32[]{:S(2)}) collective-permute-start(bf16[2,1,16640]{2,1,0:T(2,128)(2,1)S(1)} %get-tuple-element.11), channel_id=1, source_target_pairs={{0,4},{1,5},{2,6},{3,7},{8,12},{9,13},{10,14},{11,15},{16,20},{17,... | collective-permute-start | bytes 199688 | tf_op jit(solution)/shard_map/ppermute | solution.py:19
  21.8 139.9 %reduce-scatter.5.cloned.1.call-start = ((), (), s32[]{:S(2)}) async-start(), calls=%async_computation.3 | async-start | bytes 655360 | tf_op jit(solution)/shard_map/reduce_scatter | solution.py:133
  21.9 0.7 copy-start.9
  22.5 0.7 copy-start.10
  23.8 8.1 %copy-start.8 = (bf16[2,16,16384]{2,1,0:T(8,128)(2,1)S(1)}, bf16[2,16,16384]{2,1,0:T(8,128)(2,1)}, u32[]{:S(2)}) copy-start(bf16[2,16,16384]{2,1,0:T(8,128)(2,1)} %param.13) | copy-start | bytes 3145732
  25.1 21.7 %collective-permute-start.5 = (bf16[1,18,16640]{2,1,0:T(8,128)(2,1)}, bf16[1,18,16640]{2,1,0:T(8,128)(2,1)S(1)}, u32[]{:S(2)}, u32[]{:S(2)}) collective-permute-start(bf16[1,18,16640]{2,1,0:T(8,128)(2,1)} %get-tuple-element.8), channel_id=1, source_target_pairs={{1,0},{2,1},{3,2},{5,4},{6,5},{7,6},{9,8},{10,9},{11,10},{13,12},{... | collective-permute-start | bytes 1797128 | tf_op jit(solution)/shard_map/ppermute | solution.py:20
  26.4 21.7 %collective-permute-start.4 = (bf16[1,18,16640]{2,1,0:T(8,128)(2,1)}, bf16[1,18,16640]{2,1,0:T(8,128)(2,1)}, u32[]{:S(2)}, u32[]{:S(2)}) collective-permute-start(bf16[1,18,16640]{2,1,0:T(8,128)(2,1)} %get-tuple-element.7), channel_id=1, source_target_pairs={{0,1},{1,2},{2,3},{4,5},{5,6},{6,7},{8,9},{9,10},{10,11},{12,13},{... | collective-permute-start | bytes 1797128 | tf_op jit(solution)/shard_map/ppermute | solution.py:19
  35.1 3.9 %copy-start.7 = (bf16[32,64,64]{2,1,0:T(8,128)(2,1)S(1)}, bf16[32,64,64]{2,1,0:T(8,128)(2,1)}, u32[]{:S(2)}) copy-start(bf16[32,64,64]{2,1,0:T(8,128)(2,1)} %param.12) | copy-start | bytes 786436
  35.1 4.2 %copy-start.11 = (bf16[27,64]{1,0:T(8,128)(2,1)S(1)}, bf16[27,64]{1,0:T(8,128)(2,1)}, u32[]{:S(2)}) copy-start(bf16[27,64]{1,0:T(8,128)(2,1)} %param.8) | copy-start | bytes 10372
  72.8 8.9 %collective-permute-start.8 = (bf16[8,32,128]{2,1,0:T(8,128)(2,1)S(1)}, bf16[8,32,128]{2,1,0:T(8,128)(2,1)S(1)}, u32[]{:S(2)}, u32[]{:S(2)}) collective-permute-start(bf16[8,32,128]{2,1,0:T(8,128)(2,1)S(1)} %convolution_convert_fusion.2), channel_id=1, source_target_pairs={{0,24},{8,0},{16,8},{24,16},{1,25},{9,1},{17,9},{25,17},{2,26},{10... | collective-permute-start | bytes 196616 | tf_op jit(solution)/shard_map/ppermute | solution.py:55
  74.5 7.1 %collective-permute-start.7 = (bf16[8,32,128]{2,1,0:T(8,128)(2,1)S(1)}, bf16[8,32,128]{2,1,0:T(8,128)(2,1)S(1)}, u32[]{:S(2)}, u32[]{:S(2)}) collective-permute-start(bf16[8,32,128]{2,1,0:T(8,128)(2,1)S(1)} %convolution_convert_fusion.2), channel_id=1, source_target_pairs={{0,16},{8,24},{16,0},{24,8},{1,17},{9,25},{17,1},{25,9},{2,18},{10... | collective-permute-start | bytes 196616 | tf_op jit(solution)/shard_map/ppermute | solution.py:55
  75.0 6.6 %collective-permute-start.6 = (bf16[8,32,128]{2,1,0:T(8,128)(2,1)S(1)}, bf16[8,32,128]{2,1,0:T(8,128)(2,1)S(1)}, u32[]{:S(2)}, u32[]{:S(2)}) collective-permute-start(bf16[8,32,128]{2,1,0:T(8,128)(2,1)S(1)} %convolution_convert_fusion.2), channel_id=1, source_target_pairs={{0,8},{8,16},{16,24},{24,0},{1,9},{9,17},{17,25},{25,1},{2,10},{10... | collective-permute-start | bytes 196616 | tf_op jit(solution)/shard_map/ppermute | solution.py:55
  81.6 1.6 copy-start.2
  85.9 0.8 copy-start.12
  100.7 4.5 %collective-permute-start.9 = (bf16[2,16,128]{2,1,0:T(8,128)(2,1)S(1)}, bf16[2,16,128]{2,1,0:T(8,128)(2,1)S(1)}, u32[]{:S(2)}, u32[]{:S(2)}) collective-permute-start(bf16[2,16,128]{2,1,0:T(8,128)(2,1)S(1)} %get-tuple-element.14), channel_id=1, source_target_pairs={{0,8},{8,16},{16,24},{24,0},{1,9},{9,17},{17,25},{25,1},{2,10},{10... | collective-permute-start | bytes 24584 | tf_op jit(solution)/shard_map/ppermute | solution.py:19
  102.2 4.4 %collective-permute-start.10 = (bf16[2,16,128]{2,1,0:T(8,128)(2,1)S(1)}, bf16[2,16,128]{2,1,0:T(8,128)(2,1)S(1)}, u32[]{:S(2)}, u32[]{:S(2)}) collective-permute-start(bf16[2,16,128]{2,1,0:T(8,128)(2,1)S(1)} %get-tuple-element.13), channel_id=1, source_target_pairs={{8,0},{16,8},{24,16},{0,24},{9,1},{17,9},{25,17},{1,25},{10,2},{18... | collective-permute-start | bytes 24584 | tf_op jit(solution)/shard_map/ppermute | solution.py:20
  106.5 1.0 copy-start.4
  108.5 10.9 %collective-permute-start.12 = (bf16[2,1,16640]{2,1,0:T(2,128)(2,1)}, bf16[2,1,16640]{2,1,0:T(2,128)(2,1)}, u32[]{:S(2)}, u32[]{:S(2)}) collective-permute-start(bf16[2,1,16640]{2,1,0:T(2,128)(2,1)} %get-tuple-element.10), channel_id=1, source_target_pairs={{4,0},{5,1},{6,2},{7,3},{12,8},{13,9},{14,10},{15,11},{20,16},{21,... | collective-permute-start | bytes 199688 | tf_op jit(solution)/shard_map/ppermute | solution.py:20
  109.7 9.6 %collective-permute-start.11 = (bf16[2,1,16640]{2,1,0:T(2,128)(2,1)}, bf16[2,1,16640]{2,1,0:T(2,128)(2,1)}, u32[]{:S(2)}, u32[]{:S(2)}) collective-permute-start(bf16[2,1,16640]{2,1,0:T(2,128)(2,1)} %get-tuple-element.9), channel_id=1, source_target_pairs={{0,4},{1,5},{2,6},{3,7},{8,12},{9,13},{10,14},{11,15},{16,20},{17,... | collective-permute-start | bytes 199688 | tf_op jit(solution)/shard_map/ppermute | solution.py:19
  122.6 21.4 %collective-permute-start.14 = (bf16[1,18,16640]{2,1,0:T(8,128)(2,1)}, bf16[1,18,16640]{2,1,0:T(8,128)(2,1)}, u32[]{:S(2)}, u32[]{:S(2)}) collective-permute-start(bf16[1,18,16640]{2,1,0:T(8,128)(2,1)} %get-tuple-element.6), channel_id=1, source_target_pairs={{1,0},{2,1},{3,2},{5,4},{6,5},{7,6},{9,8},{10,9},{11,10},{13,12},{... | collective-permute-start | bytes 1797128 | tf_op jit(solution)/shard_map/ppermute | solution.py:20
  123.8 21.3 %collective-permute-start.13 = (bf16[1,18,16640]{2,1,0:T(8,128)(2,1)}, bf16[1,18,16640]{2,1,0:T(8,128)(2,1)}, u32[]{:S(2)}, u32[]{:S(2)}) collective-permute-start(bf16[1,18,16640]{2,1,0:T(8,128)(2,1)} %get-tuple-element.5), channel_id=1, source_target_pairs={{0,1},{1,2},{2,3},{4,5},{5,6},{6,7},{8,9},{9,10},{10,11},{12,13},{... | collective-permute-start | bytes 1797128 | tf_op jit(solution)/shard_map/ppermute | solution.py:19
  130.4 14.8 %copy-start.5 = (bf16[2,16,16640]{2,1,0:T(8,128)(2,1)S(1)}, bf16[2,16,16640]{2,1,0:T(8,128)(2,1)}, u32[]{:S(2)}) copy-start(bf16[2,16,16640]{2,1,0:T(8,128)(2,1)} %copy-done.4) | copy-start | bytes 3194884
  162.9 4.4 %collective-permute-start.17 = (bf16[8,32,128]{2,1,0:T(8,128)(2,1)S(1)}, bf16[8,32,128]{2,1,0:T(8,128)(2,1)S(1)}, u32[]{:S(2)}, u32[]{:S(2)}) collective-permute-start(bf16[8,32,128]{2,1,0:T(8,128)(2,1)S(1)} %convolution_convert_fusion.1), channel_id=1, source_target_pairs={{0,24},{8,0},{16,8},{24,16},{1,25},{9,1},{17,9},{25,17},{2,26},{10... | collective-permute-start | bytes 196616 | tf_op jit(solution)/shard_map/ppermute | solution.py:55
  164.5 4.3 %collective-permute-start.16 = (bf16[8,32,128]{2,1,0:T(8,128)(2,1)S(1)}, bf16[8,32,128]{2,1,0:T(8,128)(2,1)S(1)}, u32[]{:S(2)}, u32[]{:S(2)}) collective-permute-start(bf16[8,32,128]{2,1,0:T(8,128)(2,1)S(1)} %convolution_convert_fusion.1), channel_id=1, source_target_pairs={{0,16},{8,24},{16,0},{24,8},{1,17},{9,25},{17,1},{25,9},{2,18},{10... | collective-permute-start | bytes 196616 | tf_op jit(solution)/shard_map/ppermute | solution.py:55
  164.9 5.2 %collective-permute-start.15 = (bf16[8,32,128]{2,1,0:T(8,128)(2,1)S(1)}, bf16[8,32,128]{2,1,0:T(8,128)(2,1)S(1)}, u32[]{:S(2)}, u32[]{:S(2)}) collective-permute-start(bf16[8,32,128]{2,1,0:T(8,128)(2,1)S(1)} %convolution_convert_fusion.1), channel_id=1, source_target_pairs={{0,8},{8,16},{16,24},{24,0},{1,9},{9,17},{17,25},{25,1},{2,10},{10... | collective-permute-start | bytes 196616 | tf_op jit(solution)/shard_map/ppermute | solution.py:55
  165.8 5.1 %collective-permute-start.18 = (f32[2,8,64,64]{3,2,1,0:T(8,128)S(1)}, f32[2,8,64,64]{3,2,1,0:T(8,128)S(1)}, u32[]{:S(2)}, u32[]{:S(2)}) collective-permute-start(f32[2,8,64,64]{3,2,1,0:T(8,128)S(1)} %pad_maximum_fusion.6), channel_id=1, source_target_pairs={{0,4},{4,0},{1,5},{5,1},{2,6},{6,2},{3,7},{7,3},{8,12},{12,8},{9,1... | collective-permute-start | bytes 786440 | tf_op jit(solution)/shard_map/ppermute | solution.py:65
  171.8 11.9 %collective-permute-start.19 = (f32[2,8,64,64]{3,2,1,0:T(8,128)}, f32[2,8,64,64]{3,2,1,0:T(8,128)}, u32[]{:S(2)}, u32[]{:S(2)}) collective-permute-start(f32[2,8,64,64]{3,2,1,0:T(8,128)} %fusion.95), channel_id=1, source_target_pairs={{0,1},{1,0},{2,3},{3,2},{4,5},{5,4},{6,7},{7,6},{8,9},{9,8},{10,11... | collective-permute-start | bytes 786440 | tf_op jit(solution)/shard_map/ppermute | solution.py:65
  180.6 8.1 %copy-start.3 = (f32[2,16,16384]{2,1,0:T(8,128)S(1)}, f32[2,16,16384]{2,1,0:T(8,128)}, u32[]{:S(2)}) copy-start(f32[2,16,16384]{2,1,0:T(8,128)} %shard_map.95) | copy-start | bytes 6291460
  184.8 23.6 %collective-permute-start.20 = (f32[2,8,64,64]{3,2,1,0:T(8,128)S(1)}, f32[2,8,64,64]{3,2,1,0:T(8,128)S(1)}, u32[]{:S(2)}, u32[]{:S(2)}) collective-permute-start(f32[2,8,64,64]{3,2,1,0:T(8,128)S(1)} %fusion.117), channel_id=1, source_target_pairs={{0,2},{1,3},{2,0},{3,1},{4,6},{5,7},{6,4},{7,5},{8,10},{9,11},{10,... | collective-permute-start | bytes 786440 | tf_op jit(solution)/shard_map/ppermute | solution.py:65
  188.6 20.6 %copy-start.1 = (bf16[64,256]{1,0:T(8,128)(2,1)S(1)}, bf16[64,256]{1,0:T(8,128)(2,1)}, u32[]{:S(2)}) copy-start(bf16[64,256]{1,0:T(8,128)(2,1)} %param.9) | copy-start | bytes 98308
Sparse Core Ops, SparseCore 0:
  21.9 25.6 reduce-scatter.2
  132.2 24.8 reduce-scatter.4

commit v3 on v2

--- a/solution.py
+++ b/solution.py
@@ -179,6 +179,15 @@
     blocks = block_weights(spec_real, spec_imag)
     padded = spatial_rims(features, channels)
     activation = depthwise(padded, depth_weight, False, x_cells, channels, jnp.bfloat16)
+    field3 = features.reshape(row_count, x_cells, channels)
+    owned_blocks = lax.dynamic_slice_in_dim(
+        blocks, lax.axis_index("gx") * share_size, share_size, 0
+    )
+    coeffs = share_terms(field3, cos_part, sin_part).astype(jnp.bfloat16)
+    mixed_modes = jnp.einsum(
+        "krc,kco->kro", coeffs, owned_blocks, preferred_element_type=jnp.float32
+    ).astype(jnp.bfloat16)
+    mixed_modes, activation = lax.optimization_barrier((mixed_modes, activation))
     activation = activation.reshape(row_count * x_cells, channels)
     hidden_pre = jnp.dot(activation, expand_weight, preferred_element_type=jnp.float32)
     hidden, hidden_slope = gelu_parts(hidden_pre)
@@ -186,14 +195,6 @@
         hidden.astype(jnp.bfloat16), project_weight, preferred_element_type=jnp.float32
     )
     local_branch = local_branch.reshape(row_count, x_cells, channels)
-    field3 = features.reshape(row_count, x_cells, channels)
-    owned_blocks = lax.dynamic_slice_in_dim(
-        blocks, lax.axis_index("gx") * share_size, share_size, 0
-    )
-    coeffs = share_terms(field3, cos_part, sin_part).astype(jnp.bfloat16)
-    mixed_modes = jnp.einsum(
-        "krc,kco->kro", coeffs, owned_blocks, preferred_element_type=jnp.float32
-    ).astype(jnp.bfloat16)
     spectral = share_inverse(mixed_modes, cos_scaled, sin_scaled, channels)
     result, slopes = gelu_parts(local_branch + spectral)
     output = result.astype(jnp.bfloat16).reshape(planes, y_cells, merged)
@@ -214,9 +215,11 @@
     dmode = jnp.einsum(
         "kro,kco->krc", dcoef, owned_blocks, preferred_element_type=jnp.float32
     ).astype(jnp.bfloat16)
+    dblock = jnp.einsum("krc,kro->kco", coeffs, dcoef, preferred_element_type=jnp.float32)
+    local_grads = split_gradients(dblock, channels)
+    dmode, local_grads, grad_act = lax.optimization_barrier((dmode, local_grads, grad_act))
     spectral_grad = share_inverse(dmode, cos_order, sin_order, channels)
-    dblock = jnp.einsum("krc,kro->kco", coeffs, dcoef, preferred_element_type=jnp.float32)
-    grad_spec = sum_gradients(split_gradients(dblock, channels))
+    grad_spec = sum_gradients(local_grads)
     padded_grad = spatial_rims(grad_act, channels)
     grad_local = depthwise(padded_grad, depth_weight, True, x_cells, channels)
     grad_features = (grad_local + spectral_grad.reshape(planes, y_cells, merged)).astype(

time: 220 us -> 211 us (0.959); the launches traced: 216 us -> 210 us
  matrix products: 25.9 us -> 21.7 us
  other arithmetic: 18.7 us -> 22 us
  starting transfers between devices: 43.4 us -> 41.1 us
    reduce_scatter x2, waiting for transfers between devices: 0.01 us -> 14.6 us  [share_terms(): lax.psum_scatter(jnp.concatenate([real_part, imag_part], axis=2), 'gx', s...]
    ppermute x6, waiting for transfers between devices: 17.5 us -> 5.75 us  [padded_2(): after = lax.ppermute(leading, axis, down)]
    ppermute x6, waiting for transfers between devices: 4.22 us -> 0.02 us  [ring_gather(): lax.ppermute(block, axis, [(i, (i + shift) % size) for i in range(size)])]
    dot_general x1, matrix products: 4.5 us -> 1.22 us  [per_device(): jnp.dot(activation, expand_weight, preferred_element_type=jnp.float32)]
    ppermute x3, starting transfers between devices: 6.36 us -> 3.92 us  [butterfly_sum(): lax.ppermute(value, axis, [(i, i ^ step) for i in range(size)])]
    dot_general x1, matrix products: 5.11 us -> 2.82 us  [per_device(): jnp.dot(hidden.astype(jnp.bfloat16), project_weight, preferred_element_ty...]
    unnamed x30 -> x34, local copies, waits for them, and re-layouts: 5.23 us -> 5.99 us
  transfers between devices with their start and end apart: 23 -> 23, of which waited for: 10 -> 7; matrix products, arithmetic and copies ran while one was open for 25% -> 29% of each run, Pallas kernels for 12% -> 12%
where the time goes in v3:
time: 211 us; the launch traced here: 210 us
  waiting for transfers between devices  45.6 us (22%)
  starting transfers between devices  41.1 us (19%)
  local copies, waits for them, and re-layouts  38.6 us (18%)
  Pallas kernels  26.1 us (12%)
  other arithmetic  22 us (10%)
  matrix products  21.7 us (10%)
  between operations  14.5 us (7%)
    pallas_call x2, Pallas kernels, depthwise(): pl.pallas_call(kernel, out_shape=jax.ShapeDtypeStruct((planes, y_cells, l...  26.1 us
    ppermute x3, waiting for transfers between devices, butterfly_sum(): lax.ppermute(value, axis, [(i, i ^ step) for i in range(size)])  23.2 us
    ppermute x6, starting transfers between devices, padded_2(): before = lax.ppermute(last, axis, up)  21.5 us
    reduce_scatter x2, waiting for transfers between devices, share_terms(): lax.psum_scatter(jnp.concatenate([real_part, imag_part], axis=2), 'gx', s...  14.6 us
    ppermute x6, starting transfers between devices, ring_gather(): lax.ppermute(block, axis, [(i, (i + shift) % size) for i in range(size)])  8.12 us
    dot_general x1, matrix products, per_device(): jnp.dot(grad_hidden, expand_weight.T, preferred_element_type=jnp.float32)  7.82 us
    concatenate x4, other arithmetic, padded_2(): value = jnp.concatenate([before, value, after], axis=dim)  7.65 us
    ppermute x6, starting transfers between devices, padded_2(): after = lax.ppermute(leading, axis, down)  7.52 us
  transfers between devices with their start and end apart: 23, of which 7 were waited for; matrix products, arithmetic and copies ran while one was open for 29% of the time, Pallas kernels for 12%

profile of v3, /device:TPU:0, one launch (start us, length us, event | category | flops | bytes accessed | tf_op | source)
XLA Modules:
  0.0 209.7 jit_solution(1720329687437495343)
XLA Ops:
  7.9 2.9 %collective-permute-start = (bf16[2,16,128]{2,1,0:T(8,128)(2,1)S(1)}, bf16[2,16,128]{2,1,0:T(8,128)(2,1)S(1)}, u32[]{:S(2)}, u32[]{:S(2)}) collective-permute-start(bf16[2,16,128]{2,1,0:T(8,128)(2,1)S(1)} %get-tuple-element.26), channel_id=1, source_target_pairs={{0,8},{8,16},{16,24},{24,0},{1,9},{9,17},{17,25},{25,1},{2,10},{10... | collective-permute-start | bytes 24584 | tf_op jit(solution)/shard_map/ppermute | solution.py:19
  11.8 3.0 %reshape.91 = bf16[32,256,64]{2,1,0:T(8,128)(2,1)S(1)} reshape(bf16[2,16,16384]{2,1,0:T(8,128)(2,1)} %param.7) | data formatting | bytes 2097152 | tf_op jit(solution)/shard_map/reshape | solution.py:182
  16.4 1.3 collective-permute-start.3
  17.7 3.0 %collective-permute-start.2 = (bf16[2,1,16640]{2,1,0:T(2,128)(2,1)S(1)}, bf16[2,1,16640]{2,1,0:T(2,128)(2,1)S(1)}, u32[]{:S(2)}, u32[]{:S(2)}) collective-permute-start(bf16[2,1,16640]{2,1,0:T(2,128)(2,1)S(1)} %get-tuple-element.21), channel_id=1, source_target_pairs={{0,4},{1,5},{2,6},{3,7},{8,12},{9,13},{10,14},{11,15},{16,20},{17,... | collective-permute-start | bytes 199688 | tf_op jit(solution)/shard_map/ppermute | solution.py:19
  23.8 1.3 fusion.96
  25.1 1.3 collective-permute-start.5
  26.4 5.5 %collective-permute-start.4 = (bf16[1,18,16640]{2,1,0:T(8,128)(2,1)}, bf16[1,18,16640]{2,1,0:T(8,128)(2,1)}, u32[]{:S(2)}, u32[]{:S(2)}) collective-permute-start(bf16[1,18,16640]{2,1,0:T(8,128)(2,1)} %get-tuple-element.17), channel_id=1, source_target_pairs={{0,1},{1,2},{2,3},{4,5},{5,6},{6,7},{8,9},{9,10},{10,11},{12,13},{... | collective-permute-start | bytes 1797128 | tf_op jit(solution)/shard_map/ppermute | solution.py:19
  31.9 3.2 %reshape.98 = f32[32,256,64]{2,1,0:T(8,128)} reshape(bf16[2,16,16384]{2,1,0:T(8,128)(2,1)S(1)} %copy-done.7) | data formatting | bytes 3145728 | tf_op jit(solution)/shard_map/convert_element_type | solution.py:202
  35.1 3.9 %copy.30 = f32[32,256,64]{1,2,0:T(8,128)} copy(f32[32,256,64]{2,1,0:T(8,128)} %reshape.98) | data formatting | bytes 4194304 | tf_op jit(solution)/shard_map/convert_element_type | solution.py:202
  40.8 1.1 fusion.13
  42.0 4.8 %collective-permute-done.5 = bf16[1,18,16640]{2,1,0:T(8,128)(2,1)S(1)} collective-permute-done((bf16[1,18,16640]{2,1,0:T(8,128)(2,1)}, bf16[1,18,16640]{2,1,0:T(8,128)(2,1)S(1)}, u32[]{:S(2)}, u32[]{:S(2)}) %collective-permute-start.5) | collective-permute-done | bytes 599072 | tf_op jit(solution)/shard_map/ppermute | solution.py:20
  46.8 1.3 collective-permute-done.4
  48.1 3.2 %pad_maximum_fusion.p_ref = bf16[4,18,16640]{2,1,0:T(8,128)(2,1)} fusion(bf16[1,18,16640]{2,1,0:T(8,128)(2,1)S(1)} %collective-permute-done.5, bf16[2,1,16640]{2,1,0:T(2,128)(2,1)} %copy-done.8, bf16[2,16,16640]{2,1,0:T(8,128)(2,1)S(1)} %constant_dynamic-update-slice_fusion, bf16[2,1,16640]{2,1,0:T(2,128)(2,1)} %copy-done.9, ...), kind=kLoop, calls=%fused_computation.11 | loop fusion | flops 11980800 | bytes 4792320 | tf_op jit(solution)/shard_map/concatenate | solution.py:21
  51.3 12.9 %shard_map.94 = bf16[2,16,16384]{2,1,0:T(8,128)(2,1)} custom-call(bf16[4,18,16640]{2,1,0:T(8,128)(2,1)} %pad_maximum_fusion.p_ref, f32[27,640]{1,0:T(8,128)} %tile.9.w_ref), custom_call_target="tpu_custom_call" | custom-call | tf_op jit(solution)/shard_map/pallas_call | solution.py:123
  66.6 1.5 collective-permute-start.7
  68.2 2.3 %collective-permute-start.8 = (bf16[8,32,128]{2,1,0:T(8,128)(2,1)}, bf16[8,32,128]{2,1,0:T(8,128)(2,1)}, u32[]{:S(2)}, u32[]{:S(2)}) collective-permute-start(bf16[8,32,128]{2,1,0:T(8,128)(2,1)} %convolution_convert_fusion.2), channel_id=1, source_target_pairs={{0,24},{8,0},{16,8},{24,16},{1,25},{9,1},{17,9},{25,17},{2,26},{10... | collective-permute-start | bytes 196616 | tf_op jit(solution)/shard_map/ppermute | solution.py:55
  70.5 3.0 %reshape.92 = bf16[8192,64]{1,0:T(8,128)(2,1)S(1)} reshape(bf16[2,16,16384]{2,1,0:T(8,128)(2,1)} %shard_map.94) | data formatting | bytes 2097152 | tf_op jit(solution)/shard_map/reshape | solution.py:191
  73.6 1.2 fusion.103
  74.8 2.8 %fusion.5 = f32[8192,64]{0,1:T(8,128)S(1)} fusion(bf16[256,64]{0,1:T(8,128)(2,1)S(1)} %copy-done.11, f32[8192,256]{1,0:T(8,128)S(1)} %fusion.103), kind=kOutput, calls=%fused_computation.10 | convolution fusion | flops 278921216 | bytes 10518528 | tf_op jit(solution)/shard_map/dot_general | solution.py:194
  82.4 2.7 %fusion.11 = (bf16[32,256,64]{1,2,0:T(8,128)(2,1)S(1)}, bf16[32,256,64]{1,2,0:T(8,128)(2,1)}) fusion(f32[32,256,64]{1,2,0:T(8,128)S(1)} %copy-done.3, f32[256,32,64]{0,2,1:T(8,128)S(1)} %fusion.20, bf16[32,32,64]{2,1,0:T(8,128)(2,1)S(1)} %get-tuple-element.31, f32[32]{0:T(128)S(1)} %get-tuple-element.33, s32[32]{0:T(128)S(1)} %add.121, ...), kind=kOutput, calls=%fused_computation.19 | convolution fusion | flops 41041920 | bytes 8520960 | tf_op jit(solution)/shard_map/krc,xk->rxc/dot_general | solution.py:140
  85.1 1.4 fusion.45
  86.5 1.4 fusion.42
  88.0 2.0 copy.29
  90.0 2.5 %reshape.94 = bf16[2,16,16384]{2,1,0:T(8,128)(2,1)} reshape(bf16[32,256,64]{2,1,0:T(8,128)(2,1)S(1)} %copy.29) | data formatting | bytes 2097152 | tf_op jit(solution)/shard_map/reshape | solution.py:200
  92.5 2.2 %pad_maximum_fusion.5 = f32[32,32,128]{2,0,1:T(8,128)} fusion(f32[32,32,64]{2,0,1:T(8,128)} %fusion.45, f32[32,32,64]{2,0,1:T(8,128)} %fusion.42), kind=kLoop, calls=%fused_computation.34 | loop fusion | flops 131072 | bytes 1048576 | tf_op jit(solution)/shard_map/concatenate | solution.py:134
  94.9 7.8 %convolution_convert_fusion = bf16[8192,64]{0,1:T(8,128)(2,1)S(1)} fusion(bf16[64,256]{1,0:T(8,128)(2,1)S(1)} %copy-done, bf16[8192,64]{0,1:T(8,128)(2,1)S(1)} %bitcast.53, bf16[256,64]{0,1:T(8,128)(2,1)S(1)} %copy-done.11, f32[8192,256]{1,0:T(8,128)} %copy-done.2), kind=kOutput, calls=%fused_computation.3 | convolution fusion | flops 558366720 | bytes 10551296 | tf_op jit(solution)/shard_map/dot_general | solution.py:210
  103.8 1.7 reshape.96
  105.5 14.6 %reduce-scatter.5.cloned.1.call-done = f32[8,32,128]{2,0,1:T(8,128)} async-done(((f32[32,32,128]{2,0,1:T(8,128)}), f32[8,32,128]{2,0,1:T(8,128)}) %reduce-scatter.5.cloned.1.call-update) | async-done | bytes 131088 | tf_op jit(solution)/shard_map/reduce_scatter | solution.py:133
  121.8 1.5 collective-permute-start.9
  123.3 1.4 collective-permute-start.15
  125.3 1.4 collective-permute-start.17
  126.8 1.4 collective-permute-start.10
  128.2 1.3 constant_dynamic-update-slice_fusion.8
  130.6 1.3 collective-permute-start.12
  132.0 3.0 %collective-permute-start.11 = (bf16[2,1,16640]{2,1,0:T(2,128)(2,1)S(1)}, bf16[2,1,16640]{2,1,0:T(2,128)(2,1)S(1)}, u32[]{:S(2)}, u32[]{:S(2)}) collective-permute-start(bf16[2,1,16640]{2,1,0:T(2,128)(2,1)S(1)} %get-tuple-element.19), channel_id=1, source_target_pairs={{0,4},{1,5},{2,6},{3,7},{8,12},{9,13},{10,14},{11,15},{16,20},{17,... | collective-permute-start | bytes 199688 | tf_op jit(solution)/shard_map/ppermute | solution.py:19
  136.6 1.3 fusion.95
  137.9 1.3 collective-permute-start.14
  139.1 5.5 %collective-permute-start.13 = (bf16[1,18,16640]{2,1,0:T(8,128)(2,1)}, bf16[1,18,16640]{2,1,0:T(8,128)(2,1)}, u32[]{:S(2)}, u32[]{:S(2)}) collective-permute-start(bf16[1,18,16640]{2,1,0:T(8,128)(2,1)} %get-tuple-element.15), channel_id=1, source_target_pairs={{0,1},{1,2},{2,3},{4,5},{5,6},{6,7},{8,9},{9,10},{10,11},{12,13},{... | collective-permute-start | bytes 1797128 | tf_op jit(solution)/shard_map/ppermute | solution.py:19
  147.3 2.7 %copy.38 = f32[32,256,64]{2,1,0:T(8,128)} copy(f32[32,256,64]{1,2,0:T(8,128)S(1)} %add_bitcast_fusion) | data formatting | bytes 4194304 | tf_op jit(solution)/shard_map/add | solution.py:143
  150.1 2.9 %reshape.97 = f32[2,16,16384]{2,1,0:T(8,128)S(1)} reshape(f32[32,256,64]{2,1,0:T(8,128)} %copy.38) | data formatting | bytes 4194304 | tf_op jit(solution)/shard_map/reshape | solution.py:225
  153.0 19.6 %collective-permute-done.19 = f32[2,8,64,64]{3,2,1,0:T(8,128)} collective-permute-done((f32[2,8,64,64]{3,2,1,0:T(8,128)}, f32[2,8,64,64]{3,2,1,0:T(8,128)}, u32[]{:S(2)}, u32[]{:S(2)}) %collective-permute-start.19) | collective-permute-done | bytes 262176 | tf_op jit(solution)/shard_map/ppermute | solution.py:65
  172.5 2.1 add.135
  174.6 3.3 %collective-permute-start.20 = (f32[2,8,64,64]{3,2,1,0:T(8,128)}, f32[2,8,64,64]{3,2,1,0:T(8,128)}, u32[]{:S(2)}, u32[]{:S(2)}) collective-permute-start(f32[2,8,64,64]{3,2,1,0:T(8,128)} %add.135), channel_id=1, source_target_pairs={{0,2},{1,3},{2,0},{3,1},{4,6},{5,7},{6,4},{7,5},{8,10},{9,11},{10,... | collective-permute-start | bytes 786440 | tf_op jit(solution)/shard_map/ppermute | solution.py:65
  177.9 3.2 %pad_maximum_fusion.1.p_ref = bf16[4,18,16640]{2,1,0:T(8,128)(2,1)} fusion(bf16[1,18,16640]{2,1,0:T(8,128)(2,1)} %collective-permute-done.14, bf16[2,1,16640]{2,1,0:T(2,128)(2,1)S(1)} %collective-permute-done.12, bf16[2,16,16640]{2,1,0:T(8,128)(2,1)S(1)} %constant_dynamic-update-slice_fusion.7, bf16[2,1,16640]{2,1,0:T(2,128)(2,1)S(1)} %collective-permute-done.11, ...), kind=kLoop, calls=%fused_computation.12 | loop fusion | flops 11980800 | bytes 4792320 | tf_op jit(solution)/shard_map/concatenate | solution.py:21
  181.2 13.2 %shard_map.95 = f32[2,16,16384]{2,1,0:T(8,128)} custom-call(bf16[4,18,16640]{2,1,0:T(8,128)(2,1)} %pad_maximum_fusion.1.p_ref, f32[27,640]{1,0:T(8,128)} %tile.21.w_ref), custom_call_target="tpu_custom_call" | custom-call | tf_op jit(solution)/shard_map/pallas_call | solution.py:123
  194.4 2.8 %add_convert_fusion = bf16[2,16,16384]{2,1,0:T(8,128)(2,1)} fusion(f32[2,16,16384]{2,1,0:T(8,128)} %shard_map.95, f32[2,16,16384]{2,1,0:T(8,128)S(1)} %reshape.97), kind=kLoop, calls=%fused_computation.21 | loop fusion | flops 1048576 | bytes 5242880 | tf_op jit(solution)/shard_map/convert_element_type | solution.py:225
  197.2 3.6 %collective-permute-done.20 = f32[2,8,64,64]{3,2,1,0:T(8,128)} collective-permute-done((f32[2,8,64,64]{3,2,1,0:T(8,128)}, f32[2,8,64,64]{3,2,1,0:T(8,128)}, u32[]{:S(2)}, u32[]{:S(2)}) %collective-permute-start.20) | collective-permute-done | bytes 262176 | tf_op jit(solution)/shard_map/ppermute | solution.py:65
  200.8 2.1 add.136
  (99 shorter events, 24.1 us)
Async XLA Ops:
  7.2 66.4 %copy-start = (bf16[64,256]{1,0:T(8,128)(2,1)S(1)}, bf16[64,256]{1,0:T(8,128)(2,1)}, u32[]{:S(2)}) copy-start(bf16[64,256]{1,0:T(8,128)(2,1)} %param.9) | copy-start | bytes 98308
  7.2 57.0 %reduce-scatter.3.cloned.1.call-start = ((), (), s32[]{:S(2)}) async-start(), calls=%async_computation.2 | async-start | bytes 655360 | tf_op jit(solution)/shard_map/reduce_scatter | solution.py:133
  7.9 8.1 %collective-permute-start = (bf16[2,16,128]{2,1,0:T(8,128)(2,1)S(1)}, bf16[2,16,128]{2,1,0:T(8,128)(2,1)S(1)}, u32[]{:S(2)}, u32[]{:S(2)}) collective-permute-start(bf16[2,16,128]{2,1,0:T(8,128)(2,1)S(1)} %get-tuple-element.26), channel_id=1, source_target_pairs={{0,8},{8,16},{16,24},{24,0},{1,9},{9,17},{17,25},{25,1},{2,10},{10... | collective-permute-start | bytes 24584 | tf_op jit(solution)/shard_map/ppermute | solution.py:19
  10.9 5.3 %collective-permute-start.1 = (bf16[2,16,128]{2,1,0:T(8,128)(2,1)S(1)}, bf16[2,16,128]{2,1,0:T(8,128)(2,1)S(1)}, u32[]{:S(2)}, u32[]{:S(2)}) collective-permute-start(bf16[2,16,128]{2,1,0:T(8,128)(2,1)S(1)} %get-tuple-element.25), channel_id=1, source_target_pairs={{8,0},{16,8},{24,16},{0,24},{9,1},{17,9},{25,17},{1,25},{10,2},{18... | collective-permute-start | bytes 24584 | tf_op jit(solution)/shard_map/ppermute | solution.py:20
  14.9 1.2 copy-start.4
  16.4 5.4 %collective-permute-start.3 = (bf16[2,1,16640]{2,1,0:T(2,128)(2,1)S(1)}, bf16[2,1,16640]{2,1,0:T(2,128)(2,1)S(1)}, u32[]{:S(2)}, u32[]{:S(2)}) collective-permute-start(bf16[2,1,16640]{2,1,0:T(2,128)(2,1)S(1)} %get-tuple-element.22), channel_id=1, source_target_pairs={{4,0},{5,1},{6,2},{7,3},{12,8},{13,9},{14,10},{15,11},{20,16},{21,... | collective-permute-start | bytes 199688 | tf_op jit(solution)/shard_map/ppermute | solution.py:20
  17.7 4.1 %collective-permute-start.2 = (bf16[2,1,16640]{2,1,0:T(2,128)(2,1)S(1)}, bf16[2,1,16640]{2,1,0:T(2,128)(2,1)S(1)}, u32[]{:S(2)}, u32[]{:S(2)}) collective-permute-start(bf16[2,1,16640]{2,1,0:T(2,128)(2,1)S(1)} %get-tuple-element.21), channel_id=1, source_target_pairs={{0,4},{1,5},{2,6},{3,7},{8,12},{9,13},{10,14},{11,15},{16,20},{17,... | collective-permute-start | bytes 199688 | tf_op jit(solution)/shard_map/ppermute | solution.py:19
  21.8 98.2 %reduce-scatter.5.cloned.1.call-start = ((), (), s32[]{:S(2)}) async-start(), calls=%async_computation.3 | async-start | bytes 655360 | tf_op jit(solution)/shard_map/reduce_scatter | solution.py:133
  21.9 0.7 copy-start.8
  22.5 0.7 copy-start.9
  23.8 8.1 %copy-start.7 = (bf16[2,16,16384]{2,1,0:T(8,128)(2,1)S(1)}, bf16[2,16,16384]{2,1,0:T(8,128)(2,1)}, u32[]{:S(2)}) copy-start(bf16[2,16,16384]{2,1,0:T(8,128)(2,1)} %param.13) | copy-start | bytes 3145732
  25.1 21.7 %collective-permute-start.5 = (bf16[1,18,16640]{2,1,0:T(8,128)(2,1)}, bf16[1,18,16640]{2,1,0:T(8,128)(2,1)S(1)}, u32[]{:S(2)}, u32[]{:S(2)}) collective-permute-start(bf16[1,18,16640]{2,1,0:T(8,128)(2,1)} %get-tuple-element.18), channel_id=1, source_target_pairs={{1,0},{2,1},{3,2},{5,4},{6,5},{7,6},{9,8},{10,9},{11,10},{13,12},{... | collective-permute-start | bytes 1797128 | tf_op jit(solution)/shard_map/ppermute | solution.py:20
  26.4 21.7 %collective-permute-start.4 = (bf16[1,18,16640]{2,1,0:T(8,128)(2,1)}, bf16[1,18,16640]{2,1,0:T(8,128)(2,1)}, u32[]{:S(2)}, u32[]{:S(2)}) collective-permute-start(bf16[1,18,16640]{2,1,0:T(8,128)(2,1)} %get-tuple-element.17), channel_id=1, source_target_pairs={{0,1},{1,2},{2,3},{4,5},{5,6},{6,7},{8,9},{9,10},{10,11},{12,13},{... | collective-permute-start | bytes 1797128 | tf_op jit(solution)/shard_map/ppermute | solution.py:19
  35.1 3.9 %copy-start.6 = (bf16[32,64,64]{2,1,0:T(8,128)(2,1)S(1)}, bf16[32,64,64]{2,1,0:T(8,128)(2,1)}, u32[]{:S(2)}) copy-start(bf16[32,64,64]{2,1,0:T(8,128)(2,1)} %param.12) | copy-start | bytes 786436
  35.1 4.0 %copy-start.10 = (bf16[27,64]{1,0:T(8,128)(2,1)S(1)}, bf16[27,64]{1,0:T(8,128)(2,1)}, u32[]{:S(2)}) copy-start(bf16[27,64]{1,0:T(8,128)(2,1)} %param.8) | copy-start | bytes 10372
  65.9 13.2 %collective-permute-start.6 = (bf16[8,32,128]{2,1,0:T(8,128)(2,1)}, bf16[8,32,128]{2,1,0:T(8,128)(2,1)}, u32[]{:S(2)}, u32[]{:S(2)}) collective-permute-start(bf16[8,32,128]{2,1,0:T(8,128)(2,1)} %convolution_convert_fusion.2), channel_id=1, source_target_pairs={{0,8},{8,16},{16,24},{24,0},{1,9},{9,17},{17,25},{25,1},{2,10},{10... | collective-permute-start | bytes 196616 | tf_op jit(solution)/shard_map/ppermute | solution.py:55
  66.6 13.3 %collective-permute-start.7 = (bf16[8,32,128]{2,1,0:T(8,128)(2,1)}, bf16[8,32,128]{2,1,0:T(8,128)(2,1)}, u32[]{:S(2)}, u32[]{:S(2)}) collective-permute-start(bf16[8,32,128]{2,1,0:T(8,128)(2,1)} %convolution_convert_fusion.2), channel_id=1, source_target_pairs={{0,16},{8,24},{16,0},{24,8},{1,17},{9,25},{17,1},{25,9},{2,18},{10... | collective-permute-start | bytes 196616 | tf_op jit(solution)/shard_map/ppermute | solution.py:55
  68.2 12.6 %collective-permute-start.8 = (bf16[8,32,128]{2,1,0:T(8,128)(2,1)}, bf16[8,32,128]{2,1,0:T(8,128)(2,1)}, u32[]{:S(2)}, u32[]{:S(2)}) collective-permute-start(bf16[8,32,128]{2,1,0:T(8,128)(2,1)} %convolution_convert_fusion.2), channel_id=1, source_target_pairs={{0,24},{8,0},{16,8},{24,16},{1,25},{9,1},{17,9},{25,17},{2,26},{10... | collective-permute-start | bytes 196616 | tf_op jit(solution)/shard_map/ppermute | solution.py:55
  73.5 1.2 copy-start.11
  74.8 3.3 %copy-start.2 = (f32[8192,256]{1,0:T(8,128)}, f32[8192,256]{1,0:T(8,128)S(1)}, u32[]{:S(2)}) copy-start(f32[8192,256]{1,0:T(8,128)S(1)} %fusion.103) | copy-start | bytes 25165828
  78.1 4.4 %copy-start.3 = (f32[32,256,64]{1,2,0:T(8,128)S(1)}, f32[32,256,64]{1,2,0:T(8,128)}, u32[]{:S(2)}) copy-start(f32[32,256,64]{1,2,0:T(8,128)} %copy.30) | copy-start | bytes 6291460
  105.5 22.7 %copy-start.5 = (bf16[2,16,16384]{2,1,0:T(8,128)(2,1)}, bf16[2,16,16384]{2,1,0:T(8,128)(2,1)S(1)}, u32[]{:S(2)}) copy-start(bf16[2,16,16384]{2,1,0:T(8,128)(2,1)S(1)} %reshape.96) | copy-start | bytes 3145732
  121.8 6.4 %collective-permute-start.9 = (bf16[2,16,128]{2,1,0:T(8,128)(2,1)S(1)}, bf16[2,16,128]{2,1,0:T(8,128)(2,1)S(1)}, u32[]{:S(2)}, u32[]{:S(2)}) collective-permute-start(bf16[2,16,128]{2,1,0:T(8,128)(2,1)S(1)} %get-tuple-element.24), channel_id=1, source_target_pairs={{0,8},{8,16},{16,24},{24,0},{1,9},{9,17},{17,25},{25,1},{2,10},{10... | collective-permute-start | bytes 24584 | tf_op jit(solution)/shard_map/ppermute | solution.py:19
  123.3 8.7 %collective-permute-start.15 = (bf16[8,32,128]{2,1,0:T(8,128)(2,1)S(1)}, bf16[8,32,128]{2,1,0:T(8,128)(2,1)S(1)}, u32[]{:S(2)}, u32[]{:S(2)}) collective-permute-start(bf16[8,32,128]{2,1,0:T(8,128)(2,1)S(1)} %convolution_convert_fusion.1), channel_id=1, source_target_pairs={{0,8},{8,16},{16,24},{24,0},{1,9},{9,17},{17,25},{25,1},{2,10},{10... | collective-permute-start | bytes 196616 | tf_op jit(solution)/shard_map/ppermute | solution.py:55
  124.7 10.3 %collective-permute-start.16 = (bf16[8,32,128]{2,1,0:T(8,128)(2,1)S(1)}, bf16[8,32,128]{2,1,0:T(8,128)(2,1)S(1)}, u32[]{:S(2)}, u32[]{:S(2)}) collective-permute-start(bf16[8,32,128]{2,1,0:T(8,128)(2,1)S(1)} %convolution_convert_fusion.1), channel_id=1, source_target_pairs={{0,16},{8,24},{16,0},{24,8},{1,17},{9,25},{17,1},{25,9},{2,18},{10... | collective-permute-start | bytes 196616 | tf_op jit(solution)/shard_map/ppermute | solution.py:55
  125.3 9.7 %collective-permute-start.17 = (bf16[8,32,128]{2,1,0:T(8,128)(2,1)S(1)}, bf16[8,32,128]{2,1,0:T(8,128)(2,1)S(1)}, u32[]{:S(2)}, u32[]{:S(2)}) collective-permute-start(bf16[8,32,128]{2,1,0:T(8,128)(2,1)S(1)} %convolution_convert_fusion.1), channel_id=1, source_target_pairs={{0,24},{8,0},{16,8},{24,16},{1,25},{9,1},{17,9},{25,17},{2,26},{10... | collective-permute-start | bytes 196616 | tf_op jit(solution)/shard_map/ppermute | solution.py:55
  126.8 3.7 %collective-permute-start.10 = (bf16[2,16,128]{2,1,0:T(8,128)(2,1)S(1)}, bf16[2,16,128]{2,1,0:T(8,128)(2,1)S(1)}, u32[]{:S(2)}, u32[]{:S(2)}) collective-permute-start(bf16[2,16,128]{2,1,0:T(8,128)(2,1)S(1)} %get-tuple-element.23), channel_id=1, source_target_pairs={{8,0},{16,8},{24,16},{0,24},{9,1},{17,9},{25,17},{1,25},{10,2},{18... | collective-permute-start | bytes 24584 | tf_op jit(solution)/shard_map/ppermute | solution.py:20
  128.2 17.0 %collective-permute-start.18 = (f32[2,8,64,64]{3,2,1,0:T(8,128)S(1)}, f32[2,8,64,64]{3,2,1,0:T(8,128)S(1)}, u32[]{:S(2)}, u32[]{:S(2)}) collective-permute-start(f32[2,8,64,64]{3,2,1,0:T(8,128)S(1)} %pad_maximum_fusion.6), channel_id=1, source_target_pairs={{0,4},{4,0},{1,5},{5,1},{2,6},{6,2},{3,7},{7,3},{8,12},{12,8},{9,1... | collective-permute-start | bytes 786440 | tf_op jit(solution)/shard_map/ppermute | solution.py:65
  130.6 4.6 %collective-permute-start.12 = (bf16[2,1,16640]{2,1,0:T(2,128)(2,1)S(1)}, bf16[2,1,16640]{2,1,0:T(2,128)(2,1)S(1)}, u32[]{:S(2)}, u32[]{:S(2)}) collective-permute-start(bf16[2,1,16640]{2,1,0:T(2,128)(2,1)S(1)} %get-tuple-element.20), channel_id=1, source_target_pairs={{4,0},{5,1},{6,2},{7,3},{12,8},{13,9},{14,10},{15,11},{20,16},{21,... | collective-permute-start | bytes 199688 | tf_op jit(solution)/shard_map/ppermute | solution.py:20
  132.0 4.0 %collective-permute-start.11 = (bf16[2,1,16640]{2,1,0:T(2,128)(2,1)S(1)}, bf16[2,1,16640]{2,1,0:T(2,128)(2,1)S(1)}, u32[]{:S(2)}, u32[]{:S(2)}) collective-permute-start(bf16[2,1,16640]{2,1,0:T(2,128)(2,1)S(1)} %get-tuple-element.19), channel_id=1, source_target_pairs={{0,4},{1,5},{2,6},{3,7},{8,12},{9,13},{10,14},{11,15},{16,20},{17,... | collective-permute-start | bytes 199688 | tf_op jit(solution)/shard_map/ppermute | solution.py:19
  137.9 40.1 %collective-permute-start.14 = (bf16[1,18,16640]{2,1,0:T(8,128)(2,1)}, bf16[1,18,16640]{2,1,0:T(8,128)(2,1)}, u32[]{:S(2)}, u32[]{:S(2)}) collective-permute-start(bf16[1,18,16640]{2,1,0:T(8,128)(2,1)} %get-tuple-element.16), channel_id=1, source_target_pairs={{1,0},{2,1},{3,2},{5,4},{6,5},{7,6},{9,8},{10,9},{11,10},{13,12},{... | collective-permute-start | bytes 1797128 | tf_op jit(solution)/shard_map/ppermute | solution.py:20
  139.1 38.8 %collective-permute-start.13 = (bf16[1,18,16640]{2,1,0:T(8,128)(2,1)}, bf16[1,18,16640]{2,1,0:T(8,128)(2,1)}, u32[]{:S(2)}, u32[]{:S(2)}) collective-permute-start(bf16[1,18,16640]{2,1,0:T(8,128)(2,1)} %get-tuple-element.15), channel_id=1, source_target_pairs={{0,1},{1,2},{2,3},{4,5},{5,6},{6,7},{8,9},{9,10},{10,11},{12,13},{... | collective-permute-start | bytes 1797128 | tf_op jit(solution)/shard_map/ppermute | solution.py:19
  146.1 26.4 %collective-permute-start.19 = (f32[2,8,64,64]{3,2,1,0:T(8,128)}, f32[2,8,64,64]{3,2,1,0:T(8,128)}, u32[]{:S(2)}, u32[]{:S(2)}) collective-permute-start(f32[2,8,64,64]{3,2,1,0:T(8,128)} %add.134), channel_id=1, source_target_pairs={{0,1},{1,0},{2,3},{3,2},{4,5},{5,4},{6,7},{7,6},{8,9},{9,8},{10,11... | collective-permute-start | bytes 786440 | tf_op jit(solution)/shard_map/ppermute | solution.py:65
  174.6 26.2 %collective-permute-start.20 = (f32[2,8,64,64]{3,2,1,0:T(8,128)}, f32[2,8,64,64]{3,2,1,0:T(8,128)}, u32[]{:S(2)}, u32[]{:S(2)}) collective-permute-start(f32[2,8,64,64]{3,2,1,0:T(8,128)} %add.135), channel_id=1, source_target_pairs={{0,2},{1,3},{2,0},{3,1},{4,6},{5,7},{6,4},{7,5},{8,10},{9,11},{10,... | collective-permute-start | bytes 786440 | tf_op jit(solution)/shard_map/ppermute | solution.py:65
  194.4 8.4 %copy-start.1 = (bf16[64,256]{1,0:T(8,128)(2,1)S(1)}, bf16[64,256]{1,0:T(8,128)(2,1)}, u32[]{:S(2)}) copy-start(bf16[64,256]{1,0:T(8,128)(2,1)} %param.9) | copy-start | bytes 98308
Sparse Core Ops, SparseCore 0:
  21.9 25.6 reduce-scatter.2
  94.9 25.1 reduce-scatter.4

commit v4 on v3

--- a/solution.py
+++ b/solution.py
@@ -78,33 +78,31 @@
     return padded_2(x_wide, (("gy", 1), ("gz", 0)), 1, False)
 
 
-def stencil_kernel(chunk, x_pad, planes, y_cells, p_ref, w_ref, o_ref, s_ref):
-    s_ref[...] = p_ref[...].astype(jnp.float32)
+def stencil_kernel(chunk, x_pad, planes, y_cells, rows, p_ref, w_ref, o_ref):
     width = chunk + 2 * x_pad
     count = o_ref.shape[2] // chunk
+    shift = chunk + x_pad - x_pad // 2
 
     def body(index, carry):
         base = pl.multiple_of(index * chunk, chunk)
         for plane in range(planes):
-            left = jnp.zeros((y_cells, chunk + x_pad), jnp.float32)
-            centre = jnp.zeros((y_cells, chunk), jnp.float32)
-            right = jnp.zeros((y_cells, chunk + x_pad), jnp.float32)
-            for step_z in range(3):
-                for step_y in range(3):
-                    window = s_ref[plane + step_z, pl.ds(step_y, y_cells), pl.ds(base, width)]
-                    tap = 9 * step_z + 3 * step_y
-                    left = left + window[:, : chunk + x_pad] * w_ref[tap : tap + 1, : chunk + x_pad]
-                    centre = centre + window[:, x_pad : x_pad + chunk] * w_ref[
-                        tap + 1 : tap + 2, :chunk
-                    ]
-                    right = right + window[:, x_pad:] * w_ref[tap + 2 : tap + 3, : chunk + x_pad]
-            shift = chunk + x_pad - x_pad // 2
-            total = (
-                centre
-                + pltpu.roll(left, shift, 1)[:, :chunk]
-                + pltpu.roll(right, shift, 1)[:, :chunk]
-            )
-            o_ref[plane, :, pl.ds(base, chunk)] = total.astype(o_ref.dtype)
+            for row in range(0, y_cells, rows):
+                left = jnp.zeros((rows, chunk + x_pad), jnp.float32)
+                centre = jnp.zeros((rows, chunk), jnp.float32)
+                right = jnp.zeros((rows, chunk + x_pad), jnp.float32)
+                for step_z in range(3):
+                    for step_y in range(3):
+                        window = p_ref[plane + step_z, pl.ds(row + step_y, rows), pl.ds(base, width)]
+                        tap = 9 * step_z + 3 * step_y
+                        left = left + window[:, : chunk + x_pad] * w_ref[tap, :, : chunk + x_pad]
+                        centre = centre + window[:, x_pad : x_pad + chunk] * w_ref[tap + 1, :, :chunk]
+                        right = right + window[:, x_pad:] * w_ref[tap + 2, :, : chunk + x_pad]
+                total = (
+                    centre
+                    + pltpu.roll(left, shift, 1)[:, :chunk]
+                    + pltpu.roll(right, shift, 1)[:, :chunk]
+                )
+                o_ref[plane, pl.ds(row, rows), pl.ds(base, chunk)] = total.astype(o_ref.dtype)
         return carry
 
     lax.fori_loop(0, count, body, 0)
@@ -115,16 +113,17 @@
     y_cells = padded.shape[1] - 2
     x_pad = 2 * channels
     lanes = x_cells * channels
-    chunk = min(512, lanes)
+    chunk = min(2048, lanes)
+    rows = 8 if y_cells % 8 == 0 else y_cells
     if flipped:
         taps = taps[::-1]
     gains = jnp.tile(taps.astype(jnp.float32), (1, (chunk + x_pad) // channels))
-    kernel = functools.partial(stencil_kernel, chunk, x_pad, planes, y_cells)
+    gains = jnp.broadcast_to(gains[:, None, :], (gains.shape[0], rows, gains.shape[1]))
+    kernel = functools.partial(stencil_kernel, chunk, x_pad, planes, y_cells, rows)
     return pl.pallas_call(
         kernel,
         out_shape=jax.ShapeDtypeStruct((planes, y_cells, lanes), out_dtype),
-        scratch_shapes=[pltpu.VMEM(padded.shape, jnp.float32)],
-    )(padded, gains)
+    )(padded.astype(jnp.float32), gains)
 
 
 def share_terms(field3, cos_table, sin_table):
@@ -152,7 +151,8 @@
 
 
 def sum_gradients(local_grads):
-    return butterfly_sum(butterfly_sum(local_grads, "gy"), "gz")
+    flat = local_grads.reshape(-1, 1024)
+    return butterfly_sum(butterfly_sum(flat, "gy"), "gz").reshape(local_grads.shape)
 
 
 def per_device(

time: 211 us -> 209 us (level)
  waiting for transfers between devices: 45.6 us -> 38.5 us
  Pallas kernels: 26.1 us -> 29.5 us
  local copies, waits for them, and re-layouts: 38.6 us -> 41.5 us
    ppermute x3, waiting for transfers between devices: 23.2 us -> 14.6 us  [butterfly_sum(): lax.ppermute(value, axis, [(i, i ^ step) for i in range(size)])]
    convert_element_type x0 -> x2, other arithmetic: none -> 8.48 us  [depthwise(): padded.astype(jnp.float32)]
    concatenate x4 -> x2, other arithmetic: 7.65 us -> 1.22 us  [padded_2(): value = jnp.concatenate([before, value, after], axis=dim)]
    pallas_call x2, Pallas kernels: 26.1 us -> 29.5 us  [depthwise(): pl.pallas_call(kernel, out_shape=jax.ShapeDtypeStruct((planes, y_cells, l...]
    add x3, other arithmetic: 4.97 us -> 2.07 us  [butterfly_sum(): value + lax.ppermute(value, axis, [(i, i ^ step) for i in range(size)])]
    broadcast_in_dim x0 -> x2, local copies, waits for them, and re-layouts: none -> 2.84 us  [depthwise(): jnp.broadcast_to(gains[:, None, :], (gains.shape[0], rows, gains.shape[1]))]
    unnamed x34 -> x40, local copies, waits for them, and re-layouts: 5.99 us -> 5.34 us
  transfers between devices with their start and end apart: 23 -> 23, of which waited for: 7 -> 6; matrix products, arithmetic and copies ran while one was open for 29% -> 30% of each run, Pallas kernels for 12% -> 14%
where the time goes in v4:
time: 209 us; the launch traced here: 208 us
  local copies, waits for them, and re-layouts  41.5 us (20%)
  starting transfers between devices  41.3 us (20%)
  waiting for transfers between devices  38.5 us (18%)
  Pallas kernels  29.5 us (14%)
  matrix products  21.7 us (10%)
  other arithmetic  21.2 us (10%)
  between operations  14.6 us (7%)
    pallas_call x2, Pallas kernels, depthwise(): pl.pallas_call(kernel, out_shape=jax.ShapeDtypeStruct((planes, y_cells, l...  29.5 us
    ppermute x6, starting transfers between devices, padded_2(): before = lax.ppermute(last, axis, up)  21.6 us
    reduce_scatter x2, waiting for transfers between devices, share_terms(): lax.psum_scatter(jnp.concatenate([real_part, imag_part], axis=2), 'gx', s...  15.4 us
    ppermute x3, waiting for transfers between devices, butterfly_sum(): lax.ppermute(value, axis, [(i, i ^ step) for i in range(size)])  14.6 us
    convert_element_type x2, other arithmetic, depthwise(): padded.astype(jnp.float32)  8.48 us
    ppermute x6, starting transfers between devices, ring_gather(): lax.ppermute(block, axis, [(i, (i + shift) % size) for i in range(size)])  8.12 us
    dot_general x1, matrix products, per_device(): jnp.dot(grad_hidden, expand_weight.T, preferred_element_type=jnp.float32)  7.82 us
    ppermute x6, starting transfers between devices, padded_2(): after = lax.ppermute(leading, axis, down)  7.53 us
  transfers between devices with their start and end apart: 23, of which 6 were waited for; matrix products, arithmetic and copies ran while one was open for 30% of the time, Pallas kernels for 14%

profile of v4, /device:TPU:0, one launch (start us, length us, event | category | flops | bytes accessed | tf_op | source)
XLA Modules:
  0.0 208.3 jit_solution(11854864056463909178)
XLA Ops:
  7.9 2.9 %collective-permute-start = (bf16[2,16,128]{2,1,0:T(8,128)(2,1)S(1)}, bf16[2,16,128]{2,1,0:T(8,128)(2,1)S(1)}, u32[]{:S(2)}, u32[]{:S(2)}) collective-permute-start(bf16[2,16,128]{2,1,0:T(8,128)(2,1)S(1)} %get-tuple-element.26), channel_id=1, source_target_pairs={{0,8},{8,16},{16,24},{24,0},{1,9},{9,17},{17,25},{25,1},{2,10},{10... | collective-permute-start | bytes 24584 | tf_op jit(solution)/shard_map/ppermute | solution.py:19
  11.8 3.0 %reshape.101 = bf16[32,256,64]{2,1,0:T(8,128)(2,1)S(1)} reshape(bf16[2,16,16384]{2,1,0:T(8,128)(2,1)} %param.7) | data formatting | bytes 2097152 | tf_op jit(solution)/shard_map/reshape | solution.py:182
  16.4 1.3 collective-permute-start.3
  17.7 3.0 %collective-permute-start.2 = (bf16[2,1,16640]{2,1,0:T(2,128)(2,1)S(1)}, bf16[2,1,16640]{2,1,0:T(2,128)(2,1)S(1)}, u32[]{:S(2)}, u32[]{:S(2)}) collective-permute-start(bf16[2,1,16640]{2,1,0:T(2,128)(2,1)S(1)} %get-tuple-element.21), channel_id=1, source_target_pairs={{0,4},{1,5},{2,6},{3,7},{8,12},{9,13},{10,14},{11,15},{16,20},{17,... | collective-permute-start | bytes 199688 | tf_op jit(solution)/shard_map/ppermute | solution.py:19
  23.1 1.3 fusion.96
  24.4 1.3 collective-permute-start.5
  25.7 5.6 %collective-permute-start.4 = (bf16[1,18,16640]{2,1,0:T(8,128)(2,1)}, bf16[1,18,16640]{2,1,0:T(8,128)(2,1)}, u32[]{:S(2)}, u32[]{:S(2)}) collective-permute-start(bf16[1,18,16640]{2,1,0:T(8,128)(2,1)} %get-tuple-element.17), channel_id=1, source_target_pairs={{0,1},{1,2},{2,3},{4,5},{5,6},{6,7},{8,9},{9,10},{10,11},{12,13},{... | collective-permute-start | bytes 1797128 | tf_op jit(solution)/shard_map/ppermute | solution.py:19
  31.3 3.2 %reshape.110 = f32[32,256,64]{2,1,0:T(8,128)} reshape(bf16[2,16,16384]{2,1,0:T(8,128)(2,1)S(1)} %copy-done.8) | data formatting | bytes 3145728 | tf_op jit(solution)/shard_map/convert_element_type | solution.py:202
  34.5 3.8 %copy.30 = f32[32,256,64]{1,2,0:T(8,128)} copy(f32[32,256,64]{2,1,0:T(8,128)} %reshape.110) | data formatting | bytes 4194304 | tf_op jit(solution)/shard_map/convert_element_type | solution.py:202
  39.8 1.1 fusion.13
  41.0 5.9 %collective-permute-done.5 = bf16[1,18,16640]{2,1,0:T(8,128)(2,1)} collective-permute-done((bf16[1,18,16640]{2,1,0:T(8,128)(2,1)}, bf16[1,18,16640]{2,1,0:T(8,128)(2,1)}, u32[]{:S(2)}, u32[]{:S(2)}) %collective-permute-start.5) | collective-permute-done | bytes 599072 | tf_op jit(solution)/shard_map/ppermute | solution.py:20
  46.9 1.2 collective-permute-done.4
  48.0 4.2 %maximum_convert_fusion.p_ref = f32[4,18,16640]{2,1,0:T(8,128)} fusion(bf16[1,18,16640]{2,1,0:T(8,128)(2,1)} %collective-permute-done.5, bf16[2,1,16640]{2,1,0:T(2,128)(2,1)S(1)} %collective-permute-done.3, bf16[2,16,16640]{2,1,0:T(8,128)(2,1)S(1)} %constant_dynamic-update-slice_fusion, bf16[2,1,16640]{2,1,0:T(2,128)(2,1)} %copy-done.12, ...), kind=kLoop, calls=%fused_computation.11 | loop fusion | flops 11980800 | bytes 7188480 | tf_op jit(solution)/shard_map/convert_element_type | solution.py:126
  52.3 1.5 broadcast_in_dim.18.w_ref
  53.7 14.6 %shard_map.94 = bf16[2,16,16384]{2,1,0:T(8,128)(2,1)} custom-call(f32[4,18,16640]{2,1,0:T(8,128)} %maximum_convert_fusion.p_ref, f32[27,8,2176]{2,1,0:T(8,128)} %broadcast_in_dim.18.w_ref), custom_call_target="tpu_custom_call" | custom-call | tf_op jit(solution)/shard_map/pallas_call | solution.py:123
  70.8 1.5 collective-permute-start.7
  72.3 2.3 %collective-permute-start.8 = (bf16[8,32,128]{2,1,0:T(8,128)(2,1)}, bf16[8,32,128]{2,1,0:T(8,128)(2,1)}, u32[]{:S(2)}, u32[]{:S(2)}) collective-permute-start(bf16[8,32,128]{2,1,0:T(8,128)(2,1)} %convolution_convert_fusion.2), channel_id=1, source_target_pairs={{0,24},{8,0},{16,8},{24,16},{1,25},{9,1},{17,9},{25,17},{2,26},{10... | collective-permute-start | bytes 196616 | tf_op jit(solution)/shard_map/ppermute | solution.py:55
  74.6 3.0 %reshape.102 = bf16[8192,64]{1,0:T(8,128)(2,1)S(1)} reshape(bf16[2,16,16384]{2,1,0:T(8,128)(2,1)} %shard_map.94) | data formatting | bytes 2097152 | tf_op jit(solution)/shard_map/reshape | solution.py:191
  77.7 1.2 fusion.103
  78.9 2.8 %fusion.5 = f32[8192,64]{0,1:T(8,128)S(1)} fusion(bf16[256,64]{0,1:T(8,128)(2,1)S(1)} %copy-done.14, f32[8192,256]{1,0:T(8,128)S(1)} %fusion.103), kind=kOutput, calls=%fused_computation.10 | convolution fusion | flops 278921216 | bytes 10518528 | tf_op jit(solution)/shard_map/dot_general | solution.py:194
  86.5 2.7 %fusion.11 = (bf16[32,256,64]{1,2,0:T(8,128)(2,1)S(1)}, bf16[32,256,64]{1,2,0:T(8,128)(2,1)}) fusion(f32[32,256,64]{1,2,0:T(8,128)S(1)} %copy-done.3, f32[256,32,64]{0,2,1:T(8,128)S(1)} %fusion.20, bf16[32,32,64]{2,1,0:T(8,128)(2,1)S(1)} %get-tuple-element.31, f32[32]{0:T(128)S(1)} %get-tuple-element.33, s32[32]{0:T(128)S(1)} %add.121, ...), kind=kOutput, calls=%fused_computation.19 | convolution fusion | flops 41041920 | bytes 8520960 | tf_op jit(solution)/shard_map/krc,xk->rxc/dot_general | solution.py:139
  89.2 1.4 fusion.45
  90.7 1.4 fusion.42
  92.1 2.0 copy.29
  94.1 2.5 %reshape.104 = bf16[2,16,16384]{2,1,0:T(8,128)(2,1)} reshape(bf16[32,256,64]{2,1,0:T(8,128)(2,1)S(1)} %copy.29) | data formatting | bytes 2097152 | tf_op jit(solution)/shard_map/reshape | solution.py:200
  96.6 2.2 %pad_maximum_fusion.3 = f32[32,32,128]{2,0,1:T(8,128)} fusion(f32[32,32,64]{2,0,1:T(8,128)} %fusion.45, f32[32,32,64]{2,0,1:T(8,128)} %fusion.42), kind=kLoop, calls=%fused_computation.34 | loop fusion | flops 131072 | bytes 1048576 | tf_op jit(solution)/shard_map/concatenate | solution.py:133
  98.9 7.8 %convolution_convert_fusion = bf16[8192,64]{0,1:T(8,128)(2,1)S(1)} fusion(bf16[64,256]{1,0:T(8,128)(2,1)S(1)} %copy-done, bf16[8192,64]{0,1:T(8,128)(2,1)S(1)} %bitcast.55, bf16[256,64]{0,1:T(8,128)(2,1)S(1)} %copy-done.14, f32[8192,256]{1,0:T(8,128)} %copy-done.2), kind=kOutput, calls=%fused_computation.3 | convolution fusion | flops 558366720 | bytes 10551296 | tf_op jit(solution)/shard_map/dot_general | solution.py:210
  106.8 1.1 copy.35
  107.8 1.7 reshape.106
  109.5 15.4 %reduce-scatter.5.cloned.1.call-done = f32[8,32,128]{2,0,1:T(8,128)} async-done(((f32[32,32,128]{2,0,1:T(8,128)}), f32[8,32,128]{2,0,1:T(8,128)}) %reduce-scatter.5.cloned.1.call-update) | async-done | bytes 131088 | tf_op jit(solution)/shard_map/reduce_scatter | solution.py:132
  126.7 1.5 collective-permute-start.9
  128.2 1.5 collective-permute-start.15
  130.2 1.5 collective-permute-start.17
  131.7 1.4 collective-permute-start.10
  133.4 1.3 constant_dynamic-update-slice_fusion.8
  135.6 1.3 collective-permute-start.12
  136.9 3.0 %collective-permute-start.11 = (bf16[2,1,16640]{2,1,0:T(2,128)(2,1)S(1)}, bf16[2,1,16640]{2,1,0:T(2,128)(2,1)S(1)}, u32[]{:S(2)}, u32[]{:S(2)}) collective-permute-start(bf16[2,1,16640]{2,1,0:T(2,128)(2,1)S(1)} %get-tuple-element.19), channel_id=1, source_target_pairs={{0,4},{1,5},{2,6},{3,7},{8,12},{9,13},{10,14},{11,15},{16,20},{17,... | collective-permute-start | bytes 199688 | tf_op jit(solution)/shard_map/ppermute | solution.py:19
  141.5 1.3 fusion.95
  142.8 1.3 collective-permute-start.14
  144.1 5.5 %collective-permute-start.13 = (bf16[1,18,16640]{2,1,0:T(8,128)(2,1)}, bf16[1,18,16640]{2,1,0:T(8,128)(2,1)}, u32[]{:S(2)}, u32[]{:S(2)}) collective-permute-start(bf16[1,18,16640]{2,1,0:T(8,128)(2,1)} %get-tuple-element.15), channel_id=1, source_target_pairs={{0,1},{1,2},{2,3},{4,5},{5,6},{6,7},{8,9},{9,10},{10,11},{12,13},{... | collective-permute-start | bytes 1797128 | tf_op jit(solution)/shard_map/ppermute | solution.py:19
  151.5 2.7 %copy.38 = f32[32,256,64]{2,1,0:T(8,128)} copy(f32[32,256,64]{1,2,0:T(8,128)S(1)} %add_bitcast_fusion) | data formatting | bytes 4194304 | tf_op jit(solution)/shard_map/add | solution.py:142
  154.3 2.9 %reshape.107 = f32[2,16,16384]{2,1,0:T(8,128)S(1)} reshape(f32[32,256,64]{2,1,0:T(8,128)} %copy.38) | data formatting | bytes 4194304 | tf_op jit(solution)/shard_map/reshape | solution.py:225
  157.2 14.6 %collective-permute-done.19 = f32[64,1024]{1,0:T(8,128)} collective-permute-done((f32[64,1024]{1,0:T(8,128)S(1)}, f32[64,1024]{1,0:T(8,128)}, u32[]{:S(2)}, u32[]{:S(2)}) %collective-permute-start.19) | collective-permute-done | bytes 262176 | tf_op jit(solution)/shard_map/ppermute | solution.py:65
  172.8 3.3 %collective-permute-start.20 = (f32[64,1024]{1,0:T(8,128)S(1)}, f32[64,1024]{1,0:T(8,128)}, u32[]{:S(2)}, u32[]{:S(2)}) collective-permute-start(f32[64,1024]{1,0:T(8,128)S(1)} %add.135), channel_id=1, source_target_pairs={{0,2},{1,3},{2,0},{3,1},{4,6},{5,7},{6,4},{7,5},{8,10},{9,11},{10,... | collective-permute-start | bytes 786440 | tf_op jit(solution)/shard_map/ppermute | solution.py:65
  176.1 4.3 %maximum_convert_fusion.1.p_ref = f32[4,18,16640]{2,1,0:T(8,128)} fusion(bf16[1,18,16640]{2,1,0:T(8,128)(2,1)} %collective-permute-done.14, bf16[2,1,16640]{2,1,0:T(2,128)(2,1)} %copy-done.10, bf16[2,16,16640]{2,1,0:T(8,128)(2,1)S(1)} %constant_dynamic-update-slice_fusion.7, bf16[2,1,16640]{2,1,0:T(2,128)(2,1)} %copy-done.11, ...), kind=kLoop, calls=%fused_computation.12 | loop fusion | flops 11980800 | bytes 7188480 | tf_op jit(solution)/shard_map/convert_element_type | solution.py:126
  180.4 1.4 broadcast_in_dim.36.w_ref
  181.8 14.9 %shard_map.95 = f32[2,16,16384]{2,1,0:T(8,128)} custom-call(f32[4,18,16640]{2,1,0:T(8,128)} %maximum_convert_fusion.1.p_ref, f32[27,8,2176]{2,1,0:T(8,128)} %broadcast_in_dim.36.w_ref), custom_call_target="tpu_custom_call" | custom-call | tf_op jit(solution)/shard_map/pallas_call | solution.py:123
  196.7 2.8 %add_convert_fusion = bf16[2,16,16384]{2,1,0:T(8,128)(2,1)} fusion(f32[2,16,16384]{2,1,0:T(8,128)} %shard_map.95, f32[2,16,16384]{2,1,0:T(8,128)S(1)} %reshape.107), kind=kLoop, calls=%fused_computation.21 | loop fusion | flops 1048576 | bytes 5242880 | tf_op jit(solution)/shard_map/convert_element_type | solution.py:225
  (109 shorter events, 24.1 us)
Async XLA Ops:
  7.2 70.5 %copy-start = (bf16[64,256]{1,0:T(8,128)(2,1)S(1)}, bf16[64,256]{1,0:T(8,128)(2,1)}, u32[]{:S(2)}) copy-start(bf16[64,256]{1,0:T(8,128)(2,1)} %param.9) | copy-start | bytes 98308
  7.2 61.1 %reduce-scatter.3.cloned.1.call-start = ((), (), s32[]{:S(2)}) async-start(), calls=%async_computation.2 | async-start | bytes 655360 | tf_op jit(solution)/shard_map/reduce_scatter | solution.py:132
  7.9 8.1 %collective-permute-start = (bf16[2,16,128]{2,1,0:T(8,128)(2,1)S(1)}, bf16[2,16,128]{2,1,0:T(8,128)(2,1)S(1)}, u32[]{:S(2)}, u32[]{:S(2)}) collective-permute-start(bf16[2,16,128]{2,1,0:T(8,128)(2,1)S(1)} %get-tuple-element.26), channel_id=1, source_target_pairs={{0,8},{8,16},{16,24},{24,0},{1,9},{9,17},{17,25},{25,1},{2,10},{10... | collective-permute-start | bytes 24584 | tf_op jit(solution)/shard_map/ppermute | solution.py:19
  10.9 5.3 %collective-permute-start.1 = (bf16[2,16,128]{2,1,0:T(8,128)(2,1)S(1)}, bf16[2,16,128]{2,1,0:T(8,128)(2,1)S(1)}, u32[]{:S(2)}, u32[]{:S(2)}) collective-permute-start(bf16[2,16,128]{2,1,0:T(8,128)(2,1)S(1)} %get-tuple-element.25), channel_id=1, source_target_pairs={{8,0},{16,8},{24,16},{0,24},{9,1},{17,9},{25,17},{1,25},{10,2},{18... | collective-permute-start | bytes 24584 | tf_op jit(solution)/shard_map/ppermute | solution.py:20
  14.9 1.2 copy-start.4
  16.4 5.4 %collective-permute-start.3 = (bf16[2,1,16640]{2,1,0:T(2,128)(2,1)S(1)}, bf16[2,1,16640]{2,1,0:T(2,128)(2,1)S(1)}, u32[]{:S(2)}, u32[]{:S(2)}) collective-permute-start(bf16[2,1,16640]{2,1,0:T(2,128)(2,1)S(1)} %get-tuple-element.22), channel_id=1, source_target_pairs={{4,0},{5,1},{6,2},{7,3},{12,8},{13,9},{14,10},{15,11},{20,16},{21,... | collective-permute-start | bytes 199688 | tf_op jit(solution)/shard_map/ppermute | solution.py:20
  17.7 4.1 %collective-permute-start.2 = (bf16[2,1,16640]{2,1,0:T(2,128)(2,1)S(1)}, bf16[2,1,16640]{2,1,0:T(2,128)(2,1)S(1)}, u32[]{:S(2)}, u32[]{:S(2)}) collective-permute-start(bf16[2,1,16640]{2,1,0:T(2,128)(2,1)S(1)} %get-tuple-element.21), channel_id=1, source_target_pairs={{0,4},{1,5},{2,6},{3,7},{8,12},{9,13},{10,14},{11,15},{16,20},{17,... | collective-permute-start | bytes 199688 | tf_op jit(solution)/shard_map/ppermute | solution.py:19
  21.8 103.1 %reduce-scatter.5.cloned.1.call-start = ((), (), s32[]{:S(2)}) async-start(), calls=%async_computation.3 | async-start | bytes 655360 | tf_op jit(solution)/shard_map/reduce_scatter | solution.py:132
  21.9 0.6 copy-start.12
  23.1 8.1 %copy-start.8 = (bf16[2,16,16384]{2,1,0:T(8,128)(2,1)S(1)}, bf16[2,16,16384]{2,1,0:T(8,128)(2,1)}, u32[]{:S(2)}) copy-start(bf16[2,16,16384]{2,1,0:T(8,128)(2,1)} %param.13) | copy-start | bytes 3145732
  24.4 22.5 %collective-permute-start.5 = (bf16[1,18,16640]{2,1,0:T(8,128)(2,1)}, bf16[1,18,16640]{2,1,0:T(8,128)(2,1)}, u32[]{:S(2)}, u32[]{:S(2)}) collective-permute-start(bf16[1,18,16640]{2,1,0:T(8,128)(2,1)} %get-tuple-element.18), channel_id=1, source_target_pairs={{1,0},{2,1},{3,2},{5,4},{6,5},{7,6},{9,8},{10,9},{11,10},{13,12},{... | collective-permute-start | bytes 1797128 | tf_op jit(solution)/shard_map/ppermute | solution.py:20
  25.7 22.4 %collective-permute-start.4 = (bf16[1,18,16640]{2,1,0:T(8,128)(2,1)}, bf16[1,18,16640]{2,1,0:T(8,128)(2,1)}, u32[]{:S(2)}, u32[]{:S(2)}) collective-permute-start(bf16[1,18,16640]{2,1,0:T(8,128)(2,1)} %get-tuple-element.17), channel_id=1, source_target_pairs={{0,1},{1,2},{2,3},{4,5},{5,6},{6,7},{8,9},{9,10},{10,11},{12,13},{... | collective-permute-start | bytes 1797128 | tf_op jit(solution)/shard_map/ppermute | solution.py:19
  34.5 3.8 %copy-start.6 = (bf16[32,64,64]{2,1,0:T(8,128)(2,1)S(1)}, bf16[32,64,64]{2,1,0:T(8,128)(2,1)}, u32[]{:S(2)}) copy-start(bf16[32,64,64]{2,1,0:T(8,128)(2,1)} %param.12) | copy-start | bytes 786436
  34.5 4.0 %copy-start.13 = (bf16[27,64]{1,0:T(8,128)(2,1)S(1)}, bf16[27,64]{1,0:T(8,128)(2,1)}, u32[]{:S(2)}) copy-start(bf16[27,64]{1,0:T(8,128)(2,1)} %param.8) | copy-start | bytes 10372
  70.0 13.2 %collective-permute-start.6 = (bf16[8,32,128]{2,1,0:T(8,128)(2,1)}, bf16[8,32,128]{2,1,0:T(8,128)(2,1)}, u32[]{:S(2)}, u32[]{:S(2)}) collective-permute-start(bf16[8,32,128]{2,1,0:T(8,128)(2,1)} %convolution_convert_fusion.2), channel_id=1, source_target_pairs={{0,8},{8,16},{16,24},{24,0},{1,9},{9,17},{17,25},{25,1},{2,10},{10... | collective-permute-start | bytes 196616 | tf_op jit(solution)/shard_map/ppermute | solution.py:55
  70.8 13.3 %collective-permute-start.7 = (bf16[8,32,128]{2,1,0:T(8,128)(2,1)}, bf16[8,32,128]{2,1,0:T(8,128)(2,1)}, u32[]{:S(2)}, u32[]{:S(2)}) collective-permute-start(bf16[8,32,128]{2,1,0:T(8,128)(2,1)} %convolution_convert_fusion.2), channel_id=1, source_target_pairs={{0,16},{8,24},{16,0},{24,8},{1,17},{9,25},{17,1},{25,9},{2,18},{10... | collective-permute-start | bytes 196616 | tf_op jit(solution)/shard_map/ppermute | solution.py:55
  72.3 12.6 %collective-permute-start.8 = (bf16[8,32,128]{2,1,0:T(8,128)(2,1)}, bf16[8,32,128]{2,1,0:T(8,128)(2,1)}, u32[]{:S(2)}, u32[]{:S(2)}) collective-permute-start(bf16[8,32,128]{2,1,0:T(8,128)(2,1)} %convolution_convert_fusion.2), channel_id=1, source_target_pairs={{0,24},{8,0},{16,8},{24,16},{1,25},{9,1},{17,9},{25,17},{2,26},{10... | collective-permute-start | bytes 196616 | tf_op jit(solution)/shard_map/ppermute | solution.py:55
  77.7 1.2 copy-start.14
  78.9 3.3 %copy-start.2 = (f32[8192,256]{1,0:T(8,128)}, f32[8192,256]{1,0:T(8,128)S(1)}, u32[]{:S(2)}) copy-start(f32[8192,256]{1,0:T(8,128)S(1)} %fusion.103) | copy-start | bytes 25165828
  82.2 4.3 %copy-start.3 = (f32[32,256,64]{1,2,0:T(8,128)S(1)}, f32[32,256,64]{1,2,0:T(8,128)}, u32[]{:S(2)}) copy-start(f32[32,256,64]{1,2,0:T(8,128)} %copy.30) | copy-start | bytes 6291460
  109.5 23.8 %copy-start.5 = (bf16[2,16,16384]{2,1,0:T(8,128)(2,1)}, bf16[2,16,16384]{2,1,0:T(8,128)(2,1)S(1)}, u32[]{:S(2)}) copy-start(bf16[2,16,16384]{2,1,0:T(8,128)(2,1)S(1)} %reshape.106) | copy-start | bytes 3145732
  126.7 6.6 %collective-permute-start.9 = (bf16[2,16,128]{2,1,0:T(8,128)(2,1)S(1)}, bf16[2,16,128]{2,1,0:T(8,128)(2,1)S(1)}, u32[]{:S(2)}, u32[]{:S(2)}) collective-permute-start(bf16[2,16,128]{2,1,0:T(8,128)(2,1)S(1)} %get-tuple-element.24), channel_id=1, source_target_pairs={{0,8},{8,16},{16,24},{24,0},{1,9},{9,17},{17,25},{25,1},{2,10},{10... | collective-permute-start | bytes 24584 | tf_op jit(solution)/shard_map/ppermute | solution.py:19
  128.2 8.7 %collective-permute-start.15 = (bf16[8,32,128]{2,1,0:T(8,128)(2,1)S(1)}, bf16[8,32,128]{2,1,0:T(8,128)(2,1)S(1)}, u32[]{:S(2)}, u32[]{:S(2)}) collective-permute-start(bf16[8,32,128]{2,1,0:T(8,128)(2,1)S(1)} %convolution_convert_fusion.1), channel_id=1, source_target_pairs={{0,8},{8,16},{16,24},{24,0},{1,9},{9,17},{17,25},{25,1},{2,10},{10... | collective-permute-start | bytes 196616 | tf_op jit(solution)/shard_map/ppermute | solution.py:55
  129.6 10.3 %collective-permute-start.16 = (bf16[8,32,128]{2,1,0:T(8,128)(2,1)S(1)}, bf16[8,32,128]{2,1,0:T(8,128)(2,1)S(1)}, u32[]{:S(2)}, u32[]{:S(2)}) collective-permute-start(bf16[8,32,128]{2,1,0:T(8,128)(2,1)S(1)} %convolution_convert_fusion.1), channel_id=1, source_target_pairs={{0,16},{8,24},{16,0},{24,8},{1,17},{9,25},{17,1},{25,9},{2,18},{10... | collective-permute-start | bytes 196616 | tf_op jit(solution)/shard_map/ppermute | solution.py:55
  130.2 9.8 %collective-permute-start.17 = (bf16[8,32,128]{2,1,0:T(8,128)(2,1)S(1)}, bf16[8,32,128]{2,1,0:T(8,128)(2,1)S(1)}, u32[]{:S(2)}, u32[]{:S(2)}) collective-permute-start(bf16[8,32,128]{2,1,0:T(8,128)(2,1)S(1)} %convolution_convert_fusion.1), channel_id=1, source_target_pairs={{0,24},{8,0},{16,8},{24,16},{1,25},{9,1},{17,9},{25,17},{2,26},{10... | collective-permute-start | bytes 196616 | tf_op jit(solution)/shard_map/ppermute | solution.py:55
  131.7 3.7 %collective-permute-start.10 = (bf16[2,16,128]{2,1,0:T(8,128)(2,1)S(1)}, bf16[2,16,128]{2,1,0:T(8,128)(2,1)S(1)}, u32[]{:S(2)}, u32[]{:S(2)}) collective-permute-start(bf16[2,16,128]{2,1,0:T(8,128)(2,1)S(1)} %get-tuple-element.23), channel_id=1, source_target_pairs={{8,0},{16,8},{24,16},{0,24},{9,1},{17,9},{25,17},{1,25},{10,2},{18... | collective-permute-start | bytes 24584 | tf_op jit(solution)/shard_map/ppermute | solution.py:20
  133.3 16.9 %collective-permute-start.18 = (f32[64,1024]{1,0:T(8,128)S(1)}, f32[64,1024]{1,0:T(8,128)S(1)}, u32[]{:S(2)}, u32[]{:S(2)}) collective-permute-start(f32[64,1024]{1,0:T(8,128)S(1)} %reshape.108), channel_id=1, source_target_pairs={{0,4},{4,0},{1,5},{5,1},{2,6},{6,2},{3,7},{7,3},{8,12},{12,8},{9,1... | collective-permute-start | bytes 786440 | tf_op jit(solution)/shard_map/ppermute | solution.py:65
  135.6 4.6 %collective-permute-start.12 = (bf16[2,1,16640]{2,1,0:T(2,128)(2,1)S(1)}, bf16[2,1,16640]{2,1,0:T(2,128)(2,1)S(1)}, u32[]{:S(2)}, u32[]{:S(2)}) collective-permute-start(bf16[2,1,16640]{2,1,0:T(2,128)(2,1)S(1)} %get-tuple-element.20), channel_id=1, source_target_pairs={{4,0},{5,1},{6,2},{7,3},{12,8},{13,9},{14,10},{15,11},{20,16},{21,... | collective-permute-start | bytes 199688 | tf_op jit(solution)/shard_map/ppermute | solution.py:20
  136.9 4.0 %collective-permute-start.11 = (bf16[2,1,16640]{2,1,0:T(2,128)(2,1)S(1)}, bf16[2,1,16640]{2,1,0:T(2,128)(2,1)S(1)}, u32[]{:S(2)}, u32[]{:S(2)}) collective-permute-start(bf16[2,1,16640]{2,1,0:T(2,128)(2,1)S(1)} %get-tuple-element.19), channel_id=1, source_target_pairs={{0,4},{1,5},{2,6},{3,7},{8,12},{9,13},{10,14},{11,15},{16,20},{17,... | collective-permute-start | bytes 199688 | tf_op jit(solution)/shard_map/ppermute | solution.py:19
  140.2 2.6 %copy-start.10 = (bf16[2,1,16640]{2,1,0:T(2,128)(2,1)}, bf16[2,1,16640]{2,1,0:T(2,128)(2,1)S(1)}, u32[]{:S(2)}) copy-start(bf16[2,1,16640]{2,1,0:T(2,128)(2,1)S(1)} %collective-permute-done.12) | copy-start | bytes 199684
  140.9 1.9 copy-start.11
  142.8 33.4 %collective-permute-start.14 = (bf16[1,18,16640]{2,1,0:T(8,128)(2,1)}, bf16[1,18,16640]{2,1,0:T(8,128)(2,1)}, u32[]{:S(2)}, u32[]{:S(2)}) collective-permute-start(bf16[1,18,16640]{2,1,0:T(8,128)(2,1)} %get-tuple-element.16), channel_id=1, source_target_pairs={{1,0},{2,1},{3,2},{5,4},{6,5},{7,6},{9,8},{10,9},{11,10},{13,12},{... | collective-permute-start | bytes 1797128 | tf_op jit(solution)/shard_map/ppermute | solution.py:20
  144.1 32.1 %collective-permute-start.13 = (bf16[1,18,16640]{2,1,0:T(8,128)(2,1)}, bf16[1,18,16640]{2,1,0:T(8,128)(2,1)}, u32[]{:S(2)}, u32[]{:S(2)}) collective-permute-start(bf16[1,18,16640]{2,1,0:T(8,128)(2,1)} %get-tuple-element.15), channel_id=1, source_target_pairs={{0,1},{1,2},{2,3},{4,5},{5,6},{6,7},{8,9},{9,10},{10,11},{12,13},{... | collective-permute-start | bytes 1797128 | tf_op jit(solution)/shard_map/ppermute | solution.py:19
  150.3 1.2 copy-start.9
  150.3 21.4 %collective-permute-start.19 = (f32[64,1024]{1,0:T(8,128)S(1)}, f32[64,1024]{1,0:T(8,128)}, u32[]{:S(2)}, u32[]{:S(2)}) collective-permute-start(f32[64,1024]{1,0:T(8,128)S(1)} %add.134), channel_id=1, source_target_pairs={{0,1},{1,0},{2,3},{3,2},{4,5},{5,4},{6,7},{7,6},{8,9},{9,8},{10,11... | collective-permute-start | bytes 786440 | tf_op jit(solution)/shard_map/ppermute | solution.py:65
  172.8 7.6 %copy-start.7 = (f32[27,2176]{1,0:T(8,128)S(1)}, f32[27,2176]{1,0:T(8,128)}, u32[]{:S(2)}) copy-start(f32[27,2176]{1,0:T(8,128)} %tile.19) | copy-start | bytes 705028
  172.8 26.7 %collective-permute-start.20 = (f32[64,1024]{1,0:T(8,128)S(1)}, f32[64,1024]{1,0:T(8,128)}, u32[]{:S(2)}, u32[]{:S(2)}) collective-permute-start(f32[64,1024]{1,0:T(8,128)S(1)} %add.135), channel_id=1, source_target_pairs={{0,2},{1,3},{2,0},{3,1},{4,6},{5,7},{6,4},{7,5},{8,10},{9,11},{10,... | collective-permute-start | bytes 786440 | tf_op jit(solution)/shard_map/ppermute | solution.py:65
  196.7 4.7 %copy-start.1 = (bf16[64,256]{1,0:T(8,128)(2,1)S(1)}, bf16[64,256]{1,0:T(8,128)(2,1)}, u32[]{:S(2)}) copy-start(bf16[64,256]{1,0:T(8,128)(2,1)} %param.9) | copy-start | bytes 98308
Sparse Core Ops, SparseCore 0:
  21.9 25.6 reduce-scatter.2
  99.0 25.9 reduce-scatter.4

commit v5 on v4

--- a/solution.py
+++ b/solution.py
@@ -12,12 +12,19 @@
 def padded_2(value, sides, width, wrap):
     for axis, dim in sides:
         size, length = (lax.axis_size(axis), value.shape[dim])
-        up = [(i, (i + 1) % size) for i in range(size if wrap else size - 1)]
-        down = [(j, i) for i, j in up]
         last = lax.slice_in_dim(value, length - width, length, axis=dim)
         leading = lax.slice_in_dim(value, 0, width, axis=dim)
-        before = lax.ppermute(last, axis, up)
-        after = lax.ppermute(leading, axis, down)
+        if size == 2 and not wrap:
+            first = lax.axis_index(axis) == 0
+            swapped = lax.ppermute(jnp.where(first, last, leading), axis, [(0, 1), (1, 0)])
+            zeros = jnp.zeros_like(swapped)
+            before = jnp.where(first, zeros, swapped)
+            after = jnp.where(first, swapped, zeros)
+        else:
+            up = [(i, (i + 1) % size) for i in range(size if wrap else size - 1)]
+            down = [(j, i) for i, j in up]
+            before = lax.ppermute(last, axis, up)
+            after = lax.ppermute(leading, axis, down)
         value = jnp.concatenate([before, value, after], axis=dim)
     return value
 
@@ -217,10 +224,10 @@
     ).astype(jnp.bfloat16)
     dblock = jnp.einsum("krc,kro->kco", coeffs, dcoef, preferred_element_type=jnp.float32)
     local_grads = split_gradients(dblock, channels)
-    dmode, local_grads, grad_act = lax.optimization_barrier((dmode, local_grads, grad_act))
+    padded_grad = spatial_rims(grad_act, channels)
+    dmode, local_grads, padded_grad = lax.optimization_barrier((dmode, local_grads, padded_grad))
     spectral_grad = share_inverse(dmode, cos_order, sin_order, channels)
     grad_spec = sum_gradients(local_grads)
-    padded_grad = spatial_rims(grad_act, channels)
     grad_local = depthwise(padded_grad, depth_weight, True, x_cells, channels)
     grad_features = (grad_local + spectral_grad.reshape(planes, y_cells, merged)).astype(
         jnp.bfloat16

time: 209 us -> 217 us (1.038)
  local copies, waits for them, and re-layouts: 41.5 us -> 51.2 us
  starting transfers between devices: 41.3 us -> 34.3 us
  other arithmetic: 21.2 us -> 23.6 us
    ppermute x6 -> x4, waiting for transfers between devices: 6.55 us -> 18.9 us  [padded_2(): after = lax.ppermute(leading, axis, down)]
    reduce_scatter x2, waiting for transfers between devices: 15.4 us -> 6.87 us  [share_terms(): lax.psum_scatter(jnp.concatenate([real_part, imag_part], axis=2), 'gx', s...]
    ppermute x6 -> x4, starting transfers between devices: 21.6 us -> 14.7 us  [padded_2(): before = lax.ppermute(last, axis, up)]
    unnamed x40 -> x54, local copies, waits for them, and re-layouts: 5.34 us -> 10.5 us
    ppermute x3, waiting for transfers between devices: 14.6 us -> 10.2 us  [butterfly_sum(): lax.ppermute(value, axis, [(i, i ^ step) for i in range(size)])]
    concatenate x2 -> x3, other arithmetic: 1.22 us -> 4.79 us  [padded_2(): value = jnp.concatenate([before, value, after], axis=dim)]
    select_n x0 -> x4, other arithmetic: none -> 2.44 us  [the longest x2 1.36 us: padded_2(): before = jnp.where(first, zeros, swapped)]
    ppermute x6 -> x4, starting transfers between devices: 7.53 us -> 6.44 us  [padded_2(): after = lax.ppermute(leading, axis, down)]
  transfers between devices with their start and end apart: 23 -> 21, of which waited for: 6 -> 8; matrix products, arithmetic and copies ran while one was open for 30% -> 30% of each run, Pallas kernels for 14% -> 14%
where the time goes in v5:
time: 217 us; the launch traced here: 216 us
  local copies, waits for them, and re-layouts  51.2 us (24%)
  waiting for transfers between devices  39.5 us (18%)
  starting transfers between devices  34.3 us (16%)
  Pallas kernels  29.5 us (14%)
  other arithmetic  23.6 us (11%)
  matrix products  23.3 us (11%)
  between operations  14.5 us (7%)
    pallas_call x2, Pallas kernels, depthwise(): pl.pallas_call(kernel, out_shape=jax.ShapeDtypeStruct((planes, y_cells, l...  29.5 us
    ppermute x4, waiting for transfers between devices, padded_2(): after = lax.ppermute(leading, axis, down)  18.9 us
    ppermute x4, starting transfers between devices, padded_2(): before = lax.ppermute(last, axis, up)  14.7 us
    unnamed x54, local copies, waits for them, and re-layouts  10.5 us
    ppermute x3, waiting for transfers between devices, butterfly_sum(): lax.ppermute(value, axis, [(i, i ^ step) for i in range(size)])  10.2 us
    ppermute x6, starting transfers between devices, ring_gather(): lax.ppermute(block, axis, [(i, (i + shift) % size) for i in range(size)])  8.96 us
    dot_general x1, matrix products, per_device(): jnp.dot(grad_hidden, expand_weight.T, preferred_element_type=jnp.float32)  8.79 us
    convert_element_type x2, other arithmetic, depthwise(): padded.astype(jnp.float32)  7.31 us
  transfers between devices with their start and end apart: 21, of which 8 were waited for; matrix products, arithmetic and copies ran while one was open for 30% of the time, Pallas kernels for 14%

profile of v5, /device:TPU:0, one launch (start us, length us, event | category | flops | bytes accessed | tf_op | source)
XLA Modules:
  0.0 215.9 jit_solution(6808543675544643058)
XLA Ops:
  7.9 2.9 %collective-permute-start = (bf16[2,16,128]{2,1,0:T(8,128)(2,1)S(1)}, bf16[2,16,128]{2,1,0:T(8,128)(2,1)S(1)}, u32[]{:S(2)}, u32[]{:S(2)}) collective-permute-start(bf16[2,16,128]{2,1,0:T(8,128)(2,1)S(1)} %get-tuple-element.22), channel_id=1, source_target_pairs={{0,8},{8,16},{16,24},{24,0},{1,9},{9,17},{17,25},{25,1},{2,10},{10... | collective-permute-start | bytes 24584 | tf_op jit(solution)/shard_map/ppermute | solution.py:26
  11.8 3.0 %reshape.101 = bf16[32,256,64]{2,1,0:T(8,128)(2,1)S(1)} reshape(bf16[2,16,16384]{2,1,0:T(8,128)(2,1)} %param.7) | data formatting | bytes 2097152 | tf_op jit(solution)/shard_map/reshape | solution.py:189
  14.9 1.4 fusion.49
  16.3 1.3 fusion.51
  20.8 1.3 fusion.96
  22.0 1.3 collective-permute-start.4
  23.3 5.6 %collective-permute-start.3 = (bf16[1,18,16640]{2,1,0:T(8,128)(2,1)}, bf16[1,18,16640]{2,1,0:T(8,128)(2,1)}, u32[]{:S(2)}, u32[]{:S(2)}) collective-permute-start(bf16[1,18,16640]{2,1,0:T(8,128)(2,1)} %get-tuple-element.17), channel_id=1, source_target_pairs={{0,1},{1,2},{2,3},{4,5},{5,6},{6,7},{8,9},{9,10},{10,11},{12,13},{... | collective-permute-start | bytes 1797128 | tf_op jit(solution)/shard_map/ppermute | solution.py:26
  28.9 3.2 %reshape.110 = f32[32,256,64]{2,1,0:T(8,128)} reshape(bf16[2,16,16384]{2,1,0:T(8,128)(2,1)S(1)} %copy-done.13) | data formatting | bytes 3145728 | tf_op jit(solution)/shard_map/convert_element_type | solution.py:209
  32.2 3.8 %copy.30 = f32[32,256,64]{1,2,0:T(8,128)} copy(f32[32,256,64]{2,1,0:T(8,128)} %reshape.110) | data formatting | bytes 4194304 | tf_op jit(solution)/shard_map/convert_element_type | solution.py:209
  38.4 5.6 %collective-permute-done.4 = bf16[1,18,16640]{2,1,0:T(8,128)(2,1)} collective-permute-done((bf16[1,18,16640]{2,1,0:T(8,128)(2,1)}, bf16[1,18,16640]{2,1,0:T(8,128)(2,1)}, u32[]{:S(2)}, u32[]{:S(2)}) %collective-permute-start.4) | collective-permute-done | bytes 599072 | tf_op jit(solution)/shard_map/ppermute | solution.py:27
  44.0 1.2 collective-permute-done.3
  45.2 4.2 %maximum_convert_fusion.p_ref = f32[4,18,16640]{2,1,0:T(8,128)} fusion(bf16[1,18,16640]{2,1,0:T(8,128)(2,1)} %collective-permute-done.4, bf16[2,1,16640]{2,1,0:T(2,128)(2,1)S(1)} %get-tuple-element.32, bf16[2,16,16640]{2,1,0:T(8,128)(2,1)S(1)} %constant_dynamic-update-slice_fusion, bf16[2,1,16640]{2,1,0:T(2,128)(2,1)S(1)} %get-tuple-element.31, ...), kind=kLoop, calls=%fused_computation.11 | loop fusion | flops 11980800 | bytes 7188480 | tf_op jit(solution)/shard_map/convert_element_type | solution.py:133
  49.3 1.5 broadcast_in_dim.18.w_ref
  50.8 14.6 %shard_map.94 = bf16[2,16,16384]{2,1,0:T(8,128)(2,1)} custom-call(f32[4,18,16640]{2,1,0:T(8,128)} %maximum_convert_fusion.p_ref, f32[27,8,2176]{2,1,0:T(8,128)} %broadcast_in_dim.18.w_ref), custom_call_target="tpu_custom_call" | custom-call | tf_op jit(solution)/shard_map/pallas_call | solution.py:130
  67.8 1.5 collective-permute-start.6
  69.4 2.3 %collective-permute-start.7 = (bf16[8,32,128]{2,1,0:T(8,128)(2,1)}, bf16[8,32,128]{2,1,0:T(8,128)(2,1)}, u32[]{:S(2)}, u32[]{:S(2)}) collective-permute-start(bf16[8,32,128]{2,1,0:T(8,128)(2,1)} %convolution_convert_fusion.2), channel_id=1, source_target_pairs={{0,24},{8,0},{16,8},{24,16},{1,25},{9,1},{17,9},{25,17},{2,26},{10... | collective-permute-start | bytes 196616 | tf_op jit(solution)/shard_map/ppermute | solution.py:62
  71.7 3.0 %reshape.102 = bf16[8192,64]{1,0:T(8,128)(2,1)S(1)} reshape(bf16[2,16,16384]{2,1,0:T(8,128)(2,1)} %shard_map.94) | data formatting | bytes 2097152 | tf_op jit(solution)/shard_map/reshape | solution.py:198
  74.7 1.2 fusion.101
  76.0 2.8 %fusion.5 = f32[8192,64]{0,1:T(8,128)S(1)} fusion(bf16[256,64]{0,1:T(8,128)(2,1)S(1)} %copy-done.20, f32[8192,256]{1,0:T(8,128)S(1)} %fusion.101), kind=kOutput, calls=%fused_computation.10 | convolution fusion | flops 278921216 | bytes 10518528 | tf_op jit(solution)/shard_map/dot_general | solution.py:201
  83.6 2.7 %fusion.11 = (bf16[32,256,64]{1,2,0:T(8,128)(2,1)S(1)}, bf16[32,256,64]{1,2,0:T(8,128)(2,1)}) fusion(f32[32,256,64]{1,2,0:T(8,128)S(1)} %copy-done.3, f32[256,32,64]{0,2,1:T(8,128)S(1)} %fusion.20, bf16[32,32,64]{2,1,0:T(8,128)(2,1)S(1)} %get-tuple-element.27, f32[32]{0:T(128)S(1)} %get-tuple-element.33, s32[32]{0:T(128)S(1)} %add.121, ...), kind=kOutput, calls=%fused_computation.19 | convolution fusion | flops 41041920 | bytes 8520960 | tf_op jit(solution)/shard_map/krc,xk->rxc/dot_general | solution.py:146
  87.1 8.8 %convolution_convert_fusion = bf16[8192,64]{0,1:T(8,128)(2,1)} fusion(bf16[64,256]{1,0:T(8,128)(2,1)S(1)} %copy-done, bf16[8192,64]{0,1:T(8,128)(2,1)S(1)} %bitcast.55, bf16[256,64]{0,1:T(8,128)(2,1)S(1)} %copy-done.21, f32[8192,256]{1,0:T(8,128)} %copy-done.2), kind=kOutput, calls=%fused_computation.3 | convolution fusion | flops 558366720 | bytes 10551296 | tf_op jit(solution)/shard_map/dot_general | solution.py:217
  95.9 2.0 copy.35
  97.9 2.5 %reshape.106 = bf16[2,16,16384]{2,1,0:T(8,128)(2,1)} reshape(bf16[8192,64]{1,0:T(8,128)(2,1)S(1)} %copy.35) | data formatting | bytes 2097152 | tf_op jit(solution)/shard_map/reshape | solution.py:220
  101.1 2.9 %collective-permute-start.9 = (bf16[2,16,128]{2,1,0:T(8,128)(2,1)S(1)}, bf16[2,16,128]{2,1,0:T(8,128)(2,1)S(1)}, u32[]{:S(2)}, u32[]{:S(2)}) collective-permute-start(bf16[2,16,128]{2,1,0:T(8,128)(2,1)S(1)} %get-tuple-element.19), channel_id=1, source_target_pairs={{8,0},{16,8},{24,16},{0,24},{9,1},{17,9},{25,17},{1,25},{10,2},{18... | collective-permute-start | bytes 24584 | tf_op jit(solution)/shard_map/ppermute | solution.py:27
  104.0 1.6 collective-permute-done.8
  105.7 1.3 constant_dynamic-update-slice_fusion.8
  109.8 2.0 copy.29
  111.8 2.5 %reshape.104 = bf16[2,16,16384]{2,1,0:T(8,128)(2,1)} reshape(bf16[32,256,64]{2,1,0:T(8,128)(2,1)S(1)} %copy.29) | data formatting | bytes 2097152 | tf_op jit(solution)/shard_map/reshape | solution.py:207
  114.3 1.1 broadcast_select_fusion.1
  115.5 1.9 pad_maximum_fusion.2
  117.4 1.3 fusion.95
  118.7 1.3 collective-permute-start.12
  120.0 6.1 %collective-permute-start.11 = (bf16[1,18,16640]{2,1,0:T(8,128)(2,1)}, bf16[1,18,16640]{2,1,0:T(8,128)(2,1)}, u32[]{:S(2)}, u32[]{:S(2)}) collective-permute-start(bf16[1,18,16640]{2,1,0:T(8,128)(2,1)} %get-tuple-element.15), channel_id=1, source_target_pairs={{0,1},{1,2},{2,3},{4,5},{5,6},{6,7},{8,9},{9,10},{10,11},{12,13},{... | collective-permute-start | bytes 1797128 | tf_op jit(solution)/shard_map/ppermute | solution.py:26
  128.4 13.3 %collective-permute-done.12 = bf16[1,18,16640]{2,1,0:T(8,128)(2,1)S(1)} collective-permute-done((bf16[1,18,16640]{2,1,0:T(8,128)(2,1)}, bf16[1,18,16640]{2,1,0:T(8,128)(2,1)S(1)}, u32[]{:S(2)}, u32[]{:S(2)}) %collective-permute-start.12) | collective-permute-done | bytes 599072 | tf_op jit(solution)/shard_map/ppermute | solution.py:27
  143.3 2.2 %pad_maximum_fusion = bf16[4,18,16640]{2,1,0:T(8,128)(2,1)S(1)} fusion(bf16[1,18,16640]{2,1,0:T(8,128)(2,1)} %copy-done.14, bf16[2,1,16640]{2,1,0:T(2,128)(2,1)} %copy-done.10, bf16[2,16,16640]{2,1,0:T(8,128)(2,1)} %copy-done.4, bf16[2,1,16640]{2,1,0:T(2,128)(2,1)} %copy-done.9, bf16[1,18,16640]{2,1,0:T(8,128)(2,1)} %collective-permute-done.11), kind=kLoop, calls=%fused_computation.12 | loop fusion | flops 11980800 | bytes 4792320 | tf_op jit(solution)/shard_map/concatenate | solution.py:28
  145.5 6.9 %reduce-scatter.5.cloned.1.call-done = f32[8,32,128]{2,0,1:T(8,128)} async-done(((f32[32,32,128]{2,0,1:T(8,128)}), f32[8,32,128]{2,0,1:T(8,128)}) %reduce-scatter.5.cloned.1.call-update) | async-done | bytes 131088 | tf_op jit(solution)/shard_map/reduce_scatter | solution.py:139
  155.5 1.4 collective-permute-start.13
  157.5 2.3 %collective-permute-start.15 = (bf16[8,32,128]{2,1,0:T(8,128)(2,1)}, bf16[8,32,128]{2,1,0:T(8,128)(2,1)}, u32[]{:S(2)}, u32[]{:S(2)}) collective-permute-start(bf16[8,32,128]{2,1,0:T(8,128)(2,1)} %convolution_convert_fusion.1), channel_id=1, source_target_pairs={{0,24},{8,0},{16,8},{24,16},{1,25},{9,1},{17,9},{25,17},{2,26},{10... | collective-permute-start | bytes 196616 | tf_op jit(solution)/shard_map/ppermute | solution.py:62
  159.8 3.1 %convert_element_type.117.p_ref = f32[4,18,16640]{2,1,0:T(8,128)} convert(bf16[4,18,16640]{2,1,0:T(8,128)(2,1)S(1)} %pad_maximum_fusion) | non-fusion elementwise | flops 1198080 | bytes 7188480 | tf_op jit(solution)/shard_map/convert_element_type | solution.py:133
  163.0 1.2 reshape.108
  164.2 1.4 broadcast_in_dim.36.w_ref
  165.6 14.9 %shard_map.95 = f32[2,16,16384]{2,1,0:T(8,128)} custom-call(f32[4,18,16640]{2,1,0:T(8,128)} %convert_element_type.117.p_ref, f32[27,8,2176]{2,1,0:T(8,128)} %broadcast_in_dim.36.w_ref), custom_call_target="tpu_custom_call" | custom-call | tf_op jit(solution)/shard_map/pallas_call | solution.py:130
  184.8 1.5 collective-permute-start.17
  187.0 2.7 %copy.38 = f32[32,256,64]{2,1,0:T(8,128)} copy(f32[32,256,64]{1,2,0:T(8,128)S(1)} %add_bitcast_fusion) | data formatting | bytes 4194304 | tf_op jit(solution)/shard_map/add | solution.py:149
  189.7 2.9 %reshape.107 = f32[2,16,16384]{2,1,0:T(8,128)S(1)} reshape(f32[32,256,64]{2,1,0:T(8,128)} %copy.38) | data formatting | bytes 4194304 | tf_op jit(solution)/shard_map/reshape | solution.py:232
  193.6 2.5 %collective-permute-start.18 = (f32[64,1024]{1,0:T(8,128)S(1)}, f32[64,1024]{1,0:T(8,128)S(1)}, u32[]{:S(2)}, u32[]{:S(2)}) collective-permute-start(f32[64,1024]{1,0:T(8,128)S(1)} %add.135), channel_id=1, source_target_pairs={{0,2},{1,3},{2,0},{3,1},{4,6},{5,7},{6,4},{7,5},{8,10},{9,11},{10,... | collective-permute-start | bytes 786440 | tf_op jit(solution)/shard_map/ppermute | solution.py:72
  196.1 2.8 %add_convert_fusion = bf16[2,16,16384]{2,1,0:T(8,128)(2,1)} fusion(f32[2,16,16384]{2,1,0:T(8,128)} %shard_map.95, f32[2,16,16384]{2,1,0:T(8,128)S(1)} %reshape.107), kind=kLoop, calls=%fused_computation.21 | loop fusion | flops 1048576 | bytes 5242880 | tf_op jit(solution)/shard_map/convert_element_type | solution.py:232
  198.8 9.3 %collective-permute-done.18 = f32[64,1024]{1,0:T(8,128)S(1)} collective-permute-done((f32[64,1024]{1,0:T(8,128)S(1)}, f32[64,1024]{1,0:T(8,128)S(1)}, u32[]{:S(2)}, u32[]{:S(2)}) %collective-permute-start.18) | collective-permute-done | bytes 262176 | tf_op jit(solution)/shard_map/ppermute | solution.py:72
  (122 shorter events, 33.1 us)
Async XLA Ops:
  7.2 67.6 %copy-start = (bf16[64,256]{1,0:T(8,128)(2,1)S(1)}, bf16[64,256]{1,0:T(8,128)(2,1)}, u32[]{:S(2)}) copy-start(bf16[64,256]{1,0:T(8,128)(2,1)} %param.9) | copy-start | bytes 98308
  7.2 58.2 %reduce-scatter.3.cloned.1.call-start = ((), (), s32[]{:S(2)}) async-start(), calls=%async_computation.2 | async-start | bytes 655360 | tf_op jit(solution)/shard_map/reduce_scatter | solution.py:139
  7.9 9.7 %collective-permute-start = (bf16[2,16,128]{2,1,0:T(8,128)(2,1)S(1)}, bf16[2,16,128]{2,1,0:T(8,128)(2,1)S(1)}, u32[]{:S(2)}, u32[]{:S(2)}) collective-permute-start(bf16[2,16,128]{2,1,0:T(8,128)(2,1)S(1)} %get-tuple-element.22), channel_id=1, source_target_pairs={{0,8},{8,16},{16,24},{24,0},{1,9},{9,17},{17,25},{25,1},{2,10},{10... | collective-permute-start | bytes 24584 | tf_op jit(solution)/shard_map/ppermute | solution.py:26
  10.9 6.8 %collective-permute-start.1 = (bf16[2,16,128]{2,1,0:T(8,128)(2,1)S(1)}, bf16[2,16,128]{2,1,0:T(8,128)(2,1)S(1)}, u32[]{:S(2)}, u32[]{:S(2)}) collective-permute-start(bf16[2,16,128]{2,1,0:T(8,128)(2,1)S(1)} %get-tuple-element.21), channel_id=1, source_target_pairs={{8,0},{16,8},{24,16},{0,24},{9,1},{17,9},{25,17},{1,25},{10,2},{18... | collective-permute-start | bytes 24584 | tf_op jit(solution)/shard_map/ppermute | solution.py:27
  14.9 111.8 %copy-start.15 = (s32[256]{0:T(256)}, s32[256]{0:T(256)S(1)}, u32[]{:S(2)}) copy-start(s32[256]{0:T(256)S(1)} %iota_add_fusion.1) | copy-start | bytes 3076
  14.9 2.7 %copy-start.5 = (bf16[2,16,16384]{2,1,0:T(8,128)(2,1)S(1)}, bf16[2,16,16384]{2,1,0:T(8,128)(2,1)}, u32[]{:S(2)}) copy-start(bf16[2,16,16384]{2,1,0:T(8,128)(2,1)} %param.7) | copy-start | bytes 3145732
  17.6 1.0 copy-start.6
  17.6 1.2 copy-start.7
  18.0 1.9 collective-permute-start.2
  19.8 132.5 %reduce-scatter.5.cloned.1.call-start = ((), (), s32[]{:S(2)}) async-start(), calls=%async_computation.3 | async-start | bytes 655360 | tf_op jit(solution)/shard_map/reduce_scatter | solution.py:139
  20.8 8.2 %copy-start.13 = (bf16[2,16,16384]{2,1,0:T(8,128)(2,1)S(1)}, bf16[2,16,16384]{2,1,0:T(8,128)(2,1)}, u32[]{:S(2)}) copy-start(bf16[2,16,16384]{2,1,0:T(8,128)(2,1)} %param.13) | copy-start | bytes 3145732
  22.0 22.0 %collective-permute-start.4 = (bf16[1,18,16640]{2,1,0:T(8,128)(2,1)}, bf16[1,18,16640]{2,1,0:T(8,128)(2,1)}, u32[]{:S(2)}, u32[]{:S(2)}) collective-permute-start(bf16[1,18,16640]{2,1,0:T(8,128)(2,1)} %get-tuple-element.18), channel_id=1, source_target_pairs={{1,0},{2,1},{3,2},{5,4},{6,5},{7,6},{9,8},{10,9},{11,10},{13,12},{... | collective-permute-start | bytes 1797128 | tf_op jit(solution)/shard_map/ppermute | solution.py:27
  23.3 21.8 %collective-permute-start.3 = (bf16[1,18,16640]{2,1,0:T(8,128)(2,1)}, bf16[1,18,16640]{2,1,0:T(8,128)(2,1)}, u32[]{:S(2)}, u32[]{:S(2)}) collective-permute-start(bf16[1,18,16640]{2,1,0:T(8,128)(2,1)} %get-tuple-element.17), channel_id=1, source_target_pairs={{0,1},{1,2},{2,3},{4,5},{5,6},{6,7},{8,9},{9,10},{10,11},{12,13},{... | collective-permute-start | bytes 1797128 | tf_op jit(solution)/shard_map/ppermute | solution.py:26
  32.2 3.8 %copy-start.8 = (bf16[32,64,64]{2,1,0:T(8,128)(2,1)S(1)}, bf16[32,64,64]{2,1,0:T(8,128)(2,1)}, u32[]{:S(2)}) copy-start(bf16[32,64,64]{2,1,0:T(8,128)(2,1)} %param.12) | copy-start | bytes 786436
  32.2 4.0 %copy-start.17 = (bf16[27,64]{1,0:T(8,128)(2,1)S(1)}, bf16[27,64]{1,0:T(8,128)(2,1)}, u32[]{:S(2)}) copy-start(bf16[27,64]{1,0:T(8,128)(2,1)} %param.8) | copy-start | bytes 10372
  37.3 46.4 %copy-start.18 = (s32[32]{0:T(128)}, s32[32]{0:T(128)S(1)}, u32[]{:S(2)}) copy-start(s32[32]{0:T(128)S(1)} %add.121) | copy-start | bytes 388
  38.4 10.9 %copy-start.12 = (f32[27,2176]{1,0:T(8,128)S(1)}, f32[27,2176]{1,0:T(8,128)}, u32[]{:S(2)}) copy-start(f32[27,2176]{1,0:T(8,128)} %tile.17) | copy-start | bytes 705028
  67.1 13.2 %collective-permute-start.5 = (bf16[8,32,128]{2,1,0:T(8,128)(2,1)}, bf16[8,32,128]{2,1,0:T(8,128)(2,1)}, u32[]{:S(2)}, u32[]{:S(2)}) collective-permute-start(bf16[8,32,128]{2,1,0:T(8,128)(2,1)} %convolution_convert_fusion.2), channel_id=1, source_target_pairs={{0,8},{8,16},{16,24},{24,0},{1,9},{9,17},{17,25},{25,1},{2,10},{10... | collective-permute-start | bytes 196616 | tf_op jit(solution)/shard_map/ppermute | solution.py:62
  67.8 13.3 %collective-permute-start.6 = (bf16[8,32,128]{2,1,0:T(8,128)(2,1)}, bf16[8,32,128]{2,1,0:T(8,128)(2,1)}, u32[]{:S(2)}, u32[]{:S(2)}) collective-permute-start(bf16[8,32,128]{2,1,0:T(8,128)(2,1)} %convolution_convert_fusion.2), channel_id=1, source_target_pairs={{0,16},{8,24},{16,0},{24,8},{1,17},{9,25},{17,1},{25,9},{2,18},{10... | collective-permute-start | bytes 196616 | tf_op jit(solution)/shard_map/ppermute | solution.py:62
  69.4 12.6 %collective-permute-start.7 = (bf16[8,32,128]{2,1,0:T(8,128)(2,1)}, bf16[8,32,128]{2,1,0:T(8,128)(2,1)}, u32[]{:S(2)}, u32[]{:S(2)}) collective-permute-start(bf16[8,32,128]{2,1,0:T(8,128)(2,1)} %convolution_convert_fusion.2), channel_id=1, source_target_pairs={{0,24},{8,0},{16,8},{24,16},{1,25},{9,1},{17,9},{25,17},{2,26},{10... | collective-permute-start | bytes 196616 | tf_op jit(solution)/shard_map/ppermute | solution.py:62
  74.7 1.2 copy-start.20
  76.0 3.3 %copy-start.2 = (f32[8192,256]{1,0:T(8,128)}, f32[8192,256]{1,0:T(8,128)S(1)}, u32[]{:S(2)}) copy-start(f32[8192,256]{1,0:T(8,128)S(1)} %fusion.101) | copy-start | bytes 25165828
  79.3 4.4 %copy-start.3 = (f32[32,256,64]{1,2,0:T(8,128)S(1)}, f32[32,256,64]{1,2,0:T(8,128)}, u32[]{:S(2)}) copy-start(f32[32,256,64]{1,2,0:T(8,128)} %copy.30) | copy-start | bytes 6291460
  86.3 0.8 copy-start.21
  101.1 4.5 %collective-permute-start.8 = (bf16[2,16,128]{2,1,0:T(8,128)(2,1)S(1)}, bf16[2,16,128]{2,1,0:T(8,128)(2,1)S(1)}, u32[]{:S(2)}, u32[]{:S(2)}) collective-permute-start(bf16[2,16,128]{2,1,0:T(8,128)(2,1)S(1)} %get-tuple-element.20), channel_id=1, source_target_pairs={{0,8},{8,16},{16,24},{24,0},{1,9},{9,17},{17,25},{25,1},{2,10},{10... | collective-permute-start | bytes 24584 | tf_op jit(solution)/shard_map/ppermute | solution.py:26
  101.1 5.8 %collective-permute-start.9 = (bf16[2,16,128]{2,1,0:T(8,128)(2,1)S(1)}, bf16[2,16,128]{2,1,0:T(8,128)(2,1)S(1)}, u32[]{:S(2)}, u32[]{:S(2)}) collective-permute-start(bf16[2,16,128]{2,1,0:T(8,128)(2,1)S(1)} %get-tuple-element.19), channel_id=1, source_target_pairs={{8,0},{16,8},{24,16},{0,24},{9,1},{17,9},{25,17},{1,25},{10,2},{18... | collective-permute-start | bytes 24584 | tf_op jit(solution)/shard_map/ppermute | solution.py:27
  107.0 1.0 copy-start.4
  108.9 5.5 %collective-permute-start.10 = (bf16[2,1,16640]{2,1,0:T(2,128)(2,1)}, bf16[2,1,16640]{2,1,0:T(2,128)(2,1)}, u32[]{:S(2)}, u32[]{:S(2)}) collective-permute-start(bf16[2,1,16640]{2,1,0:T(2,128)(2,1)} %broadcast_select_fusion.2), channel_id=1, source_target_pairs={{0,4},{4,0},{1,5},{5,1},{2,6},{6,2},{3,7},{7,3},{8,12},{12,8},{9,1... | collective-permute-start | bytes 199688 | tf_op jit(solution)/shard_map/ppermute | solution.py:19
  115.5 3.2 %copy-start.9 = (bf16[2,1,16640]{2,1,0:T(2,128)(2,1)}, bf16[2,1,16640]{2,1,0:T(2,128)(2,1)S(1)}, u32[]{:S(2)}) copy-start(bf16[2,1,16640]{2,1,0:T(2,128)(2,1)S(1)} %get-tuple-element.29) | copy-start | bytes 199684
  115.5 3.2 %copy-start.10 = (bf16[2,1,16640]{2,1,0:T(2,128)(2,1)}, bf16[2,1,16640]{2,1,0:T(2,128)(2,1)S(1)}, u32[]{:S(2)}) copy-start(bf16[2,1,16640]{2,1,0:T(2,128)(2,1)S(1)} %get-tuple-element.30) | copy-start | bytes 199684
  118.7 23.1 %collective-permute-start.12 = (bf16[1,18,16640]{2,1,0:T(8,128)(2,1)}, bf16[1,18,16640]{2,1,0:T(8,128)(2,1)S(1)}, u32[]{:S(2)}, u32[]{:S(2)}) collective-permute-start(bf16[1,18,16640]{2,1,0:T(8,128)(2,1)} %get-tuple-element.16), channel_id=1, source_target_pairs={{1,0},{2,1},{3,2},{5,4},{6,5},{7,6},{9,8},{10,9},{11,10},{13,12},{... | collective-permute-start | bytes 1797128 | tf_op jit(solution)/shard_map/ppermute | solution.py:27
  120.0 23.3 %collective-permute-start.11 = (bf16[1,18,16640]{2,1,0:T(8,128)(2,1)}, bf16[1,18,16640]{2,1,0:T(8,128)(2,1)}, u32[]{:S(2)}, u32[]{:S(2)}) collective-permute-start(bf16[1,18,16640]{2,1,0:T(8,128)(2,1)} %get-tuple-element.15), channel_id=1, source_target_pairs={{0,1},{1,2},{2,3},{4,5},{5,6},{6,7},{8,9},{9,10},{10,11},{12,13},{... | collective-permute-start | bytes 1797128 | tf_op jit(solution)/shard_map/ppermute | solution.py:26
  141.7 0.9 copy-start.14
  155.5 8.7 %copy-start.11 = (f32[27,2176]{1,0:T(8,128)S(1)}, f32[27,2176]{1,0:T(8,128)}, u32[]{:S(2)}) copy-start(f32[27,2176]{1,0:T(8,128)} %tile.19) | copy-start | bytes 705028
  155.5 25.9 %collective-permute-start.13 = (bf16[8,32,128]{2,1,0:T(8,128)(2,1)}, bf16[8,32,128]{2,1,0:T(8,128)(2,1)}, u32[]{:S(2)}, u32[]{:S(2)}) collective-permute-start(bf16[8,32,128]{2,1,0:T(8,128)(2,1)} %convolution_convert_fusion.1), channel_id=1, source_target_pairs={{0,8},{8,16},{16,24},{24,0},{1,9},{9,17},{17,25},{25,1},{2,10},{10... | collective-permute-start | bytes 196616 | tf_op jit(solution)/shard_map/ppermute | solution.py:62
  156.9 25.3 %collective-permute-start.14 = (bf16[8,32,128]{2,1,0:T(8,128)(2,1)}, bf16[8,32,128]{2,1,0:T(8,128)(2,1)}, u32[]{:S(2)}, u32[]{:S(2)}) collective-permute-start(bf16[8,32,128]{2,1,0:T(8,128)(2,1)} %convolution_convert_fusion.1), channel_id=1, source_target_pairs={{0,16},{8,24},{16,0},{24,8},{1,17},{9,25},{17,1},{25,9},{2,18},{10... | collective-permute-start | bytes 196616 | tf_op jit(solution)/shard_map/ppermute | solution.py:62
  157.5 25.6 %collective-permute-start.15 = (bf16[8,32,128]{2,1,0:T(8,128)(2,1)}, bf16[8,32,128]{2,1,0:T(8,128)(2,1)}, u32[]{:S(2)}, u32[]{:S(2)}) collective-permute-start(bf16[8,32,128]{2,1,0:T(8,128)(2,1)} %convolution_convert_fusion.1), channel_id=1, source_target_pairs={{0,24},{8,0},{16,8},{24,16},{1,25},{9,1},{17,9},{25,17},{2,26},{10... | collective-permute-start | bytes 196616 | tf_op jit(solution)/shard_map/ppermute | solution.py:62
  164.2 20.6 %collective-permute-start.16 = (f32[64,1024]{1,0:T(8,128)S(1)}, f32[64,1024]{1,0:T(8,128)S(1)}, u32[]{:S(2)}, u32[]{:S(2)}) collective-permute-start(f32[64,1024]{1,0:T(8,128)S(1)} %reshape.108), channel_id=1, source_target_pairs={{0,4},{4,0},{1,5},{5,1},{2,6},{6,2},{3,7},{7,3},{8,12},{12,8},{9,1... | collective-permute-start | bytes 786440 | tf_op jit(solution)/shard_map/ppermute | solution.py:72
  165.6 18.5 %copy-start.16 = (s32[256]{0:T(256)S(1)}, s32[256]{0:T(256)}, u32[]{:S(2)}) copy-start(s32[256]{0:T(256)} %copy-done.15) | copy-start | bytes 3076
  165.6 18.5 %copy-start.19 = (s32[32]{0:T(128)S(1)}, s32[32]{0:T(128)}, u32[]{:S(2)}) copy-start(s32[32]{0:T(128)} %copy-done.18) | copy-start | bytes 388
  184.8 8.8 %collective-permute-start.17 = (f32[64,1024]{1,0:T(8,128)S(1)}, f32[64,1024]{1,0:T(8,128)S(1)}, u32[]{:S(2)}, u32[]{:S(2)}) collective-permute-start(f32[64,1024]{1,0:T(8,128)S(1)} %add.134), channel_id=1, source_target_pairs={{0,1},{1,0},{2,3},{3,2},{4,5},{5,4},{6,7},{7,6},{8,9},{9,8},{10,11... | collective-permute-start | bytes 786440 | tf_op jit(solution)/shard_map/ppermute | solution.py:72
  193.6 14.5 %collective-permute-start.18 = (f32[64,1024]{1,0:T(8,128)S(1)}, f32[64,1024]{1,0:T(8,128)S(1)}, u32[]{:S(2)}, u32[]{:S(2)}) collective-permute-start(f32[64,1024]{1,0:T(8,128)S(1)} %add.135), channel_id=1, source_target_pairs={{0,2},{1,3},{2,0},{3,1},{4,6},{5,7},{6,4},{7,5},{8,10},{9,11},{10,... | collective-permute-start | bytes 786440 | tf_op jit(solution)/shard_map/ppermute | solution.py:72
  196.1 13.0 %copy-start.1 = (bf16[64,256]{1,0:T(8,128)(2,1)S(1)}, bf16[64,256]{1,0:T(8,128)(2,1)}, u32[]{:S(2)}) copy-start(bf16[64,256]{1,0:T(8,128)(2,1)} %param.9) | copy-start | bytes 98308
Sparse Core Ops, SparseCore 0:
  20.0 25.6 reduce-scatter.2
  128.5 23.7 reduce-scatter.4

commit v6 on v4

--- a/solution.py
+++ b/solution.py
@@ -79,7 +79,6 @@
 
 
 def stencil_kernel(chunk, x_pad, planes, y_cells, rows, p_ref, w_ref, o_ref):
-    width = chunk + 2 * x_pad
     count = o_ref.shape[2] // chunk
     shift = chunk + x_pad - x_pad // 2
 
@@ -87,21 +86,19 @@
         base = pl.multiple_of(index * chunk, chunk)
         for plane in range(planes):
             for row in range(0, y_cells, rows):
-                left = jnp.zeros((rows, chunk + x_pad), jnp.float32)
-                centre = jnp.zeros((rows, chunk), jnp.float32)
-                right = jnp.zeros((rows, chunk + x_pad), jnp.float32)
-                for step_z in range(3):
-                    for step_y in range(3):
-                        window = p_ref[plane + step_z, pl.ds(row + step_y, rows), pl.ds(base, width)]
-                        tap = 9 * step_z + 3 * step_y
-                        left = left + window[:, : chunk + x_pad] * w_ref[tap, :, : chunk + x_pad]
-                        centre = centre + window[:, x_pad : x_pad + chunk] * w_ref[tap + 1, :, :chunk]
-                        right = right + window[:, x_pad:] * w_ref[tap + 2, :, : chunk + x_pad]
-                total = (
-                    centre
-                    + pltpu.roll(left, shift, 1)[:, :chunk]
-                    + pltpu.roll(right, shift, 1)[:, :chunk]
-                )
+                total = jnp.zeros((rows, chunk), jnp.float32)
+                for step_x, offset, span in ((0, 0, chunk + x_pad), (1, x_pad, chunk), (2, x_pad, chunk + x_pad)):
+                    running = jnp.zeros((rows, span), jnp.float32)
+                    for step_z in range(3):
+                        for step_y in range(3):
+                            window = p_ref[
+                                plane + step_z, pl.ds(row + step_y, rows), pl.ds(base + offset, span)
+                            ]
+                            running = running + window * w_ref[9 * step_z + 3 * step_y + step_x, :, :span]
+                    if step_x == 1:
+                        total = total + running
+                    else:
+                        total = total + pltpu.roll(running, shift, 1)[:, :chunk]
                 o_ref[plane, pl.ds(row, rows), pl.ds(base, chunk)] = total.astype(o_ref.dtype)
         return carry
 
@@ -113,7 +110,7 @@
     y_cells = padded.shape[1] - 2
     x_pad = 2 * channels
     lanes = x_cells * channels
-    chunk = min(2048, lanes)
+    chunk = min(1024, lanes)
     rows = 8 if y_cells % 8 == 0 else y_cells
     if flipped:
         taps = taps[::-1]

time: 209 us -> 210 us (level)
  Pallas kernels: 29.5 us -> 32.2 us
    pallas_call x2, Pallas kernels: 29.5 us -> 32.2 us  [depthwise(): pl.pallas_call(kernel, out_shape=jax.ShapeDtypeStruct((planes, y_cells, l...]
    unnamed x40 -> x38, local copies, waits for them, and re-layouts: 5.34 us -> 4.72 us
  transfers between devices with their start and end apart: 23 -> 23, of which waited for: 6 -> 6; matrix products, arithmetic and copies ran while one was open for 30% -> 30% of each run, Pallas kernels for 14% -> 15%
where the time goes in v6:
time: 210 us
  starting transfers between devices  41.3 us (20%)
  local copies, waits for them, and re-layouts  39.9 us (19%)
  waiting for transfers between devices  38.6 us (18%)
  Pallas kernels  32.2 us (15%)
  matrix products  21.7 us (10%)
  other arithmetic  21.3 us (10%)
  between operations  14.6 us (7%)
    pallas_call x2, Pallas kernels, depthwise(): pl.pallas_call(kernel, out_shape=jax.ShapeDtypeStruct((planes, y_cells, l...  32.2 us
    ppermute x6, starting transfers between devices, padded_2(): before = lax.ppermute(last, axis, up)  21.6 us
    reduce_scatter x2, waiting for transfers between devices, share_terms(): lax.psum_scatter(jnp.concatenate([real_part, imag_part], axis=2), 'gx', s...  15.4 us
    ppermute x3, waiting for transfers between devices, butterfly_sum(): lax.ppermute(value, axis, [(i, i ^ step) for i in range(size)])  14.6 us
    convert_element_type x2, other arithmetic, depthwise(): padded.astype(jnp.float32)  8.55 us
    ppermute x6, starting transfers between devices, ring_gather(): lax.ppermute(block, axis, [(i, (i + shift) % size) for i in range(size)])  8.1 us
    dot_general x1, matrix products, per_device(): jnp.dot(grad_hidden, expand_weight.T, preferred_element_type=jnp.float32)  7.81 us
    ppermute x6, starting transfers between devices, padded_2(): after = lax.ppermute(leading, axis, down)  7.55 us
  transfers between devices with their start and end apart: 23, of which 6 were waited for; matrix products, arithmetic and copies ran while one was open for 30% of the time, Pallas kernels for 15%

profile of v6, /device:TPU:0, one launch (start us, length us, event | category | flops | bytes accessed | tf_op | source)
XLA Modules:
  0.0 209.5 jit_solution(6197546713093498407)
XLA Ops:
  7.9 2.9 %collective-permute-start = (bf16[2,16,128]{2,1,0:T(8,128)(2,1)S(1)}, bf16[2,16,128]{2,1,0:T(8,128)(2,1)S(1)}, u32[]{:S(2)}, u32[]{:S(2)}) collective-permute-start(bf16[2,16,128]{2,1,0:T(8,128)(2,1)S(1)} %get-tuple-element.26), channel_id=1, source_target_pairs={{0,8},{8,16},{16,24},{24,0},{1,9},{9,17},{17,25},{25,1},{2,10},{10... | collective-permute-start | bytes 24584 | tf_op jit(solution)/shard_map/ppermute | solution.py:19
  11.8 3.0 %reshape.101 = bf16[32,256,64]{2,1,0:T(8,128)(2,1)S(1)} reshape(bf16[2,16,16384]{2,1,0:T(8,128)(2,1)} %param.7) | data formatting | bytes 2097152 | tf_op jit(solution)/shard_map/reshape | solution.py:179
  16.4 1.3 collective-permute-start.3
  17.7 3.0 %collective-permute-start.2 = (bf16[2,1,16640]{2,1,0:T(2,128)(2,1)S(1)}, bf16[2,1,16640]{2,1,0:T(2,128)(2,1)S(1)}, u32[]{:S(2)}, u32[]{:S(2)}) collective-permute-start(bf16[2,1,16640]{2,1,0:T(2,128)(2,1)S(1)} %get-tuple-element.21), channel_id=1, source_target_pairs={{0,4},{1,5},{2,6},{3,7},{8,12},{9,13},{10,14},{11,15},{16,20},{17,... | collective-permute-start | bytes 199688 | tf_op jit(solution)/shard_map/ppermute | solution.py:19
  22.5 1.3 fusion.96
  23.8 1.3 collective-permute-start.5
  25.1 5.6 %collective-permute-start.4 = (bf16[1,18,16640]{2,1,0:T(8,128)(2,1)}, bf16[1,18,16640]{2,1,0:T(8,128)(2,1)}, u32[]{:S(2)}, u32[]{:S(2)}) collective-permute-start(bf16[1,18,16640]{2,1,0:T(8,128)(2,1)} %get-tuple-element.17), channel_id=1, source_target_pairs={{0,1},{1,2},{2,3},{4,5},{5,6},{6,7},{8,9},{9,10},{10,11},{12,13},{... | collective-permute-start | bytes 1797128 | tf_op jit(solution)/shard_map/ppermute | solution.py:19
  30.6 3.2 %reshape.110 = f32[32,256,64]{2,1,0:T(8,128)} reshape(bf16[2,16,16384]{2,1,0:T(8,128)(2,1)S(1)} %copy-done.7) | data formatting | bytes 3145728 | tf_op jit(solution)/shard_map/convert_element_type | solution.py:199
  33.9 3.8 %copy.30 = f32[32,256,64]{1,2,0:T(8,128)} copy(f32[32,256,64]{2,1,0:T(8,128)} %reshape.110) | data formatting | bytes 4194304 | tf_op jit(solution)/shard_map/convert_element_type | solution.py:199
  39.0 1.1 fusion.13
  40.2 6.1 %collective-permute-done.5 = bf16[1,18,16640]{2,1,0:T(8,128)(2,1)} collective-permute-done((bf16[1,18,16640]{2,1,0:T(8,128)(2,1)}, bf16[1,18,16640]{2,1,0:T(8,128)(2,1)}, u32[]{:S(2)}, u32[]{:S(2)}) %collective-permute-start.5) | collective-permute-done | bytes 599072 | tf_op jit(solution)/shard_map/ppermute | solution.py:20
  46.2 1.2 collective-permute-done.4
  47.4 4.2 %maximum_convert_fusion.p_ref = f32[4,18,16640]{2,1,0:T(8,128)} fusion(bf16[1,18,16640]{2,1,0:T(8,128)(2,1)} %collective-permute-done.5, bf16[2,1,16640]{2,1,0:T(2,128)(2,1)S(1)} %collective-permute-done.3, bf16[2,16,16640]{2,1,0:T(8,128)(2,1)S(1)} %constant_dynamic-update-slice_fusion, bf16[2,1,16640]{2,1,0:T(2,128)(2,1)S(1)} %collective-permute-done.2, ...), kind=kLoop, calls=%fused_computation.11 | loop fusion | flops 11980800 | bytes 7188480 | tf_op jit(solution)/shard_map/convert_element_type | solution.py:123
  52.7 15.9 %shard_map.94 = bf16[2,16,16384]{2,1,0:T(8,128)(2,1)} custom-call(f32[4,18,16640]{2,1,0:T(8,128)} %maximum_convert_fusion.p_ref, f32[27,8,1152]{2,1,0:T(8,128)} %broadcast_in_dim.18.w_ref), custom_call_target="tpu_custom_call" | custom-call | tf_op jit(solution)/shard_map/pallas_call | solution.py:120
  71.0 1.5 collective-permute-start.7
  72.5 2.3 %collective-permute-start.8 = (bf16[8,32,128]{2,1,0:T(8,128)(2,1)}, bf16[8,32,128]{2,1,0:T(8,128)(2,1)}, u32[]{:S(2)}, u32[]{:S(2)}) collective-permute-start(bf16[8,32,128]{2,1,0:T(8,128)(2,1)} %convolution_convert_fusion.2), channel_id=1, source_target_pairs={{0,24},{8,0},{16,8},{24,16},{1,25},{9,1},{17,9},{25,17},{2,26},{10... | collective-permute-start | bytes 196616 | tf_op jit(solution)/shard_map/ppermute | solution.py:55
  74.9 3.0 %reshape.102 = bf16[8192,64]{1,0:T(8,128)(2,1)S(1)} reshape(bf16[2,16,16384]{2,1,0:T(8,128)(2,1)} %shard_map.94) | data formatting | bytes 2097152 | tf_op jit(solution)/shard_map/reshape | solution.py:188
  77.9 1.2 fusion.103
  79.2 2.8 %fusion.5 = f32[8192,64]{0,1:T(8,128)S(1)} fusion(bf16[256,64]{0,1:T(8,128)(2,1)S(1)} %copy-done.13, f32[8192,256]{1,0:T(8,128)S(1)} %fusion.103), kind=kOutput, calls=%fused_computation.10 | convolution fusion | flops 278921216 | bytes 10518528 | tf_op jit(solution)/shard_map/dot_general | solution.py:191
  86.8 2.7 %fusion.11 = (bf16[32,256,64]{1,2,0:T(8,128)(2,1)S(1)}, bf16[32,256,64]{1,2,0:T(8,128)(2,1)}) fusion(f32[32,256,64]{1,2,0:T(8,128)S(1)} %copy-done.3, f32[256,32,64]{0,2,1:T(8,128)S(1)} %fusion.20, bf16[32,32,64]{2,1,0:T(8,128)(2,1)S(1)} %get-tuple-element.31, f32[32]{0:T(128)S(1)} %get-tuple-element.33, s32[32]{0:T(128)S(1)} %add.121, ...), kind=kOutput, calls=%fused_computation.19 | convolution fusion | flops 41041920 | bytes 8520960 | tf_op jit(solution)/shard_map/krc,xk->rxc/dot_general | solution.py:136
  89.5 1.4 fusion.45
  90.9 1.4 fusion.42
  92.4 2.0 copy.29
  94.4 2.5 %reshape.104 = bf16[2,16,16384]{2,1,0:T(8,128)(2,1)} reshape(bf16[32,256,64]{2,1,0:T(8,128)(2,1)S(1)} %copy.29) | data formatting | bytes 2097152 | tf_op jit(solution)/shard_map/reshape | solution.py:197
  96.9 2.2 %pad_maximum_fusion.3 = f32[32,32,128]{2,0,1:T(8,128)} fusion(f32[32,32,64]{2,0,1:T(8,128)} %fusion.45, f32[32,32,64]{2,0,1:T(8,128)} %fusion.42), kind=kLoop, calls=%fused_computation.34 | loop fusion | flops 131072 | bytes 1048576 | tf_op jit(solution)/shard_map/concatenate | solution.py:130
  99.2 7.8 %convolution_convert_fusion = bf16[8192,64]{0,1:T(8,128)(2,1)S(1)} fusion(bf16[64,256]{1,0:T(8,128)(2,1)S(1)} %copy-done, bf16[8192,64]{0,1:T(8,128)(2,1)S(1)} %bitcast.55, bf16[256,64]{0,1:T(8,128)(2,1)S(1)} %copy-done.13, f32[8192,256]{1,0:T(8,128)} %copy-done.2), kind=kOutput, calls=%fused_computation.3 | convolution fusion | flops 558366720 | bytes 10551296 | tf_op jit(solution)/shard_map/dot_general | solution.py:207
  107.1 1.1 copy.35
  108.1 1.7 reshape.106
  109.8 15.4 %reduce-scatter.5.cloned.1.call-done = f32[8,32,128]{2,0,1:T(8,128)} async-done(((f32[32,32,128]{2,0,1:T(8,128)}), f32[8,32,128]{2,0,1:T(8,128)}) %reduce-scatter.5.cloned.1.call-update) | async-done | bytes 131088 | tf_op jit(solution)/shard_map/reduce_scatter | solution.py:129
  126.9 1.5 collective-permute-start.9
  128.4 1.5 collective-permute-start.15
  130.5 1.5 collective-permute-start.17
  131.9 1.4 collective-permute-start.10
  133.7 1.3 constant_dynamic-update-slice_fusion.8
  135.8 1.3 collective-permute-start.12
  137.1 3.0 %collective-permute-start.11 = (bf16[2,1,16640]{2,1,0:T(2,128)(2,1)S(1)}, bf16[2,1,16640]{2,1,0:T(2,128)(2,1)S(1)}, u32[]{:S(2)}, u32[]{:S(2)}) collective-permute-start(bf16[2,1,16640]{2,1,0:T(2,128)(2,1)S(1)} %get-tuple-element.19), channel_id=1, source_target_pairs={{0,4},{1,5},{2,6},{3,7},{8,12},{9,13},{10,14},{11,15},{16,20},{17,... | collective-permute-start | bytes 199688 | tf_op jit(solution)/shard_map/ppermute | solution.py:19
  141.7 1.3 fusion.95
  143.0 1.3 collective-permute-start.14
  144.3 5.5 %collective-permute-start.13 = (bf16[1,18,16640]{2,1,0:T(8,128)(2,1)}, bf16[1,18,16640]{2,1,0:T(8,128)(2,1)}, u32[]{:S(2)}, u32[]{:S(2)}) collective-permute-start(bf16[1,18,16640]{2,1,0:T(8,128)(2,1)} %get-tuple-element.15), channel_id=1, source_target_pairs={{0,1},{1,2},{2,3},{4,5},{5,6},{6,7},{8,9},{9,10},{10,11},{12,13},{... | collective-permute-start | bytes 1797128 | tf_op jit(solution)/shard_map/ppermute | solution.py:19
  151.8 2.7 %copy.38 = f32[32,256,64]{2,1,0:T(8,128)} copy(f32[32,256,64]{1,2,0:T(8,128)S(1)} %add_bitcast_fusion) | data formatting | bytes 4194304 | tf_op jit(solution)/shard_map/add | solution.py:139
  154.5 2.9 %reshape.107 = f32[2,16,16384]{2,1,0:T(8,128)S(1)} reshape(f32[32,256,64]{2,1,0:T(8,128)} %copy.38) | data formatting | bytes 4194304 | tf_op jit(solution)/shard_map/reshape | solution.py:222
  157.4 14.6 %collective-permute-done.19 = f32[64,1024]{1,0:T(8,128)} collective-permute-done((f32[64,1024]{1,0:T(8,128)S(1)}, f32[64,1024]{1,0:T(8,128)}, u32[]{:S(2)}, u32[]{:S(2)}) %collective-permute-start.19) | collective-permute-done | bytes 262176 | tf_op jit(solution)/shard_map/ppermute | solution.py:65
  172.0 1.1 add.135
  173.1 3.3 %collective-permute-start.20 = (f32[64,1024]{1,0:T(8,128)S(1)}, f32[64,1024]{1,0:T(8,128)}, u32[]{:S(2)}, u32[]{:S(2)}) collective-permute-start(f32[64,1024]{1,0:T(8,128)S(1)} %add.135), channel_id=1, source_target_pairs={{0,2},{1,3},{2,0},{3,1},{4,6},{5,7},{6,4},{7,5},{8,10},{9,11},{10,... | collective-permute-start | bytes 786440 | tf_op jit(solution)/shard_map/ppermute | solution.py:65
  176.4 4.3 %maximum_convert_fusion.1.p_ref = f32[4,18,16640]{2,1,0:T(8,128)} fusion(bf16[1,18,16640]{2,1,0:T(8,128)(2,1)} %collective-permute-done.14, bf16[2,1,16640]{2,1,0:T(2,128)(2,1)} %copy-done.10, bf16[2,16,16640]{2,1,0:T(8,128)(2,1)S(1)} %constant_dynamic-update-slice_fusion.7, bf16[2,1,16640]{2,1,0:T(2,128)(2,1)} %copy-done.11, ...), kind=kLoop, calls=%fused_computation.12 | loop fusion | flops 11980800 | bytes 7188480 | tf_op jit(solution)/shard_map/convert_element_type | solution.py:123
  180.7 1.0 broadcast_in_dim.36.w_ref
  181.7 16.3 %shard_map.95 = f32[2,16,16384]{2,1,0:T(8,128)} custom-call(f32[4,18,16640]{2,1,0:T(8,128)} %maximum_convert_fusion.1.p_ref, f32[27,8,1152]{2,1,0:T(8,128)} %broadcast_in_dim.36.w_ref), custom_call_target="tpu_custom_call" | custom-call | tf_op jit(solution)/shard_map/pallas_call | solution.py:120
  198.0 2.8 %add_convert_fusion = bf16[2,16,16384]{2,1,0:T(8,128)(2,1)} fusion(f32[2,16,16384]{2,1,0:T(8,128)} %shard_map.95, f32[2,16,16384]{2,1,0:T(8,128)S(1)} %reshape.107), kind=kLoop, calls=%fused_computation.21 | loop fusion | flops 1048576 | bytes 5242880 | tf_op jit(solution)/shard_map/convert_element_type | solution.py:222
  (107 shorter events, 23.3 us)
Async XLA Ops:
  7.2 70.8 %copy-start = (bf16[64,256]{1,0:T(8,128)(2,1)S(1)}, bf16[64,256]{1,0:T(8,128)(2,1)}, u32[]{:S(2)}) copy-start(bf16[64,256]{1,0:T(8,128)(2,1)} %param.9) | copy-start | bytes 98308
  7.2 61.4 %reduce-scatter.3.cloned.1.call-start = ((), (), s32[]{:S(2)}) async-start(), calls=%async_computation.2 | async-start | bytes 655360 | tf_op jit(solution)/shard_map/reduce_scatter | solution.py:129
  7.9 8.1 %collective-permute-start = (bf16[2,16,128]{2,1,0:T(8,128)(2,1)S(1)}, bf16[2,16,128]{2,1,0:T(8,128)(2,1)S(1)}, u32[]{:S(2)}, u32[]{:S(2)}) collective-permute-start(bf16[2,16,128]{2,1,0:T(8,128)(2,1)S(1)} %get-tuple-element.26), channel_id=1, source_target_pairs={{0,8},{8,16},{16,24},{24,0},{1,9},{9,17},{17,25},{25,1},{2,10},{10... | collective-permute-start | bytes 24584 | tf_op jit(solution)/shard_map/ppermute | solution.py:19
  10.9 5.3 %collective-permute-start.1 = (bf16[2,16,128]{2,1,0:T(8,128)(2,1)S(1)}, bf16[2,16,128]{2,1,0:T(8,128)(2,1)S(1)}, u32[]{:S(2)}, u32[]{:S(2)}) collective-permute-start(bf16[2,16,128]{2,1,0:T(8,128)(2,1)S(1)} %get-tuple-element.25), channel_id=1, source_target_pairs={{8,0},{16,8},{24,16},{0,24},{9,1},{17,9},{25,17},{1,25},{10,2},{18... | collective-permute-start | bytes 24584 | tf_op jit(solution)/shard_map/ppermute | solution.py:20
  14.9 1.2 copy-start.4
  16.4 5.4 %collective-permute-start.3 = (bf16[2,1,16640]{2,1,0:T(2,128)(2,1)S(1)}, bf16[2,1,16640]{2,1,0:T(2,128)(2,1)S(1)}, u32[]{:S(2)}, u32[]{:S(2)}) collective-permute-start(bf16[2,1,16640]{2,1,0:T(2,128)(2,1)S(1)} %get-tuple-element.22), channel_id=1, source_target_pairs={{4,0},{5,1},{6,2},{7,3},{12,8},{13,9},{14,10},{15,11},{20,16},{21,... | collective-permute-start | bytes 199688 | tf_op jit(solution)/shard_map/ppermute | solution.py:20
  17.7 4.1 %collective-permute-start.2 = (bf16[2,1,16640]{2,1,0:T(2,128)(2,1)S(1)}, bf16[2,1,16640]{2,1,0:T(2,128)(2,1)S(1)}, u32[]{:S(2)}, u32[]{:S(2)}) collective-permute-start(bf16[2,1,16640]{2,1,0:T(2,128)(2,1)S(1)} %get-tuple-element.21), channel_id=1, source_target_pairs={{0,4},{1,5},{2,6},{3,7},{8,12},{9,13},{10,14},{11,15},{16,20},{17,... | collective-permute-start | bytes 199688 | tf_op jit(solution)/shard_map/ppermute | solution.py:19
  21.8 103.4 %reduce-scatter.5.cloned.1.call-start = ((), (), s32[]{:S(2)}) async-start(), calls=%async_computation.3 | async-start | bytes 655360 | tf_op jit(solution)/shard_map/reduce_scatter | solution.py:129
  22.5 8.1 %copy-start.7 = (bf16[2,16,16384]{2,1,0:T(8,128)(2,1)S(1)}, bf16[2,16,16384]{2,1,0:T(8,128)(2,1)}, u32[]{:S(2)}) copy-start(bf16[2,16,16384]{2,1,0:T(8,128)(2,1)} %param.13) | copy-start | bytes 3145732
  23.8 22.5 %collective-permute-start.5 = (bf16[1,18,16640]{2,1,0:T(8,128)(2,1)}, bf16[1,18,16640]{2,1,0:T(8,128)(2,1)}, u32[]{:S(2)}, u32[]{:S(2)}) collective-permute-start(bf16[1,18,16640]{2,1,0:T(8,128)(2,1)} %get-tuple-element.18), channel_id=1, source_target_pairs={{1,0},{2,1},{3,2},{5,4},{6,5},{7,6},{9,8},{10,9},{11,10},{13,12},{... | collective-permute-start | bytes 1797128 | tf_op jit(solution)/shard_map/ppermute | solution.py:20
  25.1 22.4 %collective-permute-start.4 = (bf16[1,18,16640]{2,1,0:T(8,128)(2,1)}, bf16[1,18,16640]{2,1,0:T(8,128)(2,1)}, u32[]{:S(2)}, u32[]{:S(2)}) collective-permute-start(bf16[1,18,16640]{2,1,0:T(8,128)(2,1)} %get-tuple-element.17), channel_id=1, source_target_pairs={{0,1},{1,2},{2,3},{4,5},{5,6},{6,7},{8,9},{9,10},{10,11},{12,13},{... | collective-permute-start | bytes 1797128 | tf_op jit(solution)/shard_map/ppermute | solution.py:19
  33.9 3.8 %copy-start.6 = (bf16[32,64,64]{2,1,0:T(8,128)(2,1)S(1)}, bf16[32,64,64]{2,1,0:T(8,128)(2,1)}, u32[]{:S(2)}) copy-start(bf16[32,64,64]{2,1,0:T(8,128)(2,1)} %param.12) | copy-start | bytes 786436
  33.9 4.0 %copy-start.12 = (bf16[27,64]{1,0:T(8,128)(2,1)S(1)}, bf16[27,64]{1,0:T(8,128)(2,1)}, u32[]{:S(2)}) copy-start(bf16[27,64]{1,0:T(8,128)(2,1)} %param.8) | copy-start | bytes 10372
  70.3 13.2 %collective-permute-start.6 = (bf16[8,32,128]{2,1,0:T(8,128)(2,1)}, bf16[8,32,128]{2,1,0:T(8,128)(2,1)}, u32[]{:S(2)}, u32[]{:S(2)}) collective-permute-start(bf16[8,32,128]{2,1,0:T(8,128)(2,1)} %convolution_convert_fusion.2), channel_id=1, source_target_pairs={{0,8},{8,16},{16,24},{24,0},{1,9},{9,17},{17,25},{25,1},{2,10},{10... | collective-permute-start | bytes 196616 | tf_op jit(solution)/shard_map/ppermute | solution.py:55
  71.0 13.3 %collective-permute-start.7 = (bf16[8,32,128]{2,1,0:T(8,128)(2,1)}, bf16[8,32,128]{2,1,0:T(8,128)(2,1)}, u32[]{:S(2)}, u32[]{:S(2)}) collective-permute-start(bf16[8,32,128]{2,1,0:T(8,128)(2,1)} %convolution_convert_fusion.2), channel_id=1, source_target_pairs={{0,16},{8,24},{16,0},{24,8},{1,17},{9,25},{17,1},{25,9},{2,18},{10... | collective-permute-start | bytes 196616 | tf_op jit(solution)/shard_map/ppermute | solution.py:55
  72.5 12.6 %collective-permute-start.8 = (bf16[8,32,128]{2,1,0:T(8,128)(2,1)}, bf16[8,32,128]{2,1,0:T(8,128)(2,1)}, u32[]{:S(2)}, u32[]{:S(2)}) collective-permute-start(bf16[8,32,128]{2,1,0:T(8,128)(2,1)} %convolution_convert_fusion.2), channel_id=1, source_target_pairs={{0,24},{8,0},{16,8},{24,16},{1,25},{9,1},{17,9},{25,17},{2,26},{10... | collective-permute-start | bytes 196616 | tf_op jit(solution)/shard_map/ppermute | solution.py:55
  77.9 1.2 copy-start.13
  79.2 3.3 %copy-start.2 = (f32[8192,256]{1,0:T(8,128)}, f32[8192,256]{1,0:T(8,128)S(1)}, u32[]{:S(2)}) copy-start(f32[8192,256]{1,0:T(8,128)S(1)} %fusion.103) | copy-start | bytes 25165828
  82.5 4.4 %copy-start.3 = (f32[32,256,64]{1,2,0:T(8,128)S(1)}, f32[32,256,64]{1,2,0:T(8,128)}, u32[]{:S(2)}) copy-start(f32[32,256,64]{1,2,0:T(8,128)} %copy.30) | copy-start | bytes 6291460
  109.8 23.7 %copy-start.5 = (bf16[2,16,16384]{2,1,0:T(8,128)(2,1)}, bf16[2,16,16384]{2,1,0:T(8,128)(2,1)S(1)}, u32[]{:S(2)}) copy-start(bf16[2,16,16384]{2,1,0:T(8,128)(2,1)S(1)} %reshape.106) | copy-start | bytes 3145732
  126.9 6.6 %collective-permute-start.9 = (bf16[2,16,128]{2,1,0:T(8,128)(2,1)S(1)}, bf16[2,16,128]{2,1,0:T(8,128)(2,1)S(1)}, u32[]{:S(2)}, u32[]{:S(2)}) collective-permute-start(bf16[2,16,128]{2,1,0:T(8,128)(2,1)S(1)} %get-tuple-element.24), channel_id=1, source_target_pairs={{0,8},{8,16},{16,24},{24,0},{1,9},{9,17},{17,25},{25,1},{2,10},{10... | collective-permute-start | bytes 24584 | tf_op jit(solution)/shard_map/ppermute | solution.py:19
  128.4 8.7 %collective-permute-start.15 = (bf16[8,32,128]{2,1,0:T(8,128)(2,1)S(1)}, bf16[8,32,128]{2,1,0:T(8,128)(2,1)S(1)}, u32[]{:S(2)}, u32[]{:S(2)}) collective-permute-start(bf16[8,32,128]{2,1,0:T(8,128)(2,1)S(1)} %convolution_convert_fusion.1), channel_id=1, source_target_pairs={{0,8},{8,16},{16,24},{24,0},{1,9},{9,17},{17,25},{25,1},{2,10},{10... | collective-permute-start | bytes 196616 | tf_op jit(solution)/shard_map/ppermute | solution.py:55
  129.9 10.3 %collective-permute-start.16 = (bf16[8,32,128]{2,1,0:T(8,128)(2,1)S(1)}, bf16[8,32,128]{2,1,0:T(8,128)(2,1)S(1)}, u32[]{:S(2)}, u32[]{:S(2)}) collective-permute-start(bf16[8,32,128]{2,1,0:T(8,128)(2,1)S(1)} %convolution_convert_fusion.1), channel_id=1, source_target_pairs={{0,16},{8,24},{16,0},{24,8},{1,17},{9,25},{17,1},{25,9},{2,18},{10... | collective-permute-start | bytes 196616 | tf_op jit(solution)/shard_map/ppermute | solution.py:55
  130.5 9.7 %collective-permute-start.17 = (bf16[8,32,128]{2,1,0:T(8,128)(2,1)S(1)}, bf16[8,32,128]{2,1,0:T(8,128)(2,1)S(1)}, u32[]{:S(2)}, u32[]{:S(2)}) collective-permute-start(bf16[8,32,128]{2,1,0:T(8,128)(2,1)S(1)} %convolution_convert_fusion.1), channel_id=1, source_target_pairs={{0,24},{8,0},{16,8},{24,16},{1,25},{9,1},{17,9},{25,17},{2,26},{10... | collective-permute-start | bytes 196616 | tf_op jit(solution)/shard_map/ppermute | solution.py:55
  131.9 3.7 %collective-permute-start.10 = (bf16[2,16,128]{2,1,0:T(8,128)(2,1)S(1)}, bf16[2,16,128]{2,1,0:T(8,128)(2,1)S(1)}, u32[]{:S(2)}, u32[]{:S(2)}) collective-permute-start(bf16[2,16,128]{2,1,0:T(8,128)(2,1)S(1)} %get-tuple-element.23), channel_id=1, source_target_pairs={{8,0},{16,8},{24,16},{0,24},{9,1},{17,9},{25,17},{1,25},{10,2},{18... | collective-permute-start | bytes 24584 | tf_op jit(solution)/shard_map/ppermute | solution.py:20
  133.6 16.9 %collective-permute-start.18 = (f32[64,1024]{1,0:T(8,128)S(1)}, f32[64,1024]{1,0:T(8,128)S(1)}, u32[]{:S(2)}, u32[]{:S(2)}) collective-permute-start(f32[64,1024]{1,0:T(8,128)S(1)} %reshape.108), channel_id=1, source_target_pairs={{0,4},{4,0},{1,5},{5,1},{2,6},{6,2},{3,7},{7,3},{8,12},{12,8},{9,1... | collective-permute-start | bytes 786440 | tf_op jit(solution)/shard_map/ppermute | solution.py:65
  135.8 4.6 %collective-permute-start.12 = (bf16[2,1,16640]{2,1,0:T(2,128)(2,1)S(1)}, bf16[2,1,16640]{2,1,0:T(2,128)(2,1)S(1)}, u32[]{:S(2)}, u32[]{:S(2)}) collective-permute-start(bf16[2,1,16640]{2,1,0:T(2,128)(2,1)S(1)} %get-tuple-element.20), channel_id=1, source_target_pairs={{4,0},{5,1},{6,2},{7,3},{12,8},{13,9},{14,10},{15,11},{20,16},{21,... | collective-permute-start | bytes 199688 | tf_op jit(solution)/shard_map/ppermute | solution.py:20
  137.1 4.0 %collective-permute-start.11 = (bf16[2,1,16640]{2,1,0:T(2,128)(2,1)S(1)}, bf16[2,1,16640]{2,1,0:T(2,128)(2,1)S(1)}, u32[]{:S(2)}, u32[]{:S(2)}) collective-permute-start(bf16[2,1,16640]{2,1,0:T(2,128)(2,1)S(1)} %get-tuple-element.19), channel_id=1, source_target_pairs={{0,4},{1,5},{2,6},{3,7},{8,12},{9,13},{10,14},{11,15},{16,20},{17,... | collective-permute-start | bytes 199688 | tf_op jit(solution)/shard_map/ppermute | solution.py:19
  140.4 2.6 %copy-start.10 = (bf16[2,1,16640]{2,1,0:T(2,128)(2,1)}, bf16[2,1,16640]{2,1,0:T(2,128)(2,1)S(1)}, u32[]{:S(2)}) copy-start(bf16[2,1,16640]{2,1,0:T(2,128)(2,1)S(1)} %collective-permute-done.12) | copy-start | bytes 199684
  141.1 1.9 copy-start.11
  143.0 33.4 %collective-permute-start.14 = (bf16[1,18,16640]{2,1,0:T(8,128)(2,1)}, bf16[1,18,16640]{2,1,0:T(8,128)(2,1)}, u32[]{:S(2)}, u32[]{:S(2)}) collective-permute-start(bf16[1,18,16640]{2,1,0:T(8,128)(2,1)} %get-tuple-element.16), channel_id=1, source_target_pairs={{1,0},{2,1},{3,2},{5,4},{6,5},{7,6},{9,8},{10,9},{11,10},{13,12},{... | collective-permute-start | bytes 1797128 | tf_op jit(solution)/shard_map/ppermute | solution.py:20
  144.3 32.1 %collective-permute-start.13 = (bf16[1,18,16640]{2,1,0:T(8,128)(2,1)}, bf16[1,18,16640]{2,1,0:T(8,128)(2,1)}, u32[]{:S(2)}, u32[]{:S(2)}) collective-permute-start(bf16[1,18,16640]{2,1,0:T(8,128)(2,1)} %get-tuple-element.15), channel_id=1, source_target_pairs={{0,1},{1,2},{2,3},{4,5},{5,6},{6,7},{8,9},{9,10},{10,11},{12,13},{... | collective-permute-start | bytes 1797128 | tf_op jit(solution)/shard_map/ppermute | solution.py:19
  150.5 1.2 copy-start.8
  150.6 21.4 %collective-permute-start.19 = (f32[64,1024]{1,0:T(8,128)S(1)}, f32[64,1024]{1,0:T(8,128)}, u32[]{:S(2)}, u32[]{:S(2)}) collective-permute-start(f32[64,1024]{1,0:T(8,128)S(1)} %add.134), channel_id=1, source_target_pairs={{0,1},{1,0},{2,3},{3,2},{4,5},{5,4},{6,7},{7,6},{8,9},{9,8},{10,11... | collective-permute-start | bytes 786440 | tf_op jit(solution)/shard_map/ppermute | solution.py:65
  173.1 7.6 %copy-start.9 = (f32[27,1152]{1,0:T(8,128)S(1)}, f32[27,1152]{1,0:T(8,128)}, u32[]{:S(2)}) copy-start(f32[27,1152]{1,0:T(8,128)} %tile.19) | copy-start | bytes 373252
  173.1 27.7 %collective-permute-start.20 = (f32[64,1024]{1,0:T(8,128)S(1)}, f32[64,1024]{1,0:T(8,128)}, u32[]{:S(2)}, u32[]{:S(2)}) collective-permute-start(f32[64,1024]{1,0:T(8,128)S(1)} %add.135), channel_id=1, source_target_pairs={{0,2},{1,3},{2,0},{3,1},{4,6},{5,7},{6,4},{7,5},{8,10},{9,11},{10,... | collective-permute-start | bytes 786440 | tf_op jit(solution)/shard_map/ppermute | solution.py:65
  198.0 4.7 %copy-start.1 = (bf16[64,256]{1,0:T(8,128)(2,1)S(1)}, bf16[64,256]{1,0:T(8,128)(2,1)}, u32[]{:S(2)}) copy-start(bf16[64,256]{1,0:T(8,128)(2,1)} %param.9) | copy-start | bytes 98308
Sparse Core Ops, SparseCore 0:
  21.9 25.6 reduce-scatter.2
  99.3 25.8 reduce-scatter.4

commit v7 on v4

--- a/solution.py
+++ b/solution.py
@@ -82,6 +82,7 @@
     width = chunk + 2 * x_pad
     count = o_ref.shape[2] // chunk
     shift = chunk + x_pad - x_pad // 2
+    side = (chunk + x_pad) // 128
 
     def body(index, carry):
         base = pl.multiple_of(index * chunk, chunk)
@@ -94,9 +95,12 @@
                     for step_y in range(3):
                         window = p_ref[plane + step_z, pl.ds(row + step_y, rows), pl.ds(base, width)]
                         tap = 9 * step_z + 3 * step_y
-                        left = left + window[:, : chunk + x_pad] * w_ref[tap, :, : chunk + x_pad]
-                        centre = centre + window[:, x_pad : x_pad + chunk] * w_ref[tap + 1, :, :chunk]
-                        right = right + window[:, x_pad:] * w_ref[tap + 2, :, : chunk + x_pad]
+                        gain_l = jnp.concatenate([w_ref[tap]] * side, axis=1)
+                        gain_c = jnp.concatenate([w_ref[tap + 1]] * (side - 1), axis=1)
+                        gain_r = jnp.concatenate([w_ref[tap + 2]] * side, axis=1)
+                        left = left + window[:, : chunk + x_pad] * gain_l
+                        centre = centre + window[:, x_pad : x_pad + chunk] * gain_c
+                        right = right + window[:, x_pad:] * gain_r
                 total = (
                     centre
                     + pltpu.roll(left, shift, 1)[:, :chunk]
@@ -113,12 +117,12 @@
     y_cells = padded.shape[1] - 2
     x_pad = 2 * channels
     lanes = x_cells * channels
-    chunk = min(2048, lanes)
+    chunk = min(1024, lanes)
     rows = 8 if y_cells % 8 == 0 else y_cells
     if flipped:
         taps = taps[::-1]
-    gains = jnp.tile(taps.astype(jnp.float32), (1, (chunk + x_pad) // channels))
-    gains = jnp.broadcast_to(gains[:, None, :], (gains.shape[0], rows, gains.shape[1]))
+    gains = jnp.tile(taps.astype(jnp.float32), (1, 128 // channels))
+    gains = jnp.broadcast_to(gains[:, None, :], (gains.shape[0], rows, 128))
     kernel = functools.partial(stencil_kernel, chunk, x_pad, planes, y_cells, rows)
     return pl.pallas_call(
         kernel,

time: 209 us -> 204 us (0.976)
  Pallas kernels: 29.5 us -> 26.9 us
  local copies, waits for them, and re-layouts: 41.5 us -> 39 us
    pallas_call x2, Pallas kernels: 29.5 us -> 26.9 us  [depthwise(): pl.pallas_call(kernel, out_shape=jax.ShapeDtypeStruct((planes, y_cells, l...]
    unnamed x40 -> x38, local copies, waits for them, and re-layouts: 5.34 us -> 5.36 us
  transfers between devices with their start and end apart: 23 -> 23, of which waited for: 6 -> 6; matrix products, arithmetic and copies ran while one was open for 30% -> 30% of each run, Pallas kernels for 14% -> 13%
where the time goes in v7:
time: 204 us; the launch traced here: 203 us
  starting transfers between devices  41.3 us (20%)
  local copies, waits for them, and re-layouts  39 us (19%)
  waiting for transfers between devices  38.6 us (19%)
  Pallas kernels  26.9 us (13%)
  matrix products  21.7 us (11%)
  other arithmetic  21.2 us (10%)
  between operations  14.6 us (7%)
    pallas_call x2, Pallas kernels, depthwise(): pl.pallas_call(kernel, out_shape=jax.ShapeDtypeStruct((planes, y_cells, l...  26.9 us
    ppermute x6, starting transfers between devices, padded_2(): before = lax.ppermute(last, axis, up)  21.5 us
    ppermute x3, waiting for transfers between devices, butterfly_sum(): lax.ppermute(value, axis, [(i, i ^ step) for i in range(size)])  14.6 us
    reduce_scatter x2, waiting for transfers between devices, share_terms(): lax.psum_scatter(jnp.concatenate([real_part, imag_part], axis=2), 'gx', s...  14.6 us
    convert_element_type x2, other arithmetic, depthwise(): padded.astype(jnp.float32)  8.46 us
    ppermute x6, starting transfers between devices, ring_gather(): lax.ppermute(block, axis, [(i, (i + shift) % size) for i in range(size)])  8.1 us
    dot_general x1, matrix products, per_device(): jnp.dot(grad_hidden, expand_weight.T, preferred_element_type=jnp.float32)  7.84 us
    ppermute x6, starting transfers between devices, padded_2(): after = lax.ppermute(leading, axis, down)  7.55 us
  transfers between devices with their start and end apart: 23, of which 6 were waited for; matrix products, arithmetic and copies ran while one was open for 30% of the time, Pallas kernels for 13%

profile of v7, /device:TPU:0, one launch (start us, length us, event | category | flops | bytes accessed | tf_op | source)
XLA Modules:
  0.0 203.3 jit_solution(5185817754815106619)
XLA Ops:
  7.9 2.9 %collective-permute-start = (bf16[2,16,128]{2,1,0:T(8,128)(2,1)S(1)}, bf16[2,16,128]{2,1,0:T(8,128)(2,1)S(1)}, u32[]{:S(2)}, u32[]{:S(2)}) collective-permute-start(bf16[2,16,128]{2,1,0:T(8,128)(2,1)S(1)} %get-tuple-element.26), channel_id=1, source_target_pairs={{0,8},{8,16},{16,24},{24,0},{1,9},{9,17},{17,25},{25,1},{2,10},{10... | collective-permute-start | bytes 24584 | tf_op jit(solution)/shard_map/ppermute | solution.py:19
  11.8 3.0 %reshape.101 = bf16[32,256,64]{2,1,0:T(8,128)(2,1)S(1)} reshape(bf16[2,16,16384]{2,1,0:T(8,128)(2,1)} %param.7) | data formatting | bytes 2097152 | tf_op jit(solution)/shard_map/reshape | solution.py:186
  16.4 1.3 collective-permute-start.3
  17.7 3.0 %collective-permute-start.2 = (bf16[2,1,16640]{2,1,0:T(2,128)(2,1)S(1)}, bf16[2,1,16640]{2,1,0:T(2,128)(2,1)S(1)}, u32[]{:S(2)}, u32[]{:S(2)}) collective-permute-start(bf16[2,1,16640]{2,1,0:T(2,128)(2,1)S(1)} %get-tuple-element.21), channel_id=1, source_target_pairs={{0,4},{1,5},{2,6},{3,7},{8,12},{9,13},{10,14},{11,15},{16,20},{17,... | collective-permute-start | bytes 199688 | tf_op jit(solution)/shard_map/ppermute | solution.py:19
  20.8 1.0 pad_maximum_fusion.2
  23.2 1.3 fusion.96
  24.4 1.3 collective-permute-start.5
  25.7 5.5 %collective-permute-start.4 = (bf16[1,18,16640]{2,1,0:T(8,128)(2,1)}, bf16[1,18,16640]{2,1,0:T(8,128)(2,1)}, u32[]{:S(2)}, u32[]{:S(2)}) collective-permute-start(bf16[1,18,16640]{2,1,0:T(8,128)(2,1)} %get-tuple-element.17), channel_id=1, source_target_pairs={{0,1},{1,2},{2,3},{4,5},{5,6},{6,7},{8,9},{9,10},{10,11},{12,13},{... | collective-permute-start | bytes 1797128 | tf_op jit(solution)/shard_map/ppermute | solution.py:19
  31.2 3.2 %reshape.110 = f32[32,256,64]{2,1,0:T(8,128)} reshape(bf16[2,16,16384]{2,1,0:T(8,128)(2,1)S(1)} %copy-done.7) | data formatting | bytes 3145728 | tf_op jit(solution)/shard_map/convert_element_type | solution.py:206
  34.4 3.8 %copy.30 = f32[32,256,64]{1,2,0:T(8,128)} copy(f32[32,256,64]{2,1,0:T(8,128)} %reshape.110) | data formatting | bytes 4194304 | tf_op jit(solution)/shard_map/convert_element_type | solution.py:206
  38.8 1.1 fusion.13
  39.9 6.8 %collective-permute-done.5 = bf16[1,18,16640]{2,1,0:T(8,128)(2,1)S(1)} collective-permute-done((bf16[1,18,16640]{2,1,0:T(8,128)(2,1)}, bf16[1,18,16640]{2,1,0:T(8,128)(2,1)S(1)}, u32[]{:S(2)}, u32[]{:S(2)}) %collective-permute-start.5) | collective-permute-done | bytes 599072 | tf_op jit(solution)/shard_map/ppermute | solution.py:20
  46.8 1.3 collective-permute-done.4
  48.0 4.2 %maximum_convert_fusion.p_ref = f32[4,18,16640]{2,1,0:T(8,128)} fusion(bf16[1,18,16640]{2,1,0:T(8,128)(2,1)S(1)} %collective-permute-done.5, bf16[2,1,16640]{2,1,0:T(2,128)(2,1)S(1)} %collective-permute-done.3, bf16[2,16,16640]{2,1,0:T(8,128)(2,1)S(1)} %constant_dynamic-update-slice_fusion, bf16[2,1,16640]{2,1,0:T(2,128)(2,1)} %copy-done.11, ...), kind=kLoop, calls=%fused_computation.11 | loop fusion | flops 11980800 | bytes 7188480 | tf_op jit(solution)/shard_map/convert_element_type | solution.py:130
  52.9 13.3 %shard_map.94 = bf16[2,16,16384]{2,1,0:T(8,128)(2,1)} custom-call(f32[4,18,16640]{2,1,0:T(8,128)} %maximum_convert_fusion.p_ref, f32[27,8,128]{2,1,0:T(8,128)} %broadcast_in_dim.18.w_ref), custom_call_target="tpu_custom_call" | custom-call | tf_op jit(solution)/shard_map/pallas_call | solution.py:127
  68.6 1.5 collective-permute-start.7
  70.1 2.3 %collective-permute-start.8 = (bf16[8,32,128]{2,1,0:T(8,128)(2,1)}, bf16[8,32,128]{2,1,0:T(8,128)(2,1)}, u32[]{:S(2)}, u32[]{:S(2)}) collective-permute-start(bf16[8,32,128]{2,1,0:T(8,128)(2,1)} %convolution_convert_fusion.2), channel_id=1, source_target_pairs={{0,24},{8,0},{16,8},{24,16},{1,25},{9,1},{17,9},{25,17},{2,26},{10... | collective-permute-start | bytes 196616 | tf_op jit(solution)/shard_map/ppermute | solution.py:55
  72.5 3.0 %reshape.102 = bf16[8192,64]{1,0:T(8,128)(2,1)S(1)} reshape(bf16[2,16,16384]{2,1,0:T(8,128)(2,1)} %shard_map.94) | data formatting | bytes 2097152 | tf_op jit(solution)/shard_map/reshape | solution.py:195
  75.5 1.2 fusion.103
  76.8 2.8 %fusion.5 = f32[8192,64]{0,1:T(8,128)S(1)} fusion(bf16[256,64]{0,1:T(8,128)(2,1)S(1)} %copy-done.13, f32[8192,256]{1,0:T(8,128)S(1)} %fusion.103), kind=kOutput, calls=%fused_computation.10 | convolution fusion | flops 278921216 | bytes 10518528 | tf_op jit(solution)/shard_map/dot_general | solution.py:198
  84.4 2.7 %fusion.11 = (bf16[32,256,64]{1,2,0:T(8,128)(2,1)S(1)}, bf16[32,256,64]{1,2,0:T(8,128)(2,1)}) fusion(f32[32,256,64]{1,2,0:T(8,128)S(1)} %copy-done.3, f32[256,32,64]{0,2,1:T(8,128)S(1)} %fusion.20, bf16[32,32,64]{2,1,0:T(8,128)(2,1)S(1)} %get-tuple-element.31, f32[32]{0:T(128)S(1)} %get-tuple-element.33, s32[32]{0:T(128)S(1)} %add.121, ...), kind=kOutput, calls=%fused_computation.19 | convolution fusion | flops 41041920 | bytes 8520960 | tf_op jit(solution)/shard_map/krc,xk->rxc/dot_general | solution.py:143
  87.1 1.4 fusion.45
  88.5 1.4 fusion.42
  90.0 2.0 copy.29
  92.0 2.5 %reshape.104 = bf16[2,16,16384]{2,1,0:T(8,128)(2,1)} reshape(bf16[32,256,64]{2,1,0:T(8,128)(2,1)S(1)} %copy.29) | data formatting | bytes 2097152 | tf_op jit(solution)/shard_map/reshape | solution.py:204
  94.5 2.2 %pad_maximum_fusion.3 = f32[32,32,128]{2,0,1:T(8,128)} fusion(f32[32,32,64]{2,0,1:T(8,128)} %fusion.45, f32[32,32,64]{2,0,1:T(8,128)} %fusion.42), kind=kLoop, calls=%fused_computation.34 | loop fusion | flops 131072 | bytes 1048576 | tf_op jit(solution)/shard_map/concatenate | solution.py:137
  96.8 7.8 %convolution_convert_fusion = bf16[8192,64]{0,1:T(8,128)(2,1)S(1)} fusion(bf16[64,256]{1,0:T(8,128)(2,1)S(1)} %copy-done, bf16[8192,64]{0,1:T(8,128)(2,1)S(1)} %bitcast.55, bf16[256,64]{0,1:T(8,128)(2,1)} %param.10, f32[8192,256]{1,0:T(8,128)} %copy-done.2), kind=kOutput, calls=%fused_computation.3 | convolution fusion | flops 558366720 | bytes 10551296 | tf_op jit(solution)/shard_map/dot_general | solution.py:214
  104.7 1.1 copy.35
  105.7 1.7 reshape.106
  107.4 14.5 %reduce-scatter.5.cloned.1.call-done = f32[8,32,128]{2,0,1:T(8,128)} async-done(((f32[32,32,128]{2,0,1:T(8,128)}), f32[8,32,128]{2,0,1:T(8,128)}) %reduce-scatter.5.cloned.1.call-update) | async-done | bytes 131088 | tf_op jit(solution)/shard_map/reduce_scatter | solution.py:136
  123.7 1.5 collective-permute-start.9
  125.2 1.5 collective-permute-start.15
  127.3 1.5 collective-permute-start.17
  128.7 1.4 collective-permute-start.10
  130.4 1.3 constant_dynamic-update-slice_fusion.8
  132.6 1.3 collective-permute-start.12
  133.9 3.0 %collective-permute-start.11 = (bf16[2,1,16640]{2,1,0:T(2,128)(2,1)S(1)}, bf16[2,1,16640]{2,1,0:T(2,128)(2,1)S(1)}, u32[]{:S(2)}, u32[]{:S(2)}) collective-permute-start(bf16[2,1,16640]{2,1,0:T(2,128)(2,1)S(1)} %get-tuple-element.19), channel_id=1, source_target_pairs={{0,4},{1,5},{2,6},{3,7},{8,12},{9,13},{10,14},{11,15},{16,20},{17,... | collective-permute-start | bytes 199688 | tf_op jit(solution)/shard_map/ppermute | solution.py:19
  138.5 1.3 fusion.95
  139.8 1.3 collective-permute-start.14
  141.1 5.5 %collective-permute-start.13 = (bf16[1,18,16640]{2,1,0:T(8,128)(2,1)}, bf16[1,18,16640]{2,1,0:T(8,128)(2,1)}, u32[]{:S(2)}, u32[]{:S(2)}) collective-permute-start(bf16[1,18,16640]{2,1,0:T(8,128)(2,1)} %get-tuple-element.15), channel_id=1, source_target_pairs={{0,1},{1,2},{2,3},{4,5},{5,6},{6,7},{8,9},{9,10},{10,11},{12,13},{... | collective-permute-start | bytes 1797128 | tf_op jit(solution)/shard_map/ppermute | solution.py:19
  148.6 2.7 %copy.38 = f32[32,256,64]{2,1,0:T(8,128)} copy(f32[32,256,64]{1,2,0:T(8,128)S(1)} %add_bitcast_fusion) | data formatting | bytes 4194304 | tf_op jit(solution)/shard_map/add | solution.py:146
  151.3 2.9 %reshape.107 = f32[2,16,16384]{2,1,0:T(8,128)S(1)} reshape(f32[32,256,64]{2,1,0:T(8,128)} %copy.38) | data formatting | bytes 4194304 | tf_op jit(solution)/shard_map/reshape | solution.py:229
  154.2 14.6 %collective-permute-done.19 = f32[64,1024]{1,0:T(8,128)} collective-permute-done((f32[64,1024]{1,0:T(8,128)S(1)}, f32[64,1024]{1,0:T(8,128)}, u32[]{:S(2)}, u32[]{:S(2)}) %collective-permute-start.19) | collective-permute-done | bytes 262176 | tf_op jit(solution)/shard_map/ppermute | solution.py:65
  168.8 1.1 add.135
  169.9 3.3 %collective-permute-start.20 = (f32[64,1024]{1,0:T(8,128)S(1)}, f32[64,1024]{1,0:T(8,128)}, u32[]{:S(2)}, u32[]{:S(2)}) collective-permute-start(f32[64,1024]{1,0:T(8,128)S(1)} %add.135), channel_id=1, source_target_pairs={{0,2},{1,3},{2,0},{3,1},{4,6},{5,7},{6,4},{7,5},{8,10},{9,11},{10,... | collective-permute-start | bytes 786440 | tf_op jit(solution)/shard_map/ppermute | solution.py:65
  173.2 4.3 %maximum_convert_fusion.1.p_ref = f32[4,18,16640]{2,1,0:T(8,128)} fusion(bf16[1,18,16640]{2,1,0:T(8,128)(2,1)} %collective-permute-done.14, bf16[2,1,16640]{2,1,0:T(2,128)(2,1)} %copy-done.9, bf16[2,16,16640]{2,1,0:T(8,128)(2,1)S(1)} %constant_dynamic-update-slice_fusion.7, bf16[2,1,16640]{2,1,0:T(2,128)(2,1)} %copy-done.10, ...), kind=kLoop, calls=%fused_computation.12 | loop fusion | flops 11980800 | bytes 7188480 | tf_op jit(solution)/shard_map/convert_element_type | solution.py:130
  178.2 13.7 %shard_map.95 = f32[2,16,16384]{2,1,0:T(8,128)} custom-call(f32[4,18,16640]{2,1,0:T(8,128)} %maximum_convert_fusion.1.p_ref, f32[27,8,128]{2,1,0:T(8,128)} %broadcast_in_dim.36.w_ref), custom_call_target="tpu_custom_call" | custom-call | tf_op jit(solution)/shard_map/pallas_call | solution.py:127
  191.8 2.8 %add_convert_fusion = bf16[2,16,16384]{2,1,0:T(8,128)(2,1)} fusion(f32[2,16,16384]{2,1,0:T(8,128)} %shard_map.95, f32[2,16,16384]{2,1,0:T(8,128)S(1)} %reshape.107), kind=kLoop, calls=%fused_computation.21 | loop fusion | flops 1048576 | bytes 5242880 | tf_op jit(solution)/shard_map/convert_element_type | solution.py:229
  (107 shorter events, 22.5 us)
Async XLA Ops:
  7.2 68.3 %copy-start = (bf16[64,256]{1,0:T(8,128)(2,1)S(1)}, bf16[64,256]{1,0:T(8,128)(2,1)}, u32[]{:S(2)}) copy-start(bf16[64,256]{1,0:T(8,128)(2,1)} %param.9) | copy-start | bytes 98308
  7.2 58.9 %reduce-scatter.3.cloned.1.call-start = ((), (), s32[]{:S(2)}) async-start(), calls=%async_computation.2 | async-start | bytes 655360 | tf_op jit(solution)/shard_map/reduce_scatter | solution.py:136
  7.9 8.1 %collective-permute-start = (bf16[2,16,128]{2,1,0:T(8,128)(2,1)S(1)}, bf16[2,16,128]{2,1,0:T(8,128)(2,1)S(1)}, u32[]{:S(2)}, u32[]{:S(2)}) collective-permute-start(bf16[2,16,128]{2,1,0:T(8,128)(2,1)S(1)} %get-tuple-element.26), channel_id=1, source_target_pairs={{0,8},{8,16},{16,24},{24,0},{1,9},{9,17},{17,25},{25,1},{2,10},{10... | collective-permute-start | bytes 24584 | tf_op jit(solution)/shard_map/ppermute | solution.py:19
  10.9 5.3 %collective-permute-start.1 = (bf16[2,16,128]{2,1,0:T(8,128)(2,1)S(1)}, bf16[2,16,128]{2,1,0:T(8,128)(2,1)S(1)}, u32[]{:S(2)}, u32[]{:S(2)}) collective-permute-start(bf16[2,16,128]{2,1,0:T(8,128)(2,1)S(1)} %get-tuple-element.25), channel_id=1, source_target_pairs={{8,0},{16,8},{24,16},{0,24},{9,1},{17,9},{25,17},{1,25},{10,2},{18... | collective-permute-start | bytes 24584 | tf_op jit(solution)/shard_map/ppermute | solution.py:20
  14.9 1.2 copy-start.4
  16.4 5.4 %collective-permute-start.3 = (bf16[2,1,16640]{2,1,0:T(2,128)(2,1)S(1)}, bf16[2,1,16640]{2,1,0:T(2,128)(2,1)S(1)}, u32[]{:S(2)}, u32[]{:S(2)}) collective-permute-start(bf16[2,1,16640]{2,1,0:T(2,128)(2,1)S(1)} %get-tuple-element.22), channel_id=1, source_target_pairs={{4,0},{5,1},{6,2},{7,3},{12,8},{13,9},{14,10},{15,11},{20,16},{21,... | collective-permute-start | bytes 199688 | tf_op jit(solution)/shard_map/ppermute | solution.py:20
  17.7 4.1 %collective-permute-start.2 = (bf16[2,1,16640]{2,1,0:T(2,128)(2,1)S(1)}, bf16[2,1,16640]{2,1,0:T(2,128)(2,1)S(1)}, u32[]{:S(2)}, u32[]{:S(2)}) collective-permute-start(bf16[2,1,16640]{2,1,0:T(2,128)(2,1)S(1)} %get-tuple-element.21), channel_id=1, source_target_pairs={{0,4},{1,5},{2,6},{3,7},{8,12},{9,13},{10,14},{11,15},{16,20},{17,... | collective-permute-start | bytes 199688 | tf_op jit(solution)/shard_map/ppermute | solution.py:19
  21.8 100.2 %reduce-scatter.5.cloned.1.call-start = ((), (), s32[]{:S(2)}) async-start(), calls=%async_computation.3 | async-start | bytes 655360 | tf_op jit(solution)/shard_map/reduce_scatter | solution.py:136
  21.9 0.7 copy-start.11
  23.1 8.0 %copy-start.7 = (bf16[2,16,16384]{2,1,0:T(8,128)(2,1)S(1)}, bf16[2,16,16384]{2,1,0:T(8,128)(2,1)}, u32[]{:S(2)}) copy-start(bf16[2,16,16384]{2,1,0:T(8,128)(2,1)} %param.13) | copy-start | bytes 3145732
  24.4 22.3 %collective-permute-start.5 = (bf16[1,18,16640]{2,1,0:T(8,128)(2,1)}, bf16[1,18,16640]{2,1,0:T(8,128)(2,1)S(1)}, u32[]{:S(2)}, u32[]{:S(2)}) collective-permute-start(bf16[1,18,16640]{2,1,0:T(8,128)(2,1)} %get-tuple-element.18), channel_id=1, source_target_pairs={{1,0},{2,1},{3,2},{5,4},{6,5},{7,6},{9,8},{10,9},{11,10},{13,12},{... | collective-permute-start | bytes 1797128 | tf_op jit(solution)/shard_map/ppermute | solution.py:20
  25.7 22.3 %collective-permute-start.4 = (bf16[1,18,16640]{2,1,0:T(8,128)(2,1)}, bf16[1,18,16640]{2,1,0:T(8,128)(2,1)}, u32[]{:S(2)}, u32[]{:S(2)}) collective-permute-start(bf16[1,18,16640]{2,1,0:T(8,128)(2,1)} %get-tuple-element.17), channel_id=1, source_target_pairs={{0,1},{1,2},{2,3},{4,5},{5,6},{6,7},{8,9},{9,10},{10,11},{12,13},{... | collective-permute-start | bytes 1797128 | tf_op jit(solution)/shard_map/ppermute | solution.py:19
  34.4 3.8 %copy-start.6 = (bf16[32,64,64]{2,1,0:T(8,128)(2,1)S(1)}, bf16[32,64,64]{2,1,0:T(8,128)(2,1)}, u32[]{:S(2)}) copy-start(bf16[32,64,64]{2,1,0:T(8,128)(2,1)} %param.12) | copy-start | bytes 786436
  34.4 4.0 %copy-start.12 = (bf16[27,64]{1,0:T(8,128)(2,1)S(1)}, bf16[27,64]{1,0:T(8,128)(2,1)}, u32[]{:S(2)}) copy-start(bf16[27,64]{1,0:T(8,128)(2,1)} %param.8) | copy-start | bytes 10372
  67.9 13.2 %collective-permute-start.6 = (bf16[8,32,128]{2,1,0:T(8,128)(2,1)}, bf16[8,32,128]{2,1,0:T(8,128)(2,1)}, u32[]{:S(2)}, u32[]{:S(2)}) collective-permute-start(bf16[8,32,128]{2,1,0:T(8,128)(2,1)} %convolution_convert_fusion.2), channel_id=1, source_target_pairs={{0,8},{8,16},{16,24},{24,0},{1,9},{9,17},{17,25},{25,1},{2,10},{10... | collective-permute-start | bytes 196616 | tf_op jit(solution)/shard_map/ppermute | solution.py:55
  68.6 13.3 %collective-permute-start.7 = (bf16[8,32,128]{2,1,0:T(8,128)(2,1)}, bf16[8,32,128]{2,1,0:T(8,128)(2,1)}, u32[]{:S(2)}, u32[]{:S(2)}) collective-permute-start(bf16[8,32,128]{2,1,0:T(8,128)(2,1)} %convolution_convert_fusion.2), channel_id=1, source_target_pairs={{0,16},{8,24},{16,0},{24,8},{1,17},{9,25},{17,1},{25,9},{2,18},{10... | collective-permute-start | bytes 196616 | tf_op jit(solution)/shard_map/ppermute | solution.py:55
  70.1 12.6 %collective-permute-start.8 = (bf16[8,32,128]{2,1,0:T(8,128)(2,1)}, bf16[8,32,128]{2,1,0:T(8,128)(2,1)}, u32[]{:S(2)}, u32[]{:S(2)}) collective-permute-start(bf16[8,32,128]{2,1,0:T(8,128)(2,1)} %convolution_convert_fusion.2), channel_id=1, source_target_pairs={{0,24},{8,0},{16,8},{24,16},{1,25},{9,1},{17,9},{25,17},{2,26},{10... | collective-permute-start | bytes 196616 | tf_op jit(solution)/shard_map/ppermute | solution.py:55
  75.5 1.2 copy-start.13
  76.8 3.3 %copy-start.2 = (f32[8192,256]{1,0:T(8,128)}, f32[8192,256]{1,0:T(8,128)S(1)}, u32[]{:S(2)}) copy-start(f32[8192,256]{1,0:T(8,128)S(1)} %fusion.103) | copy-start | bytes 25165828
  80.0 4.4 %copy-start.3 = (f32[32,256,64]{1,2,0:T(8,128)S(1)}, f32[32,256,64]{1,2,0:T(8,128)}, u32[]{:S(2)}) copy-start(f32[32,256,64]{1,2,0:T(8,128)} %copy.30) | copy-start | bytes 6291460
  107.4 22.9 %copy-start.5 = (bf16[2,16,16384]{2,1,0:T(8,128)(2,1)}, bf16[2,16,16384]{2,1,0:T(8,128)(2,1)S(1)}, u32[]{:S(2)}) copy-start(bf16[2,16,16384]{2,1,0:T(8,128)(2,1)S(1)} %reshape.106) | copy-start | bytes 3145732
  123.7 6.6 %collective-permute-start.9 = (bf16[2,16,128]{2,1,0:T(8,128)(2,1)S(1)}, bf16[2,16,128]{2,1,0:T(8,128)(2,1)S(1)}, u32[]{:S(2)}, u32[]{:S(2)}) collective-permute-start(bf16[2,16,128]{2,1,0:T(8,128)(2,1)S(1)} %get-tuple-element.24), channel_id=1, source_target_pairs={{0,8},{8,16},{16,24},{24,0},{1,9},{9,17},{17,25},{25,1},{2,10},{10... | collective-permute-start | bytes 24584 | tf_op jit(solution)/shard_map/ppermute | solution.py:19
  125.2 8.7 %collective-permute-start.15 = (bf16[8,32,128]{2,1,0:T(8,128)(2,1)S(1)}, bf16[8,32,128]{2,1,0:T(8,128)(2,1)S(1)}, u32[]{:S(2)}, u32[]{:S(2)}) collective-permute-start(bf16[8,32,128]{2,1,0:T(8,128)(2,1)S(1)} %convolution_convert_fusion.1), channel_id=1, source_target_pairs={{0,8},{8,16},{16,24},{24,0},{1,9},{9,17},{17,25},{25,1},{2,10},{10... | collective-permute-start | bytes 196616 | tf_op jit(solution)/shard_map/ppermute | solution.py:55
  126.7 10.3 %collective-permute-start.16 = (bf16[8,32,128]{2,1,0:T(8,128)(2,1)S(1)}, bf16[8,32,128]{2,1,0:T(8,128)(2,1)S(1)}, u32[]{:S(2)}, u32[]{:S(2)}) collective-permute-start(bf16[8,32,128]{2,1,0:T(8,128)(2,1)S(1)} %convolution_convert_fusion.1), channel_id=1, source_target_pairs={{0,16},{8,24},{16,0},{24,8},{1,17},{9,25},{17,1},{25,9},{2,18},{10... | collective-permute-start | bytes 196616 | tf_op jit(solution)/shard_map/ppermute | solution.py:55
  127.3 9.7 %collective-permute-start.17 = (bf16[8,32,128]{2,1,0:T(8,128)(2,1)S(1)}, bf16[8,32,128]{2,1,0:T(8,128)(2,1)S(1)}, u32[]{:S(2)}, u32[]{:S(2)}) collective-permute-start(bf16[8,32,128]{2,1,0:T(8,128)(2,1)S(1)} %convolution_convert_fusion.1), channel_id=1, source_target_pairs={{0,24},{8,0},{16,8},{24,16},{1,25},{9,1},{17,9},{25,17},{2,26},{10... | collective-permute-start | bytes 196616 | tf_op jit(solution)/shard_map/ppermute | solution.py:55
  128.7 3.7 %collective-permute-start.10 = (bf16[2,16,128]{2,1,0:T(8,128)(2,1)S(1)}, bf16[2,16,128]{2,1,0:T(8,128)(2,1)S(1)}, u32[]{:S(2)}, u32[]{:S(2)}) collective-permute-start(bf16[2,16,128]{2,1,0:T(8,128)(2,1)S(1)} %get-tuple-element.23), channel_id=1, source_target_pairs={{8,0},{16,8},{24,16},{0,24},{9,1},{17,9},{25,17},{1,25},{10,2},{18... | collective-permute-start | bytes 24584 | tf_op jit(solution)/shard_map/ppermute | solution.py:20
  130.4 16.9 %collective-permute-start.18 = (f32[64,1024]{1,0:T(8,128)S(1)}, f32[64,1024]{1,0:T(8,128)S(1)}, u32[]{:S(2)}, u32[]{:S(2)}) collective-permute-start(f32[64,1024]{1,0:T(8,128)S(1)} %reshape.108), channel_id=1, source_target_pairs={{0,4},{4,0},{1,5},{5,1},{2,6},{6,2},{3,7},{7,3},{8,12},{12,8},{9,1... | collective-permute-start | bytes 786440 | tf_op jit(solution)/shard_map/ppermute | solution.py:65
  132.6 4.6 %collective-permute-start.12 = (bf16[2,1,16640]{2,1,0:T(2,128)(2,1)S(1)}, bf16[2,1,16640]{2,1,0:T(2,128)(2,1)S(1)}, u32[]{:S(2)}, u32[]{:S(2)}) collective-permute-start(bf16[2,1,16640]{2,1,0:T(2,128)(2,1)S(1)} %get-tuple-element.20), channel_id=1, source_target_pairs={{4,0},{5,1},{6,2},{7,3},{12,8},{13,9},{14,10},{15,11},{20,16},{21,... | collective-permute-start | bytes 199688 | tf_op jit(solution)/shard_map/ppermute | solution.py:20
  133.9 4.0 %collective-permute-start.11 = (bf16[2,1,16640]{2,1,0:T(2,128)(2,1)S(1)}, bf16[2,1,16640]{2,1,0:T(2,128)(2,1)S(1)}, u32[]{:S(2)}, u32[]{:S(2)}) collective-permute-start(bf16[2,1,16640]{2,1,0:T(2,128)(2,1)S(1)} %get-tuple-element.19), channel_id=1, source_target_pairs={{0,4},{1,5},{2,6},{3,7},{8,12},{9,13},{10,14},{11,15},{16,20},{17,... | collective-permute-start | bytes 199688 | tf_op jit(solution)/shard_map/ppermute | solution.py:19
  137.2 2.6 %copy-start.9 = (bf16[2,1,16640]{2,1,0:T(2,128)(2,1)}, bf16[2,1,16640]{2,1,0:T(2,128)(2,1)S(1)}, u32[]{:S(2)}) copy-start(bf16[2,1,16640]{2,1,0:T(2,128)(2,1)S(1)} %collective-permute-done.12) | copy-start | bytes 199684
  137.9 1.9 copy-start.10
  139.8 33.4 %collective-permute-start.14 = (bf16[1,18,16640]{2,1,0:T(8,128)(2,1)}, bf16[1,18,16640]{2,1,0:T(8,128)(2,1)}, u32[]{:S(2)}, u32[]{:S(2)}) collective-permute-start(bf16[1,18,16640]{2,1,0:T(8,128)(2,1)} %get-tuple-element.16), channel_id=1, source_target_pairs={{1,0},{2,1},{3,2},{5,4},{6,5},{7,6},{9,8},{10,9},{11,10},{13,12},{... | collective-permute-start | bytes 1797128 | tf_op jit(solution)/shard_map/ppermute | solution.py:20
  141.1 32.1 %collective-permute-start.13 = (bf16[1,18,16640]{2,1,0:T(8,128)(2,1)}, bf16[1,18,16640]{2,1,0:T(8,128)(2,1)}, u32[]{:S(2)}, u32[]{:S(2)}) collective-permute-start(bf16[1,18,16640]{2,1,0:T(8,128)(2,1)} %get-tuple-element.15), channel_id=1, source_target_pairs={{0,1},{1,2},{2,3},{4,5},{5,6},{6,7},{8,9},{9,10},{10,11},{12,13},{... | collective-permute-start | bytes 1797128 | tf_op jit(solution)/shard_map/ppermute | solution.py:19
  147.3 1.2 copy-start.8
  147.3 21.4 %collective-permute-start.19 = (f32[64,1024]{1,0:T(8,128)S(1)}, f32[64,1024]{1,0:T(8,128)}, u32[]{:S(2)}, u32[]{:S(2)}) collective-permute-start(f32[64,1024]{1,0:T(8,128)S(1)} %add.134), channel_id=1, source_target_pairs={{0,1},{1,0},{2,3},{3,2},{4,5},{5,4},{6,7},{7,6},{8,9},{9,8},{10,11... | collective-permute-start | bytes 786440 | tf_op jit(solution)/shard_map/ppermute | solution.py:65
  169.9 24.7 %collective-permute-start.20 = (f32[64,1024]{1,0:T(8,128)S(1)}, f32[64,1024]{1,0:T(8,128)}, u32[]{:S(2)}, u32[]{:S(2)}) collective-permute-start(f32[64,1024]{1,0:T(8,128)S(1)} %add.135), channel_id=1, source_target_pairs={{0,2},{1,3},{2,0},{3,1},{4,6},{5,7},{6,4},{7,5},{8,10},{9,11},{10,... | collective-permute-start | bytes 786440 | tf_op jit(solution)/shard_map/ppermute | solution.py:65
  191.8 4.7 %copy-start.1 = (bf16[64,256]{1,0:T(8,128)(2,1)S(1)}, bf16[64,256]{1,0:T(8,128)(2,1)}, u32[]{:S(2)}) copy-start(bf16[64,256]{1,0:T(8,128)(2,1)} %param.9) | copy-start | bytes 98308
Sparse Core Ops, SparseCore 0:
  21.9 25.6 reduce-scatter.2
  96.9 25.0 reduce-scatter.4

commit v8 on v3

--- a/solution.py
+++ b/solution.py
@@ -78,33 +78,37 @@
     return padded_2(x_wide, (("gy", 1), ("gz", 0)), 1, False)
 
 
-def stencil_kernel(chunk, x_pad, planes, y_cells, p_ref, w_ref, o_ref, s_ref):
-    s_ref[...] = p_ref[...].astype(jnp.float32)
+def stencil_kernel(chunk, x_pad, y_cells, rows, lo_ref, mid_ref, hi_ref, w_ref, o_ref):
     width = chunk + 2 * x_pad
-    count = o_ref.shape[2] // chunk
+    count = o_ref.shape[1] // chunk
+    shift = chunk + x_pad - x_pad // 2
+    side = (chunk + x_pad) // 128
+    sources = (lo_ref, mid_ref, hi_ref)
 
     def body(index, carry):
         base = pl.multiple_of(index * chunk, chunk)
-        for plane in range(planes):
-            left = jnp.zeros((y_cells, chunk + x_pad), jnp.float32)
-            centre = jnp.zeros((y_cells, chunk), jnp.float32)
-            right = jnp.zeros((y_cells, chunk + x_pad), jnp.float32)
+        for row in range(0, y_cells, rows):
+            left = jnp.zeros((rows, chunk + x_pad), jnp.float32)
+            centre = jnp.zeros((rows, chunk), jnp.float32)
+            right = jnp.zeros((rows, chunk + x_pad), jnp.float32)
             for step_z in range(3):
                 for step_y in range(3):
-                    window = s_ref[plane + step_z, pl.ds(step_y, y_cells), pl.ds(base, width)]
+                    window = sources[step_z][pl.ds(row + step_y, rows), pl.ds(base, width)].astype(
+                        jnp.float32
+                    )
                     tap = 9 * step_z + 3 * step_y
-                    left = left + window[:, : chunk + x_pad] * w_ref[tap : tap + 1, : chunk + x_pad]
-                    centre = centre + window[:, x_pad : x_pad + chunk] * w_ref[
-                        tap + 1 : tap + 2, :chunk
-                    ]
-                    right = right + window[:, x_pad:] * w_ref[tap + 2 : tap + 3, : chunk + x_pad]
-            shift = chunk + x_pad - x_pad // 2
+                    gain_l = jnp.concatenate([w_ref[tap]] * side, axis=1)
+                    gain_c = jnp.concatenate([w_ref[tap + 1]] * (side - 1), axis=1)
+                    gain_r = jnp.concatenate([w_ref[tap + 2]] * side, axis=1)
+                    left = left + window[:, : chunk + x_pad] * gain_l
+                    centre = centre + window[:, x_pad : x_pad + chunk] * gain_c
+                    right = right + window[:, x_pad:] * gain_r
             total = (
                 centre
                 + pltpu.roll(left, shift, 1)[:, :chunk]
                 + pltpu.roll(right, shift, 1)[:, :chunk]
             )
-            o_ref[plane, :, pl.ds(base, chunk)] = total.astype(o_ref.dtype)
+            o_ref[pl.ds(row, rows), pl.ds(base, chunk)] = total.astype(o_ref.dtype)
         return carry
 
     lax.fori_loop(0, count, body, 0)
@@ -115,16 +119,26 @@
     y_cells = padded.shape[1] - 2
     x_pad = 2 * channels
     lanes = x_cells * channels
-    chunk = min(512, lanes)
+    chunk = min(1024, lanes)
+    rows = 8 if y_cells % 8 == 0 else y_cells
     if flipped:
         taps = taps[::-1]
-    gains = jnp.tile(taps.astype(jnp.float32), (1, (chunk + x_pad) // channels))
-    kernel = functools.partial(stencil_kernel, chunk, x_pad, planes, y_cells)
+    gains = jnp.tile(taps.astype(jnp.float32), (1, 128 // channels))
+    gains = jnp.broadcast_to(gains[:, None, :], (gains.shape[0], rows, 128))
+    kernel = functools.partial(stencil_kernel, chunk, x_pad, y_cells, rows)
+    plane_block = padded.shape[1:]
+    in_specs = [
+        pl.BlockSpec((None,) + plane_block, functools.partial(lambda d, z: (z + d, 0, 0), d))
+        for d in range(3)
+    ]
+    in_specs.append(pl.BlockSpec(gains.shape, lambda z: (0, 0, 0)))
     return pl.pallas_call(
         kernel,
+        grid=(planes,),
+        in_specs=in_specs,
+        out_specs=pl.BlockSpec((None, y_cells, lanes), lambda z: (z, 0, 0)),
         out_shape=jax.ShapeDtypeStruct((planes, y_cells, lanes), out_dtype),
-        scratch_shapes=[pltpu.VMEM(padded.shape, jnp.float32)],
-    )(padded, gains)
+    )(padded, padded, padded, gains)
 
 
 def share_terms(field3, cos_table, sin_table):
@@ -152,7 +166,8 @@
 
 
 def sum_gradients(local_grads):
-    return butterfly_sum(butterfly_sum(local_grads, "gy"), "gz")
+    flat = local_grads.reshape(-1, 1024)
+    return butterfly_sum(butterfly_sum(flat, "gy"), "gz").reshape(local_grads.shape)
 
 
 def per_device(

time: 211 us -> 201 us (0.953)
  waiting for transfers between devices: 45.6 us -> 38.6 us
  other arithmetic: 22 us -> 19.1 us
    ppermute x3, waiting for transfers between devices: 23.2 us -> 14.6 us  [butterfly_sum(): lax.ppermute(value, axis, [(i, i ^ step) for i in range(size)])]
    add x3, other arithmetic: 4.97 us -> 2.07 us  [butterfly_sum(): value + lax.ppermute(value, axis, [(i, i ^ step) for i in range(size)])]
    unnamed x34 -> x38, local copies, waits for them, and re-layouts: 5.99 us -> 5.36 us
  transfers between devices with their start and end apart: 23 -> 23, of which waited for: 7 -> 6; matrix products, arithmetic and copies ran while one was open for 29% -> 29% of each run, Pallas kernels for 12% -> 13%
where the time goes in v8:
time: 201 us
  starting transfers between devices  41.3 us (21%)
  local copies, waits for them, and re-layouts  39 us (19%)
  waiting for transfers between devices  38.6 us (19%)
  Pallas kernels  26.2 us (13%)
  matrix products  21.7 us (11%)
  other arithmetic  19.1 us (10%)
  between operations  14.6 us (7%)
    pallas_call x2, Pallas kernels, depthwise(): pl.pallas_call(kernel, grid=(planes,), in_specs=in_specs, out_specs=pl.Bl...  26.2 us
    ppermute x6, starting transfers between devices, padded_2(): before = lax.ppermute(last, axis, up)  21.5 us
    ppermute x3, waiting for transfers between devices, butterfly_sum(): lax.ppermute(value, axis, [(i, i ^ step) for i in range(size)])  14.6 us
    reduce_scatter x2, waiting for transfers between devices, share_terms(): lax.psum_scatter(jnp.concatenate([real_part, imag_part], axis=2), 'gx', s...  14.5 us
    ppermute x6, starting transfers between devices, ring_gather(): lax.ppermute(block, axis, [(i, (i + shift) % size) for i in range(size)])  8.11 us
    dot_general x1, matrix products, per_device(): jnp.dot(grad_hidden, expand_weight.T, preferred_element_type=jnp.float32)  7.84 us
    concatenate x4, other arithmetic, padded_2(): value = jnp.concatenate([before, value, after], axis=dim)  7.63 us
    ppermute x6, starting transfers between devices, padded_2(): after = lax.ppermute(leading, axis, down)  7.53 us
  transfers between devices with their start and end apart: 23, of which 6 were waited for; matrix products, arithmetic and copies ran while one was open for 29% of the time, Pallas kernels for 13%

profile of v8, /device:TPU:0, one launch (start us, length us, event | category | flops | bytes accessed | tf_op | source)
XLA Modules:
  0.0 200.6 jit_solution(15588573714363795795)
XLA Ops:
  7.9 2.9 %collective-permute-start = (bf16[2,16,128]{2,1,0:T(8,128)(2,1)S(1)}, bf16[2,16,128]{2,1,0:T(8,128)(2,1)S(1)}, u32[]{:S(2)}, u32[]{:S(2)}) collective-permute-start(bf16[2,16,128]{2,1,0:T(8,128)(2,1)S(1)} %get-tuple-element.26), channel_id=1, source_target_pairs={{0,8},{8,16},{16,24},{24,0},{1,9},{9,17},{17,25},{25,1},{2,10},{10... | collective-permute-start | bytes 24584 | tf_op jit(solution)/shard_map/ppermute | solution.py:19
  11.8 3.0 %reshape.101 = bf16[32,256,64]{2,1,0:T(8,128)(2,1)S(1)} reshape(bf16[2,16,16384]{2,1,0:T(8,128)(2,1)} %param.7) | data formatting | bytes 2097152 | tf_op jit(solution)/shard_map/reshape | solution.py:197
  16.4 1.3 collective-permute-start.3
  17.7 3.0 %collective-permute-start.2 = (bf16[2,1,16640]{2,1,0:T(2,128)(2,1)S(1)}, bf16[2,1,16640]{2,1,0:T(2,128)(2,1)S(1)}, u32[]{:S(2)}, u32[]{:S(2)}) collective-permute-start(bf16[2,1,16640]{2,1,0:T(2,128)(2,1)S(1)} %get-tuple-element.21), channel_id=1, source_target_pairs={{0,4},{1,5},{2,6},{3,7},{8,12},{9,13},{10,14},{11,15},{16,20},{17,... | collective-permute-start | bytes 199688 | tf_op jit(solution)/shard_map/ppermute | solution.py:19
  20.8 1.0 pad_maximum_fusion.4
  23.2 1.3 fusion.96
  24.4 1.3 collective-permute-start.5
  25.7 5.5 %collective-permute-start.4 = (bf16[1,18,16640]{2,1,0:T(8,128)(2,1)}, bf16[1,18,16640]{2,1,0:T(8,128)(2,1)}, u32[]{:S(2)}, u32[]{:S(2)}) collective-permute-start(bf16[1,18,16640]{2,1,0:T(8,128)(2,1)} %get-tuple-element.17), channel_id=1, source_target_pairs={{0,1},{1,2},{2,3},{4,5},{5,6},{6,7},{8,9},{9,10},{10,11},{12,13},{... | collective-permute-start | bytes 1797128 | tf_op jit(solution)/shard_map/ppermute | solution.py:19
  31.2 3.2 %reshape.110 = f32[32,256,64]{2,1,0:T(8,128)} reshape(bf16[2,16,16384]{2,1,0:T(8,128)(2,1)S(1)} %copy-done.7) | data formatting | bytes 3145728 | tf_op jit(solution)/shard_map/convert_element_type | solution.py:217
  34.5 3.8 %copy.30 = f32[32,256,64]{1,2,0:T(8,128)} copy(f32[32,256,64]{2,1,0:T(8,128)} %reshape.110) | data formatting | bytes 4194304 | tf_op jit(solution)/shard_map/convert_element_type | solution.py:217
  38.8 1.1 fusion.13
  40.0 6.8 %collective-permute-done.5 = bf16[1,18,16640]{2,1,0:T(8,128)(2,1)S(1)} collective-permute-done((bf16[1,18,16640]{2,1,0:T(8,128)(2,1)}, bf16[1,18,16640]{2,1,0:T(8,128)(2,1)S(1)}, u32[]{:S(2)}, u32[]{:S(2)}) %collective-permute-start.5) | collective-permute-done | bytes 599072 | tf_op jit(solution)/shard_map/ppermute | solution.py:20
  46.8 1.3 collective-permute-done.4
  48.0 3.1 %pad_maximum_fusion.lo_ref.mid_ref.hi_ref = bf16[4,18,16640]{2,1,0:T(8,128)(2,1)} fusion(bf16[1,18,16640]{2,1,0:T(8,128)(2,1)S(1)} %collective-permute-done.5, bf16[2,1,16640]{2,1,0:T(2,128)(2,1)S(1)} %collective-permute-done.3, bf16[2,16,16640]{2,1,0:T(8,128)(2,1)S(1)} %constant_dynamic-update-slice_fusion, bf16[2,1,16640]{2,1,0:T(2,128)(2,1)} %copy-done.11, ...), kind=kLoop, calls=%fused_computation.11 | loop fusion | flops 11980800 | bytes 4792320 | tf_op jit(solution)/shard_map/concatenate | solution.py:21
  51.8 13.0 %shard_map.94 = bf16[2,16,16384]{2,1,0:T(8,128)(2,1)} custom-call(bf16[4,18,16640]{2,1,0:T(8,128)(2,1)} %pad_maximum_fusion.lo_ref.mid_ref.hi_ref, bf16[4,18,16640]{2,1,0:T(8,128)(2,1)} %pad_maximum_fusion.lo_ref.mid_ref.hi_ref, bf16[4,18,16640]{2,1,0:T(8,128)(2,1)} %pad_maximum_fusion.lo_ref.mid_ref.hi_ref, f32[27,8,128]{2,1,0:T(8,128)} %broadcast_in_dim.18.w_ref), custom_call_target="tpu_custom_call" | custom-call | tf_op jit(solution)/shard_map/pallas_call | solution.py:135
  67.3 1.5 collective-permute-start.7
  68.8 2.3 %collective-permute-start.8 = (bf16[8,32,128]{2,1,0:T(8,128)(2,1)}, bf16[8,32,128]{2,1,0:T(8,128)(2,1)}, u32[]{:S(2)}, u32[]{:S(2)}) collective-permute-start(bf16[8,32,128]{2,1,0:T(8,128)(2,1)} %convolution_convert_fusion.2), channel_id=1, source_target_pairs={{0,24},{8,0},{16,8},{24,16},{1,25},{9,1},{17,9},{25,17},{2,26},{10... | collective-permute-start | bytes 196616 | tf_op jit(solution)/shard_map/ppermute | solution.py:55
  71.2 3.0 %reshape.102 = bf16[8192,64]{1,0:T(8,128)(2,1)S(1)} reshape(bf16[2,16,16384]{2,1,0:T(8,128)(2,1)} %shard_map.94) | data formatting | bytes 2097152 | tf_op jit(solution)/shard_map/reshape | solution.py:206
  74.2 1.2 fusion.103
  75.5 2.8 %fusion.5 = f32[8192,64]{0,1:T(8,128)S(1)} fusion(bf16[256,64]{0,1:T(8,128)(2,1)S(1)} %copy-done.13, f32[8192,256]{1,0:T(8,128)S(1)} %fusion.103), kind=kOutput, calls=%fused_computation.10 | convolution fusion | flops 278921216 | bytes 10518528 | tf_op jit(solution)/shard_map/dot_general | solution.py:209
  83.1 2.7 %fusion.11 = (bf16[32,256,64]{1,2,0:T(8,128)(2,1)S(1)}, bf16[32,256,64]{1,2,0:T(8,128)(2,1)}) fusion(f32[32,256,64]{1,2,0:T(8,128)S(1)} %copy-done.3, f32[256,32,64]{0,2,1:T(8,128)S(1)} %fusion.20, bf16[32,32,64]{2,1,0:T(8,128)(2,1)S(1)} %get-tuple-element.31, f32[32]{0:T(128)S(1)} %get-tuple-element.33, s32[32]{0:T(128)S(1)} %add.121, ...), kind=kOutput, calls=%fused_computation.19 | convolution fusion | flops 41041920 | bytes 8520960 | tf_op jit(solution)/shard_map/krc,xk->rxc/dot_general | solution.py:154
  85.8 1.4 fusion.45
  87.2 1.4 fusion.42
  88.7 2.0 %copy.29 = bf16[32,256,64]{2,1,0:T(8,128)(2,1)S(1)} copy(bf16[32,256,64]{1,2,0:T(8,128)(2,1)} %get-tuple-element.14) | data formatting | bytes 2097152 | tf_op jit(solution)/shard_map/convert_element_type | solution.py:215
  90.7 2.5 %reshape.104 = bf16[2,16,16384]{2,1,0:T(8,128)(2,1)} reshape(bf16[32,256,64]{2,1,0:T(8,128)(2,1)S(1)} %copy.29) | data formatting | bytes 2097152 | tf_op jit(solution)/shard_map/reshape | solution.py:215
  93.2 2.2 %pad_maximum_fusion.5 = f32[32,32,128]{2,0,1:T(8,128)} fusion(f32[32,32,64]{2,0,1:T(8,128)} %fusion.45, f32[32,32,64]{2,0,1:T(8,128)} %fusion.42), kind=kLoop, calls=%fused_computation.34 | loop fusion | flops 131072 | bytes 1048576 | tf_op jit(solution)/shard_map/concatenate | solution.py:148
  95.5 7.8 %convolution_convert_fusion = bf16[8192,64]{0,1:T(8,128)(2,1)S(1)} fusion(bf16[64,256]{1,0:T(8,128)(2,1)S(1)} %copy-done, bf16[8192,64]{0,1:T(8,128)(2,1)S(1)} %bitcast.55, bf16[256,64]{0,1:T(8,128)(2,1)} %param.10, f32[8192,256]{1,0:T(8,128)} %copy-done.2), kind=kOutput, calls=%fused_computation.3 | convolution fusion | flops 558366720 | bytes 10551296 | tf_op jit(solution)/shard_map/dot_general | solution.py:225
  103.4 1.1 copy.35
  104.5 1.7 reshape.106
  106.2 14.5 %reduce-scatter.5.cloned.1.call-done = f32[8,32,128]{2,0,1:T(8,128)} async-done(((f32[32,32,128]{2,0,1:T(8,128)}), f32[8,32,128]{2,0,1:T(8,128)}) %reduce-scatter.5.cloned.1.call-update) | async-done | bytes 131088 | tf_op jit(solution)/shard_map/reduce_scatter | solution.py:147
  122.4 1.5 collective-permute-start.9
  123.9 1.5 collective-permute-start.15
  126.0 1.5 collective-permute-start.17
  127.4 1.4 collective-permute-start.10
  129.2 1.3 constant_dynamic-update-slice_fusion.8
  131.3 1.3 collective-permute-start.12
  132.6 3.0 %collective-permute-start.11 = (bf16[2,1,16640]{2,1,0:T(2,128)(2,1)S(1)}, bf16[2,1,16640]{2,1,0:T(2,128)(2,1)S(1)}, u32[]{:S(2)}, u32[]{:S(2)}) collective-permute-start(bf16[2,1,16640]{2,1,0:T(2,128)(2,1)S(1)} %get-tuple-element.19), channel_id=1, source_target_pairs={{0,4},{1,5},{2,6},{3,7},{8,12},{9,13},{10,14},{11,15},{16,20},{17,... | collective-permute-start | bytes 199688 | tf_op jit(solution)/shard_map/ppermute | solution.py:19
  137.3 1.3 fusion.95
  138.5 1.3 collective-permute-start.14
  139.8 5.5 %collective-permute-start.13 = (bf16[1,18,16640]{2,1,0:T(8,128)(2,1)}, bf16[1,18,16640]{2,1,0:T(8,128)(2,1)}, u32[]{:S(2)}, u32[]{:S(2)}) collective-permute-start(bf16[1,18,16640]{2,1,0:T(8,128)(2,1)} %get-tuple-element.15), channel_id=1, source_target_pairs={{0,1},{1,2},{2,3},{4,5},{5,6},{6,7},{8,9},{9,10},{10,11},{12,13},{... | collective-permute-start | bytes 1797128 | tf_op jit(solution)/shard_map/ppermute | solution.py:19
  147.3 2.7 %copy.38 = f32[32,256,64]{2,1,0:T(8,128)} copy(f32[32,256,64]{1,2,0:T(8,128)S(1)} %add_bitcast_fusion) | data formatting | bytes 4194304 | tf_op jit(solution)/shard_map/add | solution.py:157
  150.0 2.9 %reshape.107 = f32[2,16,16384]{2,1,0:T(8,128)S(1)} reshape(f32[32,256,64]{2,1,0:T(8,128)} %copy.38) | data formatting | bytes 4194304 | tf_op jit(solution)/shard_map/reshape | solution.py:240
  152.9 14.6 %collective-permute-done.19 = f32[64,1024]{1,0:T(8,128)} collective-permute-done((f32[64,1024]{1,0:T(8,128)S(1)}, f32[64,1024]{1,0:T(8,128)}, u32[]{:S(2)}, u32[]{:S(2)}) %collective-permute-start.19) | collective-permute-done | bytes 262176 | tf_op jit(solution)/shard_map/ppermute | solution.py:65
  167.5 1.1 add.135
  168.6 3.4 %collective-permute-start.20 = (f32[64,1024]{1,0:T(8,128)S(1)}, f32[64,1024]{1,0:T(8,128)}, u32[]{:S(2)}, u32[]{:S(2)}) collective-permute-start(f32[64,1024]{1,0:T(8,128)S(1)} %add.135), channel_id=1, source_target_pairs={{0,2},{1,3},{2,0},{3,1},{4,6},{5,7},{6,4},{7,5},{8,10},{9,11},{10,... | collective-permute-start | bytes 786440 | tf_op jit(solution)/shard_map/ppermute | solution.py:65
  171.9 3.3 %pad_maximum_fusion.1.lo_ref.mid_ref.hi_ref = bf16[4,18,16640]{2,1,0:T(8,128)(2,1)} fusion(bf16[1,18,16640]{2,1,0:T(8,128)(2,1)} %collective-permute-done.14, bf16[2,1,16640]{2,1,0:T(2,128)(2,1)} %copy-done.9, bf16[2,16,16640]{2,1,0:T(8,128)(2,1)S(1)} %constant_dynamic-update-slice_fusion.7, bf16[2,1,16640]{2,1,0:T(2,128)(2,1)} %copy-done.10, ...), kind=kLoop, calls=%fused_computation.12 | loop fusion | flops 11980800 | bytes 4792320 | tf_op jit(solution)/shard_map/concatenate | solution.py:21
  175.9 13.2 %shard_map.95 = f32[2,16,16384]{2,1,0:T(8,128)} custom-call(bf16[4,18,16640]{2,1,0:T(8,128)(2,1)} %pad_maximum_fusion.1.lo_ref.mid_ref.hi_ref, bf16[4,18,16640]{2,1,0:T(8,128)(2,1)} %pad_maximum_fusion.1.lo_ref.mid_ref.hi_ref, bf16[4,18,16640]{2,1,0:T(8,128)(2,1)} %pad_maximum_fusion.1.lo_ref.mid_ref.hi_ref, f32[27,8,128]{2,1,0:T(8,128)} %broadcast_in_dim.36.w_ref), custom_call_target="tpu_custom_call" | custom-call | tf_op jit(solution)/shard_map/pallas_call | solution.py:135
  189.1 2.8 %add_convert_fusion = bf16[2,16,16384]{2,1,0:T(8,128)(2,1)} fusion(f32[2,16,16384]{2,1,0:T(8,128)} %shard_map.95, f32[2,16,16384]{2,1,0:T(8,128)S(1)} %reshape.107), kind=kLoop, calls=%fused_computation.21 | loop fusion | flops 1048576 | bytes 5242880 | tf_op jit(solution)/shard_map/convert_element_type | solution.py:240
  (107 shorter events, 22.5 us)
Async XLA Ops:
  7.2 67.1 %copy-start = (bf16[64,256]{1,0:T(8,128)(2,1)S(1)}, bf16[64,256]{1,0:T(8,128)(2,1)}, u32[]{:S(2)}) copy-start(bf16[64,256]{1,0:T(8,128)(2,1)} %param.9) | copy-start | bytes 98308
  7.2 57.7 %reduce-scatter.3.cloned.1.call-start = ((), (), s32[]{:S(2)}) async-start(), calls=%async_computation.2 | async-start | bytes 655360 | tf_op jit(solution)/shard_map/reduce_scatter | solution.py:147
  7.9 8.1 %collective-permute-start = (bf16[2,16,128]{2,1,0:T(8,128)(2,1)S(1)}, bf16[2,16,128]{2,1,0:T(8,128)(2,1)S(1)}, u32[]{:S(2)}, u32[]{:S(2)}) collective-permute-start(bf16[2,16,128]{2,1,0:T(8,128)(2,1)S(1)} %get-tuple-element.26), channel_id=1, source_target_pairs={{0,8},{8,16},{16,24},{24,0},{1,9},{9,17},{17,25},{25,1},{2,10},{10... | collective-permute-start | bytes 24584 | tf_op jit(solution)/shard_map/ppermute | solution.py:19
  10.9 5.3 %collective-permute-start.1 = (bf16[2,16,128]{2,1,0:T(8,128)(2,1)S(1)}, bf16[2,16,128]{2,1,0:T(8,128)(2,1)S(1)}, u32[]{:S(2)}, u32[]{:S(2)}) collective-permute-start(bf16[2,16,128]{2,1,0:T(8,128)(2,1)S(1)} %get-tuple-element.25), channel_id=1, source_target_pairs={{8,0},{16,8},{24,16},{0,24},{9,1},{17,9},{25,17},{1,25},{10,2},{18... | collective-permute-start | bytes 24584 | tf_op jit(solution)/shard_map/ppermute | solution.py:20
  14.9 1.2 copy-start.4
  16.4 5.4 %collective-permute-start.3 = (bf16[2,1,16640]{2,1,0:T(2,128)(2,1)S(1)}, bf16[2,1,16640]{2,1,0:T(2,128)(2,1)S(1)}, u32[]{:S(2)}, u32[]{:S(2)}) collective-permute-start(bf16[2,1,16640]{2,1,0:T(2,128)(2,1)S(1)} %get-tuple-element.22), channel_id=1, source_target_pairs={{4,0},{5,1},{6,2},{7,3},{12,8},{13,9},{14,10},{15,11},{20,16},{21,... | collective-permute-start | bytes 199688 | tf_op jit(solution)/shard_map/ppermute | solution.py:20
  17.7 4.1 %collective-permute-start.2 = (bf16[2,1,16640]{2,1,0:T(2,128)(2,1)S(1)}, bf16[2,1,16640]{2,1,0:T(2,128)(2,1)S(1)}, u32[]{:S(2)}, u32[]{:S(2)}) collective-permute-start(bf16[2,1,16640]{2,1,0:T(2,128)(2,1)S(1)} %get-tuple-element.21), channel_id=1, source_target_pairs={{0,4},{1,5},{2,6},{3,7},{8,12},{9,13},{10,14},{11,15},{16,20},{17,... | collective-permute-start | bytes 199688 | tf_op jit(solution)/shard_map/ppermute | solution.py:19
  21.8 98.9 %reduce-scatter.5.cloned.1.call-start = ((), (), s32[]{:S(2)}) async-start(), calls=%async_computation.3 | async-start | bytes 655360 | tf_op jit(solution)/shard_map/reduce_scatter | solution.py:147
  21.9 0.7 copy-start.11
  23.1 8.1 %copy-start.7 = (bf16[2,16,16384]{2,1,0:T(8,128)(2,1)S(1)}, bf16[2,16,16384]{2,1,0:T(8,128)(2,1)}, u32[]{:S(2)}) copy-start(bf16[2,16,16384]{2,1,0:T(8,128)(2,1)} %param.13) | copy-start | bytes 3145732
  24.4 22.3 %collective-permute-start.5 = (bf16[1,18,16640]{2,1,0:T(8,128)(2,1)}, bf16[1,18,16640]{2,1,0:T(8,128)(2,1)S(1)}, u32[]{:S(2)}, u32[]{:S(2)}) collective-permute-start(bf16[1,18,16640]{2,1,0:T(8,128)(2,1)} %get-tuple-element.18), channel_id=1, source_target_pairs={{1,0},{2,1},{3,2},{5,4},{6,5},{7,6},{9,8},{10,9},{11,10},{13,12},{... | collective-permute-start | bytes 1797128 | tf_op jit(solution)/shard_map/ppermute | solution.py:20
  25.7 22.3 %collective-permute-start.4 = (bf16[1,18,16640]{2,1,0:T(8,128)(2,1)}, bf16[1,18,16640]{2,1,0:T(8,128)(2,1)}, u32[]{:S(2)}, u32[]{:S(2)}) collective-permute-start(bf16[1,18,16640]{2,1,0:T(8,128)(2,1)} %get-tuple-element.17), channel_id=1, source_target_pairs={{0,1},{1,2},{2,3},{4,5},{5,6},{6,7},{8,9},{9,10},{10,11},{12,13},{... | collective-permute-start | bytes 1797128 | tf_op jit(solution)/shard_map/ppermute | solution.py:19
  34.5 3.8 %copy-start.6 = (bf16[32,64,64]{2,1,0:T(8,128)(2,1)S(1)}, bf16[32,64,64]{2,1,0:T(8,128)(2,1)}, u32[]{:S(2)}) copy-start(bf16[32,64,64]{2,1,0:T(8,128)(2,1)} %param.12) | copy-start | bytes 786436
  34.5 4.0 %copy-start.12 = (bf16[27,64]{1,0:T(8,128)(2,1)S(1)}, bf16[27,64]{1,0:T(8,128)(2,1)}, u32[]{:S(2)}) copy-start(bf16[27,64]{1,0:T(8,128)(2,1)} %param.8) | copy-start | bytes 10372
  66.6 13.2 %collective-permute-start.6 = (bf16[8,32,128]{2,1,0:T(8,128)(2,1)}, bf16[8,32,128]{2,1,0:T(8,128)(2,1)}, u32[]{:S(2)}, u32[]{:S(2)}) collective-permute-start(bf16[8,32,128]{2,1,0:T(8,128)(2,1)} %convolution_convert_fusion.2), channel_id=1, source_target_pairs={{0,8},{8,16},{16,24},{24,0},{1,9},{9,17},{17,25},{25,1},{2,10},{10... | collective-permute-start | bytes 196616 | tf_op jit(solution)/shard_map/ppermute | solution.py:55
  67.3 13.3 %collective-permute-start.7 = (bf16[8,32,128]{2,1,0:T(8,128)(2,1)}, bf16[8,32,128]{2,1,0:T(8,128)(2,1)}, u32[]{:S(2)}, u32[]{:S(2)}) collective-permute-start(bf16[8,32,128]{2,1,0:T(8,128)(2,1)} %convolution_convert_fusion.2), channel_id=1, source_target_pairs={{0,16},{8,24},{16,0},{24,8},{1,17},{9,25},{17,1},{25,9},{2,18},{10... | collective-permute-start | bytes 196616 | tf_op jit(solution)/shard_map/ppermute | solution.py:55
  68.8 12.6 %collective-permute-start.8 = (bf16[8,32,128]{2,1,0:T(8,128)(2,1)}, bf16[8,32,128]{2,1,0:T(8,128)(2,1)}, u32[]{:S(2)}, u32[]{:S(2)}) collective-permute-start(bf16[8,32,128]{2,1,0:T(8,128)(2,1)} %convolution_convert_fusion.2), channel_id=1, source_target_pairs={{0,24},{8,0},{16,8},{24,16},{1,25},{9,1},{17,9},{25,17},{2,26},{10... | collective-permute-start | bytes 196616 | tf_op jit(solution)/shard_map/ppermute | solution.py:55
  74.2 1.2 copy-start.13
  75.5 3.3 %copy-start.2 = (f32[8192,256]{1,0:T(8,128)}, f32[8192,256]{1,0:T(8,128)S(1)}, u32[]{:S(2)}) copy-start(f32[8192,256]{1,0:T(8,128)S(1)} %fusion.103) | copy-start | bytes 25165828
  78.8 4.3 %copy-start.3 = (f32[32,256,64]{1,2,0:T(8,128)S(1)}, f32[32,256,64]{1,2,0:T(8,128)}, u32[]{:S(2)}) copy-start(f32[32,256,64]{1,2,0:T(8,128)} %copy.30) | copy-start | bytes 6291460
  106.2 22.9 %copy-start.5 = (bf16[2,16,16384]{2,1,0:T(8,128)(2,1)}, bf16[2,16,16384]{2,1,0:T(8,128)(2,1)S(1)}, u32[]{:S(2)}) copy-start(bf16[2,16,16384]{2,1,0:T(8,128)(2,1)S(1)} %reshape.106) | copy-start | bytes 3145732
  122.4 6.6 %collective-permute-start.9 = (bf16[2,16,128]{2,1,0:T(8,128)(2,1)S(1)}, bf16[2,16,128]{2,1,0:T(8,128)(2,1)S(1)}, u32[]{:S(2)}, u32[]{:S(2)}) collective-permute-start(bf16[2,16,128]{2,1,0:T(8,128)(2,1)S(1)} %get-tuple-element.24), channel_id=1, source_target_pairs={{0,8},{8,16},{16,24},{24,0},{1,9},{9,17},{17,25},{25,1},{2,10},{10... | collective-permute-start | bytes 24584 | tf_op jit(solution)/shard_map/ppermute | solution.py:19
  123.9 8.7 %collective-permute-start.15 = (bf16[8,32,128]{2,1,0:T(8,128)(2,1)S(1)}, bf16[8,32,128]{2,1,0:T(8,128)(2,1)S(1)}, u32[]{:S(2)}, u32[]{:S(2)}) collective-permute-start(bf16[8,32,128]{2,1,0:T(8,128)(2,1)S(1)} %convolution_convert_fusion.1), channel_id=1, source_target_pairs={{0,8},{8,16},{16,24},{24,0},{1,9},{9,17},{17,25},{25,1},{2,10},{10... | collective-permute-start | bytes 196616 | tf_op jit(solution)/shard_map/ppermute | solution.py:55
  125.4 10.3 %collective-permute-start.16 = (bf16[8,32,128]{2,1,0:T(8,128)(2,1)S(1)}, bf16[8,32,128]{2,1,0:T(8,128)(2,1)S(1)}, u32[]{:S(2)}, u32[]{:S(2)}) collective-permute-start(bf16[8,32,128]{2,1,0:T(8,128)(2,1)S(1)} %convolution_convert_fusion.1), channel_id=1, source_target_pairs={{0,16},{8,24},{16,0},{24,8},{1,17},{9,25},{17,1},{25,9},{2,18},{10... | collective-permute-start | bytes 196616 | tf_op jit(solution)/shard_map/ppermute | solution.py:55
  126.0 9.8 %collective-permute-start.17 = (bf16[8,32,128]{2,1,0:T(8,128)(2,1)S(1)}, bf16[8,32,128]{2,1,0:T(8,128)(2,1)S(1)}, u32[]{:S(2)}, u32[]{:S(2)}) collective-permute-start(bf16[8,32,128]{2,1,0:T(8,128)(2,1)S(1)} %convolution_convert_fusion.1), channel_id=1, source_target_pairs={{0,24},{8,0},{16,8},{24,16},{1,25},{9,1},{17,9},{25,17},{2,26},{10... | collective-permute-start | bytes 196616 | tf_op jit(solution)/shard_map/ppermute | solution.py:55
  127.4 3.7 %collective-permute-start.10 = (bf16[2,16,128]{2,1,0:T(8,128)(2,1)S(1)}, bf16[2,16,128]{2,1,0:T(8,128)(2,1)S(1)}, u32[]{:S(2)}, u32[]{:S(2)}) collective-permute-start(bf16[2,16,128]{2,1,0:T(8,128)(2,1)S(1)} %get-tuple-element.23), channel_id=1, source_target_pairs={{8,0},{16,8},{24,16},{0,24},{9,1},{17,9},{25,17},{1,25},{10,2},{18... | collective-permute-start | bytes 24584 | tf_op jit(solution)/shard_map/ppermute | solution.py:20
  129.1 16.9 %collective-permute-start.18 = (f32[64,1024]{1,0:T(8,128)S(1)}, f32[64,1024]{1,0:T(8,128)S(1)}, u32[]{:S(2)}, u32[]{:S(2)}) collective-permute-start(f32[64,1024]{1,0:T(8,128)S(1)} %reshape.108), channel_id=1, source_target_pairs={{0,4},{4,0},{1,5},{5,1},{2,6},{6,2},{3,7},{7,3},{8,12},{12,8},{9,1... | collective-permute-start | bytes 786440 | tf_op jit(solution)/shard_map/ppermute | solution.py:65
  131.3 4.6 %collective-permute-start.12 = (bf16[2,1,16640]{2,1,0:T(2,128)(2,1)S(1)}, bf16[2,1,16640]{2,1,0:T(2,128)(2,1)S(1)}, u32[]{:S(2)}, u32[]{:S(2)}) collective-permute-start(bf16[2,1,16640]{2,1,0:T(2,128)(2,1)S(1)} %get-tuple-element.20), channel_id=1, source_target_pairs={{4,0},{5,1},{6,2},{7,3},{12,8},{13,9},{14,10},{15,11},{20,16},{21,... | collective-permute-start | bytes 199688 | tf_op jit(solution)/shard_map/ppermute | solution.py:20
  132.6 4.0 %collective-permute-start.11 = (bf16[2,1,16640]{2,1,0:T(2,128)(2,1)S(1)}, bf16[2,1,16640]{2,1,0:T(2,128)(2,1)S(1)}, u32[]{:S(2)}, u32[]{:S(2)}) collective-permute-start(bf16[2,1,16640]{2,1,0:T(2,128)(2,1)S(1)} %get-tuple-element.19), channel_id=1, source_target_pairs={{0,4},{1,5},{2,6},{3,7},{8,12},{9,13},{10,14},{11,15},{16,20},{17,... | collective-permute-start | bytes 199688 | tf_op jit(solution)/shard_map/ppermute | solution.py:19
  135.9 2.6 %copy-start.9 = (bf16[2,1,16640]{2,1,0:T(2,128)(2,1)}, bf16[2,1,16640]{2,1,0:T(2,128)(2,1)S(1)}, u32[]{:S(2)}) copy-start(bf16[2,1,16640]{2,1,0:T(2,128)(2,1)S(1)} %collective-permute-done.12) | copy-start | bytes 199684
  136.6 1.9 copy-start.10
  138.5 33.4 %collective-permute-start.14 = (bf16[1,18,16640]{2,1,0:T(8,128)(2,1)}, bf16[1,18,16640]{2,1,0:T(8,128)(2,1)}, u32[]{:S(2)}, u32[]{:S(2)}) collective-permute-start(bf16[1,18,16640]{2,1,0:T(8,128)(2,1)} %get-tuple-element.16), channel_id=1, source_target_pairs={{1,0},{2,1},{3,2},{5,4},{6,5},{7,6},{9,8},{10,9},{11,10},{13,12},{... | collective-permute-start | bytes 1797128 | tf_op jit(solution)/shard_map/ppermute | solution.py:20
  139.8 32.1 %collective-permute-start.13 = (bf16[1,18,16640]{2,1,0:T(8,128)(2,1)}, bf16[1,18,16640]{2,1,0:T(8,128)(2,1)}, u32[]{:S(2)}, u32[]{:S(2)}) collective-permute-start(bf16[1,18,16640]{2,1,0:T(8,128)(2,1)} %get-tuple-element.15), channel_id=1, source_target_pairs={{0,1},{1,2},{2,3},{4,5},{5,6},{6,7},{8,9},{9,10},{10,11},{12,13},{... | collective-permute-start | bytes 1797128 | tf_op jit(solution)/shard_map/ppermute | solution.py:19
  146.0 1.3 copy-start.8
  146.0 21.5 %collective-permute-start.19 = (f32[64,1024]{1,0:T(8,128)S(1)}, f32[64,1024]{1,0:T(8,128)}, u32[]{:S(2)}, u32[]{:S(2)}) collective-permute-start(f32[64,1024]{1,0:T(8,128)S(1)} %add.134), channel_id=1, source_target_pairs={{0,1},{1,0},{2,3},{3,2},{4,5},{5,4},{6,7},{7,6},{8,9},{9,8},{10,11... | collective-permute-start | bytes 786440 | tf_op jit(solution)/shard_map/ppermute | solution.py:65
  168.6 23.2 %collective-permute-start.20 = (f32[64,1024]{1,0:T(8,128)S(1)}, f32[64,1024]{1,0:T(8,128)}, u32[]{:S(2)}, u32[]{:S(2)}) collective-permute-start(f32[64,1024]{1,0:T(8,128)S(1)} %add.135), channel_id=1, source_target_pairs={{0,2},{1,3},{2,0},{3,1},{4,6},{5,7},{6,4},{7,5},{8,10},{9,11},{10,... | collective-permute-start | bytes 786440 | tf_op jit(solution)/shard_map/ppermute | solution.py:65
  189.1 4.7 %copy-start.1 = (bf16[64,256]{1,0:T(8,128)(2,1)S(1)}, bf16[64,256]{1,0:T(8,128)(2,1)}, u32[]{:S(2)}) copy-start(bf16[64,256]{1,0:T(8,128)(2,1)} %param.9) | copy-start | bytes 98308
Sparse Core Ops, SparseCore 0:
  21.9 25.6 reduce-scatter.2
  95.6 25.0 reduce-scatter.4

commit v9 on v8

--- a/solution.py
+++ b/solution.py
@@ -54,6 +54,17 @@
     for shift in range(1, size):
         pieces.append(lax.ppermute(block, axis, [(i, (i + shift) % size) for i in range(size)]))
     return jnp.concatenate(pieces, axis=0)
+
+
+def ring_reduce_scatter(value, axis):
+    size = lax.axis_size(axis)
+    share = value.shape[0] // size
+    me = lax.axis_index(axis)
+    total = lax.dynamic_slice_in_dim(value, me * share, share, 0)
+    for shift in range(1, size):
+        piece = lax.dynamic_slice_in_dim(value, ((me + shift) % size) * share, share, 0)
+        total = total + lax.ppermute(piece, axis, [(i, (i + shift) % size) for i in range(size)])
+    return total
 
 
 def butterfly_sum(value, axis):
@@ -144,9 +155,7 @@
 def share_terms(field3, cos_table, sin_table):
     real_part = jnp.einsum("rxc,xk->krc", field3, cos_table, preferred_element_type=jnp.float32)
     imag_part = jnp.einsum("rxc,xk->krc", field3, sin_table, preferred_element_type=jnp.float32)
-    return lax.psum_scatter(
-        jnp.concatenate([real_part, imag_part], axis=2), "gx", scatter_dimension=0, tiled=True
-    )
+    return ring_reduce_scatter(jnp.concatenate([real_part, imag_part], axis=2), "gx")
 
 
 def share_inverse(modes_share, cos_table, sin_table, channels):

time: 201 us -> 181 us (0.900)
  waiting for transfers between devices: 38.6 us -> 24.9 us
  between operations: 14.6 us -> 1.17 us
  starting transfers between devices: 41.3 us -> 49 us
    reduce_scatter x2 -> x0, waiting for transfers between devices: 14.5 us -> none  [share_terms(): lax.psum_scatter(jnp.concatenate([real_part, imag_part], axis=2), 'gx', s...]
    ppermute x0 -> x6, starting transfers between devices: none -> 7.85 us  [ring_reduce_scatter(): lax.ppermute(piece, axis, [(i, (i + shift) % size) for i in range(size)])]
    ppermute x6, waiting for transfers between devices: 2.02 us -> 5.1 us  [padded_2(): before = lax.ppermute(last, axis, up)]
    unnamed x38 -> x34, local copies, waits for them, and re-layouts: 5.36 us -> 3.53 us
  transfers between devices with their start and end apart: 23 -> 27, of which waited for: 6 -> 7; matrix products, arithmetic and copies ran while one was open for 29% -> 33% of each run, Pallas kernels for 13% -> 7%
where the time goes in v9:
time: 181 us
  starting transfers between devices  49 us (27%)
  local copies, waits for them, and re-layouts  39.2 us (22%)
  Pallas kernels  26.2 us (14%)
  waiting for transfers between devices  24.9 us (14%)
  matrix products  20.9 us (12%)
  other arithmetic  19.2 us (11%)
    pallas_call x2, Pallas kernels, depthwise(): pl.pallas_call(kernel, grid=(planes,), in_specs=in_specs, out_specs=pl.Bl...  26.2 us
    ppermute x6, starting transfers between devices, padded_2(): before = lax.ppermute(last, axis, up)  21.4 us
    ppermute x3, waiting for transfers between devices, butterfly_sum(): lax.ppermute(value, axis, [(i, i ^ step) for i in range(size)])  14.1 us
    dot_general x1, matrix products, per_device(): jnp.dot(grad_hidden, expand_weight.T, preferred_element_type=jnp.float32)  8.78 us
    convert_element_type x2, local copies, waits for them, and re-layouts, per_device(): cotangent.reshape(row_count, x_cells, channels).astype(jnp.float32) * slopes  8.11 us
    ppermute x6, starting transfers between devices, ring_reduce_scatter(): lax.ppermute(piece, axis, [(i, (i + shift) % size) for i in range(size)])  7.85 us
    concatenate x4, other arithmetic, padded_2(): value = jnp.concatenate([before, value, after], axis=dim)  7.8 us
    ppermute x6, starting transfers between devices, ring_gather(): lax.ppermute(block, axis, [(i, (i + shift) % size) for i in range(size)])  7.56 us
  transfers between devices with their start and end apart: 27, of which 7 were waited for; matrix products, arithmetic and copies ran while one was open for 33% of the time, Pallas kernels for 7%

profile of v9, /device:TPU:0, one launch (start us, length us, event | category | flops | bytes accessed | tf_op | source)
XLA Modules:
  0.0 180.6 jit_solution(13043263730147064492)
XLA Ops:
  0.7 3.0 %reshape.101 = bf16[32,256,64]{2,1,0:T(8,128)(2,1)S(1)} reshape(bf16[2,16,16384]{2,1,0:T(8,128)(2,1)} %param.7) | data formatting | bytes 2097152 | tf_op jit(solution)/shard_map/reshape | solution.py:206
  5.7 3.9 %collective-permute-start.2 = (f32[8,32,128]{2,0,1:T(8,128)}, f32[8,32,128]{2,0,1:T(8,128)}, u32[]{:S(2)}, u32[]{:S(2)}) collective-permute-start(f32[8,32,128]{2,0,1:T(8,128)} %get-tuple-element.32), channel_id=1, source_target_pairs={{0,24},{8,0},{16,8},{24,16},{1,25},{9,1},{17,9},{25,17},{2,26},{10... | collective-permute-start | bytes 393224 | tf_op jit(solution)/shard_map/ppermute | solution.py:66
  11.5 2.4 %collective-permute-start.3 = (bf16[2,16,128]{2,1,0:T(8,128)(2,1)S(1)}, bf16[2,16,128]{2,1,0:T(8,128)(2,1)S(1)}, u32[]{:S(2)}, u32[]{:S(2)}) collective-permute-start(bf16[2,16,128]{2,1,0:T(8,128)(2,1)S(1)} %get-tuple-element.29), channel_id=1, source_target_pairs={{0,8},{8,16},{16,24},{24,0},{1,9},{9,17},{17,25},{25,1},{2,10},{10... | collective-permute-start | bytes 24584 | tf_op jit(solution)/shard_map/ppermute | solution.py:19
  14.4 2.4 %collective-permute-done.3 = bf16[2,16,128]{2,1,0:T(8,128)(2,1)S(1)} collective-permute-done((bf16[2,16,128]{2,1,0:T(8,128)(2,1)S(1)}, bf16[2,16,128]{2,1,0:T(8,128)(2,1)S(1)}, u32[]{:S(2)}, u32[]{:S(2)}) %collective-permute-start.3) | collective-permute-done | bytes 8224 | tf_op jit(solution)/shard_map/ppermute | solution.py:19
  16.8 1.3 constant_dynamic-update-slice_fusion.1
  18.3 1.3 collective-permute-start.6
  19.6 3.0 %collective-permute-start.5 = (bf16[2,1,16640]{2,1,0:T(2,128)(2,1)S(1)}, bf16[2,1,16640]{2,1,0:T(2,128)(2,1)S(1)}, u32[]{:S(2)}, u32[]{:S(2)}) collective-permute-start(bf16[2,1,16640]{2,1,0:T(2,128)(2,1)S(1)} %get-tuple-element.21), channel_id=1, source_target_pairs={{0,4},{1,5},{2,6},{3,7},{8,12},{9,13},{10,14},{11,15},{16,20},{17,... | collective-permute-start | bytes 199688 | tf_op jit(solution)/shard_map/ppermute | solution.py:19
  24.3 1.3 fusion.112
  25.5 1.3 collective-permute-start.8
  26.8 5.5 %collective-permute-start.7 = (bf16[1,18,16640]{2,1,0:T(8,128)(2,1)}, bf16[1,18,16640]{2,1,0:T(8,128)(2,1)}, u32[]{:S(2)}, u32[]{:S(2)}) collective-permute-start(bf16[1,18,16640]{2,1,0:T(8,128)(2,1)} %get-tuple-element.17), channel_id=1, source_target_pairs={{0,1},{1,2},{2,3},{4,5},{5,6},{6,7},{8,9},{9,10},{10,11},{12,13},{... | collective-permute-start | bytes 1797128 | tf_op jit(solution)/shard_map/ppermute | solution.py:19
  32.3 4.3 %reshape.110 = f32[32,256,64]{2,1,0:T(8,128)} reshape(bf16[2,16,16384]{2,1,0:T(8,128)(2,1)} %param.13) | data formatting | bytes 3145728 | tf_op jit(solution)/shard_map/convert_element_type | solution.py:226
  36.6 3.8 %copy.30 = f32[32,256,64]{1,2,0:T(8,128)} copy(f32[32,256,64]{2,1,0:T(8,128)} %reshape.110) | data formatting | bytes 4194304 | tf_op jit(solution)/shard_map/convert_element_type | solution.py:226
  41.6 1.2 fusion.13
  42.8 1.2 fusion.36
  44.1 3.7 %collective-permute-done.8 = bf16[1,18,16640]{2,1,0:T(8,128)(2,1)} collective-permute-done((bf16[1,18,16640]{2,1,0:T(8,128)(2,1)}, bf16[1,18,16640]{2,1,0:T(8,128)(2,1)}, u32[]{:S(2)}, u32[]{:S(2)}) %collective-permute-start.8) | collective-permute-done | bytes 599072 | tf_op jit(solution)/shard_map/ppermute | solution.py:20
  47.8 1.2 collective-permute-done.7
  49.0 3.2 %pad_maximum_fusion.lo_ref.mid_ref.hi_ref = bf16[4,18,16640]{2,1,0:T(8,128)(2,1)} fusion(bf16[1,18,16640]{2,1,0:T(8,128)(2,1)} %collective-permute-done.8, bf16[2,1,16640]{2,1,0:T(2,128)(2,1)S(1)} %collective-permute-done.6, bf16[2,16,16640]{2,1,0:T(8,128)(2,1)S(1)} %constant_dynamic-update-slice_fusion, bf16[2,1,16640]{2,1,0:T(2,128)(2,1)S(1)} %collective-permute-done.5, ...), kind=kLoop, calls=%fused_computation.11 | loop fusion | flops 11980800 | bytes 4792320 | tf_op jit(solution)/shard_map/concatenate | solution.py:21
  52.9 13.0 %shard_map.94 = bf16[2,16,16384]{2,1,0:T(8,128)(2,1)} custom-call(bf16[4,18,16640]{2,1,0:T(8,128)(2,1)} %pad_maximum_fusion.lo_ref.mid_ref.hi_ref, bf16[4,18,16640]{2,1,0:T(8,128)(2,1)} %pad_maximum_fusion.lo_ref.mid_ref.hi_ref, bf16[4,18,16640]{2,1,0:T(8,128)(2,1)} %pad_maximum_fusion.lo_ref.mid_ref.hi_ref, f32[27,8,128]{2,1,0:T(8,128)} %broadcast_in_dim.18.w_ref), custom_call_target="tpu_custom_call" | custom-call | tf_op jit(solution)/shard_map/pallas_call | solution.py:146
  65.9 1.4 collective-permute-start.9
  67.8 2.2 %collective-permute-start.11 = (bf16[8,32,128]{2,1,0:T(8,128)(2,1)S(1)}, bf16[8,32,128]{2,1,0:T(8,128)(2,1)S(1)}, u32[]{:S(2)}, u32[]{:S(2)}) collective-permute-start(bf16[8,32,128]{2,1,0:T(8,128)(2,1)S(1)} %convolution_convert_fusion.2), channel_id=1, source_target_pairs={{0,24},{8,0},{16,8},{24,16},{1,25},{9,1},{17,9},{25,17},{2,26},{10... | collective-permute-start | bytes 196616 | tf_op jit(solution)/shard_map/ppermute | solution.py:55
  70.0 3.0 %reshape.102 = bf16[8192,64]{1,0:T(8,128)(2,1)S(1)} reshape(bf16[2,16,16384]{2,1,0:T(8,128)(2,1)} %shard_map.94) | data formatting | bytes 2097152 | tf_op jit(solution)/shard_map/reshape | solution.py:215
  73.1 1.2 fusion.119
  74.3 2.8 %fusion.5 = f32[8192,64]{0,1:T(8,128)S(1)} fusion(bf16[256,64]{0,1:T(8,128)(2,1)S(1)} %copy-done.10, f32[8192,256]{1,0:T(8,128)S(1)} %fusion.119), kind=kOutput, calls=%fused_computation.10 | convolution fusion | flops 278921216 | bytes 10518528 | tf_op jit(solution)/shard_map/dot_general | solution.py:218
  79.2 2.6 %fusion.11 = (bf16[32,256,64]{1,2,0:T(8,128)(2,1)S(1)}, bf16[32,256,64]{1,2,0:T(8,128)(2,1)}) fusion(f32[32,256,64]{1,2,0:T(8,128)S(1)} %copy-done.3, f32[256,32,64]{0,2,1:T(8,128)S(1)} %fusion.20, bf16[32,32,64]{2,1,0:T(8,128)(2,1)S(1)} %get-tuple-element.37, f32[32]{0:T(128)S(1)} %get-tuple-element.39, s32[32]{0:T(128)S(1)} %add.186, ...), kind=kOutput, calls=%fused_computation.19 | convolution fusion | flops 41041920 | bytes 8520960 | tf_op jit(solution)/shard_map/krc,xk->rxc/dot_general | solution.py:163
  85.3 1.5 collective-permute-start.12
  86.9 8.8 %convolution_convert_fusion = bf16[8192,64]{0,1:T(8,128)(2,1)} fusion(bf16[64,256]{1,0:T(8,128)(2,1)S(1)} %copy-done, bf16[8192,64]{0,1:T(8,128)(2,1)S(1)} %bitcast.55, bf16[256,64]{0,1:T(8,128)(2,1)S(1)} %copy-done.11, f32[8192,256]{1,0:T(8,128)} %copy-done.2), kind=kOutput, calls=%fused_computation.3 | convolution fusion | flops 558366720 | bytes 10551296 | tf_op jit(solution)/shard_map/dot_general | solution.py:234
  95.7 2.0 %copy.29 = bf16[32,256,64]{2,1,0:T(8,128)(2,1)S(1)} copy(bf16[32,256,64]{1,2,0:T(8,128)(2,1)} %get-tuple-element.14) | data formatting | bytes 2097152 | tf_op jit(solution)/shard_map/convert_element_type | solution.py:224
  97.7 2.5 %reshape.104 = bf16[2,16,16384]{2,1,0:T(8,128)(2,1)} reshape(bf16[32,256,64]{2,1,0:T(8,128)(2,1)S(1)} %copy.29) | data formatting | bytes 2097152 | tf_op jit(solution)/shard_map/reshape | solution.py:224
  100.2 2.0 %copy.35 = bf16[8192,64]{1,0:T(8,128)(2,1)S(1)} copy(bf16[8192,64]{0,1:T(8,128)(2,1)} %convolution_convert_fusion) | data formatting | bytes 2097152 | tf_op jit(solution)/shard_map/convert_element_type | solution.py:234
  102.2 2.5 %reshape.106 = bf16[2,16,16384]{2,1,0:T(8,128)(2,1)} reshape(bf16[8192,64]{1,0:T(8,128)(2,1)S(1)} %copy.35) | data formatting | bytes 2097152 | tf_op jit(solution)/shard_map/reshape | solution.py:237
  107.3 1.5 collective-permute-start.15
  109.7 1.2 collective-permute-start.21
  111.7 1.4 collective-permute-start.23
  113.1 1.3 collective-permute-start.16
  114.7 2.0 %collective-permute-done.16 = bf16[2,16,128]{2,1,0:T(8,128)(2,1)S(1)} collective-permute-done((bf16[2,16,128]{2,1,0:T(8,128)(2,1)S(1)}, bf16[2,16,128]{2,1,0:T(8,128)(2,1)S(1)}, u32[]{:S(2)}, u32[]{:S(2)}) %collective-permute-start.16) | collective-permute-done | bytes 8224 | tf_op jit(solution)/shard_map/ppermute | solution.py:20
  117.0 1.3 collective-permute-start.18
  118.3 3.0 %collective-permute-start.17 = (bf16[2,1,16640]{2,1,0:T(2,128)(2,1)S(1)}, bf16[2,1,16640]{2,1,0:T(2,128)(2,1)S(1)}, u32[]{:S(2)}, u32[]{:S(2)}) collective-permute-start(bf16[2,1,16640]{2,1,0:T(2,128)(2,1)S(1)} %get-tuple-element.19), channel_id=1, source_target_pairs={{0,4},{1,5},{2,6},{3,7},{8,12},{9,13},{10,14},{11,15},{16,20},{17,... | collective-permute-start | bytes 199688 | tf_op jit(solution)/shard_map/ppermute | solution.py:19
  122.9 1.3 fusion.111
  124.2 1.3 collective-permute-start.20
  125.5 6.0 %collective-permute-start.19 = (bf16[1,18,16640]{2,1,0:T(8,128)(2,1)}, bf16[1,18,16640]{2,1,0:T(8,128)(2,1)}, u32[]{:S(2)}, u32[]{:S(2)}) collective-permute-start(bf16[1,18,16640]{2,1,0:T(8,128)(2,1)} %get-tuple-element.15), channel_id=1, source_target_pairs={{0,1},{1,2},{2,3},{4,5},{5,6},{6,7},{8,9},{9,10},{10,11},{12,13},{... | collective-permute-start | bytes 1797128 | tf_op jit(solution)/shard_map/ppermute | solution.py:19
  132.1 1.4 collective-permute-start.25
  134.2 2.7 %copy.38 = f32[32,256,64]{2,1,0:T(8,128)} copy(f32[32,256,64]{1,2,0:T(8,128)S(1)} %add_bitcast_fusion) | data formatting | bytes 4194304 | tf_op jit(solution)/shard_map/add | solution.py:166
  136.9 2.9 %reshape.107 = f32[2,16,16384]{2,1,0:T(8,128)S(1)} reshape(f32[32,256,64]{2,1,0:T(8,128)} %copy.38) | data formatting | bytes 4194304 | tf_op jit(solution)/shard_map/reshape | solution.py:249
  139.8 14.1 %collective-permute-done.25 = f32[64,1024]{1,0:T(8,128)} collective-permute-done((f32[64,1024]{1,0:T(8,128)S(1)}, f32[64,1024]{1,0:T(8,128)}, u32[]{:S(2)}, u32[]{:S(2)}) %collective-permute-start.25) | collective-permute-done | bytes 262176 | tf_op jit(solution)/shard_map/ppermute | solution.py:76
  155.0 3.8 %collective-permute-start.26 = (f32[64,1024]{1,0:T(8,128)S(1)}, f32[64,1024]{1,0:T(8,128)}, u32[]{:S(2)}, u32[]{:S(2)}) collective-permute-start(f32[64,1024]{1,0:T(8,128)S(1)} %add.203), channel_id=1, source_target_pairs={{0,2},{1,3},{2,0},{3,1},{4,6},{5,7},{6,4},{7,5},{8,10},{9,11},{10,... | collective-permute-start | bytes 786440 | tf_op jit(solution)/shard_map/ppermute | solution.py:76
  158.8 3.3 %pad_maximum_fusion.1.lo_ref.mid_ref.hi_ref = bf16[4,18,16640]{2,1,0:T(8,128)(2,1)} fusion(bf16[1,18,16640]{2,1,0:T(8,128)(2,1)} %collective-permute-done.20, bf16[2,1,16640]{2,1,0:T(2,128)(2,1)} %copy-done.7, bf16[2,16,16640]{2,1,0:T(8,128)(2,1)S(1)} %constant_dynamic-update-slice_fusion.7, bf16[2,1,16640]{2,1,0:T(2,128)(2,1)} %copy-done.8, ...), kind=kLoop, calls=%fused_computation.12 | loop fusion | flops 11980800 | bytes 4792320 | tf_op jit(solution)/shard_map/concatenate | solution.py:21
  162.8 13.2 %shard_map.95 = f32[2,16,16384]{2,1,0:T(8,128)} custom-call(bf16[4,18,16640]{2,1,0:T(8,128)(2,1)} %pad_maximum_fusion.1.lo_ref.mid_ref.hi_ref, bf16[4,18,16640]{2,1,0:T(8,128)(2,1)} %pad_maximum_fusion.1.lo_ref.mid_ref.hi_ref, bf16[4,18,16640]{2,1,0:T(8,128)(2,1)} %pad_maximum_fusion.1.lo_ref.mid_ref.hi_ref, f32[27,8,128]{2,1,0:T(8,128)} %broadcast_in_dim.36.w_ref), custom_call_target="tpu_custom_call" | custom-call | tf_op jit(solution)/shard_map/pallas_call | solution.py:146
  175.9 2.8 %add_convert_fusion = bf16[2,16,16384]{2,1,0:T(8,128)(2,1)} fusion(f32[2,16,16384]{2,1,0:T(8,128)} %shard_map.95, f32[2,16,16384]{2,1,0:T(8,128)S(1)} %reshape.107), kind=kLoop, calls=%fused_computation.21 | loop fusion | flops 1048576 | bytes 5242880 | tf_op jit(solution)/shard_map/convert_element_type | solution.py:249
  (109 shorter events, 25.5 us)
Async XLA Ops:
  0.6 72.4 %copy-start = (bf16[64,256]{1,0:T(8,128)(2,1)S(1)}, bf16[64,256]{1,0:T(8,128)(2,1)}, u32[]{:S(2)}) copy-start(bf16[64,256]{1,0:T(8,128)(2,1)} %param.9) | copy-start | bytes 98308
  5.7 37.0 %collective-permute-start.2 = (f32[8,32,128]{2,0,1:T(8,128)}, f32[8,32,128]{2,0,1:T(8,128)}, u32[]{:S(2)}, u32[]{:S(2)}) collective-permute-start(f32[8,32,128]{2,0,1:T(8,128)} %get-tuple-element.32), channel_id=1, source_target_pairs={{0,24},{8,0},{16,8},{24,16},{1,25},{9,1},{17,9},{25,17},{2,26},{10... | collective-permute-start | bytes 393224 | tf_op jit(solution)/shard_map/ppermute | solution.py:66
  9.6 33.1 %collective-permute-start.1 = (f32[8,32,128]{2,0,1:T(8,128)}, f32[8,32,128]{2,0,1:T(8,128)}, u32[]{:S(2)}, u32[]{:S(2)}) collective-permute-start(f32[8,32,128]{2,0,1:T(8,128)} %get-tuple-element.31), channel_id=1, source_target_pairs={{0,16},{8,24},{16,0},{24,8},{1,17},{9,25},{17,1},{25,9},{2,18},{10... | collective-permute-start | bytes 393224 | tf_op jit(solution)/shard_map/ppermute | solution.py:66
  10.2 32.6 %collective-permute-start = (f32[8,32,128]{2,0,1:T(8,128)}, f32[8,32,128]{2,0,1:T(8,128)}, u32[]{:S(2)}, u32[]{:S(2)}) collective-permute-start(f32[8,32,128]{2,0,1:T(8,128)} %get-tuple-element.30), channel_id=1, source_target_pairs={{0,8},{8,16},{16,24},{24,0},{1,9},{9,17},{17,25},{25,1},{2,10},{10... | collective-permute-start | bytes 393224 | tf_op jit(solution)/shard_map/ppermute | solution.py:66
  11.5 5.3 %collective-permute-start.3 = (bf16[2,16,128]{2,1,0:T(8,128)(2,1)S(1)}, bf16[2,16,128]{2,1,0:T(8,128)(2,1)S(1)}, u32[]{:S(2)}, u32[]{:S(2)}) collective-permute-start(bf16[2,16,128]{2,1,0:T(8,128)(2,1)S(1)} %get-tuple-element.29), channel_id=1, source_target_pairs={{0,8},{8,16},{16,24},{24,0},{1,9},{9,17},{17,25},{25,1},{2,10},{10... | collective-permute-start | bytes 24584 | tf_op jit(solution)/shard_map/ppermute | solution.py:19
  13.8 4.2 %collective-permute-start.4 = (bf16[2,16,128]{2,1,0:T(8,128)(2,1)S(1)}, bf16[2,16,128]{2,1,0:T(8,128)(2,1)S(1)}, u32[]{:S(2)}, u32[]{:S(2)}) collective-permute-start(bf16[2,16,128]{2,1,0:T(8,128)(2,1)S(1)} %get-tuple-element.28), channel_id=1, source_target_pairs={{8,0},{16,8},{24,16},{0,24},{9,1},{17,9},{25,17},{1,25},{10,2},{18... | collective-permute-start | bytes 24584 | tf_op jit(solution)/shard_map/ppermute | solution.py:20
  18.3 4.5 %collective-permute-start.6 = (bf16[2,1,16640]{2,1,0:T(2,128)(2,1)S(1)}, bf16[2,1,16640]{2,1,0:T(2,128)(2,1)S(1)}, u32[]{:S(2)}, u32[]{:S(2)}) collective-permute-start(bf16[2,1,16640]{2,1,0:T(2,128)(2,1)S(1)} %get-tuple-element.22), channel_id=1, source_target_pairs={{4,0},{5,1},{6,2},{7,3},{12,8},{13,9},{14,10},{15,11},{20,16},{21,... | collective-permute-start | bytes 199688 | tf_op jit(solution)/shard_map/ppermute | solution.py:20
  19.6 4.0 %collective-permute-start.5 = (bf16[2,1,16640]{2,1,0:T(2,128)(2,1)S(1)}, bf16[2,1,16640]{2,1,0:T(2,128)(2,1)S(1)}, u32[]{:S(2)}, u32[]{:S(2)}) collective-permute-start(bf16[2,1,16640]{2,1,0:T(2,128)(2,1)S(1)} %get-tuple-element.21), channel_id=1, source_target_pairs={{0,4},{1,5},{2,6},{3,7},{8,12},{9,13},{10,14},{11,15},{16,20},{17,... | collective-permute-start | bytes 199688 | tf_op jit(solution)/shard_map/ppermute | solution.py:19
  25.5 22.3 %collective-permute-start.8 = (bf16[1,18,16640]{2,1,0:T(8,128)(2,1)}, bf16[1,18,16640]{2,1,0:T(8,128)(2,1)}, u32[]{:S(2)}, u32[]{:S(2)}) collective-permute-start(bf16[1,18,16640]{2,1,0:T(8,128)(2,1)} %get-tuple-element.18), channel_id=1, source_target_pairs={{1,0},{2,1},{3,2},{5,4},{6,5},{7,6},{9,8},{10,9},{11,10},{13,12},{... | collective-permute-start | bytes 1797128 | tf_op jit(solution)/shard_map/ppermute | solution.py:20
  26.8 22.2 %collective-permute-start.7 = (bf16[1,18,16640]{2,1,0:T(8,128)(2,1)}, bf16[1,18,16640]{2,1,0:T(8,128)(2,1)}, u32[]{:S(2)}, u32[]{:S(2)}) collective-permute-start(bf16[1,18,16640]{2,1,0:T(8,128)(2,1)} %get-tuple-element.17), channel_id=1, source_target_pairs={{0,1},{1,2},{2,3},{4,5},{5,6},{6,7},{8,9},{9,10},{10,11},{12,13},{... | collective-permute-start | bytes 1797128 | tf_op jit(solution)/shard_map/ppermute | solution.py:19
  36.5 3.8 %copy-start.5 = (bf16[32,64,64]{2,1,0:T(8,128)(2,1)S(1)}, bf16[32,64,64]{2,1,0:T(8,128)(2,1)}, u32[]{:S(2)}) copy-start(bf16[32,64,64]{2,1,0:T(8,128)(2,1)} %param.12) | copy-start | bytes 786436
  36.6 4.8 %copy-start.9 = (bf16[27,64]{1,0:T(8,128)(2,1)S(1)}, bf16[27,64]{1,0:T(8,128)(2,1)}, u32[]{:S(2)}) copy-start(bf16[27,64]{1,0:T(8,128)(2,1)} %param.8) | copy-start | bytes 10372
  65.9 11.7 %collective-permute-start.9 = (bf16[8,32,128]{2,1,0:T(8,128)(2,1)S(1)}, bf16[8,32,128]{2,1,0:T(8,128)(2,1)S(1)}, u32[]{:S(2)}, u32[]{:S(2)}) collective-permute-start(bf16[8,32,128]{2,1,0:T(8,128)(2,1)S(1)} %convolution_convert_fusion.2), channel_id=1, source_target_pairs={{0,8},{8,16},{16,24},{24,0},{1,9},{9,17},{17,25},{25,1},{2,10},{10... | collective-permute-start | bytes 196616 | tf_op jit(solution)/shard_map/ppermute | solution.py:55
  67.3 10.3 %collective-permute-start.10 = (bf16[8,32,128]{2,1,0:T(8,128)(2,1)S(1)}, bf16[8,32,128]{2,1,0:T(8,128)(2,1)S(1)}, u32[]{:S(2)}, u32[]{:S(2)}) collective-permute-start(bf16[8,32,128]{2,1,0:T(8,128)(2,1)S(1)} %convolution_convert_fusion.2), channel_id=1, source_target_pairs={{0,16},{8,24},{16,0},{24,8},{1,17},{9,25},{17,1},{25,9},{2,18},{10... | collective-permute-start | bytes 196616 | tf_op jit(solution)/shard_map/ppermute | solution.py:55
  67.8 9.8 %collective-permute-start.11 = (bf16[8,32,128]{2,1,0:T(8,128)(2,1)S(1)}, bf16[8,32,128]{2,1,0:T(8,128)(2,1)S(1)}, u32[]{:S(2)}, u32[]{:S(2)}) collective-permute-start(bf16[8,32,128]{2,1,0:T(8,128)(2,1)S(1)} %convolution_convert_fusion.2), channel_id=1, source_target_pairs={{0,24},{8,0},{16,8},{24,16},{1,25},{9,1},{17,9},{25,17},{2,26},{10... | collective-permute-start | bytes 196616 | tf_op jit(solution)/shard_map/ppermute | solution.py:55
  73.1 1.2 copy-start.10
  74.3 3.3 %copy-start.2 = (f32[8192,256]{1,0:T(8,128)}, f32[8192,256]{1,0:T(8,128)S(1)}, u32[]{:S(2)}) copy-start(f32[8192,256]{1,0:T(8,128)S(1)} %fusion.119) | copy-start | bytes 25165828
  77.6 1.6 copy-start.3
  83.0 3.8 %copy-start.11 = (bf16[256,64]{0,1:T(8,128)(2,1)S(1)}, bf16[256,64]{0,1:T(8,128)(2,1)}, u32[]{:S(2)}) copy-start(bf16[256,64]{0,1:T(8,128)(2,1)} %param.10) | copy-start | bytes 98308
  84.0 20.8 %collective-permute-start.14 = (f32[8,32,128]{2,0,1:T(8,128)}, f32[8,32,128]{2,0,1:T(8,128)}, u32[]{:S(2)}, u32[]{:S(2)}) collective-permute-start(f32[8,32,128]{2,0,1:T(8,128)} %get-tuple-element.27), channel_id=1, source_target_pairs={{0,24},{8,0},{16,8},{24,16},{1,25},{9,1},{17,9},{25,17},{2,26},{10... | collective-permute-start | bytes 393224 | tf_op jit(solution)/shard_map/ppermute | solution.py:66
  84.8 20.0 %collective-permute-start.13 = (f32[8,32,128]{2,0,1:T(8,128)}, f32[8,32,128]{2,0,1:T(8,128)}, u32[]{:S(2)}, u32[]{:S(2)}) collective-permute-start(f32[8,32,128]{2,0,1:T(8,128)} %get-tuple-element.26), channel_id=1, source_target_pairs={{0,16},{8,24},{16,0},{24,8},{1,17},{9,25},{17,1},{25,9},{2,18},{10... | collective-permute-start | bytes 393224 | tf_op jit(solution)/shard_map/ppermute | solution.py:66
  85.3 19.4 %collective-permute-start.12 = (f32[8,32,128]{2,0,1:T(8,128)}, f32[8,32,128]{2,0,1:T(8,128)}, u32[]{:S(2)}, u32[]{:S(2)}) collective-permute-start(f32[8,32,128]{2,0,1:T(8,128)} %get-tuple-element.25), channel_id=1, source_target_pairs={{0,8},{8,16},{16,24},{24,0},{1,9},{9,17},{17,25},{25,1},{2,10},{10... | collective-permute-start | bytes 393224 | tf_op jit(solution)/shard_map/ppermute | solution.py:66
  105.9 1.4 copy-start.4
  107.3 7.2 %collective-permute-start.15 = (bf16[2,16,128]{2,1,0:T(8,128)(2,1)S(1)}, bf16[2,16,128]{2,1,0:T(8,128)(2,1)S(1)}, u32[]{:S(2)}, u32[]{:S(2)}) collective-permute-start(bf16[2,16,128]{2,1,0:T(8,128)(2,1)S(1)} %get-tuple-element.24), channel_id=1, source_target_pairs={{0,8},{8,16},{16,24},{24,0},{1,9},{9,17},{17,25},{25,1},{2,10},{10... | collective-permute-start | bytes 24584 | tf_op jit(solution)/shard_map/ppermute | solution.py:19
  109.7 8.6 %collective-permute-start.21 = (bf16[8,32,128]{2,1,0:T(8,128)(2,1)}, bf16[8,32,128]{2,1,0:T(8,128)(2,1)S(1)}, u32[]{:S(2)}, u32[]{:S(2)}) collective-permute-start(bf16[8,32,128]{2,1,0:T(8,128)(2,1)} %convolution_convert_fusion.1), channel_id=1, source_target_pairs={{0,8},{8,16},{16,24},{24,0},{1,9},{9,17},{17,25},{25,1},{2,10},{10... | collective-permute-start | bytes 196616 | tf_op jit(solution)/shard_map/ppermute | solution.py:55
  110.9 10.5 %collective-permute-start.22 = (bf16[8,32,128]{2,1,0:T(8,128)(2,1)}, bf16[8,32,128]{2,1,0:T(8,128)(2,1)S(1)}, u32[]{:S(2)}, u32[]{:S(2)}) collective-permute-start(bf16[8,32,128]{2,1,0:T(8,128)(2,1)} %convolution_convert_fusion.1), channel_id=1, source_target_pairs={{0,16},{8,24},{16,0},{24,8},{1,17},{9,25},{17,1},{25,9},{2,18},{10... | collective-permute-start | bytes 196616 | tf_op jit(solution)/shard_map/ppermute | solution.py:55
  111.7 9.7 %collective-permute-start.23 = (bf16[8,32,128]{2,1,0:T(8,128)(2,1)}, bf16[8,32,128]{2,1,0:T(8,128)(2,1)S(1)}, u32[]{:S(2)}, u32[]{:S(2)}) collective-permute-start(bf16[8,32,128]{2,1,0:T(8,128)(2,1)} %convolution_convert_fusion.1), channel_id=1, source_target_pairs={{0,24},{8,0},{16,8},{24,16},{1,25},{9,1},{17,9},{25,17},{2,26},{10... | collective-permute-start | bytes 196616 | tf_op jit(solution)/shard_map/ppermute | solution.py:55
  113.1 3.7 %collective-permute-start.16 = (bf16[2,16,128]{2,1,0:T(8,128)(2,1)S(1)}, bf16[2,16,128]{2,1,0:T(8,128)(2,1)S(1)}, u32[]{:S(2)}, u32[]{:S(2)}) collective-permute-start(bf16[2,16,128]{2,1,0:T(8,128)(2,1)S(1)} %get-tuple-element.23), channel_id=1, source_target_pairs={{8,0},{16,8},{24,16},{0,24},{9,1},{17,9},{25,17},{1,25},{10,2},{18... | collective-permute-start | bytes 24584 | tf_op jit(solution)/shard_map/ppermute | solution.py:20
  114.6 17.5 %collective-permute-start.24 = (f32[64,1024]{1,0:T(8,128)S(1)}, f32[64,1024]{1,0:T(8,128)S(1)}, u32[]{:S(2)}, u32[]{:S(2)}) collective-permute-start(f32[64,1024]{1,0:T(8,128)S(1)} %reshape.108), channel_id=1, source_target_pairs={{0,4},{4,0},{1,5},{5,1},{2,6},{6,2},{3,7},{7,3},{8,12},{12,8},{9,1... | collective-permute-start | bytes 786440 | tf_op jit(solution)/shard_map/ppermute | solution.py:76
  117.0 4.6 %collective-permute-start.18 = (bf16[2,1,16640]{2,1,0:T(2,128)(2,1)S(1)}, bf16[2,1,16640]{2,1,0:T(2,128)(2,1)S(1)}, u32[]{:S(2)}, u32[]{:S(2)}) collective-permute-start(bf16[2,1,16640]{2,1,0:T(2,128)(2,1)S(1)} %get-tuple-element.20), channel_id=1, source_target_pairs={{4,0},{5,1},{6,2},{7,3},{12,8},{13,9},{14,10},{15,11},{20,16},{21,... | collective-permute-start | bytes 199688 | tf_op jit(solution)/shard_map/ppermute | solution.py:20
  118.3 4.0 %collective-permute-start.17 = (bf16[2,1,16640]{2,1,0:T(2,128)(2,1)S(1)}, bf16[2,1,16640]{2,1,0:T(2,128)(2,1)S(1)}, u32[]{:S(2)}, u32[]{:S(2)}) collective-permute-start(bf16[2,1,16640]{2,1,0:T(2,128)(2,1)S(1)} %get-tuple-element.19), channel_id=1, source_target_pairs={{0,4},{1,5},{2,6},{3,7},{8,12},{9,13},{10,14},{11,15},{16,20},{17,... | collective-permute-start | bytes 199688 | tf_op jit(solution)/shard_map/ppermute | solution.py:19
  121.6 2.6 %copy-start.7 = (bf16[2,1,16640]{2,1,0:T(2,128)(2,1)}, bf16[2,1,16640]{2,1,0:T(2,128)(2,1)S(1)}, u32[]{:S(2)}) copy-start(bf16[2,1,16640]{2,1,0:T(2,128)(2,1)S(1)} %collective-permute-done.18) | copy-start | bytes 199684
  122.3 1.9 %copy-start.8 = (bf16[2,1,16640]{2,1,0:T(2,128)(2,1)}, bf16[2,1,16640]{2,1,0:T(2,128)(2,1)S(1)}, u32[]{:S(2)}) copy-start(bf16[2,1,16640]{2,1,0:T(2,128)(2,1)S(1)} %collective-permute-done.17) | copy-start | bytes 199684
  124.2 34.6 %collective-permute-start.20 = (bf16[1,18,16640]{2,1,0:T(8,128)(2,1)}, bf16[1,18,16640]{2,1,0:T(8,128)(2,1)}, u32[]{:S(2)}, u32[]{:S(2)}) collective-permute-start(bf16[1,18,16640]{2,1,0:T(8,128)(2,1)} %get-tuple-element.16), channel_id=1, source_target_pairs={{1,0},{2,1},{3,2},{5,4},{6,5},{7,6},{9,8},{10,9},{11,10},{13,12},{... | collective-permute-start | bytes 1797128 | tf_op jit(solution)/shard_map/ppermute | solution.py:20
  125.5 33.3 %collective-permute-start.19 = (bf16[1,18,16640]{2,1,0:T(8,128)(2,1)}, bf16[1,18,16640]{2,1,0:T(8,128)(2,1)}, u32[]{:S(2)}, u32[]{:S(2)}) collective-permute-start(bf16[1,18,16640]{2,1,0:T(8,128)(2,1)} %get-tuple-element.15), channel_id=1, source_target_pairs={{0,1},{1,2},{2,3},{4,5},{5,6},{6,7},{8,9},{9,10},{10,11},{12,13},{... | collective-permute-start | bytes 1797128 | tf_op jit(solution)/shard_map/ppermute | solution.py:19
  132.1 2.0 %copy-start.6 = (f32[64,1024]{1,0:T(8,128)}, f32[64,1024]{1,0:T(8,128)S(1)}, u32[]{:S(2)}) copy-start(f32[64,1024]{1,0:T(8,128)S(1)} %add.202) | copy-start | bytes 786436
  132.1 21.8 %collective-permute-start.25 = (f32[64,1024]{1,0:T(8,128)S(1)}, f32[64,1024]{1,0:T(8,128)}, u32[]{:S(2)}, u32[]{:S(2)}) collective-permute-start(f32[64,1024]{1,0:T(8,128)S(1)} %add.202), channel_id=1, source_target_pairs={{0,1},{1,0},{2,3},{3,2},{4,5},{5,4},{6,7},{7,6},{8,9},{9,8},{10,11... | collective-permute-start | bytes 786440 | tf_op jit(solution)/shard_map/ppermute | solution.py:76
  155.0 23.7 %collective-permute-start.26 = (f32[64,1024]{1,0:T(8,128)S(1)}, f32[64,1024]{1,0:T(8,128)}, u32[]{:S(2)}, u32[]{:S(2)}) collective-permute-start(f32[64,1024]{1,0:T(8,128)S(1)} %add.203), channel_id=1, source_target_pairs={{0,2},{1,3},{2,0},{3,1},{4,6},{5,7},{6,4},{7,5},{8,10},{9,11},{10,... | collective-permute-start | bytes 786440 | tf_op jit(solution)/shard_map/ppermute | solution.py:76
  175.9 4.7 %copy-start.1 = (bf16[64,256]{1,0:T(8,128)(2,1)S(1)}, bf16[64,256]{1,0:T(8,128)(2,1)}, u32[]{:S(2)}) copy-start(bf16[64,256]{1,0:T(8,128)(2,1)} %param.9) | copy-start | bytes 98308

commit v10 on v9

--- a/solution.py
+++ b/solution.py
@@ -73,7 +73,10 @@
         return lax.psum(value, axis)
     step = 1
     while step < size:
-        value = value + lax.ppermute(value, axis, [(i, i ^ step) for i in range(size)])
+        value = value.astype(jnp.bfloat16)
+        value = value.astype(jnp.float32) + lax.ppermute(
+            value, axis, [(i, i ^ step) for i in range(size)]
+        ).astype(jnp.float32)
         step *= 2
     return value
 

time: 181 us -> 177 us (0.978)
  waiting for transfers between devices: 24.9 us -> 22.7 us
  transfers between devices with their start and end apart: 27 -> 27, of which waited for: 7 -> 7; matrix products, arithmetic and copies ran while one was open for 33% -> 30% of each run, Pallas kernels for 7% -> 0%
where the time goes in v10:
time: 177 us
  starting transfers between devices  49.6 us (28%)
  local copies, waits for them, and re-layouts  38.3 us (22%)
  Pallas kernels  26.2 us (15%)
  waiting for transfers between devices  22.7 us (13%)
  matrix products  20.3 us (11%)
  other arithmetic  18.3 us (10%)
    pallas_call x2, Pallas kernels, depthwise(): pl.pallas_call(kernel, grid=(planes,), in_specs=in_specs, out_specs=pl.Bl...  26.2 us
    ppermute x6, starting transfers between devices, padded_2(): before = lax.ppermute(last, axis, up)  20.9 us
    ppermute x3, waiting for transfers between devices, butterfly_sum(): lax.ppermute(value, axis, [(i, i ^ step) for i in range(size)])  12.5 us
    dot_general x1, matrix products, per_device(): jnp.dot(grad_hidden, expand_weight.T, preferred_element_type=jnp.float32)  8.78 us
    convert_element_type x2, local copies, waits for them, and re-layouts, per_device(): cotangent.reshape(row_count, x_cells, channels).astype(jnp.float32) * slopes  8.11 us
    ppermute x6, starting transfers between devices, ring_reduce_scatter(): lax.ppermute(piece, axis, [(i, (i + shift) % size) for i in range(size)])  7.85 us
    concatenate x4, other arithmetic, padded_2(): value = jnp.concatenate([before, value, after], axis=dim)  7.8 us
    ppermute x6, starting transfers between devices, ring_gather(): lax.ppermute(block, axis, [(i, (i + shift) % size) for i in range(size)])  7.56 us
  transfers between devices with their start and end apart: 27, of which 7 were waited for; matrix products, arithmetic and copies ran while one was open for 30% of the time, Pallas kernels for 0%

profile of v10, /device:TPU:0, one launch (start us, length us, event | category | flops | bytes accessed | tf_op | source)
XLA Modules:
  0.0 176.6 jit_solution(414113556053736368)
XLA Ops:
  0.7 3.0 %reshape.100 = bf16[32,256,64]{2,1,0:T(8,128)(2,1)S(1)} reshape(bf16[2,16,16384]{2,1,0:T(8,128)(2,1)} %param.7) | data formatting | bytes 2097152 | tf_op jit(solution)/shard_map/reshape | solution.py:209
  5.7 3.9 %collective-permute-start.2 = (f32[8,32,128]{2,0,1:T(8,128)}, f32[8,32,128]{2,0,1:T(8,128)}, u32[]{:S(2)}, u32[]{:S(2)}) collective-permute-start(f32[8,32,128]{2,0,1:T(8,128)} %get-tuple-element.32), channel_id=1, source_target_pairs={{0,24},{8,0},{16,8},{24,16},{1,25},{9,1},{17,9},{25,17},{2,26},{10... | collective-permute-start | bytes 393224 | tf_op jit(solution)/shard_map/ppermute | solution.py:66
  11.5 2.4 %collective-permute-start.3 = (bf16[2,16,128]{2,1,0:T(8,128)(2,1)S(1)}, bf16[2,16,128]{2,1,0:T(8,128)(2,1)S(1)}, u32[]{:S(2)}, u32[]{:S(2)}) collective-permute-start(bf16[2,16,128]{2,1,0:T(8,128)(2,1)S(1)} %get-tuple-element.29), channel_id=1, source_target_pairs={{0,8},{8,16},{16,24},{24,0},{1,9},{9,17},{17,25},{25,1},{2,10},{10... | collective-permute-start | bytes 24584 | tf_op jit(solution)/shard_map/ppermute | solution.py:19
  14.4 2.4 %collective-permute-done.3 = bf16[2,16,128]{2,1,0:T(8,128)(2,1)S(1)} collective-permute-done((bf16[2,16,128]{2,1,0:T(8,128)(2,1)S(1)}, bf16[2,16,128]{2,1,0:T(8,128)(2,1)S(1)}, u32[]{:S(2)}, u32[]{:S(2)}) %collective-permute-start.3) | collective-permute-done | bytes 8224 | tf_op jit(solution)/shard_map/ppermute | solution.py:19
  16.8 1.3 constant_dynamic-update-slice_fusion.1
  18.3 1.3 collective-permute-start.6
  19.6 3.0 %collective-permute-start.5 = (bf16[2,1,16640]{2,1,0:T(2,128)(2,1)S(1)}, bf16[2,1,16640]{2,1,0:T(2,128)(2,1)S(1)}, u32[]{:S(2)}, u32[]{:S(2)}) collective-permute-start(bf16[2,1,16640]{2,1,0:T(2,128)(2,1)S(1)} %get-tuple-element.21), channel_id=1, source_target_pairs={{0,4},{1,5},{2,6},{3,7},{8,12},{9,13},{10,14},{11,15},{16,20},{17,... | collective-permute-start | bytes 199688 | tf_op jit(solution)/shard_map/ppermute | solution.py:19
  24.3 1.3 fusion.112
  25.5 1.3 collective-permute-start.8
  26.8 5.5 %collective-permute-start.7 = (bf16[1,18,16640]{2,1,0:T(8,128)(2,1)}, bf16[1,18,16640]{2,1,0:T(8,128)(2,1)}, u32[]{:S(2)}, u32[]{:S(2)}) collective-permute-start(bf16[1,18,16640]{2,1,0:T(8,128)(2,1)} %get-tuple-element.17), channel_id=1, source_target_pairs={{0,1},{1,2},{2,3},{4,5},{5,6},{6,7},{8,9},{9,10},{10,11},{12,13},{... | collective-permute-start | bytes 1797128 | tf_op jit(solution)/shard_map/ppermute | solution.py:19
  32.3 4.3 %reshape.108 = f32[32,256,64]{2,1,0:T(8,128)} reshape(bf16[2,16,16384]{2,1,0:T(8,128)(2,1)} %param.13) | data formatting | bytes 3145728 | tf_op jit(solution)/shard_map/convert_element_type | solution.py:229
  36.6 3.8 %copy.30 = f32[32,256,64]{1,2,0:T(8,128)} copy(f32[32,256,64]{2,1,0:T(8,128)} %reshape.108) | data formatting | bytes 4194304 | tf_op jit(solution)/shard_map/convert_element_type | solution.py:229
  41.6 1.2 fusion.13
  44.1 3.7 %collective-permute-done.8 = bf16[1,18,16640]{2,1,0:T(8,128)(2,1)} collective-permute-done((bf16[1,18,16640]{2,1,0:T(8,128)(2,1)}, bf16[1,18,16640]{2,1,0:T(8,128)(2,1)}, u32[]{:S(2)}, u32[]{:S(2)}) %collective-permute-start.8) | collective-permute-done | bytes 599072 | tf_op jit(solution)/shard_map/ppermute | solution.py:20
  47.8 1.2 collective-permute-done.7
  49.0 3.2 %pad_maximum_fusion.lo_ref.mid_ref.hi_ref = bf16[4,18,16640]{2,1,0:T(8,128)(2,1)} fusion(bf16[1,18,16640]{2,1,0:T(8,128)(2,1)} %collective-permute-done.8, bf16[2,1,16640]{2,1,0:T(2,128)(2,1)S(1)} %collective-permute-done.6, bf16[2,16,16640]{2,1,0:T(8,128)(2,1)S(1)} %constant_dynamic-update-slice_fusion, bf16[2,1,16640]{2,1,0:T(2,128)(2,1)S(1)} %collective-permute-done.5, ...), kind=kLoop, calls=%fused_computation.11 | loop fusion | flops 11980800 | bytes 4792320 | tf_op jit(solution)/shard_map/concatenate | solution.py:21
  52.9 13.0 %shard_map.94 = bf16[2,16,16384]{2,1,0:T(8,128)(2,1)} custom-call(bf16[4,18,16640]{2,1,0:T(8,128)(2,1)} %pad_maximum_fusion.lo_ref.mid_ref.hi_ref, bf16[4,18,16640]{2,1,0:T(8,128)(2,1)} %pad_maximum_fusion.lo_ref.mid_ref.hi_ref, bf16[4,18,16640]{2,1,0:T(8,128)(2,1)} %pad_maximum_fusion.lo_ref.mid_ref.hi_ref, f32[27,8,128]{2,1,0:T(8,128)} %broadcast_in_dim.18.w_ref), custom_call_target="tpu_custom_call" | custom-call | tf_op jit(solution)/shard_map/pallas_call | solution.py:149
  65.9 1.4 collective-permute-start.9
  67.8 2.2 %collective-permute-start.11 = (bf16[8,32,128]{2,1,0:T(8,128)(2,1)S(1)}, bf16[8,32,128]{2,1,0:T(8,128)(2,1)S(1)}, u32[]{:S(2)}, u32[]{:S(2)}) collective-permute-start(bf16[8,32,128]{2,1,0:T(8,128)(2,1)S(1)} %convolution_convert_fusion.2), channel_id=1, source_target_pairs={{0,24},{8,0},{16,8},{24,16},{1,25},{9,1},{17,9},{25,17},{2,26},{10... | collective-permute-start | bytes 196616 | tf_op jit(solution)/shard_map/ppermute | solution.py:55
  70.0 3.0 %reshape.101 = bf16[8192,64]{1,0:T(8,128)(2,1)S(1)} reshape(bf16[2,16,16384]{2,1,0:T(8,128)(2,1)} %shard_map.94) | data formatting | bytes 2097152 | tf_op jit(solution)/shard_map/reshape | solution.py:218
  73.1 1.2 fusion.119
  74.3 2.8 %fusion.5 = f32[8192,64]{0,1:T(8,128)S(1)} fusion(bf16[256,64]{0,1:T(8,128)(2,1)S(1)} %copy-done.10, f32[8192,256]{1,0:T(8,128)S(1)} %fusion.119), kind=kOutput, calls=%fused_computation.10 | convolution fusion | flops 278921216 | bytes 10518528 | tf_op jit(solution)/shard_map/dot_general | solution.py:221
  79.2 2.6 %fusion.11 = (bf16[32,256,64]{1,2,0:T(8,128)(2,1)S(1)}, bf16[32,256,64]{1,2,0:T(8,128)(2,1)}) fusion(f32[32,256,64]{1,2,0:T(8,128)S(1)} %copy-done.3, f32[256,32,64]{0,2,1:T(8,128)S(1)} %fusion.20, bf16[32,32,64]{2,1,0:T(8,128)(2,1)S(1)} %get-tuple-element.37, f32[32]{0:T(128)S(1)} %get-tuple-element.39, s32[32]{0:T(128)S(1)} %add.186, ...), kind=kOutput, calls=%fused_computation.19 | convolution fusion | flops 41041920 | bytes 8520960 | tf_op jit(solution)/shard_map/krc,xk->rxc/dot_general | solution.py:166
  85.3 1.5 collective-permute-start.12
  86.9 8.8 %convolution_convert_fusion = bf16[8192,64]{0,1:T(8,128)(2,1)} fusion(bf16[64,256]{1,0:T(8,128)(2,1)S(1)} %copy-done, bf16[8192,64]{0,1:T(8,128)(2,1)S(1)} %bitcast.55, bf16[256,64]{0,1:T(8,128)(2,1)S(1)} %copy-done.11, f32[8192,256]{1,0:T(8,128)} %copy-done.2), kind=kOutput, calls=%fused_computation.3 | convolution fusion | flops 558366720 | bytes 10551296 | tf_op jit(solution)/shard_map/dot_general | solution.py:237
  95.7 2.0 %copy.29 = bf16[32,256,64]{2,1,0:T(8,128)(2,1)S(1)} copy(bf16[32,256,64]{1,2,0:T(8,128)(2,1)} %get-tuple-element.14) | data formatting | bytes 2097152 | tf_op jit(solution)/shard_map/convert_element_type | solution.py:227
  97.7 2.5 %reshape.103 = bf16[2,16,16384]{2,1,0:T(8,128)(2,1)} reshape(bf16[32,256,64]{2,1,0:T(8,128)(2,1)S(1)} %copy.29) | data formatting | bytes 2097152 | tf_op jit(solution)/shard_map/reshape | solution.py:227
  100.2 2.0 %copy.35 = bf16[8192,64]{1,0:T(8,128)(2,1)S(1)} copy(bf16[8192,64]{0,1:T(8,128)(2,1)} %convolution_convert_fusion) | data formatting | bytes 2097152 | tf_op jit(solution)/shard_map/convert_element_type | solution.py:237
  102.2 2.5 %reshape.105 = bf16[2,16,16384]{2,1,0:T(8,128)(2,1)} reshape(bf16[8192,64]{1,0:T(8,128)(2,1)S(1)} %copy.35) | data formatting | bytes 2097152 | tf_op jit(solution)/shard_map/reshape | solution.py:240
  104.7 1.2 fusion.28
  106.8 1.5 collective-permute-start.15
  108.3 1.2 collective-permute-start.21
  110.3 1.4 collective-permute-start.23
  111.7 1.3 collective-permute-start.16
  113.4 2.0 %collective-permute-done.16 = bf16[2,16,128]{2,1,0:T(8,128)(2,1)S(1)} collective-permute-done((bf16[2,16,128]{2,1,0:T(8,128)(2,1)S(1)}, bf16[2,16,128]{2,1,0:T(8,128)(2,1)S(1)}, u32[]{:S(2)}, u32[]{:S(2)}) %collective-permute-start.16) | collective-permute-done | bytes 8224 | tf_op jit(solution)/shard_map/ppermute | solution.py:20
  115.6 1.3 collective-permute-start.18
  116.9 3.0 %collective-permute-start.17 = (bf16[2,1,16640]{2,1,0:T(2,128)(2,1)S(1)}, bf16[2,1,16640]{2,1,0:T(2,128)(2,1)S(1)}, u32[]{:S(2)}, u32[]{:S(2)}) collective-permute-start(bf16[2,1,16640]{2,1,0:T(2,128)(2,1)S(1)} %get-tuple-element.19), channel_id=1, source_target_pairs={{0,4},{1,5},{2,6},{3,7},{8,12},{9,13},{10,14},{11,15},{16,20},{17,... | collective-permute-start | bytes 199688 | tf_op jit(solution)/shard_map/ppermute | solution.py:19
  121.6 2.6 %collective-permute-start.25 = (bf16[64,1024]{1,0:T(8,128)(2,1)S(1)}, bf16[64,1024]{1,0:T(8,128)(2,1)S(1)}, u32[]{:S(2)}, u32[]{:S(2)}) collective-permute-start(bf16[64,1024]{1,0:T(8,128)(2,1)S(1)} %add_convert_fusion.2), channel_id=1, source_target_pairs={{0,1},{1,0},{2,3},{3,2},{4,5},{5,4},{6,7},{7,6},{8,9},{9,8},{10,11... | collective-permute-start | bytes 393224 | tf_op jit(solution)/shard_map/ppermute | solution.py:77
  124.2 1.3 fusion.111
  125.5 1.3 collective-permute-start.20
  126.7 5.5 %collective-permute-start.19 = (bf16[1,18,16640]{2,1,0:T(8,128)(2,1)}, bf16[1,18,16640]{2,1,0:T(8,128)(2,1)}, u32[]{:S(2)}, u32[]{:S(2)}) collective-permute-start(bf16[1,18,16640]{2,1,0:T(8,128)(2,1)} %get-tuple-element.15), channel_id=1, source_target_pairs={{0,1},{1,2},{2,3},{4,5},{5,6},{6,7},{8,9},{9,10},{10,11},{12,13},{... | collective-permute-start | bytes 1797128 | tf_op jit(solution)/shard_map/ppermute | solution.py:19
  132.3 3.7 %collective-permute-start.26 = (bf16[64,1024]{1,0:T(8,128)(2,1)S(1)}, bf16[64,1024]{1,0:T(8,128)(2,1)}, u32[]{:S(2)}, u32[]{:S(2)}) collective-permute-start(bf16[64,1024]{1,0:T(8,128)(2,1)S(1)} %add_convert_fusion.1), channel_id=1, source_target_pairs={{0,2},{1,3},{2,0},{3,1},{4,6},{5,7},{6,4},{7,5},{8,10},{9,11},{10,... | collective-permute-start | bytes 393224 | tf_op jit(solution)/shard_map/ppermute | solution.py:77
  136.6 2.7 %copy.38 = f32[32,256,64]{2,1,0:T(8,128)} copy(f32[32,256,64]{1,2,0:T(8,128)S(1)} %add_bitcast_fusion) | data formatting | bytes 4194304 | tf_op jit(solution)/shard_map/add | solution.py:169
  139.4 2.9 %reshape.106 = f32[2,16,16384]{2,1,0:T(8,128)S(1)} reshape(f32[32,256,64]{2,1,0:T(8,128)} %copy.38) | data formatting | bytes 4194304 | tf_op jit(solution)/shard_map/reshape | solution.py:252
  142.3 12.5 %collective-permute-done.26 = bf16[64,1024]{1,0:T(8,128)(2,1)} collective-permute-done((bf16[64,1024]{1,0:T(8,128)(2,1)S(1)}, bf16[64,1024]{1,0:T(8,128)(2,1)}, u32[]{:S(2)}, u32[]{:S(2)}) %collective-permute-start.26) | collective-permute-done | bytes 131104 | tf_op jit(solution)/shard_map/ppermute | solution.py:77
  156.7 3.3 %pad_maximum_fusion.1.lo_ref.mid_ref.hi_ref = bf16[4,18,16640]{2,1,0:T(8,128)(2,1)} fusion(bf16[1,18,16640]{2,1,0:T(8,128)(2,1)} %collective-permute-done.20, bf16[2,1,16640]{2,1,0:T(2,128)(2,1)} %copy-done.6, bf16[2,16,16640]{2,1,0:T(8,128)(2,1)S(1)} %constant_dynamic-update-slice_fusion.7, bf16[2,1,16640]{2,1,0:T(2,128)(2,1)} %copy-done.7, ...), kind=kLoop, calls=%fused_computation.12 | loop fusion | flops 11980800 | bytes 4792320 | tf_op jit(solution)/shard_map/concatenate | solution.py:21
  160.7 13.2 %shard_map.95 = f32[2,16,16384]{2,1,0:T(8,128)} custom-call(bf16[4,18,16640]{2,1,0:T(8,128)(2,1)} %pad_maximum_fusion.1.lo_ref.mid_ref.hi_ref, bf16[4,18,16640]{2,1,0:T(8,128)(2,1)} %pad_maximum_fusion.1.lo_ref.mid_ref.hi_ref, bf16[4,18,16640]{2,1,0:T(8,128)(2,1)} %pad_maximum_fusion.1.lo_ref.mid_ref.hi_ref, f32[27,8,128]{2,1,0:T(8,128)} %broadcast_in_dim.36.w_ref), custom_call_target="tpu_custom_call" | custom-call | tf_op jit(solution)/shard_map/pallas_call | solution.py:149
  173.9 2.7 %add_convert_fusion = bf16[2,16,16384]{2,1,0:T(8,128)(2,1)} fusion(f32[2,16,16384]{2,1,0:T(8,128)} %shard_map.95, f32[2,16,16384]{2,1,0:T(8,128)S(1)} %reshape.106), kind=kLoop, calls=%fused_computation.21 | loop fusion | flops 1048576 | bytes 5242880 | tf_op jit(solution)/shard_map/convert_element_type | solution.py:252
  (109 shorter events, 22.4 us)
Async XLA Ops:
  0.6 72.4 %copy-start = (bf16[64,256]{1,0:T(8,128)(2,1)S(1)}, bf16[64,256]{1,0:T(8,128)(2,1)}, u32[]{:S(2)}) copy-start(bf16[64,256]{1,0:T(8,128)(2,1)} %param.9) | copy-start | bytes 98308
  5.7 37.0 %collective-permute-start.2 = (f32[8,32,128]{2,0,1:T(8,128)}, f32[8,32,128]{2,0,1:T(8,128)}, u32[]{:S(2)}, u32[]{:S(2)}) collective-permute-start(f32[8,32,128]{2,0,1:T(8,128)} %get-tuple-element.32), channel_id=1, source_target_pairs={{0,24},{8,0},{16,8},{24,16},{1,25},{9,1},{17,9},{25,17},{2,26},{10... | collective-permute-start | bytes 393224 | tf_op jit(solution)/shard_map/ppermute | solution.py:66
  9.6 33.1 %collective-permute-start.1 = (f32[8,32,128]{2,0,1:T(8,128)}, f32[8,32,128]{2,0,1:T(8,128)}, u32[]{:S(2)}, u32[]{:S(2)}) collective-permute-start(f32[8,32,128]{2,0,1:T(8,128)} %get-tuple-element.31), channel_id=1, source_target_pairs={{0,16},{8,24},{16,0},{24,8},{1,17},{9,25},{17,1},{25,9},{2,18},{10... | collective-permute-start | bytes 393224 | tf_op jit(solution)/shard_map/ppermute | solution.py:66
  10.2 32.6 %collective-permute-start = (f32[8,32,128]{2,0,1:T(8,128)}, f32[8,32,128]{2,0,1:T(8,128)}, u32[]{:S(2)}, u32[]{:S(2)}) collective-permute-start(f32[8,32,128]{2,0,1:T(8,128)} %get-tuple-element.30), channel_id=1, source_target_pairs={{0,8},{8,16},{16,24},{24,0},{1,9},{9,17},{17,25},{25,1},{2,10},{10... | collective-permute-start | bytes 393224 | tf_op jit(solution)/shard_map/ppermute | solution.py:66
  11.5 5.3 %collective-permute-start.3 = (bf16[2,16,128]{2,1,0:T(8,128)(2,1)S(1)}, bf16[2,16,128]{2,1,0:T(8,128)(2,1)S(1)}, u32[]{:S(2)}, u32[]{:S(2)}) collective-permute-start(bf16[2,16,128]{2,1,0:T(8,128)(2,1)S(1)} %get-tuple-element.29), channel_id=1, source_target_pairs={{0,8},{8,16},{16,24},{24,0},{1,9},{9,17},{17,25},{25,1},{2,10},{10... | collective-permute-start | bytes 24584 | tf_op jit(solution)/shard_map/ppermute | solution.py:19
  13.8 4.2 %collective-permute-start.4 = (bf16[2,16,128]{2,1,0:T(8,128)(2,1)S(1)}, bf16[2,16,128]{2,1,0:T(8,128)(2,1)S(1)}, u32[]{:S(2)}, u32[]{:S(2)}) collective-permute-start(bf16[2,16,128]{2,1,0:T(8,128)(2,1)S(1)} %get-tuple-element.28), channel_id=1, source_target_pairs={{8,0},{16,8},{24,16},{0,24},{9,1},{17,9},{25,17},{1,25},{10,2},{18... | collective-permute-start | bytes 24584 | tf_op jit(solution)/shard_map/ppermute | solution.py:20
  18.3 4.5 %collective-permute-start.6 = (bf16[2,1,16640]{2,1,0:T(2,128)(2,1)S(1)}, bf16[2,1,16640]{2,1,0:T(2,128)(2,1)S(1)}, u32[]{:S(2)}, u32[]{:S(2)}) collective-permute-start(bf16[2,1,16640]{2,1,0:T(2,128)(2,1)S(1)} %get-tuple-element.22), channel_id=1, source_target_pairs={{4,0},{5,1},{6,2},{7,3},{12,8},{13,9},{14,10},{15,11},{20,16},{21,... | collective-permute-start | bytes 199688 | tf_op jit(solution)/shard_map/ppermute | solution.py:20
  19.6 4.0 %collective-permute-start.5 = (bf16[2,1,16640]{2,1,0:T(2,128)(2,1)S(1)}, bf16[2,1,16640]{2,1,0:T(2,128)(2,1)S(1)}, u32[]{:S(2)}, u32[]{:S(2)}) collective-permute-start(bf16[2,1,16640]{2,1,0:T(2,128)(2,1)S(1)} %get-tuple-element.21), channel_id=1, source_target_pairs={{0,4},{1,5},{2,6},{3,7},{8,12},{9,13},{10,14},{11,15},{16,20},{17,... | collective-permute-start | bytes 199688 | tf_op jit(solution)/shard_map/ppermute | solution.py:19
  25.5 22.3 %collective-permute-start.8 = (bf16[1,18,16640]{2,1,0:T(8,128)(2,1)}, bf16[1,18,16640]{2,1,0:T(8,128)(2,1)}, u32[]{:S(2)}, u32[]{:S(2)}) collective-permute-start(bf16[1,18,16640]{2,1,0:T(8,128)(2,1)} %get-tuple-element.18), channel_id=1, source_target_pairs={{1,0},{2,1},{3,2},{5,4},{6,5},{7,6},{9,8},{10,9},{11,10},{13,12},{... | collective-permute-start | bytes 1797128 | tf_op jit(solution)/shard_map/ppermute | solution.py:20
  26.8 22.2 %collective-permute-start.7 = (bf16[1,18,16640]{2,1,0:T(8,128)(2,1)}, bf16[1,18,16640]{2,1,0:T(8,128)(2,1)}, u32[]{:S(2)}, u32[]{:S(2)}) collective-permute-start(bf16[1,18,16640]{2,1,0:T(8,128)(2,1)} %get-tuple-element.17), channel_id=1, source_target_pairs={{0,1},{1,2},{2,3},{4,5},{5,6},{6,7},{8,9},{9,10},{10,11},{12,13},{... | collective-permute-start | bytes 1797128 | tf_op jit(solution)/shard_map/ppermute | solution.py:19
  36.5 3.8 %copy-start.5 = (bf16[32,64,64]{2,1,0:T(8,128)(2,1)S(1)}, bf16[32,64,64]{2,1,0:T(8,128)(2,1)}, u32[]{:S(2)}) copy-start(bf16[32,64,64]{2,1,0:T(8,128)(2,1)} %param.12) | copy-start | bytes 786436
  36.6 4.8 %copy-start.9 = (bf16[27,64]{1,0:T(8,128)(2,1)S(1)}, bf16[27,64]{1,0:T(8,128)(2,1)}, u32[]{:S(2)}) copy-start(bf16[27,64]{1,0:T(8,128)(2,1)} %param.8) | copy-start | bytes 10372
  65.9 11.7 %collective-permute-start.9 = (bf16[8,32,128]{2,1,0:T(8,128)(2,1)S(1)}, bf16[8,32,128]{2,1,0:T(8,128)(2,1)S(1)}, u32[]{:S(2)}, u32[]{:S(2)}) collective-permute-start(bf16[8,32,128]{2,1,0:T(8,128)(2,1)S(1)} %convolution_convert_fusion.2), channel_id=1, source_target_pairs={{0,8},{8,16},{16,24},{24,0},{1,9},{9,17},{17,25},{25,1},{2,10},{10... | collective-permute-start | bytes 196616 | tf_op jit(solution)/shard_map/ppermute | solution.py:55
  67.3 10.3 %collective-permute-start.10 = (bf16[8,32,128]{2,1,0:T(8,128)(2,1)S(1)}, bf16[8,32,128]{2,1,0:T(8,128)(2,1)S(1)}, u32[]{:S(2)}, u32[]{:S(2)}) collective-permute-start(bf16[8,32,128]{2,1,0:T(8,128)(2,1)S(1)} %convolution_convert_fusion.2), channel_id=1, source_target_pairs={{0,16},{8,24},{16,0},{24,8},{1,17},{9,25},{17,1},{25,9},{2,18},{10... | collective-permute-start | bytes 196616 | tf_op jit(solution)/shard_map/ppermute | solution.py:55
  67.8 9.8 %collective-permute-start.11 = (bf16[8,32,128]{2,1,0:T(8,128)(2,1)S(1)}, bf16[8,32,128]{2,1,0:T(8,128)(2,1)S(1)}, u32[]{:S(2)}, u32[]{:S(2)}) collective-permute-start(bf16[8,32,128]{2,1,0:T(8,128)(2,1)S(1)} %convolution_convert_fusion.2), channel_id=1, source_target_pairs={{0,24},{8,0},{16,8},{24,16},{1,25},{9,1},{17,9},{25,17},{2,26},{10... | collective-permute-start | bytes 196616 | tf_op jit(solution)/shard_map/ppermute | solution.py:55
  73.1 1.2 copy-start.10
  74.3 3.3 %copy-start.2 = (f32[8192,256]{1,0:T(8,128)}, f32[8192,256]{1,0:T(8,128)S(1)}, u32[]{:S(2)}) copy-start(f32[8192,256]{1,0:T(8,128)S(1)} %fusion.119) | copy-start | bytes 25165828
  77.6 1.6 copy-start.3
  83.0 3.8 %copy-start.11 = (bf16[256,64]{0,1:T(8,128)(2,1)S(1)}, bf16[256,64]{0,1:T(8,128)(2,1)}, u32[]{:S(2)}) copy-start(bf16[256,64]{0,1:T(8,128)(2,1)} %param.10) | copy-start | bytes 98308
  84.0 20.8 %collective-permute-start.14 = (f32[8,32,128]{2,0,1:T(8,128)}, f32[8,32,128]{2,0,1:T(8,128)}, u32[]{:S(2)}, u32[]{:S(2)}) collective-permute-start(f32[8,32,128]{2,0,1:T(8,128)} %get-tuple-element.27), channel_id=1, source_target_pairs={{0,24},{8,0},{16,8},{24,16},{1,25},{9,1},{17,9},{25,17},{2,26},{10... | collective-permute-start | bytes 393224 | tf_op jit(solution)/shard_map/ppermute | solution.py:66
  84.8 20.0 %collective-permute-start.13 = (f32[8,32,128]{2,0,1:T(8,128)}, f32[8,32,128]{2,0,1:T(8,128)}, u32[]{:S(2)}, u32[]{:S(2)}) collective-permute-start(f32[8,32,128]{2,0,1:T(8,128)} %get-tuple-element.26), channel_id=1, source_target_pairs={{0,16},{8,24},{16,0},{24,8},{1,17},{9,25},{17,1},{25,9},{2,18},{10... | collective-permute-start | bytes 393224 | tf_op jit(solution)/shard_map/ppermute | solution.py:66
  85.3 19.5 %collective-permute-start.12 = (f32[8,32,128]{2,0,1:T(8,128)}, f32[8,32,128]{2,0,1:T(8,128)}, u32[]{:S(2)}, u32[]{:S(2)}) collective-permute-start(f32[8,32,128]{2,0,1:T(8,128)} %get-tuple-element.25), channel_id=1, source_target_pairs={{0,8},{8,16},{16,24},{24,0},{1,9},{9,17},{17,25},{25,1},{2,10},{10... | collective-permute-start | bytes 393224 | tf_op jit(solution)/shard_map/ppermute | solution.py:66
  104.7 2.1 %copy-start.4 = (bf16[2,16,16384]{2,1,0:T(8,128)(2,1)S(1)}, bf16[2,16,16384]{2,1,0:T(8,128)(2,1)}, u32[]{:S(2)}) copy-start(bf16[2,16,16384]{2,1,0:T(8,128)(2,1)} %reshape.105) | copy-start | bytes 3145732
  106.8 6.4 %collective-permute-start.15 = (bf16[2,16,128]{2,1,0:T(8,128)(2,1)S(1)}, bf16[2,16,128]{2,1,0:T(8,128)(2,1)S(1)}, u32[]{:S(2)}, u32[]{:S(2)}) collective-permute-start(bf16[2,16,128]{2,1,0:T(8,128)(2,1)S(1)} %get-tuple-element.24), channel_id=1, source_target_pairs={{0,8},{8,16},{16,24},{24,0},{1,9},{9,17},{17,25},{25,1},{2,10},{10... | collective-permute-start | bytes 24584 | tf_op jit(solution)/shard_map/ppermute | solution.py:19
  108.3 8.6 %collective-permute-start.21 = (bf16[8,32,128]{2,1,0:T(8,128)(2,1)S(1)}, bf16[8,32,128]{2,1,0:T(8,128)(2,1)S(1)}, u32[]{:S(2)}, u32[]{:S(2)}) collective-permute-start(bf16[8,32,128]{2,1,0:T(8,128)(2,1)S(1)} %convolution_convert_fusion.1), channel_id=1, source_target_pairs={{0,8},{8,16},{16,24},{24,0},{1,9},{9,17},{17,25},{25,1},{2,10},{10... | collective-permute-start | bytes 196616 | tf_op jit(solution)/shard_map/ppermute | solution.py:55
  109.5 10.5 %collective-permute-start.22 = (bf16[8,32,128]{2,1,0:T(8,128)(2,1)S(1)}, bf16[8,32,128]{2,1,0:T(8,128)(2,1)S(1)}, u32[]{:S(2)}, u32[]{:S(2)}) collective-permute-start(bf16[8,32,128]{2,1,0:T(8,128)(2,1)S(1)} %convolution_convert_fusion.1), channel_id=1, source_target_pairs={{0,16},{8,24},{16,0},{24,8},{1,17},{9,25},{17,1},{25,9},{2,18},{10... | collective-permute-start | bytes 196616 | tf_op jit(solution)/shard_map/ppermute | solution.py:55
  110.3 9.7 %collective-permute-start.23 = (bf16[8,32,128]{2,1,0:T(8,128)(2,1)S(1)}, bf16[8,32,128]{2,1,0:T(8,128)(2,1)S(1)}, u32[]{:S(2)}, u32[]{:S(2)}) collective-permute-start(bf16[8,32,128]{2,1,0:T(8,128)(2,1)S(1)} %convolution_convert_fusion.1), channel_id=1, source_target_pairs={{0,24},{8,0},{16,8},{24,16},{1,25},{9,1},{17,9},{25,17},{2,26},{10... | collective-permute-start | bytes 196616 | tf_op jit(solution)/shard_map/ppermute | solution.py:55
  111.7 3.7 %collective-permute-start.16 = (bf16[2,16,128]{2,1,0:T(8,128)(2,1)S(1)}, bf16[2,16,128]{2,1,0:T(8,128)(2,1)S(1)}, u32[]{:S(2)}, u32[]{:S(2)}) collective-permute-start(bf16[2,16,128]{2,1,0:T(8,128)(2,1)S(1)} %get-tuple-element.23), channel_id=1, source_target_pairs={{8,0},{16,8},{24,16},{0,24},{9,1},{17,9},{25,17},{1,25},{10,2},{18... | collective-permute-start | bytes 24584 | tf_op jit(solution)/shard_map/ppermute | solution.py:20
  113.2 8.3 %collective-permute-start.24 = (bf16[64,1024]{1,0:T(8,128)(2,1)S(1)}, bf16[64,1024]{1,0:T(8,128)(2,1)S(1)}, u32[]{:S(2)}, u32[]{:S(2)}) collective-permute-start(bf16[64,1024]{1,0:T(8,128)(2,1)S(1)} %convert_element_type.143), channel_id=1, source_target_pairs={{0,4},{4,0},{1,5},{5,1},{2,6},{6,2},{3,7},{7,3},{8,12},{12,8},{9,1... | collective-permute-start | bytes 393224 | tf_op jit(solution)/shard_map/ppermute | solution.py:77
  115.6 5.2 %collective-permute-start.18 = (bf16[2,1,16640]{2,1,0:T(2,128)(2,1)S(1)}, bf16[2,1,16640]{2,1,0:T(2,128)(2,1)S(1)}, u32[]{:S(2)}, u32[]{:S(2)}) collective-permute-start(bf16[2,1,16640]{2,1,0:T(2,128)(2,1)S(1)} %get-tuple-element.20), channel_id=1, source_target_pairs={{4,0},{5,1},{6,2},{7,3},{12,8},{13,9},{14,10},{15,11},{20,16},{21,... | collective-permute-start | bytes 199688 | tf_op jit(solution)/shard_map/ppermute | solution.py:20
  116.9 4.0 %collective-permute-start.17 = (bf16[2,1,16640]{2,1,0:T(2,128)(2,1)S(1)}, bf16[2,1,16640]{2,1,0:T(2,128)(2,1)S(1)}, u32[]{:S(2)}, u32[]{:S(2)}) collective-permute-start(bf16[2,1,16640]{2,1,0:T(2,128)(2,1)S(1)} %get-tuple-element.19), channel_id=1, source_target_pairs={{0,4},{1,5},{2,6},{3,7},{8,12},{9,13},{10,14},{11,15},{16,20},{17,... | collective-permute-start | bytes 199688 | tf_op jit(solution)/shard_map/ppermute | solution.py:19
  120.8 4.6 %copy-start.6 = (bf16[2,1,16640]{2,1,0:T(2,128)(2,1)}, bf16[2,1,16640]{2,1,0:T(2,128)(2,1)S(1)}, u32[]{:S(2)}) copy-start(bf16[2,1,16640]{2,1,0:T(2,128)(2,1)S(1)} %collective-permute-done.18) | copy-start | bytes 199684
  120.9 4.5 %copy-start.7 = (bf16[2,1,16640]{2,1,0:T(2,128)(2,1)}, bf16[2,1,16640]{2,1,0:T(2,128)(2,1)S(1)}, u32[]{:S(2)}) copy-start(bf16[2,1,16640]{2,1,0:T(2,128)(2,1)S(1)} %collective-permute-done.17) | copy-start | bytes 199684
  121.6 10.6 %collective-permute-start.25 = (bf16[64,1024]{1,0:T(8,128)(2,1)S(1)}, bf16[64,1024]{1,0:T(8,128)(2,1)S(1)}, u32[]{:S(2)}, u32[]{:S(2)}) collective-permute-start(bf16[64,1024]{1,0:T(8,128)(2,1)S(1)} %add_convert_fusion.2), channel_id=1, source_target_pairs={{0,1},{1,0},{2,3},{3,2},{4,5},{5,4},{6,7},{7,6},{8,9},{9,8},{10,11... | collective-permute-start | bytes 393224 | tf_op jit(solution)/shard_map/ppermute | solution.py:77
  125.5 31.3 %collective-permute-start.20 = (bf16[1,18,16640]{2,1,0:T(8,128)(2,1)}, bf16[1,18,16640]{2,1,0:T(8,128)(2,1)}, u32[]{:S(2)}, u32[]{:S(2)}) collective-permute-start(bf16[1,18,16640]{2,1,0:T(8,128)(2,1)} %get-tuple-element.16), channel_id=1, source_target_pairs={{1,0},{2,1},{3,2},{5,4},{6,5},{7,6},{9,8},{10,9},{11,10},{13,12},{... | collective-permute-start | bytes 1797128 | tf_op jit(solution)/shard_map/ppermute | solution.py:20
  126.7 30.0 %collective-permute-start.19 = (bf16[1,18,16640]{2,1,0:T(8,128)(2,1)}, bf16[1,18,16640]{2,1,0:T(8,128)(2,1)}, u32[]{:S(2)}, u32[]{:S(2)}) collective-permute-start(bf16[1,18,16640]{2,1,0:T(8,128)(2,1)} %get-tuple-element.15), channel_id=1, source_target_pairs={{0,1},{1,2},{2,3},{4,5},{5,6},{6,7},{8,9},{9,10},{10,11},{12,13},{... | collective-permute-start | bytes 1797128 | tf_op jit(solution)/shard_map/ppermute | solution.py:19
  132.2 4.4 %copy-start.8 = (bf16[64,1024]{1,0:T(8,128)(2,1)}, bf16[64,1024]{1,0:T(8,128)(2,1)S(1)}, u32[]{:S(2)}) copy-start(bf16[64,1024]{1,0:T(8,128)(2,1)S(1)} %add_convert_fusion.1) | copy-start | bytes 393220
  132.3 22.5 %collective-permute-start.26 = (bf16[64,1024]{1,0:T(8,128)(2,1)S(1)}, bf16[64,1024]{1,0:T(8,128)(2,1)}, u32[]{:S(2)}, u32[]{:S(2)}) collective-permute-start(bf16[64,1024]{1,0:T(8,128)(2,1)S(1)} %add_convert_fusion.1), channel_id=1, source_target_pairs={{0,2},{1,3},{2,0},{3,1},{4,6},{5,7},{6,4},{7,5},{8,10},{9,11},{10,... | collective-permute-start | bytes 393224 | tf_op jit(solution)/shard_map/ppermute | solution.py:77
  160.7 15.9 %copy-start.1 = (bf16[64,256]{1,0:T(8,128)(2,1)S(1)}, bf16[64,256]{1,0:T(8,128)(2,1)}, u32[]{:S(2)}) copy-start(bf16[64,256]{1,0:T(8,128)(2,1)} %param.9) | copy-start | bytes 98308

commit v11 on v7

--- a/solution.py
+++ b/solution.py
@@ -56,13 +56,27 @@
     return jnp.concatenate(pieces, axis=0)
 
 
+def ring_reduce_scatter(value, axis):
+    size = lax.axis_size(axis)
+    share = value.shape[0] // size
+    me = lax.axis_index(axis)
+    total = lax.dynamic_slice_in_dim(value, me * share, share, 0)
+    for shift in range(1, size):
+        piece = lax.dynamic_slice_in_dim(value, ((me + shift) % size) * share, share, 0)
+        total = total + lax.ppermute(piece, axis, [(i, (i + shift) % size) for i in range(size)])
+    return total
+
+
 def butterfly_sum(value, axis):
     size = lax.axis_size(axis)
     if size & (size - 1):
         return lax.psum(value, axis)
     step = 1
     while step < size:
-        value = value + lax.ppermute(value, axis, [(i, i ^ step) for i in range(size)])
+        value = value.astype(jnp.bfloat16)
+        value = value.astype(jnp.float32) + lax.ppermute(
+            value, axis, [(i, i ^ step) for i in range(size)]
+        ).astype(jnp.float32)
         step *= 2
     return value
 
@@ -75,10 +89,19 @@
 
 def spatial_rims(field_block, channels):
     x_wide = padded_2(field_block, (("gx", 2),), 2 * channels, True)
-    return padded_2(x_wide, (("gy", 1), ("gz", 0)), 1, False)
-
-
-def stencil_kernel(chunk, x_pad, planes, y_cells, rows, p_ref, w_ref, o_ref):
+    inner = padded_2(x_wide, (("gy", 1),), 1, False)
+    size = lax.axis_size("gz")
+    up = [(i, i + 1) for i in range(size - 1)]
+    down = [(j, i) for i, j in up]
+    below = lax.ppermute(inner[-1:], "gz", up)
+    above = lax.ppermute(inner[:1], "gz", down)
+    return (inner, below, above)
+
+
+def stencil_kernel(chunk, x_pad, y_cells, rows, plan, sources, has_acc, *refs):
+    src_refs = refs[:sources]
+    acc_ref = refs[sources] if has_acc else None
+    w_ref, o_ref = refs[sources + has_acc :]
     width = chunk + 2 * x_pad
     count = o_ref.shape[2] // chunk
     shift = chunk + x_pad - x_pad // 2
@@ -86,14 +109,16 @@
 
     def body(index, carry):
         base = pl.multiple_of(index * chunk, chunk)
-        for plane in range(planes):
+        for plane, terms in enumerate(plan):
             for row in range(0, y_cells, rows):
                 left = jnp.zeros((rows, chunk + x_pad), jnp.float32)
                 centre = jnp.zeros((rows, chunk), jnp.float32)
                 right = jnp.zeros((rows, chunk + x_pad), jnp.float32)
-                for step_z in range(3):
+                for source, source_plane, step_z in terms:
                     for step_y in range(3):
-                        window = p_ref[plane + step_z, pl.ds(row + step_y, rows), pl.ds(base, width)]
+                        window = src_refs[source][
+                            source_plane, pl.ds(row + step_y, rows), pl.ds(base, width)
+                        ].astype(jnp.float32)
                         tap = 9 * step_z + 3 * step_y
                         gain_l = jnp.concatenate([w_ref[tap]] * side, axis=1)
                         gain_c = jnp.concatenate([w_ref[tap + 1]] * (side - 1), axis=1)
@@ -106,36 +131,53 @@
                     + pltpu.roll(left, shift, 1)[:, :chunk]
                     + pltpu.roll(right, shift, 1)[:, :chunk]
                 )
+                if has_acc:
+                    total = total + acc_ref[plane, pl.ds(row, rows), pl.ds(base, chunk)]
                 o_ref[plane, pl.ds(row, rows), pl.ds(base, chunk)] = total.astype(o_ref.dtype)
         return carry
 
     lax.fori_loop(0, count, body, 0)
 
 
-def depthwise(padded, taps, flipped, x_cells, channels, out_dtype=jnp.float32):
-    planes = padded.shape[0] - 2
-    y_cells = padded.shape[1] - 2
-    x_pad = 2 * channels
+def stencil_call(plan, inputs, acc, gains, y_cells, lanes, channels, out_dtype):
+    chunk = min(1024, lanes)
+    rows = 8 if y_cells % 8 == 0 else y_cells
+    kernel = functools.partial(
+        stencil_kernel, chunk, 2 * channels, y_cells, rows, plan, len(inputs), acc is not None
+    )
+    operands = list(inputs) + ([acc] if acc is not None else []) + [gains]
+    return pl.pallas_call(
+        kernel,
+        out_shape=jax.ShapeDtypeStruct((len(plan), y_cells, lanes), out_dtype),
+    )(*operands)
+
+
+def depthwise(rims, taps, flipped, x_cells, channels, out_dtype=jnp.float32):
+    inner, below, above = rims
+    planes = inner.shape[0]
+    y_cells = inner.shape[1] - 2
     lanes = x_cells * channels
-    chunk = min(1024, lanes)
     rows = 8 if y_cells % 8 == 0 else y_cells
     if flipped:
         taps = taps[::-1]
     gains = jnp.tile(taps.astype(jnp.float32), (1, 128 // channels))
     gains = jnp.broadcast_to(gains[:, None, :], (gains.shape[0], rows, 128))
-    kernel = functools.partial(stencil_kernel, chunk, x_pad, planes, y_cells, rows)
-    return pl.pallas_call(
-        kernel,
-        out_shape=jax.ShapeDtypeStruct((planes, y_cells, lanes), out_dtype),
-    )(padded.astype(jnp.float32), gains)
+    local_plan = tuple(
+        tuple((0, plane + step_z - 1, step_z) for step_z in range(3) if 0 <= plane + step_z - 1 < planes)
+        for plane in range(planes)
+    )
+    local = stencil_call(local_plan, (inner,), None, gains, y_cells, lanes, channels, jnp.float32)
+    rim_plan = tuple(
+        ((((0, 0, 0),) if plane == 0 else ()) + (((1, 0, 2),) if plane == planes - 1 else ()))
+        for plane in range(planes)
+    )
+    return stencil_call(rim_plan, (below, above), local, gains, y_cells, lanes, channels, out_dtype)
 
 
 def share_terms(field3, cos_table, sin_table):
     real_part = jnp.einsum("rxc,xk->krc", field3, cos_table, preferred_element_type=jnp.float32)
     imag_part = jnp.einsum("rxc,xk->krc", field3, sin_table, preferred_element_type=jnp.float32)
-    return lax.psum_scatter(
-        jnp.concatenate([real_part, imag_part], axis=2), "gx", scatter_dimension=0, tiled=True
-    )
+    return ring_reduce_scatter(jnp.concatenate([real_part, imag_part], axis=2), "gx")
 
 
 def share_inverse(modes_share, cos_table, sin_table, channels):

time: 204 us -> 166 us (0.81)
  waiting for transfers between devices: 38.6 us -> 10.9 us
  between operations: 14.6 us -> 1.2 us
  other arithmetic: 21.2 us -> 12.2 us
  Pallas kernels: 26.9 us -> 33 us
  starting transfers between devices: 41.3 us -> 46.3 us
    ppermute x0 -> x10, starting transfers between devices: none -> 17.9 us  [the longest x6 8.46 us: ring_reduce_scatter(): lax.ppermute(piece, axis, [(i, (i + shift) % size) for i in range(size)])]
    reduce_scatter x2 -> x0, waiting for transfers between devices: 14.6 us -> none  [share_terms(): lax.psum_scatter(jnp.concatenate([real_part, imag_part], axis=2), 'gx', s...]
    ppermute x6 -> x4, starting transfers between devices: 21.5 us -> 9.43 us  [padded_2(): before = lax.ppermute(last, axis, up)]
    ppermute x3, waiting for transfers between devices: 14.6 us -> 4 us  [butterfly_sum(): lax.ppermute(value, axis, [(i, i ^ step) for i in range(size)])]
    convert_element_type x2, other arithmetic: 8.46 us -> 0.07 us  [butterfly_sum(): value = value.astype(jnp.bfloat16)]
    pallas_call x2 -> x4, Pallas kernels: 26.9 us -> 33 us  [stencil_call(): pl.pallas_call(kernel, out_shape=jax.ShapeDtypeStruct((len(plan), y_cells...]
    ppermute x6 -> x4, starting transfers between devices: 7.55 us -> 3.46 us  [padded_2(): after = lax.ppermute(leading, axis, down)]
    ppermute x6 -> x4, waiting for transfers between devices: 7.46 us -> 3.57 us  [padded_2(): after = lax.ppermute(leading, axis, down)]
  transfers between devices with their start and end apart: 23 -> 27, of which waited for: 6 -> 6; matrix products, arithmetic and copies ran while one was open for 30% -> 34% of each run, Pallas kernels for 13% -> 12%
where the time goes in v11:
time: 166 us; the launch traced here: 165 us
  starting transfers between devices  46.3 us (28%)
  local copies, waits for them, and re-layouts  40.2 us (24%)
  Pallas kernels  33 us (20%)
  matrix products  21.7 us (13%)
  other arithmetic  12.2 us (7%)
  waiting for transfers between devices  10.9 us (7%)
    pallas_call x4, Pallas kernels, stencil_call(): pl.pallas_call(kernel, out_shape=jax.ShapeDtypeStruct((len(plan), y_cells...  33 us
    ppermute x4, starting transfers between devices, padded_2(): before = lax.ppermute(last, axis, up)  9.43 us
    dot_general x1, matrix products, per_device(): jnp.dot(grad_hidden, expand_weight.T, preferred_element_type=jnp.float32)  8.78 us
    ppermute x6, starting transfers between devices, ring_reduce_scatter(): lax.ppermute(piece, axis, [(i, (i + shift) % size) for i in range(size)])  8.46 us
    convert_element_type x2, local copies, waits for them, and re-layouts, per_device(): cotangent.reshape(row_count, x_cells, channels).astype(jnp.float32) * slopes  8.07 us
    ppermute x6, starting transfers between devices, ring_gather(): lax.ppermute(block, axis, [(i, (i + shift) % size) for i in range(size)])  7.81 us
    ppermute x3, starting transfers between devices, butterfly_sum(): lax.ppermute(value, axis, [(i, i ^ step) for i in range(size)])  7.71 us
    ppermute x2, starting transfers between devices, spatial_rims(): below = lax.ppermute(inner[-1:], 'gz', up)  6.65 us
  transfers between devices with their start and end apart: 27, of which 6 were waited for; matrix products, arithmetic and copies ran while one was open for 34% of the time, Pallas kernels for 12%

profile of v11, /device:TPU:0, one launch (start us, length us, event | category | flops | bytes accessed | tf_op | source)
XLA Modules:
  0.0 165.5 jit_solution(13144648133599445154)
XLA Ops:
  0.7 3.0 %reshape.100 = bf16[32,256,64]{2,1,0:T(8,128)(2,1)S(1)} reshape(bf16[2,16,16384]{2,1,0:T(8,128)(2,1)} %param.7) | data formatting | bytes 2097152 | tf_op jit(solution)/shard_map/reshape | solution.py:228
  5.8 3.9 %collective-permute-start.2 = (f32[8,32,128]{2,0,1:T(8,128)}, f32[8,32,128]{2,0,1:T(8,128)}, u32[]{:S(2)}, u32[]{:S(2)}) collective-permute-start(f32[8,32,128]{2,0,1:T(8,128)} %get-tuple-element.32), channel_id=1, source_target_pairs={{0,24},{8,0},{16,8},{24,16},{1,25},{9,1},{17,9},{25,17},{2,26},{10... | collective-permute-start | bytes 393224 | tf_op jit(solution)/shard_map/ppermute | solution.py:66
  11.5 2.4 %collective-permute-start.3 = (bf16[2,16,128]{2,1,0:T(8,128)(2,1)S(1)}, bf16[2,16,128]{2,1,0:T(8,128)(2,1)S(1)}, u32[]{:S(2)}, u32[]{:S(2)}) collective-permute-start(bf16[2,16,128]{2,1,0:T(8,128)(2,1)S(1)} %get-tuple-element.29), channel_id=1, source_target_pairs={{0,8},{8,16},{16,24},{24,0},{1,9},{9,17},{17,25},{25,1},{2,10},{10... | collective-permute-start | bytes 24584 | tf_op jit(solution)/shard_map/ppermute | solution.py:19
  14.4 2.4 %collective-permute-done.3 = bf16[2,16,128]{2,1,0:T(8,128)(2,1)S(1)} collective-permute-done((bf16[2,16,128]{2,1,0:T(8,128)(2,1)S(1)}, bf16[2,16,128]{2,1,0:T(8,128)(2,1)S(1)}, u32[]{:S(2)}, u32[]{:S(2)}) %collective-permute-start.3) | collective-permute-done | bytes 8224 | tf_op jit(solution)/shard_map/ppermute | solution.py:19
  18.8 1.3 collective-permute-start.6
  20.1 3.0 %collective-permute-start.5 = (bf16[2,1,16640]{2,1,0:T(2,128)(2,1)S(1)}, bf16[2,1,16640]{2,1,0:T(2,128)(2,1)S(1)}, u32[]{:S(2)}, u32[]{:S(2)}) collective-permute-start(bf16[2,1,16640]{2,1,0:T(2,128)(2,1)S(1)} %get-tuple-element.21), channel_id=1, source_target_pairs={{0,4},{1,5},{2,6},{3,7},{8,12},{9,13},{10,14},{11,15},{16,20},{17,... | collective-permute-start | bytes 199688 | tf_op jit(solution)/shard_map/ppermute | solution.py:19
  24.1 1.8 %pad_maximum_fusion.refs_0_ = bf16[2,18,16640]{2,1,0:T(8,128)(2,1)S(1)} fusion(bf16[2,1,16640]{2,1,0:T(2,128)(2,1)S(1)} %collective-permute-done.6, bf16[2,16,16640]{2,1,0:T(8,128)(2,1)} %copy-done.8, bf16[2,1,16640]{2,1,0:T(2,128)(2,1)S(1)} %collective-permute-done.5), kind=kLoop, calls=%fused_computation.23 | loop fusion | flops 3594240 | bytes 2396160 | tf_op jit(solution)/shard_map/concatenate | solution.py:21
  25.9 1.4 fusion.112
  27.3 4.4 %collective-permute-start.7 = (bf16[1,18,16640]{2,1,0:T(8,128)(2,1)}, bf16[1,18,16640]{2,1,0:T(8,128)(2,1)}, u32[]{:S(2)}, u32[]{:S(2)}) collective-permute-start(bf16[1,18,16640]{2,1,0:T(8,128)(2,1)} %get-tuple-element.18), channel_id=1, source_target_pairs={{0,1},{1,2},{2,3},{4,5},{5,6},{6,7},{8,9},{9,10},{10,11},{12,13},{... | collective-permute-start | bytes 1797128 | tf_op jit(solution)/shard_map/ppermute | solution.py:96
  31.7 1.3 collective-permute-start.8
  33.0 4.3 %reshape.108 = f32[32,256,64]{2,1,0:T(8,128)} reshape(bf16[2,16,16384]{2,1,0:T(8,128)(2,1)} %param.13) | data formatting | bytes 3145728 | tf_op jit(solution)/shard_map/convert_element_type | solution.py:248
  37.3 3.8 %copy.30 = f32[32,256,64]{1,2,0:T(8,128)} copy(f32[32,256,64]{2,1,0:T(8,128)} %reshape.108) | data formatting | bytes 4194304 | tf_op jit(solution)/shard_map/convert_element_type | solution.py:248
  41.1 1.2 neg.10
  42.6 1.2 fusion.13
  44.4 9.6 %shard_map.94.refs_2_ = f32[2,16,16384]{2,1,0:T(8,128)} custom-call(bf16[2,18,16640]{2,1,0:T(8,128)(2,1)} %copy-done.3, f32[27,8,128]{2,1,0:T(8,128)} %broadcast_in_dim.18.refs_1_.refs_3_), custom_call_target="tpu_custom_call" | custom-call | tf_op jit(solution)/shard_map/pallas_call | solution.py:149
  54.0 1.2 fusion.36
  55.3 6.8 %shard_map.95 = bf16[2,16,16384]{2,1,0:T(8,128)(2,1)} custom-call(bf16[1,18,16640]{2,1,0:T(8,128)(2,1)} %collective-permute-done.7.refs_0_, bf16[1,18,16640]{2,1,0:T(8,128)(2,1)} %collective-permute-done.8.refs_1_, f32[2,16,16384]{2,1,0:T(8,128)} %shard_map.94.refs_2_, f32[27,8,128]{2,1,0:T(8,128)} %broadcast_in_dim.18.refs_1_.refs_3_), custom_call_target="tpu_custom_call" | custom-call | tf_op jit(solution)/shard_map/pallas_call | solution.py:149
  63.0 1.4 collective-permute-start.10
  64.3 1.3 collective-permute-start.11
  65.6 3.0 %reshape.101 = bf16[8192,64]{1,0:T(8,128)(2,1)S(1)} reshape(bf16[2,16,16384]{2,1,0:T(8,128)(2,1)} %shard_map.95) | data formatting | bytes 2097152 | tf_op jit(solution)/shard_map/reshape | solution.py:237
  68.7 1.2 fusion.119
  69.9 2.8 %fusion.5 = f32[8192,64]{0,1:T(8,128)S(1)} fusion(bf16[256,64]{0,1:T(8,128)(2,1)S(1)} %copy-done.11, f32[8192,256]{1,0:T(8,128)S(1)} %fusion.119), kind=kOutput, calls=%fused_computation.10 | convolution fusion | flops 278921216 | bytes 10518528 | tf_op jit(solution)/shard_map/dot_general | solution.py:240
  74.8 2.6 %fusion.11 = (bf16[32,256,64]{1,2,0:T(8,128)(2,1)S(1)}, bf16[32,256,64]{1,2,0:T(8,128)(2,1)}) fusion(f32[32,256,64]{1,2,0:T(8,128)S(1)} %copy-done.5, f32[256,32,64]{0,2,1:T(8,128)S(1)} %fusion.20, bf16[32,32,64]{2,1,0:T(8,128)(2,1)S(1)} %get-tuple-element.37, f32[32]{0:T(128)S(1)} %get-tuple-element.39, s32[32]{0:T(128)S(1)} %add.186, ...), kind=kOutput, calls=%fused_computation.17 | convolution fusion | flops 41041920 | bytes 8520960 | tf_op jit(solution)/shard_map/krc,xk->rxc/dot_general | solution.py:185
  80.4 1.4 collective-permute-start.13
  81.8 1.2 collective-permute-start.12
  83.1 8.8 %convolution_convert_fusion = bf16[8192,64]{0,1:T(8,128)(2,1)} fusion(bf16[64,256]{1,0:T(8,128)(2,1)S(1)} %copy-done, bf16[8192,64]{0,1:T(8,128)(2,1)S(1)} %bitcast.55, bf16[256,64]{0,1:T(8,128)(2,1)S(1)} %copy-done.12, f32[8192,256]{1,0:T(8,128)} %copy-done.4), kind=kOutput, calls=%fused_computation.3 | convolution fusion | flops 558366720 | bytes 10551296 | tf_op jit(solution)/shard_map/dot_general | solution.py:256
  91.9 2.0 %copy.29 = bf16[32,256,64]{2,1,0:T(8,128)(2,1)S(1)} copy(bf16[32,256,64]{1,2,0:T(8,128)(2,1)} %get-tuple-element.14) | data formatting | bytes 2097152 | tf_op jit(solution)/shard_map/convert_element_type | solution.py:246
  93.9 2.5 %reshape.103 = bf16[2,16,16384]{2,1,0:T(8,128)(2,1)} reshape(bf16[32,256,64]{2,1,0:T(8,128)(2,1)S(1)} %copy.29) | data formatting | bytes 2097152 | tf_op jit(solution)/shard_map/reshape | solution.py:246
  96.4 2.0 %copy.35 = bf16[8192,64]{1,0:T(8,128)(2,1)S(1)} copy(bf16[8192,64]{0,1:T(8,128)(2,1)} %convolution_convert_fusion) | data formatting | bytes 2097152 | tf_op jit(solution)/shard_map/convert_element_type | solution.py:256
  98.4 2.5 %reshape.105 = bf16[2,16,16384]{2,1,0:T(8,128)(2,1)} reshape(bf16[8192,64]{1,0:T(8,128)(2,1)S(1)} %copy.35) | data formatting | bytes 2097152 | tf_op jit(solution)/shard_map/reshape | solution.py:259
  100.9 1.2 fusion.28
  105.1 1.4 collective-permute-start.22
  106.5 1.7 %collective-permute-start.23 = (bf16[8,32,128]{2,1,0:T(8,128)(2,1)S(1)}, bf16[8,32,128]{2,1,0:T(8,128)(2,1)S(1)}, u32[]{:S(2)}, u32[]{:S(2)}) collective-permute-start(bf16[8,32,128]{2,1,0:T(8,128)(2,1)S(1)} %convolution_convert_fusion.1), channel_id=1, source_target_pairs={{0,24},{8,0},{16,8},{24,16},{1,25},{9,1},{17,9},{25,17},{2,26},{10... | collective-permute-start | bytes 196616 | tf_op jit(solution)/shard_map/ppermute | solution.py:55
  109.0 2.9 %collective-permute-done.16 = bf16[2,16,128]{2,1,0:T(8,128)(2,1)S(1)} collective-permute-done((bf16[2,16,128]{2,1,0:T(8,128)(2,1)S(1)}, bf16[2,16,128]{2,1,0:T(8,128)(2,1)S(1)}, u32[]{:S(2)}, u32[]{:S(2)}) %collective-permute-start.16) | collective-permute-done | bytes 8224 | tf_op jit(solution)/shard_map/ppermute | solution.py:20
  112.1 1.3 collective-permute-start.18
  113.4 3.0 %collective-permute-start.17 = (bf16[2,1,16640]{2,1,0:T(2,128)(2,1)S(1)}, bf16[2,1,16640]{2,1,0:T(2,128)(2,1)S(1)}, u32[]{:S(2)}, u32[]{:S(2)}) collective-permute-start(bf16[2,1,16640]{2,1,0:T(2,128)(2,1)S(1)} %get-tuple-element.19), channel_id=1, source_target_pairs={{0,4},{1,5},{2,6},{3,7},{8,12},{9,13},{10,14},{11,15},{16,20},{17,... | collective-permute-start | bytes 199688 | tf_op jit(solution)/shard_map/ppermute | solution.py:19
  118.1 2.7 %collective-permute-start.25 = (bf16[64,1024]{1,0:T(8,128)(2,1)S(1)}, bf16[64,1024]{1,0:T(8,128)(2,1)S(1)}, u32[]{:S(2)}, u32[]{:S(2)}) collective-permute-start(bf16[64,1024]{1,0:T(8,128)(2,1)S(1)} %add_convert_fusion.2), channel_id=1, source_target_pairs={{0,1},{1,0},{2,3},{3,2},{4,5},{5,4},{6,7},{7,6},{8,9},{9,8},{10,11... | collective-permute-start | bytes 393224 | tf_op jit(solution)/shard_map/ppermute | solution.py:77
  120.8 1.2 fusion.111
  122.1 2.3 %collective-permute-start.19 = (bf16[1,18,16640]{2,1,0:T(8,128)(2,1)}, bf16[1,18,16640]{2,1,0:T(8,128)(2,1)S(1)}, u32[]{:S(2)}, u32[]{:S(2)}) collective-permute-start(bf16[1,18,16640]{2,1,0:T(8,128)(2,1)} %get-tuple-element.16), channel_id=1, source_target_pairs={{0,1},{1,2},{2,3},{4,5},{5,6},{6,7},{8,9},{9,10},{10,11},{12,13},{... | collective-permute-start | bytes 1797128 | tf_op jit(solution)/shard_map/ppermute | solution.py:96
  124.3 1.5 collective-permute-start.20
  125.9 4.9 %collective-permute-start.26 = (bf16[64,1024]{1,0:T(8,128)(2,1)S(1)}, bf16[64,1024]{1,0:T(8,128)(2,1)S(1)}, u32[]{:S(2)}, u32[]{:S(2)}) collective-permute-start(bf16[64,1024]{1,0:T(8,128)(2,1)S(1)} %add_convert_fusion.1), channel_id=1, source_target_pairs={{0,2},{1,3},{2,0},{3,1},{4,6},{5,7},{6,4},{7,5},{8,10},{9,11},{10,... | collective-permute-start | bytes 393224 | tf_op jit(solution)/shard_map/ppermute | solution.py:77
  130.8 2.0 %add_bitcast_fusion = f32[32,256,64]{1,2,0:T(8,128)} fusion(f32[256,32,64]{0,2,1:T(8,128)S(1)} %fusion.17, bf16[32,32,64]{2,1,0:T(8,128)(2,1)S(1)} %get-tuple-element.35, s32[32]{0:T(128)S(1)} %add.186, s32[256]{0:T(256)S(1)} %iota_add_fusion.1), kind=kOutput, calls=%fused_computation.20 | convolution fusion | flops 34201600 | bytes 4326528 | tf_op jit(solution)/shard_map/krc,xk->rxc/dot_general | solution.py:185
  132.8 3.8 %copy.38 = f32[32,256,64]{2,1,0:T(8,128)} copy(f32[32,256,64]{1,2,0:T(8,128)} %add_bitcast_fusion) | data formatting | bytes 4194304 | tf_op jit(solution)/shard_map/add | solution.py:188
  136.6 2.9 %reshape.106 = f32[2,16,16384]{2,1,0:T(8,128)S(1)} reshape(f32[32,256,64]{2,1,0:T(8,128)} %copy.38) | data formatting | bytes 4194304 | tf_op jit(solution)/shard_map/reshape | solution.py:271
  140.2 9.6 %shard_map.96.refs_2_ = f32[2,16,16384]{2,1,0:T(8,128)} custom-call(bf16[2,18,16640]{2,1,0:T(8,128)(2,1)} %copy-done.2, f32[27,8,128]{2,1,0:T(8,128)} %broadcast_in_dim.36.refs_1_.refs_3_), custom_call_target="tpu_custom_call" | custom-call | tf_op jit(solution)/shard_map/pallas_call | solution.py:149
  149.8 4.0 %collective-permute-done.26 = bf16[64,1024]{1,0:T(8,128)(2,1)S(1)} collective-permute-done((bf16[64,1024]{1,0:T(8,128)(2,1)S(1)}, bf16[64,1024]{1,0:T(8,128)(2,1)S(1)}, u32[]{:S(2)}, u32[]{:S(2)}) %collective-permute-start.26) | collective-permute-done | bytes 131104 | tf_op jit(solution)/shard_map/ppermute | solution.py:77
  155.6 7.1 %shard_map.97 = f32[2,16,16384]{2,1,0:T(8,128)} custom-call(bf16[1,18,16640]{2,1,0:T(8,128)(2,1)} %copy-done.9, bf16[1,18,16640]{2,1,0:T(8,128)(2,1)} %collective-permute-done.20.refs_1_, f32[2,16,16384]{2,1,0:T(8,128)} %shard_map.96.refs_2_, f32[27,8,128]{2,1,0:T(8,128)} %broadcast_in_dim.36.refs_1_.refs_3_), custom_call_target="tpu_custom_call" | custom-call | tf_op jit(solution)/shard_map/pallas_call | solution.py:149
  162.7 2.7 %add_convert_fusion = bf16[2,16,16384]{2,1,0:T(8,128)(2,1)} fusion(f32[2,16,16384]{2,1,0:T(8,128)} %shard_map.97, f32[2,16,16384]{2,1,0:T(8,128)S(1)} %reshape.106), kind=kLoop, calls=%fused_computation.19 | loop fusion | flops 1048576 | bytes 5242880 | tf_op jit(solution)/shard_map/convert_element_type | solution.py:271
  (111 shorter events, 22.4 us)
Async XLA Ops:
  0.6 68.0 %copy-start = (bf16[64,256]{1,0:T(8,128)(2,1)S(1)}, bf16[64,256]{1,0:T(8,128)(2,1)}, u32[]{:S(2)}) copy-start(bf16[64,256]{1,0:T(8,128)(2,1)} %param.9) | copy-start | bytes 98308
  4.8 12.0 %copy-start.6 = (bf16[2,16,16384]{2,1,0:T(8,128)(2,1)S(1)}, bf16[2,16,16384]{2,1,0:T(8,128)(2,1)}, u32[]{:S(2)}) copy-start(bf16[2,16,16384]{2,1,0:T(8,128)(2,1)} %param.7) | copy-start | bytes 3145732
  5.8 48.2 %collective-permute-start.2 = (f32[8,32,128]{2,0,1:T(8,128)}, f32[8,32,128]{2,0,1:T(8,128)}, u32[]{:S(2)}, u32[]{:S(2)}) collective-permute-start(f32[8,32,128]{2,0,1:T(8,128)} %get-tuple-element.32), channel_id=1, source_target_pairs={{0,24},{8,0},{16,8},{24,16},{1,25},{9,1},{17,9},{25,17},{2,26},{10... | collective-permute-start | bytes 393224 | tf_op jit(solution)/shard_map/ppermute | solution.py:66
  9.7 44.3 %collective-permute-start.1 = (f32[8,32,128]{2,0,1:T(8,128)}, f32[8,32,128]{2,0,1:T(8,128)}, u32[]{:S(2)}, u32[]{:S(2)}) collective-permute-start(f32[8,32,128]{2,0,1:T(8,128)} %get-tuple-element.31), channel_id=1, source_target_pairs={{0,16},{8,24},{16,0},{24,8},{1,17},{9,25},{17,1},{25,9},{2,18},{10... | collective-permute-start | bytes 393224 | tf_op jit(solution)/shard_map/ppermute | solution.py:66
  10.2 43.8 %collective-permute-start = (f32[8,32,128]{2,0,1:T(8,128)}, f32[8,32,128]{2,0,1:T(8,128)}, u32[]{:S(2)}, u32[]{:S(2)}) collective-permute-start(f32[8,32,128]{2,0,1:T(8,128)} %get-tuple-element.30), channel_id=1, source_target_pairs={{0,8},{8,16},{16,24},{24,0},{1,9},{9,17},{17,25},{25,1},{2,10},{10... | collective-permute-start | bytes 393224 | tf_op jit(solution)/shard_map/ppermute | solution.py:66
  11.5 5.3 %collective-permute-start.3 = (bf16[2,16,128]{2,1,0:T(8,128)(2,1)S(1)}, bf16[2,16,128]{2,1,0:T(8,128)(2,1)S(1)}, u32[]{:S(2)}, u32[]{:S(2)}) collective-permute-start(bf16[2,16,128]{2,1,0:T(8,128)(2,1)S(1)} %get-tuple-element.29), channel_id=1, source_target_pairs={{0,8},{8,16},{16,24},{24,0},{1,9},{9,17},{17,25},{25,1},{2,10},{10... | collective-permute-start | bytes 24584 | tf_op jit(solution)/shard_map/ppermute | solution.py:19
  13.9 3.7 %collective-permute-start.4 = (bf16[2,16,128]{2,1,0:T(8,128)(2,1)S(1)}, bf16[2,16,128]{2,1,0:T(8,128)(2,1)S(1)}, u32[]{:S(2)}, u32[]{:S(2)}) collective-permute-start(bf16[2,16,128]{2,1,0:T(8,128)(2,1)S(1)} %get-tuple-element.28), channel_id=1, source_target_pairs={{8,0},{16,8},{24,16},{0,24},{9,1},{17,9},{25,17},{1,25},{10,2},{18... | collective-permute-start | bytes 24584 | tf_op jit(solution)/shard_map/ppermute | solution.py:20
  17.5 1.0 copy-start.8
  18.8 4.5 %collective-permute-start.6 = (bf16[2,1,16640]{2,1,0:T(2,128)(2,1)S(1)}, bf16[2,1,16640]{2,1,0:T(2,128)(2,1)S(1)}, u32[]{:S(2)}, u32[]{:S(2)}) collective-permute-start(bf16[2,1,16640]{2,1,0:T(2,128)(2,1)S(1)} %get-tuple-element.22), channel_id=1, source_target_pairs={{4,0},{5,1},{6,2},{7,3},{12,8},{13,9},{14,10},{15,11},{20,16},{21,... | collective-permute-start | bytes 199688 | tf_op jit(solution)/shard_map/ppermute | solution.py:20
  20.1 4.0 %collective-permute-start.5 = (bf16[2,1,16640]{2,1,0:T(2,128)(2,1)S(1)}, bf16[2,1,16640]{2,1,0:T(2,128)(2,1)S(1)}, u32[]{:S(2)}, u32[]{:S(2)}) collective-permute-start(bf16[2,1,16640]{2,1,0:T(2,128)(2,1)S(1)} %get-tuple-element.21), channel_id=1, source_target_pairs={{0,4},{1,5},{2,6},{3,7},{8,12},{9,13},{10,14},{11,15},{16,20},{17,... | collective-permute-start | bytes 199688 | tf_op jit(solution)/shard_map/ppermute | solution.py:19
  25.9 11.4 %copy-start.3 = (bf16[2,18,16640]{2,1,0:T(8,128)(2,1)}, bf16[2,18,16640]{2,1,0:T(8,128)(2,1)S(1)}, u32[]{:S(2)}) copy-start(bf16[2,18,16640]{2,1,0:T(8,128)(2,1)S(1)} %pad_maximum_fusion.refs_0_) | copy-start | bytes 3594244
  27.3 28.0 %collective-permute-start.7 = (bf16[1,18,16640]{2,1,0:T(8,128)(2,1)}, bf16[1,18,16640]{2,1,0:T(8,128)(2,1)}, u32[]{:S(2)}, u32[]{:S(2)}) collective-permute-start(bf16[1,18,16640]{2,1,0:T(8,128)(2,1)} %get-tuple-element.18), channel_id=1, source_target_pairs={{0,1},{1,2},{2,3},{4,5},{5,6},{6,7},{8,9},{9,10},{10,11},{12,13},{... | collective-permute-start | bytes 1797128 | tf_op jit(solution)/shard_map/ppermute | solution.py:96
  31.7 23.6 %collective-permute-start.8 = (bf16[1,18,16640]{2,1,0:T(8,128)(2,1)}, bf16[1,18,16640]{2,1,0:T(8,128)(2,1)}, u32[]{:S(2)}, u32[]{:S(2)}) collective-permute-start(bf16[1,18,16640]{2,1,0:T(8,128)(2,1)} %get-tuple-element.17), channel_id=1, source_target_pairs={{1,0},{2,1},{3,2},{5,4},{6,5},{7,6},{9,8},{10,9},{11,10},{13,12},{... | collective-permute-start | bytes 1797128 | tf_op jit(solution)/shard_map/ppermute | solution.py:97
  37.3 5.0 %copy-start.10 = (bf16[27,64]{1,0:T(8,128)(2,1)S(1)}, bf16[27,64]{1,0:T(8,128)(2,1)}, u32[]{:S(2)}) copy-start(bf16[27,64]{1,0:T(8,128)(2,1)} %param.8) | copy-start | bytes 10372
  62.1 11.1 %collective-permute-start.9 = (bf16[8,32,128]{2,1,0:T(8,128)(2,1)S(1)}, bf16[8,32,128]{2,1,0:T(8,128)(2,1)S(1)}, u32[]{:S(2)}, u32[]{:S(2)}) collective-permute-start(bf16[8,32,128]{2,1,0:T(8,128)(2,1)S(1)} %convolution_convert_fusion.2), channel_id=1, source_target_pairs={{0,8},{8,16},{16,24},{24,0},{1,9},{9,17},{17,25},{25,1},{2,10},{10... | collective-permute-start | bytes 196616 | tf_op jit(solution)/shard_map/ppermute | solution.py:55
  63.0 10.2 %collective-permute-start.10 = (bf16[8,32,128]{2,1,0:T(8,128)(2,1)S(1)}, bf16[8,32,128]{2,1,0:T(8,128)(2,1)S(1)}, u32[]{:S(2)}, u32[]{:S(2)}) collective-permute-start(bf16[8,32,128]{2,1,0:T(8,128)(2,1)S(1)} %convolution_convert_fusion.2), channel_id=1, source_target_pairs={{0,16},{8,24},{16,0},{24,8},{1,17},{9,25},{17,1},{25,9},{2,18},{10... | collective-permute-start | bytes 196616 | tf_op jit(solution)/shard_map/ppermute | solution.py:55
  64.3 8.9 %collective-permute-start.11 = (bf16[8,32,128]{2,1,0:T(8,128)(2,1)S(1)}, bf16[8,32,128]{2,1,0:T(8,128)(2,1)S(1)}, u32[]{:S(2)}, u32[]{:S(2)}) collective-permute-start(bf16[8,32,128]{2,1,0:T(8,128)(2,1)S(1)} %convolution_convert_fusion.2), channel_id=1, source_target_pairs={{0,24},{8,0},{16,8},{24,16},{1,25},{9,1},{17,9},{25,17},{2,26},{10... | collective-permute-start | bytes 196616 | tf_op jit(solution)/shard_map/ppermute | solution.py:55
  68.6 1.2 copy-start.11
  69.9 3.3 %copy-start.4 = (f32[8192,256]{1,0:T(8,128)}, f32[8192,256]{1,0:T(8,128)S(1)}, u32[]{:S(2)}) copy-start(f32[8192,256]{1,0:T(8,128)S(1)} %fusion.119) | copy-start | bytes 25165828
  73.2 1.6 copy-start.5
  78.6 4.5 %copy-start.12 = (bf16[256,64]{0,1:T(8,128)(2,1)S(1)}, bf16[256,64]{0,1:T(8,128)(2,1)}, u32[]{:S(2)}) copy-start(bf16[256,64]{0,1:T(8,128)(2,1)} %param.10) | copy-start | bytes 98308
  79.5 21.4 %collective-permute-start.14 = (f32[8,32,128]{2,0,1:T(8,128)}, f32[8,32,128]{2,0,1:T(8,128)}, u32[]{:S(2)}, u32[]{:S(2)}) collective-permute-start(f32[8,32,128]{2,0,1:T(8,128)} %get-tuple-element.27), channel_id=1, source_target_pairs={{0,24},{8,0},{16,8},{24,16},{1,25},{9,1},{17,9},{25,17},{2,26},{10... | collective-permute-start | bytes 393224 | tf_op jit(solution)/shard_map/ppermute | solution.py:66
  80.4 20.5 %collective-permute-start.13 = (f32[8,32,128]{2,0,1:T(8,128)}, f32[8,32,128]{2,0,1:T(8,128)}, u32[]{:S(2)}, u32[]{:S(2)}) collective-permute-start(f32[8,32,128]{2,0,1:T(8,128)} %get-tuple-element.26), channel_id=1, source_target_pairs={{0,16},{8,24},{16,0},{24,8},{1,17},{9,25},{17,1},{25,9},{2,18},{10... | collective-permute-start | bytes 393224 | tf_op jit(solution)/shard_map/ppermute | solution.py:66
  81.8 19.1 %collective-permute-start.12 = (f32[8,32,128]{2,0,1:T(8,128)}, f32[8,32,128]{2,0,1:T(8,128)}, u32[]{:S(2)}, u32[]{:S(2)}) collective-permute-start(f32[8,32,128]{2,0,1:T(8,128)} %get-tuple-element.25), channel_id=1, source_target_pairs={{0,8},{8,16},{16,24},{24,0},{1,9},{9,17},{17,25},{25,1},{2,10},{10... | collective-permute-start | bytes 393224 | tf_op jit(solution)/shard_map/ppermute | solution.py:66
  100.9 2.1 %copy-start.7 = (bf16[2,16,16384]{2,1,0:T(8,128)(2,1)S(1)}, bf16[2,16,16384]{2,1,0:T(8,128)(2,1)}, u32[]{:S(2)}) copy-start(bf16[2,16,16384]{2,1,0:T(8,128)(2,1)} %reshape.105) | copy-start | bytes 3145732
  103.0 5.8 %collective-permute-start.15 = (bf16[2,16,128]{2,1,0:T(8,128)(2,1)S(1)}, bf16[2,16,128]{2,1,0:T(8,128)(2,1)S(1)}, u32[]{:S(2)}, u32[]{:S(2)}) collective-permute-start(bf16[2,16,128]{2,1,0:T(8,128)(2,1)S(1)} %get-tuple-element.24), channel_id=1, source_target_pairs={{0,8},{8,16},{16,24},{24,0},{1,9},{9,17},{17,25},{25,1},{2,10},{10... | collective-permute-start | bytes 24584 | tf_op jit(solution)/shard_map/ppermute | solution.py:19
  103.9 9.5 %collective-permute-start.21 = (bf16[8,32,128]{2,1,0:T(8,128)(2,1)S(1)}, bf16[8,32,128]{2,1,0:T(8,128)(2,1)S(1)}, u32[]{:S(2)}, u32[]{:S(2)}) collective-permute-start(bf16[8,32,128]{2,1,0:T(8,128)(2,1)S(1)} %convolution_convert_fusion.1), channel_id=1, source_target_pairs={{0,8},{8,16},{16,24},{24,0},{1,9},{9,17},{17,25},{25,1},{2,10},{10... | collective-permute-start | bytes 196616 | tf_op jit(solution)/shard_map/ppermute | solution.py:55
  105.1 11.4 %collective-permute-start.22 = (bf16[8,32,128]{2,1,0:T(8,128)(2,1)S(1)}, bf16[8,32,128]{2,1,0:T(8,128)(2,1)S(1)}, u32[]{:S(2)}, u32[]{:S(2)}) collective-permute-start(bf16[8,32,128]{2,1,0:T(8,128)(2,1)S(1)} %convolution_convert_fusion.1), channel_id=1, source_target_pairs={{0,16},{8,24},{16,0},{24,8},{1,17},{9,25},{17,1},{25,9},{2,18},{10... | collective-permute-start | bytes 196616 | tf_op jit(solution)/shard_map/ppermute | solution.py:55
  106.5 10.0 %collective-permute-start.23 = (bf16[8,32,128]{2,1,0:T(8,128)(2,1)S(1)}, bf16[8,32,128]{2,1,0:T(8,128)(2,1)S(1)}, u32[]{:S(2)}, u32[]{:S(2)}) collective-permute-start(bf16[8,32,128]{2,1,0:T(8,128)(2,1)S(1)} %convolution_convert_fusion.1), channel_id=1, source_target_pairs={{0,24},{8,0},{16,8},{24,16},{1,25},{9,1},{17,9},{25,17},{2,26},{10... | collective-permute-start | bytes 196616 | tf_op jit(solution)/shard_map/ppermute | solution.py:55
  108.2 3.7 %collective-permute-start.16 = (bf16[2,16,128]{2,1,0:T(8,128)(2,1)S(1)}, bf16[2,16,128]{2,1,0:T(8,128)(2,1)S(1)}, u32[]{:S(2)}, u32[]{:S(2)}) collective-permute-start(bf16[2,16,128]{2,1,0:T(8,128)(2,1)S(1)} %get-tuple-element.23), channel_id=1, source_target_pairs={{8,0},{16,8},{24,16},{0,24},{9,1},{17,9},{25,17},{1,25},{10,2},{18... | collective-permute-start | bytes 24584 | tf_op jit(solution)/shard_map/ppermute | solution.py:20
  108.8 9.3 %collective-permute-start.24 = (bf16[64,1024]{1,0:T(8,128)(2,1)S(1)}, bf16[64,1024]{1,0:T(8,128)(2,1)S(1)}, u32[]{:S(2)}, u32[]{:S(2)}) collective-permute-start(bf16[64,1024]{1,0:T(8,128)(2,1)S(1)} %convert_element_type.143), channel_id=1, source_target_pairs={{0,4},{4,0},{1,5},{5,1},{2,6},{6,2},{3,7},{7,3},{8,12},{12,8},{9,1... | collective-permute-start | bytes 393224 | tf_op jit(solution)/shard_map/ppermute | solution.py:77
  112.1 5.2 %collective-permute-start.18 = (bf16[2,1,16640]{2,1,0:T(2,128)(2,1)S(1)}, bf16[2,1,16640]{2,1,0:T(2,128)(2,1)S(1)}, u32[]{:S(2)}, u32[]{:S(2)}) collective-permute-start(bf16[2,1,16640]{2,1,0:T(2,128)(2,1)S(1)} %get-tuple-element.20), channel_id=1, source_target_pairs={{4,0},{5,1},{6,2},{7,3},{12,8},{13,9},{14,10},{15,11},{20,16},{21,... | collective-permute-start | bytes 199688 | tf_op jit(solution)/shard_map/ppermute | solution.py:20
  113.4 4.0 %collective-permute-start.17 = (bf16[2,1,16640]{2,1,0:T(2,128)(2,1)S(1)}, bf16[2,1,16640]{2,1,0:T(2,128)(2,1)S(1)}, u32[]{:S(2)}, u32[]{:S(2)}) collective-permute-start(bf16[2,1,16640]{2,1,0:T(2,128)(2,1)S(1)} %get-tuple-element.19), channel_id=1, source_target_pairs={{0,4},{1,5},{2,6},{3,7},{8,12},{9,13},{10,14},{11,15},{16,20},{17,... | collective-permute-start | bytes 199688 | tf_op jit(solution)/shard_map/ppermute | solution.py:19
  118.0 14.8 %copy-start.2 = (bf16[2,18,16640]{2,1,0:T(8,128)(2,1)}, bf16[2,18,16640]{2,1,0:T(8,128)(2,1)S(1)}, u32[]{:S(2)}) copy-start(bf16[2,18,16640]{2,1,0:T(8,128)(2,1)S(1)} %pad_maximum_fusion.1.refs_0_) | copy-start | bytes 3594244
  118.1 7.7 %collective-permute-start.25 = (bf16[64,1024]{1,0:T(8,128)(2,1)S(1)}, bf16[64,1024]{1,0:T(8,128)(2,1)S(1)}, u32[]{:S(2)}, u32[]{:S(2)}) collective-permute-start(bf16[64,1024]{1,0:T(8,128)(2,1)S(1)} %add_convert_fusion.2), channel_id=1, source_target_pairs={{0,1},{1,0},{2,3},{3,2},{4,5},{5,4},{6,7},{7,6},{8,9},{9,8},{10,11... | collective-permute-start | bytes 393224 | tf_op jit(solution)/shard_map/ppermute | solution.py:77
  122.1 32.7 %collective-permute-start.19 = (bf16[1,18,16640]{2,1,0:T(8,128)(2,1)}, bf16[1,18,16640]{2,1,0:T(8,128)(2,1)S(1)}, u32[]{:S(2)}, u32[]{:S(2)}) collective-permute-start(bf16[1,18,16640]{2,1,0:T(8,128)(2,1)} %get-tuple-element.16), channel_id=1, source_target_pairs={{0,1},{1,2},{2,3},{4,5},{5,6},{6,7},{8,9},{9,10},{10,11},{12,13},{... | collective-permute-start | bytes 1797128 | tf_op jit(solution)/shard_map/ppermute | solution.py:96
  124.3 30.4 %collective-permute-start.20 = (bf16[1,18,16640]{2,1,0:T(8,128)(2,1)}, bf16[1,18,16640]{2,1,0:T(8,128)(2,1)}, u32[]{:S(2)}, u32[]{:S(2)}) collective-permute-start(bf16[1,18,16640]{2,1,0:T(8,128)(2,1)} %get-tuple-element.15), channel_id=1, source_target_pairs={{1,0},{2,1},{3,2},{5,4},{6,5},{7,6},{9,8},{10,9},{11,10},{13,12},{... | collective-permute-start | bytes 1797128 | tf_op jit(solution)/shard_map/ppermute | solution.py:97
  125.9 27.9 %collective-permute-start.26 = (bf16[64,1024]{1,0:T(8,128)(2,1)S(1)}, bf16[64,1024]{1,0:T(8,128)(2,1)S(1)}, u32[]{:S(2)}, u32[]{:S(2)}) collective-permute-start(bf16[64,1024]{1,0:T(8,128)(2,1)S(1)} %add_convert_fusion.1), channel_id=1, source_target_pairs={{0,2},{1,3},{2,0},{3,1},{4,6},{5,7},{6,4},{7,5},{8,10},{9,11},{10,... | collective-permute-start | bytes 393224 | tf_op jit(solution)/shard_map/ppermute | solution.py:77
  154.7 0.9 copy-start.9
  155.6 9.8 %copy-start.1 = (bf16[64,256]{1,0:T(8,128)(2,1)S(1)}, bf16[64,256]{1,0:T(8,128)(2,1)}, u32[]{:S(2)}) copy-start(bf16[64,256]{1,0:T(8,128)(2,1)} %param.9) | copy-start | bytes 98308

commit v12 on v11

--- a/solution.py
+++ b/solution.py
@@ -12,12 +12,19 @@
 def padded_2(value, sides, width, wrap):
     for axis, dim in sides:
         size, length = (lax.axis_size(axis), value.shape[dim])
-        up = [(i, (i + 1) % size) for i in range(size if wrap else size - 1)]
-        down = [(j, i) for i, j in up]
         last = lax.slice_in_dim(value, length - width, length, axis=dim)
         leading = lax.slice_in_dim(value, 0, width, axis=dim)
-        before = lax.ppermute(last, axis, up)
-        after = lax.ppermute(leading, axis, down)
+        if size == 2 and not wrap:
+            first = lax.axis_index(axis) == 0
+            swapped = lax.ppermute(jnp.where(first, last, leading), axis, [(0, 1), (1, 0)])
+            zeros = jnp.zeros_like(swapped)
+            before = jnp.where(first, zeros, swapped)
+            after = jnp.where(first, swapped, zeros)
+        else:
+            up = [(i, (i + 1) % size) for i in range(size if wrap else size - 1)]
+            down = [(j, i) for i, j in up]
+            before = lax.ppermute(last, axis, up)
+            after = lax.ppermute(leading, axis, down)
         value = jnp.concatenate([before, value, after], axis=dim)
     return value
 

time: 166 us -> 159 us (0.958)
  starting transfers between devices: 46.3 us -> 37.8 us
    ppermute x4 -> x2, starting transfers between devices: 9.43 us -> 3.33 us  [padded_2(): before = lax.ppermute(last, axis, up)]
    ppermute x4 -> x2, starting transfers between devices: 3.46 us -> 0.9 us  [padded_2(): after = lax.ppermute(leading, axis, down)]
    ppermute x4 -> x2, waiting for transfers between devices: 3.57 us -> 3.54 us  [padded_2(): after = lax.ppermute(leading, axis, down)]
  transfers between devices with their start and end apart: 27 -> 25, of which waited for: 6 -> 6; matrix products, arithmetic and copies ran while one was open for 34% -> 35% of each run, Pallas kernels for 12% -> 12%
where the time goes in v12:
time: 159 us; the launch traced here: 158 us
  local copies, waits for them, and re-layouts  39.8 us (25%)
  starting transfers between devices  37.8 us (24%)
  Pallas kernels  33 us (21%)
  matrix products  21.7 us (14%)
  other arithmetic  13.1 us (8%)
  waiting for transfers between devices  11.5 us (7%)
    pallas_call x4, Pallas kernels, stencil_call(): pl.pallas_call(kernel, out_shape=jax.ShapeDtypeStruct((len(plan), y_cells...  33 us
    dot_general x1, matrix products, per_device(): jnp.dot(grad_hidden, expand_weight.T, preferred_element_type=jnp.float32)  8.79 us
    ppermute x6, starting transfers between devices, ring_reduce_scatter(): lax.ppermute(piece, axis, [(i, (i + shift) % size) for i in range(size)])  8.46 us
    convert_element_type x2, local copies, waits for them, and re-layouts, per_device(): cotangent.reshape(row_count, x_cells, channels).astype(jnp.float32) * slopes  8.07 us
    ppermute x6, starting transfers between devices, ring_gather(): lax.ppermute(block, axis, [(i, (i + shift) % size) for i in range(size)])  7.79 us
    ppermute x3, starting transfers between devices, butterfly_sum(): lax.ppermute(value, axis, [(i, i ^ step) for i in range(size)])  7.71 us
    ppermute x2, starting transfers between devices, spatial_rims(): below = lax.ppermute(inner[-1:], 'gz', up)  6.65 us
    dot_general x2, matrix products, share_inverse(): jnp.einsum('krc,xk->rxc', segment[:, :, :channels], cos_table, preferred_...  4.55 us
  transfers between devices with their start and end apart: 25, of which 6 were waited for; matrix products, arithmetic and copies ran while one was open for 35% of the time, Pallas kernels for 12%

profile of v12, /device:TPU:0, one launch (start us, length us, event | category | flops | bytes accessed | tf_op | source)
XLA Modules:
  0.0 158.0 jit_solution(14821636379059219916)
XLA Ops:
  0.7 3.0 %reshape.100 = bf16[32,256,64]{2,1,0:T(8,128)(2,1)S(1)} reshape(bf16[2,16,16384]{2,1,0:T(8,128)(2,1)} %param.7) | data formatting | bytes 2097152 | tf_op jit(solution)/shard_map/reshape | solution.py:235
  5.8 3.9 %collective-permute-start.2 = (f32[8,32,128]{2,0,1:T(8,128)}, f32[8,32,128]{2,0,1:T(8,128)}, u32[]{:S(2)}, u32[]{:S(2)}) collective-permute-start(f32[8,32,128]{2,0,1:T(8,128)} %get-tuple-element.28), channel_id=1, source_target_pairs={{0,24},{8,0},{16,8},{24,16},{1,25},{9,1},{17,9},{25,17},{2,26},{10... | collective-permute-start | bytes 393224 | tf_op jit(solution)/shard_map/ppermute | solution.py:73
  11.5 2.4 %collective-permute-start.3 = (bf16[2,16,128]{2,1,0:T(8,128)(2,1)S(1)}, bf16[2,16,128]{2,1,0:T(8,128)(2,1)S(1)}, u32[]{:S(2)}, u32[]{:S(2)}) collective-permute-start(bf16[2,16,128]{2,1,0:T(8,128)(2,1)S(1)} %get-tuple-element.25), channel_id=1, source_target_pairs={{0,8},{8,16},{16,24},{24,0},{1,9},{9,17},{17,25},{25,1},{2,10},{10... | collective-permute-start | bytes 24584 | tf_op jit(solution)/shard_map/ppermute | solution.py:26
  14.4 2.4 %collective-permute-done.3 = bf16[2,16,128]{2,1,0:T(8,128)(2,1)S(1)} collective-permute-done((bf16[2,16,128]{2,1,0:T(8,128)(2,1)S(1)}, bf16[2,16,128]{2,1,0:T(8,128)(2,1)S(1)}, u32[]{:S(2)}, u32[]{:S(2)}) %collective-permute-start.3) | collective-permute-done | bytes 8224 | tf_op jit(solution)/shard_map/ppermute | solution.py:26
  17.5 1.0 copy-done.8
  19.0 1.2 collective-permute-done.5
  20.4 1.8 %pad_maximum_fusion.refs_0_ = bf16[2,18,16640]{2,1,0:T(8,128)(2,1)S(1)} fusion(bf16[2,1,16640]{2,1,0:T(2,128)(2,1)S(1)} %get-tuple-element.38, bf16[2,16,16640]{2,1,0:T(8,128)(2,1)} %copy-done.8, bf16[2,1,16640]{2,1,0:T(2,128)(2,1)S(1)} %get-tuple-element.37), kind=kLoop, calls=%fused_computation.23 | loop fusion | flops 3594240 | bytes 2396160 | tf_op jit(solution)/shard_map/concatenate | solution.py:28
  22.2 1.4 fusion.112
  23.7 4.4 %collective-permute-start.6 = (bf16[1,18,16640]{2,1,0:T(8,128)(2,1)}, bf16[1,18,16640]{2,1,0:T(8,128)(2,1)}, u32[]{:S(2)}, u32[]{:S(2)}) collective-permute-start(bf16[1,18,16640]{2,1,0:T(8,128)(2,1)} %get-tuple-element.18), channel_id=1, source_target_pairs={{0,1},{1,2},{2,3},{4,5},{5,6},{6,7},{8,9},{9,10},{10,11},{12,13},{... | collective-permute-start | bytes 1797128 | tf_op jit(solution)/shard_map/ppermute | solution.py:103
  28.1 1.3 collective-permute-start.7
  29.4 4.3 %reshape.108 = f32[32,256,64]{2,1,0:T(8,128)} reshape(bf16[2,16,16384]{2,1,0:T(8,128)(2,1)} %param.13) | data formatting | bytes 3145728 | tf_op jit(solution)/shard_map/convert_element_type | solution.py:255
  33.6 3.8 %copy.30 = f32[32,256,64]{1,2,0:T(8,128)} copy(f32[32,256,64]{2,1,0:T(8,128)} %reshape.108) | data formatting | bytes 4194304 | tf_op jit(solution)/shard_map/convert_element_type | solution.py:255
  37.4 1.2 neg.10
  38.9 1.2 fusion.13
  40.7 9.6 %shard_map.94.refs_2_ = f32[2,16,16384]{2,1,0:T(8,128)} custom-call(bf16[2,18,16640]{2,1,0:T(8,128)(2,1)} %copy-done.3, f32[27,8,128]{2,1,0:T(8,128)} %broadcast_in_dim.18.refs_1_.refs_3_), custom_call_target="tpu_custom_call" | custom-call | tf_op jit(solution)/shard_map/pallas_call | solution.py:156
  50.3 1.2 fusion.36
  51.6 6.8 %shard_map.95 = bf16[2,16,16384]{2,1,0:T(8,128)(2,1)} custom-call(bf16[1,18,16640]{2,1,0:T(8,128)(2,1)} %collective-permute-done.6.refs_0_, bf16[1,18,16640]{2,1,0:T(8,128)(2,1)} %collective-permute-done.7.refs_1_, f32[2,16,16384]{2,1,0:T(8,128)} %shard_map.94.refs_2_, f32[27,8,128]{2,1,0:T(8,128)} %broadcast_in_dim.18.refs_1_.refs_3_), custom_call_target="tpu_custom_call" | custom-call | tf_op jit(solution)/shard_map/pallas_call | solution.py:156
  59.3 1.4 collective-permute-start.9
  60.7 1.2 collective-permute-start.10
  61.9 3.0 %reshape.101 = bf16[8192,64]{1,0:T(8,128)(2,1)S(1)} reshape(bf16[2,16,16384]{2,1,0:T(8,128)(2,1)} %shard_map.95) | data formatting | bytes 2097152 | tf_op jit(solution)/shard_map/reshape | solution.py:244
  65.0 1.2 fusion.117
  66.2 2.8 %fusion.5 = f32[8192,64]{0,1:T(8,128)S(1)} fusion(bf16[256,64]{0,1:T(8,128)(2,1)S(1)} %copy-done.11, f32[8192,256]{1,0:T(8,128)S(1)} %fusion.117), kind=kOutput, calls=%fused_computation.10 | convolution fusion | flops 278921216 | bytes 10518528 | tf_op jit(solution)/shard_map/dot_general | solution.py:247
  71.1 2.6 %fusion.11 = (bf16[32,256,64]{1,2,0:T(8,128)(2,1)S(1)}, bf16[32,256,64]{1,2,0:T(8,128)(2,1)}) fusion(f32[32,256,64]{1,2,0:T(8,128)S(1)} %copy-done.5, f32[256,32,64]{0,2,1:T(8,128)S(1)} %fusion.20, bf16[32,32,64]{2,1,0:T(8,128)(2,1)S(1)} %get-tuple-element.33, f32[32]{0:T(128)S(1)} %get-tuple-element.39, s32[32]{0:T(128)S(1)} %add.186, ...), kind=kOutput, calls=%fused_computation.17 | convolution fusion | flops 41041920 | bytes 8520960 | tf_op jit(solution)/shard_map/krc,xk->rxc/dot_general | solution.py:192
  76.7 1.4 collective-permute-start.12
  78.1 1.2 collective-permute-start.11
  79.4 8.8 %convolution_convert_fusion = bf16[8192,64]{0,1:T(8,128)(2,1)} fusion(bf16[64,256]{1,0:T(8,128)(2,1)S(1)} %copy-done, bf16[8192,64]{0,1:T(8,128)(2,1)S(1)} %bitcast.55, bf16[256,64]{0,1:T(8,128)(2,1)S(1)} %copy-done.12, f32[8192,256]{1,0:T(8,128)} %copy-done.4), kind=kOutput, calls=%fused_computation.3 | convolution fusion | flops 558366720 | bytes 10551296 | tf_op jit(solution)/shard_map/dot_general | solution.py:263
  88.2 2.0 %copy.29 = bf16[32,256,64]{2,1,0:T(8,128)(2,1)S(1)} copy(bf16[32,256,64]{1,2,0:T(8,128)(2,1)} %get-tuple-element.14) | data formatting | bytes 2097152 | tf_op jit(solution)/shard_map/convert_element_type | solution.py:253
  90.2 2.5 %reshape.103 = bf16[2,16,16384]{2,1,0:T(8,128)(2,1)} reshape(bf16[32,256,64]{2,1,0:T(8,128)(2,1)S(1)} %copy.29) | data formatting | bytes 2097152 | tf_op jit(solution)/shard_map/reshape | solution.py:253
  92.7 2.0 %copy.35 = bf16[8192,64]{1,0:T(8,128)(2,1)S(1)} copy(bf16[8192,64]{0,1:T(8,128)(2,1)} %convolution_convert_fusion) | data formatting | bytes 2097152 | tf_op jit(solution)/shard_map/convert_element_type | solution.py:263
  94.8 2.5 %reshape.105 = bf16[2,16,16384]{2,1,0:T(8,128)(2,1)} reshape(bf16[8192,64]{1,0:T(8,128)(2,1)S(1)} %copy.35) | data formatting | bytes 2097152 | tf_op jit(solution)/shard_map/reshape | solution.py:266
  97.3 1.2 fusion.28
  99.3 0.9 collective-permute-start.14
  100.3 1.2 collective-permute-start.19
  101.4 1.4 collective-permute-start.20
  102.9 1.7 %collective-permute-start.21 = (bf16[8,32,128]{2,1,0:T(8,128)(2,1)S(1)}, bf16[8,32,128]{2,1,0:T(8,128)(2,1)S(1)}, u32[]{:S(2)}, u32[]{:S(2)}) collective-permute-start(bf16[8,32,128]{2,1,0:T(8,128)(2,1)S(1)} %convolution_convert_fusion.1), channel_id=1, source_target_pairs={{0,24},{8,0},{16,8},{24,16},{1,25},{9,1},{17,9},{25,17},{2,26},{10... | collective-permute-start | bytes 196616 | tf_op jit(solution)/shard_map/ppermute | solution.py:62
  105.3 2.9 %collective-permute-done.15 = bf16[2,16,128]{2,1,0:T(8,128)(2,1)S(1)} collective-permute-done((bf16[2,16,128]{2,1,0:T(8,128)(2,1)S(1)}, bf16[2,16,128]{2,1,0:T(8,128)(2,1)S(1)}, u32[]{:S(2)}, u32[]{:S(2)}) %collective-permute-start.15) | collective-permute-done | bytes 8224 | tf_op jit(solution)/shard_map/ppermute | solution.py:27
  110.8 2.7 %collective-permute-start.23 = (bf16[64,1024]{1,0:T(8,128)(2,1)S(1)}, bf16[64,1024]{1,0:T(8,128)(2,1)S(1)}, u32[]{:S(2)}, u32[]{:S(2)}) collective-permute-start(bf16[64,1024]{1,0:T(8,128)(2,1)S(1)} %add_convert_fusion.2), channel_id=1, source_target_pairs={{0,1},{1,0},{2,3},{3,2},{4,5},{5,4},{6,7},{7,6},{8,9},{9,8},{10,11... | collective-permute-start | bytes 393224 | tf_op jit(solution)/shard_map/ppermute | solution.py:84
  113.5 1.3 fusion.111
  114.7 2.3 %collective-permute-start.17 = (bf16[1,18,16640]{2,1,0:T(8,128)(2,1)}, bf16[1,18,16640]{2,1,0:T(8,128)(2,1)S(1)}, u32[]{:S(2)}, u32[]{:S(2)}) collective-permute-start(bf16[1,18,16640]{2,1,0:T(8,128)(2,1)} %get-tuple-element.16), channel_id=1, source_target_pairs={{0,1},{1,2},{2,3},{4,5},{5,6},{6,7},{8,9},{9,10},{10,11},{12,13},{... | collective-permute-start | bytes 1797128 | tf_op jit(solution)/shard_map/ppermute | solution.py:103
  117.0 1.5 collective-permute-start.18
  118.6 4.9 %collective-permute-start.24 = (bf16[64,1024]{1,0:T(8,128)(2,1)S(1)}, bf16[64,1024]{1,0:T(8,128)(2,1)S(1)}, u32[]{:S(2)}, u32[]{:S(2)}) collective-permute-start(bf16[64,1024]{1,0:T(8,128)(2,1)S(1)} %add_convert_fusion.1), channel_id=1, source_target_pairs={{0,2},{1,3},{2,0},{3,1},{4,6},{5,7},{6,4},{7,5},{8,10},{9,11},{10,... | collective-permute-start | bytes 393224 | tf_op jit(solution)/shard_map/ppermute | solution.py:84
  123.5 2.0 %add_bitcast_fusion = f32[32,256,64]{1,2,0:T(8,128)} fusion(f32[256,32,64]{0,2,1:T(8,128)S(1)} %fusion.17, bf16[32,32,64]{2,1,0:T(8,128)(2,1)S(1)} %get-tuple-element.31, s32[32]{0:T(128)S(1)} %add.186, s32[256]{0:T(256)S(1)} %iota_add_fusion.1), kind=kOutput, calls=%fused_computation.20 | convolution fusion | flops 34201600 | bytes 4326528 | tf_op jit(solution)/shard_map/krc,xk->rxc/dot_general | solution.py:192
  125.5 3.8 %copy.38 = f32[32,256,64]{2,1,0:T(8,128)} copy(f32[32,256,64]{1,2,0:T(8,128)} %add_bitcast_fusion) | data formatting | bytes 4194304 | tf_op jit(solution)/shard_map/add | solution.py:195
  129.2 2.9 %reshape.106 = f32[2,16,16384]{2,1,0:T(8,128)S(1)} reshape(f32[32,256,64]{2,1,0:T(8,128)} %copy.38) | data formatting | bytes 4194304 | tf_op jit(solution)/shard_map/reshape | solution.py:278
  132.8 9.6 %shard_map.96.refs_2_ = f32[2,16,16384]{2,1,0:T(8,128)} custom-call(bf16[2,18,16640]{2,1,0:T(8,128)(2,1)} %copy-done.2, f32[27,8,128]{2,1,0:T(8,128)} %broadcast_in_dim.36.refs_1_.refs_3_), custom_call_target="tpu_custom_call" | custom-call | tf_op jit(solution)/shard_map/pallas_call | solution.py:156
  142.4 3.8 %collective-permute-done.24 = bf16[64,1024]{1,0:T(8,128)(2,1)S(1)} collective-permute-done((bf16[64,1024]{1,0:T(8,128)(2,1)S(1)}, bf16[64,1024]{1,0:T(8,128)(2,1)S(1)}, u32[]{:S(2)}, u32[]{:S(2)}) %collective-permute-start.24) | collective-permute-done | bytes 131104 | tf_op jit(solution)/shard_map/ppermute | solution.py:84
  148.1 7.1 %shard_map.97 = f32[2,16,16384]{2,1,0:T(8,128)} custom-call(bf16[1,18,16640]{2,1,0:T(8,128)(2,1)} %copy-done.9, bf16[1,18,16640]{2,1,0:T(8,128)(2,1)} %collective-permute-done.18.refs_1_, f32[2,16,16384]{2,1,0:T(8,128)} %shard_map.96.refs_2_, f32[27,8,128]{2,1,0:T(8,128)} %broadcast_in_dim.36.refs_1_.refs_3_), custom_call_target="tpu_custom_call" | custom-call | tf_op jit(solution)/shard_map/pallas_call | solution.py:156
  155.2 2.7 %add_convert_fusion = bf16[2,16,16384]{2,1,0:T(8,128)(2,1)} fusion(f32[2,16,16384]{2,1,0:T(8,128)} %shard_map.97, f32[2,16,16384]{2,1,0:T(8,128)S(1)} %reshape.106), kind=kLoop, calls=%fused_computation.19 | loop fusion | flops 1048576 | bytes 5242880 | tf_op jit(solution)/shard_map/convert_element_type | solution.py:278
  (109 shorter events, 19.5 us)
Async XLA Ops:
  0.6 64.3 %copy-start = (bf16[64,256]{1,0:T(8,128)(2,1)S(1)}, bf16[64,256]{1,0:T(8,128)(2,1)}, u32[]{:S(2)}) copy-start(bf16[64,256]{1,0:T(8,128)(2,1)} %param.9) | copy-start | bytes 98308
  4.8 12.0 %copy-start.6 = (bf16[2,16,16384]{2,1,0:T(8,128)(2,1)S(1)}, bf16[2,16,16384]{2,1,0:T(8,128)(2,1)}, u32[]{:S(2)}) copy-start(bf16[2,16,16384]{2,1,0:T(8,128)(2,1)} %param.7) | copy-start | bytes 3145732
  5.8 44.5 %collective-permute-start.2 = (f32[8,32,128]{2,0,1:T(8,128)}, f32[8,32,128]{2,0,1:T(8,128)}, u32[]{:S(2)}, u32[]{:S(2)}) collective-permute-start(f32[8,32,128]{2,0,1:T(8,128)} %get-tuple-element.28), channel_id=1, source_target_pairs={{0,24},{8,0},{16,8},{24,16},{1,25},{9,1},{17,9},{25,17},{2,26},{10... | collective-permute-start | bytes 393224 | tf_op jit(solution)/shard_map/ppermute | solution.py:73
  9.7 40.6 %collective-permute-start.1 = (f32[8,32,128]{2,0,1:T(8,128)}, f32[8,32,128]{2,0,1:T(8,128)}, u32[]{:S(2)}, u32[]{:S(2)}) collective-permute-start(f32[8,32,128]{2,0,1:T(8,128)} %get-tuple-element.27), channel_id=1, source_target_pairs={{0,16},{8,24},{16,0},{24,8},{1,17},{9,25},{17,1},{25,9},{2,18},{10... | collective-permute-start | bytes 393224 | tf_op jit(solution)/shard_map/ppermute | solution.py:73
  10.2 40.1 %collective-permute-start = (f32[8,32,128]{2,0,1:T(8,128)}, f32[8,32,128]{2,0,1:T(8,128)}, u32[]{:S(2)}, u32[]{:S(2)}) collective-permute-start(f32[8,32,128]{2,0,1:T(8,128)} %get-tuple-element.26), channel_id=1, source_target_pairs={{0,8},{8,16},{16,24},{24,0},{1,9},{9,17},{17,25},{25,1},{2,10},{10... | collective-permute-start | bytes 393224 | tf_op jit(solution)/shard_map/ppermute | solution.py:73
  11.5 5.3 %collective-permute-start.3 = (bf16[2,16,128]{2,1,0:T(8,128)(2,1)S(1)}, bf16[2,16,128]{2,1,0:T(8,128)(2,1)S(1)}, u32[]{:S(2)}, u32[]{:S(2)}) collective-permute-start(bf16[2,16,128]{2,1,0:T(8,128)(2,1)S(1)} %get-tuple-element.25), channel_id=1, source_target_pairs={{0,8},{8,16},{16,24},{24,0},{1,9},{9,17},{17,25},{25,1},{2,10},{10... | collective-permute-start | bytes 24584 | tf_op jit(solution)/shard_map/ppermute | solution.py:26
  13.9 3.7 %collective-permute-start.4 = (bf16[2,16,128]{2,1,0:T(8,128)(2,1)S(1)}, bf16[2,16,128]{2,1,0:T(8,128)(2,1)S(1)}, u32[]{:S(2)}, u32[]{:S(2)}) collective-permute-start(bf16[2,16,128]{2,1,0:T(8,128)(2,1)S(1)} %get-tuple-element.24), channel_id=1, source_target_pairs={{8,0},{16,8},{24,16},{0,24},{9,1},{17,9},{25,17},{1,25},{10,2},{18... | collective-permute-start | bytes 24584 | tf_op jit(solution)/shard_map/ppermute | solution.py:27
  17.5 1.0 copy-start.8
  18.7 1.4 collective-permute-start.5
  22.2 11.4 %copy-start.3 = (bf16[2,18,16640]{2,1,0:T(8,128)(2,1)}, bf16[2,18,16640]{2,1,0:T(8,128)(2,1)S(1)}, u32[]{:S(2)}) copy-start(bf16[2,18,16640]{2,1,0:T(8,128)(2,1)S(1)} %pad_maximum_fusion.refs_0_) | copy-start | bytes 3594244
  23.7 27.9 %collective-permute-start.6 = (bf16[1,18,16640]{2,1,0:T(8,128)(2,1)}, bf16[1,18,16640]{2,1,0:T(8,128)(2,1)}, u32[]{:S(2)}, u32[]{:S(2)}) collective-permute-start(bf16[1,18,16640]{2,1,0:T(8,128)(2,1)} %get-tuple-element.18), channel_id=1, source_target_pairs={{0,1},{1,2},{2,3},{4,5},{5,6},{6,7},{8,9},{9,10},{10,11},{12,13},{... | collective-permute-start | bytes 1797128 | tf_op jit(solution)/shard_map/ppermute | solution.py:103
  28.1 23.6 %collective-permute-start.7 = (bf16[1,18,16640]{2,1,0:T(8,128)(2,1)}, bf16[1,18,16640]{2,1,0:T(8,128)(2,1)}, u32[]{:S(2)}, u32[]{:S(2)}) collective-permute-start(bf16[1,18,16640]{2,1,0:T(8,128)(2,1)} %get-tuple-element.17), channel_id=1, source_target_pairs={{1,0},{2,1},{3,2},{5,4},{6,5},{7,6},{9,8},{10,9},{11,10},{13,12},{... | collective-permute-start | bytes 1797128 | tf_op jit(solution)/shard_map/ppermute | solution.py:104
  33.6 5.0 %copy-start.10 = (bf16[27,64]{1,0:T(8,128)(2,1)S(1)}, bf16[27,64]{1,0:T(8,128)(2,1)}, u32[]{:S(2)}) copy-start(bf16[27,64]{1,0:T(8,128)(2,1)} %param.8) | copy-start | bytes 10372
  58.4 11.1 %collective-permute-start.8 = (bf16[8,32,128]{2,1,0:T(8,128)(2,1)S(1)}, bf16[8,32,128]{2,1,0:T(8,128)(2,1)S(1)}, u32[]{:S(2)}, u32[]{:S(2)}) collective-permute-start(bf16[8,32,128]{2,1,0:T(8,128)(2,1)S(1)} %convolution_convert_fusion.2), channel_id=1, source_target_pairs={{0,8},{8,16},{16,24},{24,0},{1,9},{9,17},{17,25},{25,1},{2,10},{10... | collective-permute-start | bytes 196616 | tf_op jit(solution)/shard_map/ppermute | solution.py:62
  59.3 10.2 %collective-permute-start.9 = (bf16[8,32,128]{2,1,0:T(8,128)(2,1)S(1)}, bf16[8,32,128]{2,1,0:T(8,128)(2,1)S(1)}, u32[]{:S(2)}, u32[]{:S(2)}) collective-permute-start(bf16[8,32,128]{2,1,0:T(8,128)(2,1)S(1)} %convolution_convert_fusion.2), channel_id=1, source_target_pairs={{0,16},{8,24},{16,0},{24,8},{1,17},{9,25},{17,1},{25,9},{2,18},{10... | collective-permute-start | bytes 196616 | tf_op jit(solution)/shard_map/ppermute | solution.py:62
  60.7 8.9 %collective-permute-start.10 = (bf16[8,32,128]{2,1,0:T(8,128)(2,1)S(1)}, bf16[8,32,128]{2,1,0:T(8,128)(2,1)S(1)}, u32[]{:S(2)}, u32[]{:S(2)}) collective-permute-start(bf16[8,32,128]{2,1,0:T(8,128)(2,1)S(1)} %convolution_convert_fusion.2), channel_id=1, source_target_pairs={{0,24},{8,0},{16,8},{24,16},{1,25},{9,1},{17,9},{25,17},{2,26},{10... | collective-permute-start | bytes 196616 | tf_op jit(solution)/shard_map/ppermute | solution.py:62
  65.0 1.2 copy-start.11
  66.2 3.3 %copy-start.4 = (f32[8192,256]{1,0:T(8,128)}, f32[8192,256]{1,0:T(8,128)S(1)}, u32[]{:S(2)}) copy-start(f32[8192,256]{1,0:T(8,128)S(1)} %fusion.117) | copy-start | bytes 25165828
  69.5 1.6 %copy-start.5 = (f32[32,256,64]{1,2,0:T(8,128)S(1)}, f32[32,256,64]{1,2,0:T(8,128)}, u32[]{:S(2)}) copy-start(f32[32,256,64]{1,2,0:T(8,128)} %copy.30) | copy-start | bytes 6291460
  74.9 4.5 %copy-start.12 = (bf16[256,64]{0,1:T(8,128)(2,1)S(1)}, bf16[256,64]{0,1:T(8,128)(2,1)}, u32[]{:S(2)}) copy-start(bf16[256,64]{0,1:T(8,128)(2,1)} %param.10) | copy-start | bytes 98308
  75.9 21.4 %collective-permute-start.13 = (f32[8,32,128]{2,0,1:T(8,128)}, f32[8,32,128]{2,0,1:T(8,128)}, u32[]{:S(2)}, u32[]{:S(2)}) collective-permute-start(f32[8,32,128]{2,0,1:T(8,128)} %get-tuple-element.23), channel_id=1, source_target_pairs={{0,24},{8,0},{16,8},{24,16},{1,25},{9,1},{17,9},{25,17},{2,26},{10... | collective-permute-start | bytes 393224 | tf_op jit(solution)/shard_map/ppermute | solution.py:73
  76.7 20.5 %collective-permute-start.12 = (f32[8,32,128]{2,0,1:T(8,128)}, f32[8,32,128]{2,0,1:T(8,128)}, u32[]{:S(2)}, u32[]{:S(2)}) collective-permute-start(f32[8,32,128]{2,0,1:T(8,128)} %get-tuple-element.22), channel_id=1, source_target_pairs={{0,16},{8,24},{16,0},{24,8},{1,17},{9,25},{17,1},{25,9},{2,18},{10... | collective-permute-start | bytes 393224 | tf_op jit(solution)/shard_map/ppermute | solution.py:73
  78.1 19.2 %collective-permute-start.11 = (f32[8,32,128]{2,0,1:T(8,128)}, f32[8,32,128]{2,0,1:T(8,128)}, u32[]{:S(2)}, u32[]{:S(2)}) collective-permute-start(f32[8,32,128]{2,0,1:T(8,128)} %get-tuple-element.21), channel_id=1, source_target_pairs={{0,8},{8,16},{16,24},{24,0},{1,9},{9,17},{17,25},{25,1},{2,10},{10... | collective-permute-start | bytes 393224 | tf_op jit(solution)/shard_map/ppermute | solution.py:73
  97.2 2.1 %copy-start.7 = (bf16[2,16,16384]{2,1,0:T(8,128)(2,1)S(1)}, bf16[2,16,16384]{2,1,0:T(8,128)(2,1)}, u32[]{:S(2)}) copy-start(bf16[2,16,16384]{2,1,0:T(8,128)(2,1)} %reshape.105) | copy-start | bytes 3145732
  99.3 5.8 %collective-permute-start.14 = (bf16[2,16,128]{2,1,0:T(8,128)(2,1)S(1)}, bf16[2,16,128]{2,1,0:T(8,128)(2,1)S(1)}, u32[]{:S(2)}, u32[]{:S(2)}) collective-permute-start(bf16[2,16,128]{2,1,0:T(8,128)(2,1)S(1)} %get-tuple-element.20), channel_id=1, source_target_pairs={{0,8},{8,16},{16,24},{24,0},{1,9},{9,17},{17,25},{25,1},{2,10},{10... | collective-permute-start | bytes 24584 | tf_op jit(solution)/shard_map/ppermute | solution.py:26
  100.3 8.2 %collective-permute-start.19 = (bf16[8,32,128]{2,1,0:T(8,128)(2,1)S(1)}, bf16[8,32,128]{2,1,0:T(8,128)(2,1)S(1)}, u32[]{:S(2)}, u32[]{:S(2)}) collective-permute-start(bf16[8,32,128]{2,1,0:T(8,128)(2,1)S(1)} %convolution_convert_fusion.1), channel_id=1, source_target_pairs={{0,8},{8,16},{16,24},{24,0},{1,9},{9,17},{17,25},{25,1},{2,10},{10... | collective-permute-start | bytes 196616 | tf_op jit(solution)/shard_map/ppermute | solution.py:62
  101.4 7.1 %collective-permute-start.20 = (bf16[8,32,128]{2,1,0:T(8,128)(2,1)S(1)}, bf16[8,32,128]{2,1,0:T(8,128)(2,1)S(1)}, u32[]{:S(2)}, u32[]{:S(2)}) collective-permute-start(bf16[8,32,128]{2,1,0:T(8,128)(2,1)S(1)} %convolution_convert_fusion.1), channel_id=1, source_target_pairs={{0,16},{8,24},{16,0},{24,8},{1,17},{9,25},{17,1},{25,9},{2,18},{10... | collective-permute-start | bytes 196616 | tf_op jit(solution)/shard_map/ppermute | solution.py:62
  102.9 5.7 %collective-permute-start.21 = (bf16[8,32,128]{2,1,0:T(8,128)(2,1)S(1)}, bf16[8,32,128]{2,1,0:T(8,128)(2,1)S(1)}, u32[]{:S(2)}, u32[]{:S(2)}) collective-permute-start(bf16[8,32,128]{2,1,0:T(8,128)(2,1)S(1)} %convolution_convert_fusion.1), channel_id=1, source_target_pairs={{0,24},{8,0},{16,8},{24,16},{1,25},{9,1},{17,9},{25,17},{2,26},{10... | collective-permute-start | bytes 196616 | tf_op jit(solution)/shard_map/ppermute | solution.py:62
  104.6 3.7 %collective-permute-start.15 = (bf16[2,16,128]{2,1,0:T(8,128)(2,1)S(1)}, bf16[2,16,128]{2,1,0:T(8,128)(2,1)S(1)}, u32[]{:S(2)}, u32[]{:S(2)}) collective-permute-start(bf16[2,16,128]{2,1,0:T(8,128)(2,1)S(1)} %get-tuple-element.19), channel_id=1, source_target_pairs={{8,0},{16,8},{24,16},{0,24},{9,1},{17,9},{25,17},{1,25},{10,2},{18... | collective-permute-start | bytes 24584 | tf_op jit(solution)/shard_map/ppermute | solution.py:27
  105.1 5.6 %collective-permute-start.22 = (bf16[64,1024]{1,0:T(8,128)(2,1)S(1)}, bf16[64,1024]{1,0:T(8,128)(2,1)S(1)}, u32[]{:S(2)}, u32[]{:S(2)}) collective-permute-start(bf16[64,1024]{1,0:T(8,128)(2,1)S(1)} %convert_element_type.143), channel_id=1, source_target_pairs={{0,4},{4,0},{1,5},{5,1},{2,6},{6,2},{3,7},{7,3},{8,12},{12,8},{9,1... | collective-permute-start | bytes 393224 | tf_op jit(solution)/shard_map/ppermute | solution.py:84
  108.4 1.4 collective-permute-start.16
  110.7 14.8 %copy-start.2 = (bf16[2,18,16640]{2,1,0:T(8,128)(2,1)}, bf16[2,18,16640]{2,1,0:T(8,128)(2,1)S(1)}, u32[]{:S(2)}) copy-start(bf16[2,18,16640]{2,1,0:T(8,128)(2,1)S(1)} %pad_maximum_fusion.1.refs_0_) | copy-start | bytes 3594244
  110.8 7.8 %collective-permute-start.23 = (bf16[64,1024]{1,0:T(8,128)(2,1)S(1)}, bf16[64,1024]{1,0:T(8,128)(2,1)S(1)}, u32[]{:S(2)}, u32[]{:S(2)}) collective-permute-start(bf16[64,1024]{1,0:T(8,128)(2,1)S(1)} %add_convert_fusion.2), channel_id=1, source_target_pairs={{0,1},{1,0},{2,3},{3,2},{4,5},{5,4},{6,7},{7,6},{8,9},{9,8},{10,11... | collective-permute-start | bytes 393224 | tf_op jit(solution)/shard_map/ppermute | solution.py:84
  114.7 32.5 %collective-permute-start.17 = (bf16[1,18,16640]{2,1,0:T(8,128)(2,1)}, bf16[1,18,16640]{2,1,0:T(8,128)(2,1)S(1)}, u32[]{:S(2)}, u32[]{:S(2)}) collective-permute-start(bf16[1,18,16640]{2,1,0:T(8,128)(2,1)} %get-tuple-element.16), channel_id=1, source_target_pairs={{0,1},{1,2},{2,3},{4,5},{5,6},{6,7},{8,9},{9,10},{10,11},{12,13},{... | collective-permute-start | bytes 1797128 | tf_op jit(solution)/shard_map/ppermute | solution.py:103
  117.0 30.2 %collective-permute-start.18 = (bf16[1,18,16640]{2,1,0:T(8,128)(2,1)}, bf16[1,18,16640]{2,1,0:T(8,128)(2,1)}, u32[]{:S(2)}, u32[]{:S(2)}) collective-permute-start(bf16[1,18,16640]{2,1,0:T(8,128)(2,1)} %get-tuple-element.15), channel_id=1, source_target_pairs={{1,0},{2,1},{3,2},{5,4},{6,5},{7,6},{9,8},{10,9},{11,10},{13,12},{... | collective-permute-start | bytes 1797128 | tf_op jit(solution)/shard_map/ppermute | solution.py:104
  118.6 27.7 %collective-permute-start.24 = (bf16[64,1024]{1,0:T(8,128)(2,1)S(1)}, bf16[64,1024]{1,0:T(8,128)(2,1)S(1)}, u32[]{:S(2)}, u32[]{:S(2)}) collective-permute-start(bf16[64,1024]{1,0:T(8,128)(2,1)S(1)} %add_convert_fusion.1), channel_id=1, source_target_pairs={{0,2},{1,3},{2,0},{3,1},{4,6},{5,7},{6,4},{7,5},{8,10},{9,11},{10,... | collective-permute-start | bytes 393224 | tf_op jit(solution)/shard_map/ppermute | solution.py:84
  147.2 0.9 copy-start.9
  148.1 9.8 %copy-start.1 = (bf16[64,256]{1,0:T(8,128)(2,1)S(1)}, bf16[64,256]{1,0:T(8,128)(2,1)}, u32[]{:S(2)}) copy-start(bf16[64,256]{1,0:T(8,128)(2,1)} %param.9) | copy-start | bytes 98308

commit v13 on v12

--- a/solution.py
+++ b/solution.py
@@ -252,7 +252,8 @@
     result, slopes = gelu_parts(local_branch + spectral)
     output = result.astype(jnp.bfloat16).reshape(planes, y_cells, merged)
     grad_pre = (
-        cotangent.reshape(row_count, x_cells, channels).astype(jnp.float32) * slopes
+        lax.optimization_barrier(cotangent.reshape(row_count, x_cells, channels)).astype(jnp.float32)
+        * slopes
     ).astype(jnp.bfloat16)
     hidden_grad = jnp.dot(
         grad_pre.reshape(row_count * x_cells, channels),

time: 159 us -> 157 us (0.987)
  local copies, waits for them, and re-layouts: 39.8 us -> 38 us
    convert_element_type x2 -> x0, local copies, waits for them, and re-layouts: 8.07 us -> none  [per_device(): cotangent.reshape(row_count, x_cells, channels).astype(jnp.float32) * slopes]
    reshape x0 -> x1, local copies, waits for them, and re-layouts: none -> 4.05 us  [per_device(): cotangent.reshape(row_count, x_cells, channels)]
    optimization_barrier x0 -> x1, local copies, waits for them, and re-layouts: none -> 2.69 us  [per_device(): lax.optimization_barrier(cotangent.reshape(row_count, x_cells, channels))]
where the time goes in v13:
time: 157 us; the launch traced here: 156 us
  local copies, waits for them, and re-layouts  38 us (24%)
  starting transfers between devices  37.8 us (24%)
  Pallas kernels  33 us (21%)
  matrix products  21.8 us (14%)
  other arithmetic  13.1 us (8%)
  waiting for transfers between devices  11.4 us (7%)
    pallas_call x4, Pallas kernels, stencil_call(): pl.pallas_call(kernel, out_shape=jax.ShapeDtypeStruct((len(plan), y_cells...  33 us
    dot_general x1, matrix products, per_device(): jnp.dot(grad_hidden, expand_weight.T, preferred_element_type=jnp.float32)  8.79 us
    ppermute x6, starting transfers between devices, ring_reduce_scatter(): lax.ppermute(piece, axis, [(i, (i + shift) % size) for i in range(size)])  8.46 us
    ppermute x6, starting transfers between devices, ring_gather(): lax.ppermute(block, axis, [(i, (i + shift) % size) for i in range(size)])  7.79 us
    ppermute x3, starting transfers between devices, butterfly_sum(): lax.ppermute(value, axis, [(i, i ^ step) for i in range(size)])  7.71 us
    ppermute x2, starting transfers between devices, spatial_rims(): below = lax.ppermute(inner[-1:], 'gz', up)  6.65 us
    dot_general x2, matrix products, share_inverse(): jnp.einsum('krc,xk->rxc', segment[:, :, :channels], cos_table, preferred_...  4.64 us
    reshape x1, local copies, waits for them, and re-layouts, per_device(): cotangent.reshape(row_count, x_cells, channels)  4.05 us
  transfers between devices with their start and end apart: 25, of which 6 were waited for; matrix products, arithmetic and copies ran while one was open for 35% of the time, Pallas kernels for 12%

profile of v13, /device:TPU:0, one launch (start us, length us, event | category | flops | bytes accessed | tf_op | source)
XLA Modules:
  0.0 156.3 jit_solution(5630135771314626042)
XLA Ops:
  0.7 3.0 %reshape.100 = bf16[32,256,64]{2,1,0:T(8,128)(2,1)S(1)} reshape(bf16[2,16,16384]{2,1,0:T(8,128)(2,1)} %param.7) | data formatting | bytes 2097152 | tf_op jit(solution)/shard_map/reshape | solution.py:235
  5.8 3.9 %collective-permute-start.2 = (f32[8,32,128]{2,0,1:T(8,128)}, f32[8,32,128]{2,0,1:T(8,128)}, u32[]{:S(2)}, u32[]{:S(2)}) collective-permute-start(f32[8,32,128]{2,0,1:T(8,128)} %get-tuple-element.28), channel_id=1, source_target_pairs={{0,24},{8,0},{16,8},{24,16},{1,25},{9,1},{17,9},{25,17},{2,26},{10... | collective-permute-start | bytes 393224 | tf_op jit(solution)/shard_map/ppermute | solution.py:73
  11.5 2.4 %collective-permute-start.3 = (bf16[2,16,128]{2,1,0:T(8,128)(2,1)S(1)}, bf16[2,16,128]{2,1,0:T(8,128)(2,1)S(1)}, u32[]{:S(2)}, u32[]{:S(2)}) collective-permute-start(bf16[2,16,128]{2,1,0:T(8,128)(2,1)S(1)} %get-tuple-element.25), channel_id=1, source_target_pairs={{0,8},{8,16},{16,24},{24,0},{1,9},{9,17},{17,25},{25,1},{2,10},{10... | collective-permute-start | bytes 24584 | tf_op jit(solution)/shard_map/ppermute | solution.py:26
  14.4 2.4 %collective-permute-done.3 = bf16[2,16,128]{2,1,0:T(8,128)(2,1)S(1)} collective-permute-done((bf16[2,16,128]{2,1,0:T(8,128)(2,1)S(1)}, bf16[2,16,128]{2,1,0:T(8,128)(2,1)S(1)}, u32[]{:S(2)}, u32[]{:S(2)}) %collective-permute-start.3) | collective-permute-done | bytes 8224 | tf_op jit(solution)/shard_map/ppermute | solution.py:26
  17.5 1.0 copy-done.7
  19.0 1.2 collective-permute-done.5
  20.4 1.8 %pad_maximum_fusion.refs_0_ = bf16[2,18,16640]{2,1,0:T(8,128)(2,1)S(1)} fusion(bf16[2,1,16640]{2,1,0:T(2,128)(2,1)S(1)} %get-tuple-element.38, bf16[2,16,16640]{2,1,0:T(8,128)(2,1)} %copy-done.7, bf16[2,1,16640]{2,1,0:T(2,128)(2,1)S(1)} %get-tuple-element.37), kind=kLoop, calls=%fused_computation.23 | loop fusion | flops 3594240 | bytes 2396160 | tf_op jit(solution)/shard_map/concatenate | solution.py:28
  22.2 1.4 fusion.112
  23.6 4.4 %collective-permute-start.6 = (bf16[1,18,16640]{2,1,0:T(8,128)(2,1)}, bf16[1,18,16640]{2,1,0:T(8,128)(2,1)}, u32[]{:S(2)}, u32[]{:S(2)}) collective-permute-start(bf16[1,18,16640]{2,1,0:T(8,128)(2,1)} %get-tuple-element.18), channel_id=1, source_target_pairs={{0,1},{1,2},{2,3},{4,5},{5,6},{6,7},{8,9},{9,10},{10,11},{12,13},{... | collective-permute-start | bytes 1797128 | tf_op jit(solution)/shard_map/ppermute | solution.py:103
  28.0 1.3 collective-permute-start.7
  29.3 4.0 %reshape.104 = bf16[32,256,64]{2,1,0:T(8,128)(2,1)} reshape(bf16[2,16,16384]{2,1,0:T(8,128)(2,1)} %param.13) | data formatting | bytes 2097152 | tf_op jit(solution)/shard_map/reshape | solution.py:255
  33.4 2.7 %copy.30 = bf16[32,256,64]{1,2,0:T(8,128)(2,1)} copy(bf16[32,256,64]{2,1,0:T(8,128)(2,1)} %reshape.104) | data formatting | bytes 2097152 | tf_op jit(solution)/shard_map/optimization_barrier | solution.py:255
  36.0 1.2 neg.10
  37.5 1.2 fusion.13
  39.3 9.6 %shard_map.94.refs_2_ = f32[2,16,16384]{2,1,0:T(8,128)} custom-call(bf16[2,18,16640]{2,1,0:T(8,128)(2,1)} %copy-done.3, f32[27,8,128]{2,1,0:T(8,128)} %broadcast_in_dim.18.refs_1_.refs_3_), custom_call_target="tpu_custom_call" | custom-call | tf_op jit(solution)/shard_map/pallas_call | solution.py:156
  48.9 1.2 fusion.36
  50.2 6.8 %shard_map.95 = bf16[2,16,16384]{2,1,0:T(8,128)(2,1)} custom-call(bf16[1,18,16640]{2,1,0:T(8,128)(2,1)} %collective-permute-done.6.refs_0_, bf16[1,18,16640]{2,1,0:T(8,128)(2,1)} %collective-permute-done.7.refs_1_, f32[2,16,16384]{2,1,0:T(8,128)} %shard_map.94.refs_2_, f32[27,8,128]{2,1,0:T(8,128)} %broadcast_in_dim.18.refs_1_.refs_3_), custom_call_target="tpu_custom_call" | custom-call | tf_op jit(solution)/shard_map/pallas_call | solution.py:156
  57.9 1.4 collective-permute-start.9
  59.3 1.2 collective-permute-start.10
  60.5 3.0 %reshape.101 = bf16[8192,64]{1,0:T(8,128)(2,1)S(1)} reshape(bf16[2,16,16384]{2,1,0:T(8,128)(2,1)} %shard_map.95) | data formatting | bytes 2097152 | tf_op jit(solution)/shard_map/reshape | solution.py:244
  63.6 1.2 fusion.117
  64.8 2.8 %fusion.5 = f32[8192,64]{0,1:T(8,128)S(1)} fusion(bf16[256,64]{0,1:T(8,128)(2,1)S(1)} %copy-done.11, f32[8192,256]{1,0:T(8,128)S(1)} %fusion.117), kind=kOutput, calls=%fused_computation.10 | convolution fusion | flops 278921216 | bytes 10518528 | tf_op jit(solution)/shard_map/dot_general | solution.py:247
  69.3 2.7 %fusion.11 = (bf16[32,256,64]{1,2,0:T(8,128)(2,1)S(1)}, bf16[32,256,64]{1,2,0:T(8,128)(2,1)}) fusion(bf16[32,256,64]{1,2,0:T(8,128)(2,1)S(1)} %copy-done.8, f32[256,32,64]{0,2,1:T(8,128)S(1)} %fusion.20, bf16[32,32,64]{2,1,0:T(8,128)(2,1)S(1)} %get-tuple-element.33, f32[32]{0:T(128)S(1)} %get-tuple-element.39, s32[32]{0:T(128)S(1)} %add.186, ...), kind=kOutput, calls=%fused_computation.17 | convolution fusion | flops 41566208 | bytes 7472384 | tf_op jit(solution)/shard_map/krc,xk->rxc/dot_general | solution.py:192
  75.1 1.4 collective-permute-start.12
  76.4 1.2 collective-permute-start.11
  77.7 8.8 %convolution_convert_fusion = bf16[8192,64]{0,1:T(8,128)(2,1)} fusion(bf16[64,256]{1,0:T(8,128)(2,1)S(1)} %copy-done, bf16[8192,64]{0,1:T(8,128)(2,1)S(1)} %bitcast.54, bf16[256,64]{0,1:T(8,128)(2,1)S(1)} %copy-done.12, f32[8192,256]{1,0:T(8,128)} %copy-done.4), kind=kOutput, calls=%fused_computation.3 | convolution fusion | flops 558366720 | bytes 10551296 | tf_op jit(solution)/shard_map/dot_general | solution.py:264
  86.5 2.0 %copy.29 = bf16[32,256,64]{2,1,0:T(8,128)(2,1)S(1)} copy(bf16[32,256,64]{1,2,0:T(8,128)(2,1)} %get-tuple-element.14) | data formatting | bytes 2097152 | tf_op jit(solution)/shard_map/convert_element_type | solution.py:253
  88.5 2.5 %reshape.103 = bf16[2,16,16384]{2,1,0:T(8,128)(2,1)} reshape(bf16[32,256,64]{2,1,0:T(8,128)(2,1)S(1)} %copy.29) | data formatting | bytes 2097152 | tf_op jit(solution)/shard_map/reshape | solution.py:253
  91.0 2.0 %copy.35 = bf16[8192,64]{1,0:T(8,128)(2,1)S(1)} copy(bf16[8192,64]{0,1:T(8,128)(2,1)} %convolution_convert_fusion) | data formatting | bytes 2097152 | tf_op jit(solution)/shard_map/convert_element_type | solution.py:264
  93.1 2.5 %reshape.106 = bf16[2,16,16384]{2,1,0:T(8,128)(2,1)} reshape(bf16[8192,64]{1,0:T(8,128)(2,1)S(1)} %copy.35) | data formatting | bytes 2097152 | tf_op jit(solution)/shard_map/reshape | solution.py:267
  95.6 1.2 fusion.28
  97.6 1.0 collective-permute-start.14
  98.6 1.2 collective-permute-start.19
  99.7 1.4 collective-permute-start.20
  101.2 1.7 %collective-permute-start.21 = (bf16[8,32,128]{2,1,0:T(8,128)(2,1)S(1)}, bf16[8,32,128]{2,1,0:T(8,128)(2,1)S(1)}, u32[]{:S(2)}, u32[]{:S(2)}) collective-permute-start(bf16[8,32,128]{2,1,0:T(8,128)(2,1)S(1)} %convolution_convert_fusion.1), channel_id=1, source_target_pairs={{0,24},{8,0},{16,8},{24,16},{1,25},{9,1},{17,9},{25,17},{2,26},{10... | collective-permute-start | bytes 196616 | tf_op jit(solution)/shard_map/ppermute | solution.py:62
  103.6 2.9 %collective-permute-done.15 = bf16[2,16,128]{2,1,0:T(8,128)(2,1)S(1)} collective-permute-done((bf16[2,16,128]{2,1,0:T(8,128)(2,1)S(1)}, bf16[2,16,128]{2,1,0:T(8,128)(2,1)S(1)}, u32[]{:S(2)}, u32[]{:S(2)}) %collective-permute-start.15) | collective-permute-done | bytes 8224 | tf_op jit(solution)/shard_map/ppermute | solution.py:27
  109.1 2.7 %collective-permute-start.23 = (bf16[64,1024]{1,0:T(8,128)(2,1)S(1)}, bf16[64,1024]{1,0:T(8,128)(2,1)S(1)}, u32[]{:S(2)}, u32[]{:S(2)}) collective-permute-start(bf16[64,1024]{1,0:T(8,128)(2,1)S(1)} %add_convert_fusion.2), channel_id=1, source_target_pairs={{0,1},{1,0},{2,3},{3,2},{4,5},{5,4},{6,7},{7,6},{8,9},{9,8},{10,11... | collective-permute-start | bytes 393224 | tf_op jit(solution)/shard_map/ppermute | solution.py:84
  111.8 1.3 fusion.111
  113.0 2.3 %collective-permute-start.17 = (bf16[1,18,16640]{2,1,0:T(8,128)(2,1)}, bf16[1,18,16640]{2,1,0:T(8,128)(2,1)S(1)}, u32[]{:S(2)}, u32[]{:S(2)}) collective-permute-start(bf16[1,18,16640]{2,1,0:T(8,128)(2,1)} %get-tuple-element.16), channel_id=1, source_target_pairs={{0,1},{1,2},{2,3},{4,5},{5,6},{6,7},{8,9},{9,10},{10,11},{12,13},{... | collective-permute-start | bytes 1797128 | tf_op jit(solution)/shard_map/ppermute | solution.py:103
  115.3 1.5 collective-permute-start.18
  116.9 4.9 %collective-permute-start.24 = (bf16[64,1024]{1,0:T(8,128)(2,1)S(1)}, bf16[64,1024]{1,0:T(8,128)(2,1)S(1)}, u32[]{:S(2)}, u32[]{:S(2)}) collective-permute-start(bf16[64,1024]{1,0:T(8,128)(2,1)S(1)} %add_convert_fusion.1), channel_id=1, source_target_pairs={{0,2},{1,3},{2,0},{3,1},{4,6},{5,7},{6,4},{7,5},{8,10},{9,11},{10,... | collective-permute-start | bytes 393224 | tf_op jit(solution)/shard_map/ppermute | solution.py:84
  121.8 2.0 %add_bitcast_fusion = f32[32,256,64]{1,2,0:T(8,128)} fusion(f32[256,32,64]{0,2,1:T(8,128)S(1)} %fusion.17, bf16[32,32,64]{2,1,0:T(8,128)(2,1)S(1)} %get-tuple-element.31, s32[32]{0:T(128)S(1)} %add.186, s32[256]{0:T(256)S(1)} %iota_add_fusion.1), kind=kOutput, calls=%fused_computation.20 | convolution fusion | flops 34201600 | bytes 4326528 | tf_op jit(solution)/shard_map/krc,xk->rxc/dot_general | solution.py:192
  123.8 3.8 %copy.38 = f32[32,256,64]{2,1,0:T(8,128)} copy(f32[32,256,64]{1,2,0:T(8,128)} %add_bitcast_fusion) | data formatting | bytes 4194304 | tf_op jit(solution)/shard_map/add | solution.py:195
  127.6 2.9 %reshape.107 = f32[2,16,16384]{2,1,0:T(8,128)S(1)} reshape(f32[32,256,64]{2,1,0:T(8,128)} %copy.38) | data formatting | bytes 4194304 | tf_op jit(solution)/shard_map/reshape | solution.py:279
  131.2 9.6 %shard_map.96.refs_2_ = f32[2,16,16384]{2,1,0:T(8,128)} custom-call(bf16[2,18,16640]{2,1,0:T(8,128)(2,1)} %copy-done.2, f32[27,8,128]{2,1,0:T(8,128)} %broadcast_in_dim.36.refs_1_.refs_3_), custom_call_target="tpu_custom_call" | custom-call | tf_op jit(solution)/shard_map/pallas_call | solution.py:156
  140.7 3.8 %collective-permute-done.24 = bf16[64,1024]{1,0:T(8,128)(2,1)S(1)} collective-permute-done((bf16[64,1024]{1,0:T(8,128)(2,1)S(1)}, bf16[64,1024]{1,0:T(8,128)(2,1)S(1)}, u32[]{:S(2)}, u32[]{:S(2)}) %collective-permute-start.24) | collective-permute-done | bytes 131104 | tf_op jit(solution)/shard_map/ppermute | solution.py:84
  146.4 7.1 %shard_map.97 = f32[2,16,16384]{2,1,0:T(8,128)} custom-call(bf16[1,18,16640]{2,1,0:T(8,128)(2,1)} %copy-done.9, bf16[1,18,16640]{2,1,0:T(8,128)(2,1)} %collective-permute-done.18.refs_1_, f32[2,16,16384]{2,1,0:T(8,128)} %shard_map.96.refs_2_, f32[27,8,128]{2,1,0:T(8,128)} %broadcast_in_dim.36.refs_1_.refs_3_), custom_call_target="tpu_custom_call" | custom-call | tf_op jit(solution)/shard_map/pallas_call | solution.py:156
  153.5 2.7 %add_convert_fusion = bf16[2,16,16384]{2,1,0:T(8,128)(2,1)} fusion(f32[2,16,16384]{2,1,0:T(8,128)} %shard_map.97, f32[2,16,16384]{2,1,0:T(8,128)S(1)} %reshape.107), kind=kLoop, calls=%fused_computation.19 | loop fusion | flops 1048576 | bytes 5242880 | tf_op jit(solution)/shard_map/convert_element_type | solution.py:279
  (109 shorter events, 19.1 us)
Async XLA Ops:
  0.6 62.9 %copy-start = (bf16[64,256]{1,0:T(8,128)(2,1)S(1)}, bf16[64,256]{1,0:T(8,128)(2,1)}, u32[]{:S(2)}) copy-start(bf16[64,256]{1,0:T(8,128)(2,1)} %param.9) | copy-start | bytes 98308
  4.8 12.0 %copy-start.5 = (bf16[2,16,16384]{2,1,0:T(8,128)(2,1)S(1)}, bf16[2,16,16384]{2,1,0:T(8,128)(2,1)}, u32[]{:S(2)}) copy-start(bf16[2,16,16384]{2,1,0:T(8,128)(2,1)} %param.7) | copy-start | bytes 3145732
  5.8 43.1 %collective-permute-start.2 = (f32[8,32,128]{2,0,1:T(8,128)}, f32[8,32,128]{2,0,1:T(8,128)}, u32[]{:S(2)}, u32[]{:S(2)}) collective-permute-start(f32[8,32,128]{2,0,1:T(8,128)} %get-tuple-element.28), channel_id=1, source_target_pairs={{0,24},{8,0},{16,8},{24,16},{1,25},{9,1},{17,9},{25,17},{2,26},{10... | collective-permute-start | bytes 393224 | tf_op jit(solution)/shard_map/ppermute | solution.py:73
  9.6 39.2 %collective-permute-start.1 = (f32[8,32,128]{2,0,1:T(8,128)}, f32[8,32,128]{2,0,1:T(8,128)}, u32[]{:S(2)}, u32[]{:S(2)}) collective-permute-start(f32[8,32,128]{2,0,1:T(8,128)} %get-tuple-element.27), channel_id=1, source_target_pairs={{0,16},{8,24},{16,0},{24,8},{1,17},{9,25},{17,1},{25,9},{2,18},{10... | collective-permute-start | bytes 393224 | tf_op jit(solution)/shard_map/ppermute | solution.py:73
  10.2 38.7 %collective-permute-start = (f32[8,32,128]{2,0,1:T(8,128)}, f32[8,32,128]{2,0,1:T(8,128)}, u32[]{:S(2)}, u32[]{:S(2)}) collective-permute-start(f32[8,32,128]{2,0,1:T(8,128)} %get-tuple-element.26), channel_id=1, source_target_pairs={{0,8},{8,16},{16,24},{24,0},{1,9},{9,17},{17,25},{25,1},{2,10},{10... | collective-permute-start | bytes 393224 | tf_op jit(solution)/shard_map/ppermute | solution.py:73
  11.5 5.3 %collective-permute-start.3 = (bf16[2,16,128]{2,1,0:T(8,128)(2,1)S(1)}, bf16[2,16,128]{2,1,0:T(8,128)(2,1)S(1)}, u32[]{:S(2)}, u32[]{:S(2)}) collective-permute-start(bf16[2,16,128]{2,1,0:T(8,128)(2,1)S(1)} %get-tuple-element.25), channel_id=1, source_target_pairs={{0,8},{8,16},{16,24},{24,0},{1,9},{9,17},{17,25},{25,1},{2,10},{10... | collective-permute-start | bytes 24584 | tf_op jit(solution)/shard_map/ppermute | solution.py:26
  13.9 3.7 %collective-permute-start.4 = (bf16[2,16,128]{2,1,0:T(8,128)(2,1)S(1)}, bf16[2,16,128]{2,1,0:T(8,128)(2,1)S(1)}, u32[]{:S(2)}, u32[]{:S(2)}) collective-permute-start(bf16[2,16,128]{2,1,0:T(8,128)(2,1)S(1)} %get-tuple-element.24), channel_id=1, source_target_pairs={{8,0},{16,8},{24,16},{0,24},{9,1},{17,9},{25,17},{1,25},{10,2},{18... | collective-permute-start | bytes 24584 | tf_op jit(solution)/shard_map/ppermute | solution.py:27
  17.5 1.0 copy-start.7
  18.7 1.4 collective-permute-start.5
  22.2 11.1 %copy-start.3 = (bf16[2,18,16640]{2,1,0:T(8,128)(2,1)}, bf16[2,18,16640]{2,1,0:T(8,128)(2,1)S(1)}, u32[]{:S(2)}) copy-start(bf16[2,18,16640]{2,1,0:T(8,128)(2,1)S(1)} %pad_maximum_fusion.refs_0_) | copy-start | bytes 3594244
  23.6 26.6 %collective-permute-start.6 = (bf16[1,18,16640]{2,1,0:T(8,128)(2,1)}, bf16[1,18,16640]{2,1,0:T(8,128)(2,1)}, u32[]{:S(2)}, u32[]{:S(2)}) collective-permute-start(bf16[1,18,16640]{2,1,0:T(8,128)(2,1)} %get-tuple-element.18), channel_id=1, source_target_pairs={{0,1},{1,2},{2,3},{4,5},{5,6},{6,7},{8,9},{9,10},{10,11},{12,13},{... | collective-permute-start | bytes 1797128 | tf_op jit(solution)/shard_map/ppermute | solution.py:103
  28.0 22.2 %collective-permute-start.7 = (bf16[1,18,16640]{2,1,0:T(8,128)(2,1)}, bf16[1,18,16640]{2,1,0:T(8,128)(2,1)}, u32[]{:S(2)}, u32[]{:S(2)}) collective-permute-start(bf16[1,18,16640]{2,1,0:T(8,128)(2,1)} %get-tuple-element.17), channel_id=1, source_target_pairs={{1,0},{2,1},{3,2},{5,4},{6,5},{7,6},{9,8},{10,9},{11,10},{13,12},{... | collective-permute-start | bytes 1797128 | tf_op jit(solution)/shard_map/ppermute | solution.py:104
  33.3 3.9 %copy-start.10 = (bf16[27,64]{1,0:T(8,128)(2,1)S(1)}, bf16[27,64]{1,0:T(8,128)(2,1)}, u32[]{:S(2)}) copy-start(bf16[27,64]{1,0:T(8,128)(2,1)} %param.8) | copy-start | bytes 10372
  57.0 11.1 %collective-permute-start.8 = (bf16[8,32,128]{2,1,0:T(8,128)(2,1)S(1)}, bf16[8,32,128]{2,1,0:T(8,128)(2,1)S(1)}, u32[]{:S(2)}, u32[]{:S(2)}) collective-permute-start(bf16[8,32,128]{2,1,0:T(8,128)(2,1)S(1)} %convolution_convert_fusion.2), channel_id=1, source_target_pairs={{0,8},{8,16},{16,24},{24,0},{1,9},{9,17},{17,25},{25,1},{2,10},{10... | collective-permute-start | bytes 196616 | tf_op jit(solution)/shard_map/ppermute | solution.py:62
  57.9 10.2 %collective-permute-start.9 = (bf16[8,32,128]{2,1,0:T(8,128)(2,1)S(1)}, bf16[8,32,128]{2,1,0:T(8,128)(2,1)S(1)}, u32[]{:S(2)}, u32[]{:S(2)}) collective-permute-start(bf16[8,32,128]{2,1,0:T(8,128)(2,1)S(1)} %convolution_convert_fusion.2), channel_id=1, source_target_pairs={{0,16},{8,24},{16,0},{24,8},{1,17},{9,25},{17,1},{25,9},{2,18},{10... | collective-permute-start | bytes 196616 | tf_op jit(solution)/shard_map/ppermute | solution.py:62
  59.3 8.9 %collective-permute-start.10 = (bf16[8,32,128]{2,1,0:T(8,128)(2,1)S(1)}, bf16[8,32,128]{2,1,0:T(8,128)(2,1)S(1)}, u32[]{:S(2)}, u32[]{:S(2)}) collective-permute-start(bf16[8,32,128]{2,1,0:T(8,128)(2,1)S(1)} %convolution_convert_fusion.2), channel_id=1, source_target_pairs={{0,24},{8,0},{16,8},{24,16},{1,25},{9,1},{17,9},{25,17},{2,26},{10... | collective-permute-start | bytes 196616 | tf_op jit(solution)/shard_map/ppermute | solution.py:62
  63.6 1.2 copy-start.11
  64.8 3.3 %copy-start.4 = (f32[8192,256]{1,0:T(8,128)}, f32[8192,256]{1,0:T(8,128)S(1)}, u32[]{:S(2)}) copy-start(f32[8192,256]{1,0:T(8,128)S(1)} %fusion.117) | copy-start | bytes 25165828
  68.1 1.2 copy-start.8
  73.3 4.5 %copy-start.12 = (bf16[256,64]{0,1:T(8,128)(2,1)S(1)}, bf16[256,64]{0,1:T(8,128)(2,1)}, u32[]{:S(2)}) copy-start(bf16[256,64]{0,1:T(8,128)(2,1)} %param.10) | copy-start | bytes 98308
  74.2 21.4 %collective-permute-start.13 = (f32[8,32,128]{2,0,1:T(8,128)}, f32[8,32,128]{2,0,1:T(8,128)}, u32[]{:S(2)}, u32[]{:S(2)}) collective-permute-start(f32[8,32,128]{2,0,1:T(8,128)} %get-tuple-element.23), channel_id=1, source_target_pairs={{0,24},{8,0},{16,8},{24,16},{1,25},{9,1},{17,9},{25,17},{2,26},{10... | collective-permute-start | bytes 393224 | tf_op jit(solution)/shard_map/ppermute | solution.py:73
  75.1 20.5 %collective-permute-start.12 = (f32[8,32,128]{2,0,1:T(8,128)}, f32[8,32,128]{2,0,1:T(8,128)}, u32[]{:S(2)}, u32[]{:S(2)}) collective-permute-start(f32[8,32,128]{2,0,1:T(8,128)} %get-tuple-element.22), channel_id=1, source_target_pairs={{0,16},{8,24},{16,0},{24,8},{1,17},{9,25},{17,1},{25,9},{2,18},{10... | collective-permute-start | bytes 393224 | tf_op jit(solution)/shard_map/ppermute | solution.py:73
  76.4 19.1 %collective-permute-start.11 = (f32[8,32,128]{2,0,1:T(8,128)}, f32[8,32,128]{2,0,1:T(8,128)}, u32[]{:S(2)}, u32[]{:S(2)}) collective-permute-start(f32[8,32,128]{2,0,1:T(8,128)} %get-tuple-element.21), channel_id=1, source_target_pairs={{0,8},{8,16},{16,24},{24,0},{1,9},{9,17},{17,25},{25,1},{2,10},{10... | collective-permute-start | bytes 393224 | tf_op jit(solution)/shard_map/ppermute | solution.py:73
  95.5 2.1 %copy-start.6 = (bf16[2,16,16384]{2,1,0:T(8,128)(2,1)S(1)}, bf16[2,16,16384]{2,1,0:T(8,128)(2,1)}, u32[]{:S(2)}) copy-start(bf16[2,16,16384]{2,1,0:T(8,128)(2,1)} %reshape.106) | copy-start | bytes 3145732
  97.6 5.8 %collective-permute-start.14 = (bf16[2,16,128]{2,1,0:T(8,128)(2,1)S(1)}, bf16[2,16,128]{2,1,0:T(8,128)(2,1)S(1)}, u32[]{:S(2)}, u32[]{:S(2)}) collective-permute-start(bf16[2,16,128]{2,1,0:T(8,128)(2,1)S(1)} %get-tuple-element.20), channel_id=1, source_target_pairs={{0,8},{8,16},{16,24},{24,0},{1,9},{9,17},{17,25},{25,1},{2,10},{10... | collective-permute-start | bytes 24584 | tf_op jit(solution)/shard_map/ppermute | solution.py:26
  98.6 8.2 %collective-permute-start.19 = (bf16[8,32,128]{2,1,0:T(8,128)(2,1)S(1)}, bf16[8,32,128]{2,1,0:T(8,128)(2,1)S(1)}, u32[]{:S(2)}, u32[]{:S(2)}) collective-permute-start(bf16[8,32,128]{2,1,0:T(8,128)(2,1)S(1)} %convolution_convert_fusion.1), channel_id=1, source_target_pairs={{0,8},{8,16},{16,24},{24,0},{1,9},{9,17},{17,25},{25,1},{2,10},{10... | collective-permute-start | bytes 196616 | tf_op jit(solution)/shard_map/ppermute | solution.py:62
  99.7 7.1 %collective-permute-start.20 = (bf16[8,32,128]{2,1,0:T(8,128)(2,1)S(1)}, bf16[8,32,128]{2,1,0:T(8,128)(2,1)S(1)}, u32[]{:S(2)}, u32[]{:S(2)}) collective-permute-start(bf16[8,32,128]{2,1,0:T(8,128)(2,1)S(1)} %convolution_convert_fusion.1), channel_id=1, source_target_pairs={{0,16},{8,24},{16,0},{24,8},{1,17},{9,25},{17,1},{25,9},{2,18},{10... | collective-permute-start | bytes 196616 | tf_op jit(solution)/shard_map/ppermute | solution.py:62
  101.2 5.7 %collective-permute-start.21 = (bf16[8,32,128]{2,1,0:T(8,128)(2,1)S(1)}, bf16[8,32,128]{2,1,0:T(8,128)(2,1)S(1)}, u32[]{:S(2)}, u32[]{:S(2)}) collective-permute-start(bf16[8,32,128]{2,1,0:T(8,128)(2,1)S(1)} %convolution_convert_fusion.1), channel_id=1, source_target_pairs={{0,24},{8,0},{16,8},{24,16},{1,25},{9,1},{17,9},{25,17},{2,26},{10... | collective-permute-start | bytes 196616 | tf_op jit(solution)/shard_map/ppermute | solution.py:62
  102.9 3.7 %collective-permute-start.15 = (bf16[2,16,128]{2,1,0:T(8,128)(2,1)S(1)}, bf16[2,16,128]{2,1,0:T(8,128)(2,1)S(1)}, u32[]{:S(2)}, u32[]{:S(2)}) collective-permute-start(bf16[2,16,128]{2,1,0:T(8,128)(2,1)S(1)} %get-tuple-element.19), channel_id=1, source_target_pairs={{8,0},{16,8},{24,16},{0,24},{9,1},{17,9},{25,17},{1,25},{10,2},{18... | collective-permute-start | bytes 24584 | tf_op jit(solution)/shard_map/ppermute | solution.py:27
  103.4 5.6 %collective-permute-start.22 = (bf16[64,1024]{1,0:T(8,128)(2,1)S(1)}, bf16[64,1024]{1,0:T(8,128)(2,1)S(1)}, u32[]{:S(2)}, u32[]{:S(2)}) collective-permute-start(bf16[64,1024]{1,0:T(8,128)(2,1)S(1)} %convert_element_type.139), channel_id=1, source_target_pairs={{0,4},{4,0},{1,5},{5,1},{2,6},{6,2},{3,7},{7,3},{8,12},{12,8},{9,1... | collective-permute-start | bytes 393224 | tf_op jit(solution)/shard_map/ppermute | solution.py:84
  106.7 1.4 collective-permute-start.16
  109.0 14.8 %copy-start.2 = (bf16[2,18,16640]{2,1,0:T(8,128)(2,1)}, bf16[2,18,16640]{2,1,0:T(8,128)(2,1)S(1)}, u32[]{:S(2)}) copy-start(bf16[2,18,16640]{2,1,0:T(8,128)(2,1)S(1)} %pad_maximum_fusion.1.refs_0_) | copy-start | bytes 3594244
  109.1 7.8 %collective-permute-start.23 = (bf16[64,1024]{1,0:T(8,128)(2,1)S(1)}, bf16[64,1024]{1,0:T(8,128)(2,1)S(1)}, u32[]{:S(2)}, u32[]{:S(2)}) collective-permute-start(bf16[64,1024]{1,0:T(8,128)(2,1)S(1)} %add_convert_fusion.2), channel_id=1, source_target_pairs={{0,1},{1,0},{2,3},{3,2},{4,5},{5,4},{6,7},{7,6},{8,9},{9,8},{10,11... | collective-permute-start | bytes 393224 | tf_op jit(solution)/shard_map/ppermute | solution.py:84
  113.0 32.5 %collective-permute-start.17 = (bf16[1,18,16640]{2,1,0:T(8,128)(2,1)}, bf16[1,18,16640]{2,1,0:T(8,128)(2,1)S(1)}, u32[]{:S(2)}, u32[]{:S(2)}) collective-permute-start(bf16[1,18,16640]{2,1,0:T(8,128)(2,1)} %get-tuple-element.16), channel_id=1, source_target_pairs={{0,1},{1,2},{2,3},{4,5},{5,6},{6,7},{8,9},{9,10},{10,11},{12,13},{... | collective-permute-start | bytes 1797128 | tf_op jit(solution)/shard_map/ppermute | solution.py:103
  115.3 30.2 %collective-permute-start.18 = (bf16[1,18,16640]{2,1,0:T(8,128)(2,1)}, bf16[1,18,16640]{2,1,0:T(8,128)(2,1)}, u32[]{:S(2)}, u32[]{:S(2)}) collective-permute-start(bf16[1,18,16640]{2,1,0:T(8,128)(2,1)} %get-tuple-element.15), channel_id=1, source_target_pairs={{1,0},{2,1},{3,2},{5,4},{6,5},{7,6},{9,8},{10,9},{11,10},{13,12},{... | collective-permute-start | bytes 1797128 | tf_op jit(solution)/shard_map/ppermute | solution.py:104
  116.9 27.7 %collective-permute-start.24 = (bf16[64,1024]{1,0:T(8,128)(2,1)S(1)}, bf16[64,1024]{1,0:T(8,128)(2,1)S(1)}, u32[]{:S(2)}, u32[]{:S(2)}) collective-permute-start(bf16[64,1024]{1,0:T(8,128)(2,1)S(1)} %add_convert_fusion.1), channel_id=1, source_target_pairs={{0,2},{1,3},{2,0},{3,1},{4,6},{5,7},{6,4},{7,5},{8,10},{9,11},{10,... | collective-permute-start | bytes 393224 | tf_op jit(solution)/shard_map/ppermute | solution.py:84
  145.5 0.9 copy-start.9
  146.4 9.8 %copy-start.1 = (bf16[64,256]{1,0:T(8,128)(2,1)S(1)}, bf16[64,256]{1,0:T(8,128)(2,1)}, u32[]{:S(2)}) copy-start(bf16[64,256]{1,0:T(8,128)(2,1)} %param.9) | copy-start | bytes 98308

commit v14 on v13

--- a/solution.py
+++ b/solution.py
@@ -110,13 +110,14 @@
     acc_ref = refs[sources] if has_acc else None
     w_ref, o_ref = refs[sources + has_acc :]
     width = chunk + 2 * x_pad
-    count = o_ref.shape[2] // chunk
+    count = o_ref.shape[1] // chunk
     shift = chunk + x_pad - x_pad // 2
     side = (chunk + x_pad) // 128
-
-    def body(index, carry):
-        base = pl.multiple_of(index * chunk, chunk)
-        for plane, terms in enumerate(plan):
+    current = pl.program_id(0)
+
+    def run(terms):
+        def body(index, carry):
+            base = pl.multiple_of(index * chunk, chunk)
             for row in range(0, y_cells, rows):
                 left = jnp.zeros((rows, chunk + x_pad), jnp.float32)
                 centre = jnp.zeros((rows, chunk), jnp.float32)
@@ -139,11 +140,14 @@
                     + pltpu.roll(right, shift, 1)[:, :chunk]
                 )
                 if has_acc:
-                    total = total + acc_ref[plane, pl.ds(row, rows), pl.ds(base, chunk)]
-                o_ref[plane, pl.ds(row, rows), pl.ds(base, chunk)] = total.astype(o_ref.dtype)
-        return carry
-
-    lax.fori_loop(0, count, body, 0)
+                    total = total + acc_ref[pl.ds(row, rows), pl.ds(base, chunk)]
+                o_ref[pl.ds(row, rows), pl.ds(base, chunk)] = total.astype(o_ref.dtype)
+            return carry
+
+        lax.fori_loop(0, count, body, 0)
+
+    for plane, terms in enumerate(plan):
+        pl.when(current == plane)(functools.partial(run, terms))
 
 
 def stencil_call(plan, inputs, acc, gains, y_cells, lanes, channels, out_dtype):
@@ -152,9 +156,19 @@
     kernel = functools.partial(
         stencil_kernel, chunk, 2 * channels, y_cells, rows, plan, len(inputs), acc is not None
     )
-    operands = list(inputs) + ([acc] if acc is not None else []) + [gains]
+    plane_spec = pl.BlockSpec((None, y_cells, lanes), lambda z: (z, 0, 0))
+    in_specs = [pl.BlockSpec(value.shape, lambda z: (0, 0, 0)) for value in inputs]
+    operands = list(inputs)
+    if acc is not None:
+        in_specs.append(plane_spec)
+        operands.append(acc)
+    in_specs.append(pl.BlockSpec(gains.shape, lambda z: (0, 0, 0)))
+    operands.append(gains)
     return pl.pallas_call(
         kernel,
+        grid=(len(plan),),
+        in_specs=in_specs,
+        out_specs=plane_spec,
         out_shape=jax.ShapeDtypeStruct((len(plan), y_cells, lanes), out_dtype),
     )(*operands)
 

time: 157 us -> 158 us (level)
  no operation moved by 1% of the time
where the time goes in v14:
time: 158 us; the launch traced here: 157 us
  local copies, waits for them, and re-layouts  38 us (24%)
  starting transfers between devices  37.8 us (24%)
  Pallas kernels  33.5 us (21%)
  matrix products  21.8 us (14%)
  other arithmetic  13.1 us (8%)
  waiting for transfers between devices  11.6 us (7%)
    pallas_call x4, Pallas kernels, stencil_call(): pl.pallas_call(kernel, grid=(len(plan),), in_specs=in_specs, out_specs=pl...  33.5 us
    dot_general x1, matrix products, per_device(): jnp.dot(grad_hidden, expand_weight.T, preferred_element_type=jnp.float32)  8.79 us
    ppermute x6, starting transfers between devices, ring_reduce_scatter(): lax.ppermute(piece, axis, [(i, (i + shift) % size) for i in range(size)])  8.46 us
    ppermute x6, starting transfers between devices, ring_gather(): lax.ppermute(block, axis, [(i, (i + shift) % size) for i in range(size)])  7.79 us
    ppermute x3, starting transfers between devices, butterfly_sum(): lax.ppermute(value, axis, [(i, i ^ step) for i in range(size)])  7.69 us
    ppermute x2, starting transfers between devices, spatial_rims(): below = lax.ppermute(inner[-1:], 'gz', up)  6.65 us
    dot_general x2, matrix products, share_inverse(): jnp.einsum('krc,xk->rxc', segment[:, :, :channels], cos_table, preferred_...  4.64 us
    reshape x1, local copies, waits for them, and re-layouts, per_device(): cotangent.reshape(row_count, x_cells, channels)  4.05 us
  transfers between devices with their start and end apart: 25, of which 6 were waited for; matrix products, arithmetic and copies ran while one was open for 35% of the time, Pallas kernels for 12%

profile of v14, /device:TPU:0, one launch (start us, length us, event | category | flops | bytes accessed | tf_op | source)
XLA Modules:
  0.0 156.9 jit_solution(3007609010788623291)
XLA Ops:
  0.7 3.0 %reshape.100 = bf16[32,256,64]{2,1,0:T(8,128)(2,1)S(1)} reshape(bf16[2,16,16384]{2,1,0:T(8,128)(2,1)} %param.7) | data formatting | bytes 2097152 | tf_op jit(solution)/shard_map/reshape | solution.py:249
  5.8 3.9 %collective-permute-start.2 = (f32[8,32,128]{2,0,1:T(8,128)}, f32[8,32,128]{2,0,1:T(8,128)}, u32[]{:S(2)}, u32[]{:S(2)}) collective-permute-start(f32[8,32,128]{2,0,1:T(8,128)} %get-tuple-element.28), channel_id=1, source_target_pairs={{0,24},{8,0},{16,8},{24,16},{1,25},{9,1},{17,9},{25,17},{2,26},{10... | collective-permute-start | bytes 393224 | tf_op jit(solution)/shard_map/ppermute | solution.py:73
  11.5 2.4 %collective-permute-start.3 = (bf16[2,16,128]{2,1,0:T(8,128)(2,1)S(1)}, bf16[2,16,128]{2,1,0:T(8,128)(2,1)S(1)}, u32[]{:S(2)}, u32[]{:S(2)}) collective-permute-start(bf16[2,16,128]{2,1,0:T(8,128)(2,1)S(1)} %get-tuple-element.25), channel_id=1, source_target_pairs={{0,8},{8,16},{16,24},{24,0},{1,9},{9,17},{17,25},{25,1},{2,10},{10... | collective-permute-start | bytes 24584 | tf_op jit(solution)/shard_map/ppermute | solution.py:26
  14.4 2.4 %collective-permute-done.3 = bf16[2,16,128]{2,1,0:T(8,128)(2,1)S(1)} collective-permute-done((bf16[2,16,128]{2,1,0:T(8,128)(2,1)S(1)}, bf16[2,16,128]{2,1,0:T(8,128)(2,1)S(1)}, u32[]{:S(2)}, u32[]{:S(2)}) %collective-permute-start.3) | collective-permute-done | bytes 8224 | tf_op jit(solution)/shard_map/ppermute | solution.py:26
  17.5 1.0 copy-done.7
  19.0 1.2 collective-permute-done.5
  20.4 1.8 %pad_maximum_fusion.refs_0_ = bf16[2,18,16640]{2,1,0:T(8,128)(2,1)S(1)} fusion(bf16[2,1,16640]{2,1,0:T(2,128)(2,1)S(1)} %get-tuple-element.38, bf16[2,16,16640]{2,1,0:T(8,128)(2,1)} %copy-done.7, bf16[2,1,16640]{2,1,0:T(2,128)(2,1)S(1)} %get-tuple-element.37), kind=kLoop, calls=%fused_computation.23 | loop fusion | flops 3594240 | bytes 2396160 | tf_op jit(solution)/shard_map/concatenate | solution.py:28
  22.2 1.4 fusion.112
  23.6 4.4 %collective-permute-start.6 = (bf16[1,18,16640]{2,1,0:T(8,128)(2,1)}, bf16[1,18,16640]{2,1,0:T(8,128)(2,1)}, u32[]{:S(2)}, u32[]{:S(2)}) collective-permute-start(bf16[1,18,16640]{2,1,0:T(8,128)(2,1)} %get-tuple-element.18), channel_id=1, source_target_pairs={{0,1},{1,2},{2,3},{4,5},{5,6},{6,7},{8,9},{9,10},{10,11},{12,13},{... | collective-permute-start | bytes 1797128 | tf_op jit(solution)/shard_map/ppermute | solution.py:103
  28.0 1.3 collective-permute-start.7
  29.3 4.0 %reshape.104 = bf16[32,256,64]{2,1,0:T(8,128)(2,1)} reshape(bf16[2,16,16384]{2,1,0:T(8,128)(2,1)} %param.13) | data formatting | bytes 2097152 | tf_op jit(solution)/shard_map/reshape | solution.py:269
  33.4 2.7 %copy.30 = bf16[32,256,64]{1,2,0:T(8,128)(2,1)} copy(bf16[32,256,64]{2,1,0:T(8,128)(2,1)} %reshape.104) | data formatting | bytes 2097152 | tf_op jit(solution)/shard_map/optimization_barrier | solution.py:269
  36.0 1.2 neg.10
  37.5 1.2 fusion.13
  39.3 9.5 %shard_map.94.refs_2_ = f32[2,16,16384]{2,1,0:T(8,128)} custom-call(bf16[2,18,16640]{2,1,0:T(8,128)(2,1)} %copy-done.3, f32[27,8,128]{2,1,0:T(8,128)} %broadcast_in_dim.18.refs_1_.refs_3_), custom_call_target="tpu_custom_call" | custom-call | tf_op jit(solution)/shard_map/pallas_call | solution.py:167
  48.8 1.2 fusion.36
  50.1 7.2 %shard_map.95 = bf16[2,16,16384]{2,1,0:T(8,128)(2,1)} custom-call(bf16[1,18,16640]{2,1,0:T(8,128)(2,1)} %collective-permute-done.6.refs_0_, bf16[1,18,16640]{2,1,0:T(8,128)(2,1)} %collective-permute-done.7.refs_1_, f32[2,16,16384]{2,1,0:T(8,128)} %shard_map.94.refs_2_, f32[27,8,128]{2,1,0:T(8,128)} %broadcast_in_dim.18.refs_1_.refs_3_), custom_call_target="tpu_custom_call" | custom-call | tf_op jit(solution)/shard_map/pallas_call | solution.py:167
  58.3 1.4 collective-permute-start.9
  59.6 1.2 collective-permute-start.10
  60.9 3.0 %reshape.101 = bf16[8192,64]{1,0:T(8,128)(2,1)S(1)} reshape(bf16[2,16,16384]{2,1,0:T(8,128)(2,1)} %shard_map.95) | data formatting | bytes 2097152 | tf_op jit(solution)/shard_map/reshape | solution.py:258
  63.9 1.2 fusion.117
  65.2 2.8 %fusion.5 = f32[8192,64]{0,1:T(8,128)S(1)} fusion(bf16[256,64]{0,1:T(8,128)(2,1)S(1)} %copy-done.11, f32[8192,256]{1,0:T(8,128)S(1)} %fusion.117), kind=kOutput, calls=%fused_computation.10 | convolution fusion | flops 278921216 | bytes 10518528 | tf_op jit(solution)/shard_map/dot_general | solution.py:261
  69.7 2.7 %fusion.11 = (bf16[32,256,64]{1,2,0:T(8,128)(2,1)S(1)}, bf16[32,256,64]{1,2,0:T(8,128)(2,1)}) fusion(bf16[32,256,64]{1,2,0:T(8,128)(2,1)S(1)} %copy-done.8, f32[256,32,64]{0,2,1:T(8,128)S(1)} %fusion.20, bf16[32,32,64]{2,1,0:T(8,128)(2,1)S(1)} %get-tuple-element.33, f32[32]{0:T(128)S(1)} %get-tuple-element.39, s32[32]{0:T(128)S(1)} %add.186, ...), kind=kOutput, calls=%fused_computation.17 | convolution fusion | flops 41566208 | bytes 7472384 | tf_op jit(solution)/shard_map/krc,xk->rxc/dot_general | solution.py:206
  75.4 1.4 collective-permute-start.12
  76.8 1.2 collective-permute-start.11
  78.1 8.8 %convolution_convert_fusion = bf16[8192,64]{0,1:T(8,128)(2,1)} fusion(bf16[64,256]{1,0:T(8,128)(2,1)S(1)} %copy-done, bf16[8192,64]{0,1:T(8,128)(2,1)S(1)} %bitcast.54, bf16[256,64]{0,1:T(8,128)(2,1)S(1)} %copy-done.12, f32[8192,256]{1,0:T(8,128)} %copy-done.4), kind=kOutput, calls=%fused_computation.3 | convolution fusion | flops 558366720 | bytes 10551296 | tf_op jit(solution)/shard_map/dot_general | solution.py:278
  86.9 2.0 %copy.29 = bf16[32,256,64]{2,1,0:T(8,128)(2,1)S(1)} copy(bf16[32,256,64]{1,2,0:T(8,128)(2,1)} %get-tuple-element.14) | data formatting | bytes 2097152 | tf_op jit(solution)/shard_map/convert_element_type | solution.py:267
  88.9 2.5 %reshape.103 = bf16[2,16,16384]{2,1,0:T(8,128)(2,1)} reshape(bf16[32,256,64]{2,1,0:T(8,128)(2,1)S(1)} %copy.29) | data formatting | bytes 2097152 | tf_op jit(solution)/shard_map/reshape | solution.py:267
  91.4 2.0 %copy.35 = bf16[8192,64]{1,0:T(8,128)(2,1)S(1)} copy(bf16[8192,64]{0,1:T(8,128)(2,1)} %convolution_convert_fusion) | data formatting | bytes 2097152 | tf_op jit(solution)/shard_map/convert_element_type | solution.py:278
  93.4 2.5 %reshape.106 = bf16[2,16,16384]{2,1,0:T(8,128)(2,1)} reshape(bf16[8192,64]{1,0:T(8,128)(2,1)S(1)} %copy.35) | data formatting | bytes 2097152 | tf_op jit(solution)/shard_map/reshape | solution.py:281
  95.9 1.2 fusion.28
  98.0 1.0 collective-permute-start.14
  99.0 1.1 collective-permute-start.19
  100.1 1.4 collective-permute-start.20
  101.5 1.7 %collective-permute-start.21 = (bf16[8,32,128]{2,1,0:T(8,128)(2,1)S(1)}, bf16[8,32,128]{2,1,0:T(8,128)(2,1)S(1)}, u32[]{:S(2)}, u32[]{:S(2)}) collective-permute-start(bf16[8,32,128]{2,1,0:T(8,128)(2,1)S(1)} %convolution_convert_fusion.1), channel_id=1, source_target_pairs={{0,24},{8,0},{16,8},{24,16},{1,25},{9,1},{17,9},{25,17},{2,26},{10... | collective-permute-start | bytes 196616 | tf_op jit(solution)/shard_map/ppermute | solution.py:62
  104.0 2.9 %collective-permute-done.15 = bf16[2,16,128]{2,1,0:T(8,128)(2,1)S(1)} collective-permute-done((bf16[2,16,128]{2,1,0:T(8,128)(2,1)S(1)}, bf16[2,16,128]{2,1,0:T(8,128)(2,1)S(1)}, u32[]{:S(2)}, u32[]{:S(2)}) %collective-permute-start.15) | collective-permute-done | bytes 8224 | tf_op jit(solution)/shard_map/ppermute | solution.py:27
  109.4 2.7 %collective-permute-start.23 = (bf16[64,1024]{1,0:T(8,128)(2,1)S(1)}, bf16[64,1024]{1,0:T(8,128)(2,1)S(1)}, u32[]{:S(2)}, u32[]{:S(2)}) collective-permute-start(bf16[64,1024]{1,0:T(8,128)(2,1)S(1)} %add_convert_fusion.2), channel_id=1, source_target_pairs={{0,1},{1,0},{2,3},{3,2},{4,5},{5,4},{6,7},{7,6},{8,9},{9,8},{10,11... | collective-permute-start | bytes 393224 | tf_op jit(solution)/shard_map/ppermute | solution.py:84
  112.1 1.3 fusion.111
  113.4 2.3 %collective-permute-start.17 = (bf16[1,18,16640]{2,1,0:T(8,128)(2,1)}, bf16[1,18,16640]{2,1,0:T(8,128)(2,1)S(1)}, u32[]{:S(2)}, u32[]{:S(2)}) collective-permute-start(bf16[1,18,16640]{2,1,0:T(8,128)(2,1)} %get-tuple-element.16), channel_id=1, source_target_pairs={{0,1},{1,2},{2,3},{4,5},{5,6},{6,7},{8,9},{9,10},{10,11},{12,13},{... | collective-permute-start | bytes 1797128 | tf_op jit(solution)/shard_map/ppermute | solution.py:103
  115.7 1.5 collective-permute-start.18
  117.2 4.9 %collective-permute-start.24 = (bf16[64,1024]{1,0:T(8,128)(2,1)S(1)}, bf16[64,1024]{1,0:T(8,128)(2,1)S(1)}, u32[]{:S(2)}, u32[]{:S(2)}) collective-permute-start(bf16[64,1024]{1,0:T(8,128)(2,1)S(1)} %add_convert_fusion.1), channel_id=1, source_target_pairs={{0,2},{1,3},{2,0},{3,1},{4,6},{5,7},{6,4},{7,5},{8,10},{9,11},{10,... | collective-permute-start | bytes 393224 | tf_op jit(solution)/shard_map/ppermute | solution.py:84
  122.2 2.0 %add_bitcast_fusion = f32[32,256,64]{1,2,0:T(8,128)} fusion(f32[256,32,64]{0,2,1:T(8,128)S(1)} %fusion.17, bf16[32,32,64]{2,1,0:T(8,128)(2,1)S(1)} %get-tuple-element.31, s32[32]{0:T(128)S(1)} %add.186, s32[256]{0:T(256)S(1)} %iota_add_fusion.1), kind=kOutput, calls=%fused_computation.20 | convolution fusion | flops 34201600 | bytes 4326528 | tf_op jit(solution)/shard_map/krc,xk->rxc/dot_general | solution.py:206
  124.1 3.8 %copy.38 = f32[32,256,64]{2,1,0:T(8,128)} copy(f32[32,256,64]{1,2,0:T(8,128)} %add_bitcast_fusion) | data formatting | bytes 4194304 | tf_op jit(solution)/shard_map/add | solution.py:209
  127.9 2.9 %reshape.107 = f32[2,16,16384]{2,1,0:T(8,128)S(1)} reshape(f32[32,256,64]{2,1,0:T(8,128)} %copy.38) | data formatting | bytes 4194304 | tf_op jit(solution)/shard_map/reshape | solution.py:293
  131.5 9.5 %shard_map.96.refs_2_ = f32[2,16,16384]{2,1,0:T(8,128)} custom-call(bf16[2,18,16640]{2,1,0:T(8,128)(2,1)} %copy-done.2, f32[27,8,128]{2,1,0:T(8,128)} %broadcast_in_dim.36.refs_1_.refs_3_), custom_call_target="tpu_custom_call" | custom-call | tf_op jit(solution)/shard_map/pallas_call | solution.py:167
  141.0 3.9 %collective-permute-done.24 = bf16[64,1024]{1,0:T(8,128)(2,1)S(1)} collective-permute-done((bf16[64,1024]{1,0:T(8,128)(2,1)S(1)}, bf16[64,1024]{1,0:T(8,128)(2,1)S(1)}, u32[]{:S(2)}, u32[]{:S(2)}) %collective-permute-start.24) | collective-permute-done | bytes 131104 | tf_op jit(solution)/shard_map/ppermute | solution.py:84
  146.8 7.4 %shard_map.97 = f32[2,16,16384]{2,1,0:T(8,128)} custom-call(bf16[1,18,16640]{2,1,0:T(8,128)(2,1)} %copy-done.9, bf16[1,18,16640]{2,1,0:T(8,128)(2,1)} %collective-permute-done.18.refs_1_, f32[2,16,16384]{2,1,0:T(8,128)} %shard_map.96.refs_2_, f32[27,8,128]{2,1,0:T(8,128)} %broadcast_in_dim.36.refs_1_.refs_3_), custom_call_target="tpu_custom_call" | custom-call | tf_op jit(solution)/shard_map/pallas_call | solution.py:167
  154.2 2.7 %add_convert_fusion = bf16[2,16,16384]{2,1,0:T(8,128)(2,1)} fusion(f32[2,16,16384]{2,1,0:T(8,128)} %shard_map.97, f32[2,16,16384]{2,1,0:T(8,128)S(1)} %reshape.107), kind=kLoop, calls=%fused_computation.19 | loop fusion | flops 1048576 | bytes 5242880 | tf_op jit(solution)/shard_map/convert_element_type | solution.py:293
  (109 shorter events, 19.1 us)
Async XLA Ops:
  0.6 63.3 %copy-start = (bf16[64,256]{1,0:T(8,128)(2,1)S(1)}, bf16[64,256]{1,0:T(8,128)(2,1)}, u32[]{:S(2)}) copy-start(bf16[64,256]{1,0:T(8,128)(2,1)} %param.9) | copy-start | bytes 98308
  4.8 12.0 %copy-start.5 = (bf16[2,16,16384]{2,1,0:T(8,128)(2,1)S(1)}, bf16[2,16,16384]{2,1,0:T(8,128)(2,1)}, u32[]{:S(2)}) copy-start(bf16[2,16,16384]{2,1,0:T(8,128)(2,1)} %param.7) | copy-start | bytes 3145732
  5.8 43.0 %collective-permute-start.2 = (f32[8,32,128]{2,0,1:T(8,128)}, f32[8,32,128]{2,0,1:T(8,128)}, u32[]{:S(2)}, u32[]{:S(2)}) collective-permute-start(f32[8,32,128]{2,0,1:T(8,128)} %get-tuple-element.28), channel_id=1, source_target_pairs={{0,24},{8,0},{16,8},{24,16},{1,25},{9,1},{17,9},{25,17},{2,26},{10... | collective-permute-start | bytes 393224 | tf_op jit(solution)/shard_map/ppermute | solution.py:73
  9.6 39.1 %collective-permute-start.1 = (f32[8,32,128]{2,0,1:T(8,128)}, f32[8,32,128]{2,0,1:T(8,128)}, u32[]{:S(2)}, u32[]{:S(2)}) collective-permute-start(f32[8,32,128]{2,0,1:T(8,128)} %get-tuple-element.27), channel_id=1, source_target_pairs={{0,16},{8,24},{16,0},{24,8},{1,17},{9,25},{17,1},{25,9},{2,18},{10... | collective-permute-start | bytes 393224 | tf_op jit(solution)/shard_map/ppermute | solution.py:73
  10.2 38.6 %collective-permute-start = (f32[8,32,128]{2,0,1:T(8,128)}, f32[8,32,128]{2,0,1:T(8,128)}, u32[]{:S(2)}, u32[]{:S(2)}) collective-permute-start(f32[8,32,128]{2,0,1:T(8,128)} %get-tuple-element.26), channel_id=1, source_target_pairs={{0,8},{8,16},{16,24},{24,0},{1,9},{9,17},{17,25},{25,1},{2,10},{10... | collective-permute-start | bytes 393224 | tf_op jit(solution)/shard_map/ppermute | solution.py:73
  11.5 5.3 %collective-permute-start.3 = (bf16[2,16,128]{2,1,0:T(8,128)(2,1)S(1)}, bf16[2,16,128]{2,1,0:T(8,128)(2,1)S(1)}, u32[]{:S(2)}, u32[]{:S(2)}) collective-permute-start(bf16[2,16,128]{2,1,0:T(8,128)(2,1)S(1)} %get-tuple-element.25), channel_id=1, source_target_pairs={{0,8},{8,16},{16,24},{24,0},{1,9},{9,17},{17,25},{25,1},{2,10},{10... | collective-permute-start | bytes 24584 | tf_op jit(solution)/shard_map/ppermute | solution.py:26
  13.9 3.7 %collective-permute-start.4 = (bf16[2,16,128]{2,1,0:T(8,128)(2,1)S(1)}, bf16[2,16,128]{2,1,0:T(8,128)(2,1)S(1)}, u32[]{:S(2)}, u32[]{:S(2)}) collective-permute-start(bf16[2,16,128]{2,1,0:T(8,128)(2,1)S(1)} %get-tuple-element.24), channel_id=1, source_target_pairs={{8,0},{16,8},{24,16},{0,24},{9,1},{17,9},{25,17},{1,25},{10,2},{18... | collective-permute-start | bytes 24584 | tf_op jit(solution)/shard_map/ppermute | solution.py:27
  17.5 1.0 copy-start.7
  18.7 1.4 collective-permute-start.5
  22.2 11.1 %copy-start.3 = (bf16[2,18,16640]{2,1,0:T(8,128)(2,1)}, bf16[2,18,16640]{2,1,0:T(8,128)(2,1)S(1)}, u32[]{:S(2)}) copy-start(bf16[2,18,16640]{2,1,0:T(8,128)(2,1)S(1)} %pad_maximum_fusion.refs_0_) | copy-start | bytes 3594244
  23.6 26.5 %collective-permute-start.6 = (bf16[1,18,16640]{2,1,0:T(8,128)(2,1)}, bf16[1,18,16640]{2,1,0:T(8,128)(2,1)}, u32[]{:S(2)}, u32[]{:S(2)}) collective-permute-start(bf16[1,18,16640]{2,1,0:T(8,128)(2,1)} %get-tuple-element.18), channel_id=1, source_target_pairs={{0,1},{1,2},{2,3},{4,5},{5,6},{6,7},{8,9},{9,10},{10,11},{12,13},{... | collective-permute-start | bytes 1797128 | tf_op jit(solution)/shard_map/ppermute | solution.py:103
  28.0 22.1 %collective-permute-start.7 = (bf16[1,18,16640]{2,1,0:T(8,128)(2,1)}, bf16[1,18,16640]{2,1,0:T(8,128)(2,1)}, u32[]{:S(2)}, u32[]{:S(2)}) collective-permute-start(bf16[1,18,16640]{2,1,0:T(8,128)(2,1)} %get-tuple-element.17), channel_id=1, source_target_pairs={{1,0},{2,1},{3,2},{5,4},{6,5},{7,6},{9,8},{10,9},{11,10},{13,12},{... | collective-permute-start | bytes 1797128 | tf_op jit(solution)/shard_map/ppermute | solution.py:104
  33.3 3.9 %copy-start.10 = (bf16[27,64]{1,0:T(8,128)(2,1)S(1)}, bf16[27,64]{1,0:T(8,128)(2,1)}, u32[]{:S(2)}) copy-start(bf16[27,64]{1,0:T(8,128)(2,1)} %param.8) | copy-start | bytes 10372
  57.4 11.1 %collective-permute-start.8 = (bf16[8,32,128]{2,1,0:T(8,128)(2,1)S(1)}, bf16[8,32,128]{2,1,0:T(8,128)(2,1)S(1)}, u32[]{:S(2)}, u32[]{:S(2)}) collective-permute-start(bf16[8,32,128]{2,1,0:T(8,128)(2,1)S(1)} %convolution_convert_fusion.2), channel_id=1, source_target_pairs={{0,8},{8,16},{16,24},{24,0},{1,9},{9,17},{17,25},{25,1},{2,10},{10... | collective-permute-start | bytes 196616 | tf_op jit(solution)/shard_map/ppermute | solution.py:62
  58.3 10.2 %collective-permute-start.9 = (bf16[8,32,128]{2,1,0:T(8,128)(2,1)S(1)}, bf16[8,32,128]{2,1,0:T(8,128)(2,1)S(1)}, u32[]{:S(2)}, u32[]{:S(2)}) collective-permute-start(bf16[8,32,128]{2,1,0:T(8,128)(2,1)S(1)} %convolution_convert_fusion.2), channel_id=1, source_target_pairs={{0,16},{8,24},{16,0},{24,8},{1,17},{9,25},{17,1},{25,9},{2,18},{10... | collective-permute-start | bytes 196616 | tf_op jit(solution)/shard_map/ppermute | solution.py:62
  59.6 8.9 %collective-permute-start.10 = (bf16[8,32,128]{2,1,0:T(8,128)(2,1)S(1)}, bf16[8,32,128]{2,1,0:T(8,128)(2,1)S(1)}, u32[]{:S(2)}, u32[]{:S(2)}) collective-permute-start(bf16[8,32,128]{2,1,0:T(8,128)(2,1)S(1)} %convolution_convert_fusion.2), channel_id=1, source_target_pairs={{0,24},{8,0},{16,8},{24,16},{1,25},{9,1},{17,9},{25,17},{2,26},{10... | collective-permute-start | bytes 196616 | tf_op jit(solution)/shard_map/ppermute | solution.py:62
  63.9 1.2 copy-start.11
  65.2 3.3 %copy-start.4 = (f32[8192,256]{1,0:T(8,128)}, f32[8192,256]{1,0:T(8,128)S(1)}, u32[]{:S(2)}) copy-start(f32[8192,256]{1,0:T(8,128)S(1)} %fusion.117) | copy-start | bytes 25165828
  68.5 1.2 copy-start.8
  73.6 4.5 %copy-start.12 = (bf16[256,64]{0,1:T(8,128)(2,1)S(1)}, bf16[256,64]{0,1:T(8,128)(2,1)}, u32[]{:S(2)}) copy-start(bf16[256,64]{0,1:T(8,128)(2,1)} %param.10) | copy-start | bytes 98308
  74.5 21.4 %collective-permute-start.13 = (f32[8,32,128]{2,0,1:T(8,128)}, f32[8,32,128]{2,0,1:T(8,128)}, u32[]{:S(2)}, u32[]{:S(2)}) collective-permute-start(f32[8,32,128]{2,0,1:T(8,128)} %get-tuple-element.23), channel_id=1, source_target_pairs={{0,24},{8,0},{16,8},{24,16},{1,25},{9,1},{17,9},{25,17},{2,26},{10... | collective-permute-start | bytes 393224 | tf_op jit(solution)/shard_map/ppermute | solution.py:73
  75.4 20.5 %collective-permute-start.12 = (f32[8,32,128]{2,0,1:T(8,128)}, f32[8,32,128]{2,0,1:T(8,128)}, u32[]{:S(2)}, u32[]{:S(2)}) collective-permute-start(f32[8,32,128]{2,0,1:T(8,128)} %get-tuple-element.22), channel_id=1, source_target_pairs={{0,16},{8,24},{16,0},{24,8},{1,17},{9,25},{17,1},{25,9},{2,18},{10... | collective-permute-start | bytes 393224 | tf_op jit(solution)/shard_map/ppermute | solution.py:73
  76.8 19.1 %collective-permute-start.11 = (f32[8,32,128]{2,0,1:T(8,128)}, f32[8,32,128]{2,0,1:T(8,128)}, u32[]{:S(2)}, u32[]{:S(2)}) collective-permute-start(f32[8,32,128]{2,0,1:T(8,128)} %get-tuple-element.21), channel_id=1, source_target_pairs={{0,8},{8,16},{16,24},{24,0},{1,9},{9,17},{17,25},{25,1},{2,10},{10... | collective-permute-start | bytes 393224 | tf_op jit(solution)/shard_map/ppermute | solution.py:73
  95.9 2.1 %copy-start.6 = (bf16[2,16,16384]{2,1,0:T(8,128)(2,1)S(1)}, bf16[2,16,16384]{2,1,0:T(8,128)(2,1)}, u32[]{:S(2)}) copy-start(bf16[2,16,16384]{2,1,0:T(8,128)(2,1)} %reshape.106) | copy-start | bytes 3145732
  98.0 5.8 %collective-permute-start.14 = (bf16[2,16,128]{2,1,0:T(8,128)(2,1)S(1)}, bf16[2,16,128]{2,1,0:T(8,128)(2,1)S(1)}, u32[]{:S(2)}, u32[]{:S(2)}) collective-permute-start(bf16[2,16,128]{2,1,0:T(8,128)(2,1)S(1)} %get-tuple-element.20), channel_id=1, source_target_pairs={{0,8},{8,16},{16,24},{24,0},{1,9},{9,17},{17,25},{25,1},{2,10},{10... | collective-permute-start | bytes 24584 | tf_op jit(solution)/shard_map/ppermute | solution.py:26
  99.0 8.2 %collective-permute-start.19 = (bf16[8,32,128]{2,1,0:T(8,128)(2,1)S(1)}, bf16[8,32,128]{2,1,0:T(8,128)(2,1)S(1)}, u32[]{:S(2)}, u32[]{:S(2)}) collective-permute-start(bf16[8,32,128]{2,1,0:T(8,128)(2,1)S(1)} %convolution_convert_fusion.1), channel_id=1, source_target_pairs={{0,8},{8,16},{16,24},{24,0},{1,9},{9,17},{17,25},{25,1},{2,10},{10... | collective-permute-start | bytes 196616 | tf_op jit(solution)/shard_map/ppermute | solution.py:62
  100.1 7.1 %collective-permute-start.20 = (bf16[8,32,128]{2,1,0:T(8,128)(2,1)S(1)}, bf16[8,32,128]{2,1,0:T(8,128)(2,1)S(1)}, u32[]{:S(2)}, u32[]{:S(2)}) collective-permute-start(bf16[8,32,128]{2,1,0:T(8,128)(2,1)S(1)} %convolution_convert_fusion.1), channel_id=1, source_target_pairs={{0,16},{8,24},{16,0},{24,8},{1,17},{9,25},{17,1},{25,9},{2,18},{10... | collective-permute-start | bytes 196616 | tf_op jit(solution)/shard_map/ppermute | solution.py:62
  101.5 5.7 %collective-permute-start.21 = (bf16[8,32,128]{2,1,0:T(8,128)(2,1)S(1)}, bf16[8,32,128]{2,1,0:T(8,128)(2,1)S(1)}, u32[]{:S(2)}, u32[]{:S(2)}) collective-permute-start(bf16[8,32,128]{2,1,0:T(8,128)(2,1)S(1)} %convolution_convert_fusion.1), channel_id=1, source_target_pairs={{0,24},{8,0},{16,8},{24,16},{1,25},{9,1},{17,9},{25,17},{2,26},{10... | collective-permute-start | bytes 196616 | tf_op jit(solution)/shard_map/ppermute | solution.py:62
  103.2 3.7 %collective-permute-start.15 = (bf16[2,16,128]{2,1,0:T(8,128)(2,1)S(1)}, bf16[2,16,128]{2,1,0:T(8,128)(2,1)S(1)}, u32[]{:S(2)}, u32[]{:S(2)}) collective-permute-start(bf16[2,16,128]{2,1,0:T(8,128)(2,1)S(1)} %get-tuple-element.19), channel_id=1, source_target_pairs={{8,0},{16,8},{24,16},{0,24},{9,1},{17,9},{25,17},{1,25},{10,2},{18... | collective-permute-start | bytes 24584 | tf_op jit(solution)/shard_map/ppermute | solution.py:27
  103.8 5.6 %collective-permute-start.22 = (bf16[64,1024]{1,0:T(8,128)(2,1)S(1)}, bf16[64,1024]{1,0:T(8,128)(2,1)S(1)}, u32[]{:S(2)}, u32[]{:S(2)}) collective-permute-start(bf16[64,1024]{1,0:T(8,128)(2,1)S(1)} %convert_element_type.139), channel_id=1, source_target_pairs={{0,4},{4,0},{1,5},{5,1},{2,6},{6,2},{3,7},{7,3},{8,12},{12,8},{9,1... | collective-permute-start | bytes 393224 | tf_op jit(solution)/shard_map/ppermute | solution.py:84
  107.1 1.4 collective-permute-start.16
  109.4 14.8 %copy-start.2 = (bf16[2,18,16640]{2,1,0:T(8,128)(2,1)}, bf16[2,18,16640]{2,1,0:T(8,128)(2,1)S(1)}, u32[]{:S(2)}) copy-start(bf16[2,18,16640]{2,1,0:T(8,128)(2,1)S(1)} %pad_maximum_fusion.1.refs_0_) | copy-start | bytes 3594244
  109.4 7.7 %collective-permute-start.23 = (bf16[64,1024]{1,0:T(8,128)(2,1)S(1)}, bf16[64,1024]{1,0:T(8,128)(2,1)S(1)}, u32[]{:S(2)}, u32[]{:S(2)}) collective-permute-start(bf16[64,1024]{1,0:T(8,128)(2,1)S(1)} %add_convert_fusion.2), channel_id=1, source_target_pairs={{0,1},{1,0},{2,3},{3,2},{4,5},{5,4},{6,7},{7,6},{8,9},{9,8},{10,11... | collective-permute-start | bytes 393224 | tf_op jit(solution)/shard_map/ppermute | solution.py:84
  113.4 32.5 %collective-permute-start.17 = (bf16[1,18,16640]{2,1,0:T(8,128)(2,1)}, bf16[1,18,16640]{2,1,0:T(8,128)(2,1)S(1)}, u32[]{:S(2)}, u32[]{:S(2)}) collective-permute-start(bf16[1,18,16640]{2,1,0:T(8,128)(2,1)} %get-tuple-element.16), channel_id=1, source_target_pairs={{0,1},{1,2},{2,3},{4,5},{5,6},{6,7},{8,9},{9,10},{10,11},{12,13},{... | collective-permute-start | bytes 1797128 | tf_op jit(solution)/shard_map/ppermute | solution.py:103
  115.7 30.2 %collective-permute-start.18 = (bf16[1,18,16640]{2,1,0:T(8,128)(2,1)}, bf16[1,18,16640]{2,1,0:T(8,128)(2,1)}, u32[]{:S(2)}, u32[]{:S(2)}) collective-permute-start(bf16[1,18,16640]{2,1,0:T(8,128)(2,1)} %get-tuple-element.15), channel_id=1, source_target_pairs={{1,0},{2,1},{3,2},{5,4},{6,5},{7,6},{9,8},{10,9},{11,10},{13,12},{... | collective-permute-start | bytes 1797128 | tf_op jit(solution)/shard_map/ppermute | solution.py:104
  117.2 27.7 %collective-permute-start.24 = (bf16[64,1024]{1,0:T(8,128)(2,1)S(1)}, bf16[64,1024]{1,0:T(8,128)(2,1)S(1)}, u32[]{:S(2)}, u32[]{:S(2)}) collective-permute-start(bf16[64,1024]{1,0:T(8,128)(2,1)S(1)} %add_convert_fusion.1), channel_id=1, source_target_pairs={{0,2},{1,3},{2,0},{3,1},{4,6},{5,7},{6,4},{7,5},{8,10},{9,11},{10,... | collective-permute-start | bytes 393224 | tf_op jit(solution)/shard_map/ppermute | solution.py:84
  145.9 0.9 copy-start.9
  146.8 10.1 %copy-start.1 = (bf16[64,256]{1,0:T(8,128)(2,1)S(1)}, bf16[64,256]{1,0:T(8,128)(2,1)}, u32[]{:S(2)}) copy-start(bf16[64,256]{1,0:T(8,128)(2,1)} %param.9) | copy-start | bytes 98308

commit v15 on v13

--- a/solution.py
+++ b/solution.py
@@ -50,13 +50,25 @@
 def gathered_order(axis, share_size):
     size = lax.axis_size(axis)
     shifts = jnp.arange(size, dtype=jnp.int32)
-    sources = (lax.axis_index(axis) - shifts) % size
+    me = lax.axis_index(axis)
+    if size & (size - 1):
+        sources = (me - shifts) % size
+    else:
+        sources = jnp.bitwise_xor(me, shifts)
     local = jnp.arange(share_size, dtype=jnp.int32)
     return (sources[:, None] * share_size + local[None, :]).reshape(-1)
 
 
 def ring_gather(block, axis):
     size = lax.axis_size(axis)
+    if size & (size - 1) == 0:
+        step = 1
+        while step < size:
+            block = jnp.concatenate(
+                [block, lax.ppermute(block, axis, [(i, i ^ step) for i in range(size)])], axis=0
+            )
+            step *= 2
+        return block
     pieces = [block]
     for shift in range(1, size):
         pieces.append(lax.ppermute(block, axis, [(i, (i + shift) % size) for i in range(size)]))
@@ -67,6 +79,17 @@
     size = lax.axis_size(axis)
     share = value.shape[0] // size
     me = lax.axis_index(axis)
+    if size & (size - 1) == 0:
+        step = size // 2
+        count = size
+        while step >= 1:
+            count //= 2
+            upper = jnp.bitwise_and(me, step) != 0
+            keep = lax.dynamic_slice_in_dim(value, jnp.where(upper, count, 0) * share, count * share, 0)
+            send = lax.dynamic_slice_in_dim(value, jnp.where(upper, 0, count) * share, count * share, 0)
+            value = keep + lax.ppermute(send, axis, [(i, i ^ step) for i in range(size)])
+            step //= 2
+        return value
     total = lax.dynamic_slice_in_dim(value, me * share, share, 0)
     for shift in range(1, size):
         piece = lax.dynamic_slice_in_dim(value, ((me + shift) % size) * share, share, 0)

time: 157 us -> 155 us (0.987)
  waiting for transfers between devices: 11.4 us -> 21 us
  local copies, waits for them, and re-layouts: 38 us -> 33.8 us
  other arithmetic: 13.1 us -> 10 us
  matrix products: 21.8 us -> 19.6 us
  starting transfers between devices: 37.8 us -> 35.6 us
    ppermute x12 -> x8, waiting for transfers between devices: 0.03 us -> 7.13 us  [the longest x4 3.69 us: ring_reduce_scatter(): lax.ppermute(send, axis, [(i, i ^ step) for i in range(size)])]
    ppermute x3, waiting for transfers between devices: 3.81 us -> 8.49 us  [butterfly_sum(): lax.ppermute(value, axis, [(i, i ^ step) for i in range(size)])]
    ppermute x12 -> x8, starting transfers between devices: 16.2 us -> 12 us  [the longest x4 6.64 us: ring_reduce_scatter(): lax.ppermute(send, axis, [(i, i ^ step) for i in range(size)])]
    ppermute x2, starting transfers between devices: 6.65 us -> 8.98 us  [spatial_rims(): below = lax.ppermute(inner[-1:], 'gz', up)]
    ppermute x2, starting transfers between devices: 0.89 us -> 3.16 us  [padded_2(): after = lax.ppermute(leading, axis, down)]
    ppermute x3, starting transfers between devices: 7.71 us -> 5.7 us  [butterfly_sum(): lax.ppermute(value, axis, [(i, i ^ step) for i in range(size)])]
    ppermute x2, waiting for transfers between devices: 3.55 us -> 1.95 us  [padded_2(): after = lax.ppermute(leading, axis, down)]
    reshape x1, local copies, waits for them, and re-layouts: 4.05 us -> 2.47 us  [per_device(): cotangent.reshape(row_count, x_cells, channels)]
  transfers between devices with their start and end apart: 25 -> 21, of which waited for: 6 -> 9; matrix products, arithmetic and copies ran while one was open for 35% -> 31% of each run, Pallas kernels for 12% -> 12%
where the time goes in v15:
time: 155 us; the launch traced here: 154 us
  starting transfers between devices  35.6 us (23%)
  local copies, waits for them, and re-layouts  33.8 us (22%)
  Pallas kernels  33 us (21%)
  waiting for transfers between devices  21 us (14%)
  matrix products  19.6 us (13%)
  other arithmetic  10 us (6%)
    pallas_call x4, Pallas kernels, stencil_call(): pl.pallas_call(kernel, out_shape=jax.ShapeDtypeStruct((len(plan), y_cells...  33 us
    ppermute x2, starting transfers between devices, spatial_rims(): below = lax.ppermute(inner[-1:], 'gz', up)  8.98 us
    ppermute x3, waiting for transfers between devices, butterfly_sum(): lax.ppermute(value, axis, [(i, i ^ step) for i in range(size)])  8.49 us
    dot_general x1, matrix products, per_device(): jnp.dot(grad_hidden, expand_weight.T, preferred_element_type=jnp.float32)  7.9 us
    ppermute x4, starting transfers between devices, ring_reduce_scatter(): lax.ppermute(send, axis, [(i, i ^ step) for i in range(size)])  6.64 us
    ppermute x3, starting transfers between devices, butterfly_sum(): lax.ppermute(value, axis, [(i, i ^ step) for i in range(size)])  5.7 us
    ppermute x4, starting transfers between devices, ring_gather(): lax.ppermute(block, axis, [(i, i ^ step) for i in range(size)])  5.36 us
    ppermute x4, waiting for transfers between devices, ring_reduce_scatter(): lax.ppermute(send, axis, [(i, i ^ step) for i in range(size)])  3.69 us
  transfers between devices with their start and end apart: 21, of which 9 were waited for; matrix products, arithmetic and copies ran while one was open for 31% of the time, Pallas kernels for 12%

profile of v15, /device:TPU:0, one launch (start us, length us, event | category | flops | bytes accessed | tf_op | source)
XLA Modules:
  0.0 154.2 jit_solution(6416324903592834643)
XLA Ops:
  0.7 3.0 %reshape.89 = bf16[32,256,64]{2,1,0:T(8,128)(2,1)S(1)} reshape(bf16[2,16,16384]{2,1,0:T(8,128)(2,1)} %param.7) | data formatting | bytes 2097152 | tf_op jit(solution)/shard_map/reshape | solution.py:258
  5.0 3.0 %collective-permute-start = (f32[16,32,128]{2,0,1:T(8,128)S(1)}, f32[16,32,128]{2,0,1:T(8,128)}, u32[]{:S(2)}, u32[]{:S(2)}) collective-permute-start(f32[16,32,128]{2,0,1:T(8,128)S(1)} %fusion.15), channel_id=1, source_target_pairs={{0,16},{8,24},{16,0},{24,8},{1,17},{9,25},{17,1},{25,9},{2,18},{10... | collective-permute-start | bytes 786440 | tf_op jit(solution)/shard_map/ppermute | solution.py:90
  8.7 1.5 collective-permute-start.2
  10.2 1.4 collective-permute-start.3
  11.7 1.7 %collective-permute-done.2 = bf16[2,16,128]{2,1,0:T(8,128)(2,1)S(1)} collective-permute-done((bf16[2,16,128]{2,1,0:T(8,128)(2,1)S(1)}, bf16[2,16,128]{2,1,0:T(8,128)(2,1)S(1)}, u32[]{:S(2)}, u32[]{:S(2)}) %collective-permute-start.2) | collective-permute-done | bytes 8224 | tf_op jit(solution)/shard_map/ppermute | solution.py:26
  14.3 1.2 collective-permute-done.4
  16.4 1.3 fusion.100
  17.6 4.4 %collective-permute-start.5 = (bf16[1,18,16640]{2,1,0:T(8,128)(2,1)}, bf16[1,18,16640]{2,1,0:T(8,128)(2,1)}, u32[]{:S(2)}, u32[]{:S(2)}) collective-permute-start(bf16[1,18,16640]{2,1,0:T(8,128)(2,1)} %get-tuple-element.18), channel_id=1, source_target_pairs={{0,1},{1,2},{2,3},{4,5},{5,6},{6,7},{8,9},{9,10},{10,11},{12,13},{... | collective-permute-start | bytes 1797128 | tf_op jit(solution)/shard_map/ppermute | solution.py:126
  22.0 1.3 collective-permute-start.6
  23.3 1.1 fusion.17
  25.2 1.5 collective-permute-start.1
  26.7 2.5 %reshape.93 = bf16[32,256,64]{2,1,0:T(8,128)(2,1)S(1)} reshape(bf16[2,16,16384]{2,1,0:T(8,128)(2,1)S(1)} %copy-done.7) | data formatting | bytes 2097152 | tf_op jit(solution)/shard_map/reshape | solution.py:278
  29.2 1.6 %copy.30 = bf16[32,256,64]{1,2,0:T(8,128)(2,1)} copy(bf16[32,256,64]{2,1,0:T(8,128)(2,1)S(1)} %reshape.93) | data formatting | bytes 2097152 | tf_op jit(solution)/shard_map/optimization_barrier | solution.py:278
  31.1 1.1 fusion.19
  32.9 9.6 %shard_map.94.refs_2_ = f32[2,16,16384]{2,1,0:T(8,128)} custom-call(bf16[2,18,16640]{2,1,0:T(8,128)(2,1)} %copy-done.2, f32[27,8,128]{2,1,0:T(8,128)} %broadcast_in_dim.18.refs_1_.refs_3_), custom_call_target="tpu_custom_call" | custom-call | tf_op jit(solution)/shard_map/pallas_call | solution.py:179
  43.8 6.7 %shard_map.95 = bf16[2,16,16384]{2,1,0:T(8,128)(2,1)} custom-call(bf16[1,18,16640]{2,1,0:T(8,128)(2,1)} %collective-permute-done.5.refs_0_, bf16[1,18,16640]{2,1,0:T(8,128)(2,1)} %collective-permute-done.6.refs_1_, f32[2,16,16384]{2,1,0:T(8,128)} %shard_map.94.refs_2_, f32[27,8,128]{2,1,0:T(8,128)} %broadcast_in_dim.18.refs_1_.refs_3_), custom_call_target="tpu_custom_call" | custom-call | tf_op jit(solution)/shard_map/pallas_call | solution.py:179
  50.6 1.5 collective-permute-start.7
  52.1 3.0 %reshape.90 = bf16[8192,64]{1,0:T(8,128)(2,1)S(1)} reshape(bf16[2,16,16384]{2,1,0:T(8,128)(2,1)} %shard_map.95) | data formatting | bytes 2097152 | tf_op jit(solution)/shard_map/reshape | solution.py:267
  55.1 1.2 fusion.105
  56.4 2.8 %fusion.5 = f32[8192,64]{0,1:T(8,128)S(1)} fusion(bf16[256,64]{0,1:T(8,128)(2,1)S(1)} %copy-done.16, f32[8192,256]{1,0:T(8,128)S(1)} %fusion.105), kind=kOutput, calls=%fused_computation.10 | convolution fusion | flops 278921216 | bytes 10518528 | tf_op jit(solution)/shard_map/dot_general | solution.py:270
  59.7 1.6 %collective-permute-start.8 = (bf16[16,32,128]{2,1,0:T(8,128)(2,1)S(1)}, bf16[16,32,128]{2,1,0:T(8,128)(2,1)S(1)}, u32[]{:S(2)}, u32[]{:S(2)}) collective-permute-start(bf16[16,32,128]{2,1,0:T(8,128)(2,1)S(1)} %pad_maximum_fusion.3), channel_id=1, source_target_pairs={{0,16},{8,24},{16,0},{24,8},{1,17},{9,25},{17,1},{25,9},{2,18},{10... | collective-permute-start | bytes 393224 | tf_op jit(solution)/shard_map/ppermute | solution.py:68
  61.3 3.4 %collective-permute-done.8 = bf16[16,32,128]{2,1,0:T(8,128)(2,1)S(1)} collective-permute-done((bf16[16,32,128]{2,1,0:T(8,128)(2,1)S(1)}, bf16[16,32,128]{2,1,0:T(8,128)(2,1)S(1)}, u32[]{:S(2)}, u32[]{:S(2)}) %collective-permute-start.8) | collective-permute-done | bytes 131104 | tf_op jit(solution)/shard_map/ppermute | solution.py:68
  65.5 2.7 %fusion.11 = (bf16[32,256,64]{1,2,0:T(8,128)(2,1)S(1)}, bf16[32,256,64]{1,2,0:T(8,128)(2,1)}) fusion(bf16[32,256,64]{1,2,0:T(8,128)(2,1)S(1)} %copy-done.8, f32[256,32,64]{0,2,1:T(8,128)S(1)} %fusion.26, bf16[32,32,64]{2,1,0:T(8,128)(2,1)S(1)} %get-tuple-element.27, f32[32]{0:T(128)S(1)} %get-tuple-element.33, s32[32]{0:T(128)S(1)} %add.140, ...), kind=kOutput, calls=%fused_computation.17 | convolution fusion | flops 41566208 | bytes 7472384 | tf_op jit(solution)/shard_map/krc,xk->rxc/dot_general | solution.py:215
  69.7 1.6 %collective-permute-start.9 = (f32[16,32,128]{2,0,1:T(8,128)S(1)}, f32[16,32,128]{2,0,1:T(8,128)S(1)}, u32[]{:S(2)}, u32[]{:S(2)}) collective-permute-start(f32[16,32,128]{2,0,1:T(8,128)S(1)} %fusion.12), channel_id=1, source_target_pairs={{0,16},{8,24},{16,0},{24,8},{1,17},{9,25},{17,1},{25,9},{2,18},{10... | collective-permute-start | bytes 786440 | tf_op jit(solution)/shard_map/ppermute | solution.py:90
  71.4 1.0 copy.42
  72.4 3.7 %collective-permute-done.9 = f32[16,32,128]{2,0,1:T(8,128)S(1)} collective-permute-done((f32[16,32,128]{2,0,1:T(8,128)S(1)}, f32[16,32,128]{2,0,1:T(8,128)S(1)}, u32[]{:S(2)}, u32[]{:S(2)}) %collective-permute-start.9) | collective-permute-done | bytes 262176 | tf_op jit(solution)/shard_map/ppermute | solution.py:90
  77.6 7.9 %convolution_convert_fusion = bf16[8192,64]{0,1:T(8,128)(2,1)} fusion(bf16[64,256]{1,0:T(8,128)(2,1)S(1)} %copy-done, bf16[8192,64]{0,1:T(8,128)(2,1)} %bitcast.54, bf16[256,64]{0,1:T(8,128)(2,1)} %param.10, f32[8192,256]{1,0:T(8,128)} %copy-done.4), kind=kOutput, calls=%fused_computation.3 | convolution fusion | flops 558366720 | bytes 10551296 | tf_op jit(solution)/shard_map/dot_general | solution.py:287
  85.5 1.1 copy.29
  86.5 2.5 %reshape.92 = bf16[2,16,16384]{2,1,0:T(8,128)(2,1)} reshape(bf16[32,256,64]{2,1,0:T(8,128)(2,1)S(1)} %copy.29) | data formatting | bytes 2097152 | tf_op jit(solution)/shard_map/reshape | solution.py:276
  89.0 1.1 copy.35
  90.1 1.9 %reshape.95 = bf16[2,16,16384]{2,1,0:T(8,128)(2,1)S(1)} reshape(bf16[8192,64]{1,0:T(8,128)(2,1)S(1)} %copy.35) | data formatting | bytes 2097152 | tf_op jit(solution)/shard_map/reshape | solution.py:290
  92.0 1.0 add_convert_fusion.3
  93.8 1.5 collective-permute-start.11
  95.4 1.3 collective-permute-start.16
  96.6 1.7 %collective-permute-start.12 = (bf16[2,16,128]{2,1,0:T(8,128)(2,1)S(1)}, bf16[2,16,128]{2,1,0:T(8,128)(2,1)S(1)}, u32[]{:S(2)}, u32[]{:S(2)}) collective-permute-start(bf16[2,16,128]{2,1,0:T(8,128)(2,1)S(1)} %get-tuple-element.19), channel_id=1, source_target_pairs={{8,0},{16,8},{24,16},{0,24},{9,1},{17,9},{25,17},{1,25},{10,2},{18... | collective-permute-start | bytes 24584 | tf_op jit(solution)/shard_map/ppermute | solution.py:27
  98.8 1.5 %collective-permute-done.12 = bf16[2,16,128]{2,1,0:T(8,128)(2,1)S(1)} collective-permute-done((bf16[2,16,128]{2,1,0:T(8,128)(2,1)S(1)}, bf16[2,16,128]{2,1,0:T(8,128)(2,1)S(1)}, u32[]{:S(2)}, u32[]{:S(2)}) %collective-permute-start.12) | collective-permute-done | bytes 8224 | tf_op jit(solution)/shard_map/ppermute | solution.py:27
  100.6 1.0 collective-permute-start.17
  102.8 1.4 fusion.99
  104.2 4.6 %collective-permute-start.14 = (bf16[1,18,16640]{2,1,0:T(8,128)(2,1)}, bf16[1,18,16640]{2,1,0:T(8,128)(2,1)S(1)}, u32[]{:S(2)}, u32[]{:S(2)}) collective-permute-start(bf16[1,18,16640]{2,1,0:T(8,128)(2,1)} %get-tuple-element.16), channel_id=1, source_target_pairs={{0,1},{1,2},{2,3},{4,5},{5,6},{6,7},{8,9},{9,10},{10,11},{12,13},{... | collective-permute-start | bytes 1797128 | tf_op jit(solution)/shard_map/ppermute | solution.py:126
  108.8 1.3 collective-permute-start.15
  110.7 9.6 %shard_map.96.refs_2_ = f32[2,16,16384]{2,1,0:T(8,128)} custom-call(bf16[2,18,16640]{2,1,0:T(8,128)(2,1)} %copy-done.3, f32[27,8,128]{2,1,0:T(8,128)} %broadcast_in_dim.36.refs_1_.refs_3_), custom_call_target="tpu_custom_call" | custom-call | tf_op jit(solution)/shard_map/pallas_call | solution.py:179
  120.4 2.7 %collective-permute-start.19 = (bf16[64,1024]{1,0:T(8,128)(2,1)S(1)}, bf16[64,1024]{1,0:T(8,128)(2,1)S(1)}, u32[]{:S(2)}, u32[]{:S(2)}) collective-permute-start(bf16[64,1024]{1,0:T(8,128)(2,1)S(1)} %add_convert_fusion.2), channel_id=1, source_target_pairs={{0,1},{1,0},{2,3},{3,2},{4,5},{5,4},{6,7},{7,6},{8,9},{9,8},{10,11... | collective-permute-start | bytes 393224 | tf_op jit(solution)/shard_map/ppermute | solution.py:107
  124.8 8.5 %collective-permute-done.19 = bf16[64,1024]{1,0:T(8,128)(2,1)S(1)} collective-permute-done((bf16[64,1024]{1,0:T(8,128)(2,1)S(1)}, bf16[64,1024]{1,0:T(8,128)(2,1)S(1)}, u32[]{:S(2)}, u32[]{:S(2)}) %collective-permute-start.19) | collective-permute-done | bytes 131104 | tf_op jit(solution)/shard_map/ppermute | solution.py:107
  133.3 2.9 %collective-permute-start.20 = (bf16[64,1024]{1,0:T(8,128)(2,1)S(1)}, bf16[64,1024]{1,0:T(8,128)(2,1)S(1)}, u32[]{:S(2)}, u32[]{:S(2)}) collective-permute-start(bf16[64,1024]{1,0:T(8,128)(2,1)S(1)} %add_convert_fusion.1), channel_id=1, source_target_pairs={{0,2},{1,3},{2,0},{3,1},{4,6},{5,7},{6,4},{7,5},{8,10},{9,11},{10,... | collective-permute-start | bytes 393224 | tf_op jit(solution)/shard_map/ppermute | solution.py:107
  136.9 2.7 %copy.38 = f32[32,256,64]{2,1,0:T(8,128)} copy(f32[32,256,64]{1,2,0:T(8,128)S(1)} %add_bitcast_fusion) | data formatting | bytes 4194304 | tf_op jit(solution)/shard_map/add | solution.py:218
  139.6 2.9 %reshape.96 = f32[2,16,16384]{2,1,0:T(8,128)S(1)} reshape(f32[32,256,64]{2,1,0:T(8,128)} %copy.38) | data formatting | bytes 4194304 | tf_op jit(solution)/shard_map/reshape | solution.py:302
  144.4 7.1 %shard_map.97 = f32[2,16,16384]{2,1,0:T(8,128)} custom-call(bf16[1,18,16640]{2,1,0:T(8,128)(2,1)} %copy-done.14, bf16[1,18,16640]{2,1,0:T(8,128)(2,1)} %collective-permute-done.15.refs_1_, f32[2,16,16384]{2,1,0:T(8,128)} %shard_map.96.refs_2_, f32[27,8,128]{2,1,0:T(8,128)} %broadcast_in_dim.36.refs_1_.refs_3_), custom_call_target="tpu_custom_call" | custom-call | tf_op jit(solution)/shard_map/pallas_call | solution.py:179
  151.5 2.7 %add_convert_fusion = bf16[2,16,16384]{2,1,0:T(8,128)(2,1)} fusion(f32[2,16,16384]{2,1,0:T(8,128)} %shard_map.97, f32[2,16,16384]{2,1,0:T(8,128)S(1)} %reshape.96), kind=kLoop, calls=%fused_computation.19 | loop fusion | flops 1048576 | bytes 5242880 | tf_op jit(solution)/shard_map/convert_element_type | solution.py:302
  (113 shorter events, 18.5 us)
Async XLA Ops:
  0.6 54.5 %copy-start = (bf16[64,256]{1,0:T(8,128)(2,1)S(1)}, bf16[64,256]{1,0:T(8,128)(2,1)}, u32[]{:S(2)}) copy-start(bf16[64,256]{1,0:T(8,128)(2,1)} %param.9) | copy-start | bytes 98308
  4.8 8.6 %copy-start.5 = (bf16[2,16,16384]{2,1,0:T(8,128)(2,1)S(1)}, bf16[2,16,16384]{2,1,0:T(8,128)(2,1)}, u32[]{:S(2)}) copy-start(bf16[2,16,16384]{2,1,0:T(8,128)(2,1)} %param.7) | copy-start | bytes 3145732
  5.0 18.4 %collective-permute-start = (f32[16,32,128]{2,0,1:T(8,128)S(1)}, f32[16,32,128]{2,0,1:T(8,128)}, u32[]{:S(2)}, u32[]{:S(2)}) collective-permute-start(f32[16,32,128]{2,0,1:T(8,128)S(1)} %fusion.15), channel_id=1, source_target_pairs={{0,16},{8,24},{16,0},{24,8},{1,17},{9,25},{17,1},{25,9},{2,18},{10... | collective-permute-start | bytes 786440 | tf_op jit(solution)/shard_map/ppermute | solution.py:90
  8.7 4.7 %collective-permute-start.2 = (bf16[2,16,128]{2,1,0:T(8,128)(2,1)S(1)}, bf16[2,16,128]{2,1,0:T(8,128)(2,1)S(1)}, u32[]{:S(2)}, u32[]{:S(2)}) collective-permute-start(bf16[2,16,128]{2,1,0:T(8,128)(2,1)S(1)} %get-tuple-element.22), channel_id=1, source_target_pairs={{0,8},{8,16},{16,24},{24,0},{1,9},{9,17},{17,25},{25,1},{2,10},{10... | collective-permute-start | bytes 24584 | tf_op jit(solution)/shard_map/ppermute | solution.py:26
  10.2 3.7 %collective-permute-start.3 = (bf16[2,16,128]{2,1,0:T(8,128)(2,1)S(1)}, bf16[2,16,128]{2,1,0:T(8,128)(2,1)S(1)}, u32[]{:S(2)}, u32[]{:S(2)}) collective-permute-start(bf16[2,16,128]{2,1,0:T(8,128)(2,1)S(1)} %get-tuple-element.21), channel_id=1, source_target_pairs={{8,0},{16,8},{24,16},{0,24},{9,1},{17,9},{25,17},{1,25},{10,2},{18... | collective-permute-start | bytes 24584 | tf_op jit(solution)/shard_map/ppermute | solution.py:27
  14.1 1.4 collective-permute-start.4
  16.3 8.1 %copy-start.2 = (bf16[2,18,16640]{2,1,0:T(8,128)(2,1)}, bf16[2,18,16640]{2,1,0:T(8,128)(2,1)S(1)}, u32[]{:S(2)}) copy-start(bf16[2,18,16640]{2,1,0:T(8,128)(2,1)S(1)} %pad_maximum_fusion.refs_0_) | copy-start | bytes 3594244
  16.4 10.3 %copy-start.7 = (bf16[2,16,16384]{2,1,0:T(8,128)(2,1)S(1)}, bf16[2,16,16384]{2,1,0:T(8,128)(2,1)}, u32[]{:S(2)}) copy-start(bf16[2,16,16384]{2,1,0:T(8,128)(2,1)} %param.13) | copy-start | bytes 3145732
  17.6 25.9 %collective-permute-start.5 = (bf16[1,18,16640]{2,1,0:T(8,128)(2,1)}, bf16[1,18,16640]{2,1,0:T(8,128)(2,1)}, u32[]{:S(2)}, u32[]{:S(2)}) collective-permute-start(bf16[1,18,16640]{2,1,0:T(8,128)(2,1)} %get-tuple-element.18), channel_id=1, source_target_pairs={{0,1},{1,2},{2,3},{4,5},{5,6},{6,7},{8,9},{9,10},{10,11},{12,13},{... | collective-permute-start | bytes 1797128 | tf_op jit(solution)/shard_map/ppermute | solution.py:126
  22.0 21.8 %collective-permute-start.6 = (bf16[1,18,16640]{2,1,0:T(8,128)(2,1)}, bf16[1,18,16640]{2,1,0:T(8,128)(2,1)}, u32[]{:S(2)}, u32[]{:S(2)}) collective-permute-start(bf16[1,18,16640]{2,1,0:T(8,128)(2,1)} %get-tuple-element.17), channel_id=1, source_target_pairs={{1,0},{2,1},{3,2},{5,4},{6,5},{7,6},{9,8},{10,9},{11,10},{13,12},{... | collective-permute-start | bytes 1797128 | tf_op jit(solution)/shard_map/ppermute | solution.py:127
  24.5 2.2 %copy-start.11 = (f32[16,32,128]{2,0,1:T(8,128)}, f32[16,32,128]{2,0,1:T(8,128)S(1)}, u32[]{:S(2)}) copy-start(f32[16,32,128]{2,0,1:T(8,128)S(1)} %fusion.17) | copy-start | bytes 786436
  25.2 17.3 %collective-permute-start.1 = (f32[8,32,128]{2,0,1:T(8,128)}, f32[8,32,128]{2,0,1:T(8,128)}, u32[]{:S(2)}, u32[]{:S(2)}) collective-permute-start(f32[8,32,128]{2,0,1:T(8,128)} %constant_dynamic-slice_fusion.1), channel_id=1, source_target_pairs={{0,8},{8,0},{16,24},{24,16},{1,9},{9,1},{17,25},{25,17},{2,10},{10... | collective-permute-start | bytes 393224 | tf_op jit(solution)/shard_map/ppermute | solution.py:90
  29.2 1.6 %copy-start.6 = (bf16[32,64,64]{2,1,0:T(8,128)(2,1)S(1)}, bf16[32,64,64]{2,1,0:T(8,128)(2,1)}, u32[]{:S(2)}) copy-start(bf16[32,64,64]{2,1,0:T(8,128)(2,1)} %param.12) | copy-start | bytes 786436
  29.2 1.8 %copy-start.15 = (bf16[27,64]{1,0:T(8,128)(2,1)S(1)}, bf16[27,64]{1,0:T(8,128)(2,1)}, u32[]{:S(2)}) copy-start(bf16[27,64]{1,0:T(8,128)(2,1)} %param.8) | copy-start | bytes 10372
  32.2 10.3 %copy-start.12 = (f32[16,32,128]{2,0,1:T(8,128)S(1)}, f32[16,32,128]{2,0,1:T(8,128)}, u32[]{:S(2)}) copy-start(f32[16,32,128]{2,0,1:T(8,128)} %copy-done.11) | copy-start | bytes 786436
  50.6 9.1 %collective-permute-start.7 = (bf16[8,32,128]{2,1,0:T(8,128)(2,1)S(1)}, bf16[8,32,128]{2,1,0:T(8,128)(2,1)S(1)}, u32[]{:S(2)}, u32[]{:S(2)}) collective-permute-start(bf16[8,32,128]{2,1,0:T(8,128)(2,1)S(1)} %convolution_convert_fusion.2), channel_id=1, source_target_pairs={{0,8},{8,0},{16,24},{24,16},{1,9},{9,1},{17,25},{25,17},{2,10},{10... | collective-permute-start | bytes 196616 | tf_op jit(solution)/shard_map/ppermute | solution.py:68
  55.1 1.2 copy-start.16
  56.4 3.3 %copy-start.4 = (f32[8192,256]{1,0:T(8,128)}, f32[8192,256]{1,0:T(8,128)S(1)}, u32[]{:S(2)}) copy-start(f32[8192,256]{1,0:T(8,128)S(1)} %fusion.105) | copy-start | bytes 25165828
  59.6 5.8 %copy-start.8 = (bf16[32,256,64]{1,2,0:T(8,128)(2,1)S(1)}, bf16[32,256,64]{1,2,0:T(8,128)(2,1)}, u32[]{:S(2)}) copy-start(bf16[32,256,64]{1,2,0:T(8,128)(2,1)} %copy.30) | copy-start | bytes 3145732
  59.7 5.0 %collective-permute-start.8 = (bf16[16,32,128]{2,1,0:T(8,128)(2,1)S(1)}, bf16[16,32,128]{2,1,0:T(8,128)(2,1)S(1)}, u32[]{:S(2)}, u32[]{:S(2)}) collective-permute-start(bf16[16,32,128]{2,1,0:T(8,128)(2,1)S(1)} %pad_maximum_fusion.3), channel_id=1, source_target_pairs={{0,16},{8,24},{16,0},{24,8},{1,17},{9,25},{17,1},{25,9},{2,18},{10... | collective-permute-start | bytes 393224 | tf_op jit(solution)/shard_map/ppermute | solution.py:68
  69.7 6.4 %collective-permute-start.9 = (f32[16,32,128]{2,0,1:T(8,128)S(1)}, f32[16,32,128]{2,0,1:T(8,128)S(1)}, u32[]{:S(2)}, u32[]{:S(2)}) collective-permute-start(f32[16,32,128]{2,0,1:T(8,128)S(1)} %fusion.12), channel_id=1, source_target_pairs={{0,16},{8,24},{16,0},{24,8},{1,17},{9,25},{17,1},{25,9},{2,18},{10... | collective-permute-start | bytes 786440 | tf_op jit(solution)/shard_map/ppermute | solution.py:90
  76.3 1.3 copy-start.13
  77.0 15.0 %collective-permute-start.10 = (f32[8,32,128]{2,0,1:T(8,128)}, f32[8,32,128]{2,0,1:T(8,128)}, u32[]{:S(2)}, u32[]{:S(2)}) collective-permute-start(f32[8,32,128]{2,0,1:T(8,128)} %constant_dynamic-slice_fusion), channel_id=1, source_target_pairs={{0,8},{8,0},{16,24},{24,16},{1,9},{9,1},{17,25},{25,17},{2,10},{10... | collective-permute-start | bytes 393224 | tf_op jit(solution)/shard_map/ppermute | solution.py:90
  77.6 7.9 %copy-start.9 = (bf16[32,256,64]{1,2,0:T(8,128)(2,1)S(1)}, bf16[32,256,64]{1,2,0:T(8,128)(2,1)}, u32[]{:S(2)}) copy-start(bf16[32,256,64]{1,2,0:T(8,128)(2,1)} %get-tuple-element.14) | copy-start | bytes 3145732
  86.5 2.5 %copy-start.10 = (bf16[8192,64]{0,1:T(8,128)(2,1)S(1)}, bf16[8192,64]{0,1:T(8,128)(2,1)}, u32[]{:S(2)}) copy-start(bf16[8192,64]{0,1:T(8,128)(2,1)} %convolution_convert_fusion) | copy-start | bytes 3145732
  93.8 4.8 %collective-permute-start.11 = (bf16[2,16,128]{2,1,0:T(8,128)(2,1)S(1)}, bf16[2,16,128]{2,1,0:T(8,128)(2,1)S(1)}, u32[]{:S(2)}, u32[]{:S(2)}) collective-permute-start(bf16[2,16,128]{2,1,0:T(8,128)(2,1)S(1)} %get-tuple-element.20), channel_id=1, source_target_pairs={{0,8},{8,16},{16,24},{24,0},{1,9},{9,17},{17,25},{25,1},{2,10},{10... | collective-permute-start | bytes 24584 | tf_op jit(solution)/shard_map/ppermute | solution.py:26
  95.4 5.2 %collective-permute-start.16 = (bf16[8,32,128]{2,1,0:T(8,128)(2,1)S(1)}, bf16[8,32,128]{2,1,0:T(8,128)(2,1)S(1)}, u32[]{:S(2)}, u32[]{:S(2)}) collective-permute-start(bf16[8,32,128]{2,1,0:T(8,128)(2,1)S(1)} %convolution_convert_fusion.1), channel_id=1, source_target_pairs={{0,8},{8,0},{16,24},{24,16},{1,9},{9,1},{17,25},{25,17},{2,10},{10... | collective-permute-start | bytes 196616 | tf_op jit(solution)/shard_map/ppermute | solution.py:68
  96.6 3.7 %collective-permute-start.12 = (bf16[2,16,128]{2,1,0:T(8,128)(2,1)S(1)}, bf16[2,16,128]{2,1,0:T(8,128)(2,1)S(1)}, u32[]{:S(2)}, u32[]{:S(2)}) collective-permute-start(bf16[2,16,128]{2,1,0:T(8,128)(2,1)S(1)} %get-tuple-element.19), channel_id=1, source_target_pairs={{8,0},{16,8},{24,16},{0,24},{9,1},{17,9},{25,17},{1,25},{10,2},{18... | collective-permute-start | bytes 24584 | tf_op jit(solution)/shard_map/ppermute | solution.py:27
  98.6 21.8 %collective-permute-start.18 = (bf16[64,1024]{1,0:T(8,128)(2,1)S(1)}, bf16[64,1024]{1,0:T(8,128)(2,1)S(1)}, u32[]{:S(2)}, u32[]{:S(2)}) collective-permute-start(bf16[64,1024]{1,0:T(8,128)(2,1)S(1)} %convert_element_type.139), channel_id=1, source_target_pairs={{0,4},{4,0},{1,5},{5,1},{2,6},{6,2},{3,7},{7,3},{8,12},{12,8},{9,1... | collective-permute-start | bytes 393224 | tf_op jit(solution)/shard_map/ppermute | solution.py:107
  100.5 1.4 collective-permute-start.13
  100.6 22.5 %collective-permute-start.17 = (bf16[16,32,128]{2,1,0:T(8,128)(2,1)S(1)}, bf16[16,32,128]{2,1,0:T(8,128)(2,1)}, u32[]{:S(2)}, u32[]{:S(2)}) collective-permute-start(bf16[16,32,128]{2,1,0:T(8,128)(2,1)S(1)} %pad_maximum_fusion.4), channel_id=1, source_target_pairs={{0,16},{8,24},{16,0},{24,8},{1,17},{9,25},{17,1},{25,9},{2,18},{10... | collective-permute-start | bytes 393224 | tf_op jit(solution)/shard_map/ppermute | solution.py:68
  102.8 8.0 %copy-start.3 = (bf16[2,18,16640]{2,1,0:T(8,128)(2,1)}, bf16[2,18,16640]{2,1,0:T(8,128)(2,1)S(1)}, u32[]{:S(2)}) copy-start(bf16[2,18,16640]{2,1,0:T(8,128)(2,1)S(1)} %pad_maximum_fusion.1.refs_0_) | copy-start | bytes 3594244
  104.2 39.3 %collective-permute-start.14 = (bf16[1,18,16640]{2,1,0:T(8,128)(2,1)}, bf16[1,18,16640]{2,1,0:T(8,128)(2,1)S(1)}, u32[]{:S(2)}, u32[]{:S(2)}) collective-permute-start(bf16[1,18,16640]{2,1,0:T(8,128)(2,1)} %get-tuple-element.16), channel_id=1, source_target_pairs={{0,1},{1,2},{2,3},{4,5},{5,6},{6,7},{8,9},{9,10},{10,11},{12,13},{... | collective-permute-start | bytes 1797128 | tf_op jit(solution)/shard_map/ppermute | solution.py:126
  108.8 34.7 %collective-permute-start.15 = (bf16[1,18,16640]{2,1,0:T(8,128)(2,1)}, bf16[1,18,16640]{2,1,0:T(8,128)(2,1)}, u32[]{:S(2)}, u32[]{:S(2)}) collective-permute-start(bf16[1,18,16640]{2,1,0:T(8,128)(2,1)} %get-tuple-element.15), channel_id=1, source_target_pairs={{1,0},{2,1},{3,2},{5,4},{6,5},{7,6},{9,8},{10,9},{11,10},{13,12},{... | collective-permute-start | bytes 1797128 | tf_op jit(solution)/shard_map/ppermute | solution.py:127
  120.4 12.9 %collective-permute-start.19 = (bf16[64,1024]{1,0:T(8,128)(2,1)S(1)}, bf16[64,1024]{1,0:T(8,128)(2,1)S(1)}, u32[]{:S(2)}, u32[]{:S(2)}) collective-permute-start(bf16[64,1024]{1,0:T(8,128)(2,1)S(1)} %add_convert_fusion.2), channel_id=1, source_target_pairs={{0,1},{1,0},{2,3},{3,2},{4,5},{5,4},{6,7},{7,6},{8,9},{9,8},{10,11... | collective-permute-start | bytes 393224 | tf_op jit(solution)/shard_map/ppermute | solution.py:107
  133.3 9.2 %collective-permute-start.20 = (bf16[64,1024]{1,0:T(8,128)(2,1)S(1)}, bf16[64,1024]{1,0:T(8,128)(2,1)S(1)}, u32[]{:S(2)}, u32[]{:S(2)}) collective-permute-start(bf16[64,1024]{1,0:T(8,128)(2,1)S(1)} %add_convert_fusion.1), channel_id=1, source_target_pairs={{0,2},{1,3},{2,0},{3,1},{4,6},{5,7},{6,4},{7,5},{8,10},{9,11},{10,... | collective-permute-start | bytes 393224 | tf_op jit(solution)/shard_map/ppermute | solution.py:107
  143.5 0.9 copy-start.14
  144.4 9.8 %copy-start.1 = (bf16[64,256]{1,0:T(8,128)(2,1)S(1)}, bf16[64,256]{1,0:T(8,128)(2,1)}, u32[]{:S(2)}) copy-start(bf16[64,256]{1,0:T(8,128)(2,1)} %param.9) | copy-start | bytes 98308

commit v16 on v15

--- a/solution.py
+++ b/solution.py
@@ -296,10 +296,12 @@
     local_grads = split_gradients(dblock, channels)
     dmode, local_grads, grad_act = lax.optimization_barrier((dmode, local_grads, grad_act))
     spectral_grad = share_inverse(dmode, cos_order, sin_order, channels)
+    spectral_grad = spectral_grad.reshape(planes, y_cells, merged)
+    spectral_grad, local_grads = lax.optimization_barrier((spectral_grad, local_grads))
     grad_spec = sum_gradients(local_grads)
     padded_grad = spatial_rims(grad_act, channels)
     grad_local = depthwise(padded_grad, depth_weight, True, x_cells, channels)
-    grad_features = (grad_local + spectral_grad.reshape(planes, y_cells, merged)).astype(
+    grad_features = (grad_local + spectral_grad).astype(
         jnp.bfloat16
     )
     return (output, grad_features, grad_spec)

time: 155 us -> 163 us (1.052)
  waiting for transfers between devices: 21 us -> 25.4 us
  local copies, waits for them, and re-layouts: 33.8 us -> 36.4 us
  other arithmetic: 10 us -> 11.9 us
    ppermute x4, waiting for transfers between devices: 3.44 us -> 7.81 us  [ring_gather(): lax.ppermute(block, axis, [(i, i ^ step) for i in range(size)])]
    ppermute x2, starting transfers between devices: 8.98 us -> 6.33 us  [spatial_rims(): below = lax.ppermute(inner[-1:], 'gz', up)]
    ppermute x3, starting transfers between devices: 5.7 us -> 7.83 us  [butterfly_sum(): lax.ppermute(value, axis, [(i, i ^ step) for i in range(size)])]
  transfers between devices with their start and end apart: 21 -> 21, of which waited for: 9 -> 11; matrix products, arithmetic and copies ran while one was open for 31% -> 26% of each run, Pallas kernels for 12% -> 12%
where the time goes in v16:
time: 163 us
  local copies, waits for them, and re-layouts  36.4 us (22%)
  starting transfers between devices  35.4 us (22%)
  Pallas kernels  33.1 us (20%)
  waiting for transfers between devices  25.4 us (16%)
  matrix products  19.5 us (12%)
  other arithmetic  11.9 us (7%)
    pallas_call x4, Pallas kernels, stencil_call(): pl.pallas_call(kernel, out_shape=jax.ShapeDtypeStruct((len(plan), y_cells...  33.1 us
    ppermute x3, starting transfers between devices, butterfly_sum(): lax.ppermute(value, axis, [(i, i ^ step) for i in range(size)])  7.83 us
    ppermute x4, waiting for transfers between devices, ring_gather(): lax.ppermute(block, axis, [(i, i ^ step) for i in range(size)])  7.81 us
    dot_general x1, matrix products, per_device(): jnp.dot(grad_hidden, expand_weight.T, preferred_element_type=jnp.float32)  7.81 us
    ppermute x3, waiting for transfers between devices, butterfly_sum(): lax.ppermute(value, axis, [(i, i ^ step) for i in range(size)])  7.22 us
    ppermute x4, starting transfers between devices, ring_reduce_scatter(): lax.ppermute(send, axis, [(i, i ^ step) for i in range(size)])  6.64 us
    ppermute x2, starting transfers between devices, spatial_rims(): below = lax.ppermute(inner[-1:], 'gz', up)  6.33 us
    ppermute x4, starting transfers between devices, ring_gather(): lax.ppermute(block, axis, [(i, i ^ step) for i in range(size)])  5.36 us
  transfers between devices with their start and end apart: 21, of which 11 were waited for; matrix products, arithmetic and copies ran while one was open for 26% of the time, Pallas kernels for 12%

profile of v16, /device:TPU:0, one launch (start us, length us, event | category | flops | bytes accessed | tf_op | source)
XLA Modules:
  0.0 162.8 jit_solution(5522313831988299433)
XLA Ops:
  0.7 3.0 %reshape.89 = bf16[32,256,64]{2,1,0:T(8,128)(2,1)S(1)} reshape(bf16[2,16,16384]{2,1,0:T(8,128)(2,1)} %param.7) | data formatting | bytes 2097152 | tf_op jit(solution)/shard_map/reshape | solution.py:258
  5.0 3.0 %collective-permute-start = (f32[16,32,128]{2,0,1:T(8,128)S(1)}, f32[16,32,128]{2,0,1:T(8,128)S(1)}, u32[]{:S(2)}, u32[]{:S(2)}) collective-permute-start(f32[16,32,128]{2,0,1:T(8,128)S(1)} %fusion.15), channel_id=1, source_target_pairs={{0,16},{8,24},{16,0},{24,8},{1,17},{9,25},{17,1},{25,9},{2,18},{10... | collective-permute-start | bytes 786440 | tf_op jit(solution)/shard_map/ppermute | solution.py:90
  8.7 1.5 collective-permute-start.2
  10.2 1.4 collective-permute-start.3
  11.7 1.7 %collective-permute-done.2 = bf16[2,16,128]{2,1,0:T(8,128)(2,1)S(1)} collective-permute-done((bf16[2,16,128]{2,1,0:T(8,128)(2,1)S(1)}, bf16[2,16,128]{2,1,0:T(8,128)(2,1)S(1)}, u32[]{:S(2)}, u32[]{:S(2)}) %collective-permute-start.2) | collective-permute-done | bytes 8224 | tf_op jit(solution)/shard_map/ppermute | solution.py:26
  13.9 1.0 copy-done.10
  15.3 1.2 collective-permute-done.4
  16.7 1.8 %pad_maximum_fusion.refs_0_ = bf16[2,18,16640]{2,1,0:T(8,128)(2,1)S(1)} fusion(bf16[2,1,16640]{2,1,0:T(2,128)(2,1)S(1)} %get-tuple-element.36, bf16[2,16,16640]{2,1,0:T(8,128)(2,1)} %copy-done.10, bf16[2,1,16640]{2,1,0:T(2,128)(2,1)S(1)} %get-tuple-element.35), kind=kLoop, calls=%fused_computation.23 | loop fusion | flops 3594240 | bytes 2396160 | tf_op jit(solution)/shard_map/concatenate | solution.py:28
  18.6 1.4 fusion.100
  20.0 4.4 %collective-permute-start.5 = (bf16[1,18,16640]{2,1,0:T(8,128)(2,1)}, bf16[1,18,16640]{2,1,0:T(8,128)(2,1)}, u32[]{:S(2)}, u32[]{:S(2)}) collective-permute-start(bf16[1,18,16640]{2,1,0:T(8,128)(2,1)} %get-tuple-element.22), channel_id=1, source_target_pairs={{0,1},{1,2},{2,3},{4,5},{5,6},{6,7},{8,9},{9,10},{10,11},{12,13},{... | collective-permute-start | bytes 1797128 | tf_op jit(solution)/shard_map/ppermute | solution.py:126
  24.3 1.3 collective-permute-start.6
  26.6 1.5 collective-permute-start.1
  28.0 3.0 %reshape.93 = bf16[32,256,64]{2,1,0:T(8,128)(2,1)S(1)} reshape(bf16[2,16,16384]{2,1,0:T(8,128)(2,1)} %param.13) | data formatting | bytes 2097152 | tf_op jit(solution)/shard_map/reshape | solution.py:278
  31.1 1.6 copy.30
  33.0 1.1 fusion.19
  34.8 9.6 %shard_map.94.refs_2_ = f32[2,16,16384]{2,1,0:T(8,128)} custom-call(bf16[2,18,16640]{2,1,0:T(8,128)(2,1)} %copy-done.2, f32[27,8,128]{2,1,0:T(8,128)} %broadcast_in_dim.18.refs_1_.refs_3_), custom_call_target="tpu_custom_call" | custom-call | tf_op jit(solution)/shard_map/pallas_call | solution.py:179
  46.1 6.7 %shard_map.95 = bf16[2,16,16384]{2,1,0:T(8,128)(2,1)} custom-call(bf16[1,18,16640]{2,1,0:T(8,128)(2,1)} %collective-permute-done.5.refs_0_, bf16[1,18,16640]{2,1,0:T(8,128)(2,1)} %collective-permute-done.6.refs_1_, f32[2,16,16384]{2,1,0:T(8,128)} %shard_map.94.refs_2_, f32[27,8,128]{2,1,0:T(8,128)} %broadcast_in_dim.18.refs_1_.refs_3_), custom_call_target="tpu_custom_call" | custom-call | tf_op jit(solution)/shard_map/pallas_call | solution.py:179
  52.9 1.5 collective-permute-start.7
  54.4 3.0 %reshape.90 = bf16[8192,64]{1,0:T(8,128)(2,1)S(1)} reshape(bf16[2,16,16384]{2,1,0:T(8,128)(2,1)} %shard_map.95) | data formatting | bytes 2097152 | tf_op jit(solution)/shard_map/reshape | solution.py:267
  57.4 1.2 fusion.105
  58.7 2.8 %fusion.5 = f32[8192,64]{0,1:T(8,128)S(1)} fusion(bf16[256,64]{0,1:T(8,128)(2,1)S(1)} %copy-done.18, f32[8192,256]{1,0:T(8,128)S(1)} %fusion.105), kind=kOutput, calls=%fused_computation.10 | convolution fusion | flops 278921216 | bytes 10518528 | tf_op jit(solution)/shard_map/dot_general | solution.py:270
  62.0 1.6 collective-permute-start.8
  63.6 3.4 %collective-permute-done.8 = bf16[16,32,128]{2,1,0:T(8,128)(2,1)S(1)} collective-permute-done((bf16[16,32,128]{2,1,0:T(8,128)(2,1)S(1)}, bf16[16,32,128]{2,1,0:T(8,128)(2,1)S(1)}, u32[]{:S(2)}, u32[]{:S(2)}) %collective-permute-start.8) | collective-permute-done | bytes 131104 | tf_op jit(solution)/shard_map/ppermute | solution.py:68
  67.8 2.7 %fusion.11 = (bf16[32,256,64]{1,2,0:T(8,128)(2,1)S(1)}, bf16[32,256,64]{1,2,0:T(8,128)(2,1)}) fusion(bf16[32,256,64]{1,2,0:T(8,128)(2,1)S(1)} %copy-done.12, f32[256,32,64]{0,2,1:T(8,128)S(1)} %fusion.26, bf16[32,32,64]{2,1,0:T(8,128)(2,1)S(1)} %get-tuple-element.31, f32[32]{0:T(128)S(1)} %get-tuple-element.37, s32[32]{0:T(128)S(1)} %add.140, ...), kind=kOutput, calls=%fused_computation.17 | convolution fusion | flops 41566208 | bytes 7472384 | tf_op jit(solution)/shard_map/krc,xk->rxc/dot_general | solution.py:215
  71.9 1.6 collective-permute-start.9
  73.6 4.8 %collective-permute-done.9 = f32[16,32,128]{2,0,1:T(8,128)S(1)} collective-permute-done((f32[16,32,128]{2,0,1:T(8,128)S(1)}, f32[16,32,128]{2,0,1:T(8,128)S(1)}, u32[]{:S(2)}, u32[]{:S(2)}) %collective-permute-start.9) | collective-permute-done | bytes 262176 | tf_op jit(solution)/shard_map/ppermute | solution.py:90
  79.8 7.8 %convolution_convert_fusion = bf16[8192,64]{0,1:T(8,128)(2,1)S(1)} fusion(bf16[64,256]{1,0:T(8,128)(2,1)S(1)} %copy-done, bf16[8192,64]{0,1:T(8,128)(2,1)S(1)} %bitcast.54, bf16[256,64]{0,1:T(8,128)(2,1)S(1)} %copy-done.19, f32[8192,256]{1,0:T(8,128)} %copy-done.4), kind=kOutput, calls=%fused_computation.3 | convolution fusion | flops 558366720 | bytes 10551296 | tf_op jit(solution)/shard_map/dot_general | solution.py:287
  87.6 1.1 copy.35
  88.7 1.9 %reshape.95 = bf16[2,16,16384]{2,1,0:T(8,128)(2,1)S(1)} reshape(bf16[8192,64]{1,0:T(8,128)(2,1)S(1)} %copy.35) | data formatting | bytes 2097152 | tf_op jit(solution)/shard_map/reshape | solution.py:290
  92.4 1.5 collective-permute-start.11
  95.0 2.0 %collective-permute-start.12 = (bf16[2,16,128]{2,1,0:T(8,128)(2,1)S(1)}, bf16[2,16,128]{2,1,0:T(8,128)(2,1)S(1)}, u32[]{:S(2)}, u32[]{:S(2)}) collective-permute-start(bf16[2,16,128]{2,1,0:T(8,128)(2,1)S(1)} %get-tuple-element.23), channel_id=1, source_target_pairs={{8,0},{16,8},{24,16},{0,24},{9,1},{17,9},{25,17},{1,25},{10,2},{18... | collective-permute-start | bytes 24584 | tf_op jit(solution)/shard_map/ppermute | solution.py:27
  97.1 1.5 collective-permute-done.12
  98.9 1.3 collective-permute-start.17
  100.5 4.4 %collective-permute-done.17 = bf16[16,32,128]{2,1,0:T(8,128)(2,1)S(1)} collective-permute-done((bf16[16,32,128]{2,1,0:T(8,128)(2,1)S(1)}, bf16[16,32,128]{2,1,0:T(8,128)(2,1)S(1)}, u32[]{:S(2)}, u32[]{:S(2)}) %collective-permute-start.17) | collective-permute-done | bytes 131104 | tf_op jit(solution)/shard_map/ppermute | solution.py:68
  106.3 2.7 %copy.38 = f32[32,256,64]{2,1,0:T(8,128)} copy(f32[32,256,64]{1,2,0:T(8,128)S(1)} %add_bitcast_fusion) | data formatting | bytes 4194304 | tf_op jit(solution)/shard_map/add | solution.py:218
  109.0 4.0 %reshape.96 = f32[2,16,16384]{2,1,0:T(8,128)} reshape(f32[32,256,64]{2,1,0:T(8,128)} %copy.38) | data formatting | bytes 4194304 | tf_op jit(solution)/shard_map/reshape | solution.py:299
  114.7 2.6 %collective-permute-start.19 = (bf16[64,1024]{1,0:T(8,128)(2,1)S(1)}, bf16[64,1024]{1,0:T(8,128)(2,1)S(1)}, u32[]{:S(2)}, u32[]{:S(2)}) collective-permute-start(bf16[64,1024]{1,0:T(8,128)(2,1)S(1)} %add_convert_fusion.2), channel_id=1, source_target_pairs={{0,1},{1,0},{2,3},{3,2},{4,5},{5,4},{6,7},{7,6},{8,9},{9,8},{10,11... | collective-permute-start | bytes 393224 | tf_op jit(solution)/shard_map/ppermute | solution.py:107
  117.3 1.3 fusion.99
  118.5 2.0 %collective-permute-start.14 = (bf16[1,18,16640]{2,1,0:T(8,128)(2,1)}, bf16[1,18,16640]{2,1,0:T(8,128)(2,1)S(1)}, u32[]{:S(2)}, u32[]{:S(2)}) collective-permute-start(bf16[1,18,16640]{2,1,0:T(8,128)(2,1)} %get-tuple-element.20), channel_id=1, source_target_pairs={{0,1},{1,2},{2,3},{4,5},{5,6},{6,7},{8,9},{9,10},{10,11},{12,13},{... | collective-permute-start | bytes 1797128 | tf_op jit(solution)/shard_map/ppermute | solution.py:126
  120.5 1.3 collective-permute-start.15
  122.5 5.2 %collective-permute-start.20 = (bf16[64,1024]{1,0:T(8,128)(2,1)}, bf16[64,1024]{1,0:T(8,128)(2,1)}, u32[]{:S(2)}, u32[]{:S(2)}) collective-permute-start(bf16[64,1024]{1,0:T(8,128)(2,1)} %add_convert_fusion.1), channel_id=1, source_target_pairs={{0,2},{1,3},{2,0},{3,1},{4,6},{5,7},{6,4},{7,5},{8,10},{9,11},{10,... | collective-permute-start | bytes 393224 | tf_op jit(solution)/shard_map/ppermute | solution.py:107
  127.8 1.9 %copy.29 = bf16[32,256,64]{2,1,0:T(8,128)(2,1)} copy(bf16[32,256,64]{1,2,0:T(8,128)(2,1)S(1)} %copy-done.11) | data formatting | bytes 2097152 | tf_op jit(solution)/shard_map/convert_element_type | solution.py:276
  129.6 3.7 %reshape.92 = bf16[2,16,16384]{2,1,0:T(8,128)(2,1)} reshape(bf16[32,256,64]{2,1,0:T(8,128)(2,1)} %copy.29) | data formatting | bytes 2097152 | tf_op jit(solution)/shard_map/reshape | solution.py:276
  134.0 9.6 %shard_map.96.refs_2_ = f32[2,16,16384]{2,1,0:T(8,128)} custom-call(bf16[2,18,16640]{2,1,0:T(8,128)(2,1)} %copy-done.3, f32[27,8,128]{2,1,0:T(8,128)} %broadcast_in_dim.36.refs_1_.refs_3_), custom_call_target="tpu_custom_call" | custom-call | tf_op jit(solution)/shard_map/pallas_call | solution.py:179
  143.6 6.5 %collective-permute-done.20 = bf16[64,1024]{1,0:T(8,128)(2,1)} collective-permute-done((bf16[64,1024]{1,0:T(8,128)(2,1)}, bf16[64,1024]{1,0:T(8,128)(2,1)}, u32[]{:S(2)}, u32[]{:S(2)}) %collective-permute-start.20) | collective-permute-done | bytes 131104 | tf_op jit(solution)/shard_map/ppermute | solution.py:107
  150.1 1.0 convert_add_fusion
  153.0 7.1 %shard_map.97 = f32[2,16,16384]{2,1,0:T(8,128)} custom-call(bf16[1,18,16640]{2,1,0:T(8,128)(2,1)} %copy-done.16, bf16[1,18,16640]{2,1,0:T(8,128)(2,1)} %collective-permute-done.15.refs_1_, f32[2,16,16384]{2,1,0:T(8,128)} %shard_map.96.refs_2_, f32[27,8,128]{2,1,0:T(8,128)} %broadcast_in_dim.36.refs_1_.refs_3_), custom_call_target="tpu_custom_call" | custom-call | tf_op jit(solution)/shard_map/pallas_call | solution.py:179
  160.1 2.7 %add_convert_fusion = bf16[2,16,16384]{2,1,0:T(8,128)(2,1)} fusion(f32[2,16,16384]{2,1,0:T(8,128)} %shard_map.97, f32[2,16,16384]{2,1,0:T(8,128)S(1)} %copy-done.5), kind=kLoop, calls=%fused_computation.19 | loop fusion | flops 1048576 | bytes 5242880 | tf_op jit(solution)/shard_map/convert_element_type | solution.py:304
  (119 shorter events, 20.7 us)
Async XLA Ops:
  0.6 56.8 %copy-start = (bf16[64,256]{1,0:T(8,128)(2,1)S(1)}, bf16[64,256]{1,0:T(8,128)(2,1)}, u32[]{:S(2)}) copy-start(bf16[64,256]{1,0:T(8,128)(2,1)} %param.9) | copy-start | bytes 98308
  4.8 8.6 %copy-start.6 = (bf16[2,16,16384]{2,1,0:T(8,128)(2,1)S(1)}, bf16[2,16,16384]{2,1,0:T(8,128)(2,1)}, u32[]{:S(2)}) copy-start(bf16[2,16,16384]{2,1,0:T(8,128)(2,1)} %param.7) | copy-start | bytes 3145732
  5.0 20.7 %collective-permute-start = (f32[16,32,128]{2,0,1:T(8,128)S(1)}, f32[16,32,128]{2,0,1:T(8,128)S(1)}, u32[]{:S(2)}, u32[]{:S(2)}) collective-permute-start(f32[16,32,128]{2,0,1:T(8,128)S(1)} %fusion.15), channel_id=1, source_target_pairs={{0,16},{8,24},{16,0},{24,8},{1,17},{9,25},{17,1},{25,9},{2,18},{10... | collective-permute-start | bytes 786440 | tf_op jit(solution)/shard_map/ppermute | solution.py:90
  8.7 4.7 %collective-permute-start.2 = (bf16[2,16,128]{2,1,0:T(8,128)(2,1)S(1)}, bf16[2,16,128]{2,1,0:T(8,128)(2,1)S(1)}, u32[]{:S(2)}, u32[]{:S(2)}) collective-permute-start(bf16[2,16,128]{2,1,0:T(8,128)(2,1)S(1)} %get-tuple-element.26), channel_id=1, source_target_pairs={{0,8},{8,16},{16,24},{24,0},{1,9},{9,17},{17,25},{25,1},{2,10},{10... | collective-permute-start | bytes 24584 | tf_op jit(solution)/shard_map/ppermute | solution.py:26
  10.2 3.7 %collective-permute-start.3 = (bf16[2,16,128]{2,1,0:T(8,128)(2,1)S(1)}, bf16[2,16,128]{2,1,0:T(8,128)(2,1)S(1)}, u32[]{:S(2)}, u32[]{:S(2)}) collective-permute-start(bf16[2,16,128]{2,1,0:T(8,128)(2,1)S(1)} %get-tuple-element.25), channel_id=1, source_target_pairs={{8,0},{16,8},{24,16},{0,24},{9,1},{17,9},{25,17},{1,25},{10,2},{18... | collective-permute-start | bytes 24584 | tf_op jit(solution)/shard_map/ppermute | solution.py:27
  13.9 1.0 copy-start.10
  15.1 1.4 collective-permute-start.4
  18.6 7.2 %copy-start.2 = (bf16[2,18,16640]{2,1,0:T(8,128)(2,1)}, bf16[2,18,16640]{2,1,0:T(8,128)(2,1)S(1)}, u32[]{:S(2)}) copy-start(bf16[2,18,16640]{2,1,0:T(8,128)(2,1)S(1)} %pad_maximum_fusion.refs_0_) | copy-start | bytes 3594244
  20.0 25.5 %collective-permute-start.5 = (bf16[1,18,16640]{2,1,0:T(8,128)(2,1)}, bf16[1,18,16640]{2,1,0:T(8,128)(2,1)}, u32[]{:S(2)}, u32[]{:S(2)}) collective-permute-start(bf16[1,18,16640]{2,1,0:T(8,128)(2,1)} %get-tuple-element.22), channel_id=1, source_target_pairs={{0,1},{1,2},{2,3},{4,5},{5,6},{6,7},{8,9},{9,10},{10,11},{12,13},{... | collective-permute-start | bytes 1797128 | tf_op jit(solution)/shard_map/ppermute | solution.py:126
  24.3 21.8 %collective-permute-start.6 = (bf16[1,18,16640]{2,1,0:T(8,128)(2,1)}, bf16[1,18,16640]{2,1,0:T(8,128)(2,1)}, u32[]{:S(2)}, u32[]{:S(2)}) collective-permute-start(bf16[1,18,16640]{2,1,0:T(8,128)(2,1)} %get-tuple-element.21), channel_id=1, source_target_pairs={{1,0},{2,1},{3,2},{5,4},{6,5},{7,6},{9,8},{10,9},{11,10},{13,12},{... | collective-permute-start | bytes 1797128 | tf_op jit(solution)/shard_map/ppermute | solution.py:127
  25.8 0.7 copy-start.13
  26.6 17.8 %collective-permute-start.1 = (f32[8,32,128]{2,0,1:T(8,128)}, f32[8,32,128]{2,0,1:T(8,128)}, u32[]{:S(2)}, u32[]{:S(2)}) collective-permute-start(f32[8,32,128]{2,0,1:T(8,128)} %constant_dynamic-slice_fusion.1), channel_id=1, source_target_pairs={{0,8},{8,0},{16,24},{24,16},{1,9},{9,1},{17,25},{25,17},{2,10},{10... | collective-permute-start | bytes 393224 | tf_op jit(solution)/shard_map/ppermute | solution.py:90
  31.1 1.6 %copy-start.7 = (bf16[32,64,64]{2,1,0:T(8,128)(2,1)S(1)}, bf16[32,64,64]{2,1,0:T(8,128)(2,1)}, u32[]{:S(2)}) copy-start(bf16[32,64,64]{2,1,0:T(8,128)(2,1)} %param.12) | copy-start | bytes 786436
  31.1 1.8 %copy-start.17 = (bf16[27,64]{1,0:T(8,128)(2,1)S(1)}, bf16[27,64]{1,0:T(8,128)(2,1)}, u32[]{:S(2)}) copy-start(bf16[27,64]{1,0:T(8,128)(2,1)} %param.8) | copy-start | bytes 10372
  34.1 10.2 %copy-start.14 = (f32[16,32,128]{2,0,1:T(8,128)S(1)}, f32[16,32,128]{2,0,1:T(8,128)}, u32[]{:S(2)}) copy-start(f32[16,32,128]{2,0,1:T(8,128)} %copy-done.13) | copy-start | bytes 786436
  52.9 9.1 %collective-permute-start.7 = (bf16[8,32,128]{2,1,0:T(8,128)(2,1)S(1)}, bf16[8,32,128]{2,1,0:T(8,128)(2,1)S(1)}, u32[]{:S(2)}, u32[]{:S(2)}) collective-permute-start(bf16[8,32,128]{2,1,0:T(8,128)(2,1)S(1)} %convolution_convert_fusion.2), channel_id=1, source_target_pairs={{0,8},{8,0},{16,24},{24,16},{1,9},{9,1},{17,25},{25,17},{2,10},{10... | collective-permute-start | bytes 196616 | tf_op jit(solution)/shard_map/ppermute | solution.py:68
  57.4 1.2 copy-start.18
  58.6 3.3 %copy-start.4 = (f32[8192,256]{1,0:T(8,128)}, f32[8192,256]{1,0:T(8,128)S(1)}, u32[]{:S(2)}) copy-start(f32[8192,256]{1,0:T(8,128)S(1)} %fusion.105) | copy-start | bytes 25165828
  61.9 5.8 %copy-start.12 = (bf16[32,256,64]{1,2,0:T(8,128)(2,1)S(1)}, bf16[32,256,64]{1,2,0:T(8,128)(2,1)}, u32[]{:S(2)}) copy-start(bf16[32,256,64]{1,2,0:T(8,128)(2,1)} %copy.30) | copy-start | bytes 3145732
  62.0 5.0 %collective-permute-start.8 = (bf16[16,32,128]{2,1,0:T(8,128)(2,1)S(1)}, bf16[16,32,128]{2,1,0:T(8,128)(2,1)S(1)}, u32[]{:S(2)}, u32[]{:S(2)}) collective-permute-start(bf16[16,32,128]{2,1,0:T(8,128)(2,1)S(1)} %pad_maximum_fusion.3), channel_id=1, source_target_pairs={{0,16},{8,24},{16,0},{24,8},{1,17},{9,25},{17,1},{25,9},{2,18},{10... | collective-permute-start | bytes 393224 | tf_op jit(solution)/shard_map/ppermute | solution.py:68
  71.9 7.9 %copy-start.19 = (bf16[256,64]{0,1:T(8,128)(2,1)S(1)}, bf16[256,64]{0,1:T(8,128)(2,1)}, u32[]{:S(2)}) copy-start(bf16[256,64]{0,1:T(8,128)(2,1)} %param.10) | copy-start | bytes 98308
  71.9 6.4 %collective-permute-start.9 = (f32[16,32,128]{2,0,1:T(8,128)S(1)}, f32[16,32,128]{2,0,1:T(8,128)S(1)}, u32[]{:S(2)}, u32[]{:S(2)}) collective-permute-start(f32[16,32,128]{2,0,1:T(8,128)S(1)} %fusion.12), channel_id=1, source_target_pairs={{0,16},{8,24},{16,0},{24,8},{1,17},{9,25},{17,1},{25,9},{2,18},{10... | collective-permute-start | bytes 786440 | tf_op jit(solution)/shard_map/ppermute | solution.py:90
  78.5 1.3 copy-start.15
  79.3 11.4 %collective-permute-start.10 = (f32[8,32,128]{2,0,1:T(8,128)}, f32[8,32,128]{2,0,1:T(8,128)}, u32[]{:S(2)}, u32[]{:S(2)}) collective-permute-start(f32[8,32,128]{2,0,1:T(8,128)} %constant_dynamic-slice_fusion), channel_id=1, source_target_pairs={{0,8},{8,0},{16,24},{24,16},{1,9},{9,1},{17,25},{25,17},{2,10},{10... | collective-permute-start | bytes 393224 | tf_op jit(solution)/shard_map/ppermute | solution.py:90
  92.4 4.6 %collective-permute-start.11 = (bf16[2,16,128]{2,1,0:T(8,128)(2,1)S(1)}, bf16[2,16,128]{2,1,0:T(8,128)(2,1)S(1)}, u32[]{:S(2)}, u32[]{:S(2)}) collective-permute-start(bf16[2,16,128]{2,1,0:T(8,128)(2,1)S(1)} %get-tuple-element.24), channel_id=1, source_target_pairs={{0,8},{8,16},{16,24},{24,0},{1,9},{9,17},{17,25},{25,1},{2,10},{10... | collective-permute-start | bytes 24584 | tf_op jit(solution)/shard_map/ppermute | solution.py:26
  94.0 4.9 %collective-permute-start.16 = (bf16[8,32,128]{2,1,0:T(8,128)(2,1)S(1)}, bf16[8,32,128]{2,1,0:T(8,128)(2,1)S(1)}, u32[]{:S(2)}, u32[]{:S(2)}) collective-permute-start(bf16[8,32,128]{2,1,0:T(8,128)(2,1)S(1)} %convolution_convert_fusion.1), channel_id=1, source_target_pairs={{0,8},{8,0},{16,24},{24,16},{1,9},{9,1},{17,25},{25,17},{2,10},{10... | collective-permute-start | bytes 196616 | tf_op jit(solution)/shard_map/ppermute | solution.py:68
  95.0 3.7 %collective-permute-start.12 = (bf16[2,16,128]{2,1,0:T(8,128)(2,1)S(1)}, bf16[2,16,128]{2,1,0:T(8,128)(2,1)S(1)}, u32[]{:S(2)}, u32[]{:S(2)}) collective-permute-start(bf16[2,16,128]{2,1,0:T(8,128)(2,1)S(1)} %get-tuple-element.23), channel_id=1, source_target_pairs={{8,0},{16,8},{24,16},{0,24},{9,1},{17,9},{25,17},{1,25},{10,2},{18... | collective-permute-start | bytes 24584 | tf_op jit(solution)/shard_map/ppermute | solution.py:27
  98.6 6.5 %copy-start.8 = (bf16[2,16,16640]{2,1,0:T(8,128)(2,1)}, bf16[2,16,16640]{2,1,0:T(8,128)(2,1)S(1)}, u32[]{:S(2)}) copy-start(bf16[2,16,16640]{2,1,0:T(8,128)(2,1)S(1)} %constant_dynamic-update-slice_fusion.6) | copy-start | bytes 3194884
  98.8 1.4 collective-permute-start.13
  98.9 6.0 %collective-permute-start.17 = (bf16[16,32,128]{2,1,0:T(8,128)(2,1)S(1)}, bf16[16,32,128]{2,1,0:T(8,128)(2,1)S(1)}, u32[]{:S(2)}, u32[]{:S(2)}) collective-permute-start(bf16[16,32,128]{2,1,0:T(8,128)(2,1)S(1)} %pad_maximum_fusion.4), channel_id=1, source_target_pairs={{0,16},{8,24},{16,0},{24,8},{1,17},{9,25},{17,1},{25,9},{2,18},{10... | collective-permute-start | bytes 393224 | tf_op jit(solution)/shard_map/ppermute | solution.py:68
  109.0 4.2 %copy-start.9 = (bf16[2,16,16640]{2,1,0:T(8,128)(2,1)S(1)}, bf16[2,16,16640]{2,1,0:T(8,128)(2,1)}, u32[]{:S(2)}) copy-start(bf16[2,16,16640]{2,1,0:T(8,128)(2,1)} %copy-done.8) | copy-start | bytes 3194884
  113.2 1.4 collective-permute-start.18
  113.9 15.7 %copy-start.3 = (bf16[2,18,16640]{2,1,0:T(8,128)(2,1)}, bf16[2,18,16640]{2,1,0:T(8,128)(2,1)S(1)}, u32[]{:S(2)}) copy-start(bf16[2,18,16640]{2,1,0:T(8,128)(2,1)S(1)} %pad_maximum_fusion.1.refs_0_) | copy-start | bytes 3594244
  113.9 13.9 %copy-start.11 = (bf16[32,256,64]{1,2,0:T(8,128)(2,1)S(1)}, bf16[32,256,64]{1,2,0:T(8,128)(2,1)}, u32[]{:S(2)}) copy-start(bf16[32,256,64]{1,2,0:T(8,128)(2,1)} %get-tuple-element.18) | copy-start | bytes 3145732
  114.7 7.1 %collective-permute-start.19 = (bf16[64,1024]{1,0:T(8,128)(2,1)S(1)}, bf16[64,1024]{1,0:T(8,128)(2,1)S(1)}, u32[]{:S(2)}, u32[]{:S(2)}) collective-permute-start(bf16[64,1024]{1,0:T(8,128)(2,1)S(1)} %add_convert_fusion.2), channel_id=1, source_target_pairs={{0,1},{1,0},{2,3},{3,2},{4,5},{5,4},{6,7},{7,6},{8,9},{9,8},{10,11... | collective-permute-start | bytes 393224 | tf_op jit(solution)/shard_map/ppermute | solution.py:107
  118.5 33.6 %collective-permute-start.14 = (bf16[1,18,16640]{2,1,0:T(8,128)(2,1)}, bf16[1,18,16640]{2,1,0:T(8,128)(2,1)S(1)}, u32[]{:S(2)}, u32[]{:S(2)}) collective-permute-start(bf16[1,18,16640]{2,1,0:T(8,128)(2,1)} %get-tuple-element.20), channel_id=1, source_target_pairs={{0,1},{1,2},{2,3},{4,5},{5,6},{6,7},{8,9},{9,10},{10,11},{12,13},{... | collective-permute-start | bytes 1797128 | tf_op jit(solution)/shard_map/ppermute | solution.py:126
  120.5 31.6 %collective-permute-start.15 = (bf16[1,18,16640]{2,1,0:T(8,128)(2,1)}, bf16[1,18,16640]{2,1,0:T(8,128)(2,1)}, u32[]{:S(2)}, u32[]{:S(2)}) collective-permute-start(bf16[1,18,16640]{2,1,0:T(8,128)(2,1)} %get-tuple-element.19), channel_id=1, source_target_pairs={{1,0},{2,1},{3,2},{5,4},{6,5},{7,6},{9,8},{10,9},{11,10},{13,12},{... | collective-permute-start | bytes 1797128 | tf_op jit(solution)/shard_map/ppermute | solution.py:127
  122.5 27.6 %collective-permute-start.20 = (bf16[64,1024]{1,0:T(8,128)(2,1)}, bf16[64,1024]{1,0:T(8,128)(2,1)}, u32[]{:S(2)}, u32[]{:S(2)}) collective-permute-start(bf16[64,1024]{1,0:T(8,128)(2,1)} %add_convert_fusion.1), channel_id=1, source_target_pairs={{0,2},{1,3},{2,0},{3,1},{4,6},{5,7},{6,4},{7,5},{8,10},{9,11},{10,... | collective-permute-start | bytes 393224 | tf_op jit(solution)/shard_map/ppermute | solution.py:107
  152.1 8.0 %copy-start.5 = (f32[2,16,16384]{2,1,0:T(8,128)S(1)}, f32[2,16,16384]{2,1,0:T(8,128)}, u32[]{:S(2)}) copy-start(f32[2,16,16384]{2,1,0:T(8,128)} %reshape.96) | copy-start | bytes 6291460
  152.1 0.9 copy-start.16
  153.0 9.9 %copy-start.1 = (bf16[64,256]{1,0:T(8,128)(2,1)S(1)}, bf16[64,256]{1,0:T(8,128)(2,1)}, u32[]{:S(2)}) copy-start(bf16[64,256]{1,0:T(8,128)(2,1)} %param.9) | copy-start | bytes 98308

commit v17 on v15

--- a/solution.py
+++ b/solution.py
@@ -205,19 +205,17 @@
 
 
 def share_terms(field3, cos_table, sin_table):
-    real_part = jnp.einsum("rxc,xk->krc", field3, cos_table, preferred_element_type=jnp.float32)
-    imag_part = jnp.einsum("rxc,xk->krc", field3, sin_table, preferred_element_type=jnp.float32)
-    return ring_reduce_scatter(jnp.concatenate([real_part, imag_part], axis=2), "gx")
+    modes = cos_table.shape[1]
+    table = jnp.concatenate([cos_table, sin_table], axis=1)
+    both = jnp.einsum("rxc,xk->krc", field3, table, preferred_element_type=jnp.float32)
+    return ring_reduce_scatter(jnp.concatenate([both[:modes], both[modes:]], axis=2), "gx")
 
 
 def share_inverse(modes_share, cos_table, sin_table, channels):
     segment = ring_gather(modes_share, "gx")
-    running = jnp.einsum(
-        "krc,xk->rxc", segment[:, :, :channels], cos_table, preferred_element_type=jnp.float32
-    )
-    return running + jnp.einsum(
-        "krc,xk->rxc", segment[:, :, channels:], sin_table, preferred_element_type=jnp.float32
-    )
+    stacked = jnp.concatenate([segment[:, :, :channels], segment[:, :, channels:]], axis=0)
+    table = jnp.concatenate([cos_table, sin_table], axis=1)
+    return jnp.einsum("krc,xk->rxc", stacked, table, preferred_element_type=jnp.float32)
 
 
 def split_gradients(dblock, channels):

time: 155 us -> 159 us (1.026)
  other arithmetic: 10 us -> 17.4 us
  starting transfers between devices: 35.6 us -> 31.7 us
  local copies, waits for them, and re-layouts: 33.8 us -> 37.4 us
  matrix products: 19.6 us -> 17.4 us
    dot_general x8 -> x2, matrix products: 6.95 us -> 1.1 us  [share_terms(): jnp.einsum('rxc,xk->krc', field3, table, preferred_element_type=jnp.float32)]
    unnamed x42 -> x50, local copies, waits for them, and re-layouts: 1.6 us -> 5.63 us
    convert_element_type x0 -> x2, other arithmetic: none -> 2.85 us  [the longest x1 1.93 us: per_device(): grad_pre = (lax.optimization_barrier(cotangent.reshape(row_count, x_cells...]
    transpose x0 -> x1, local copies, waits for them, and re-layouts: none -> 2.75 us  [share_inverse(): jnp.einsum('krc,xk->rxc', stacked, table, preferred_element_type=jnp.floa...]
    add x1 -> x0, local copies, waits for them, and re-layouts: 2.74 us -> none  [share_inverse(): running + jnp.einsum('krc,xk->rxc', segment[:, :, channels:], sin_table,...]
    ppermute x4, waiting for transfers between devices: 3.69 us -> 5.42 us  [ring_reduce_scatter(): lax.ppermute(send, axis, [(i, i ^ step) for i in range(size)])]
    ppermute x4, starting transfers between devices: 6.64 us -> 4.98 us  [ring_reduce_scatter(): lax.ppermute(send, axis, [(i, i ^ step) for i in range(size)])]
  transfers between devices with their start and end apart: 21 -> 21, of which waited for: 9 -> 7; matrix products, arithmetic and copies ran while one was open for 31% -> 35% of each run, Pallas kernels for 12% -> 12%
where the time goes in v17:
time: 159 us; the launch traced here: 158 us
  local copies, waits for them, and re-layouts  37.4 us (24%)
  Pallas kernels  33 us (21%)
  starting transfers between devices  31.7 us (20%)
  waiting for transfers between devices  20.3 us (13%)
  other arithmetic  17.4 us (11%)
  matrix products  17.4 us (11%)
    pallas_call x4, Pallas kernels, stencil_call(): pl.pallas_call(kernel, out_shape=jax.ShapeDtypeStruct((len(plan), y_cells...  33 us
    ppermute x3, waiting for transfers between devices, butterfly_sum(): lax.ppermute(value, axis, [(i, i ^ step) for i in range(size)])  9.29 us
    dot_general x1, matrix products, per_device(): jnp.dot(grad_hidden, expand_weight.T, preferred_element_type=jnp.float32)  8.88 us
    ppermute x2, starting transfers between devices, spatial_rims(): below = lax.ppermute(inner[-1:], 'gz', up)  8.35 us
    unnamed x50, local copies, waits for them, and re-layouts  5.63 us
    ppermute x4, waiting for transfers between devices, ring_reduce_scatter(): lax.ppermute(send, axis, [(i, i ^ step) for i in range(size)])  5.42 us
    ppermute x3, starting transfers between devices, butterfly_sum(): lax.ppermute(value, axis, [(i, i ^ step) for i in range(size)])  5.36 us
    ppermute x4, starting transfers between devices, ring_reduce_scatter(): lax.ppermute(send, axis, [(i, i ^ step) for i in range(size)])  4.98 us
  transfers between devices with their start and end apart: 21, of which 7 were waited for; matrix products, arithmetic and copies ran while one was open for 35% of the time, Pallas kernels for 12%

profile of v17, /device:TPU:0, one launch (start us, length us, event | category | flops | bytes accessed | tf_op | source)
XLA Modules:
  0.0 158.4 jit_solution(12209915181643329655)
XLA Ops:
  1.4 2.9 %collective-permute-start.2 = (bf16[2,16,128]{2,1,0:T(8,128)(2,1)S(1)}, bf16[2,16,128]{2,1,0:T(8,128)(2,1)S(1)}, u32[]{:S(2)}, u32[]{:S(2)}) collective-permute-start(bf16[2,16,128]{2,1,0:T(8,128)(2,1)S(1)} %get-tuple-element.24), channel_id=1, source_target_pairs={{0,8},{8,16},{16,24},{24,0},{1,9},{9,17},{17,25},{25,1},{2,10},{10... | collective-permute-start | bytes 24584 | tf_op jit(solution)/shard_map/ppermute | solution.py:26
  4.3 1.0 collective-permute-start.3
  5.3 3.0 %reshape.89 = bf16[32,256,64]{2,1,0:T(8,128)(2,1)S(1)} reshape(bf16[2,16,16384]{2,1,0:T(8,128)(2,1)} %param.7) | data formatting | bytes 2097152 | tf_op jit(solution)/shard_map/reshape | solution.py:256
  8.5 0.9 multiply_convert_fusion.4
  10.7 1.0 copy-done.8
  12.2 2.1 %collective-permute-start = (f32[16,32,128]{2,0,1:T(8,128)S(1)}, f32[16,32,128]{2,0,1:T(8,128)S(1)}, u32[]{:S(2)}, u32[]{:S(2)}) collective-permute-start(f32[16,32,128]{2,0,1:T(8,128)S(1)} %fusion.15), channel_id=1, source_target_pairs={{0,16},{8,24},{16,0},{24,8},{1,17},{9,25},{17,1},{25,9},{2,18},{10... | collective-permute-start | bytes 786440 | tf_op jit(solution)/shard_map/ppermute | solution.py:90
  15.1 1.4 fusion.60
  16.6 4.4 %collective-permute-start.5 = (bf16[1,18,16640]{2,1,0:T(8,128)(2,1)}, bf16[1,18,16640]{2,1,0:T(8,128)(2,1)}, u32[]{:S(2)}, u32[]{:S(2)}) collective-permute-start(bf16[1,18,16640]{2,1,0:T(8,128)(2,1)} %get-tuple-element.18), channel_id=1, source_target_pairs={{0,1},{1,2},{2,3},{4,5},{5,6},{6,7},{8,9},{9,10},{10,11},{12,13},{... | collective-permute-start | bytes 1797128 | tf_op jit(solution)/shard_map/ppermute | solution.py:126
  20.9 1.3 collective-permute-start.6
  23.7 3.0 %reshape.93 = bf16[32,256,64]{2,1,0:T(8,128)(2,1)S(1)} reshape(bf16[2,16,16384]{2,1,0:T(8,128)(2,1)} %param.13) | data formatting | bytes 2097152 | tf_op jit(solution)/shard_map/reshape | solution.py:276
  27.6 1.2 neg.10
  28.9 1.2 fusion.19
  30.8 9.6 %shard_map.94.refs_2_ = f32[2,16,16384]{2,1,0:T(8,128)} custom-call(bf16[2,18,16640]{2,1,0:T(8,128)(2,1)} %copy-done.2, f32[27,8,128]{2,1,0:T(8,128)} %broadcast_in_dim.18.refs_1_.refs_3_), custom_call_target="tpu_custom_call" | custom-call | tf_op jit(solution)/shard_map/pallas_call | solution.py:179
  40.4 0.9 add_convert_fusion.4
  42.8 6.7 %shard_map.95 = bf16[2,16,16384]{2,1,0:T(8,128)(2,1)} custom-call(bf16[1,18,16640]{2,1,0:T(8,128)(2,1)} %collective-permute-done.5.refs_0_, bf16[1,18,16640]{2,1,0:T(8,128)(2,1)} %collective-permute-done.6.refs_1_, f32[2,16,16384]{2,1,0:T(8,128)} %shard_map.94.refs_2_, f32[27,8,128]{2,1,0:T(8,128)} %broadcast_in_dim.18.refs_1_.refs_3_), custom_call_target="tpu_custom_call" | custom-call | tf_op jit(solution)/shard_map/pallas_call | solution.py:179
  50.3 3.0 %reshape.90 = bf16[8192,64]{1,0:T(8,128)(2,1)S(1)} reshape(bf16[2,16,16384]{2,1,0:T(8,128)(2,1)} %shard_map.95) | data formatting | bytes 2097152 | tf_op jit(solution)/shard_map/reshape | solution.py:265
  53.3 1.2 fusion.67
  54.6 4.0 %fusion.5 = f32[8192,64]{0,1:T(8,128)} fusion(bf16[256,64]{0,1:T(8,128)(2,1)S(1)} %copy-done.20, f32[8192,256]{1,0:T(8,128)S(1)} %fusion.67), kind=kOutput, calls=%fused_computation.10 | convolution fusion | flops 278921216 | bytes 10518528 | tf_op jit(solution)/shard_map/dot_general | solution.py:268
  59.5 1.2 collective-permute-start.8
  62.4 2.1 %collective-permute-done.8 = bf16[16,32,128]{2,1,0:T(8,128)(2,1)S(1)} collective-permute-done((bf16[16,32,128]{2,1,0:T(8,128)(2,1)S(1)}, bf16[16,32,128]{2,1,0:T(8,128)(2,1)S(1)}, u32[]{:S(2)}, u32[]{:S(2)}) %collective-permute-start.8) | collective-permute-done | bytes 131104 | tf_op jit(solution)/shard_map/ppermute | solution.py:68
  65.9 1.2 copy-done.7
  67.1 1.9 %fusion.11 = (bf16[32,256,64]{1,2,0:T(8,128)(2,1)S(1)}, bf16[32,256,64]{1,2,0:T(8,128)(2,1)}) fusion(bf16[32,256,64]{1,2,0:T(8,128)(2,1)S(1)} %copy.25, f32[32,256,64]{1,2,0:T(8,128)S(1)} %bitcast.48, f32[8,32,8,256]{3,2,1,0:T(8,128)S(1)} %bitcast.50), kind=kLoop, calls=%fused_computation.17 | loop fusion | flops 7340032 | bytes 7340032 | tf_op jit(solution)/shard_map/convert_element_type | solution.py:278
  70.5 1.1 collective-permute-start.9
  71.9 5.4 %collective-permute-done.9 = f32[16,32,128]{2,0,1:T(8,128)} collective-permute-done((f32[16,32,128]{2,0,1:T(8,128)}, f32[16,32,128]{2,0,1:T(8,128)}, u32[]{:S(2)}, u32[]{:S(2)}) %collective-permute-start.9) | collective-permute-done | bytes 262176 | tf_op jit(solution)/shard_map/ppermute | solution.py:90
  77.3 1.1 fusion.14
  79.1 1.2 collective-permute-start.10
  80.3 8.9 %convolution_convert_fusion = bf16[8192,64]{0,1:T(8,128)(2,1)} fusion(bf16[64,256]{1,0:T(8,128)(2,1)S(1)} %copy-done, bf16[8192,64]{0,1:T(8,128)(2,1)S(1)} %bitcast.53, bf16[256,64]{0,1:T(8,128)(2,1)} %param.10, f32[8192,256]{1,0:T(8,128)} %copy-done.4), kind=kOutput, calls=%fused_computation.3 | convolution fusion | flops 558366720 | bytes 10551296 | tf_op jit(solution)/shard_map/dot_general | solution.py:285
  89.2 1.1 copy.24
  90.3 2.7 %reshape.92 = bf16[2,16,16384]{2,1,0:T(8,128)(2,1)} reshape(bf16[32,256,64]{2,1,0:T(8,128)(2,1)S(1)} %copy.24) | data formatting | bytes 2097152 | tf_op jit(solution)/shard_map/reshape | solution.py:274
  93.0 1.1 copy.30
  94.1 1.7 %reshape.95 = bf16[2,16,16384]{2,1,0:T(8,128)(2,1)S(1)} reshape(bf16[8192,64]{1,0:T(8,128)(2,1)S(1)} %copy.30) | data formatting | bytes 2097152 | tf_op jit(solution)/shard_map/reshape | solution.py:288
  95.8 1.0 add_convert_fusion.3
  98.5 1.7 %collective-permute-start.16 = (bf16[8,32,128]{2,1,0:T(8,128)(2,1)S(1)}, bf16[8,32,128]{2,1,0:T(8,128)(2,1)S(1)}, u32[]{:S(2)}, u32[]{:S(2)}) collective-permute-start(bf16[8,32,128]{2,1,0:T(8,128)(2,1)S(1)} %convolution_convert_fusion.1), channel_id=1, source_target_pairs={{0,8},{8,0},{16,24},{24,16},{1,9},{9,1},{17,25},{25,17},{2,10},{10... | collective-permute-start | bytes 196616 | tf_op jit(solution)/shard_map/ppermute | solution.py:68
  102.3 1.6 collective-permute-done.12
  104.2 1.0 collective-permute-start.17
  106.3 1.5 fusion.59
  107.8 4.0 %collective-permute-start.14 = (bf16[1,18,16640]{2,1,0:T(8,128)(2,1)}, bf16[1,18,16640]{2,1,0:T(8,128)(2,1)S(1)}, u32[]{:S(2)}, u32[]{:S(2)}) collective-permute-start(bf16[1,18,16640]{2,1,0:T(8,128)(2,1)} %get-tuple-element.16), channel_id=1, source_target_pairs={{0,1},{1,2},{2,3},{4,5},{5,6},{6,7},{8,9},{9,10},{10,11},{12,13},{... | collective-permute-start | bytes 1797128 | tf_op jit(solution)/shard_map/ppermute | solution.py:126
  111.8 1.3 collective-permute-start.15
  113.8 9.6 %shard_map.96.refs_2_ = f32[2,16,16384]{2,1,0:T(8,128)} custom-call(bf16[2,18,16640]{2,1,0:T(8,128)(2,1)} %copy-done.3, f32[27,8,128]{2,1,0:T(8,128)} %broadcast_in_dim.36.refs_1_.refs_3_), custom_call_target="tpu_custom_call" | custom-call | tf_op jit(solution)/shard_map/pallas_call | solution.py:179
  123.4 2.7 %collective-permute-start.19 = (bf16[64,1024]{1,0:T(8,128)(2,1)S(1)}, bf16[64,1024]{1,0:T(8,128)(2,1)S(1)}, u32[]{:S(2)}, u32[]{:S(2)}) collective-permute-start(bf16[64,1024]{1,0:T(8,128)(2,1)S(1)} %add_convert_fusion.2), channel_id=1, source_target_pairs={{0,1},{1,0},{2,3},{3,2},{4,5},{5,4},{6,7},{7,6},{8,9},{9,8},{10,11... | collective-permute-start | bytes 393224 | tf_op jit(solution)/shard_map/ppermute | solution.py:107
  127.0 9.3 %collective-permute-done.19 = bf16[64,1024]{1,0:T(8,128)(2,1)S(1)} collective-permute-done((bf16[64,1024]{1,0:T(8,128)(2,1)S(1)}, bf16[64,1024]{1,0:T(8,128)(2,1)S(1)}, u32[]{:S(2)}, u32[]{:S(2)}) %collective-permute-start.19) | collective-permute-done | bytes 131104 | tf_op jit(solution)/shard_map/ppermute | solution.py:107
  137.0 2.6 %collective-permute-start.20 = (bf16[64,1024]{1,0:T(8,128)(2,1)}, bf16[64,1024]{1,0:T(8,128)(2,1)}, u32[]{:S(2)}, u32[]{:S(2)}) collective-permute-start(bf16[64,1024]{1,0:T(8,128)(2,1)} %add_convert_fusion.1), channel_id=1, source_target_pairs={{0,2},{1,3},{2,0},{3,1},{4,6},{5,7},{6,4},{7,5},{8,10},{9,11},{10,... | collective-permute-start | bytes 393224 | tf_op jit(solution)/shard_map/ppermute | solution.py:107
  140.0 2.8 %copy.32 = f32[32,256,64]{2,1,0:T(8,128)} copy(f32[32,256,64]{1,2,0:T(8,128)S(1)} %bitcast.49) | data formatting | bytes 4194304 | tf_op jit(solution)/shard_map/krc,xk->rxc/transpose | solution.py:218
  142.7 2.9 %reshape.96 = f32[2,16,16384]{2,1,0:T(8,128)S(1)} reshape(f32[32,256,64]{2,1,0:T(8,128)} %copy.32) | data formatting | bytes 4194304 | tf_op jit(solution)/shard_map/reshape | solution.py:300
  145.7 1.0 convert_add_fusion
  146.7 0.9 reshape.97
  148.5 7.1 %shard_map.97 = f32[2,16,16384]{2,1,0:T(8,128)} custom-call(bf16[1,18,16640]{2,1,0:T(8,128)(2,1)} %copy-done.14, bf16[1,18,16640]{2,1,0:T(8,128)(2,1)} %collective-permute-done.15.refs_1_, f32[2,16,16384]{2,1,0:T(8,128)} %shard_map.96.refs_2_, f32[27,8,128]{2,1,0:T(8,128)} %broadcast_in_dim.36.refs_1_.refs_3_), custom_call_target="tpu_custom_call" | custom-call | tf_op jit(solution)/shard_map/pallas_call | solution.py:179
  155.6 2.7 %add_convert_fusion = bf16[2,16,16384]{2,1,0:T(8,128)(2,1)} fusion(f32[2,16,16384]{2,1,0:T(8,128)} %shard_map.97, f32[2,16,16384]{2,1,0:T(8,128)S(1)} %reshape.96), kind=kLoop, calls=%fused_computation.19 | loop fusion | flops 1048576 | bytes 5242880 | tf_op jit(solution)/shard_map/convert_element_type | solution.py:300
  (125 shorter events, 23.9 us)
Async XLA Ops:
  0.6 52.7 %copy-start = (bf16[64,256]{1,0:T(8,128)(2,1)S(1)}, bf16[64,256]{1,0:T(8,128)(2,1)}, u32[]{:S(2)}) copy-start(bf16[64,256]{1,0:T(8,128)(2,1)} %param.9) | copy-start | bytes 98308
  1.4 8.6 %collective-permute-start.2 = (bf16[2,16,128]{2,1,0:T(8,128)(2,1)S(1)}, bf16[2,16,128]{2,1,0:T(8,128)(2,1)S(1)}, u32[]{:S(2)}, u32[]{:S(2)}) collective-permute-start(bf16[2,16,128]{2,1,0:T(8,128)(2,1)S(1)} %get-tuple-element.24), channel_id=1, source_target_pairs={{0,8},{8,16},{16,24},{24,0},{1,9},{9,17},{17,25},{25,1},{2,10},{10... | collective-permute-start | bytes 24584 | tf_op jit(solution)/shard_map/ppermute | solution.py:26
  4.3 6.4 %collective-permute-start.3 = (bf16[2,16,128]{2,1,0:T(8,128)(2,1)S(1)}, bf16[2,16,128]{2,1,0:T(8,128)(2,1)S(1)}, u32[]{:S(2)}, u32[]{:S(2)}) collective-permute-start(bf16[2,16,128]{2,1,0:T(8,128)(2,1)S(1)} %get-tuple-element.23), channel_id=1, source_target_pairs={{8,0},{16,8},{24,16},{0,24},{9,1},{17,9},{25,17},{1,25},{10,2},{18... | collective-permute-start | bytes 24584 | tf_op jit(solution)/shard_map/ppermute | solution.py:27
  9.4 1.2 copy-start.5
  10.7 1.0 copy-start.8
  12.0 2.5 %copy-start.9 = (bf16[2,16,16640]{2,1,0:T(8,128)(2,1)S(1)}, bf16[2,16,16640]{2,1,0:T(8,128)(2,1)}, u32[]{:S(2)}) copy-start(bf16[2,16,16640]{2,1,0:T(8,128)(2,1)} %copy-done.8) | copy-start | bytes 3194884
  12.0 2.3 %collective-permute-start.4 = (bf16[2,1,16640]{2,1,0:T(2,128)(2,1)S(1)}, bf16[2,1,16640]{2,1,0:T(2,128)(2,1)S(1)}, u32[]{:S(2)}, u32[]{:S(2)}) collective-permute-start(bf16[2,1,16640]{2,1,0:T(2,128)(2,1)S(1)} %broadcast_select_fusion.5), channel_id=1, source_target_pairs={{0,4},{4,0},{1,5},{5,1},{2,6},{6,2},{3,7},{7,3},{8,12},{12,8},{9,1... | collective-permute-start | bytes 199688 | tf_op jit(solution)/shard_map/ppermute | solution.py:19
  12.2 10.0 %collective-permute-start = (f32[16,32,128]{2,0,1:T(8,128)S(1)}, f32[16,32,128]{2,0,1:T(8,128)S(1)}, u32[]{:S(2)}, u32[]{:S(2)}) collective-permute-start(f32[16,32,128]{2,0,1:T(8,128)S(1)} %fusion.15), channel_id=1, source_target_pairs={{0,16},{8,24},{16,0},{24,8},{1,17},{9,25},{17,1},{25,9},{2,18},{10... | collective-permute-start | bytes 786440 | tf_op jit(solution)/shard_map/ppermute | solution.py:90
  15.1 7.3 %copy-start.2 = (bf16[2,18,16640]{2,1,0:T(8,128)(2,1)}, bf16[2,18,16640]{2,1,0:T(8,128)(2,1)S(1)}, u32[]{:S(2)}) copy-start(bf16[2,18,16640]{2,1,0:T(8,128)(2,1)S(1)} %pad_maximum_fusion.refs_0_) | copy-start | bytes 3594244
  16.6 25.5 %collective-permute-start.5 = (bf16[1,18,16640]{2,1,0:T(8,128)(2,1)}, bf16[1,18,16640]{2,1,0:T(8,128)(2,1)}, u32[]{:S(2)}, u32[]{:S(2)}) collective-permute-start(bf16[1,18,16640]{2,1,0:T(8,128)(2,1)} %get-tuple-element.18), channel_id=1, source_target_pairs={{0,1},{1,2},{2,3},{4,5},{5,6},{6,7},{8,9},{9,10},{10,11},{12,13},{... | collective-permute-start | bytes 1797128 | tf_op jit(solution)/shard_map/ppermute | solution.py:126
  20.9 21.8 %collective-permute-start.6 = (bf16[1,18,16640]{2,1,0:T(8,128)(2,1)}, bf16[1,18,16640]{2,1,0:T(8,128)(2,1)}, u32[]{:S(2)}, u32[]{:S(2)}) collective-permute-start(bf16[1,18,16640]{2,1,0:T(8,128)(2,1)} %get-tuple-element.17), channel_id=1, source_target_pairs={{1,0},{2,1},{3,2},{5,4},{6,5},{7,6},{9,8},{10,9},{11,10},{13,12},{... | collective-permute-start | bytes 1797128 | tf_op jit(solution)/shard_map/ppermute | solution.py:127
  22.4 0.7 copy-start.11
  23.1 17.2 %collective-permute-start.1 = (f32[8,32,128]{2,0,1:T(8,128)}, f32[8,32,128]{2,0,1:T(8,128)}, u32[]{:S(2)}, u32[]{:S(2)}) collective-permute-start(f32[8,32,128]{2,0,1:T(8,128)} %constant_dynamic-slice_fusion.1), channel_id=1, source_target_pairs={{0,8},{8,0},{16,24},{24,16},{1,9},{9,1},{17,25},{25,17},{2,10},{10... | collective-permute-start | bytes 393224 | tf_op jit(solution)/shard_map/ppermute | solution.py:90
  26.8 2.0 %copy-start.18 = (bf16[27,64]{1,0:T(8,128)(2,1)S(1)}, bf16[27,64]{1,0:T(8,128)(2,1)}, u32[]{:S(2)}) copy-start(bf16[27,64]{1,0:T(8,128)(2,1)} %param.8) | copy-start | bytes 10372
  30.1 10.2 %copy-start.12 = (f32[16,32,128]{2,0,1:T(8,128)S(1)}, f32[16,32,128]{2,0,1:T(8,128)}, u32[]{:S(2)}) copy-start(f32[16,32,128]{2,0,1:T(8,128)} %copy-done.11) | copy-start | bytes 786436
  49.5 9.1 %collective-permute-start.7 = (bf16[8,32,128]{2,1,0:T(8,128)(2,1)}, bf16[8,32,128]{2,1,0:T(8,128)(2,1)}, u32[]{:S(2)}, u32[]{:S(2)}) collective-permute-start(bf16[8,32,128]{2,1,0:T(8,128)(2,1)} %convolution_convert_fusion.2), channel_id=1, source_target_pairs={{0,8},{8,0},{16,24},{24,16},{1,9},{9,1},{17,25},{25,17},{2,10},{10... | collective-permute-start | bytes 196616 | tf_op jit(solution)/shard_map/ppermute | solution.py:68
  53.3 1.2 copy-start.20
  54.6 4.0 %copy-start.4 = (f32[8192,256]{1,0:T(8,128)}, f32[8192,256]{1,0:T(8,128)S(1)}, u32[]{:S(2)}) copy-start(f32[8192,256]{1,0:T(8,128)S(1)} %fusion.67) | copy-start | bytes 25165828
  58.6 6.9 %copy-start.16 = (bf16[256,32]{0,1:T(8,128)(2,1)S(1)}, bf16[256,32]{0,1:T(8,128)(2,1)}, u32[]{:S(2)}) copy-start(bf16[256,32]{0,1:T(8,128)(2,1)} %get-tuple-element.45) | copy-start | bytes 49156
  58.6 6.9 %copy-start.17 = (bf16[256,32]{0,1:T(8,128)(2,1)S(1)}, bf16[256,32]{0,1:T(8,128)(2,1)}, u32[]{:S(2)}) copy-start(bf16[256,32]{0,1:T(8,128)(2,1)} %get-tuple-element.46) | copy-start | bytes 49156
  59.5 5.0 %collective-permute-start.8 = (bf16[16,32,128]{2,1,0:T(8,128)(2,1)S(1)}, bf16[16,32,128]{2,1,0:T(8,128)(2,1)S(1)}, u32[]{:S(2)}, u32[]{:S(2)}) collective-permute-start(bf16[16,32,128]{2,1,0:T(8,128)(2,1)S(1)} %pad_maximum_fusion.5), channel_id=1, source_target_pairs={{0,16},{8,24},{16,0},{24,8},{1,17},{9,25},{17,1},{25,9},{2,18},{10... | collective-permute-start | bytes 393224 | tf_op jit(solution)/shard_map/ppermute | solution.py:68
  65.5 1.6 %copy-start.7 = (f32[8192,64]{0,1:T(8,128)S(1)}, f32[8192,64]{0,1:T(8,128)}, u32[]{:S(2)}) copy-start(f32[8192,64]{0,1:T(8,128)} %fusion.5) | copy-start | bytes 6291460
  69.6 2.1 %copy-start.19 = (bf16[27,64]{1,0:T(8,128)(2,1)S(1)}, bf16[27,64]{1,0:T(8,128)(2,1)}, u32[]{:S(2)}) copy-start(bf16[27,64]{1,0:T(8,128)(2,1)} %param.8) | copy-start | bytes 10372
  70.5 6.7 %collective-permute-start.9 = (f32[16,32,128]{2,0,1:T(8,128)}, f32[16,32,128]{2,0,1:T(8,128)}, u32[]{:S(2)}, u32[]{:S(2)}) collective-permute-start(f32[16,32,128]{2,0,1:T(8,128)} %fusion.12), channel_id=1, source_target_pairs={{0,16},{8,24},{16,0},{24,8},{1,17},{9,25},{17,1},{25,9},{2,18},{10... | collective-permute-start | bytes 786440 | tf_op jit(solution)/shard_map/ppermute | solution.py:90
  78.4 10.8 %copy-start.13 = (f32[16,32,128]{2,0,1:T(8,128)}, f32[16,32,128]{2,0,1:T(8,128)S(1)}, u32[]{:S(2)}) copy-start(f32[16,32,128]{2,0,1:T(8,128)S(1)} %fusion.14) | copy-start | bytes 786436
  79.1 16.7 %collective-permute-start.10 = (f32[8,32,128]{2,0,1:T(8,128)}, f32[8,32,128]{2,0,1:T(8,128)}, u32[]{:S(2)}, u32[]{:S(2)}) collective-permute-start(f32[8,32,128]{2,0,1:T(8,128)} %constant_dynamic-slice_fusion), channel_id=1, source_target_pairs={{0,8},{8,0},{16,24},{24,16},{1,9},{9,1},{17,25},{25,17},{2,10},{10... | collective-permute-start | bytes 393224 | tf_op jit(solution)/shard_map/ppermute | solution.py:90
  80.3 8.9 %copy-start.6 = (bf16[32,256,64]{1,2,0:T(8,128)(2,1)S(1)}, bf16[32,256,64]{1,2,0:T(8,128)(2,1)}, u32[]{:S(2)}) copy-start(bf16[32,256,64]{1,2,0:T(8,128)(2,1)} %get-tuple-element.14) | copy-start | bytes 3145732
  90.3 2.7 %copy-start.10 = (bf16[8192,64]{0,1:T(8,128)(2,1)S(1)}, bf16[8192,64]{0,1:T(8,128)(2,1)}, u32[]{:S(2)}) copy-start(bf16[8192,64]{0,1:T(8,128)(2,1)} %convolution_convert_fusion) | copy-start | bytes 3145732
  97.6 4.6 %collective-permute-start.11 = (bf16[2,16,128]{2,1,0:T(8,128)(2,1)S(1)}, bf16[2,16,128]{2,1,0:T(8,128)(2,1)S(1)}, u32[]{:S(2)}, u32[]{:S(2)}) collective-permute-start(bf16[2,16,128]{2,1,0:T(8,128)(2,1)S(1)} %get-tuple-element.20), channel_id=1, source_target_pairs={{0,8},{8,16},{16,24},{24,0},{1,9},{9,17},{17,25},{25,1},{2,10},{10... | collective-permute-start | bytes 24584 | tf_op jit(solution)/shard_map/ppermute | solution.py:26
  98.5 5.7 %collective-permute-start.16 = (bf16[8,32,128]{2,1,0:T(8,128)(2,1)S(1)}, bf16[8,32,128]{2,1,0:T(8,128)(2,1)S(1)}, u32[]{:S(2)}, u32[]{:S(2)}) collective-permute-start(bf16[8,32,128]{2,1,0:T(8,128)(2,1)S(1)} %convolution_convert_fusion.1), channel_id=1, source_target_pairs={{0,8},{8,0},{16,24},{24,16},{1,9},{9,1},{17,25},{25,17},{2,10},{10... | collective-permute-start | bytes 196616 | tf_op jit(solution)/shard_map/ppermute | solution.py:68
  100.2 3.7 %collective-permute-start.12 = (bf16[2,16,128]{2,1,0:T(8,128)(2,1)S(1)}, bf16[2,16,128]{2,1,0:T(8,128)(2,1)S(1)}, u32[]{:S(2)}, u32[]{:S(2)}) collective-permute-start(bf16[2,16,128]{2,1,0:T(8,128)(2,1)S(1)} %get-tuple-element.19), channel_id=1, source_target_pairs={{8,0},{16,8},{24,16},{0,24},{9,1},{17,9},{25,17},{1,25},{10,2},{18... | collective-permute-start | bytes 24584 | tf_op jit(solution)/shard_map/ppermute | solution.py:27
  101.2 22.1 %collective-permute-start.18 = (bf16[64,1024]{1,0:T(8,128)(2,1)S(1)}, bf16[64,1024]{1,0:T(8,128)(2,1)S(1)}, u32[]{:S(2)}, u32[]{:S(2)}) collective-permute-start(bf16[64,1024]{1,0:T(8,128)(2,1)S(1)} %convert_element_type.139), channel_id=1, source_target_pairs={{0,4},{4,0},{1,5},{5,1},{2,6},{6,2},{3,7},{7,3},{8,12},{12,8},{9,1... | collective-permute-start | bytes 393224 | tf_op jit(solution)/shard_map/ppermute | solution.py:107
  104.1 1.4 collective-permute-start.13
  104.2 21.9 %collective-permute-start.17 = (bf16[16,32,128]{2,1,0:T(8,128)(2,1)S(1)}, bf16[16,32,128]{2,1,0:T(8,128)(2,1)S(1)}, u32[]{:S(2)}, u32[]{:S(2)}) collective-permute-start(bf16[16,32,128]{2,1,0:T(8,128)(2,1)S(1)} %pad_maximum_fusion.6), channel_id=1, source_target_pairs={{0,16},{8,24},{16,0},{24,8},{1,17},{9,25},{17,1},{25,9},{2,18},{10... | collective-permute-start | bytes 393224 | tf_op jit(solution)/shard_map/ppermute | solution.py:68
  106.3 7.4 %copy-start.3 = (bf16[2,18,16640]{2,1,0:T(8,128)(2,1)}, bf16[2,18,16640]{2,1,0:T(8,128)(2,1)S(1)}, u32[]{:S(2)}) copy-start(bf16[2,18,16640]{2,1,0:T(8,128)(2,1)S(1)} %pad_maximum_fusion.1.refs_0_) | copy-start | bytes 3594244
  107.8 39.8 %collective-permute-start.14 = (bf16[1,18,16640]{2,1,0:T(8,128)(2,1)}, bf16[1,18,16640]{2,1,0:T(8,128)(2,1)S(1)}, u32[]{:S(2)}, u32[]{:S(2)}) collective-permute-start(bf16[1,18,16640]{2,1,0:T(8,128)(2,1)} %get-tuple-element.16), channel_id=1, source_target_pairs={{0,1},{1,2},{2,3},{4,5},{5,6},{6,7},{8,9},{9,10},{10,11},{12,13},{... | collective-permute-start | bytes 1797128 | tf_op jit(solution)/shard_map/ppermute | solution.py:126
  111.8 35.8 %collective-permute-start.15 = (bf16[1,18,16640]{2,1,0:T(8,128)(2,1)}, bf16[1,18,16640]{2,1,0:T(8,128)(2,1)}, u32[]{:S(2)}, u32[]{:S(2)}) collective-permute-start(bf16[1,18,16640]{2,1,0:T(8,128)(2,1)} %get-tuple-element.15), channel_id=1, source_target_pairs={{1,0},{2,1},{3,2},{5,4},{6,5},{7,6},{9,8},{10,9},{11,10},{13,12},{... | collective-permute-start | bytes 1797128 | tf_op jit(solution)/shard_map/ppermute | solution.py:127
  123.4 16.2 %copy-start.15 = (bf16[256,32]{0,1:T(8,128)(2,1)S(1)}, bf16[256,32]{0,1:T(8,128)(2,1)}, u32[]{:S(2)}) copy-start(bf16[256,32]{0,1:T(8,128)(2,1)} %get-tuple-element.44) | copy-start | bytes 49156
  123.4 12.9 %collective-permute-start.19 = (bf16[64,1024]{1,0:T(8,128)(2,1)S(1)}, bf16[64,1024]{1,0:T(8,128)(2,1)S(1)}, u32[]{:S(2)}, u32[]{:S(2)}) collective-permute-start(bf16[64,1024]{1,0:T(8,128)(2,1)S(1)} %add_convert_fusion.2), channel_id=1, source_target_pairs={{0,1},{1,0},{2,3},{3,2},{4,5},{5,4},{6,7},{7,6},{8,9},{9,8},{10,11... | collective-permute-start | bytes 393224 | tf_op jit(solution)/shard_map/ppermute | solution.py:107
  137.0 8.7 %collective-permute-start.20 = (bf16[64,1024]{1,0:T(8,128)(2,1)}, bf16[64,1024]{1,0:T(8,128)(2,1)}, u32[]{:S(2)}, u32[]{:S(2)}) collective-permute-start(bf16[64,1024]{1,0:T(8,128)(2,1)} %add_convert_fusion.1), channel_id=1, source_target_pairs={{0,2},{1,3},{2,0},{3,1},{4,6},{5,7},{6,4},{7,5},{8,10},{9,11},{10,... | collective-permute-start | bytes 393224 | tf_op jit(solution)/shard_map/ppermute | solution.py:107
  147.6 0.9 copy-start.14
  148.5 9.8 %copy-start.1 = (bf16[64,256]{1,0:T(8,128)(2,1)S(1)}, bf16[64,256]{1,0:T(8,128)(2,1)}, u32[]{:S(2)}) copy-start(bf16[64,256]{1,0:T(8,128)(2,1)} %param.9) | copy-start | bytes 98308

commit v18 on v15

--- a/solution.py
+++ b/solution.py
@@ -294,7 +294,6 @@
     ).astype(jnp.bfloat16)
     dblock = jnp.einsum("krc,kro->kco", coeffs, dcoef, preferred_element_type=jnp.float32)
     local_grads = split_gradients(dblock, channels)
-    dmode, local_grads, grad_act = lax.optimization_barrier((dmode, local_grads, grad_act))
     spectral_grad = share_inverse(dmode, cos_order, sin_order, channels)
     grad_spec = sum_gradients(local_grads)
     padded_grad = spatial_rims(grad_act, channels)

time: 155 us -> 159 us (1.026)
  local copies, waits for them, and re-layouts: 33.8 us -> 37.9 us
    ppermute x3, waiting for transfers between devices: 8.49 us -> 0.49 us  [butterfly_sum(): lax.ppermute(value, axis, [(i, i ^ step) for i in range(size)])]
    ppermute x4, waiting for transfers between devices: 3.69 us -> 10 us  [ring_reduce_scatter(): lax.ppermute(send, axis, [(i, i ^ step) for i in range(size)])]
    unnamed x42 -> x36, local copies, waits for them, and re-layouts: 1.6 us -> 4.5 us
    ppermute x4, starting transfers between devices: 6.64 us -> 8.77 us  [ring_reduce_scatter(): lax.ppermute(send, axis, [(i, i ^ step) for i in range(size)])]
    ppermute x4, waiting for transfers between devices: 3.44 us -> 5.27 us  [ring_gather(): lax.ppermute(block, axis, [(i, i ^ step) for i in range(size)])]
    ppermute x2, starting transfers between devices: 8.98 us -> 7.18 us  [spatial_rims(): below = lax.ppermute(inner[-1:], 'gz', up)]
  transfers between devices with their start and end apart: 21 -> 21, of which waited for: 9 -> 10; matrix products, arithmetic and copies ran while one was open for 31% -> 26% of each run, Pallas kernels for 12% -> 17%
where the time goes in v18:
time: 159 us; the launch traced here: 158 us
  local copies, waits for them, and re-layouts  37.9 us (24%)
  starting transfers between devices  36.2 us (23%)
  Pallas kernels  33 us (21%)
  matrix products  20.5 us (13%)
  waiting for transfers between devices  19.8 us (12%)
  other arithmetic  9.35 us (6%)
    pallas_call x4, Pallas kernels, stencil_call(): pl.pallas_call(kernel, out_shape=jax.ShapeDtypeStruct((len(plan), y_cells...  33 us
    ppermute x4, waiting for transfers between devices, ring_reduce_scatter(): lax.ppermute(send, axis, [(i, i ^ step) for i in range(size)])  10 us
    dot_general x1, matrix products, per_device(): jnp.dot(grad_hidden, expand_weight.T, preferred_element_type=jnp.float32)  8.79 us
    ppermute x4, starting transfers between devices, ring_reduce_scatter(): lax.ppermute(send, axis, [(i, i ^ step) for i in range(size)])  8.77 us
    ppermute x2, starting transfers between devices, spatial_rims(): below = lax.ppermute(inner[-1:], 'gz', up)  7.18 us
    ppermute x4, starting transfers between devices, ring_gather(): lax.ppermute(block, axis, [(i, i ^ step) for i in range(size)])  5.97 us
    ppermute x3, starting transfers between devices, butterfly_sum(): lax.ppermute(value, axis, [(i, i ^ step) for i in range(size)])  5.54 us
    ppermute x4, waiting for transfers between devices, ring_gather(): lax.ppermute(block, axis, [(i, i ^ step) for i in range(size)])  5.27 us
  transfers between devices with their start and end apart: 21, of which 10 were waited for; matrix products, arithmetic and copies ran while one was open for 26% of the time, Pallas kernels for 17%

profile of v18, /device:TPU:0, one launch (start us, length us, event | category | flops | bytes accessed | tf_op | source)
XLA Modules:
  0.0 158.0 jit_solution(11871597362866049056)
XLA Ops:
  0.7 3.0 %reshape.89 = bf16[32,256,64]{2,1,0:T(8,128)(2,1)S(1)} reshape(bf16[2,16,16384]{2,1,0:T(8,128)(2,1)} %param.7) | data formatting | bytes 2097152 | tf_op jit(solution)/shard_map/reshape | solution.py:258
  5.0 3.0 %collective-permute-start = (f32[16,32,128]{2,0,1:T(8,128)S(1)}, f32[16,32,128]{2,0,1:T(8,128)S(1)}, u32[]{:S(2)}, u32[]{:S(2)}) collective-permute-start(f32[16,32,128]{2,0,1:T(8,128)S(1)} %fusion.15), channel_id=1, source_target_pairs={{0,16},{8,24},{16,0},{24,8},{1,17},{9,25},{17,1},{25,9},{2,18},{10... | collective-permute-start | bytes 786440 | tf_op jit(solution)/shard_map/ppermute | solution.py:90
  8.7 1.5 collective-permute-start.2
  10.2 1.4 collective-permute-start.3
  11.7 1.7 %collective-permute-done.2 = bf16[2,16,128]{2,1,0:T(8,128)(2,1)S(1)} collective-permute-done((bf16[2,16,128]{2,1,0:T(8,128)(2,1)S(1)}, bf16[2,16,128]{2,1,0:T(8,128)(2,1)S(1)}, u32[]{:S(2)}, u32[]{:S(2)}) %collective-permute-start.2) | collective-permute-done | bytes 8224 | tf_op jit(solution)/shard_map/ppermute | solution.py:26
  13.9 1.0 copy-done.7
  15.3 1.2 collective-permute-done.4
  16.7 1.8 %pad_maximum_fusion.refs_0_ = bf16[2,18,16640]{2,1,0:T(8,128)(2,1)S(1)} fusion(bf16[2,1,16640]{2,1,0:T(2,128)(2,1)S(1)} %get-tuple-element.26, bf16[2,16,16640]{2,1,0:T(8,128)(2,1)} %copy-done.7, bf16[2,1,16640]{2,1,0:T(2,128)(2,1)S(1)} %get-tuple-element.25), kind=kLoop, calls=%fused_computation.23 | loop fusion | flops 3594240 | bytes 2396160 | tf_op jit(solution)/shard_map/concatenate | solution.py:28
  18.6 1.4 fusion.102
  20.0 4.4 %collective-permute-start.5 = (bf16[1,18,16640]{2,1,0:T(8,128)(2,1)}, bf16[1,18,16640]{2,1,0:T(8,128)(2,1)}, u32[]{:S(2)}, u32[]{:S(2)}) collective-permute-start(bf16[1,18,16640]{2,1,0:T(8,128)(2,1)} %get-tuple-element.12), channel_id=1, source_target_pairs={{0,1},{1,2},{2,3},{4,5},{5,6},{6,7},{8,9},{9,10},{10,11},{12,13},{... | collective-permute-start | bytes 1797128 | tf_op jit(solution)/shard_map/ppermute | solution.py:126
  24.4 1.5 collective-permute-start.6
  26.8 1.5 collective-permute-start.1
  28.3 3.0 %reshape.93 = bf16[32,256,64]{2,1,0:T(8,128)(2,1)S(1)} reshape(bf16[2,16,16384]{2,1,0:T(8,128)(2,1)} %param.13) | data formatting | bytes 2097152 | tf_op jit(solution)/shard_map/reshape | solution.py:278
  31.3 1.6 %copy.30 = bf16[32,256,64]{1,2,0:T(8,128)(2,1)} copy(bf16[32,256,64]{2,1,0:T(8,128)(2,1)S(1)} %reshape.93) | data formatting | bytes 2097152 | tf_op jit(solution)/shard_map/optimization_barrier | solution.py:278
  33.3 1.1 fusion.19
  35.1 9.6 %shard_map.94.refs_2_ = f32[2,16,16384]{2,1,0:T(8,128)} custom-call(bf16[2,18,16640]{2,1,0:T(8,128)(2,1)} %copy-done.2, f32[27,8,128]{2,1,0:T(8,128)} %broadcast_in_dim.18.refs_1_.refs_3_), custom_call_target="tpu_custom_call" | custom-call | tf_op jit(solution)/shard_map/pallas_call | solution.py:179
  46.2 6.7 %shard_map.95 = bf16[2,16,16384]{2,1,0:T(8,128)(2,1)} custom-call(bf16[1,18,16640]{2,1,0:T(8,128)(2,1)} %collective-permute-done.5.refs_0_, bf16[1,18,16640]{2,1,0:T(8,128)(2,1)} %collective-permute-done.6.refs_1_, f32[2,16,16384]{2,1,0:T(8,128)} %shard_map.94.refs_2_, f32[27,8,128]{2,1,0:T(8,128)} %broadcast_in_dim.18.refs_1_.refs_3_), custom_call_target="tpu_custom_call" | custom-call | tf_op jit(solution)/shard_map/pallas_call | solution.py:179
  52.9 1.5 collective-permute-start.7
  54.4 3.0 %reshape.90 = bf16[8192,64]{1,0:T(8,128)(2,1)S(1)} reshape(bf16[2,16,16384]{2,1,0:T(8,128)(2,1)} %shard_map.95) | data formatting | bytes 2097152 | tf_op jit(solution)/shard_map/reshape | solution.py:267
  57.5 1.2 fusion.107
  58.7 2.8 %fusion.5 = f32[8192,64]{0,1:T(8,128)S(1)} fusion(bf16[256,64]{0,1:T(8,128)(2,1)S(1)} %copy-done.13, f32[8192,256]{1,0:T(8,128)S(1)} %fusion.107), kind=kOutput, calls=%fused_computation.10 | convolution fusion | flops 278921216 | bytes 10518528 | tf_op jit(solution)/shard_map/dot_general | solution.py:270
  62.0 1.6 %collective-permute-start.8 = (bf16[16,32,128]{2,1,0:T(8,128)(2,1)S(1)}, bf16[16,32,128]{2,1,0:T(8,128)(2,1)S(1)}, u32[]{:S(2)}, u32[]{:S(2)}) collective-permute-start(bf16[16,32,128]{2,1,0:T(8,128)(2,1)S(1)} %pad_maximum_fusion.4), channel_id=1, source_target_pairs={{0,16},{8,24},{16,0},{24,8},{1,17},{9,25},{17,1},{25,9},{2,18},{10... | collective-permute-start | bytes 393224 | tf_op jit(solution)/shard_map/ppermute | solution.py:68
  63.6 3.4 %collective-permute-done.8 = bf16[16,32,128]{2,1,0:T(8,128)(2,1)S(1)} collective-permute-done((bf16[16,32,128]{2,1,0:T(8,128)(2,1)S(1)}, bf16[16,32,128]{2,1,0:T(8,128)(2,1)S(1)}, u32[]{:S(2)}, u32[]{:S(2)}) %collective-permute-start.8) | collective-permute-done | bytes 131104 | tf_op jit(solution)/shard_map/ppermute | solution.py:68
  67.8 2.7 %fusion.11 = (bf16[32,256,64]{1,2,0:T(8,128)(2,1)S(1)}, bf16[32,256,64]{1,2,0:T(8,128)(2,1)}) fusion(bf16[32,256,64]{1,2,0:T(8,128)(2,1)S(1)} %copy-done.8, f32[256,32,64]{0,2,1:T(8,128)S(1)} %fusion.26, bf16[32,32,64]{2,1,0:T(8,128)(2,1)S(1)} %get-tuple-element.21, f32[32]{0:T(128)S(1)} %get-tuple-element.27, s32[32]{0:T(128)S(1)} %add.140, ...), kind=kOutput, calls=%fused_computation.17 | convolution fusion | flops 41566208 | bytes 7472384 | tf_op jit(solution)/shard_map/krc,xk->rxc/dot_general | solution.py:215
  71.3 8.8 %convolution_convert_fusion = bf16[8192,64]{0,1:T(8,128)(2,1)} fusion(bf16[64,256]{1,0:T(8,128)(2,1)S(1)} %copy-done, bf16[8192,64]{0,1:T(8,128)(2,1)S(1)} %bitcast.54, bf16[256,64]{0,1:T(8,128)(2,1)S(1)} %copy-done.14, f32[8192,256]{1,0:T(8,128)} %copy-done.4), kind=kOutput, calls=%fused_computation.3 | convolution fusion | flops 558366720 | bytes 10551296 | tf_op jit(solution)/shard_map/dot_general | solution.py:287
  80.1 2.0 %copy.32 = bf16[8192,64]{1,0:T(8,128)(2,1)S(1)} copy(bf16[8192,64]{0,1:T(8,128)(2,1)} %convolution_convert_fusion) | data formatting | bytes 2097152 | tf_op jit(solution)/shard_map/convert_element_type | solution.py:287
  82.2 2.5 %reshape.95 = bf16[2,16,16384]{2,1,0:T(8,128)(2,1)} reshape(bf16[8192,64]{1,0:T(8,128)(2,1)S(1)} %copy.32) | data formatting | bytes 2097152 | tf_op jit(solution)/shard_map/reshape | solution.py:290
  87.2 2.0 %copy.29 = bf16[32,256,64]{2,1,0:T(8,128)(2,1)S(1)} copy(bf16[32,256,64]{1,2,0:T(8,128)(2,1)} %get-tuple-element.8) | data formatting | bytes 2097152 | tf_op jit(solution)/shard_map/convert_element_type | solution.py:276
  89.3 2.5 %reshape.92 = bf16[2,16,16384]{2,1,0:T(8,128)(2,1)} reshape(bf16[32,256,64]{2,1,0:T(8,128)(2,1)S(1)} %copy.29) | data formatting | bytes 2097152 | tf_op jit(solution)/shard_map/reshape | solution.py:276
  91.7 2.4 %collective-permute-start.10 = (bf16[2,16,128]{2,1,0:T(8,128)(2,1)S(1)}, bf16[2,16,128]{2,1,0:T(8,128)(2,1)S(1)}, u32[]{:S(2)}, u32[]{:S(2)}) collective-permute-start(bf16[2,16,128]{2,1,0:T(8,128)(2,1)S(1)} %get-tuple-element.13), channel_id=1, source_target_pairs={{8,0},{16,8},{24,16},{0,24},{9,1},{17,9},{25,17},{1,25},{10,2},{18... | collective-permute-start | bytes 24584 | tf_op jit(solution)/shard_map/ppermute | solution.py:27
  94.1 1.3 constant_dynamic-update-slice_fusion.7
  96.3 1.3 collective-permute-start.14
  97.8 7.3 %collective-permute-done.14 = f32[16,32,128]{2,0,1:T(8,128)S(1)} collective-permute-done((f32[16,32,128]{2,0,1:T(8,128)S(1)}, f32[16,32,128]{2,0,1:T(8,128)S(1)}, u32[]{:S(2)}, u32[]{:S(2)}) %collective-permute-start.14) | collective-permute-done | bytes 262176 | tf_op jit(solution)/shard_map/ppermute | solution.py:90
  105.2 3.0 %collective-permute-start.15 = (f32[8,32,128]{2,0,1:T(8,128)S(1)}, f32[8,32,128]{2,0,1:T(8,128)S(1)}, u32[]{:S(2)}, u32[]{:S(2)}) collective-permute-start(f32[8,32,128]{2,0,1:T(8,128)S(1)} %constant_dynamic-slice_fusion), channel_id=1, source_target_pairs={{0,8},{8,0},{16,24},{24,16},{1,9},{9,1},{17,25},{25,17},{2,10},{10... | collective-permute-start | bytes 393224 | tf_op jit(solution)/shard_map/ppermute | solution.py:90
  108.8 2.8 %collective-permute-done.15 = f32[8,32,128]{2,0,1:T(8,128)S(1)} collective-permute-done((f32[8,32,128]{2,0,1:T(8,128)S(1)}, f32[8,32,128]{2,0,1:T(8,128)S(1)}, u32[]{:S(2)}, u32[]{:S(2)}) %collective-permute-start.15) | collective-permute-done | bytes 131104 | tf_op jit(solution)/shard_map/ppermute | solution.py:90
  112.1 1.8 %collective-permute-start.16 = (bf16[8,32,128]{2,1,0:T(8,128)(2,1)S(1)}, bf16[8,32,128]{2,1,0:T(8,128)(2,1)S(1)}, u32[]{:S(2)}, u32[]{:S(2)}) collective-permute-start(bf16[8,32,128]{2,1,0:T(8,128)(2,1)S(1)} %convolution_convert_fusion.1), channel_id=1, source_target_pairs={{0,8},{8,0},{16,24},{24,16},{1,9},{9,1},{17,25},{25,17},{2,10},{10... | collective-permute-start | bytes 196616 | tf_op jit(solution)/shard_map/ppermute | solution.py:68
  114.5 1.3 fusion.101
  115.8 2.8 %collective-permute-start.12 = (bf16[1,18,16640]{2,1,0:T(8,128)(2,1)}, bf16[1,18,16640]{2,1,0:T(8,128)(2,1)S(1)}, u32[]{:S(2)}, u32[]{:S(2)}) collective-permute-start(bf16[1,18,16640]{2,1,0:T(8,128)(2,1)} %get-tuple-element.10), channel_id=1, source_target_pairs={{0,1},{1,2},{2,3},{4,5},{5,6},{6,7},{8,9},{9,10},{10,11},{12,13},{... | collective-permute-start | bytes 1797128 | tf_op jit(solution)/shard_map/ppermute | solution.py:126
  118.6 1.3 collective-permute-start.13
  120.6 9.6 %shard_map.96.refs_2_ = f32[2,16,16384]{2,1,0:T(8,128)} custom-call(bf16[2,18,16640]{2,1,0:T(8,128)(2,1)} %copy-done.3, f32[27,8,128]{2,1,0:T(8,128)} %broadcast_in_dim.36.refs_1_.refs_3_), custom_call_target="tpu_custom_call" | custom-call | tf_op jit(solution)/shard_map/pallas_call | solution.py:179
  130.2 1.1 collective-permute-start.17
  131.3 2.7 %collective-permute-start.19 = (bf16[64,1024]{1,0:T(8,128)(2,1)S(1)}, bf16[64,1024]{1,0:T(8,128)(2,1)S(1)}, u32[]{:S(2)}, u32[]{:S(2)}) collective-permute-start(bf16[64,1024]{1,0:T(8,128)(2,1)S(1)} %add_convert_fusion.2), channel_id=1, source_target_pairs={{0,1},{1,0},{2,3},{3,2},{4,5},{5,4},{6,7},{7,6},{8,9},{9,8},{10,11... | collective-permute-start | bytes 393224 | tf_op jit(solution)/shard_map/ppermute | solution.py:107
  134.0 1.8 %collective-permute-done.17 = bf16[16,32,128]{2,1,0:T(8,128)(2,1)S(1)} collective-permute-done((bf16[16,32,128]{2,1,0:T(8,128)(2,1)S(1)}, bf16[16,32,128]{2,1,0:T(8,128)(2,1)S(1)}, u32[]{:S(2)}, u32[]{:S(2)}) %collective-permute-start.17) | collective-permute-done | bytes 131104 | tf_op jit(solution)/shard_map/ppermute | solution.py:68
  137.3 2.7 %copy.36 = f32[32,256,64]{2,1,0:T(8,128)} copy(f32[32,256,64]{1,2,0:T(8,128)S(1)} %add_bitcast_fusion) | data formatting | bytes 4194304 | tf_op jit(solution)/shard_map/add | solution.py:218
  140.0 2.9 %reshape.96 = f32[2,16,16384]{2,1,0:T(8,128)S(1)} reshape(f32[32,256,64]{2,1,0:T(8,128)} %copy.36) | data formatting | bytes 4194304 | tf_op jit(solution)/shard_map/reshape | solution.py:301
  143.5 2.8 %collective-permute-start.20 = (bf16[64,1024]{1,0:T(8,128)(2,1)S(1)}, bf16[64,1024]{1,0:T(8,128)(2,1)S(1)}, u32[]{:S(2)}, u32[]{:S(2)}) collective-permute-start(bf16[64,1024]{1,0:T(8,128)(2,1)S(1)} %add_convert_fusion.1), channel_id=1, source_target_pairs={{0,2},{1,3},{2,0},{3,1},{4,6},{5,7},{6,4},{7,5},{8,10},{9,11},{10,... | collective-permute-start | bytes 393224 | tf_op jit(solution)/shard_map/ppermute | solution.py:107
  147.1 7.1 %shard_map.97 = f32[2,16,16384]{2,1,0:T(8,128)} custom-call(bf16[1,18,16640]{2,1,0:T(8,128)(2,1)} %copy-done.11, bf16[1,18,16640]{2,1,0:T(8,128)(2,1)} %collective-permute-done.13.refs_1_, f32[2,16,16384]{2,1,0:T(8,128)} %shard_map.96.refs_2_, f32[27,8,128]{2,1,0:T(8,128)} %broadcast_in_dim.36.refs_1_.refs_3_), custom_call_target="tpu_custom_call" | custom-call | tf_op jit(solution)/shard_map/pallas_call | solution.py:179
  154.2 2.7 %add_convert_fusion = bf16[2,16,16384]{2,1,0:T(8,128)(2,1)} fusion(f32[2,16,16384]{2,1,0:T(8,128)} %shard_map.97, f32[2,16,16384]{2,1,0:T(8,128)S(1)} %reshape.96), kind=kLoop, calls=%fused_computation.19 | loop fusion | flops 1048576 | bytes 5242880 | tf_op jit(solution)/shard_map/convert_element_type | solution.py:301
  (107 shorter events, 18.4 us)
Async XLA Ops:
  0.6 56.8 %copy-start = (bf16[64,256]{1,0:T(8,128)(2,1)S(1)}, bf16[64,256]{1,0:T(8,128)(2,1)}, u32[]{:S(2)}) copy-start(bf16[64,256]{1,0:T(8,128)(2,1)} %param.9) | copy-start | bytes 98308
  4.8 8.6 %copy-start.5 = (bf16[2,16,16384]{2,1,0:T(8,128)(2,1)S(1)}, bf16[2,16,16384]{2,1,0:T(8,128)(2,1)}, u32[]{:S(2)}) copy-start(bf16[2,16,16384]{2,1,0:T(8,128)(2,1)} %param.7) | copy-start | bytes 3145732
  5.0 20.9 %collective-permute-start = (f32[16,32,128]{2,0,1:T(8,128)S(1)}, f32[16,32,128]{2,0,1:T(8,128)S(1)}, u32[]{:S(2)}, u32[]{:S(2)}) collective-permute-start(f32[16,32,128]{2,0,1:T(8,128)S(1)} %fusion.15), channel_id=1, source_target_pairs={{0,16},{8,24},{16,0},{24,8},{1,17},{9,25},{17,1},{25,9},{2,18},{10... | collective-permute-start | bytes 786440 | tf_op jit(solution)/shard_map/ppermute | solution.py:90
  8.7 4.7 %collective-permute-start.2 = (bf16[2,16,128]{2,1,0:T(8,128)(2,1)S(1)}, bf16[2,16,128]{2,1,0:T(8,128)(2,1)S(1)}, u32[]{:S(2)}, u32[]{:S(2)}) collective-permute-start(bf16[2,16,128]{2,1,0:T(8,128)(2,1)S(1)} %get-tuple-element.16), channel_id=1, source_target_pairs={{0,8},{8,16},{16,24},{24,0},{1,9},{9,17},{17,25},{25,1},{2,10},{10... | collective-permute-start | bytes 24584 | tf_op jit(solution)/shard_map/ppermute | solution.py:26
  10.2 3.7 %collective-permute-start.3 = (bf16[2,16,128]{2,1,0:T(8,128)(2,1)S(1)}, bf16[2,16,128]{2,1,0:T(8,128)(2,1)S(1)}, u32[]{:S(2)}, u32[]{:S(2)}) collective-permute-start(bf16[2,16,128]{2,1,0:T(8,128)(2,1)S(1)} %get-tuple-element.15), channel_id=1, source_target_pairs={{8,0},{16,8},{24,16},{0,24},{9,1},{17,9},{25,17},{1,25},{10,2},{18... | collective-permute-start | bytes 24584 | tf_op jit(solution)/shard_map/ppermute | solution.py:27
  13.9 1.0 copy-start.7
  15.1 1.4 collective-permute-start.4
  18.6 7.4 %copy-start.2 = (bf16[2,18,16640]{2,1,0:T(8,128)(2,1)}, bf16[2,18,16640]{2,1,0:T(8,128)(2,1)S(1)}, u32[]{:S(2)}) copy-start(bf16[2,18,16640]{2,1,0:T(8,128)(2,1)S(1)} %pad_maximum_fusion.refs_0_) | copy-start | bytes 3594244
  20.0 25.8 %collective-permute-start.5 = (bf16[1,18,16640]{2,1,0:T(8,128)(2,1)}, bf16[1,18,16640]{2,1,0:T(8,128)(2,1)}, u32[]{:S(2)}, u32[]{:S(2)}) collective-permute-start(bf16[1,18,16640]{2,1,0:T(8,128)(2,1)} %get-tuple-element.12), channel_id=1, source_target_pairs={{0,1},{1,2},{2,3},{4,5},{5,6},{6,7},{8,9},{9,10},{10,11},{12,13},{... | collective-permute-start | bytes 1797128 | tf_op jit(solution)/shard_map/ppermute | solution.py:126
  24.4 21.8 %collective-permute-start.6 = (bf16[1,18,16640]{2,1,0:T(8,128)(2,1)}, bf16[1,18,16640]{2,1,0:T(8,128)(2,1)}, u32[]{:S(2)}, u32[]{:S(2)}) collective-permute-start(bf16[1,18,16640]{2,1,0:T(8,128)(2,1)} %get-tuple-element.11), channel_id=1, source_target_pairs={{1,0},{2,1},{3,2},{5,4},{6,5},{7,6},{9,8},{10,9},{11,10},{13,12},{... | collective-permute-start | bytes 1797128 | tf_op jit(solution)/shard_map/ppermute | solution.py:127
  26.0 0.7 copy-start.9
  26.8 17.9 %collective-permute-start.1 = (f32[8,32,128]{2,0,1:T(8,128)}, f32[8,32,128]{2,0,1:T(8,128)}, u32[]{:S(2)}, u32[]{:S(2)}) collective-permute-start(f32[8,32,128]{2,0,1:T(8,128)} %constant_dynamic-slice_fusion.1), channel_id=1, source_target_pairs={{0,8},{8,0},{16,24},{24,16},{1,9},{9,1},{17,25},{25,17},{2,10},{10... | collective-permute-start | bytes 393224 | tf_op jit(solution)/shard_map/ppermute | solution.py:90
  31.3 1.6 %copy-start.6 = (bf16[32,64,64]{2,1,0:T(8,128)(2,1)S(1)}, bf16[32,64,64]{2,1,0:T(8,128)(2,1)}, u32[]{:S(2)}) copy-start(bf16[32,64,64]{2,1,0:T(8,128)(2,1)} %param.12) | copy-start | bytes 786436
  31.3 1.8 %copy-start.12 = (bf16[27,64]{1,0:T(8,128)(2,1)S(1)}, bf16[27,64]{1,0:T(8,128)(2,1)}, u32[]{:S(2)}) copy-start(bf16[27,64]{1,0:T(8,128)(2,1)} %param.8) | copy-start | bytes 10372
  34.5 10.2 %copy-start.10 = (f32[16,32,128]{2,0,1:T(8,128)S(1)}, f32[16,32,128]{2,0,1:T(8,128)}, u32[]{:S(2)}) copy-start(f32[16,32,128]{2,0,1:T(8,128)} %copy-done.9) | copy-start | bytes 786436
  52.9 9.1 %collective-permute-start.7 = (bf16[8,32,128]{2,1,0:T(8,128)(2,1)S(1)}, bf16[8,32,128]{2,1,0:T(8,128)(2,1)S(1)}, u32[]{:S(2)}, u32[]{:S(2)}) collective-permute-start(bf16[8,32,128]{2,1,0:T(8,128)(2,1)S(1)} %convolution_convert_fusion.2), channel_id=1, source_target_pairs={{0,8},{8,0},{16,24},{24,16},{1,9},{9,1},{17,25},{25,17},{2,10},{10... | collective-permute-start | bytes 196616 | tf_op jit(solution)/shard_map/ppermute | solution.py:68
  57.5 1.2 copy-start.13
  58.7 3.3 %copy-start.4 = (f32[8192,256]{1,0:T(8,128)}, f32[8192,256]{1,0:T(8,128)S(1)}, u32[]{:S(2)}) copy-start(f32[8192,256]{1,0:T(8,128)S(1)} %fusion.107) | copy-start | bytes 25165828
  62.0 5.8 %copy-start.8 = (bf16[32,256,64]{1,2,0:T(8,128)(2,1)S(1)}, bf16[32,256,64]{1,2,0:T(8,128)(2,1)}, u32[]{:S(2)}) copy-start(bf16[32,256,64]{1,2,0:T(8,128)(2,1)} %copy.30) | copy-start | bytes 3145732
  62.0 5.0 %collective-permute-start.8 = (bf16[16,32,128]{2,1,0:T(8,128)(2,1)S(1)}, bf16[16,32,128]{2,1,0:T(8,128)(2,1)S(1)}, u32[]{:S(2)}, u32[]{:S(2)}) collective-permute-start(bf16[16,32,128]{2,1,0:T(8,128)(2,1)S(1)} %pad_maximum_fusion.4), channel_id=1, source_target_pairs={{0,16},{8,24},{16,0},{24,8},{1,17},{9,25},{17,1},{25,9},{2,18},{10... | collective-permute-start | bytes 393224 | tf_op jit(solution)/shard_map/ppermute | solution.py:68
  70.6 0.8 copy-start.14
  85.4 8.7 %collective-permute-start.9 = (bf16[2,16,128]{2,1,0:T(8,128)(2,1)S(1)}, bf16[2,16,128]{2,1,0:T(8,128)(2,1)S(1)}, u32[]{:S(2)}, u32[]{:S(2)}) collective-permute-start(bf16[2,16,128]{2,1,0:T(8,128)(2,1)S(1)} %get-tuple-element.14), channel_id=1, source_target_pairs={{0,8},{8,16},{16,24},{24,0},{1,9},{9,17},{17,25},{25,1},{2,10},{10... | collective-permute-start | bytes 24584 | tf_op jit(solution)/shard_map/ppermute | solution.py:26
  91.7 4.1 %collective-permute-start.10 = (bf16[2,16,128]{2,1,0:T(8,128)(2,1)S(1)}, bf16[2,16,128]{2,1,0:T(8,128)(2,1)S(1)}, u32[]{:S(2)}, u32[]{:S(2)}) collective-permute-start(bf16[2,16,128]{2,1,0:T(8,128)(2,1)S(1)} %get-tuple-element.13), channel_id=1, source_target_pairs={{8,0},{16,8},{24,16},{0,24},{9,1},{17,9},{25,17},{1,25},{10,2},{18... | collective-permute-start | bytes 24584 | tf_op jit(solution)/shard_map/ppermute | solution.py:27
  96.0 1.5 collective-permute-start.11
  96.3 8.8 %collective-permute-start.14 = (f32[16,32,128]{2,0,1:T(8,128)S(1)}, f32[16,32,128]{2,0,1:T(8,128)S(1)}, u32[]{:S(2)}, u32[]{:S(2)}) collective-permute-start(f32[16,32,128]{2,0,1:T(8,128)S(1)} %fusion.12), channel_id=1, source_target_pairs={{0,16},{8,24},{16,0},{24,8},{1,17},{9,25},{17,1},{25,9},{2,18},{10... | collective-permute-start | bytes 786440 | tf_op jit(solution)/shard_map/ppermute | solution.py:90
  105.2 6.4 %collective-permute-start.15 = (f32[8,32,128]{2,0,1:T(8,128)S(1)}, f32[8,32,128]{2,0,1:T(8,128)S(1)}, u32[]{:S(2)}, u32[]{:S(2)}) collective-permute-start(f32[8,32,128]{2,0,1:T(8,128)S(1)} %constant_dynamic-slice_fusion), channel_id=1, source_target_pairs={{0,8},{8,0},{16,24},{24,16},{1,9},{9,1},{17,25},{25,17},{2,10},{10... | collective-permute-start | bytes 393224 | tf_op jit(solution)/shard_map/ppermute | solution.py:90
  108.8 7.0 %copy-start.3 = (bf16[2,18,16640]{2,1,0:T(8,128)(2,1)}, bf16[2,18,16640]{2,1,0:T(8,128)(2,1)S(1)}, u32[]{:S(2)}) copy-start(bf16[2,18,16640]{2,1,0:T(8,128)(2,1)S(1)} %pad_maximum_fusion.1.refs_0_) | copy-start | bytes 3594244
  112.1 18.0 %collective-permute-start.16 = (bf16[8,32,128]{2,1,0:T(8,128)(2,1)S(1)}, bf16[8,32,128]{2,1,0:T(8,128)(2,1)S(1)}, u32[]{:S(2)}, u32[]{:S(2)}) collective-permute-start(bf16[8,32,128]{2,1,0:T(8,128)(2,1)S(1)} %convolution_convert_fusion.1), channel_id=1, source_target_pairs={{0,8},{8,0},{16,24},{24,16},{1,9},{9,1},{17,25},{25,17},{2,10},{10... | collective-permute-start | bytes 196616 | tf_op jit(solution)/shard_map/ppermute | solution.py:68
  114.4 16.9 %collective-permute-start.18 = (bf16[64,1024]{1,0:T(8,128)(2,1)S(1)}, bf16[64,1024]{1,0:T(8,128)(2,1)S(1)}, u32[]{:S(2)}, u32[]{:S(2)}) collective-permute-start(bf16[64,1024]{1,0:T(8,128)(2,1)S(1)} %convert_element_type.136), channel_id=1, source_target_pairs={{0,4},{4,0},{1,5},{5,1},{2,6},{6,2},{3,7},{7,3},{8,12},{12,8},{9,1... | collective-permute-start | bytes 393224 | tf_op jit(solution)/shard_map/ppermute | solution.py:107
  115.8 30.4 %collective-permute-start.12 = (bf16[1,18,16640]{2,1,0:T(8,128)(2,1)}, bf16[1,18,16640]{2,1,0:T(8,128)(2,1)S(1)}, u32[]{:S(2)}, u32[]{:S(2)}) collective-permute-start(bf16[1,18,16640]{2,1,0:T(8,128)(2,1)} %get-tuple-element.10), channel_id=1, source_target_pairs={{0,1},{1,2},{2,3},{4,5},{5,6},{6,7},{8,9},{9,10},{10,11},{12,13},{... | collective-permute-start | bytes 1797128 | tf_op jit(solution)/shard_map/ppermute | solution.py:126
  118.6 27.6 %collective-permute-start.13 = (bf16[1,18,16640]{2,1,0:T(8,128)(2,1)}, bf16[1,18,16640]{2,1,0:T(8,128)(2,1)}, u32[]{:S(2)}, u32[]{:S(2)}) collective-permute-start(bf16[1,18,16640]{2,1,0:T(8,128)(2,1)} %get-tuple-element.9), channel_id=1, source_target_pairs={{1,0},{2,1},{3,2},{5,4},{6,5},{7,6},{9,8},{10,9},{11,10},{13,12},{... | collective-permute-start | bytes 1797128 | tf_op jit(solution)/shard_map/ppermute | solution.py:127
  130.2 5.7 %collective-permute-start.17 = (bf16[16,32,128]{2,1,0:T(8,128)(2,1)S(1)}, bf16[16,32,128]{2,1,0:T(8,128)(2,1)S(1)}, u32[]{:S(2)}, u32[]{:S(2)}) collective-permute-start(bf16[16,32,128]{2,1,0:T(8,128)(2,1)S(1)} %pad_maximum_fusion.5), channel_id=1, source_target_pairs={{0,16},{8,24},{16,0},{24,8},{1,17},{9,25},{17,1},{25,9},{2,18},{10... | collective-permute-start | bytes 393224 | tf_op jit(solution)/shard_map/ppermute | solution.py:68
  131.3 12.1 %collective-permute-start.19 = (bf16[64,1024]{1,0:T(8,128)(2,1)S(1)}, bf16[64,1024]{1,0:T(8,128)(2,1)S(1)}, u32[]{:S(2)}, u32[]{:S(2)}) collective-permute-start(bf16[64,1024]{1,0:T(8,128)(2,1)S(1)} %add_convert_fusion.2), channel_id=1, source_target_pairs={{0,1},{1,0},{2,3},{3,2},{4,5},{5,4},{6,7},{7,6},{8,9},{9,8},{10,11... | collective-permute-start | bytes 393224 | tf_op jit(solution)/shard_map/ppermute | solution.py:107
  143.5 13.5 %collective-permute-start.20 = (bf16[64,1024]{1,0:T(8,128)(2,1)S(1)}, bf16[64,1024]{1,0:T(8,128)(2,1)S(1)}, u32[]{:S(2)}, u32[]{:S(2)}) collective-permute-start(bf16[64,1024]{1,0:T(8,128)(2,1)S(1)} %add_convert_fusion.1), channel_id=1, source_target_pairs={{0,2},{1,3},{2,0},{3,1},{4,6},{5,7},{6,4},{7,5},{8,10},{9,11},{10,... | collective-permute-start | bytes 393224 | tf_op jit(solution)/shard_map/ppermute | solution.py:107
  146.2 0.9 copy-start.11
  147.1 10.8 %copy-start.1 = (bf16[64,256]{1,0:T(8,128)(2,1)S(1)}, bf16[64,256]{1,0:T(8,128)(2,1)}, u32[]{:S(2)}) copy-start(bf16[64,256]{1,0:T(8,128)(2,1)} %param.9) | copy-start | bytes 98308

commit v19 on v15

--- a/solution.py
+++ b/solution.py
@@ -263,7 +263,6 @@
     mixed_modes = jnp.einsum(
         "krc,kco->kro", coeffs, owned_blocks, preferred_element_type=jnp.float32
     ).astype(jnp.bfloat16)
-    mixed_modes, activation = lax.optimization_barrier((mixed_modes, activation))
     activation = activation.reshape(row_count * x_cells, channels)
     hidden_pre = jnp.dot(activation, expand_weight, preferred_element_type=jnp.float32)
     hidden, hidden_slope = gelu_parts(hidden_pre)

time: 155 us -> 160 us (1.032)
  waiting for transfers between devices: 21 us -> 29 us
  starting transfers between devices: 35.6 us -> 29.2 us
  local copies, waits for them, and re-layouts: 33.8 us -> 36.5 us
    ppermute x4, waiting for transfers between devices: 3.69 us -> 8.73 us  [ring_reduce_scatter(): lax.ppermute(send, axis, [(i, i ^ step) for i in range(size)])]
    ppermute x2, waiting for transfers between devices: 0.28 us -> 4.17 us  [spatial_rims(): above = lax.ppermute(inner[:1], 'gz', down)]
    unnamed x42 -> x38, local copies, waits for them, and re-layouts: 1.6 us -> 3.91 us
    ppermute x4, starting transfers between devices: 5.36 us -> 3.07 us  [ring_gather(): lax.ppermute(block, axis, [(i, i ^ step) for i in range(size)])]
    ppermute x2, waiting for transfers between devices: 1.73 us -> 0.01 us  [padded_2(): before = lax.ppermute(last, axis, up)]
  transfers between devices with their start and end apart: 21 -> 21, of which waited for: 9 -> 8; matrix products, arithmetic and copies ran while one was open for 31% -> 27% of each run, Pallas kernels for 12% -> 12%
where the time goes in v19:
time: 160 us
  local copies, waits for them, and re-layouts  36.5 us (23%)
  Pallas kernels  33 us (21%)
  starting transfers between devices  29.2 us (18%)
  waiting for transfers between devices  29 us (18%)
  matrix products  20.9 us (13%)
  other arithmetic  9.92 us (6%)
    pallas_call x4, Pallas kernels, stencil_call(): pl.pallas_call(kernel, out_shape=jax.ShapeDtypeStruct((len(plan), y_cells...  33 us
    ppermute x3, waiting for transfers between devices, butterfly_sum(): lax.ppermute(value, axis, [(i, i ^ step) for i in range(size)])  9.4 us
    ppermute x4, waiting for transfers between devices, ring_reduce_scatter(): lax.ppermute(send, axis, [(i, i ^ step) for i in range(size)])  8.73 us
    dot_general x1, matrix products, per_device(): jnp.dot(grad_hidden, expand_weight.T, preferred_element_type=jnp.float32)  7.88 us
    ppermute x2, starting transfers between devices, spatial_rims(): below = lax.ppermute(inner[-1:], 'gz', up)  7.44 us
    ppermute x4, starting transfers between devices, ring_reduce_scatter(): lax.ppermute(send, axis, [(i, i ^ step) for i in range(size)])  5.81 us
    ppermute x2, waiting for transfers between devices, spatial_rims(): above = lax.ppermute(inner[:1], 'gz', down)  4.17 us
    ppermute x3, starting transfers between devices, butterfly_sum(): lax.ppermute(value, axis, [(i, i ^ step) for i in range(size)])  4.11 us
  transfers between devices with their start and end apart: 21, of which 8 were waited for; matrix products, arithmetic and copies ran while one was open for 27% of the time, Pallas kernels for 12%

profile of v19, /device:TPU:0, one launch (start us, length us, event | category | flops | bytes accessed | tf_op | source)
XLA Modules:
  0.0 159.7 jit_solution(13926003379313193172)
XLA Ops:
  0.7 3.0 %reshape.91 = bf16[32,256,64]{2,1,0:T(8,128)(2,1)S(1)} reshape(bf16[2,16,16384]{2,1,0:T(8,128)(2,1)} %param.7) | data formatting | bytes 2097152 | tf_op jit(solution)/shard_map/reshape | solution.py:258
  5.7 3.0 %collective-permute-start.5 = (f32[16,32,128]{2,0,1:T(8,128)}, f32[16,32,128]{2,0,1:T(8,128)}, u32[]{:S(2)}, u32[]{:S(2)}) collective-permute-start(f32[16,32,128]{2,0,1:T(8,128)} %fusion.19), channel_id=1, source_target_pairs={{0,16},{8,24},{16,0},{24,8},{1,17},{9,25},{17,1},{25,9},{2,18},{10... | collective-permute-start | bytes 786440 | tf_op jit(solution)/shard_map/ppermute | solution.py:90
  9.4 1.5 collective-permute-start
  10.9 1.4 collective-permute-start.1
  12.3 1.2 neg.10
  13.8 3.0 %reshape.93 = bf16[32,256,64]{2,1,0:T(8,128)(2,1)S(1)} reshape(bf16[2,16,16384]{2,1,0:T(8,128)(2,1)} %param.13) | data formatting | bytes 2097152 | tf_op jit(solution)/shard_map/reshape | solution.py:277
  16.9 1.6 %copy.30 = bf16[32,256,64]{1,2,0:T(8,128)(2,1)} copy(bf16[32,256,64]{2,1,0:T(8,128)(2,1)S(1)} %reshape.93) | data formatting | bytes 2097152 | tf_op jit(solution)/shard_map/optimization_barrier | solution.py:277
  18.6 1.3 constant_dynamic-update-slice_fusion.1
  20.2 1.1 fusion.21
  22.3 5.1 %collective-permute-done.6 = f32[8,32,128]{2,0,1:T(8,128)S(1)} collective-permute-done((f32[8,32,128]{2,0,1:T(8,128)S(1)}, f32[8,32,128]{2,0,1:T(8,128)S(1)}, u32[]{:S(2)}, u32[]{:S(2)}) %collective-permute-start.6) | collective-permute-done | bytes 131104 | tf_op jit(solution)/shard_map/ppermute | solution.py:90
  28.8 3.1 %collective-permute-done.7 = bf16[8,32,128]{2,1,0:T(8,128)(2,1)S(1)} collective-permute-done((bf16[8,32,128]{2,1,0:T(8,128)(2,1)S(1)}, bf16[8,32,128]{2,1,0:T(8,128)(2,1)S(1)}, u32[]{:S(2)}, u32[]{:S(2)}) %collective-permute-start.7) | collective-permute-done | bytes 65568 | tf_op jit(solution)/shard_map/ppermute | solution.py:68
  32.0 1.3 fusion.104
  33.3 4.0 %collective-permute-start.3 = (bf16[1,18,16640]{2,1,0:T(8,128)(2,1)}, bf16[1,18,16640]{2,1,0:T(8,128)(2,1)S(1)}, u32[]{:S(2)}, u32[]{:S(2)}) collective-permute-start(bf16[1,18,16640]{2,1,0:T(8,128)(2,1)} %get-tuple-element.14), channel_id=1, source_target_pairs={{0,1},{1,2},{2,3},{4,5},{5,6},{6,7},{8,9},{9,10},{10,11},{12,13},{... | collective-permute-start | bytes 1797128 | tf_op jit(solution)/shard_map/ppermute | solution.py:126
  37.3 1.5 collective-permute-start.4
  39.4 9.6 %shard_map.94.refs_2_ = f32[2,16,16384]{2,1,0:T(8,128)} custom-call(bf16[2,18,16640]{2,1,0:T(8,128)(2,1)} %copy-done.2, f32[27,8,128]{2,1,0:T(8,128)} %broadcast_in_dim.18.refs_1_.refs_3_), custom_call_target="tpu_custom_call" | custom-call | tf_op jit(solution)/shard_map/pallas_call | solution.py:179
  49.8 1.9 %fusion.30 = f32[256,32,64]{0,2,1:T(8,128)} fusion(bf16[32,32,64]{2,1,0:T(8,128)(2,1)S(1)} %get-tuple-element.24, f32[32]{0:T(128)S(1)} %get-tuple-element.29, s32[32]{0:T(128)S(1)} %add.132, s32[256]{0:T(256)S(1)} %iota_add_fusion.1), kind=kOutput, calls=%fused_computation.64 | convolution fusion | flops 33710080 | bytes 2229504 | tf_op jit(solution)/shard_map/krc,xk->rxc/dot_general | solution.py:218
  51.7 1.3 collective-permute-done.3.refs_0_
  53.0 4.2 %collective-permute-done.4.refs_1_ = bf16[1,18,16640]{2,1,0:T(8,128)(2,1)} collective-permute-done((bf16[1,18,16640]{2,1,0:T(8,128)(2,1)}, bf16[1,18,16640]{2,1,0:T(8,128)(2,1)}, u32[]{:S(2)}, u32[]{:S(2)}) %collective-permute-start.4) | collective-permute-done | bytes 599072 | tf_op jit(solution)/shard_map/ppermute | solution.py:127
  57.2 6.7 %shard_map.95 = bf16[2,16,16384]{2,1,0:T(8,128)(2,1)} custom-call(bf16[1,18,16640]{2,1,0:T(8,128)(2,1)} %copy-done.11, bf16[1,18,16640]{2,1,0:T(8,128)(2,1)} %collective-permute-done.4.refs_1_, f32[2,16,16384]{2,1,0:T(8,128)} %shard_map.94.refs_2_, f32[27,8,128]{2,1,0:T(8,128)} %broadcast_in_dim.18.refs_1_.refs_3_), custom_call_target="tpu_custom_call" | custom-call | tf_op jit(solution)/shard_map/pallas_call | solution.py:179
  63.9 3.0 %reshape.89 = bf16[8192,64]{1,0:T(8,128)(2,1)S(1)} reshape(bf16[2,16,16384]{2,1,0:T(8,128)(2,1)} %shard_map.95) | data formatting | bytes 2097152 | tf_op jit(solution)/shard_map/reshape | solution.py:266
  67.0 1.2 fusion.109
  68.3 2.8 %fusion.6 = f32[8192,64]{0,1:T(8,128)S(1)} fusion(bf16[256,64]{0,1:T(8,128)(2,1)S(1)} %copy-done.15, f32[8192,256]{1,0:T(8,128)S(1)} %fusion.109), kind=kOutput, calls=%fused_computation.10 | convolution fusion | flops 278921216 | bytes 10518528 | tf_op jit(solution)/shard_map/dot_general | solution.py:269
  71.1 1.2 copy-done.4
  72.7 2.7 %fusion.15 = (bf16[32,256,64]{1,2,0:T(8,128)(2,1)S(1)}, bf16[32,256,64]{1,2,0:T(8,128)(2,1)}) fusion(bf16[32,256,64]{1,2,0:T(8,128)(2,1)S(1)} %copy-done.7, f32[256,32,64]{0,2,1:T(8,128)S(1)} %copy-done.5, bf16[32,32,64]{2,1,0:T(8,128)(2,1)S(1)} %copy-done.13, f32[32]{0:T(128)S(1)} %get-tuple-element.29, s32[32]{0:T(128)S(1)} %add.132, ...), kind=kOutput, calls=%fused_computation.18 | convolution fusion | flops 41566208 | bytes 7472384 | tf_op jit(solution)/shard_map/krc,xk->rxc/dot_general | solution.py:215
  76.8 1.6 %collective-permute-start.9 = (f32[16,32,128]{2,0,1:T(8,128)S(1)}, f32[16,32,128]{2,0,1:T(8,128)S(1)}, u32[]{:S(2)}, u32[]{:S(2)}) collective-permute-start(f32[16,32,128]{2,0,1:T(8,128)S(1)} %fusion.16), channel_id=1, source_target_pairs={{0,16},{8,24},{16,0},{24,8},{1,17},{9,25},{17,1},{25,9},{2,18},{10... | collective-permute-start | bytes 786440 | tf_op jit(solution)/shard_map/ppermute | solution.py:90
  78.5 1.0 copy.42
  79.6 3.7 %collective-permute-done.9 = f32[16,32,128]{2,0,1:T(8,128)S(1)} collective-permute-done((f32[16,32,128]{2,0,1:T(8,128)S(1)}, f32[16,32,128]{2,0,1:T(8,128)S(1)}, u32[]{:S(2)}, u32[]{:S(2)}) %collective-permute-start.9) | collective-permute-done | bytes 262176 | tf_op jit(solution)/shard_map/ppermute | solution.py:90
  84.7 7.9 %convolution_convert_fusion = bf16[8192,64]{0,1:T(8,128)(2,1)} fusion(bf16[64,256]{1,0:T(8,128)(2,1)S(1)} %copy-done, f32[8192,256]{1,0:T(8,128)} %copy-done.4, bf16[8192,64]{0,1:T(8,128)(2,1)} %bitcast.54, bf16[256,64]{0,1:T(8,128)(2,1)} %param.10), kind=kOutput, calls=%fused_computation.1 | convolution fusion | flops 558366720 | bytes 10551296 | tf_op jit(solution)/shard_map/dot_general | solution.py:286
  92.6 1.1 copy.29
  93.7 2.5 %reshape.92 = bf16[2,16,16384]{2,1,0:T(8,128)(2,1)} reshape(bf16[32,256,64]{2,1,0:T(8,128)(2,1)S(1)} %copy.29) | data formatting | bytes 2097152 | tf_op jit(solution)/shard_map/reshape | solution.py:275
  96.1 2.0 %copy.35 = bf16[8192,64]{1,0:T(8,128)(2,1)S(1)} copy(bf16[8192,64]{0,1:T(8,128)(2,1)} %convolution_convert_fusion) | data formatting | bytes 2097152 | tf_op jit(solution)/shard_map/convert_element_type | solution.py:286
  98.2 1.7 %reshape.95 = bf16[2,16,16384]{2,1,0:T(8,128)(2,1)S(1)} reshape(bf16[8192,64]{1,0:T(8,128)(2,1)S(1)} %copy.35) | data formatting | bytes 2097152 | tf_op jit(solution)/shard_map/reshape | solution.py:289
  99.9 1.0 add_convert_fusion.3
  101.7 1.5 collective-permute-start.11
  103.2 1.6 collective-permute-start.16
  104.8 1.4 collective-permute-start.12
  106.6 1.8 %collective-permute-done.12 = bf16[2,16,128]{2,1,0:T(8,128)(2,1)S(1)} collective-permute-done((bf16[2,16,128]{2,1,0:T(8,128)(2,1)S(1)}, bf16[2,16,128]{2,1,0:T(8,128)(2,1)S(1)}, u32[]{:S(2)}, u32[]{:S(2)}) %collective-permute-start.12) | collective-permute-done | bytes 8224 | tf_op jit(solution)/shard_map/ppermute | solution.py:27
  110.9 1.5 fusion.103
  112.4 3.4 %collective-permute-start.14 = (bf16[1,18,16640]{2,1,0:T(8,128)(2,1)}, bf16[1,18,16640]{2,1,0:T(8,128)(2,1)S(1)}, u32[]{:S(2)}, u32[]{:S(2)}) collective-permute-start(bf16[1,18,16640]{2,1,0:T(8,128)(2,1)} %get-tuple-element.12), channel_id=1, source_target_pairs={{0,1},{1,2},{2,3},{4,5},{5,6},{6,7},{8,9},{9,10},{10,11},{12,13},{... | collective-permute-start | bytes 1797128 | tf_op jit(solution)/shard_map/ppermute | solution.py:126
  115.8 1.3 collective-permute-start.15
  117.8 9.6 %shard_map.96.refs_2_ = f32[2,16,16384]{2,1,0:T(8,128)} custom-call(bf16[2,18,16640]{2,1,0:T(8,128)(2,1)} %copy-done.3, f32[27,8,128]{2,1,0:T(8,128)} %broadcast_in_dim.36.refs_1_.refs_3_), custom_call_target="tpu_custom_call" | custom-call | tf_op jit(solution)/shard_map/pallas_call | solution.py:179
  127.4 2.7 %collective-permute-start.19 = (bf16[64,1024]{1,0:T(8,128)(2,1)S(1)}, bf16[64,1024]{1,0:T(8,128)(2,1)S(1)}, u32[]{:S(2)}, u32[]{:S(2)}) collective-permute-start(bf16[64,1024]{1,0:T(8,128)(2,1)S(1)} %add_convert_fusion.2), channel_id=1, source_target_pairs={{0,1},{1,0},{2,3},{3,2},{4,5},{5,4},{6,7},{7,6},{8,9},{9,8},{10,11... | collective-permute-start | bytes 393224 | tf_op jit(solution)/shard_map/ppermute | solution.py:107
  130.9 9.4 %collective-permute-done.19 = bf16[64,1024]{1,0:T(8,128)(2,1)S(1)} collective-permute-done((bf16[64,1024]{1,0:T(8,128)(2,1)S(1)}, bf16[64,1024]{1,0:T(8,128)(2,1)S(1)}, u32[]{:S(2)}, u32[]{:S(2)}) %collective-permute-start.19) | collective-permute-done | bytes 131104 | tf_op jit(solution)/shard_map/ppermute | solution.py:107
  140.3 1.3 collective-permute-start.20
  142.3 2.7 %copy.38 = f32[32,256,64]{2,1,0:T(8,128)} copy(f32[32,256,64]{1,2,0:T(8,128)S(1)} %add_bitcast_fusion) | data formatting | bytes 4194304 | tf_op jit(solution)/shard_map/add | solution.py:218
  145.0 2.9 %reshape.96 = f32[2,16,16384]{2,1,0:T(8,128)S(1)} reshape(f32[32,256,64]{2,1,0:T(8,128)} %copy.38) | data formatting | bytes 4194304 | tf_op jit(solution)/shard_map/reshape | solution.py:301
  149.8 7.1 %shard_map.97 = f32[2,16,16384]{2,1,0:T(8,128)} custom-call(bf16[1,18,16640]{2,1,0:T(8,128)(2,1)} %copy-done.10, bf16[1,18,16640]{2,1,0:T(8,128)(2,1)} %collective-permute-done.15.refs_1_, f32[2,16,16384]{2,1,0:T(8,128)} %shard_map.96.refs_2_, f32[27,8,128]{2,1,0:T(8,128)} %broadcast_in_dim.36.refs_1_.refs_3_), custom_call_target="tpu_custom_call" | custom-call | tf_op jit(solution)/shard_map/pallas_call | solution.py:179
  156.9 2.7 %add_convert_fusion = bf16[2,16,16384]{2,1,0:T(8,128)(2,1)} fusion(f32[2,16,16384]{2,1,0:T(8,128)} %shard_map.97, f32[2,16,16384]{2,1,0:T(8,128)S(1)} %reshape.96), kind=kLoop, calls=%fused_computation.20 | loop fusion | flops 1048576 | bytes 5242880 | tf_op jit(solution)/shard_map/convert_element_type | solution.py:301
  (109 shorter events, 18.4 us)
Async XLA Ops:
  0.6 66.3 %copy-start = (bf16[64,256]{1,0:T(8,128)(2,1)S(1)}, bf16[64,256]{1,0:T(8,128)(2,1)}, u32[]{:S(2)}) copy-start(bf16[64,256]{1,0:T(8,128)(2,1)} %param.9) | copy-start | bytes 98308
  4.8 8.8 %copy-start.6 = (bf16[32,64,64]{2,1,0:T(8,128)(2,1)S(1)}, bf16[32,64,64]{2,1,0:T(8,128)(2,1)}, u32[]{:S(2)}) copy-start(bf16[32,64,64]{2,1,0:T(8,128)(2,1)} %param.12) | copy-start | bytes 786436
  4.8 8.8 %copy-start.12 = (bf16[32,64,64]{2,1,0:T(8,128)(2,1)S(1)}, bf16[32,64,64]{2,1,0:T(8,128)(2,1)}, u32[]{:S(2)}) copy-start(bf16[32,64,64]{2,1,0:T(8,128)(2,1)} %param.11) | copy-start | bytes 786436
  5.7 14.5 %collective-permute-start.5 = (f32[16,32,128]{2,0,1:T(8,128)}, f32[16,32,128]{2,0,1:T(8,128)}, u32[]{:S(2)}, u32[]{:S(2)}) collective-permute-start(f32[16,32,128]{2,0,1:T(8,128)} %fusion.19), channel_id=1, source_target_pairs={{0,16},{8,24},{16,0},{24,8},{1,17},{9,25},{17,1},{25,9},{2,18},{10... | collective-permute-start | bytes 786440 | tf_op jit(solution)/shard_map/ppermute | solution.py:90
  9.4 9.2 %collective-permute-start = (bf16[2,16,128]{2,1,0:T(8,128)(2,1)S(1)}, bf16[2,16,128]{2,1,0:T(8,128)(2,1)S(1)}, u32[]{:S(2)}, u32[]{:S(2)}) collective-permute-start(bf16[2,16,128]{2,1,0:T(8,128)(2,1)S(1)} %get-tuple-element.18), channel_id=1, source_target_pairs={{0,8},{8,16},{16,24},{24,0},{1,9},{9,17},{17,25},{25,1},{2,10},{10... | collective-permute-start | bytes 24584 | tf_op jit(solution)/shard_map/ppermute | solution.py:26
  10.9 9.1 %collective-permute-start.1 = (bf16[2,16,128]{2,1,0:T(8,128)(2,1)S(1)}, bf16[2,16,128]{2,1,0:T(8,128)(2,1)S(1)}, u32[]{:S(2)}, u32[]{:S(2)}) collective-permute-start(bf16[2,16,128]{2,1,0:T(8,128)(2,1)S(1)} %get-tuple-element.17), channel_id=1, source_target_pairs={{8,0},{16,8},{24,16},{0,24},{9,1},{17,9},{25,17},{1,25},{10,2},{18... | collective-permute-start | bytes 24584 | tf_op jit(solution)/shard_map/ppermute | solution.py:27
  16.9 1.6 %copy-start.14 = (bf16[27,64]{1,0:T(8,128)(2,1)S(1)}, bf16[27,64]{1,0:T(8,128)(2,1)}, u32[]{:S(2)}) copy-start(bf16[27,64]{1,0:T(8,128)(2,1)} %param.8) | copy-start | bytes 10372
  20.1 1.9 %collective-permute-start.2 = (bf16[2,1,16640]{2,1,0:T(2,128)(2,1)S(1)}, bf16[2,1,16640]{2,1,0:T(2,128)(2,1)S(1)}, u32[]{:S(2)}, u32[]{:S(2)}) collective-permute-start(bf16[2,1,16640]{2,1,0:T(2,128)(2,1)S(1)} %broadcast_select_fusion.5), channel_id=1, source_target_pairs={{0,4},{4,0},{1,5},{5,1},{2,6},{6,2},{3,7},{7,3},{8,12},{12,8},{9,1... | collective-permute-start | bytes 199688 | tf_op jit(solution)/shard_map/ppermute | solution.py:19
  21.4 6.0 %collective-permute-start.6 = (f32[8,32,128]{2,0,1:T(8,128)S(1)}, f32[8,32,128]{2,0,1:T(8,128)S(1)}, u32[]{:S(2)}, u32[]{:S(2)}) collective-permute-start(f32[8,32,128]{2,0,1:T(8,128)S(1)} %constant_dynamic-slice_fusion.1), channel_id=1, source_target_pairs={{0,8},{8,0},{16,24},{24,16},{1,9},{9,1},{17,25},{25,17},{2,10},{10... | collective-permute-start | bytes 393224 | tf_op jit(solution)/shard_map/ppermute | solution.py:90
  27.5 4.3 %collective-permute-start.7 = (bf16[8,32,128]{2,1,0:T(8,128)(2,1)S(1)}, bf16[8,32,128]{2,1,0:T(8,128)(2,1)S(1)}, u32[]{:S(2)}, u32[]{:S(2)}) collective-permute-start(bf16[8,32,128]{2,1,0:T(8,128)(2,1)S(1)} %convolution_convert_fusion.2), channel_id=1, source_target_pairs={{0,8},{8,0},{16,24},{24,16},{1,9},{9,1},{17,25},{25,17},{2,10},{10... | collective-permute-start | bytes 196616 | tf_op jit(solution)/shard_map/ppermute | solution.py:68
  28.8 10.6 %copy-start.2 = (bf16[2,18,16640]{2,1,0:T(8,128)(2,1)}, bf16[2,18,16640]{2,1,0:T(8,128)(2,1)S(1)}, u32[]{:S(2)}) copy-start(bf16[2,18,16640]{2,1,0:T(8,128)(2,1)S(1)} %pad_maximum_fusion.refs_0_) | copy-start | bytes 3594244
  31.9 17.1 %collective-permute-start.8 = (bf16[16,32,128]{2,1,0:T(8,128)(2,1)S(1)}, bf16[16,32,128]{2,1,0:T(8,128)(2,1)S(1)}, u32[]{:S(2)}, u32[]{:S(2)}) collective-permute-start(bf16[16,32,128]{2,1,0:T(8,128)(2,1)S(1)} %pad_maximum_fusion.4), channel_id=1, source_target_pairs={{0,16},{8,24},{16,0},{24,8},{1,17},{9,25},{17,1},{25,9},{2,18},{10... | collective-permute-start | bytes 393224 | tf_op jit(solution)/shard_map/ppermute | solution.py:68
  33.3 19.8 %collective-permute-start.3 = (bf16[1,18,16640]{2,1,0:T(8,128)(2,1)}, bf16[1,18,16640]{2,1,0:T(8,128)(2,1)S(1)}, u32[]{:S(2)}, u32[]{:S(2)}) collective-permute-start(bf16[1,18,16640]{2,1,0:T(8,128)(2,1)} %get-tuple-element.14), channel_id=1, source_target_pairs={{0,1},{1,2},{2,3},{4,5},{5,6},{6,7},{8,9},{9,10},{10,11},{12,13},{... | collective-permute-start | bytes 1797128 | tf_op jit(solution)/shard_map/ppermute | solution.py:126
  37.3 19.9 %collective-permute-start.4 = (bf16[1,18,16640]{2,1,0:T(8,128)(2,1)}, bf16[1,18,16640]{2,1,0:T(8,128)(2,1)}, u32[]{:S(2)}, u32[]{:S(2)}) collective-permute-start(bf16[1,18,16640]{2,1,0:T(8,128)(2,1)} %get-tuple-element.13), channel_id=1, source_target_pairs={{1,0},{2,1},{3,2},{5,4},{6,5},{7,6},{9,8},{10,9},{11,10},{13,12},{... | collective-permute-start | bytes 1797128 | tf_op jit(solution)/shard_map/ppermute | solution.py:127
  53.0 4.2 %copy-start.11 = (bf16[1,18,16640]{2,1,0:T(8,128)(2,1)}, bf16[1,18,16640]{2,1,0:T(8,128)(2,1)S(1)}, u32[]{:S(2)}) copy-start(bf16[1,18,16640]{2,1,0:T(8,128)(2,1)S(1)} %collective-permute-done.3.refs_0_) | copy-start | bytes 1797124
  67.0 1.2 copy-start.15
  68.2 4.0 %copy-start.4 = (f32[8192,256]{1,0:T(8,128)}, f32[8192,256]{1,0:T(8,128)S(1)}, u32[]{:S(2)}) copy-start(f32[8192,256]{1,0:T(8,128)S(1)} %fusion.109) | copy-start | bytes 25165828
  68.2 4.0 %copy-start.5 = (f32[256,32,64]{0,2,1:T(8,128)S(1)}, f32[256,32,64]{0,2,1:T(8,128)}, u32[]{:S(2)}) copy-start(f32[256,32,64]{0,2,1:T(8,128)} %fusion.30) | copy-start | bytes 6291460
  68.2 4.2 %copy-start.7 = (bf16[32,256,64]{1,2,0:T(8,128)(2,1)S(1)}, bf16[32,256,64]{1,2,0:T(8,128)(2,1)}, u32[]{:S(2)}) copy-start(bf16[32,256,64]{1,2,0:T(8,128)(2,1)} %copy.30) | copy-start | bytes 3145732
  68.3 4.4 %copy-start.13 = (bf16[32,32,64]{2,1,0:T(8,128)(2,1)S(1)}, bf16[32,32,64]{2,1,0:T(8,128)(2,1)}, u32[]{:S(2)}) copy-start(bf16[32,32,64]{2,1,0:T(8,128)(2,1)} %get-tuple-element.23) | copy-start | bytes 393220
  76.8 6.4 %collective-permute-start.9 = (f32[16,32,128]{2,0,1:T(8,128)S(1)}, f32[16,32,128]{2,0,1:T(8,128)S(1)}, u32[]{:S(2)}, u32[]{:S(2)}) collective-permute-start(f32[16,32,128]{2,0,1:T(8,128)S(1)} %fusion.16), channel_id=1, source_target_pairs={{0,16},{8,24},{16,0},{24,8},{1,17},{9,25},{17,1},{25,9},{2,18},{10... | collective-permute-start | bytes 786440 | tf_op jit(solution)/shard_map/ppermute | solution.py:90
  83.4 1.3 copy-start.9
  84.1 15.8 %collective-permute-start.10 = (f32[8,32,128]{2,0,1:T(8,128)}, f32[8,32,128]{2,0,1:T(8,128)}, u32[]{:S(2)}, u32[]{:S(2)}) collective-permute-start(f32[8,32,128]{2,0,1:T(8,128)} %constant_dynamic-slice_fusion), channel_id=1, source_target_pairs={{0,8},{8,0},{16,24},{24,16},{1,9},{9,1},{17,25},{25,17},{2,10},{10... | collective-permute-start | bytes 393224 | tf_op jit(solution)/shard_map/ppermute | solution.py:90
  84.7 7.9 %copy-start.8 = (bf16[32,256,64]{1,2,0:T(8,128)(2,1)S(1)}, bf16[32,256,64]{1,2,0:T(8,128)(2,1)}, u32[]{:S(2)}) copy-start(bf16[32,256,64]{1,2,0:T(8,128)(2,1)} %get-tuple-element.10) | copy-start | bytes 3145732
  101.7 4.8 %collective-permute-start.11 = (bf16[2,16,128]{2,1,0:T(8,128)(2,1)S(1)}, bf16[2,16,128]{2,1,0:T(8,128)(2,1)S(1)}, u32[]{:S(2)}, u32[]{:S(2)}) collective-permute-start(bf16[2,16,128]{2,1,0:T(8,128)(2,1)S(1)} %get-tuple-element.16), channel_id=1, source_target_pairs={{0,8},{8,16},{16,24},{24,0},{1,9},{9,17},{17,25},{25,1},{2,10},{10... | collective-permute-start | bytes 24584 | tf_op jit(solution)/shard_map/ppermute | solution.py:26
  103.2 5.5 %collective-permute-start.16 = (bf16[8,32,128]{2,1,0:T(8,128)(2,1)S(1)}, bf16[8,32,128]{2,1,0:T(8,128)(2,1)S(1)}, u32[]{:S(2)}, u32[]{:S(2)}) collective-permute-start(bf16[8,32,128]{2,1,0:T(8,128)(2,1)S(1)} %convolution_convert_fusion.1), channel_id=1, source_target_pairs={{0,8},{8,0},{16,24},{24,16},{1,9},{9,1},{17,25},{25,17},{2,10},{10... | collective-permute-start | bytes 196616 | tf_op jit(solution)/shard_map/ppermute | solution.py:68
  104.8 3.7 %collective-permute-start.12 = (bf16[2,16,128]{2,1,0:T(8,128)(2,1)S(1)}, bf16[2,16,128]{2,1,0:T(8,128)(2,1)S(1)}, u32[]{:S(2)}, u32[]{:S(2)}) collective-permute-start(bf16[2,16,128]{2,1,0:T(8,128)(2,1)S(1)} %get-tuple-element.15), channel_id=1, source_target_pairs={{8,0},{16,8},{24,16},{0,24},{9,1},{17,9},{25,17},{1,25},{10,2},{18... | collective-permute-start | bytes 24584 | tf_op jit(solution)/shard_map/ppermute | solution.py:27
  106.4 21.0 %collective-permute-start.18 = (bf16[64,1024]{1,0:T(8,128)(2,1)S(1)}, bf16[64,1024]{1,0:T(8,128)(2,1)S(1)}, u32[]{:S(2)}, u32[]{:S(2)}) collective-permute-start(bf16[64,1024]{1,0:T(8,128)(2,1)S(1)} %convert_element_type.139), channel_id=1, source_target_pairs={{0,4},{4,0},{1,5},{5,1},{2,6},{6,2},{3,7},{7,3},{8,12},{12,8},{9,1... | collective-permute-start | bytes 393224 | tf_op jit(solution)/shard_map/ppermute | solution.py:107
  108.6 1.4 collective-permute-start.13
  108.7 21.4 %collective-permute-start.17 = (bf16[16,32,128]{2,1,0:T(8,128)(2,1)S(1)}, bf16[16,32,128]{2,1,0:T(8,128)(2,1)S(1)}, u32[]{:S(2)}, u32[]{:S(2)}) collective-permute-start(bf16[16,32,128]{2,1,0:T(8,128)(2,1)S(1)} %pad_maximum_fusion.5), channel_id=1, source_target_pairs={{0,16},{8,24},{16,0},{24,8},{1,17},{9,25},{17,1},{25,9},{2,18},{10... | collective-permute-start | bytes 393224 | tf_op jit(solution)/shard_map/ppermute | solution.py:68
  110.9 6.9 %copy-start.3 = (bf16[2,18,16640]{2,1,0:T(8,128)(2,1)}, bf16[2,18,16640]{2,1,0:T(8,128)(2,1)S(1)}, u32[]{:S(2)}) copy-start(bf16[2,18,16640]{2,1,0:T(8,128)(2,1)S(1)} %pad_maximum_fusion.1.refs_0_) | copy-start | bytes 3594244
  112.4 36.6 %collective-permute-start.14 = (bf16[1,18,16640]{2,1,0:T(8,128)(2,1)}, bf16[1,18,16640]{2,1,0:T(8,128)(2,1)S(1)}, u32[]{:S(2)}, u32[]{:S(2)}) collective-permute-start(bf16[1,18,16640]{2,1,0:T(8,128)(2,1)} %get-tuple-element.12), channel_id=1, source_target_pairs={{0,1},{1,2},{2,3},{4,5},{5,6},{6,7},{8,9},{9,10},{10,11},{12,13},{... | collective-permute-start | bytes 1797128 | tf_op jit(solution)/shard_map/ppermute | solution.py:126
  115.8 33.1 %collective-permute-start.15 = (bf16[1,18,16640]{2,1,0:T(8,128)(2,1)}, bf16[1,18,16640]{2,1,0:T(8,128)(2,1)}, u32[]{:S(2)}, u32[]{:S(2)}) collective-permute-start(bf16[1,18,16640]{2,1,0:T(8,128)(2,1)} %get-tuple-element.11), channel_id=1, source_target_pairs={{1,0},{2,1},{3,2},{5,4},{6,5},{7,6},{9,8},{10,9},{11,10},{13,12},{... | collective-permute-start | bytes 1797128 | tf_op jit(solution)/shard_map/ppermute | solution.py:127
  127.4 12.9 %collective-permute-start.19 = (bf16[64,1024]{1,0:T(8,128)(2,1)S(1)}, bf16[64,1024]{1,0:T(8,128)(2,1)S(1)}, u32[]{:S(2)}, u32[]{:S(2)}) collective-permute-start(bf16[64,1024]{1,0:T(8,128)(2,1)S(1)} %add_convert_fusion.2), channel_id=1, source_target_pairs={{0,1},{1,0},{2,3},{3,2},{4,5},{5,4},{6,7},{7,6},{8,9},{9,8},{10,11... | collective-permute-start | bytes 393224 | tf_op jit(solution)/shard_map/ppermute | solution.py:107
  140.3 7.6 %collective-permute-start.20 = (bf16[64,1024]{1,0:T(8,128)(2,1)S(1)}, bf16[64,1024]{1,0:T(8,128)(2,1)S(1)}, u32[]{:S(2)}, u32[]{:S(2)}) collective-permute-start(bf16[64,1024]{1,0:T(8,128)(2,1)S(1)} %add_convert_fusion.1), channel_id=1, source_target_pairs={{0,2},{1,3},{2,0},{3,1},{4,6},{5,7},{6,4},{7,5},{8,10},{9,11},{10,... | collective-permute-start | bytes 393224 | tf_op jit(solution)/shard_map/ppermute | solution.py:107
  149.0 0.9 copy-start.10
  149.8 9.8 %copy-start.1 = (bf16[64,256]{1,0:T(8,128)(2,1)S(1)}, bf16[64,256]{1,0:T(8,128)(2,1)}, u32[]{:S(2)}) copy-start(bf16[64,256]{1,0:T(8,128)(2,1)} %param.9) | copy-start | bytes 98308

commit v20 on v15

--- a/solution.py
+++ b/solution.py
@@ -130,7 +130,7 @@
 
 def stencil_kernel(chunk, x_pad, y_cells, rows, plan, sources, has_acc, *refs):
     src_refs = refs[:sources]
-    acc_ref = refs[sources] if has_acc else None
+    acc_refs = refs[sources : sources + has_acc]
     w_ref, o_ref = refs[sources + has_acc :]
     width = chunk + 2 * x_pad
     count = o_ref.shape[2] // chunk
@@ -161,7 +161,7 @@
                     + pltpu.roll(left, shift, 1)[:, :chunk]
                     + pltpu.roll(right, shift, 1)[:, :chunk]
                 )
-                if has_acc:
+                for acc_ref in acc_refs:
                     total = total + acc_ref[plane, pl.ds(row, rows), pl.ds(base, chunk)]
                 o_ref[plane, pl.ds(row, rows), pl.ds(base, chunk)] = total.astype(o_ref.dtype)
         return carry
@@ -169,20 +169,20 @@
     lax.fori_loop(0, count, body, 0)
 
 
-def stencil_call(plan, inputs, acc, gains, y_cells, lanes, channels, out_dtype):
+def stencil_call(plan, inputs, accs, gains, y_cells, lanes, channels, out_dtype):
     chunk = min(1024, lanes)
     rows = 8 if y_cells % 8 == 0 else y_cells
     kernel = functools.partial(
-        stencil_kernel, chunk, 2 * channels, y_cells, rows, plan, len(inputs), acc is not None
-    )
-    operands = list(inputs) + ([acc] if acc is not None else []) + [gains]
+        stencil_kernel, chunk, 2 * channels, y_cells, rows, plan, len(inputs), len(accs)
+    )
+    operands = list(inputs) + list(accs) + [gains]
     return pl.pallas_call(
         kernel,
         out_shape=jax.ShapeDtypeStruct((len(plan), y_cells, lanes), out_dtype),
     )(*operands)
 
 
-def depthwise(rims, taps, flipped, x_cells, channels, out_dtype=jnp.float32):
+def depthwise(rims, taps, flipped, x_cells, channels, out_dtype=jnp.float32, extra=()):
     inner, below, above = rims
     planes = inner.shape[0]
     y_cells = inner.shape[1] - 2
@@ -196,12 +196,13 @@
         tuple((0, plane + step_z - 1, step_z) for step_z in range(3) if 0 <= plane + step_z - 1 < planes)
         for plane in range(planes)
     )
-    local = stencil_call(local_plan, (inner,), None, gains, y_cells, lanes, channels, jnp.float32)
+    local = stencil_call(local_plan, (inner,), (), gains, y_cells, lanes, channels, jnp.float32)
     rim_plan = tuple(
         ((((0, 0, 0),) if plane == 0 else ()) + (((1, 0, 2),) if plane == planes - 1 else ()))
         for plane in range(planes)
     )
-    return stencil_call(rim_plan, (below, above), local, gains, y_cells, lanes, channels, out_dtype)
+    accs = (local,) + tuple(extra)
+    return stencil_call(rim_plan, (below, above), accs, gains, y_cells, lanes, channels, out_dtype)
 
 
 def share_terms(field3, cos_table, sin_table):
@@ -298,9 +299,14 @@
     spectral_grad = share_inverse(dmode, cos_order, sin_order, channels)
     grad_spec = sum_gradients(local_grads)
     padded_grad = spatial_rims(grad_act, channels)
-    grad_local = depthwise(padded_grad, depth_weight, True, x_cells, channels)
-    grad_features = (grad_local + spectral_grad.reshape(planes, y_cells, merged)).astype(
-        jnp.bfloat16
+    grad_features = depthwise(
+        padded_grad,
+        depth_weight,
+        True,
+        x_cells,
+        channels,
+        jnp.bfloat16,
+        (spectral_grad.reshape(planes, y_cells, merged),),
     )
     return (output, grad_features, grad_spec)
 

time: 155 us -> 153 us (0.987)
  other arithmetic: 10 us -> 7.28 us
    convert_element_type x1 -> x0, other arithmetic: 2.74 us -> none  [per_device(): (grad_local + spectral_grad.reshape(planes, y_cells, merged)).astype(jnp....]
  transfers between devices with their start and end apart: 21 -> 21, of which waited for: 9 -> 9; matrix products, arithmetic and copies ran while one was open for 31% -> 31% of each run, Pallas kernels for 12% -> 13%
where the time goes in v20:
time: 153 us
  starting transfers between devices  35.6 us (23%)
  local copies, waits for them, and re-layouts  33.9 us (22%)
  Pallas kernels  33.3 us (22%)
  waiting for transfers between devices  21.9 us (14%)
  matrix products  19.6 us (13%)
  other arithmetic  7.28 us (5%)
    pallas_call x4, Pallas kernels, stencil_call(): pl.pallas_call(kernel, out_shape=jax.ShapeDtypeStruct((len(plan), y_cells...  33.3 us
    ppermute x3, waiting for transfers between devices, butterfly_sum(): lax.ppermute(value, axis, [(i, i ^ step) for i in range(size)])  9.39 us
    ppermute x2, starting transfers between devices, spatial_rims(): below = lax.ppermute(inner[-1:], 'gz', up)  8.98 us
    dot_general x1, matrix products, per_device(): jnp.dot(grad_hidden, expand_weight.T, preferred_element_type=jnp.float32)  7.9 us
    ppermute x4, starting transfers between devices, ring_reduce_scatter(): lax.ppermute(send, axis, [(i, i ^ step) for i in range(size)])  6.64 us
    ppermute x3, starting transfers between devices, butterfly_sum(): lax.ppermute(value, axis, [(i, i ^ step) for i in range(size)])  5.7 us
    ppermute x4, starting transfers between devices, ring_gather(): lax.ppermute(block, axis, [(i, i ^ step) for i in range(size)])  5.36 us
    reshape x1, local copies, waits for them, and re-layouts, per_device(): spectral_grad.reshape(planes, y_cells, merged)  3.92 us
  transfers between devices with their start and end apart: 21, of which 9 were waited for; matrix products, arithmetic and copies ran while one was open for 31% of the time, Pallas kernels for 13%

profile of v20, /device:TPU:0, one launch (start us, length us, event | category | flops | bytes accessed | tf_op | source)
XLA Modules:
  0.0 152.8 jit_solution(8362435461620460791)
XLA Ops:
  0.7 3.0 %reshape.89 = bf16[32,256,64]{2,1,0:T(8,128)(2,1)S(1)} reshape(bf16[2,16,16384]{2,1,0:T(8,128)(2,1)} %param.7) | data formatting | bytes 2097152 | tf_op jit(solution)/shard_map/reshape | solution.py:259
  5.0 3.0 %collective-permute-start = (f32[16,32,128]{2,0,1:T(8,128)S(1)}, f32[16,32,128]{2,0,1:T(8,128)}, u32[]{:S(2)}, u32[]{:S(2)}) collective-permute-start(f32[16,32,128]{2,0,1:T(8,128)S(1)} %fusion.15), channel_id=1, source_target_pairs={{0,16},{8,24},{16,0},{24,8},{1,17},{9,25},{17,1},{25,9},{2,18},{10... | collective-permute-start | bytes 786440 | tf_op jit(solution)/shard_map/ppermute | solution.py:90
  8.7 1.5 collective-permute-start.2
  10.2 1.4 collective-permute-start.3
  11.7 1.7 %collective-permute-done.2 = bf16[2,16,128]{2,1,0:T(8,128)(2,1)S(1)} collective-permute-done((bf16[2,16,128]{2,1,0:T(8,128)(2,1)S(1)}, bf16[2,16,128]{2,1,0:T(8,128)(2,1)S(1)}, u32[]{:S(2)}, u32[]{:S(2)}) %collective-permute-start.2) | collective-permute-done | bytes 8224 | tf_op jit(solution)/shard_map/ppermute | solution.py:26
  14.3 1.2 collective-permute-done.4
  16.4 1.3 fusion.100
  17.6 4.4 %collective-permute-start.5 = (bf16[1,18,16640]{2,1,0:T(8,128)(2,1)}, bf16[1,18,16640]{2,1,0:T(8,128)(2,1)}, u32[]{:S(2)}, u32[]{:S(2)}) collective-permute-start(bf16[1,18,16640]{2,1,0:T(8,128)(2,1)} %get-tuple-element.18), channel_id=1, source_target_pairs={{0,1},{1,2},{2,3},{4,5},{5,6},{6,7},{8,9},{9,10},{10,11},{12,13},{... | collective-permute-start | bytes 1797128 | tf_op jit(solution)/shard_map/ppermute | solution.py:126
  22.0 1.3 collective-permute-start.6
  23.3 1.1 fusion.17
  25.2 1.5 collective-permute-start.1
  26.7 2.5 %reshape.93 = bf16[32,256,64]{2,1,0:T(8,128)(2,1)S(1)} reshape(bf16[2,16,16384]{2,1,0:T(8,128)(2,1)S(1)} %copy-done.7) | data formatting | bytes 2097152 | tf_op jit(solution)/shard_map/reshape | solution.py:279
  29.2 1.6 %copy.30 = bf16[32,256,64]{1,2,0:T(8,128)(2,1)} copy(bf16[32,256,64]{2,1,0:T(8,128)(2,1)S(1)} %reshape.93) | data formatting | bytes 2097152 | tf_op jit(solution)/shard_map/optimization_barrier | solution.py:279
  31.1 1.1 fusion.19
  32.9 9.6 %shard_map.94.refs_2_ = f32[2,16,16384]{2,1,0:T(8,128)} custom-call(bf16[2,18,16640]{2,1,0:T(8,128)(2,1)} %copy-done.2, f32[27,8,128]{2,1,0:T(8,128)} %broadcast_in_dim.18.refs_1_.refs_3_), custom_call_target="tpu_custom_call" | custom-call | tf_op jit(solution)/shard_map/pallas_call | solution.py:179
  43.8 6.7 %shard_map.95 = bf16[2,16,16384]{2,1,0:T(8,128)(2,1)} custom-call(bf16[1,18,16640]{2,1,0:T(8,128)(2,1)} %collective-permute-done.5.refs_0_, bf16[1,18,16640]{2,1,0:T(8,128)(2,1)} %collective-permute-done.6.refs_1_, f32[2,16,16384]{2,1,0:T(8,128)} %shard_map.94.refs_2_, f32[27,8,128]{2,1,0:T(8,128)} %broadcast_in_dim.18.refs_1_.refs_3_), custom_call_target="tpu_custom_call" | custom-call | tf_op jit(solution)/shard_map/pallas_call | solution.py:179
  50.6 1.5 collective-permute-start.7
  52.1 3.0 %reshape.90 = bf16[8192,64]{1,0:T(8,128)(2,1)S(1)} reshape(bf16[2,16,16384]{2,1,0:T(8,128)(2,1)} %shard_map.95) | data formatting | bytes 2097152 | tf_op jit(solution)/shard_map/reshape | solution.py:268
  55.1 1.2 fusion.105
  56.4 2.8 %fusion.5 = f32[8192,64]{0,1:T(8,128)S(1)} fusion(bf16[256,64]{0,1:T(8,128)(2,1)S(1)} %copy-done.16, f32[8192,256]{1,0:T(8,128)S(1)} %fusion.105), kind=kOutput, calls=%fused_computation.10 | convolution fusion | flops 278921216 | bytes 10518528 | tf_op jit(solution)/shard_map/dot_general | solution.py:271
  59.7 1.6 %collective-permute-start.8 = (bf16[16,32,128]{2,1,0:T(8,128)(2,1)S(1)}, bf16[16,32,128]{2,1,0:T(8,128)(2,1)S(1)}, u32[]{:S(2)}, u32[]{:S(2)}) collective-permute-start(bf16[16,32,128]{2,1,0:T(8,128)(2,1)S(1)} %pad_maximum_fusion.3), channel_id=1, source_target_pairs={{0,16},{8,24},{16,0},{24,8},{1,17},{9,25},{17,1},{25,9},{2,18},{10... | collective-permute-start | bytes 393224 | tf_op jit(solution)/shard_map/ppermute | solution.py:68
  61.3 3.4 %collective-permute-done.8 = bf16[16,32,128]{2,1,0:T(8,128)(2,1)S(1)} collective-permute-done((bf16[16,32,128]{2,1,0:T(8,128)(2,1)S(1)}, bf16[16,32,128]{2,1,0:T(8,128)(2,1)S(1)}, u32[]{:S(2)}, u32[]{:S(2)}) %collective-permute-start.8) | collective-permute-done | bytes 131104 | tf_op jit(solution)/shard_map/ppermute | solution.py:68
  65.5 2.7 %fusion.11 = (bf16[32,256,64]{1,2,0:T(8,128)(2,1)S(1)}, bf16[32,256,64]{1,2,0:T(8,128)(2,1)}) fusion(bf16[32,256,64]{1,2,0:T(8,128)(2,1)S(1)} %copy-done.8, f32[256,32,64]{0,2,1:T(8,128)S(1)} %fusion.26, bf16[32,32,64]{2,1,0:T(8,128)(2,1)S(1)} %get-tuple-element.27, f32[32]{0:T(128)S(1)} %get-tuple-element.33, s32[32]{0:T(128)S(1)} %add.137, ...), kind=kOutput, calls=%fused_computation.17 | convolution fusion | flops 41566208 | bytes 7472384 | tf_op jit(solution)/shard_map/krc,xk->rxc/dot_general | solution.py:216
  69.7 1.6 %collective-permute-start.9 = (f32[16,32,128]{2,0,1:T(8,128)S(1)}, f32[16,32,128]{2,0,1:T(8,128)S(1)}, u32[]{:S(2)}, u32[]{:S(2)}) collective-permute-start(f32[16,32,128]{2,0,1:T(8,128)S(1)} %fusion.12), channel_id=1, source_target_pairs={{0,16},{8,24},{16,0},{24,8},{1,17},{9,25},{17,1},{25,9},{2,18},{10... | collective-permute-start | bytes 786440 | tf_op jit(solution)/shard_map/ppermute | solution.py:90
  71.4 1.0 copy.42
  72.4 3.7 %collective-permute-done.9 = f32[16,32,128]{2,0,1:T(8,128)S(1)} collective-permute-done((f32[16,32,128]{2,0,1:T(8,128)S(1)}, f32[16,32,128]{2,0,1:T(8,128)S(1)}, u32[]{:S(2)}, u32[]{:S(2)}) %collective-permute-start.9) | collective-permute-done | bytes 262176 | tf_op jit(solution)/shard_map/ppermute | solution.py:90
  77.6 7.9 %convolution_convert_fusion = bf16[8192,64]{0,1:T(8,128)(2,1)} fusion(bf16[64,256]{1,0:T(8,128)(2,1)S(1)} %copy-done, bf16[8192,64]{0,1:T(8,128)(2,1)} %bitcast.54, bf16[256,64]{0,1:T(8,128)(2,1)} %param.10, f32[8192,256]{1,0:T(8,128)} %copy-done.4), kind=kOutput, calls=%fused_computation.3 | convolution fusion | flops 558366720 | bytes 10551296 | tf_op jit(solution)/shard_map/dot_general | solution.py:288
  85.5 1.1 copy.29
  86.5 2.5 %reshape.92 = bf16[2,16,16384]{2,1,0:T(8,128)(2,1)} reshape(bf16[32,256,64]{2,1,0:T(8,128)(2,1)S(1)} %copy.29) | data formatting | bytes 2097152 | tf_op jit(solution)/shard_map/reshape | solution.py:277
  89.0 1.1 copy.35
  90.1 1.9 %reshape.95 = bf16[2,16,16384]{2,1,0:T(8,128)(2,1)S(1)} reshape(bf16[8192,64]{1,0:T(8,128)(2,1)S(1)} %copy.35) | data formatting | bytes 2097152 | tf_op jit(solution)/shard_map/reshape | solution.py:291
  92.0 1.0 add_convert_fusion.2
  93.8 1.5 %collective-permute-start.11 = (bf16[2,16,128]{2,1,0:T(8,128)(2,1)S(1)}, bf16[2,16,128]{2,1,0:T(8,128)(2,1)S(1)}, u32[]{:S(2)}, u32[]{:S(2)}) collective-permute-start(bf16[2,16,128]{2,1,0:T(8,128)(2,1)S(1)} %get-tuple-element.20), channel_id=1, source_target_pairs={{0,8},{8,16},{16,24},{24,0},{1,9},{9,17},{17,25},{25,1},{2,10},{10... | collective-permute-start | bytes 24584 | tf_op jit(solution)/shard_map/ppermute | solution.py:26
  95.4 1.3 collective-permute-start.16
  96.6 1.7 %collective-permute-start.12 = (bf16[2,16,128]{2,1,0:T(8,128)(2,1)S(1)}, bf16[2,16,128]{2,1,0:T(8,128)(2,1)S(1)}, u32[]{:S(2)}, u32[]{:S(2)}) collective-permute-start(bf16[2,16,128]{2,1,0:T(8,128)(2,1)S(1)} %get-tuple-element.19), channel_id=1, source_target_pairs={{8,0},{16,8},{24,16},{0,24},{9,1},{17,9},{25,17},{1,25},{10,2},{18... | collective-permute-start | bytes 24584 | tf_op jit(solution)/shard_map/ppermute | solution.py:27
  98.8 1.5 %collective-permute-done.12 = bf16[2,16,128]{2,1,0:T(8,128)(2,1)S(1)} collective-permute-done((bf16[2,16,128]{2,1,0:T(8,128)(2,1)S(1)}, bf16[2,16,128]{2,1,0:T(8,128)(2,1)S(1)}, u32[]{:S(2)}, u32[]{:S(2)}) %collective-permute-start.12) | collective-permute-done | bytes 8224 | tf_op jit(solution)/shard_map/ppermute | solution.py:27
  100.6 1.0 collective-permute-start.17
  102.8 1.3 fusion.99
  104.1 4.6 %collective-permute-start.14 = (bf16[1,18,16640]{2,1,0:T(8,128)(2,1)}, bf16[1,18,16640]{2,1,0:T(8,128)(2,1)S(1)}, u32[]{:S(2)}, u32[]{:S(2)}) collective-permute-start(bf16[1,18,16640]{2,1,0:T(8,128)(2,1)} %get-tuple-element.16), channel_id=1, source_target_pairs={{0,1},{1,2},{2,3},{4,5},{5,6},{6,7},{8,9},{9,10},{10,11},{12,13},{... | collective-permute-start | bytes 1797128 | tf_op jit(solution)/shard_map/ppermute | solution.py:126
  108.7 1.3 collective-permute-start.15
  110.7 9.6 %shard_map.96.refs_2_ = f32[2,16,16384]{2,1,0:T(8,128)} custom-call(bf16[2,18,16640]{2,1,0:T(8,128)(2,1)} %copy-done.3, f32[27,8,128]{2,1,0:T(8,128)} %broadcast_in_dim.36.refs_1_.refs_4_), custom_call_target="tpu_custom_call" | custom-call | tf_op jit(solution)/shard_map/pallas_call | solution.py:179
  120.3 2.7 %collective-permute-start.19 = (bf16[64,1024]{1,0:T(8,128)(2,1)S(1)}, bf16[64,1024]{1,0:T(8,128)(2,1)S(1)}, u32[]{:S(2)}, u32[]{:S(2)}) collective-permute-start(bf16[64,1024]{1,0:T(8,128)(2,1)S(1)} %add_convert_fusion.1), channel_id=1, source_target_pairs={{0,1},{1,0},{2,3},{3,2},{4,5},{5,4},{6,7},{7,6},{8,9},{9,8},{10,11... | collective-permute-start | bytes 393224 | tf_op jit(solution)/shard_map/ppermute | solution.py:107
  123.8 9.4 %collective-permute-done.19 = bf16[64,1024]{1,0:T(8,128)(2,1)S(1)} collective-permute-done((bf16[64,1024]{1,0:T(8,128)(2,1)S(1)}, bf16[64,1024]{1,0:T(8,128)(2,1)S(1)}, u32[]{:S(2)}, u32[]{:S(2)}) %collective-permute-start.19) | collective-permute-done | bytes 131104 | tf_op jit(solution)/shard_map/ppermute | solution.py:107
  133.3 2.9 %collective-permute-start.20 = (bf16[64,1024]{1,0:T(8,128)(2,1)S(1)}, bf16[64,1024]{1,0:T(8,128)(2,1)S(1)}, u32[]{:S(2)}, u32[]{:S(2)}) collective-permute-start(bf16[64,1024]{1,0:T(8,128)(2,1)S(1)} %add_convert_fusion), channel_id=1, source_target_pairs={{0,2},{1,3},{2,0},{3,1},{4,6},{5,7},{6,4},{7,5},{8,10},{9,11},{10,... | collective-permute-start | bytes 393224 | tf_op jit(solution)/shard_map/ppermute | solution.py:107
  136.8 2.7 %copy.38 = f32[32,256,64]{2,1,0:T(8,128)} copy(f32[32,256,64]{1,2,0:T(8,128)S(1)} %add_bitcast_fusion) | data formatting | bytes 4194304 | tf_op jit(solution)/shard_map/add | solution.py:219
  139.5 3.9 %reshape.96.refs_3_ = f32[2,16,16384]{2,1,0:T(8,128)} reshape(f32[32,256,64]{2,1,0:T(8,128)} %copy.38) | data formatting | bytes 4194304 | tf_op jit(solution)/shard_map/reshape | solution.py:309
  143.5 0.9 reshape.97
  145.4 7.4 %shard_map.97 = bf16[2,16,16384]{2,1,0:T(8,128)(2,1)} custom-call(bf16[1,18,16640]{2,1,0:T(8,128)(2,1)} %copy-done.14, bf16[1,18,16640]{2,1,0:T(8,128)(2,1)} %collective-permute-done.15.refs_1_, f32[2,16,16384]{2,1,0:T(8,128)} %shard_map.96.refs_2_, f32[2,16,16384]{2,1,0:T(8,128)} %reshape.96.refs_3_, f32[27,8,128]{2,1,0:T(8,128)} %broadcast_in_dim.36.refs_1_.refs_4_), custom_call_target="tpu_custom_call" | custom-call | tf_op jit(solution)/shard_map/pallas_call | solution.py:179
  (112 shorter events, 16.7 us)
Async XLA Ops:
  0.6 54.5 %copy-start = (bf16[64,256]{1,0:T(8,128)(2,1)S(1)}, bf16[64,256]{1,0:T(8,128)(2,1)}, u32[]{:S(2)}) copy-start(bf16[64,256]{1,0:T(8,128)(2,1)} %param.9) | copy-start | bytes 98308
  4.8 8.6 %copy-start.5 = (bf16[2,16,16384]{2,1,0:T(8,128)(2,1)S(1)}, bf16[2,16,16384]{2,1,0:T(8,128)(2,1)}, u32[]{:S(2)}) copy-start(bf16[2,16,16384]{2,1,0:T(8,128)(2,1)} %param.7) | copy-start | bytes 3145732
  5.0 18.4 %collective-permute-start = (f32[16,32,128]{2,0,1:T(8,128)S(1)}, f32[16,32,128]{2,0,1:T(8,128)}, u32[]{:S(2)}, u32[]{:S(2)}) collective-permute-start(f32[16,32,128]{2,0,1:T(8,128)S(1)} %fusion.15), channel_id=1, source_target_pairs={{0,16},{8,24},{16,0},{24,8},{1,17},{9,25},{17,1},{25,9},{2,18},{10... | collective-permute-start | bytes 786440 | tf_op jit(solution)/shard_map/ppermute | solution.py:90
  8.7 4.7 %collective-permute-start.2 = (bf16[2,16,128]{2,1,0:T(8,128)(2,1)S(1)}, bf16[2,16,128]{2,1,0:T(8,128)(2,1)S(1)}, u32[]{:S(2)}, u32[]{:S(2)}) collective-permute-start(bf16[2,16,128]{2,1,0:T(8,128)(2,1)S(1)} %get-tuple-element.22), channel_id=1, source_target_pairs={{0,8},{8,16},{16,24},{24,0},{1,9},{9,17},{17,25},{25,1},{2,10},{10... | collective-permute-start | bytes 24584 | tf_op jit(solution)/shard_map/ppermute | solution.py:26
  10.2 3.7 %collective-permute-start.3 = (bf16[2,16,128]{2,1,0:T(8,128)(2,1)S(1)}, bf16[2,16,128]{2,1,0:T(8,128)(2,1)S(1)}, u32[]{:S(2)}, u32[]{:S(2)}) collective-permute-start(bf16[2,16,128]{2,1,0:T(8,128)(2,1)S(1)} %get-tuple-element.21), channel_id=1, source_target_pairs={{8,0},{16,8},{24,16},{0,24},{9,1},{17,9},{25,17},{1,25},{10,2},{18... | collective-permute-start | bytes 24584 | tf_op jit(solution)/shard_map/ppermute | solution.py:27
  14.1 1.4 collective-permute-start.4
  16.3 8.1 %copy-start.2 = (bf16[2,18,16640]{2,1,0:T(8,128)(2,1)}, bf16[2,18,16640]{2,1,0:T(8,128)(2,1)S(1)}, u32[]{:S(2)}) copy-start(bf16[2,18,16640]{2,1,0:T(8,128)(2,1)S(1)} %pad_maximum_fusion.refs_0_) | copy-start | bytes 3594244
  16.4 10.3 %copy-start.7 = (bf16[2,16,16384]{2,1,0:T(8,128)(2,1)S(1)}, bf16[2,16,16384]{2,1,0:T(8,128)(2,1)}, u32[]{:S(2)}) copy-start(bf16[2,16,16384]{2,1,0:T(8,128)(2,1)} %param.13) | copy-start | bytes 3145732
  17.6 25.9 %collective-permute-start.5 = (bf16[1,18,16640]{2,1,0:T(8,128)(2,1)}, bf16[1,18,16640]{2,1,0:T(8,128)(2,1)}, u32[]{:S(2)}, u32[]{:S(2)}) collective-permute-start(bf16[1,18,16640]{2,1,0:T(8,128)(2,1)} %get-tuple-element.18), channel_id=1, source_target_pairs={{0,1},{1,2},{2,3},{4,5},{5,6},{6,7},{8,9},{9,10},{10,11},{12,13},{... | collective-permute-start | bytes 1797128 | tf_op jit(solution)/shard_map/ppermute | solution.py:126
  22.0 21.8 %collective-permute-start.6 = (bf16[1,18,16640]{2,1,0:T(8,128)(2,1)}, bf16[1,18,16640]{2,1,0:T(8,128)(2,1)}, u32[]{:S(2)}, u32[]{:S(2)}) collective-permute-start(bf16[1,18,16640]{2,1,0:T(8,128)(2,1)} %get-tuple-element.17), channel_id=1, source_target_pairs={{1,0},{2,1},{3,2},{5,4},{6,5},{7,6},{9,8},{10,9},{11,10},{13,12},{... | collective-permute-start | bytes 1797128 | tf_op jit(solution)/shard_map/ppermute | solution.py:127
  24.5 2.2 %copy-start.11 = (f32[16,32,128]{2,0,1:T(8,128)}, f32[16,32,128]{2,0,1:T(8,128)S(1)}, u32[]{:S(2)}) copy-start(f32[16,32,128]{2,0,1:T(8,128)S(1)} %fusion.17) | copy-start | bytes 786436
  25.2 17.3 %collective-permute-start.1 = (f32[8,32,128]{2,0,1:T(8,128)}, f32[8,32,128]{2,0,1:T(8,128)}, u32[]{:S(2)}, u32[]{:S(2)}) collective-permute-start(f32[8,32,128]{2,0,1:T(8,128)} %constant_dynamic-slice_fusion.1), channel_id=1, source_target_pairs={{0,8},{8,0},{16,24},{24,16},{1,9},{9,1},{17,25},{25,17},{2,10},{10... | collective-permute-start | bytes 393224 | tf_op jit(solution)/shard_map/ppermute | solution.py:90
  29.2 1.6 %copy-start.6 = (bf16[32,64,64]{2,1,0:T(8,128)(2,1)S(1)}, bf16[32,64,64]{2,1,0:T(8,128)(2,1)}, u32[]{:S(2)}) copy-start(bf16[32,64,64]{2,1,0:T(8,128)(2,1)} %param.12) | copy-start | bytes 786436
  29.2 1.8 %copy-start.15 = (bf16[27,64]{1,0:T(8,128)(2,1)S(1)}, bf16[27,64]{1,0:T(8,128)(2,1)}, u32[]{:S(2)}) copy-start(bf16[27,64]{1,0:T(8,128)(2,1)} %param.8) | copy-start | bytes 10372
  32.2 10.3 %copy-start.12 = (f32[16,32,128]{2,0,1:T(8,128)S(1)}, f32[16,32,128]{2,0,1:T(8,128)}, u32[]{:S(2)}) copy-start(f32[16,32,128]{2,0,1:T(8,128)} %copy-done.11) | copy-start | bytes 786436
  50.6 9.1 %collective-permute-start.7 = (bf16[8,32,128]{2,1,0:T(8,128)(2,1)S(1)}, bf16[8,32,128]{2,1,0:T(8,128)(2,1)S(1)}, u32[]{:S(2)}, u32[]{:S(2)}) collective-permute-start(bf16[8,32,128]{2,1,0:T(8,128)(2,1)S(1)} %convolution_convert_fusion.2), channel_id=1, source_target_pairs={{0,8},{8,0},{16,24},{24,16},{1,9},{9,1},{17,25},{25,17},{2,10},{10... | collective-permute-start | bytes 196616 | tf_op jit(solution)/shard_map/ppermute | solution.py:68
  55.1 1.2 copy-start.16
  56.4 3.3 %copy-start.4 = (f32[8192,256]{1,0:T(8,128)}, f32[8192,256]{1,0:T(8,128)S(1)}, u32[]{:S(2)}) copy-start(f32[8192,256]{1,0:T(8,128)S(1)} %fusion.105) | copy-start | bytes 25165828
  59.6 5.8 %copy-start.8 = (bf16[32,256,64]{1,2,0:T(8,128)(2,1)S(1)}, bf16[32,256,64]{1,2,0:T(8,128)(2,1)}, u32[]{:S(2)}) copy-start(bf16[32,256,64]{1,2,0:T(8,128)(2,1)} %copy.30) | copy-start | bytes 3145732
  59.7 5.0 %collective-permute-start.8 = (bf16[16,32,128]{2,1,0:T(8,128)(2,1)S(1)}, bf16[16,32,128]{2,1,0:T(8,128)(2,1)S(1)}, u32[]{:S(2)}, u32[]{:S(2)}) collective-permute-start(bf16[16,32,128]{2,1,0:T(8,128)(2,1)S(1)} %pad_maximum_fusion.3), channel_id=1, source_target_pairs={{0,16},{8,24},{16,0},{24,8},{1,17},{9,25},{17,1},{25,9},{2,18},{10... | collective-permute-start | bytes 393224 | tf_op jit(solution)/shard_map/ppermute | solution.py:68
  69.7 6.4 %collective-permute-start.9 = (f32[16,32,128]{2,0,1:T(8,128)S(1)}, f32[16,32,128]{2,0,1:T(8,128)S(1)}, u32[]{:S(2)}, u32[]{:S(2)}) collective-permute-start(f32[16,32,128]{2,0,1:T(8,128)S(1)} %fusion.12), channel_id=1, source_target_pairs={{0,16},{8,24},{16,0},{24,8},{1,17},{9,25},{17,1},{25,9},{2,18},{10... | collective-permute-start | bytes 786440 | tf_op jit(solution)/shard_map/ppermute | solution.py:90
  76.3 1.3 copy-start.13
  77.0 15.0 %collective-permute-start.10 = (f32[8,32,128]{2,0,1:T(8,128)}, f32[8,32,128]{2,0,1:T(8,128)}, u32[]{:S(2)}, u32[]{:S(2)}) collective-permute-start(f32[8,32,128]{2,0,1:T(8,128)} %constant_dynamic-slice_fusion), channel_id=1, source_target_pairs={{0,8},{8,0},{16,24},{24,16},{1,9},{9,1},{17,25},{25,17},{2,10},{10... | collective-permute-start | bytes 393224 | tf_op jit(solution)/shard_map/ppermute | solution.py:90
  77.6 7.9 %copy-start.9 = (bf16[32,256,64]{1,2,0:T(8,128)(2,1)S(1)}, bf16[32,256,64]{1,2,0:T(8,128)(2,1)}, u32[]{:S(2)}) copy-start(bf16[32,256,64]{1,2,0:T(8,128)(2,1)} %get-tuple-element.14) | copy-start | bytes 3145732
  86.5 2.5 %copy-start.10 = (bf16[8192,64]{0,1:T(8,128)(2,1)S(1)}, bf16[8192,64]{0,1:T(8,128)(2,1)}, u32[]{:S(2)}) copy-start(bf16[8192,64]{0,1:T(8,128)(2,1)} %convolution_convert_fusion) | copy-start | bytes 3145732
  93.8 4.8 %collective-permute-start.11 = (bf16[2,16,128]{2,1,0:T(8,128)(2,1)S(1)}, bf16[2,16,128]{2,1,0:T(8,128)(2,1)S(1)}, u32[]{:S(2)}, u32[]{:S(2)}) collective-permute-start(bf16[2,16,128]{2,1,0:T(8,128)(2,1)S(1)} %get-tuple-element.20), channel_id=1, source_target_pairs={{0,8},{8,16},{16,24},{24,0},{1,9},{9,17},{17,25},{25,1},{2,10},{10... | collective-permute-start | bytes 24584 | tf_op jit(solution)/shard_map/ppermute | solution.py:26
  95.4 5.2 %collective-permute-start.16 = (bf16[8,32,128]{2,1,0:T(8,128)(2,1)S(1)}, bf16[8,32,128]{2,1,0:T(8,128)(2,1)S(1)}, u32[]{:S(2)}, u32[]{:S(2)}) collective-permute-start(bf16[8,32,128]{2,1,0:T(8,128)(2,1)S(1)} %convolution_convert_fusion.1), channel_id=1, source_target_pairs={{0,8},{8,0},{16,24},{24,16},{1,9},{9,1},{17,25},{25,17},{2,10},{10... | collective-permute-start | bytes 196616 | tf_op jit(solution)/shard_map/ppermute | solution.py:68
  96.6 3.7 %collective-permute-start.12 = (bf16[2,16,128]{2,1,0:T(8,128)(2,1)S(1)}, bf16[2,16,128]{2,1,0:T(8,128)(2,1)S(1)}, u32[]{:S(2)}, u32[]{:S(2)}) collective-permute-start(bf16[2,16,128]{2,1,0:T(8,128)(2,1)S(1)} %get-tuple-element.19), channel_id=1, source_target_pairs={{8,0},{16,8},{24,16},{0,24},{9,1},{17,9},{25,17},{1,25},{10,2},{18... | collective-permute-start | bytes 24584 | tf_op jit(solution)/shard_map/ppermute | solution.py:27
  98.6 21.7 %collective-permute-start.18 = (bf16[64,1024]{1,0:T(8,128)(2,1)S(1)}, bf16[64,1024]{1,0:T(8,128)(2,1)S(1)}, u32[]{:S(2)}, u32[]{:S(2)}) collective-permute-start(bf16[64,1024]{1,0:T(8,128)(2,1)S(1)} %convert_element_type.135), channel_id=1, source_target_pairs={{0,4},{4,0},{1,5},{5,1},{2,6},{6,2},{3,7},{7,3},{8,12},{12,8},{9,1... | collective-permute-start | bytes 393224 | tf_op jit(solution)/shard_map/ppermute | solution.py:107
  100.5 1.4 collective-permute-start.13
  100.6 22.4 %collective-permute-start.17 = (bf16[16,32,128]{2,1,0:T(8,128)(2,1)S(1)}, bf16[16,32,128]{2,1,0:T(8,128)(2,1)S(1)}, u32[]{:S(2)}, u32[]{:S(2)}) collective-permute-start(bf16[16,32,128]{2,1,0:T(8,128)(2,1)S(1)} %pad_maximum_fusion.4), channel_id=1, source_target_pairs={{0,16},{8,24},{16,0},{24,8},{1,17},{9,25},{17,1},{25,9},{2,18},{10... | collective-permute-start | bytes 393224 | tf_op jit(solution)/shard_map/ppermute | solution.py:68
  102.8 7.9 %copy-start.3 = (bf16[2,18,16640]{2,1,0:T(8,128)(2,1)}, bf16[2,18,16640]{2,1,0:T(8,128)(2,1)S(1)}, u32[]{:S(2)}) copy-start(bf16[2,18,16640]{2,1,0:T(8,128)(2,1)S(1)} %pad_maximum_fusion.1.refs_0_) | copy-start | bytes 3594244
  104.1 40.3 %collective-permute-start.14 = (bf16[1,18,16640]{2,1,0:T(8,128)(2,1)}, bf16[1,18,16640]{2,1,0:T(8,128)(2,1)S(1)}, u32[]{:S(2)}, u32[]{:S(2)}) collective-permute-start(bf16[1,18,16640]{2,1,0:T(8,128)(2,1)} %get-tuple-element.16), channel_id=1, source_target_pairs={{0,1},{1,2},{2,3},{4,5},{5,6},{6,7},{8,9},{9,10},{10,11},{12,13},{... | collective-permute-start | bytes 1797128 | tf_op jit(solution)/shard_map/ppermute | solution.py:126
  108.7 35.7 %collective-permute-start.15 = (bf16[1,18,16640]{2,1,0:T(8,128)(2,1)}, bf16[1,18,16640]{2,1,0:T(8,128)(2,1)}, u32[]{:S(2)}, u32[]{:S(2)}) collective-permute-start(bf16[1,18,16640]{2,1,0:T(8,128)(2,1)} %get-tuple-element.15), channel_id=1, source_target_pairs={{1,0},{2,1},{3,2},{5,4},{6,5},{7,6},{9,8},{10,9},{11,10},{13,12},{... | collective-permute-start | bytes 1797128 | tf_op jit(solution)/shard_map/ppermute | solution.py:127
  120.3 12.9 %collective-permute-start.19 = (bf16[64,1024]{1,0:T(8,128)(2,1)S(1)}, bf16[64,1024]{1,0:T(8,128)(2,1)S(1)}, u32[]{:S(2)}, u32[]{:S(2)}) collective-permute-start(bf16[64,1024]{1,0:T(8,128)(2,1)S(1)} %add_convert_fusion.1), channel_id=1, source_target_pairs={{0,1},{1,0},{2,3},{3,2},{4,5},{5,4},{6,7},{7,6},{8,9},{9,8},{10,11... | collective-permute-start | bytes 393224 | tf_op jit(solution)/shard_map/ppermute | solution.py:107
  133.3 10.2 %collective-permute-start.20 = (bf16[64,1024]{1,0:T(8,128)(2,1)S(1)}, bf16[64,1024]{1,0:T(8,128)(2,1)S(1)}, u32[]{:S(2)}, u32[]{:S(2)}) collective-permute-start(bf16[64,1024]{1,0:T(8,128)(2,1)S(1)} %add_convert_fusion), channel_id=1, source_target_pairs={{0,2},{1,3},{2,0},{3,1},{4,6},{5,7},{6,4},{7,5},{8,10},{9,11},{10,... | collective-permute-start | bytes 393224 | tf_op jit(solution)/shard_map/ppermute | solution.py:107
  143.5 9.3 %copy-start.1 = (bf16[64,256]{1,0:T(8,128)(2,1)S(1)}, bf16[64,256]{1,0:T(8,128)(2,1)}, u32[]{:S(2)}) copy-start(bf16[64,256]{1,0:T(8,128)(2,1)} %param.9) | copy-start | bytes 98308
  144.5 0.9 copy-start.14

commit v21 on v20

--- a/solution.py
+++ b/solution.py
@@ -162,7 +162,9 @@
                     + pltpu.roll(right, shift, 1)[:, :chunk]
                 )
                 for acc_ref in acc_refs:
-                    total = total + acc_ref[plane, pl.ds(row, rows), pl.ds(base, chunk)]
+                    total = total + acc_ref[plane, pl.ds(row, rows), pl.ds(base, chunk)].astype(
+                        jnp.float32
+                    )
                 o_ref[plane, pl.ds(row, rows), pl.ds(base, chunk)] = total.astype(o_ref.dtype)
         return carry
 
@@ -306,7 +308,7 @@
         x_cells,
         channels,
         jnp.bfloat16,
-        (spectral_grad.reshape(planes, y_cells, merged),),
+        (spectral_grad.astype(jnp.bfloat16).reshape(planes, y_cells, merged),),
     )
     return (output, grad_features, grad_spec)
 

time: 153 us -> 150 us (0.980)
  local copies, waits for them, and re-layouts: 33.9 us -> 29.9 us
    add x1 -> x0, local copies, waits for them, and re-layouts: 2.74 us -> none  [share_inverse(): running + jnp.einsum('krc,xk->rxc', segment[:, :, channels:], sin_table,...]
  transfers between devices with their start and end apart: 21 -> 21, of which waited for: 9 -> 10; matrix products, arithmetic and copies ran while one was open for 31% -> 30% of each run, Pallas kernels for 13% -> 13%
where the time goes in v21:
time: 150 us; the launch traced here: 149 us
  starting transfers between devices  35.3 us (24%)
  Pallas kernels  33 us (22%)
  local copies, waits for them, and re-layouts  29.9 us (20%)
  waiting for transfers between devices  23.2 us (15%)
  matrix products  19.6 us (13%)
  other arithmetic  7.28 us (5%)
    pallas_call x4, Pallas kernels, stencil_call(): pl.pallas_call(kernel, out_shape=jax.ShapeDtypeStruct((len(plan), y_cells...  33 us
    ppermute x3, waiting for transfers between devices, butterfly_sum(): lax.ppermute(value, axis, [(i, i ^ step) for i in range(size)])  10.6 us
    ppermute x2, starting transfers between devices, spatial_rims(): below = lax.ppermute(inner[-1:], 'gz', up)  9.88 us
    dot_general x1, matrix products, per_device(): jnp.dot(grad_hidden, expand_weight.T, preferred_element_type=jnp.float32)  7.88 us
    ppermute x4, starting transfers between devices, ring_reduce_scatter(): lax.ppermute(send, axis, [(i, i ^ step) for i in range(size)])  6.66 us
    ppermute x4, starting transfers between devices, ring_gather(): lax.ppermute(block, axis, [(i, i ^ step) for i in range(size)])  5.36 us
    ppermute x3, starting transfers between devices, butterfly_sum(): lax.ppermute(value, axis, [(i, i ^ step) for i in range(size)])  4.5 us
    ppermute x4, waiting for transfers between devices, ring_reduce_scatter(): lax.ppermute(send, axis, [(i, i ^ step) for i in range(size)])  3.69 us
  transfers between devices with their start and end apart: 21, of which 10 were waited for; matrix products, arithmetic and copies ran while one was open for 30% of the time, Pallas kernels for 13%

profile of v21, /device:TPU:0, one launch (start us, length us, event | category | flops | bytes accessed | tf_op | source)
XLA Modules:
  0.0 149.4 jit_solution(16354286005228454535)
XLA Ops:
  0.7 3.0 %reshape.89 = bf16[32,256,64]{2,1,0:T(8,128)(2,1)S(1)} reshape(bf16[2,16,16384]{2,1,0:T(8,128)(2,1)} %param.7) | data formatting | bytes 2097152 | tf_op jit(solution)/shard_map/reshape | solution.py:261
  5.0 3.0 %collective-permute-start = (f32[16,32,128]{2,0,1:T(8,128)S(1)}, f32[16,32,128]{2,0,1:T(8,128)}, u32[]{:S(2)}, u32[]{:S(2)}) collective-permute-start(f32[16,32,128]{2,0,1:T(8,128)S(1)} %fusion.16), channel_id=1, source_target_pairs={{0,16},{8,24},{16,0},{24,8},{1,17},{9,25},{17,1},{25,9},{2,18},{10... | collective-permute-start | bytes 786440 | tf_op jit(solution)/shard_map/ppermute | solution.py:90
  8.7 1.5 collective-permute-start.2
  10.2 1.4 collective-permute-start.3
  11.7 1.7 %collective-permute-done.2 = bf16[2,16,128]{2,1,0:T(8,128)(2,1)S(1)} collective-permute-done((bf16[2,16,128]{2,1,0:T(8,128)(2,1)S(1)}, bf16[2,16,128]{2,1,0:T(8,128)(2,1)S(1)}, u32[]{:S(2)}, u32[]{:S(2)}) %collective-permute-start.2) | collective-permute-done | bytes 8224 | tf_op jit(solution)/shard_map/ppermute | solution.py:26
  14.3 1.2 collective-permute-done.4
  16.4 1.3 fusion.101
  17.6 4.4 %collective-permute-start.5 = (bf16[1,18,16640]{2,1,0:T(8,128)(2,1)}, bf16[1,18,16640]{2,1,0:T(8,128)(2,1)}, u32[]{:S(2)}, u32[]{:S(2)}) collective-permute-start(bf16[1,18,16640]{2,1,0:T(8,128)(2,1)} %get-tuple-element.18), channel_id=1, source_target_pairs={{0,1},{1,2},{2,3},{4,5},{5,6},{6,7},{8,9},{9,10},{10,11},{12,13},{... | collective-permute-start | bytes 1797128 | tf_op jit(solution)/shard_map/ppermute | solution.py:126
  22.0 1.3 collective-permute-start.6
  23.3 1.1 fusion.18
  25.2 1.5 collective-permute-start.1
  26.7 2.5 %reshape.93 = bf16[32,256,64]{2,1,0:T(8,128)(2,1)S(1)} reshape(bf16[2,16,16384]{2,1,0:T(8,128)(2,1)S(1)} %copy-done.7) | data formatting | bytes 2097152 | tf_op jit(solution)/shard_map/reshape | solution.py:281
  29.2 1.6 %copy.30 = bf16[32,256,64]{1,2,0:T(8,128)(2,1)} copy(bf16[32,256,64]{2,1,0:T(8,128)(2,1)S(1)} %reshape.93) | data formatting | bytes 2097152 | tf_op jit(solution)/shard_map/optimization_barrier | solution.py:281
  31.0 1.1 fusion.20
  32.8 9.6 %shard_map.94.refs_2_ = f32[2,16,16384]{2,1,0:T(8,128)} custom-call(bf16[2,18,16640]{2,1,0:T(8,128)(2,1)} %copy-done.2, f32[27,8,128]{2,1,0:T(8,128)} %broadcast_in_dim.18.refs_1_.refs_3_), custom_call_target="tpu_custom_call" | custom-call | tf_op jit(solution)/shard_map/pallas_call | solution.py:181
  43.8 6.7 %shard_map.95 = bf16[2,16,16384]{2,1,0:T(8,128)(2,1)} custom-call(bf16[1,18,16640]{2,1,0:T(8,128)(2,1)} %collective-permute-done.5.refs_0_, bf16[1,18,16640]{2,1,0:T(8,128)(2,1)} %collective-permute-done.6.refs_1_, f32[2,16,16384]{2,1,0:T(8,128)} %shard_map.94.refs_2_, f32[27,8,128]{2,1,0:T(8,128)} %broadcast_in_dim.18.refs_1_.refs_3_), custom_call_target="tpu_custom_call" | custom-call | tf_op jit(solution)/shard_map/pallas_call | solution.py:181
  50.6 1.5 collective-permute-start.7
  52.0 3.0 %reshape.90 = bf16[8192,64]{1,0:T(8,128)(2,1)S(1)} reshape(bf16[2,16,16384]{2,1,0:T(8,128)(2,1)} %shard_map.95) | data formatting | bytes 2097152 | tf_op jit(solution)/shard_map/reshape | solution.py:270
  55.1 1.2 fusion.106
  56.4 2.8 %fusion.5 = f32[8192,64]{0,1:T(8,128)S(1)} fusion(bf16[256,64]{0,1:T(8,128)(2,1)S(1)} %copy-done.15, f32[8192,256]{1,0:T(8,128)S(1)} %fusion.106), kind=kOutput, calls=%fused_computation.10 | convolution fusion | flops 278921216 | bytes 10518528 | tf_op jit(solution)/shard_map/dot_general | solution.py:273
  59.6 1.6 %collective-permute-start.8 = (bf16[16,32,128]{2,1,0:T(8,128)(2,1)S(1)}, bf16[16,32,128]{2,1,0:T(8,128)(2,1)S(1)}, u32[]{:S(2)}, u32[]{:S(2)}) collective-permute-start(bf16[16,32,128]{2,1,0:T(8,128)(2,1)S(1)} %pad_maximum_fusion.3), channel_id=1, source_target_pairs={{0,16},{8,24},{16,0},{24,8},{1,17},{9,25},{17,1},{25,9},{2,18},{10... | collective-permute-start | bytes 393224 | tf_op jit(solution)/shard_map/ppermute | solution.py:68
  61.3 3.4 %collective-permute-done.8 = bf16[16,32,128]{2,1,0:T(8,128)(2,1)S(1)} collective-permute-done((bf16[16,32,128]{2,1,0:T(8,128)(2,1)S(1)}, bf16[16,32,128]{2,1,0:T(8,128)(2,1)S(1)}, u32[]{:S(2)}, u32[]{:S(2)}) %collective-permute-start.8) | collective-permute-done | bytes 131104 | tf_op jit(solution)/shard_map/ppermute | solution.py:68
  65.5 2.7 %fusion.11 = (bf16[32,256,64]{1,2,0:T(8,128)(2,1)S(1)}, bf16[32,256,64]{1,2,0:T(8,128)(2,1)}) fusion(bf16[32,256,64]{1,2,0:T(8,128)(2,1)S(1)} %copy-done.8, f32[256,32,64]{0,2,1:T(8,128)S(1)} %fusion.27, bf16[32,32,64]{2,1,0:T(8,128)(2,1)S(1)} %get-tuple-element.27, f32[32]{0:T(128)S(1)} %get-tuple-element.33, s32[32]{0:T(128)S(1)} %add.135, ...), kind=kOutput, calls=%fused_computation.17 | convolution fusion | flops 41566208 | bytes 7472384 | tf_op jit(solution)/shard_map/krc,xk->rxc/dot_general | solution.py:218
  69.6 1.6 %collective-permute-start.9 = (f32[16,32,128]{2,0,1:T(8,128)S(1)}, f32[16,32,128]{2,0,1:T(8,128)S(1)}, u32[]{:S(2)}, u32[]{:S(2)}) collective-permute-start(f32[16,32,128]{2,0,1:T(8,128)S(1)} %fusion.13), channel_id=1, source_target_pairs={{0,16},{8,24},{16,0},{24,8},{1,17},{9,25},{17,1},{25,9},{2,18},{10... | collective-permute-start | bytes 786440 | tf_op jit(solution)/shard_map/ppermute | solution.py:90
  71.3 1.0 copy.42
  72.4 3.7 %collective-permute-done.9 = f32[16,32,128]{2,0,1:T(8,128)S(1)} collective-permute-done((f32[16,32,128]{2,0,1:T(8,128)S(1)}, f32[16,32,128]{2,0,1:T(8,128)S(1)}, u32[]{:S(2)}, u32[]{:S(2)}) %collective-permute-start.9) | collective-permute-done | bytes 262176 | tf_op jit(solution)/shard_map/ppermute | solution.py:90
  77.5 7.9 %convolution_convert_fusion = bf16[8192,64]{0,1:T(8,128)(2,1)} fusion(bf16[64,256]{1,0:T(8,128)(2,1)S(1)} %copy-done, bf16[8192,64]{0,1:T(8,128)(2,1)} %bitcast.54, bf16[256,64]{0,1:T(8,128)(2,1)} %param.10, f32[8192,256]{1,0:T(8,128)} %copy-done.4), kind=kOutput, calls=%fused_computation.3 | convolution fusion | flops 558366720 | bytes 10551296 | tf_op jit(solution)/shard_map/dot_general | solution.py:290
  85.4 1.1 copy.29
  86.5 2.5 %reshape.92 = bf16[2,16,16384]{2,1,0:T(8,128)(2,1)} reshape(bf16[32,256,64]{2,1,0:T(8,128)(2,1)S(1)} %copy.29) | data formatting | bytes 2097152 | tf_op jit(solution)/shard_map/reshape | solution.py:279
  89.0 1.1 copy.35
  90.0 1.9 %reshape.95 = bf16[2,16,16384]{2,1,0:T(8,128)(2,1)S(1)} reshape(bf16[8192,64]{1,0:T(8,128)(2,1)S(1)} %copy.35) | data formatting | bytes 2097152 | tf_op jit(solution)/shard_map/reshape | solution.py:293
  92.0 1.0 add_convert_fusion.3
  93.8 1.5 %collective-permute-start.11 = (bf16[2,16,128]{2,1,0:T(8,128)(2,1)S(1)}, bf16[2,16,128]{2,1,0:T(8,128)(2,1)S(1)}, u32[]{:S(2)}, u32[]{:S(2)}) collective-permute-start(bf16[2,16,128]{2,1,0:T(8,128)(2,1)S(1)} %get-tuple-element.20), channel_id=1, source_target_pairs={{0,8},{8,16},{16,24},{24,0},{1,9},{9,17},{17,25},{25,1},{2,10},{10... | collective-permute-start | bytes 24584 | tf_op jit(solution)/shard_map/ppermute | solution.py:26
  95.3 1.3 collective-permute-start.16
  96.6 1.7 %collective-permute-start.12 = (bf16[2,16,128]{2,1,0:T(8,128)(2,1)S(1)}, bf16[2,16,128]{2,1,0:T(8,128)(2,1)S(1)}, u32[]{:S(2)}, u32[]{:S(2)}) collective-permute-start(bf16[2,16,128]{2,1,0:T(8,128)(2,1)S(1)} %get-tuple-element.19), channel_id=1, source_target_pairs={{8,0},{16,8},{24,16},{0,24},{9,1},{17,9},{25,17},{1,25},{10,2},{18... | collective-permute-start | bytes 24584 | tf_op jit(solution)/shard_map/ppermute | solution.py:27
  98.7 1.5 %collective-permute-done.12 = bf16[2,16,128]{2,1,0:T(8,128)(2,1)S(1)} collective-permute-done((bf16[2,16,128]{2,1,0:T(8,128)(2,1)S(1)}, bf16[2,16,128]{2,1,0:T(8,128)(2,1)S(1)}, u32[]{:S(2)}, u32[]{:S(2)}) %collective-permute-start.12) | collective-permute-done | bytes 8224 | tf_op jit(solution)/shard_map/ppermute | solution.py:27
  100.6 1.0 collective-permute-start.17
  102.7 1.4 fusion.100
  104.1 5.5 %collective-permute-start.14 = (bf16[1,18,16640]{2,1,0:T(8,128)(2,1)}, bf16[1,18,16640]{2,1,0:T(8,128)(2,1)}, u32[]{:S(2)}, u32[]{:S(2)}) collective-permute-start(bf16[1,18,16640]{2,1,0:T(8,128)(2,1)} %get-tuple-element.16), channel_id=1, source_target_pairs={{0,1},{1,2},{2,3},{4,5},{5,6},{6,7},{8,9},{9,10},{10,11},{12,13},{... | collective-permute-start | bytes 1797128 | tf_op jit(solution)/shard_map/ppermute | solution.py:126
  109.6 1.3 collective-permute-start.15
  111.5 9.6 %shard_map.96.refs_2_ = f32[2,16,16384]{2,1,0:T(8,128)} custom-call(bf16[2,18,16640]{2,1,0:T(8,128)(2,1)} %copy-done.3, f32[27,8,128]{2,1,0:T(8,128)} %broadcast_in_dim.36.refs_1_.refs_4_), custom_call_target="tpu_custom_call" | custom-call | tf_op jit(solution)/shard_map/pallas_call | solution.py:181
  121.1 2.7 %collective-permute-start.19 = (bf16[64,1024]{1,0:T(8,128)(2,1)S(1)}, bf16[64,1024]{1,0:T(8,128)(2,1)S(1)}, u32[]{:S(2)}, u32[]{:S(2)}) collective-permute-start(bf16[64,1024]{1,0:T(8,128)(2,1)S(1)} %add_convert_fusion.2), channel_id=1, source_target_pairs={{0,1},{1,0},{2,3},{3,2},{4,5},{5,4},{6,7},{7,6},{8,9},{9,8},{10,11... | collective-permute-start | bytes 393224 | tf_op jit(solution)/shard_map/ppermute | solution.py:107
  124.6 9.4 %collective-permute-done.19 = bf16[64,1024]{1,0:T(8,128)(2,1)S(1)} collective-permute-done((bf16[64,1024]{1,0:T(8,128)(2,1)S(1)}, bf16[64,1024]{1,0:T(8,128)(2,1)S(1)}, u32[]{:S(2)}, u32[]{:S(2)}) %collective-permute-start.19) | collective-permute-done | bytes 131104 | tf_op jit(solution)/shard_map/ppermute | solution.py:107
  134.1 1.7 %collective-permute-start.20 = (bf16[64,1024]{1,0:T(8,128)(2,1)S(1)}, bf16[64,1024]{1,0:T(8,128)(2,1)S(1)}, u32[]{:S(2)}, u32[]{:S(2)}) collective-permute-start(bf16[64,1024]{1,0:T(8,128)(2,1)S(1)} %add_convert_fusion.1), channel_id=1, source_target_pairs={{0,2},{1,3},{2,0},{3,1},{4,6},{5,7},{6,4},{7,5},{8,10},{9,11},{10,... | collective-permute-start | bytes 393224 | tf_op jit(solution)/shard_map/ppermute | solution.py:107
  136.4 1.1 copy.38
  137.5 2.5 %reshape.96.refs_3_ = bf16[2,16,16384]{2,1,0:T(8,128)(2,1)} reshape(bf16[32,256,64]{2,1,0:T(8,128)(2,1)S(1)} %copy.38) | data formatting | bytes 2097152 | tf_op jit(solution)/shard_map/reshape | solution.py:311
  140.0 1.2 collective-permute-done.20
  142.2 7.1 %shard_map.97 = bf16[2,16,16384]{2,1,0:T(8,128)(2,1)} custom-call(bf16[1,18,16640]{2,1,0:T(8,128)(2,1)} %collective-permute-done.14.refs_0_, bf16[1,18,16640]{2,1,0:T(8,128)(2,1)} %collective-permute-done.15.refs_1_, f32[2,16,16384]{2,1,0:T(8,128)} %shard_map.96.refs_2_, bf16[2,16,16384]{2,1,0:T(8,128)(2,1)} %reshape.96.refs_3_, ...), custom_call_target="tpu_custom_call" | custom-call | tf_op jit(solution)/shard_map/pallas_call | solution.py:181
  (110 shorter events, 16.7 us)
Async XLA Ops:
  0.6 54.5 %copy-start = (bf16[64,256]{1,0:T(8,128)(2,1)S(1)}, bf16[64,256]{1,0:T(8,128)(2,1)}, u32[]{:S(2)}) copy-start(bf16[64,256]{1,0:T(8,128)(2,1)} %param.9) | copy-start | bytes 98308
  4.8 8.6 %copy-start.5 = (bf16[2,16,16384]{2,1,0:T(8,128)(2,1)S(1)}, bf16[2,16,16384]{2,1,0:T(8,128)(2,1)}, u32[]{:S(2)}) copy-start(bf16[2,16,16384]{2,1,0:T(8,128)(2,1)} %param.7) | copy-start | bytes 3145732
  5.0 18.4 %collective-permute-start = (f32[16,32,128]{2,0,1:T(8,128)S(1)}, f32[16,32,128]{2,0,1:T(8,128)}, u32[]{:S(2)}, u32[]{:S(2)}) collective-permute-start(f32[16,32,128]{2,0,1:T(8,128)S(1)} %fusion.16), channel_id=1, source_target_pairs={{0,16},{8,24},{16,0},{24,8},{1,17},{9,25},{17,1},{25,9},{2,18},{10... | collective-permute-start | bytes 786440 | tf_op jit(solution)/shard_map/ppermute | solution.py:90
  8.7 4.7 %collective-permute-start.2 = (bf16[2,16,128]{2,1,0:T(8,128)(2,1)S(1)}, bf16[2,16,128]{2,1,0:T(8,128)(2,1)S(1)}, u32[]{:S(2)}, u32[]{:S(2)}) collective-permute-start(bf16[2,16,128]{2,1,0:T(8,128)(2,1)S(1)} %get-tuple-element.22), channel_id=1, source_target_pairs={{0,8},{8,16},{16,24},{24,0},{1,9},{9,17},{17,25},{25,1},{2,10},{10... | collective-permute-start | bytes 24584 | tf_op jit(solution)/shard_map/ppermute | solution.py:26
  10.2 3.7 %collective-permute-start.3 = (bf16[2,16,128]{2,1,0:T(8,128)(2,1)S(1)}, bf16[2,16,128]{2,1,0:T(8,128)(2,1)S(1)}, u32[]{:S(2)}, u32[]{:S(2)}) collective-permute-start(bf16[2,16,128]{2,1,0:T(8,128)(2,1)S(1)} %get-tuple-element.21), channel_id=1, source_target_pairs={{8,0},{16,8},{24,16},{0,24},{9,1},{17,9},{25,17},{1,25},{10,2},{18... | collective-permute-start | bytes 24584 | tf_op jit(solution)/shard_map/ppermute | solution.py:27
  14.1 1.4 collective-permute-start.4
  16.3 8.1 %copy-start.2 = (bf16[2,18,16640]{2,1,0:T(8,128)(2,1)}, bf16[2,18,16640]{2,1,0:T(8,128)(2,1)S(1)}, u32[]{:S(2)}) copy-start(bf16[2,18,16640]{2,1,0:T(8,128)(2,1)S(1)} %pad_maximum_fusion.refs_0_) | copy-start | bytes 3594244
  16.4 10.3 %copy-start.7 = (bf16[2,16,16384]{2,1,0:T(8,128)(2,1)S(1)}, bf16[2,16,16384]{2,1,0:T(8,128)(2,1)}, u32[]{:S(2)}) copy-start(bf16[2,16,16384]{2,1,0:T(8,128)(2,1)} %param.13) | copy-start | bytes 3145732
  17.6 25.9 %collective-permute-start.5 = (bf16[1,18,16640]{2,1,0:T(8,128)(2,1)}, bf16[1,18,16640]{2,1,0:T(8,128)(2,1)}, u32[]{:S(2)}, u32[]{:S(2)}) collective-permute-start(bf16[1,18,16640]{2,1,0:T(8,128)(2,1)} %get-tuple-element.18), channel_id=1, source_target_pairs={{0,1},{1,2},{2,3},{4,5},{5,6},{6,7},{8,9},{9,10},{10,11},{12,13},{... | collective-permute-start | bytes 1797128 | tf_op jit(solution)/shard_map/ppermute | solution.py:126
  22.0 21.8 %collective-permute-start.6 = (bf16[1,18,16640]{2,1,0:T(8,128)(2,1)}, bf16[1,18,16640]{2,1,0:T(8,128)(2,1)}, u32[]{:S(2)}, u32[]{:S(2)}) collective-permute-start(bf16[1,18,16640]{2,1,0:T(8,128)(2,1)} %get-tuple-element.17), channel_id=1, source_target_pairs={{1,0},{2,1},{3,2},{5,4},{6,5},{7,6},{9,8},{10,9},{11,10},{13,12},{... | collective-permute-start | bytes 1797128 | tf_op jit(solution)/shard_map/ppermute | solution.py:127
  24.4 2.2 %copy-start.11 = (f32[16,32,128]{2,0,1:T(8,128)}, f32[16,32,128]{2,0,1:T(8,128)S(1)}, u32[]{:S(2)}) copy-start(f32[16,32,128]{2,0,1:T(8,128)S(1)} %fusion.18) | copy-start | bytes 786436
  25.2 17.2 %collective-permute-start.1 = (f32[8,32,128]{2,0,1:T(8,128)}, f32[8,32,128]{2,0,1:T(8,128)}, u32[]{:S(2)}, u32[]{:S(2)}) collective-permute-start(f32[8,32,128]{2,0,1:T(8,128)} %constant_dynamic-slice_fusion.1), channel_id=1, source_target_pairs={{0,8},{8,0},{16,24},{24,16},{1,9},{9,1},{17,25},{25,17},{2,10},{10... | collective-permute-start | bytes 393224 | tf_op jit(solution)/shard_map/ppermute | solution.py:90
  29.1 1.6 %copy-start.6 = (bf16[32,64,64]{2,1,0:T(8,128)(2,1)S(1)}, bf16[32,64,64]{2,1,0:T(8,128)(2,1)}, u32[]{:S(2)}) copy-start(bf16[32,64,64]{2,1,0:T(8,128)(2,1)} %param.12) | copy-start | bytes 786436
  29.2 1.8 %copy-start.14 = (bf16[27,64]{1,0:T(8,128)(2,1)S(1)}, bf16[27,64]{1,0:T(8,128)(2,1)}, u32[]{:S(2)}) copy-start(bf16[27,64]{1,0:T(8,128)(2,1)} %param.8) | copy-start | bytes 10372
  32.2 10.2 %copy-start.12 = (f32[16,32,128]{2,0,1:T(8,128)S(1)}, f32[16,32,128]{2,0,1:T(8,128)}, u32[]{:S(2)}) copy-start(f32[16,32,128]{2,0,1:T(8,128)} %copy-done.11) | copy-start | bytes 786436
  50.6 9.1 %collective-permute-start.7 = (bf16[8,32,128]{2,1,0:T(8,128)(2,1)S(1)}, bf16[8,32,128]{2,1,0:T(8,128)(2,1)S(1)}, u32[]{:S(2)}, u32[]{:S(2)}) collective-permute-start(bf16[8,32,128]{2,1,0:T(8,128)(2,1)S(1)} %convolution_convert_fusion.2), channel_id=1, source_target_pairs={{0,8},{8,0},{16,24},{24,16},{1,9},{9,1},{17,25},{25,17},{2,10},{10... | collective-permute-start | bytes 196616 | tf_op jit(solution)/shard_map/ppermute | solution.py:68
  55.1 1.2 copy-start.15
  56.3 3.3 %copy-start.4 = (f32[8192,256]{1,0:T(8,128)}, f32[8192,256]{1,0:T(8,128)S(1)}, u32[]{:S(2)}) copy-start(f32[8192,256]{1,0:T(8,128)S(1)} %fusion.106) | copy-start | bytes 25165828
  59.6 5.8 %copy-start.8 = (bf16[32,256,64]{1,2,0:T(8,128)(2,1)S(1)}, bf16[32,256,64]{1,2,0:T(8,128)(2,1)}, u32[]{:S(2)}) copy-start(bf16[32,256,64]{1,2,0:T(8,128)(2,1)} %copy.30) | copy-start | bytes 3145732
  59.6 5.0 %collective-permute-start.8 = (bf16[16,32,128]{2,1,0:T(8,128)(2,1)S(1)}, bf16[16,32,128]{2,1,0:T(8,128)(2,1)S(1)}, u32[]{:S(2)}, u32[]{:S(2)}) collective-permute-start(bf16[16,32,128]{2,1,0:T(8,128)(2,1)S(1)} %pad_maximum_fusion.3), channel_id=1, source_target_pairs={{0,16},{8,24},{16,0},{24,8},{1,17},{9,25},{17,1},{25,9},{2,18},{10... | collective-permute-start | bytes 393224 | tf_op jit(solution)/shard_map/ppermute | solution.py:68
  69.6 6.4 %collective-permute-start.9 = (f32[16,32,128]{2,0,1:T(8,128)S(1)}, f32[16,32,128]{2,0,1:T(8,128)S(1)}, u32[]{:S(2)}, u32[]{:S(2)}) collective-permute-start(f32[16,32,128]{2,0,1:T(8,128)S(1)} %fusion.13), channel_id=1, source_target_pairs={{0,16},{8,24},{16,0},{24,8},{1,17},{9,25},{17,1},{25,9},{2,18},{10... | collective-permute-start | bytes 786440 | tf_op jit(solution)/shard_map/ppermute | solution.py:90
  76.2 1.3 copy-start.13
  77.0 15.0 %collective-permute-start.10 = (f32[8,32,128]{2,0,1:T(8,128)}, f32[8,32,128]{2,0,1:T(8,128)}, u32[]{:S(2)}, u32[]{:S(2)}) collective-permute-start(f32[8,32,128]{2,0,1:T(8,128)} %constant_dynamic-slice_fusion), channel_id=1, source_target_pairs={{0,8},{8,0},{16,24},{24,16},{1,9},{9,1},{17,25},{25,17},{2,10},{10... | collective-permute-start | bytes 393224 | tf_op jit(solution)/shard_map/ppermute | solution.py:90
  77.5 7.9 %copy-start.9 = (bf16[32,256,64]{1,2,0:T(8,128)(2,1)S(1)}, bf16[32,256,64]{1,2,0:T(8,128)(2,1)}, u32[]{:S(2)}) copy-start(bf16[32,256,64]{1,2,0:T(8,128)(2,1)} %get-tuple-element.14) | copy-start | bytes 3145732
  86.5 2.5 %copy-start.10 = (bf16[8192,64]{0,1:T(8,128)(2,1)S(1)}, bf16[8192,64]{0,1:T(8,128)(2,1)}, u32[]{:S(2)}) copy-start(bf16[8192,64]{0,1:T(8,128)(2,1)} %convolution_convert_fusion) | copy-start | bytes 3145732
  93.8 4.8 %collective-permute-start.11 = (bf16[2,16,128]{2,1,0:T(8,128)(2,1)S(1)}, bf16[2,16,128]{2,1,0:T(8,128)(2,1)S(1)}, u32[]{:S(2)}, u32[]{:S(2)}) collective-permute-start(bf16[2,16,128]{2,1,0:T(8,128)(2,1)S(1)} %get-tuple-element.20), channel_id=1, source_target_pairs={{0,8},{8,16},{16,24},{24,0},{1,9},{9,17},{17,25},{25,1},{2,10},{10... | collective-permute-start | bytes 24584 | tf_op jit(solution)/shard_map/ppermute | solution.py:26
  95.3 5.2 %collective-permute-start.16 = (bf16[8,32,128]{2,1,0:T(8,128)(2,1)S(1)}, bf16[8,32,128]{2,1,0:T(8,128)(2,1)S(1)}, u32[]{:S(2)}, u32[]{:S(2)}) collective-permute-start(bf16[8,32,128]{2,1,0:T(8,128)(2,1)S(1)} %convolution_convert_fusion.1), channel_id=1, source_target_pairs={{0,8},{8,0},{16,24},{24,16},{1,9},{9,1},{17,25},{25,17},{2,10},{10... | collective-permute-start | bytes 196616 | tf_op jit(solution)/shard_map/ppermute | solution.py:68
  96.6 3.7 %collective-permute-start.12 = (bf16[2,16,128]{2,1,0:T(8,128)(2,1)S(1)}, bf16[2,16,128]{2,1,0:T(8,128)(2,1)S(1)}, u32[]{:S(2)}, u32[]{:S(2)}) collective-permute-start(bf16[2,16,128]{2,1,0:T(8,128)(2,1)S(1)} %get-tuple-element.19), channel_id=1, source_target_pairs={{8,0},{16,8},{24,16},{0,24},{9,1},{17,9},{25,17},{1,25},{10,2},{18... | collective-permute-start | bytes 24584 | tf_op jit(solution)/shard_map/ppermute | solution.py:27
  98.5 22.6 %collective-permute-start.18 = (bf16[64,1024]{1,0:T(8,128)(2,1)S(1)}, bf16[64,1024]{1,0:T(8,128)(2,1)S(1)}, u32[]{:S(2)}, u32[]{:S(2)}) collective-permute-start(bf16[64,1024]{1,0:T(8,128)(2,1)S(1)} %convert_element_type.143), channel_id=1, source_target_pairs={{0,4},{4,0},{1,5},{5,1},{2,6},{6,2},{3,7},{7,3},{8,12},{12,8},{9,1... | collective-permute-start | bytes 393224 | tf_op jit(solution)/shard_map/ppermute | solution.py:107
  100.5 1.4 collective-permute-start.13
  100.6 23.3 %collective-permute-start.17 = (bf16[16,32,128]{2,1,0:T(8,128)(2,1)S(1)}, bf16[16,32,128]{2,1,0:T(8,128)(2,1)S(1)}, u32[]{:S(2)}, u32[]{:S(2)}) collective-permute-start(bf16[16,32,128]{2,1,0:T(8,128)(2,1)S(1)} %pad_maximum_fusion.4), channel_id=1, source_target_pairs={{0,16},{8,24},{16,0},{24,8},{1,17},{9,25},{17,1},{25,9},{2,18},{10... | collective-permute-start | bytes 393224 | tf_op jit(solution)/shard_map/ppermute | solution.py:68
  102.7 8.8 %copy-start.3 = (bf16[2,18,16640]{2,1,0:T(8,128)(2,1)}, bf16[2,18,16640]{2,1,0:T(8,128)(2,1)S(1)}, u32[]{:S(2)}) copy-start(bf16[2,18,16640]{2,1,0:T(8,128)(2,1)S(1)} %pad_maximum_fusion.1.refs_0_) | copy-start | bytes 3594244
  104.1 38.1 %collective-permute-start.14 = (bf16[1,18,16640]{2,1,0:T(8,128)(2,1)}, bf16[1,18,16640]{2,1,0:T(8,128)(2,1)}, u32[]{:S(2)}, u32[]{:S(2)}) collective-permute-start(bf16[1,18,16640]{2,1,0:T(8,128)(2,1)} %get-tuple-element.16), channel_id=1, source_target_pairs={{0,1},{1,2},{2,3},{4,5},{5,6},{6,7},{8,9},{9,10},{10,11},{12,13},{... | collective-permute-start | bytes 1797128 | tf_op jit(solution)/shard_map/ppermute | solution.py:126
  109.6 32.7 %collective-permute-start.15 = (bf16[1,18,16640]{2,1,0:T(8,128)(2,1)}, bf16[1,18,16640]{2,1,0:T(8,128)(2,1)}, u32[]{:S(2)}, u32[]{:S(2)}) collective-permute-start(bf16[1,18,16640]{2,1,0:T(8,128)(2,1)} %get-tuple-element.15), channel_id=1, source_target_pairs={{1,0},{2,1},{3,2},{5,4},{6,5},{7,6},{9,8},{10,9},{11,10},{13,12},{... | collective-permute-start | bytes 1797128 | tf_op jit(solution)/shard_map/ppermute | solution.py:127
  121.1 12.9 %collective-permute-start.19 = (bf16[64,1024]{1,0:T(8,128)(2,1)S(1)}, bf16[64,1024]{1,0:T(8,128)(2,1)S(1)}, u32[]{:S(2)}, u32[]{:S(2)}) collective-permute-start(bf16[64,1024]{1,0:T(8,128)(2,1)S(1)} %add_convert_fusion.2), channel_id=1, source_target_pairs={{0,1},{1,0},{2,3},{3,2},{4,5},{5,4},{6,7},{7,6},{8,9},{9,8},{10,11... | collective-permute-start | bytes 393224 | tf_op jit(solution)/shard_map/ppermute | solution.py:107
  134.1 7.2 %collective-permute-start.20 = (bf16[64,1024]{1,0:T(8,128)(2,1)S(1)}, bf16[64,1024]{1,0:T(8,128)(2,1)S(1)}, u32[]{:S(2)}, u32[]{:S(2)}) collective-permute-start(bf16[64,1024]{1,0:T(8,128)(2,1)S(1)} %add_convert_fusion.1), channel_id=1, source_target_pairs={{0,2},{1,3},{2,0},{3,1},{4,6},{5,7},{6,4},{7,5},{8,10},{9,11},{10,... | collective-permute-start | bytes 393224 | tf_op jit(solution)/shard_map/ppermute | solution.py:107
  141.3 8.1 %copy-start.1 = (bf16[64,256]{1,0:T(8,128)(2,1)S(1)}, bf16[64,256]{1,0:T(8,128)(2,1)}, u32[]{:S(2)}) copy-start(bf16[64,256]{1,0:T(8,128)(2,1)} %param.9) | copy-start | bytes 98308

commit v22 on v21

--- a/solution.py
+++ b/solution.py
@@ -198,7 +198,7 @@
         tuple((0, plane + step_z - 1, step_z) for step_z in range(3) if 0 <= plane + step_z - 1 < planes)
         for plane in range(planes)
     )
-    local = stencil_call(local_plan, (inner,), (), gains, y_cells, lanes, channels, jnp.float32)
+    local = stencil_call(local_plan, (inner,), (), gains, y_cells, lanes, channels, jnp.bfloat16)
     rim_plan = tuple(
         ((((0, 0, 0),) if plane == 0 else ()) + (((1, 0, 2),) if plane == planes - 1 else ()))
         for plane in range(planes)

time: 150 us -> 149 us (level)
  transfers between devices with their start and end apart: 21 -> 21, of which waited for: 10 -> 9; matrix products, arithmetic and copies ran while one was open for 30% -> 30% of each run, Pallas kernels for 13% -> 12%
where the time goes in v22:
time: 149 us; the launch traced here: 148 us
  starting transfers between devices  35.5 us (24%)
  Pallas kernels  31.7 us (21%)
  local copies, waits for them, and re-layouts  29.8 us (20%)
  waiting for transfers between devices  23.4 us (16%)
  matrix products  19.6 us (13%)
  other arithmetic  7.32 us (5%)
    pallas_call x4, Pallas kernels, stencil_call(): pl.pallas_call(kernel, out_shape=jax.ShapeDtypeStruct((len(plan), y_cells...  31.7 us
    ppermute x3, waiting for transfers between devices, butterfly_sum(): lax.ppermute(value, axis, [(i, i ^ step) for i in range(size)])  11.1 us
    ppermute x2, starting transfers between devices, spatial_rims(): below = lax.ppermute(inner[-1:], 'gz', up)  9.77 us
    dot_general x1, matrix products, per_device(): jnp.dot(grad_hidden, expand_weight.T, preferred_element_type=jnp.float32)  7.88 us
    ppermute x4, starting transfers between devices, ring_reduce_scatter(): lax.ppermute(send, axis, [(i, i ^ step) for i in range(size)])  6.65 us
    ppermute x4, starting transfers between devices, ring_gather(): lax.ppermute(block, axis, [(i, i ^ step) for i in range(size)])  5.36 us
    ppermute x3, starting transfers between devices, butterfly_sum(): lax.ppermute(value, axis, [(i, i ^ step) for i in range(size)])  4.36 us
    ppermute x4, waiting for transfers between devices, ring_reduce_scatter(): lax.ppermute(send, axis, [(i, i ^ step) for i in range(size)])  3.69 us
  transfers between devices with their start and end apart: 21, of which 9 were waited for; matrix products, arithmetic and copies ran while one was open for 30% of the time, Pallas kernels for 12%

profile of v22, /device:TPU:0, one launch (start us, length us, event | category | flops | bytes accessed | tf_op | source)
XLA Modules:
  0.0 148.4 jit_solution(1794023957647179867)
XLA Ops:
  0.7 3.0 %reshape.89 = bf16[32,256,64]{2,1,0:T(8,128)(2,1)S(1)} reshape(bf16[2,16,16384]{2,1,0:T(8,128)(2,1)} %param.7) | data formatting | bytes 2097152 | tf_op jit(solution)/shard_map/reshape | solution.py:261
  5.0 3.0 %collective-permute-start = (f32[16,32,128]{2,0,1:T(8,128)S(1)}, f32[16,32,128]{2,0,1:T(8,128)}, u32[]{:S(2)}, u32[]{:S(2)}) collective-permute-start(f32[16,32,128]{2,0,1:T(8,128)S(1)} %fusion.16), channel_id=1, source_target_pairs={{0,16},{8,24},{16,0},{24,8},{1,17},{9,25},{17,1},{25,9},{2,18},{10... | collective-permute-start | bytes 786440 | tf_op jit(solution)/shard_map/ppermute | solution.py:90
  8.7 1.5 %collective-permute-start.2 = (bf16[2,16,128]{2,1,0:T(8,128)(2,1)S(1)}, bf16[2,16,128]{2,1,0:T(8,128)(2,1)S(1)}, u32[]{:S(2)}, u32[]{:S(2)}) collective-permute-start(bf16[2,16,128]{2,1,0:T(8,128)(2,1)S(1)} %get-tuple-element.22), channel_id=1, source_target_pairs={{0,8},{8,16},{16,24},{24,0},{1,9},{9,17},{17,25},{25,1},{2,10},{10... | collective-permute-start | bytes 24584 | tf_op jit(solution)/shard_map/ppermute | solution.py:26
  10.2 1.4 collective-permute-start.3
  11.7 1.7 %collective-permute-done.2 = bf16[2,16,128]{2,1,0:T(8,128)(2,1)S(1)} collective-permute-done((bf16[2,16,128]{2,1,0:T(8,128)(2,1)S(1)}, bf16[2,16,128]{2,1,0:T(8,128)(2,1)S(1)}, u32[]{:S(2)}, u32[]{:S(2)}) %collective-permute-start.2) | collective-permute-done | bytes 8224 | tf_op jit(solution)/shard_map/ppermute | solution.py:26
  14.3 1.2 collective-permute-done.4
  16.4 1.3 fusion.101
  17.6 4.4 %collective-permute-start.5 = (bf16[1,18,16640]{2,1,0:T(8,128)(2,1)}, bf16[1,18,16640]{2,1,0:T(8,128)(2,1)}, u32[]{:S(2)}, u32[]{:S(2)}) collective-permute-start(bf16[1,18,16640]{2,1,0:T(8,128)(2,1)} %get-tuple-element.18), channel_id=1, source_target_pairs={{0,1},{1,2},{2,3},{4,5},{5,6},{6,7},{8,9},{9,10},{10,11},{12,13},{... | collective-permute-start | bytes 1797128 | tf_op jit(solution)/shard_map/ppermute | solution.py:126
  22.0 1.5 collective-permute-start.6
  23.5 1.1 fusion.18
  25.4 1.5 %collective-permute-start.1 = (f32[8,32,128]{2,0,1:T(8,128)}, f32[8,32,128]{2,0,1:T(8,128)}, u32[]{:S(2)}, u32[]{:S(2)}) collective-permute-start(f32[8,32,128]{2,0,1:T(8,128)} %constant_dynamic-slice_fusion.1), channel_id=1, source_target_pairs={{0,8},{8,0},{16,24},{24,16},{1,9},{9,1},{17,25},{25,17},{2,10},{10... | collective-permute-start | bytes 393224 | tf_op jit(solution)/shard_map/ppermute | solution.py:90
  26.9 2.3 %reshape.93 = bf16[32,256,64]{2,1,0:T(8,128)(2,1)S(1)} reshape(bf16[2,16,16384]{2,1,0:T(8,128)(2,1)S(1)} %copy-done.7) | data formatting | bytes 2097152 | tf_op jit(solution)/shard_map/reshape | solution.py:281
  29.2 1.6 %copy.30 = bf16[32,256,64]{1,2,0:T(8,128)(2,1)} copy(bf16[32,256,64]{2,1,0:T(8,128)(2,1)S(1)} %reshape.93) | data formatting | bytes 2097152 | tf_op jit(solution)/shard_map/optimization_barrier | solution.py:281
  31.1 1.2 fusion.20
  32.9 9.2 %shard_map.94.refs_2_ = bf16[2,16,16384]{2,1,0:T(8,128)(2,1)} custom-call(bf16[2,18,16640]{2,1,0:T(8,128)(2,1)} %copy-done.2, f32[27,8,128]{2,1,0:T(8,128)} %broadcast_in_dim.18.refs_1_.refs_3_), custom_call_target="tpu_custom_call" | custom-call | tf_op jit(solution)/shard_map/pallas_call | solution.py:181
  43.8 6.4 %shard_map.95 = bf16[2,16,16384]{2,1,0:T(8,128)(2,1)} custom-call(bf16[1,18,16640]{2,1,0:T(8,128)(2,1)} %collective-permute-done.5.refs_0_, bf16[1,18,16640]{2,1,0:T(8,128)(2,1)} %collective-permute-done.6.refs_1_, bf16[2,16,16384]{2,1,0:T(8,128)(2,1)} %shard_map.94.refs_2_, f32[27,8,128]{2,1,0:T(8,128)} %broadcast_in_dim.18.refs_1_.refs_3_), custom_call_target="tpu_custom_call" | custom-call | tf_op jit(solution)/shard_map/pallas_call | solution.py:181
  50.2 1.5 %collective-permute-start.7 = (bf16[8,32,128]{2,1,0:T(8,128)(2,1)S(1)}, bf16[8,32,128]{2,1,0:T(8,128)(2,1)S(1)}, u32[]{:S(2)}, u32[]{:S(2)}) collective-permute-start(bf16[8,32,128]{2,1,0:T(8,128)(2,1)S(1)} %convolution_convert_fusion.2), channel_id=1, source_target_pairs={{0,8},{8,0},{16,24},{24,16},{1,9},{9,1},{17,25},{25,17},{2,10},{10... | collective-permute-start | bytes 196616 | tf_op jit(solution)/shard_map/ppermute | solution.py:68
  51.7 3.0 %reshape.90 = bf16[8192,64]{1,0:T(8,128)(2,1)S(1)} reshape(bf16[2,16,16384]{2,1,0:T(8,128)(2,1)} %shard_map.95) | data formatting | bytes 2097152 | tf_op jit(solution)/shard_map/reshape | solution.py:270
  54.8 1.2 fusion.106
  56.0 2.8 %fusion.5 = f32[8192,64]{0,1:T(8,128)S(1)} fusion(bf16[256,64]{0,1:T(8,128)(2,1)S(1)} %copy-done.15, f32[8192,256]{1,0:T(8,128)S(1)} %fusion.106), kind=kOutput, calls=%fused_computation.10 | convolution fusion | flops 278921216 | bytes 10518528 | tf_op jit(solution)/shard_map/dot_general | solution.py:273
  59.3 1.6 %collective-permute-start.8 = (bf16[16,32,128]{2,1,0:T(8,128)(2,1)S(1)}, bf16[16,32,128]{2,1,0:T(8,128)(2,1)S(1)}, u32[]{:S(2)}, u32[]{:S(2)}) collective-permute-start(bf16[16,32,128]{2,1,0:T(8,128)(2,1)S(1)} %pad_maximum_fusion.3), channel_id=1, source_target_pairs={{0,16},{8,24},{16,0},{24,8},{1,17},{9,25},{17,1},{25,9},{2,18},{10... | collective-permute-start | bytes 393224 | tf_op jit(solution)/shard_map/ppermute | solution.py:68
  60.9 3.4 %collective-permute-done.8 = bf16[16,32,128]{2,1,0:T(8,128)(2,1)S(1)} collective-permute-done((bf16[16,32,128]{2,1,0:T(8,128)(2,1)S(1)}, bf16[16,32,128]{2,1,0:T(8,128)(2,1)S(1)}, u32[]{:S(2)}, u32[]{:S(2)}) %collective-permute-start.8) | collective-permute-done | bytes 131104 | tf_op jit(solution)/shard_map/ppermute | solution.py:68
  65.1 2.7 %fusion.11 = (bf16[32,256,64]{1,2,0:T(8,128)(2,1)S(1)}, bf16[32,256,64]{1,2,0:T(8,128)(2,1)}) fusion(bf16[32,256,64]{1,2,0:T(8,128)(2,1)S(1)} %copy-done.8, f32[256,32,64]{0,2,1:T(8,128)S(1)} %fusion.27, bf16[32,32,64]{2,1,0:T(8,128)(2,1)S(1)} %get-tuple-element.27, f32[32]{0:T(128)S(1)} %get-tuple-element.33, s32[32]{0:T(128)S(1)} %add.135, ...), kind=kOutput, calls=%fused_computation.17 | convolution fusion | flops 41566208 | bytes 7472384 | tf_op jit(solution)/shard_map/krc,xk->rxc/dot_general | solution.py:218
  69.3 1.6 %collective-permute-start.9 = (f32[16,32,128]{2,0,1:T(8,128)S(1)}, f32[16,32,128]{2,0,1:T(8,128)S(1)}, u32[]{:S(2)}, u32[]{:S(2)}) collective-permute-start(f32[16,32,128]{2,0,1:T(8,128)S(1)} %fusion.13), channel_id=1, source_target_pairs={{0,16},{8,24},{16,0},{24,8},{1,17},{9,25},{17,1},{25,9},{2,18},{10... | collective-permute-start | bytes 786440 | tf_op jit(solution)/shard_map/ppermute | solution.py:90
  71.0 1.0 copy.42
  72.1 3.7 %collective-permute-done.9 = f32[16,32,128]{2,0,1:T(8,128)S(1)} collective-permute-done((f32[16,32,128]{2,0,1:T(8,128)S(1)}, f32[16,32,128]{2,0,1:T(8,128)S(1)}, u32[]{:S(2)}, u32[]{:S(2)}) %collective-permute-start.9) | collective-permute-done | bytes 262176 | tf_op jit(solution)/shard_map/ppermute | solution.py:90
  77.2 7.9 %convolution_convert_fusion = bf16[8192,64]{0,1:T(8,128)(2,1)} fusion(bf16[64,256]{1,0:T(8,128)(2,1)S(1)} %copy-done, bf16[8192,64]{0,1:T(8,128)(2,1)} %bitcast.54, bf16[256,64]{0,1:T(8,128)(2,1)} %param.10, f32[8192,256]{1,0:T(8,128)} %copy-done.4), kind=kOutput, calls=%fused_computation.3 | convolution fusion | flops 558366720 | bytes 10551296 | tf_op jit(solution)/shard_map/dot_general | solution.py:290
  85.1 1.1 copy.29
  86.1 2.5 %reshape.92 = bf16[2,16,16384]{2,1,0:T(8,128)(2,1)} reshape(bf16[32,256,64]{2,1,0:T(8,128)(2,1)S(1)} %copy.29) | data formatting | bytes 2097152 | tf_op jit(solution)/shard_map/reshape | solution.py:279
  88.6 1.1 copy.35
  89.7 1.9 %reshape.95 = bf16[2,16,16384]{2,1,0:T(8,128)(2,1)S(1)} reshape(bf16[8192,64]{1,0:T(8,128)(2,1)S(1)} %copy.35) | data formatting | bytes 2097152 | tf_op jit(solution)/shard_map/reshape | solution.py:293
  91.6 1.0 add_convert_fusion.3
  93.4 1.5 %collective-permute-start.11 = (bf16[2,16,128]{2,1,0:T(8,128)(2,1)S(1)}, bf16[2,16,128]{2,1,0:T(8,128)(2,1)S(1)}, u32[]{:S(2)}, u32[]{:S(2)}) collective-permute-start(bf16[2,16,128]{2,1,0:T(8,128)(2,1)S(1)} %get-tuple-element.20), channel_id=1, source_target_pairs={{0,8},{8,16},{16,24},{24,0},{1,9},{9,17},{17,25},{25,1},{2,10},{10... | collective-permute-start | bytes 24584 | tf_op jit(solution)/shard_map/ppermute | solution.py:26
  95.0 1.0 collective-permute-start.16
  95.9 2.0 %collective-permute-start.12 = (bf16[2,16,128]{2,1,0:T(8,128)(2,1)S(1)}, bf16[2,16,128]{2,1,0:T(8,128)(2,1)S(1)}, u32[]{:S(2)}, u32[]{:S(2)}) collective-permute-start(bf16[2,16,128]{2,1,0:T(8,128)(2,1)S(1)} %get-tuple-element.19), channel_id=1, source_target_pairs={{8,0},{16,8},{24,16},{0,24},{9,1},{17,9},{25,17},{1,25},{10,2},{18... | collective-permute-start | bytes 24584 | tf_op jit(solution)/shard_map/ppermute | solution.py:27
  98.3 1.3 collective-permute-done.12
  99.9 1.3 collective-permute-start.17
  102.1 1.4 fusion.100
  103.5 5.4 %collective-permute-start.14 = (bf16[1,18,16640]{2,1,0:T(8,128)(2,1)}, bf16[1,18,16640]{2,1,0:T(8,128)(2,1)}, u32[]{:S(2)}, u32[]{:S(2)}) collective-permute-start(bf16[1,18,16640]{2,1,0:T(8,128)(2,1)} %get-tuple-element.16), channel_id=1, source_target_pairs={{0,1},{1,2},{2,3},{4,5},{5,6},{6,7},{8,9},{9,10},{10,11},{12,13},{... | collective-permute-start | bytes 1797128 | tf_op jit(solution)/shard_map/ppermute | solution.py:126
  108.9 1.3 collective-permute-start.15
  110.8 9.2 %shard_map.96.refs_2_ = bf16[2,16,16384]{2,1,0:T(8,128)(2,1)} custom-call(bf16[2,18,16640]{2,1,0:T(8,128)(2,1)} %copy-done.3, f32[27,8,128]{2,1,0:T(8,128)} %broadcast_in_dim.36.refs_1_.refs_4_), custom_call_target="tpu_custom_call" | custom-call | tf_op jit(solution)/shard_map/pallas_call | solution.py:181
  120.1 2.7 %collective-permute-start.19 = (bf16[64,1024]{1,0:T(8,128)(2,1)S(1)}, bf16[64,1024]{1,0:T(8,128)(2,1)S(1)}, u32[]{:S(2)}, u32[]{:S(2)}) collective-permute-start(bf16[64,1024]{1,0:T(8,128)(2,1)S(1)} %add_convert_fusion.2), channel_id=1, source_target_pairs={{0,1},{1,0},{2,3},{3,2},{4,5},{5,4},{6,7},{7,6},{8,9},{9,8},{10,11... | collective-permute-start | bytes 393224 | tf_op jit(solution)/shard_map/ppermute | solution.py:107
  123.6 9.7 %collective-permute-done.19 = bf16[64,1024]{1,0:T(8,128)(2,1)S(1)} collective-permute-done((bf16[64,1024]{1,0:T(8,128)(2,1)S(1)}, bf16[64,1024]{1,0:T(8,128)(2,1)S(1)}, u32[]{:S(2)}, u32[]{:S(2)}) %collective-permute-start.19) | collective-permute-done | bytes 131104 | tf_op jit(solution)/shard_map/ppermute | solution.py:107
  133.4 1.6 %collective-permute-start.20 = (bf16[64,1024]{1,0:T(8,128)(2,1)S(1)}, bf16[64,1024]{1,0:T(8,128)(2,1)S(1)}, u32[]{:S(2)}, u32[]{:S(2)}) collective-permute-start(bf16[64,1024]{1,0:T(8,128)(2,1)S(1)} %add_convert_fusion.1), channel_id=1, source_target_pairs={{0,2},{1,3},{2,0},{3,1},{4,6},{5,7},{6,4},{7,5},{8,10},{9,11},{10,... | collective-permute-start | bytes 393224 | tf_op jit(solution)/shard_map/ppermute | solution.py:107
  135.6 1.1 copy.38
  136.7 2.5 %reshape.96.refs_3_ = bf16[2,16,16384]{2,1,0:T(8,128)(2,1)} reshape(bf16[32,256,64]{2,1,0:T(8,128)(2,1)S(1)} %copy.38) | data formatting | bytes 2097152 | tf_op jit(solution)/shard_map/reshape | solution.py:311
  139.2 1.3 collective-permute-done.20
  141.6 6.8 %shard_map.97 = bf16[2,16,16384]{2,1,0:T(8,128)(2,1)} custom-call(bf16[1,18,16640]{2,1,0:T(8,128)(2,1)} %collective-permute-done.14.refs_0_, bf16[1,18,16640]{2,1,0:T(8,128)(2,1)} %collective-permute-done.15.refs_1_, bf16[2,16,16384]{2,1,0:T(8,128)(2,1)} %shard_map.96.refs_2_, bf16[2,16,16384]{2,1,0:T(8,128)(2,1)} %reshape.96.refs_3_, ...), custom_call_target="tpu_custom_call" | custom-call | tf_op jit(solution)/shard_map/pallas_call | solution.py:181
  (110 shorter events, 16.7 us)
Async XLA Ops:
  0.6 54.1 %copy-start = (bf16[64,256]{1,0:T(8,128)(2,1)S(1)}, bf16[64,256]{1,0:T(8,128)(2,1)}, u32[]{:S(2)}) copy-start(bf16[64,256]{1,0:T(8,128)(2,1)} %param.9) | copy-start | bytes 98308
  4.8 8.6 %copy-start.5 = (bf16[2,16,16384]{2,1,0:T(8,128)(2,1)S(1)}, bf16[2,16,16384]{2,1,0:T(8,128)(2,1)}, u32[]{:S(2)}) copy-start(bf16[2,16,16384]{2,1,0:T(8,128)(2,1)} %param.7) | copy-start | bytes 3145732
  5.0 18.5 %collective-permute-start = (f32[16,32,128]{2,0,1:T(8,128)S(1)}, f32[16,32,128]{2,0,1:T(8,128)}, u32[]{:S(2)}, u32[]{:S(2)}) collective-permute-start(f32[16,32,128]{2,0,1:T(8,128)S(1)} %fusion.16), channel_id=1, source_target_pairs={{0,16},{8,24},{16,0},{24,8},{1,17},{9,25},{17,1},{25,9},{2,18},{10... | collective-permute-start | bytes 786440 | tf_op jit(solution)/shard_map/ppermute | solution.py:90
  8.7 4.7 %collective-permute-start.2 = (bf16[2,16,128]{2,1,0:T(8,128)(2,1)S(1)}, bf16[2,16,128]{2,1,0:T(8,128)(2,1)S(1)}, u32[]{:S(2)}, u32[]{:S(2)}) collective-permute-start(bf16[2,16,128]{2,1,0:T(8,128)(2,1)S(1)} %get-tuple-element.22), channel_id=1, source_target_pairs={{0,8},{8,16},{16,24},{24,0},{1,9},{9,17},{17,25},{25,1},{2,10},{10... | collective-permute-start | bytes 24584 | tf_op jit(solution)/shard_map/ppermute | solution.py:26
  10.2 3.7 %collective-permute-start.3 = (bf16[2,16,128]{2,1,0:T(8,128)(2,1)S(1)}, bf16[2,16,128]{2,1,0:T(8,128)(2,1)S(1)}, u32[]{:S(2)}, u32[]{:S(2)}) collective-permute-start(bf16[2,16,128]{2,1,0:T(8,128)(2,1)S(1)} %get-tuple-element.21), channel_id=1, source_target_pairs={{8,0},{16,8},{24,16},{0,24},{9,1},{17,9},{25,17},{1,25},{10,2},{18... | collective-permute-start | bytes 24584 | tf_op jit(solution)/shard_map/ppermute | solution.py:27
  14.1 1.4 collective-permute-start.4
  16.3 8.3 %copy-start.2 = (bf16[2,18,16640]{2,1,0:T(8,128)(2,1)}, bf16[2,18,16640]{2,1,0:T(8,128)(2,1)S(1)}, u32[]{:S(2)}) copy-start(bf16[2,18,16640]{2,1,0:T(8,128)(2,1)S(1)} %pad_maximum_fusion.refs_0_) | copy-start | bytes 3594244
  16.4 10.5 %copy-start.7 = (bf16[2,16,16384]{2,1,0:T(8,128)(2,1)S(1)}, bf16[2,16,16384]{2,1,0:T(8,128)(2,1)}, u32[]{:S(2)}) copy-start(bf16[2,16,16384]{2,1,0:T(8,128)(2,1)} %param.13) | copy-start | bytes 3145732
  17.6 25.6 %collective-permute-start.5 = (bf16[1,18,16640]{2,1,0:T(8,128)(2,1)}, bf16[1,18,16640]{2,1,0:T(8,128)(2,1)}, u32[]{:S(2)}, u32[]{:S(2)}) collective-permute-start(bf16[1,18,16640]{2,1,0:T(8,128)(2,1)} %get-tuple-element.18), channel_id=1, source_target_pairs={{0,1},{1,2},{2,3},{4,5},{5,6},{6,7},{8,9},{9,10},{10,11},{12,13},{... | collective-permute-start | bytes 1797128 | tf_op jit(solution)/shard_map/ppermute | solution.py:126
  22.0 21.8 %collective-permute-start.6 = (bf16[1,18,16640]{2,1,0:T(8,128)(2,1)}, bf16[1,18,16640]{2,1,0:T(8,128)(2,1)}, u32[]{:S(2)}, u32[]{:S(2)}) collective-permute-start(bf16[1,18,16640]{2,1,0:T(8,128)(2,1)} %get-tuple-element.17), channel_id=1, source_target_pairs={{1,0},{2,1},{3,2},{5,4},{6,5},{7,6},{9,8},{10,9},{11,10},{13,12},{... | collective-permute-start | bytes 1797128 | tf_op jit(solution)/shard_map/ppermute | solution.py:127
  24.6 2.2 %copy-start.11 = (f32[16,32,128]{2,0,1:T(8,128)}, f32[16,32,128]{2,0,1:T(8,128)S(1)}, u32[]{:S(2)}) copy-start(f32[16,32,128]{2,0,1:T(8,128)S(1)} %fusion.18) | copy-start | bytes 786436
  25.4 16.8 %collective-permute-start.1 = (f32[8,32,128]{2,0,1:T(8,128)}, f32[8,32,128]{2,0,1:T(8,128)}, u32[]{:S(2)}, u32[]{:S(2)}) collective-permute-start(f32[8,32,128]{2,0,1:T(8,128)} %constant_dynamic-slice_fusion.1), channel_id=1, source_target_pairs={{0,8},{8,0},{16,24},{24,16},{1,9},{9,1},{17,25},{25,17},{2,10},{10... | collective-permute-start | bytes 393224 | tf_op jit(solution)/shard_map/ppermute | solution.py:90
  29.2 1.6 %copy-start.6 = (bf16[32,64,64]{2,1,0:T(8,128)(2,1)S(1)}, bf16[32,64,64]{2,1,0:T(8,128)(2,1)}, u32[]{:S(2)}) copy-start(bf16[32,64,64]{2,1,0:T(8,128)(2,1)} %param.12) | copy-start | bytes 786436
  29.2 1.8 %copy-start.14 = (bf16[27,64]{1,0:T(8,128)(2,1)S(1)}, bf16[27,64]{1,0:T(8,128)(2,1)}, u32[]{:S(2)}) copy-start(bf16[27,64]{1,0:T(8,128)(2,1)} %param.8) | copy-start | bytes 10372
  31.1 11.1 %copy-start.12 = (f32[16,32,128]{2,0,1:T(8,128)S(1)}, f32[16,32,128]{2,0,1:T(8,128)}, u32[]{:S(2)}) copy-start(f32[16,32,128]{2,0,1:T(8,128)} %copy-done.11) | copy-start | bytes 786436
  50.2 9.1 %collective-permute-start.7 = (bf16[8,32,128]{2,1,0:T(8,128)(2,1)S(1)}, bf16[8,32,128]{2,1,0:T(8,128)(2,1)S(1)}, u32[]{:S(2)}, u32[]{:S(2)}) collective-permute-start(bf16[8,32,128]{2,1,0:T(8,128)(2,1)S(1)} %convolution_convert_fusion.2), channel_id=1, source_target_pairs={{0,8},{8,0},{16,24},{24,16},{1,9},{9,1},{17,25},{25,17},{2,10},{10... | collective-permute-start | bytes 196616 | tf_op jit(solution)/shard_map/ppermute | solution.py:68
  54.7 1.2 copy-start.15
  56.0 3.3 %copy-start.4 = (f32[8192,256]{1,0:T(8,128)}, f32[8192,256]{1,0:T(8,128)S(1)}, u32[]{:S(2)}) copy-start(f32[8192,256]{1,0:T(8,128)S(1)} %fusion.106) | copy-start | bytes 25165828
  59.3 5.8 %copy-start.8 = (bf16[32,256,64]{1,2,0:T(8,128)(2,1)S(1)}, bf16[32,256,64]{1,2,0:T(8,128)(2,1)}, u32[]{:S(2)}) copy-start(bf16[32,256,64]{1,2,0:T(8,128)(2,1)} %copy.30) | copy-start | bytes 3145732
  59.3 5.0 %collective-permute-start.8 = (bf16[16,32,128]{2,1,0:T(8,128)(2,1)S(1)}, bf16[16,32,128]{2,1,0:T(8,128)(2,1)S(1)}, u32[]{:S(2)}, u32[]{:S(2)}) collective-permute-start(bf16[16,32,128]{2,1,0:T(8,128)(2,1)S(1)} %pad_maximum_fusion.3), channel_id=1, source_target_pairs={{0,16},{8,24},{16,0},{24,8},{1,17},{9,25},{17,1},{25,9},{2,18},{10... | collective-permute-start | bytes 393224 | tf_op jit(solution)/shard_map/ppermute | solution.py:68
  69.3 6.4 %collective-permute-start.9 = (f32[16,32,128]{2,0,1:T(8,128)S(1)}, f32[16,32,128]{2,0,1:T(8,128)S(1)}, u32[]{:S(2)}, u32[]{:S(2)}) collective-permute-start(f32[16,32,128]{2,0,1:T(8,128)S(1)} %fusion.13), channel_id=1, source_target_pairs={{0,16},{8,24},{16,0},{24,8},{1,17},{9,25},{17,1},{25,9},{2,18},{10... | collective-permute-start | bytes 786440 | tf_op jit(solution)/shard_map/ppermute | solution.py:90
  75.9 1.3 copy-start.13
  76.6 15.0 %collective-permute-start.10 = (f32[8,32,128]{2,0,1:T(8,128)}, f32[8,32,128]{2,0,1:T(8,128)}, u32[]{:S(2)}, u32[]{:S(2)}) collective-permute-start(f32[8,32,128]{2,0,1:T(8,128)} %constant_dynamic-slice_fusion), channel_id=1, source_target_pairs={{0,8},{8,0},{16,24},{24,16},{1,9},{9,1},{17,25},{25,17},{2,10},{10... | collective-permute-start | bytes 393224 | tf_op jit(solution)/shard_map/ppermute | solution.py:90
  77.2 7.9 %copy-start.9 = (bf16[32,256,64]{1,2,0:T(8,128)(2,1)S(1)}, bf16[32,256,64]{1,2,0:T(8,128)(2,1)}, u32[]{:S(2)}) copy-start(bf16[32,256,64]{1,2,0:T(8,128)(2,1)} %get-tuple-element.14) | copy-start | bytes 3145732
  86.1 2.5 %copy-start.10 = (bf16[8192,64]{0,1:T(8,128)(2,1)S(1)}, bf16[8192,64]{0,1:T(8,128)(2,1)}, u32[]{:S(2)}) copy-start(bf16[8192,64]{0,1:T(8,128)(2,1)} %convolution_convert_fusion) | copy-start | bytes 3145732
  93.4 4.8 %collective-permute-start.11 = (bf16[2,16,128]{2,1,0:T(8,128)(2,1)S(1)}, bf16[2,16,128]{2,1,0:T(8,128)(2,1)S(1)}, u32[]{:S(2)}, u32[]{:S(2)}) collective-permute-start(bf16[2,16,128]{2,1,0:T(8,128)(2,1)S(1)} %get-tuple-element.20), channel_id=1, source_target_pairs={{0,8},{8,16},{16,24},{24,0},{1,9},{9,17},{17,25},{25,1},{2,10},{10... | collective-permute-start | bytes 24584 | tf_op jit(solution)/shard_map/ppermute | solution.py:26
  95.0 4.9 %collective-permute-start.16 = (bf16[8,32,128]{2,1,0:T(8,128)(2,1)S(1)}, bf16[8,32,128]{2,1,0:T(8,128)(2,1)S(1)}, u32[]{:S(2)}, u32[]{:S(2)}) collective-permute-start(bf16[8,32,128]{2,1,0:T(8,128)(2,1)S(1)} %convolution_convert_fusion.1), channel_id=1, source_target_pairs={{0,8},{8,0},{16,24},{24,16},{1,9},{9,1},{17,25},{25,17},{2,10},{10... | collective-permute-start | bytes 196616 | tf_op jit(solution)/shard_map/ppermute | solution.py:68
  95.9 3.7 %collective-permute-start.12 = (bf16[2,16,128]{2,1,0:T(8,128)(2,1)S(1)}, bf16[2,16,128]{2,1,0:T(8,128)(2,1)S(1)}, u32[]{:S(2)}, u32[]{:S(2)}) collective-permute-start(bf16[2,16,128]{2,1,0:T(8,128)(2,1)S(1)} %get-tuple-element.19), channel_id=1, source_target_pairs={{8,0},{16,8},{24,16},{0,24},{9,1},{17,9},{25,17},{1,25},{10,2},{18... | collective-permute-start | bytes 24584 | tf_op jit(solution)/shard_map/ppermute | solution.py:27
  98.2 21.9 %collective-permute-start.18 = (bf16[64,1024]{1,0:T(8,128)(2,1)S(1)}, bf16[64,1024]{1,0:T(8,128)(2,1)S(1)}, u32[]{:S(2)}, u32[]{:S(2)}) collective-permute-start(bf16[64,1024]{1,0:T(8,128)(2,1)S(1)} %convert_element_type.143), channel_id=1, source_target_pairs={{0,4},{4,0},{1,5},{5,1},{2,6},{6,2},{3,7},{7,3},{8,12},{12,8},{9,1... | collective-permute-start | bytes 393224 | tf_op jit(solution)/shard_map/ppermute | solution.py:107
  99.8 1.5 collective-permute-start.13
  99.9 22.9 %collective-permute-start.17 = (bf16[16,32,128]{2,1,0:T(8,128)(2,1)S(1)}, bf16[16,32,128]{2,1,0:T(8,128)(2,1)S(1)}, u32[]{:S(2)}, u32[]{:S(2)}) collective-permute-start(bf16[16,32,128]{2,1,0:T(8,128)(2,1)S(1)} %pad_maximum_fusion.4), channel_id=1, source_target_pairs={{0,16},{8,24},{16,0},{24,8},{1,17},{9,25},{17,1},{25,9},{2,18},{10... | collective-permute-start | bytes 393224 | tf_op jit(solution)/shard_map/ppermute | solution.py:68
  102.1 8.7 %copy-start.3 = (bf16[2,18,16640]{2,1,0:T(8,128)(2,1)}, bf16[2,18,16640]{2,1,0:T(8,128)(2,1)S(1)}, u32[]{:S(2)}) copy-start(bf16[2,18,16640]{2,1,0:T(8,128)(2,1)S(1)} %pad_maximum_fusion.1.refs_0_) | copy-start | bytes 3594244
  103.5 38.1 %collective-permute-start.14 = (bf16[1,18,16640]{2,1,0:T(8,128)(2,1)}, bf16[1,18,16640]{2,1,0:T(8,128)(2,1)}, u32[]{:S(2)}, u32[]{:S(2)}) collective-permute-start(bf16[1,18,16640]{2,1,0:T(8,128)(2,1)} %get-tuple-element.16), channel_id=1, source_target_pairs={{0,1},{1,2},{2,3},{4,5},{5,6},{6,7},{8,9},{9,10},{10,11},{12,13},{... | collective-permute-start | bytes 1797128 | tf_op jit(solution)/shard_map/ppermute | solution.py:126
  108.9 32.7 %collective-permute-start.15 = (bf16[1,18,16640]{2,1,0:T(8,128)(2,1)}, bf16[1,18,16640]{2,1,0:T(8,128)(2,1)}, u32[]{:S(2)}, u32[]{:S(2)}) collective-permute-start(bf16[1,18,16640]{2,1,0:T(8,128)(2,1)} %get-tuple-element.15), channel_id=1, source_target_pairs={{1,0},{2,1},{3,2},{5,4},{6,5},{7,6},{9,8},{10,9},{11,10},{13,12},{... | collective-permute-start | bytes 1797128 | tf_op jit(solution)/shard_map/ppermute | solution.py:127
  120.1 13.2 %collective-permute-start.19 = (bf16[64,1024]{1,0:T(8,128)(2,1)S(1)}, bf16[64,1024]{1,0:T(8,128)(2,1)S(1)}, u32[]{:S(2)}, u32[]{:S(2)}) collective-permute-start(bf16[64,1024]{1,0:T(8,128)(2,1)S(1)} %add_convert_fusion.2), channel_id=1, source_target_pairs={{0,1},{1,0},{2,3},{3,2},{4,5},{5,4},{6,7},{7,6},{8,9},{9,8},{10,11... | collective-permute-start | bytes 393224 | tf_op jit(solution)/shard_map/ppermute | solution.py:107
  133.4 7.2 %collective-permute-start.20 = (bf16[64,1024]{1,0:T(8,128)(2,1)S(1)}, bf16[64,1024]{1,0:T(8,128)(2,1)S(1)}, u32[]{:S(2)}, u32[]{:S(2)}) collective-permute-start(bf16[64,1024]{1,0:T(8,128)(2,1)S(1)} %add_convert_fusion.1), channel_id=1, source_target_pairs={{0,2},{1,3},{2,0},{3,1},{4,6},{5,7},{6,4},{7,5},{8,10},{9,11},{10,... | collective-permute-start | bytes 393224 | tf_op jit(solution)/shard_map/ppermute | solution.py:107
  140.6 7.8 %copy-start.1 = (bf16[64,256]{1,0:T(8,128)(2,1)S(1)}, bf16[64,256]{1,0:T(8,128)(2,1)}, u32[]{:S(2)}) copy-start(bf16[64,256]{1,0:T(8,128)(2,1)} %param.9) | copy-start | bytes 98308

commit v23 on v21

--- a/solution.py
+++ b/solution.py
@@ -276,7 +276,7 @@
     local_branch = local_branch.reshape(row_count, x_cells, channels)
     spectral = share_inverse(mixed_modes, cos_scaled, sin_scaled, channels)
     result, slopes = gelu_parts(local_branch + spectral)
-    output = result.astype(jnp.bfloat16).reshape(planes, y_cells, merged)
+    out_points = result.astype(jnp.bfloat16)
     grad_pre = (
         lax.optimization_barrier(cotangent.reshape(row_count, x_cells, channels)).astype(jnp.float32)
         * slopes
@@ -301,6 +301,9 @@
     spectral_grad = share_inverse(dmode, cos_order, sin_order, channels)
     grad_spec = sum_gradients(local_grads)
     padded_grad = spatial_rims(grad_act, channels)
+    out_points, inner_grad = lax.optimization_barrier((out_points, padded_grad[0]))
+    padded_grad = (inner_grad,) + padded_grad[1:]
+    output = out_points.reshape(planes, y_cells, merged)
     grad_features = depthwise(
         padded_grad,
         depth_weight,

time: 150 us -> 153 us (1.020)
  local copies, waits for them, and re-layouts: 29.9 us -> 33.3 us
    optimization_barrier x0 -> x1, local copies, waits for them, and re-layouts: none -> 1.78 us  [per_device(): lax.optimization_barrier((out_points, padded_grad[0]))]
  transfers between devices with their start and end apart: 21 -> 21, of which waited for: 10 -> 10; matrix products, arithmetic and copies ran while one was open for 30% -> 31% of each run, Pallas kernels for 13% -> 13%
where the time goes in v23:
time: 153 us; the launch traced here: 152 us
  starting transfers between devices  35.3 us (23%)
  local copies, waits for them, and re-layouts  33.3 us (22%)
  Pallas kernels  33 us (22%)
  waiting for transfers between devices  22.2 us (15%)
  matrix products  19.9 us (13%)
  other arithmetic  7.28 us (5%)
    pallas_call x4, Pallas kernels, stencil_call(): pl.pallas_call(kernel, out_shape=jax.ShapeDtypeStruct((len(plan), y_cells...  33 us
    ppermute x2, starting transfers between devices, spatial_rims(): below = lax.ppermute(inner[-1:], 'gz', up)  9.84 us
    ppermute x3, waiting for transfers between devices, butterfly_sum(): lax.ppermute(value, axis, [(i, i ^ step) for i in range(size)])  9.69 us
    dot_general x1, matrix products, per_device(): jnp.dot(grad_hidden, expand_weight.T, preferred_element_type=jnp.float32)  8.16 us
    ppermute x4, starting transfers between devices, ring_reduce_scatter(): lax.ppermute(send, axis, [(i, i ^ step) for i in range(size)])  6.64 us
    ppermute x4, starting transfers between devices, ring_gather(): lax.ppermute(block, axis, [(i, i ^ step) for i in range(size)])  5.36 us
    ppermute x3, starting transfers between devices, butterfly_sum(): lax.ppermute(value, axis, [(i, i ^ step) for i in range(size)])  4.53 us
    ppermute x4, waiting for transfers between devices, ring_reduce_scatter(): lax.ppermute(send, axis, [(i, i ^ step) for i in range(size)])  3.69 us
  transfers between devices with their start and end apart: 21, of which 10 were waited for; matrix products, arithmetic and copies ran while one was open for 31% of the time, Pallas kernels for 13%

profile of v23, /device:TPU:0, one launch (start us, length us, event | category | flops | bytes accessed | tf_op | source)
XLA Modules:
  0.0 152.1 jit_solution(9142094669746971742)
XLA Ops:
  0.7 3.0 %reshape.89 = bf16[32,256,64]{2,1,0:T(8,128)(2,1)S(1)} reshape(bf16[2,16,16384]{2,1,0:T(8,128)(2,1)} %param.7) | data formatting | bytes 2097152 | tf_op jit(solution)/shard_map/reshape | solution.py:261
  5.0 3.0 %collective-permute-start = (f32[16,32,128]{2,0,1:T(8,128)S(1)}, f32[16,32,128]{2,0,1:T(8,128)}, u32[]{:S(2)}, u32[]{:S(2)}) collective-permute-start(f32[16,32,128]{2,0,1:T(8,128)S(1)} %fusion.16), channel_id=1, source_target_pairs={{0,16},{8,24},{16,0},{24,8},{1,17},{9,25},{17,1},{25,9},{2,18},{10... | collective-permute-start | bytes 786440 | tf_op jit(solution)/shard_map/ppermute | solution.py:90
  8.7 1.5 collective-permute-start.2
  10.2 1.4 collective-permute-start.3
  11.7 1.7 %collective-permute-done.2 = bf16[2,16,128]{2,1,0:T(8,128)(2,1)S(1)} collective-permute-done((bf16[2,16,128]{2,1,0:T(8,128)(2,1)S(1)}, bf16[2,16,128]{2,1,0:T(8,128)(2,1)S(1)}, u32[]{:S(2)}, u32[]{:S(2)}) %collective-permute-start.2) | collective-permute-done | bytes 8224 | tf_op jit(solution)/shard_map/ppermute | solution.py:26
  14.3 1.2 collective-permute-done.4
  16.4 1.3 fusion.101
  17.6 4.4 %collective-permute-start.5 = (bf16[1,18,16640]{2,1,0:T(8,128)(2,1)}, bf16[1,18,16640]{2,1,0:T(8,128)(2,1)}, u32[]{:S(2)}, u32[]{:S(2)}) collective-permute-start(bf16[1,18,16640]{2,1,0:T(8,128)(2,1)} %get-tuple-element.22), channel_id=1, source_target_pairs={{0,1},{1,2},{2,3},{4,5},{5,6},{6,7},{8,9},{9,10},{10,11},{12,13},{... | collective-permute-start | bytes 1797128 | tf_op jit(solution)/shard_map/ppermute | solution.py:126
  22.0 1.3 collective-permute-start.6
  23.3 1.1 fusion.18
  25.2 1.5 collective-permute-start.1
  26.6 2.5 %reshape.92 = bf16[32,256,64]{2,1,0:T(8,128)(2,1)S(1)} reshape(bf16[2,16,16384]{2,1,0:T(8,128)(2,1)S(1)} %copy-done.7) | data formatting | bytes 2097152 | tf_op jit(solution)/shard_map/reshape | solution.py:281
  29.1 1.6 %copy.29 = bf16[32,256,64]{1,2,0:T(8,128)(2,1)} copy(bf16[32,256,64]{2,1,0:T(8,128)(2,1)S(1)} %reshape.92) | data formatting | bytes 2097152 | tf_op jit(solution)/shard_map/optimization_barrier | solution.py:281
  31.0 1.1 fusion.20
  32.8 9.6 %shard_map.94.refs_2_ = f32[2,16,16384]{2,1,0:T(8,128)} custom-call(bf16[2,18,16640]{2,1,0:T(8,128)(2,1)} %copy-done.2, f32[27,8,128]{2,1,0:T(8,128)} %broadcast_in_dim.18.refs_1_.refs_3_), custom_call_target="tpu_custom_call" | custom-call | tf_op jit(solution)/shard_map/pallas_call | solution.py:181
  43.8 6.7 %shard_map.95 = bf16[2,16,16384]{2,1,0:T(8,128)(2,1)} custom-call(bf16[1,18,16640]{2,1,0:T(8,128)(2,1)} %collective-permute-done.5.refs_0_, bf16[1,18,16640]{2,1,0:T(8,128)(2,1)} %collective-permute-done.6.refs_1_, f32[2,16,16384]{2,1,0:T(8,128)} %shard_map.94.refs_2_, f32[27,8,128]{2,1,0:T(8,128)} %broadcast_in_dim.18.refs_1_.refs_3_), custom_call_target="tpu_custom_call" | custom-call | tf_op jit(solution)/shard_map/pallas_call | solution.py:181
  50.6 1.5 collective-permute-start.7
  52.0 3.0 %reshape.90 = bf16[8192,64]{1,0:T(8,128)(2,1)S(1)} reshape(bf16[2,16,16384]{2,1,0:T(8,128)(2,1)} %shard_map.95) | data formatting | bytes 2097152 | tf_op jit(solution)/shard_map/reshape | solution.py:270
  55.1 1.2 fusion.106
  56.3 2.8 %fusion.5 = f32[8192,64]{0,1:T(8,128)S(1)} fusion(bf16[256,64]{0,1:T(8,128)(2,1)S(1)} %copy-done.14, f32[8192,256]{1,0:T(8,128)S(1)} %fusion.106), kind=kOutput, calls=%fused_computation.10 | convolution fusion | flops 278921216 | bytes 10518528 | tf_op jit(solution)/shard_map/dot_general | solution.py:273
  59.6 1.6 %collective-permute-start.8 = (bf16[16,32,128]{2,1,0:T(8,128)(2,1)S(1)}, bf16[16,32,128]{2,1,0:T(8,128)(2,1)S(1)}, u32[]{:S(2)}, u32[]{:S(2)}) collective-permute-start(bf16[16,32,128]{2,1,0:T(8,128)(2,1)S(1)} %pad_maximum_fusion.3), channel_id=1, source_target_pairs={{0,16},{8,24},{16,0},{24,8},{1,17},{9,25},{17,1},{25,9},{2,18},{10... | collective-permute-start | bytes 393224 | tf_op jit(solution)/shard_map/ppermute | solution.py:68
  61.2 3.4 %collective-permute-done.8 = bf16[16,32,128]{2,1,0:T(8,128)(2,1)S(1)} collective-permute-done((bf16[16,32,128]{2,1,0:T(8,128)(2,1)S(1)}, bf16[16,32,128]{2,1,0:T(8,128)(2,1)S(1)}, u32[]{:S(2)}, u32[]{:S(2)}) %collective-permute-start.8) | collective-permute-done | bytes 131104 | tf_op jit(solution)/shard_map/ppermute | solution.py:68
  65.5 2.7 %fusion.11 = (bf16[32,256,64]{1,2,0:T(8,128)(2,1)S(1)}, bf16[32,256,64]{1,2,0:T(8,128)(2,1)}) fusion(bf16[32,256,64]{1,2,0:T(8,128)(2,1)S(1)} %copy-done.9, f32[256,32,64]{0,2,1:T(8,128)S(1)} %fusion.27, bf16[32,32,64]{2,1,0:T(8,128)(2,1)S(1)} %get-tuple-element.31, f32[32]{0:T(128)S(1)} %get-tuple-element.37, s32[32]{0:T(128)S(1)} %add.135, ...), kind=kOutput, calls=%fused_computation.17 | convolution fusion | flops 41566208 | bytes 7472384 | tf_op jit(solution)/shard_map/krc,xk->rxc/dot_general | solution.py:218
  69.6 1.6 %collective-permute-start.9 = (f32[16,32,128]{2,0,1:T(8,128)S(1)}, f32[16,32,128]{2,0,1:T(8,128)S(1)}, u32[]{:S(2)}, u32[]{:S(2)}) collective-permute-start(f32[16,32,128]{2,0,1:T(8,128)S(1)} %fusion.13), channel_id=1, source_target_pairs={{0,16},{8,24},{16,0},{24,8},{1,17},{9,25},{17,1},{25,9},{2,18},{10... | collective-permute-start | bytes 786440 | tf_op jit(solution)/shard_map/ppermute | solution.py:90
  71.4 1.0 copy.42
  72.4 3.7 %collective-permute-done.9 = f32[16,32,128]{2,0,1:T(8,128)S(1)} collective-permute-done((f32[16,32,128]{2,0,1:T(8,128)S(1)}, f32[16,32,128]{2,0,1:T(8,128)S(1)}, u32[]{:S(2)}, u32[]{:S(2)}) %collective-permute-start.9) | collective-permute-done | bytes 262176 | tf_op jit(solution)/shard_map/ppermute | solution.py:90
  77.5 8.2 %convolution_convert_fusion = bf16[8192,64]{0,1:T(8,128)(2,1)S(1)} fusion(bf16[64,256]{1,0:T(8,128)(2,1)S(1)} %copy-done, bf16[8192,64]{0,1:T(8,128)(2,1)} %bitcast.54, bf16[256,64]{0,1:T(8,128)(2,1)} %param.10, f32[8192,256]{1,0:T(8,128)} %copy-done.4), kind=kOutput, calls=%fused_computation.3 | convolution fusion | flops 558366720 | bytes 10551296 | tf_op jit(solution)/shard_map/dot_general | solution.py:290
  85.7 1.1 copy.34
  86.8 1.9 %reshape.94 = bf16[2,16,16384]{2,1,0:T(8,128)(2,1)S(1)} reshape(bf16[8192,64]{1,0:T(8,128)(2,1)S(1)} %copy.34) | data formatting | bytes 2097152 | tf_op jit(solution)/shard_map/reshape | solution.py:293
  88.7 1.0 add_convert_fusion.3
  90.5 1.5 %collective-permute-start.11 = (bf16[2,16,128]{2,1,0:T(8,128)(2,1)S(1)}, bf16[2,16,128]{2,1,0:T(8,128)(2,1)S(1)}, u32[]{:S(2)}, u32[]{:S(2)}) collective-permute-start(bf16[2,16,128]{2,1,0:T(8,128)(2,1)S(1)} %get-tuple-element.24), channel_id=1, source_target_pairs={{0,8},{8,16},{16,24},{24,0},{1,9},{9,17},{17,25},{25,1},{2,10},{10... | collective-permute-start | bytes 24584 | tf_op jit(solution)/shard_map/ppermute | solution.py:26
  92.0 1.2 collective-permute-start.16
  93.3 1.7 %collective-permute-start.12 = (bf16[2,16,128]{2,1,0:T(8,128)(2,1)S(1)}, bf16[2,16,128]{2,1,0:T(8,128)(2,1)S(1)}, u32[]{:S(2)}, u32[]{:S(2)}) collective-permute-start(bf16[2,16,128]{2,1,0:T(8,128)(2,1)S(1)} %get-tuple-element.23), channel_id=1, source_target_pairs={{8,0},{16,8},{24,16},{0,24},{9,1},{17,9},{25,17},{1,25},{10,2},{18... | collective-permute-start | bytes 24584 | tf_op jit(solution)/shard_map/ppermute | solution.py:27
  95.4 1.5 %collective-permute-done.12 = bf16[2,16,128]{2,1,0:T(8,128)(2,1)S(1)} collective-permute-done((bf16[2,16,128]{2,1,0:T(8,128)(2,1)S(1)}, bf16[2,16,128]{2,1,0:T(8,128)(2,1)S(1)}, u32[]{:S(2)}, u32[]{:S(2)}) %collective-permute-start.12) | collective-permute-done | bytes 8224 | tf_op jit(solution)/shard_map/ppermute | solution.py:27
  97.3 1.0 collective-permute-start.17
  99.5 1.3 fusion.100
  101.4 1.8 %copy.35 = bf16[32,256,64]{2,1,0:T(8,128)(2,1)} copy(bf16[32,256,64]{1,2,0:T(8,128)(2,1)S(1)} %copy-done.8) | data formatting | bytes 2097152 | tf_op jit(solution)/shard_map/optimization_barrier | solution.py:304
  103.2 3.7 %reshape.95 = bf16[2,16,16384]{2,1,0:T(8,128)(2,1)} reshape(bf16[32,256,64]{2,1,0:T(8,128)(2,1)} %copy.35) | data formatting | bytes 2097152 | tf_op jit(solution)/shard_map/reshape | solution.py:306
  106.9 5.4 %collective-permute-start.14 = (bf16[1,18,16640]{2,1,0:T(8,128)(2,1)}, bf16[1,18,16640]{2,1,0:T(8,128)(2,1)}, u32[]{:S(2)}, u32[]{:S(2)}) collective-permute-start(bf16[1,18,16640]{2,1,0:T(8,128)(2,1)} %get-tuple-element.20), channel_id=1, source_target_pairs={{0,1},{1,2},{2,3},{4,5},{5,6},{6,7},{8,9},{9,10},{10,11},{12,13},{... | collective-permute-start | bytes 1797128 | tf_op jit(solution)/shard_map/ppermute | solution.py:126
  112.3 1.3 collective-permute-start.15
  114.3 9.6 %shard_map.96.refs_2_ = f32[2,16,16384]{2,1,0:T(8,128)} custom-call(bf16[2,18,16640]{2,1,0:T(8,128)(2,1)} %copy-done.3, f32[27,8,128]{2,1,0:T(8,128)} %broadcast_in_dim.36.refs_1_.refs_4_), custom_call_target="tpu_custom_call" | custom-call | tf_op jit(solution)/shard_map/pallas_call | solution.py:181
  123.9 2.7 %collective-permute-start.19 = (bf16[64,1024]{1,0:T(8,128)(2,1)S(1)}, bf16[64,1024]{1,0:T(8,128)(2,1)S(1)}, u32[]{:S(2)}, u32[]{:S(2)}) collective-permute-start(bf16[64,1024]{1,0:T(8,128)(2,1)S(1)} %add_convert_fusion.2), channel_id=1, source_target_pairs={{0,1},{1,0},{2,3},{3,2},{4,5},{5,4},{6,7},{7,6},{8,9},{9,8},{10,11... | collective-permute-start | bytes 393224 | tf_op jit(solution)/shard_map/ppermute | solution.py:107
  128.3 8.5 %collective-permute-done.19 = bf16[64,1024]{1,0:T(8,128)(2,1)S(1)} collective-permute-done((bf16[64,1024]{1,0:T(8,128)(2,1)S(1)}, bf16[64,1024]{1,0:T(8,128)(2,1)S(1)}, u32[]{:S(2)}, u32[]{:S(2)}) %collective-permute-start.19) | collective-permute-done | bytes 131104 | tf_op jit(solution)/shard_map/ppermute | solution.py:107
  136.9 1.8 %collective-permute-start.20 = (bf16[64,1024]{1,0:T(8,128)(2,1)S(1)}, bf16[64,1024]{1,0:T(8,128)(2,1)S(1)}, u32[]{:S(2)}, u32[]{:S(2)}) collective-permute-start(bf16[64,1024]{1,0:T(8,128)(2,1)S(1)} %add_convert_fusion.1), channel_id=1, source_target_pairs={{0,2},{1,3},{2,0},{3,1},{4,6},{5,7},{6,4},{7,5},{8,10},{9,11},{10,... | collective-permute-start | bytes 393224 | tf_op jit(solution)/shard_map/ppermute | solution.py:107
  139.2 1.1 copy.38
  140.3 2.5 %reshape.96.refs_3_ = bf16[2,16,16384]{2,1,0:T(8,128)(2,1)} reshape(bf16[32,256,64]{2,1,0:T(8,128)(2,1)S(1)} %copy.38) | data formatting | bytes 2097152 | tf_op jit(solution)/shard_map/reshape | solution.py:314
  142.8 1.2 collective-permute-done.20
  145.0 7.1 %shard_map.97 = bf16[2,16,16384]{2,1,0:T(8,128)(2,1)} custom-call(bf16[1,18,16640]{2,1,0:T(8,128)(2,1)} %collective-permute-done.14.refs_0_, bf16[1,18,16640]{2,1,0:T(8,128)(2,1)} %collective-permute-done.15.refs_1_, f32[2,16,16384]{2,1,0:T(8,128)} %shard_map.96.refs_2_, bf16[2,16,16384]{2,1,0:T(8,128)(2,1)} %reshape.96.refs_3_, ...), custom_call_target="tpu_custom_call" | custom-call | tf_op jit(solution)/shard_map/pallas_call | solution.py:181
  (108 shorter events, 18.3 us)
Async XLA Ops:
  0.6 54.5 %copy-start = (bf16[64,256]{1,0:T(8,128)(2,1)S(1)}, bf16[64,256]{1,0:T(8,128)(2,1)}, u32[]{:S(2)}) copy-start(bf16[64,256]{1,0:T(8,128)(2,1)} %param.9) | copy-start | bytes 98308
  4.8 8.6 %copy-start.5 = (bf16[2,16,16384]{2,1,0:T(8,128)(2,1)S(1)}, bf16[2,16,16384]{2,1,0:T(8,128)(2,1)}, u32[]{:S(2)}) copy-start(bf16[2,16,16384]{2,1,0:T(8,128)(2,1)} %param.7) | copy-start | bytes 3145732
  5.0 18.3 %collective-permute-start = (f32[16,32,128]{2,0,1:T(8,128)S(1)}, f32[16,32,128]{2,0,1:T(8,128)}, u32[]{:S(2)}, u32[]{:S(2)}) collective-permute-start(f32[16,32,128]{2,0,1:T(8,128)S(1)} %fusion.16), channel_id=1, source_target_pairs={{0,16},{8,24},{16,0},{24,8},{1,17},{9,25},{17,1},{25,9},{2,18},{10... | collective-permute-start | bytes 786440 | tf_op jit(solution)/shard_map/ppermute | solution.py:90
  8.7 4.7 %collective-permute-start.2 = (bf16[2,16,128]{2,1,0:T(8,128)(2,1)S(1)}, bf16[2,16,128]{2,1,0:T(8,128)(2,1)S(1)}, u32[]{:S(2)}, u32[]{:S(2)}) collective-permute-start(bf16[2,16,128]{2,1,0:T(8,128)(2,1)S(1)} %get-tuple-element.26), channel_id=1, source_target_pairs={{0,8},{8,16},{16,24},{24,0},{1,9},{9,17},{17,25},{25,1},{2,10},{10... | collective-permute-start | bytes 24584 | tf_op jit(solution)/shard_map/ppermute | solution.py:26
  10.2 3.7 %collective-permute-start.3 = (bf16[2,16,128]{2,1,0:T(8,128)(2,1)S(1)}, bf16[2,16,128]{2,1,0:T(8,128)(2,1)S(1)}, u32[]{:S(2)}, u32[]{:S(2)}) collective-permute-start(bf16[2,16,128]{2,1,0:T(8,128)(2,1)S(1)} %get-tuple-element.25), channel_id=1, source_target_pairs={{8,0},{16,8},{24,16},{0,24},{9,1},{17,9},{25,17},{1,25},{10,2},{18... | collective-permute-start | bytes 24584 | tf_op jit(solution)/shard_map/ppermute | solution.py:27
  14.1 1.4 collective-permute-start.4
  16.3 8.1 %copy-start.2 = (bf16[2,18,16640]{2,1,0:T(8,128)(2,1)}, bf16[2,18,16640]{2,1,0:T(8,128)(2,1)S(1)}, u32[]{:S(2)}) copy-start(bf16[2,18,16640]{2,1,0:T(8,128)(2,1)S(1)} %pad_maximum_fusion.refs_0_) | copy-start | bytes 3594244
  16.4 10.3 %copy-start.7 = (bf16[2,16,16384]{2,1,0:T(8,128)(2,1)S(1)}, bf16[2,16,16384]{2,1,0:T(8,128)(2,1)}, u32[]{:S(2)}) copy-start(bf16[2,16,16384]{2,1,0:T(8,128)(2,1)} %param.13) | copy-start | bytes 3145732
  17.6 25.9 %collective-permute-start.5 = (bf16[1,18,16640]{2,1,0:T(8,128)(2,1)}, bf16[1,18,16640]{2,1,0:T(8,128)(2,1)}, u32[]{:S(2)}, u32[]{:S(2)}) collective-permute-start(bf16[1,18,16640]{2,1,0:T(8,128)(2,1)} %get-tuple-element.22), channel_id=1, source_target_pairs={{0,1},{1,2},{2,3},{4,5},{5,6},{6,7},{8,9},{9,10},{10,11},{12,13},{... | collective-permute-start | bytes 1797128 | tf_op jit(solution)/shard_map/ppermute | solution.py:126
  22.0 21.8 %collective-permute-start.6 = (bf16[1,18,16640]{2,1,0:T(8,128)(2,1)}, bf16[1,18,16640]{2,1,0:T(8,128)(2,1)}, u32[]{:S(2)}, u32[]{:S(2)}) collective-permute-start(bf16[1,18,16640]{2,1,0:T(8,128)(2,1)} %get-tuple-element.21), channel_id=1, source_target_pairs={{1,0},{2,1},{3,2},{5,4},{6,5},{7,6},{9,8},{10,9},{11,10},{13,12},{... | collective-permute-start | bytes 1797128 | tf_op jit(solution)/shard_map/ppermute | solution.py:127
  24.4 2.2 %copy-start.10 = (f32[16,32,128]{2,0,1:T(8,128)}, f32[16,32,128]{2,0,1:T(8,128)S(1)}, u32[]{:S(2)}) copy-start(f32[16,32,128]{2,0,1:T(8,128)S(1)} %fusion.18) | copy-start | bytes 786436
  25.2 17.2 %collective-permute-start.1 = (f32[8,32,128]{2,0,1:T(8,128)}, f32[8,32,128]{2,0,1:T(8,128)}, u32[]{:S(2)}, u32[]{:S(2)}) collective-permute-start(f32[8,32,128]{2,0,1:T(8,128)} %constant_dynamic-slice_fusion.1), channel_id=1, source_target_pairs={{0,8},{8,0},{16,24},{24,16},{1,9},{9,1},{17,25},{25,17},{2,10},{10... | collective-permute-start | bytes 393224 | tf_op jit(solution)/shard_map/ppermute | solution.py:90
  29.1 1.6 %copy-start.6 = (bf16[32,64,64]{2,1,0:T(8,128)(2,1)S(1)}, bf16[32,64,64]{2,1,0:T(8,128)(2,1)}, u32[]{:S(2)}) copy-start(bf16[32,64,64]{2,1,0:T(8,128)(2,1)} %param.12) | copy-start | bytes 786436
  29.1 1.8 %copy-start.13 = (bf16[27,64]{1,0:T(8,128)(2,1)S(1)}, bf16[27,64]{1,0:T(8,128)(2,1)}, u32[]{:S(2)}) copy-start(bf16[27,64]{1,0:T(8,128)(2,1)} %param.8) | copy-start | bytes 10372
  32.2 10.2 %copy-start.11 = (f32[16,32,128]{2,0,1:T(8,128)S(1)}, f32[16,32,128]{2,0,1:T(8,128)}, u32[]{:S(2)}) copy-start(f32[16,32,128]{2,0,1:T(8,128)} %copy-done.10) | copy-start | bytes 786436
  50.6 9.1 %collective-permute-start.7 = (bf16[8,32,128]{2,1,0:T(8,128)(2,1)S(1)}, bf16[8,32,128]{2,1,0:T(8,128)(2,1)S(1)}, u32[]{:S(2)}, u32[]{:S(2)}) collective-permute-start(bf16[8,32,128]{2,1,0:T(8,128)(2,1)S(1)} %convolution_convert_fusion.2), channel_id=1, source_target_pairs={{0,8},{8,0},{16,24},{24,16},{1,9},{9,1},{17,25},{25,17},{2,10},{10... | collective-permute-start | bytes 196616 | tf_op jit(solution)/shard_map/ppermute | solution.py:68
  55.1 1.2 copy-start.14
  56.3 3.3 %copy-start.4 = (f32[8192,256]{1,0:T(8,128)}, f32[8192,256]{1,0:T(8,128)S(1)}, u32[]{:S(2)}) copy-start(f32[8192,256]{1,0:T(8,128)S(1)} %fusion.106) | copy-start | bytes 25165828
  59.6 5.8 %copy-start.9 = (bf16[32,256,64]{1,2,0:T(8,128)(2,1)S(1)}, bf16[32,256,64]{1,2,0:T(8,128)(2,1)}, u32[]{:S(2)}) copy-start(bf16[32,256,64]{1,2,0:T(8,128)(2,1)} %copy.29) | copy-start | bytes 3145732
  59.6 5.0 %collective-permute-start.8 = (bf16[16,32,128]{2,1,0:T(8,128)(2,1)S(1)}, bf16[16,32,128]{2,1,0:T(8,128)(2,1)S(1)}, u32[]{:S(2)}, u32[]{:S(2)}) collective-permute-start(bf16[16,32,128]{2,1,0:T(8,128)(2,1)S(1)} %pad_maximum_fusion.3), channel_id=1, source_target_pairs={{0,16},{8,24},{16,0},{24,8},{1,17},{9,25},{17,1},{25,9},{2,18},{10... | collective-permute-start | bytes 393224 | tf_op jit(solution)/shard_map/ppermute | solution.py:68
  69.6 6.4 %collective-permute-start.9 = (f32[16,32,128]{2,0,1:T(8,128)S(1)}, f32[16,32,128]{2,0,1:T(8,128)S(1)}, u32[]{:S(2)}, u32[]{:S(2)}) collective-permute-start(f32[16,32,128]{2,0,1:T(8,128)S(1)} %fusion.13), channel_id=1, source_target_pairs={{0,16},{8,24},{16,0},{24,8},{1,17},{9,25},{17,1},{25,9},{2,18},{10... | collective-permute-start | bytes 786440 | tf_op jit(solution)/shard_map/ppermute | solution.py:90
  76.2 1.3 copy-start.12
  77.0 11.7 %collective-permute-start.10 = (f32[8,32,128]{2,0,1:T(8,128)}, f32[8,32,128]{2,0,1:T(8,128)}, u32[]{:S(2)}, u32[]{:S(2)}) collective-permute-start(f32[8,32,128]{2,0,1:T(8,128)} %constant_dynamic-slice_fusion), channel_id=1, source_target_pairs={{0,8},{8,0},{16,24},{24,16},{1,9},{9,1},{17,25},{25,17},{2,10},{10... | collective-permute-start | bytes 393224 | tf_op jit(solution)/shard_map/ppermute | solution.py:90
  90.5 4.8 %collective-permute-start.11 = (bf16[2,16,128]{2,1,0:T(8,128)(2,1)S(1)}, bf16[2,16,128]{2,1,0:T(8,128)(2,1)S(1)}, u32[]{:S(2)}, u32[]{:S(2)}) collective-permute-start(bf16[2,16,128]{2,1,0:T(8,128)(2,1)S(1)} %get-tuple-element.24), channel_id=1, source_target_pairs={{0,8},{8,16},{16,24},{24,0},{1,9},{9,17},{17,25},{25,1},{2,10},{10... | collective-permute-start | bytes 24584 | tf_op jit(solution)/shard_map/ppermute | solution.py:26
  92.0 5.2 %collective-permute-start.16 = (bf16[8,32,128]{2,1,0:T(8,128)(2,1)S(1)}, bf16[8,32,128]{2,1,0:T(8,128)(2,1)S(1)}, u32[]{:S(2)}, u32[]{:S(2)}) collective-permute-start(bf16[8,32,128]{2,1,0:T(8,128)(2,1)S(1)} %convolution_convert_fusion.1), channel_id=1, source_target_pairs={{0,8},{8,0},{16,24},{24,16},{1,9},{9,1},{17,25},{25,17},{2,10},{10... | collective-permute-start | bytes 196616 | tf_op jit(solution)/shard_map/ppermute | solution.py:68
  93.3 3.7 %collective-permute-start.12 = (bf16[2,16,128]{2,1,0:T(8,128)(2,1)S(1)}, bf16[2,16,128]{2,1,0:T(8,128)(2,1)S(1)}, u32[]{:S(2)}, u32[]{:S(2)}) collective-permute-start(bf16[2,16,128]{2,1,0:T(8,128)(2,1)S(1)} %get-tuple-element.23), channel_id=1, source_target_pairs={{8,0},{16,8},{24,16},{0,24},{9,1},{17,9},{25,17},{1,25},{10,2},{18... | collective-permute-start | bytes 24584 | tf_op jit(solution)/shard_map/ppermute | solution.py:27
  95.2 28.6 %collective-permute-start.18 = (bf16[64,1024]{1,0:T(8,128)(2,1)S(1)}, bf16[64,1024]{1,0:T(8,128)(2,1)S(1)}, u32[]{:S(2)}, u32[]{:S(2)}) collective-permute-start(bf16[64,1024]{1,0:T(8,128)(2,1)S(1)} %convert_element_type.143), channel_id=1, source_target_pairs={{0,4},{4,0},{1,5},{5,1},{2,6},{6,2},{3,7},{7,3},{8,12},{12,8},{9,1... | collective-permute-start | bytes 393224 | tf_op jit(solution)/shard_map/ppermute | solution.py:107
  97.2 1.4 collective-permute-start.13
  97.3 29.3 %collective-permute-start.17 = (bf16[16,32,128]{2,1,0:T(8,128)(2,1)S(1)}, bf16[16,32,128]{2,1,0:T(8,128)(2,1)}, u32[]{:S(2)}, u32[]{:S(2)}) collective-permute-start(bf16[16,32,128]{2,1,0:T(8,128)(2,1)S(1)} %pad_maximum_fusion.4), channel_id=1, source_target_pairs={{0,16},{8,24},{16,0},{24,8},{1,17},{9,25},{17,1},{25,9},{2,18},{10... | collective-permute-start | bytes 393224 | tf_op jit(solution)/shard_map/ppermute | solution.py:68
  99.4 3.8 %copy-start.3 = (bf16[2,18,16640]{2,1,0:T(8,128)(2,1)}, bf16[2,18,16640]{2,1,0:T(8,128)(2,1)S(1)}, u32[]{:S(2)}) copy-start(bf16[2,18,16640]{2,1,0:T(8,128)(2,1)S(1)} %pad_maximum_fusion.1.refs_0_) | copy-start | bytes 3594244
  99.4 2.0 %copy-start.8 = (bf16[32,256,64]{1,2,0:T(8,128)(2,1)S(1)}, bf16[32,256,64]{1,2,0:T(8,128)(2,1)}, u32[]{:S(2)}) copy-start(bf16[32,256,64]{1,2,0:T(8,128)(2,1)} %get-tuple-element.13) | copy-start | bytes 3145732
  106.9 38.1 %collective-permute-start.14 = (bf16[1,18,16640]{2,1,0:T(8,128)(2,1)}, bf16[1,18,16640]{2,1,0:T(8,128)(2,1)}, u32[]{:S(2)}, u32[]{:S(2)}) collective-permute-start(bf16[1,18,16640]{2,1,0:T(8,128)(2,1)} %get-tuple-element.20), channel_id=1, source_target_pairs={{0,1},{1,2},{2,3},{4,5},{5,6},{6,7},{8,9},{9,10},{10,11},{12,13},{... | collective-permute-start | bytes 1797128 | tf_op jit(solution)/shard_map/ppermute | solution.py:126
  112.3 32.7 %collective-permute-start.15 = (bf16[1,18,16640]{2,1,0:T(8,128)(2,1)}, bf16[1,18,16640]{2,1,0:T(8,128)(2,1)}, u32[]{:S(2)}, u32[]{:S(2)}) collective-permute-start(bf16[1,18,16640]{2,1,0:T(8,128)(2,1)} %get-tuple-element.19), channel_id=1, source_target_pairs={{1,0},{2,1},{3,2},{5,4},{6,5},{7,6},{9,8},{10,9},{11,10},{13,12},{... | collective-permute-start | bytes 1797128 | tf_op jit(solution)/shard_map/ppermute | solution.py:127
  123.9 12.9 %collective-permute-start.19 = (bf16[64,1024]{1,0:T(8,128)(2,1)S(1)}, bf16[64,1024]{1,0:T(8,128)(2,1)S(1)}, u32[]{:S(2)}, u32[]{:S(2)}) collective-permute-start(bf16[64,1024]{1,0:T(8,128)(2,1)S(1)} %add_convert_fusion.2), channel_id=1, source_target_pairs={{0,1},{1,0},{2,3},{3,2},{4,5},{5,4},{6,7},{7,6},{8,9},{9,8},{10,11... | collective-permute-start | bytes 393224 | tf_op jit(solution)/shard_map/ppermute | solution.py:107
  136.9 7.2 %collective-permute-start.20 = (bf16[64,1024]{1,0:T(8,128)(2,1)S(1)}, bf16[64,1024]{1,0:T(8,128)(2,1)S(1)}, u32[]{:S(2)}, u32[]{:S(2)}) collective-permute-start(bf16[64,1024]{1,0:T(8,128)(2,1)S(1)} %add_convert_fusion.1), channel_id=1, source_target_pairs={{0,2},{1,3},{2,0},{3,1},{4,6},{5,7},{6,4},{7,5},{8,10},{9,11},{10,... | collective-permute-start | bytes 393224 | tf_op jit(solution)/shard_map/ppermute | solution.py:107
  144.0 8.1 %copy-start.1 = (bf16[64,256]{1,0:T(8,128)(2,1)S(1)}, bf16[64,256]{1,0:T(8,128)(2,1)}, u32[]{:S(2)}) copy-start(bf16[64,256]{1,0:T(8,128)(2,1)} %param.9) | copy-start | bytes 98308

commit v24 on v21

--- a/solution.py
+++ b/solution.py
@@ -172,8 +172,8 @@
 
 
 def stencil_call(plan, inputs, accs, gains, y_cells, lanes, channels, out_dtype):
-    chunk = min(1024, lanes)
-    rows = 8 if y_cells % 8 == 0 else y_cells
+    chunk = min(512, lanes)
+    rows = 16 if y_cells % 16 == 0 else y_cells
     kernel = functools.partial(
         stencil_kernel, chunk, 2 * channels, y_cells, rows, plan, len(inputs), len(accs)
     )
@@ -189,7 +189,7 @@
     planes = inner.shape[0]
     y_cells = inner.shape[1] - 2
     lanes = x_cells * channels
-    rows = 8 if y_cells % 8 == 0 else y_cells
+    rows = 16 if y_cells % 16 == 0 else y_cells
     if flipped:
         taps = taps[::-1]
     gains = jnp.tile(taps.astype(jnp.float32), (1, 128 // channels))

time: 150 us -> 152 us (1.013)
  Pallas kernels: 33 us -> 34.6 us
    pallas_call x4, Pallas kernels: 33 us -> 34.6 us  [stencil_call(): pl.pallas_call(kernel, out_shape=jax.ShapeDtypeStruct((len(plan), y_cells...]
  transfers between devices with their start and end apart: 21 -> 21, of which waited for: 10 -> 10; matrix products, arithmetic and copies ran while one was open for 30% -> 29% of each run, Pallas kernels for 13% -> 13%
where the time goes in v24:
time: 152 us; the launch traced here: 151 us
  starting transfers between devices  35.3 us (23%)
  Pallas kernels  34.6 us (23%)
  local copies, waits for them, and re-layouts  29.8 us (20%)
  waiting for transfers between devices  23.4 us (15%)
  matrix products  19.6 us (13%)
  other arithmetic  7.28 us (5%)
    pallas_call x4, Pallas kernels, stencil_call(): pl.pallas_call(kernel, out_shape=jax.ShapeDtypeStruct((len(plan), y_cells...  34.6 us
    ppermute x3, waiting for transfers between devices, butterfly_sum(): lax.ppermute(value, axis, [(i, i ^ step) for i in range(size)])  10.9 us
    ppermute x2, starting transfers between devices, spatial_rims(): below = lax.ppermute(inner[-1:], 'gz', up)  9.9 us
    dot_general x1, matrix products, per_device(): jnp.dot(grad_hidden, expand_weight.T, preferred_element_type=jnp.float32)  7.88 us
    ppermute x4, starting transfers between devices, ring_reduce_scatter(): lax.ppermute(send, axis, [(i, i ^ step) for i in range(size)])  6.66 us
    ppermute x4, starting transfers between devices, ring_gather(): lax.ppermute(block, axis, [(i, i ^ step) for i in range(size)])  5.36 us
    ppermute x3, starting transfers between devices, butterfly_sum(): lax.ppermute(value, axis, [(i, i ^ step) for i in range(size)])  4.32 us
    ppermute x4, waiting for transfers between devices, ring_reduce_scatter(): lax.ppermute(send, axis, [(i, i ^ step) for i in range(size)])  3.69 us
  transfers between devices with their start and end apart: 21, of which 10 were waited for; matrix products, arithmetic and copies ran while one was open for 29% of the time, Pallas kernels for 13%

profile of v24, /device:TPU:0, one launch (start us, length us, event | category | flops | bytes accessed | tf_op | source)
XLA Modules:
  0.0 151.1 jit_solution(6982106690793953099)
XLA Ops:
  0.7 3.0 %reshape.89 = bf16[32,256,64]{2,1,0:T(8,128)(2,1)S(1)} reshape(bf16[2,16,16384]{2,1,0:T(8,128)(2,1)} %param.7) | data formatting | bytes 2097152 | tf_op jit(solution)/shard_map/reshape | solution.py:261
  5.0 3.0 %collective-permute-start = (f32[16,32,128]{2,0,1:T(8,128)S(1)}, f32[16,32,128]{2,0,1:T(8,128)}, u32[]{:S(2)}, u32[]{:S(2)}) collective-permute-start(f32[16,32,128]{2,0,1:T(8,128)S(1)} %fusion.16), channel_id=1, source_target_pairs={{0,16},{8,24},{16,0},{24,8},{1,17},{9,25},{17,1},{25,9},{2,18},{10... | collective-permute-start | bytes 786440 | tf_op jit(solution)/shard_map/ppermute | solution.py:90
  8.7 1.5 collective-permute-start.2
  10.2 1.4 collective-permute-start.3
  11.7 1.7 %collective-permute-done.2 = bf16[2,16,128]{2,1,0:T(8,128)(2,1)S(1)} collective-permute-done((bf16[2,16,128]{2,1,0:T(8,128)(2,1)S(1)}, bf16[2,16,128]{2,1,0:T(8,128)(2,1)S(1)}, u32[]{:S(2)}, u32[]{:S(2)}) %collective-permute-start.2) | collective-permute-done | bytes 8224 | tf_op jit(solution)/shard_map/ppermute | solution.py:26
  14.3 1.2 collective-permute-done.4
  16.4 1.3 fusion.101
  17.6 4.4 %collective-permute-start.5 = (bf16[1,18,16640]{2,1,0:T(8,128)(2,1)}, bf16[1,18,16640]{2,1,0:T(8,128)(2,1)}, u32[]{:S(2)}, u32[]{:S(2)}) collective-permute-start(bf16[1,18,16640]{2,1,0:T(8,128)(2,1)} %get-tuple-element.18), channel_id=1, source_target_pairs={{0,1},{1,2},{2,3},{4,5},{5,6},{6,7},{8,9},{9,10},{10,11},{12,13},{... | collective-permute-start | bytes 1797128 | tf_op jit(solution)/shard_map/ppermute | solution.py:126
  22.0 1.5 collective-permute-start.6
  23.5 1.1 fusion.18
  25.4 1.5 collective-permute-start.1
  26.9 2.3 %reshape.93 = bf16[32,256,64]{2,1,0:T(8,128)(2,1)S(1)} reshape(bf16[2,16,16384]{2,1,0:T(8,128)(2,1)S(1)} %copy-done.7) | data formatting | bytes 2097152 | tf_op jit(solution)/shard_map/reshape | solution.py:281
  29.2 1.6 %copy.30 = bf16[32,256,64]{1,2,0:T(8,128)(2,1)} copy(bf16[32,256,64]{2,1,0:T(8,128)(2,1)S(1)} %reshape.93) | data formatting | bytes 2097152 | tf_op jit(solution)/shard_map/optimization_barrier | solution.py:281
  31.1 1.1 fusion.20
  32.9 9.5 %shard_map.94.refs_2_ = f32[2,16,16384]{2,1,0:T(8,128)} custom-call(bf16[2,18,16640]{2,1,0:T(8,128)(2,1)} %copy-done.2, f32[27,16,128]{2,1,0:T(8,128)} %broadcast_in_dim.18.refs_1_.refs_3_), custom_call_target="tpu_custom_call" | custom-call | tf_op jit(solution)/shard_map/pallas_call | solution.py:181
  43.8 7.6 %shard_map.95 = bf16[2,16,16384]{2,1,0:T(8,128)(2,1)} custom-call(bf16[1,18,16640]{2,1,0:T(8,128)(2,1)} %collective-permute-done.5.refs_0_, bf16[1,18,16640]{2,1,0:T(8,128)(2,1)} %collective-permute-done.6.refs_1_, f32[2,16,16384]{2,1,0:T(8,128)} %shard_map.94.refs_2_, f32[27,16,128]{2,1,0:T(8,128)} %broadcast_in_dim.18.refs_1_.refs_3_), custom_call_target="tpu_custom_call" | custom-call | tf_op jit(solution)/shard_map/pallas_call | solution.py:181
  51.5 1.5 collective-permute-start.7
  52.9 3.0 %reshape.90 = bf16[8192,64]{1,0:T(8,128)(2,1)S(1)} reshape(bf16[2,16,16384]{2,1,0:T(8,128)(2,1)} %shard_map.95) | data formatting | bytes 2097152 | tf_op jit(solution)/shard_map/reshape | solution.py:270
  56.0 1.2 fusion.106
  57.2 2.8 %fusion.5 = f32[8192,64]{0,1:T(8,128)S(1)} fusion(bf16[256,64]{0,1:T(8,128)(2,1)S(1)} %copy-done.15, f32[8192,256]{1,0:T(8,128)S(1)} %fusion.106), kind=kOutput, calls=%fused_computation.10 | convolution fusion | flops 278921216 | bytes 10518528 | tf_op jit(solution)/shard_map/dot_general | solution.py:273
  60.5 1.6 %collective-permute-start.8 = (bf16[16,32,128]{2,1,0:T(8,128)(2,1)S(1)}, bf16[16,32,128]{2,1,0:T(8,128)(2,1)S(1)}, u32[]{:S(2)}, u32[]{:S(2)}) collective-permute-start(bf16[16,32,128]{2,1,0:T(8,128)(2,1)S(1)} %pad_maximum_fusion.3), channel_id=1, source_target_pairs={{0,16},{8,24},{16,0},{24,8},{1,17},{9,25},{17,1},{25,9},{2,18},{10... | collective-permute-start | bytes 393224 | tf_op jit(solution)/shard_map/ppermute | solution.py:68
  62.1 3.4 %collective-permute-done.8 = bf16[16,32,128]{2,1,0:T(8,128)(2,1)S(1)} collective-permute-done((bf16[16,32,128]{2,1,0:T(8,128)(2,1)S(1)}, bf16[16,32,128]{2,1,0:T(8,128)(2,1)S(1)}, u32[]{:S(2)}, u32[]{:S(2)}) %collective-permute-start.8) | collective-permute-done | bytes 131104 | tf_op jit(solution)/shard_map/ppermute | solution.py:68
  66.4 2.7 %fusion.11 = (bf16[32,256,64]{1,2,0:T(8,128)(2,1)S(1)}, bf16[32,256,64]{1,2,0:T(8,128)(2,1)}) fusion(bf16[32,256,64]{1,2,0:T(8,128)(2,1)S(1)} %copy-done.8, f32[256,32,64]{0,2,1:T(8,128)S(1)} %fusion.27, bf16[32,32,64]{2,1,0:T(8,128)(2,1)S(1)} %get-tuple-element.27, f32[32]{0:T(128)S(1)} %get-tuple-element.33, s32[32]{0:T(128)S(1)} %add.135, ...), kind=kOutput, calls=%fused_computation.17 | convolution fusion | flops 41566208 | bytes 7472384 | tf_op jit(solution)/shard_map/krc,xk->rxc/dot_general | solution.py:218
  70.5 1.6 %collective-permute-start.9 = (f32[16,32,128]{2,0,1:T(8,128)S(1)}, f32[16,32,128]{2,0,1:T(8,128)S(1)}, u32[]{:S(2)}, u32[]{:S(2)}) collective-permute-start(f32[16,32,128]{2,0,1:T(8,128)S(1)} %fusion.13), channel_id=1, source_target_pairs={{0,16},{8,24},{16,0},{24,8},{1,17},{9,25},{17,1},{25,9},{2,18},{10... | collective-permute-start | bytes 786440 | tf_op jit(solution)/shard_map/ppermute | solution.py:90
  72.2 1.0 copy.42
  73.3 3.7 %collective-permute-done.9 = f32[16,32,128]{2,0,1:T(8,128)S(1)} collective-permute-done((f32[16,32,128]{2,0,1:T(8,128)S(1)}, f32[16,32,128]{2,0,1:T(8,128)S(1)}, u32[]{:S(2)}, u32[]{:S(2)}) %collective-permute-start.9) | collective-permute-done | bytes 262176 | tf_op jit(solution)/shard_map/ppermute | solution.py:90
  78.4 7.9 %convolution_convert_fusion = bf16[8192,64]{0,1:T(8,128)(2,1)} fusion(bf16[64,256]{1,0:T(8,128)(2,1)S(1)} %copy-done, bf16[8192,64]{0,1:T(8,128)(2,1)} %bitcast.54, bf16[256,64]{0,1:T(8,128)(2,1)} %param.10, f32[8192,256]{1,0:T(8,128)} %copy-done.4), kind=kOutput, calls=%fused_computation.3 | convolution fusion | flops 558366720 | bytes 10551296 | tf_op jit(solution)/shard_map/dot_general | solution.py:290
  86.3 1.1 copy.29
  87.4 2.5 %reshape.92 = bf16[2,16,16384]{2,1,0:T(8,128)(2,1)} reshape(bf16[32,256,64]{2,1,0:T(8,128)(2,1)S(1)} %copy.29) | data formatting | bytes 2097152 | tf_op jit(solution)/shard_map/reshape | solution.py:279
  89.9 1.1 copy.35
  90.9 1.9 %reshape.95 = bf16[2,16,16384]{2,1,0:T(8,128)(2,1)S(1)} reshape(bf16[8192,64]{1,0:T(8,128)(2,1)S(1)} %copy.35) | data formatting | bytes 2097152 | tf_op jit(solution)/shard_map/reshape | solution.py:293
  92.9 1.0 add_convert_fusion.3
  94.7 1.5 %collective-permute-start.11 = (bf16[2,16,128]{2,1,0:T(8,128)(2,1)S(1)}, bf16[2,16,128]{2,1,0:T(8,128)(2,1)S(1)}, u32[]{:S(2)}, u32[]{:S(2)}) collective-permute-start(bf16[2,16,128]{2,1,0:T(8,128)(2,1)S(1)} %get-tuple-element.20), channel_id=1, source_target_pairs={{0,8},{8,16},{16,24},{24,0},{1,9},{9,17},{17,25},{25,1},{2,10},{10... | collective-permute-start | bytes 24584 | tf_op jit(solution)/shard_map/ppermute | solution.py:26
  96.2 1.2 collective-permute-start.16
  97.4 1.8 %collective-permute-start.12 = (bf16[2,16,128]{2,1,0:T(8,128)(2,1)S(1)}, bf16[2,16,128]{2,1,0:T(8,128)(2,1)S(1)}, u32[]{:S(2)}, u32[]{:S(2)}) collective-permute-start(bf16[2,16,128]{2,1,0:T(8,128)(2,1)S(1)} %get-tuple-element.19), channel_id=1, source_target_pairs={{8,0},{16,8},{24,16},{0,24},{9,1},{17,9},{25,17},{1,25},{10,2},{18... | collective-permute-start | bytes 24584 | tf_op jit(solution)/shard_map/ppermute | solution.py:27
  99.6 1.5 %collective-permute-done.12 = bf16[2,16,128]{2,1,0:T(8,128)(2,1)S(1)} collective-permute-done((bf16[2,16,128]{2,1,0:T(8,128)(2,1)S(1)}, bf16[2,16,128]{2,1,0:T(8,128)(2,1)S(1)}, u32[]{:S(2)}, u32[]{:S(2)}) %collective-permute-start.12) | collective-permute-done | bytes 8224 | tf_op jit(solution)/shard_map/ppermute | solution.py:27
  101.4 1.1 collective-permute-start.17
  103.6 1.4 fusion.100
  105.0 5.5 %collective-permute-start.14 = (bf16[1,18,16640]{2,1,0:T(8,128)(2,1)}, bf16[1,18,16640]{2,1,0:T(8,128)(2,1)}, u32[]{:S(2)}, u32[]{:S(2)}) collective-permute-start(bf16[1,18,16640]{2,1,0:T(8,128)(2,1)} %get-tuple-element.16), channel_id=1, source_target_pairs={{0,1},{1,2},{2,3},{4,5},{5,6},{6,7},{8,9},{9,10},{10,11},{12,13},{... | collective-permute-start | bytes 1797128 | tf_op jit(solution)/shard_map/ppermute | solution.py:126
  110.4 1.3 collective-permute-start.15
  112.5 9.5 %shard_map.96.refs_2_ = f32[2,16,16384]{2,1,0:T(8,128)} custom-call(bf16[2,18,16640]{2,1,0:T(8,128)(2,1)} %copy-done.3, f32[27,16,128]{2,1,0:T(8,128)} %broadcast_in_dim.36.refs_1_.refs_4_), custom_call_target="tpu_custom_call" | custom-call | tf_op jit(solution)/shard_map/pallas_call | solution.py:181
  122.0 2.7 %collective-permute-start.19 = (bf16[64,1024]{1,0:T(8,128)(2,1)S(1)}, bf16[64,1024]{1,0:T(8,128)(2,1)S(1)}, u32[]{:S(2)}, u32[]{:S(2)}) collective-permute-start(bf16[64,1024]{1,0:T(8,128)(2,1)S(1)} %add_convert_fusion.2), channel_id=1, source_target_pairs={{0,1},{1,0},{2,3},{3,2},{4,5},{5,4},{6,7},{7,6},{8,9},{9,8},{10,11... | collective-permute-start | bytes 393224 | tf_op jit(solution)/shard_map/ppermute | solution.py:107
  125.5 9.5 %collective-permute-done.19 = bf16[64,1024]{1,0:T(8,128)(2,1)S(1)} collective-permute-done((bf16[64,1024]{1,0:T(8,128)(2,1)S(1)}, bf16[64,1024]{1,0:T(8,128)(2,1)S(1)}, u32[]{:S(2)}, u32[]{:S(2)}) %collective-permute-start.19) | collective-permute-done | bytes 131104 | tf_op jit(solution)/shard_map/ppermute | solution.py:107
  135.0 1.5 %collective-permute-start.20 = (bf16[64,1024]{1,0:T(8,128)(2,1)S(1)}, bf16[64,1024]{1,0:T(8,128)(2,1)S(1)}, u32[]{:S(2)}, u32[]{:S(2)}) collective-permute-start(bf16[64,1024]{1,0:T(8,128)(2,1)S(1)} %add_convert_fusion.1), channel_id=1, source_target_pairs={{0,2},{1,3},{2,0},{3,1},{4,6},{5,7},{6,4},{7,5},{8,10},{9,11},{10,... | collective-permute-start | bytes 393224 | tf_op jit(solution)/shard_map/ppermute | solution.py:107
  137.1 1.1 copy.38
  138.2 2.5 %reshape.96.refs_3_ = bf16[2,16,16384]{2,1,0:T(8,128)(2,1)} reshape(bf16[32,256,64]{2,1,0:T(8,128)(2,1)S(1)} %copy.38) | data formatting | bytes 2097152 | tf_op jit(solution)/shard_map/reshape | solution.py:311
  140.7 1.4 collective-permute-done.20
  143.1 8.0 %shard_map.97 = bf16[2,16,16384]{2,1,0:T(8,128)(2,1)} custom-call(bf16[1,18,16640]{2,1,0:T(8,128)(2,1)} %collective-permute-done.14.refs_0_, bf16[1,18,16640]{2,1,0:T(8,128)(2,1)} %collective-permute-done.15.refs_1_, f32[2,16,16384]{2,1,0:T(8,128)} %shard_map.96.refs_2_, bf16[2,16,16384]{2,1,0:T(8,128)(2,1)} %reshape.96.refs_3_, ...), custom_call_target="tpu_custom_call" | custom-call | tf_op jit(solution)/shard_map/pallas_call | solution.py:181
  (110 shorter events, 16.8 us)
Async XLA Ops:
  0.6 55.4 %copy-start = (bf16[64,256]{1,0:T(8,128)(2,1)S(1)}, bf16[64,256]{1,0:T(8,128)(2,1)}, u32[]{:S(2)}) copy-start(bf16[64,256]{1,0:T(8,128)(2,1)} %param.9) | copy-start | bytes 98308
  4.8 8.6 %copy-start.5 = (bf16[2,16,16384]{2,1,0:T(8,128)(2,1)S(1)}, bf16[2,16,16384]{2,1,0:T(8,128)(2,1)}, u32[]{:S(2)}) copy-start(bf16[2,16,16384]{2,1,0:T(8,128)(2,1)} %param.7) | copy-start | bytes 3145732
  5.0 18.5 %collective-permute-start = (f32[16,32,128]{2,0,1:T(8,128)S(1)}, f32[16,32,128]{2,0,1:T(8,128)}, u32[]{:S(2)}, u32[]{:S(2)}) collective-permute-start(f32[16,32,128]{2,0,1:T(8,128)S(1)} %fusion.16), channel_id=1, source_target_pairs={{0,16},{8,24},{16,0},{24,8},{1,17},{9,25},{17,1},{25,9},{2,18},{10... | collective-permute-start | bytes 786440 | tf_op jit(solution)/shard_map/ppermute | solution.py:90
  8.7 4.7 %collective-permute-start.2 = (bf16[2,16,128]{2,1,0:T(8,128)(2,1)S(1)}, bf16[2,16,128]{2,1,0:T(8,128)(2,1)S(1)}, u32[]{:S(2)}, u32[]{:S(2)}) collective-permute-start(bf16[2,16,128]{2,1,0:T(8,128)(2,1)S(1)} %get-tuple-element.22), channel_id=1, source_target_pairs={{0,8},{8,16},{16,24},{24,0},{1,9},{9,17},{17,25},{25,1},{2,10},{10... | collective-permute-start | bytes 24584 | tf_op jit(solution)/shard_map/ppermute | solution.py:26
  10.2 3.7 %collective-permute-start.3 = (bf16[2,16,128]{2,1,0:T(8,128)(2,1)S(1)}, bf16[2,16,128]{2,1,0:T(8,128)(2,1)S(1)}, u32[]{:S(2)}, u32[]{:S(2)}) collective-permute-start(bf16[2,16,128]{2,1,0:T(8,128)(2,1)S(1)} %get-tuple-element.21), channel_id=1, source_target_pairs={{8,0},{16,8},{24,16},{0,24},{9,1},{17,9},{25,17},{1,25},{10,2},{18... | collective-permute-start | bytes 24584 | tf_op jit(solution)/shard_map/ppermute | solution.py:27
  14.1 1.4 collective-permute-start.4
  16.3 8.3 %copy-start.2 = (bf16[2,18,16640]{2,1,0:T(8,128)(2,1)}, bf16[2,18,16640]{2,1,0:T(8,128)(2,1)S(1)}, u32[]{:S(2)}) copy-start(bf16[2,18,16640]{2,1,0:T(8,128)(2,1)S(1)} %pad_maximum_fusion.refs_0_) | copy-start | bytes 3594244
  16.4 10.5 %copy-start.7 = (bf16[2,16,16384]{2,1,0:T(8,128)(2,1)S(1)}, bf16[2,16,16384]{2,1,0:T(8,128)(2,1)}, u32[]{:S(2)}) copy-start(bf16[2,16,16384]{2,1,0:T(8,128)(2,1)} %param.13) | copy-start | bytes 3145732
  17.6 25.9 %collective-permute-start.5 = (bf16[1,18,16640]{2,1,0:T(8,128)(2,1)}, bf16[1,18,16640]{2,1,0:T(8,128)(2,1)}, u32[]{:S(2)}, u32[]{:S(2)}) collective-permute-start(bf16[1,18,16640]{2,1,0:T(8,128)(2,1)} %get-tuple-element.18), channel_id=1, source_target_pairs={{0,1},{1,2},{2,3},{4,5},{5,6},{6,7},{8,9},{9,10},{10,11},{12,13},{... | collective-permute-start | bytes 1797128 | tf_op jit(solution)/shard_map/ppermute | solution.py:126
  22.0 21.8 %collective-permute-start.6 = (bf16[1,18,16640]{2,1,0:T(8,128)(2,1)}, bf16[1,18,16640]{2,1,0:T(8,128)(2,1)}, u32[]{:S(2)}, u32[]{:S(2)}) collective-permute-start(bf16[1,18,16640]{2,1,0:T(8,128)(2,1)} %get-tuple-element.17), channel_id=1, source_target_pairs={{1,0},{2,1},{3,2},{5,4},{6,5},{7,6},{9,8},{10,9},{11,10},{13,12},{... | collective-permute-start | bytes 1797128 | tf_op jit(solution)/shard_map/ppermute | solution.py:127
  24.6 2.2 %copy-start.11 = (f32[16,32,128]{2,0,1:T(8,128)}, f32[16,32,128]{2,0,1:T(8,128)S(1)}, u32[]{:S(2)}) copy-start(f32[16,32,128]{2,0,1:T(8,128)S(1)} %fusion.18) | copy-start | bytes 786436
  25.4 17.0 %collective-permute-start.1 = (f32[8,32,128]{2,0,1:T(8,128)}, f32[8,32,128]{2,0,1:T(8,128)}, u32[]{:S(2)}, u32[]{:S(2)}) collective-permute-start(f32[8,32,128]{2,0,1:T(8,128)} %constant_dynamic-slice_fusion.1), channel_id=1, source_target_pairs={{0,8},{8,0},{16,24},{24,16},{1,9},{9,1},{17,25},{25,17},{2,10},{10... | collective-permute-start | bytes 393224 | tf_op jit(solution)/shard_map/ppermute | solution.py:90
  29.2 1.6 %copy-start.6 = (bf16[32,64,64]{2,1,0:T(8,128)(2,1)S(1)}, bf16[32,64,64]{2,1,0:T(8,128)(2,1)}, u32[]{:S(2)}) copy-start(bf16[32,64,64]{2,1,0:T(8,128)(2,1)} %param.12) | copy-start | bytes 786436
  29.2 1.8 %copy-start.14 = (bf16[27,64]{1,0:T(8,128)(2,1)S(1)}, bf16[27,64]{1,0:T(8,128)(2,1)}, u32[]{:S(2)}) copy-start(bf16[27,64]{1,0:T(8,128)(2,1)} %param.8) | copy-start | bytes 10372
  32.2 10.2 %copy-start.12 = (f32[16,32,128]{2,0,1:T(8,128)S(1)}, f32[16,32,128]{2,0,1:T(8,128)}, u32[]{:S(2)}) copy-start(f32[16,32,128]{2,0,1:T(8,128)} %copy-done.11) | copy-start | bytes 786436
  51.5 9.1 %collective-permute-start.7 = (bf16[8,32,128]{2,1,0:T(8,128)(2,1)S(1)}, bf16[8,32,128]{2,1,0:T(8,128)(2,1)S(1)}, u32[]{:S(2)}, u32[]{:S(2)}) collective-permute-start(bf16[8,32,128]{2,1,0:T(8,128)(2,1)S(1)} %convolution_convert_fusion.2), channel_id=1, source_target_pairs={{0,8},{8,0},{16,24},{24,16},{1,9},{9,1},{17,25},{25,17},{2,10},{10... | collective-permute-start | bytes 196616 | tf_op jit(solution)/shard_map/ppermute | solution.py:68
  56.0 1.2 copy-start.15
  57.2 3.3 %copy-start.4 = (f32[8192,256]{1,0:T(8,128)}, f32[8192,256]{1,0:T(8,128)S(1)}, u32[]{:S(2)}) copy-start(f32[8192,256]{1,0:T(8,128)S(1)} %fusion.106) | copy-start | bytes 25165828
  60.5 5.8 %copy-start.8 = (bf16[32,256,64]{1,2,0:T(8,128)(2,1)S(1)}, bf16[32,256,64]{1,2,0:T(8,128)(2,1)}, u32[]{:S(2)}) copy-start(bf16[32,256,64]{1,2,0:T(8,128)(2,1)} %copy.30) | copy-start | bytes 3145732
  60.5 5.0 %collective-permute-start.8 = (bf16[16,32,128]{2,1,0:T(8,128)(2,1)S(1)}, bf16[16,32,128]{2,1,0:T(8,128)(2,1)S(1)}, u32[]{:S(2)}, u32[]{:S(2)}) collective-permute-start(bf16[16,32,128]{2,1,0:T(8,128)(2,1)S(1)} %pad_maximum_fusion.3), channel_id=1, source_target_pairs={{0,16},{8,24},{16,0},{24,8},{1,17},{9,25},{17,1},{25,9},{2,18},{10... | collective-permute-start | bytes 393224 | tf_op jit(solution)/shard_map/ppermute | solution.py:68
  70.5 6.4 %collective-permute-start.9 = (f32[16,32,128]{2,0,1:T(8,128)S(1)}, f32[16,32,128]{2,0,1:T(8,128)S(1)}, u32[]{:S(2)}, u32[]{:S(2)}) collective-permute-start(f32[16,32,128]{2,0,1:T(8,128)S(1)} %fusion.13), channel_id=1, source_target_pairs={{0,16},{8,24},{16,0},{24,8},{1,17},{9,25},{17,1},{25,9},{2,18},{10... | collective-permute-start | bytes 786440 | tf_op jit(solution)/shard_map/ppermute | solution.py:90
  77.1 1.3 copy-start.13
  77.8 15.0 %collective-permute-start.10 = (f32[8,32,128]{2,0,1:T(8,128)}, f32[8,32,128]{2,0,1:T(8,128)}, u32[]{:S(2)}, u32[]{:S(2)}) collective-permute-start(f32[8,32,128]{2,0,1:T(8,128)} %constant_dynamic-slice_fusion), channel_id=1, source_target_pairs={{0,8},{8,0},{16,24},{24,16},{1,9},{9,1},{17,25},{25,17},{2,10},{10... | collective-permute-start | bytes 393224 | tf_op jit(solution)/shard_map/ppermute | solution.py:90
  78.4 7.9 %copy-start.9 = (bf16[32,256,64]{1,2,0:T(8,128)(2,1)S(1)}, bf16[32,256,64]{1,2,0:T(8,128)(2,1)}, u32[]{:S(2)}) copy-start(bf16[32,256,64]{1,2,0:T(8,128)(2,1)} %get-tuple-element.14) | copy-start | bytes 3145732
  87.4 2.5 %copy-start.10 = (bf16[8192,64]{0,1:T(8,128)(2,1)S(1)}, bf16[8192,64]{0,1:T(8,128)(2,1)}, u32[]{:S(2)}) copy-start(bf16[8192,64]{0,1:T(8,128)(2,1)} %convolution_convert_fusion) | copy-start | bytes 3145732
  94.7 4.8 %collective-permute-start.11 = (bf16[2,16,128]{2,1,0:T(8,128)(2,1)S(1)}, bf16[2,16,128]{2,1,0:T(8,128)(2,1)S(1)}, u32[]{:S(2)}, u32[]{:S(2)}) collective-permute-start(bf16[2,16,128]{2,1,0:T(8,128)(2,1)S(1)} %get-tuple-element.20), channel_id=1, source_target_pairs={{0,8},{8,16},{16,24},{24,0},{1,9},{9,17},{17,25},{25,1},{2,10},{10... | collective-permute-start | bytes 24584 | tf_op jit(solution)/shard_map/ppermute | solution.py:26
  96.2 5.2 %collective-permute-start.16 = (bf16[8,32,128]{2,1,0:T(8,128)(2,1)S(1)}, bf16[8,32,128]{2,1,0:T(8,128)(2,1)S(1)}, u32[]{:S(2)}, u32[]{:S(2)}) collective-permute-start(bf16[8,32,128]{2,1,0:T(8,128)(2,1)S(1)} %convolution_convert_fusion.1), channel_id=1, source_target_pairs={{0,8},{8,0},{16,24},{24,16},{1,9},{9,1},{17,25},{25,17},{2,10},{10... | collective-permute-start | bytes 196616 | tf_op jit(solution)/shard_map/ppermute | solution.py:68
  97.4 3.7 %collective-permute-start.12 = (bf16[2,16,128]{2,1,0:T(8,128)(2,1)S(1)}, bf16[2,16,128]{2,1,0:T(8,128)(2,1)S(1)}, u32[]{:S(2)}, u32[]{:S(2)}) collective-permute-start(bf16[2,16,128]{2,1,0:T(8,128)(2,1)S(1)} %get-tuple-element.19), channel_id=1, source_target_pairs={{8,0},{16,8},{24,16},{0,24},{9,1},{17,9},{25,17},{1,25},{10,2},{18... | collective-permute-start | bytes 24584 | tf_op jit(solution)/shard_map/ppermute | solution.py:27
  99.4 22.5 %collective-permute-start.18 = (bf16[64,1024]{1,0:T(8,128)(2,1)S(1)}, bf16[64,1024]{1,0:T(8,128)(2,1)S(1)}, u32[]{:S(2)}, u32[]{:S(2)}) collective-permute-start(bf16[64,1024]{1,0:T(8,128)(2,1)S(1)} %convert_element_type.143), channel_id=1, source_target_pairs={{0,4},{4,0},{1,5},{5,1},{2,6},{6,2},{3,7},{7,3},{8,12},{12,8},{9,1... | collective-permute-start | bytes 393224 | tf_op jit(solution)/shard_map/ppermute | solution.py:107
  101.3 1.4 collective-permute-start.13
  101.4 23.2 %collective-permute-start.17 = (bf16[16,32,128]{2,1,0:T(8,128)(2,1)S(1)}, bf16[16,32,128]{2,1,0:T(8,128)(2,1)S(1)}, u32[]{:S(2)}, u32[]{:S(2)}) collective-permute-start(bf16[16,32,128]{2,1,0:T(8,128)(2,1)S(1)} %pad_maximum_fusion.4), channel_id=1, source_target_pairs={{0,16},{8,24},{16,0},{24,8},{1,17},{9,25},{17,1},{25,9},{2,18},{10... | collective-permute-start | bytes 393224 | tf_op jit(solution)/shard_map/ppermute | solution.py:68
  103.6 8.9 %copy-start.3 = (bf16[2,18,16640]{2,1,0:T(8,128)(2,1)}, bf16[2,18,16640]{2,1,0:T(8,128)(2,1)S(1)}, u32[]{:S(2)}) copy-start(bf16[2,18,16640]{2,1,0:T(8,128)(2,1)S(1)} %pad_maximum_fusion.1.refs_0_) | copy-start | bytes 3594244
  105.0 38.2 %collective-permute-start.14 = (bf16[1,18,16640]{2,1,0:T(8,128)(2,1)}, bf16[1,18,16640]{2,1,0:T(8,128)(2,1)}, u32[]{:S(2)}, u32[]{:S(2)}) collective-permute-start(bf16[1,18,16640]{2,1,0:T(8,128)(2,1)} %get-tuple-element.16), channel_id=1, source_target_pairs={{0,1},{1,2},{2,3},{4,5},{5,6},{6,7},{8,9},{9,10},{10,11},{12,13},{... | collective-permute-start | bytes 1797128 | tf_op jit(solution)/shard_map/ppermute | solution.py:126
  110.4 32.7 %collective-permute-start.15 = (bf16[1,18,16640]{2,1,0:T(8,128)(2,1)}, bf16[1,18,16640]{2,1,0:T(8,128)(2,1)}, u32[]{:S(2)}, u32[]{:S(2)}) collective-permute-start(bf16[1,18,16640]{2,1,0:T(8,128)(2,1)} %get-tuple-element.15), channel_id=1, source_target_pairs={{1,0},{2,1},{3,2},{5,4},{6,5},{7,6},{9,8},{10,9},{11,10},{13,12},{... | collective-permute-start | bytes 1797128 | tf_op jit(solution)/shard_map/ppermute | solution.py:127
  122.0 13.0 %collective-permute-start.19 = (bf16[64,1024]{1,0:T(8,128)(2,1)S(1)}, bf16[64,1024]{1,0:T(8,128)(2,1)S(1)}, u32[]{:S(2)}, u32[]{:S(2)}) collective-permute-start(bf16[64,1024]{1,0:T(8,128)(2,1)S(1)} %add_convert_fusion.2), channel_id=1, source_target_pairs={{0,1},{1,0},{2,3},{3,2},{4,5},{5,4},{6,7},{7,6},{8,9},{9,8},{10,11... | collective-permute-start | bytes 393224 | tf_op jit(solution)/shard_map/ppermute | solution.py:107
  135.0 7.2 %collective-permute-start.20 = (bf16[64,1024]{1,0:T(8,128)(2,1)S(1)}, bf16[64,1024]{1,0:T(8,128)(2,1)S(1)}, u32[]{:S(2)}, u32[]{:S(2)}) collective-permute-start(bf16[64,1024]{1,0:T(8,128)(2,1)S(1)} %add_convert_fusion.1), channel_id=1, source_target_pairs={{0,2},{1,3},{2,0},{3,1},{4,6},{5,7},{6,4},{7,5},{8,10},{9,11},{10,... | collective-permute-start | bytes 393224 | tf_op jit(solution)/shard_map/ppermute | solution.py:107
  142.2 9.0 %copy-start.1 = (bf16[64,256]{1,0:T(8,128)(2,1)S(1)}, bf16[64,256]{1,0:T(8,128)(2,1)}, u32[]{:S(2)}) copy-start(bf16[64,256]{1,0:T(8,128)(2,1)} %param.9) | copy-start | bytes 98308

commit v25 on v21

--- a/solution.py
+++ b/solution.py
@@ -172,7 +172,7 @@
 
 
 def stencil_call(plan, inputs, accs, gains, y_cells, lanes, channels, out_dtype):
-    chunk = min(1024, lanes)
+    chunk = min(2048, lanes)
     rows = 8 if y_cells % 8 == 0 else y_cells
     kernel = functools.partial(
         stencil_kernel, chunk, 2 * channels, y_cells, rows, plan, len(inputs), len(accs)

time: 150 us -> 149 us (level)
  transfers between devices with their start and end apart: 21 -> 21, of which waited for: 10 -> 9; matrix products, arithmetic and copies ran while one was open for 30% -> 30% of each run, Pallas kernels for 13% -> 12%
where the time goes in v25:
time: 149 us
  starting transfers between devices  35.5 us (24%)
  Pallas kernels  32 us (21%)
  local copies, waits for them, and re-layouts  29.9 us (20%)
  waiting for transfers between devices  23.2 us (16%)
  matrix products  19.6 us (13%)
  other arithmetic  7.28 us (5%)
    pallas_call x4, Pallas kernels, stencil_call(): pl.pallas_call(kernel, out_shape=jax.ShapeDtypeStruct((len(plan), y_cells...  32 us
    ppermute x3, waiting for transfers between devices, butterfly_sum(): lax.ppermute(value, axis, [(i, i ^ step) for i in range(size)])  10.9 us
    ppermute x2, starting transfers between devices, spatial_rims(): below = lax.ppermute(inner[-1:], 'gz', up)  9.81 us
    dot_general x1, matrix products, per_device(): jnp.dot(grad_hidden, expand_weight.T, preferred_element_type=jnp.float32)  7.88 us
    ppermute x4, starting transfers between devices, ring_reduce_scatter(): lax.ppermute(send, axis, [(i, i ^ step) for i in range(size)])  6.66 us
    ppermute x4, starting transfers between devices, ring_gather(): lax.ppermute(block, axis, [(i, i ^ step) for i in range(size)])  5.36 us
    ppermute x3, starting transfers between devices, butterfly_sum(): lax.ppermute(value, axis, [(i, i ^ step) for i in range(size)])  4.51 us
    ppermute x4, waiting for transfers between devices, ring_reduce_scatter(): lax.ppermute(send, axis, [(i, i ^ step) for i in range(size)])  3.69 us
  transfers between devices with their start and end apart: 21, of which 9 were waited for; matrix products, arithmetic and copies ran while one was open for 30% of the time, Pallas kernels for 12%

profile of v25, /device:TPU:0, one launch (start us, length us, event | category | flops | bytes accessed | tf_op | source)
XLA Modules:
  0.0 148.6 jit_solution(12398262369475006895)
XLA Ops:
  0.7 3.0 %reshape.89 = bf16[32,256,64]{2,1,0:T(8,128)(2,1)S(1)} reshape(bf16[2,16,16384]{2,1,0:T(8,128)(2,1)} %param.7) | data formatting | bytes 2097152 | tf_op jit(solution)/shard_map/reshape | solution.py:261
  5.0 3.0 %collective-permute-start = (f32[16,32,128]{2,0,1:T(8,128)S(1)}, f32[16,32,128]{2,0,1:T(8,128)}, u32[]{:S(2)}, u32[]{:S(2)}) collective-permute-start(f32[16,32,128]{2,0,1:T(8,128)S(1)} %fusion.16), channel_id=1, source_target_pairs={{0,16},{8,24},{16,0},{24,8},{1,17},{9,25},{17,1},{25,9},{2,18},{10... | collective-permute-start | bytes 786440 | tf_op jit(solution)/shard_map/ppermute | solution.py:90
  8.7 1.5 %collective-permute-start.2 = (bf16[2,16,128]{2,1,0:T(8,128)(2,1)S(1)}, bf16[2,16,128]{2,1,0:T(8,128)(2,1)S(1)}, u32[]{:S(2)}, u32[]{:S(2)}) collective-permute-start(bf16[2,16,128]{2,1,0:T(8,128)(2,1)S(1)} %get-tuple-element.22), channel_id=1, source_target_pairs={{0,8},{8,16},{16,24},{24,0},{1,9},{9,17},{17,25},{25,1},{2,10},{10... | collective-permute-start | bytes 24584 | tf_op jit(solution)/shard_map/ppermute | solution.py:26
  10.2 1.4 collective-permute-start.3
  11.7 1.7 %collective-permute-done.2 = bf16[2,16,128]{2,1,0:T(8,128)(2,1)S(1)} collective-permute-done((bf16[2,16,128]{2,1,0:T(8,128)(2,1)S(1)}, bf16[2,16,128]{2,1,0:T(8,128)(2,1)S(1)}, u32[]{:S(2)}, u32[]{:S(2)}) %collective-permute-start.2) | collective-permute-done | bytes 8224 | tf_op jit(solution)/shard_map/ppermute | solution.py:26
  14.3 1.2 collective-permute-done.4
  16.4 1.3 fusion.101
  17.6 4.4 %collective-permute-start.5 = (bf16[1,18,16640]{2,1,0:T(8,128)(2,1)}, bf16[1,18,16640]{2,1,0:T(8,128)(2,1)}, u32[]{:S(2)}, u32[]{:S(2)}) collective-permute-start(bf16[1,18,16640]{2,1,0:T(8,128)(2,1)} %get-tuple-element.18), channel_id=1, source_target_pairs={{0,1},{1,2},{2,3},{4,5},{5,6},{6,7},{8,9},{9,10},{10,11},{12,13},{... | collective-permute-start | bytes 1797128 | tf_op jit(solution)/shard_map/ppermute | solution.py:126
  22.0 1.3 collective-permute-start.6
  23.3 1.1 fusion.18
  25.2 1.5 collective-permute-start.1
  26.7 2.5 %reshape.93 = bf16[32,256,64]{2,1,0:T(8,128)(2,1)S(1)} reshape(bf16[2,16,16384]{2,1,0:T(8,128)(2,1)S(1)} %copy-done.7) | data formatting | bytes 2097152 | tf_op jit(solution)/shard_map/reshape | solution.py:281
  29.2 1.6 %copy.30 = bf16[32,256,64]{1,2,0:T(8,128)(2,1)} copy(bf16[32,256,64]{2,1,0:T(8,128)(2,1)S(1)} %reshape.93) | data formatting | bytes 2097152 | tf_op jit(solution)/shard_map/optimization_barrier | solution.py:281
  31.0 1.1 fusion.20
  32.8 9.3 %shard_map.94.refs_2_ = f32[2,16,16384]{2,1,0:T(8,128)} custom-call(bf16[2,18,16640]{2,1,0:T(8,128)(2,1)} %copy-done.2, f32[27,8,128]{2,1,0:T(8,128)} %broadcast_in_dim.18.refs_1_.refs_3_), custom_call_target="tpu_custom_call" | custom-call | tf_op jit(solution)/shard_map/pallas_call | solution.py:181
  43.8 6.5 %shard_map.95 = bf16[2,16,16384]{2,1,0:T(8,128)(2,1)} custom-call(bf16[1,18,16640]{2,1,0:T(8,128)(2,1)} %collective-permute-done.5.refs_0_, bf16[1,18,16640]{2,1,0:T(8,128)(2,1)} %collective-permute-done.6.refs_1_, f32[2,16,16384]{2,1,0:T(8,128)} %shard_map.94.refs_2_, f32[27,8,128]{2,1,0:T(8,128)} %broadcast_in_dim.18.refs_1_.refs_3_), custom_call_target="tpu_custom_call" | custom-call | tf_op jit(solution)/shard_map/pallas_call | solution.py:181
  50.3 1.5 collective-permute-start.7
  51.8 3.0 %reshape.90 = bf16[8192,64]{1,0:T(8,128)(2,1)S(1)} reshape(bf16[2,16,16384]{2,1,0:T(8,128)(2,1)} %shard_map.95) | data formatting | bytes 2097152 | tf_op jit(solution)/shard_map/reshape | solution.py:270
  54.9 1.2 fusion.106
  56.1 2.8 %fusion.5 = f32[8192,64]{0,1:T(8,128)S(1)} fusion(bf16[256,64]{0,1:T(8,128)(2,1)S(1)} %copy-done.15, f32[8192,256]{1,0:T(8,128)S(1)} %fusion.106), kind=kOutput, calls=%fused_computation.10 | convolution fusion | flops 278921216 | bytes 10518528 | tf_op jit(solution)/shard_map/dot_general | solution.py:273
  59.4 1.6 %collective-permute-start.8 = (bf16[16,32,128]{2,1,0:T(8,128)(2,1)S(1)}, bf16[16,32,128]{2,1,0:T(8,128)(2,1)S(1)}, u32[]{:S(2)}, u32[]{:S(2)}) collective-permute-start(bf16[16,32,128]{2,1,0:T(8,128)(2,1)S(1)} %pad_maximum_fusion.3), channel_id=1, source_target_pairs={{0,16},{8,24},{16,0},{24,8},{1,17},{9,25},{17,1},{25,9},{2,18},{10... | collective-permute-start | bytes 393224 | tf_op jit(solution)/shard_map/ppermute | solution.py:68
  61.0 3.4 %collective-permute-done.8 = bf16[16,32,128]{2,1,0:T(8,128)(2,1)S(1)} collective-permute-done((bf16[16,32,128]{2,1,0:T(8,128)(2,1)S(1)}, bf16[16,32,128]{2,1,0:T(8,128)(2,1)S(1)}, u32[]{:S(2)}, u32[]{:S(2)}) %collective-permute-start.8) | collective-permute-done | bytes 131104 | tf_op jit(solution)/shard_map/ppermute | solution.py:68
  65.2 2.7 %fusion.11 = (bf16[32,256,64]{1,2,0:T(8,128)(2,1)S(1)}, bf16[32,256,64]{1,2,0:T(8,128)(2,1)}) fusion(bf16[32,256,64]{1,2,0:T(8,128)(2,1)S(1)} %copy-done.8, f32[256,32,64]{0,2,1:T(8,128)S(1)} %fusion.27, bf16[32,32,64]{2,1,0:T(8,128)(2,1)S(1)} %get-tuple-element.27, f32[32]{0:T(128)S(1)} %get-tuple-element.33, s32[32]{0:T(128)S(1)} %add.135, ...), kind=kOutput, calls=%fused_computation.17 | convolution fusion | flops 41566208 | bytes 7472384 | tf_op jit(solution)/shard_map/krc,xk->rxc/dot_general | solution.py:218
  69.4 1.6 %collective-permute-start.9 = (f32[16,32,128]{2,0,1:T(8,128)S(1)}, f32[16,32,128]{2,0,1:T(8,128)S(1)}, u32[]{:S(2)}, u32[]{:S(2)}) collective-permute-start(f32[16,32,128]{2,0,1:T(8,128)S(1)} %fusion.13), channel_id=1, source_target_pairs={{0,16},{8,24},{16,0},{24,8},{1,17},{9,25},{17,1},{25,9},{2,18},{10... | collective-permute-start | bytes 786440 | tf_op jit(solution)/shard_map/ppermute | solution.py:90
  71.1 1.0 copy.42
  72.2 3.7 %collective-permute-done.9 = f32[16,32,128]{2,0,1:T(8,128)S(1)} collective-permute-done((f32[16,32,128]{2,0,1:T(8,128)S(1)}, f32[16,32,128]{2,0,1:T(8,128)S(1)}, u32[]{:S(2)}, u32[]{:S(2)}) %collective-permute-start.9) | collective-permute-done | bytes 262176 | tf_op jit(solution)/shard_map/ppermute | solution.py:90
  77.3 7.9 %convolution_convert_fusion = bf16[8192,64]{0,1:T(8,128)(2,1)} fusion(bf16[64,256]{1,0:T(8,128)(2,1)S(1)} %copy-done, bf16[8192,64]{0,1:T(8,128)(2,1)} %bitcast.54, bf16[256,64]{0,1:T(8,128)(2,1)} %param.10, f32[8192,256]{1,0:T(8,128)} %copy-done.4), kind=kOutput, calls=%fused_computation.3 | convolution fusion | flops 558366720 | bytes 10551296 | tf_op jit(solution)/shard_map/dot_general | solution.py:290
  85.2 1.1 copy.29
  86.3 2.5 %reshape.92 = bf16[2,16,16384]{2,1,0:T(8,128)(2,1)} reshape(bf16[32,256,64]{2,1,0:T(8,128)(2,1)S(1)} %copy.29) | data formatting | bytes 2097152 | tf_op jit(solution)/shard_map/reshape | solution.py:279
  88.7 1.1 copy.35
  89.8 1.9 %reshape.95 = bf16[2,16,16384]{2,1,0:T(8,128)(2,1)S(1)} reshape(bf16[8192,64]{1,0:T(8,128)(2,1)S(1)} %copy.35) | data formatting | bytes 2097152 | tf_op jit(solution)/shard_map/reshape | solution.py:293
  91.7 1.0 add_convert_fusion.3
  93.6 1.5 %collective-permute-start.11 = (bf16[2,16,128]{2,1,0:T(8,128)(2,1)S(1)}, bf16[2,16,128]{2,1,0:T(8,128)(2,1)S(1)}, u32[]{:S(2)}, u32[]{:S(2)}) collective-permute-start(bf16[2,16,128]{2,1,0:T(8,128)(2,1)S(1)} %get-tuple-element.20), channel_id=1, source_target_pairs={{0,8},{8,16},{16,24},{24,0},{1,9},{9,17},{17,25},{25,1},{2,10},{10... | collective-permute-start | bytes 24584 | tf_op jit(solution)/shard_map/ppermute | solution.py:26
  95.1 1.0 collective-permute-start.16
  96.1 2.0 %collective-permute-start.12 = (bf16[2,16,128]{2,1,0:T(8,128)(2,1)S(1)}, bf16[2,16,128]{2,1,0:T(8,128)(2,1)S(1)}, u32[]{:S(2)}, u32[]{:S(2)}) collective-permute-start(bf16[2,16,128]{2,1,0:T(8,128)(2,1)S(1)} %get-tuple-element.19), channel_id=1, source_target_pairs={{8,0},{16,8},{24,16},{0,24},{9,1},{17,9},{25,17},{1,25},{10,2},{18... | collective-permute-start | bytes 24584 | tf_op jit(solution)/shard_map/ppermute | solution.py:27
  98.5 1.3 collective-permute-done.12
  100.0 1.3 collective-permute-start.17
  102.2 1.4 fusion.100
  103.6 5.4 %collective-permute-start.14 = (bf16[1,18,16640]{2,1,0:T(8,128)(2,1)}, bf16[1,18,16640]{2,1,0:T(8,128)(2,1)}, u32[]{:S(2)}, u32[]{:S(2)}) collective-permute-start(bf16[1,18,16640]{2,1,0:T(8,128)(2,1)} %get-tuple-element.16), channel_id=1, source_target_pairs={{0,1},{1,2},{2,3},{4,5},{5,6},{6,7},{8,9},{9,10},{10,11},{12,13},{... | collective-permute-start | bytes 1797128 | tf_op jit(solution)/shard_map/ppermute | solution.py:126
  109.0 1.3 collective-permute-start.15
  111.0 9.3 %shard_map.96.refs_2_ = f32[2,16,16384]{2,1,0:T(8,128)} custom-call(bf16[2,18,16640]{2,1,0:T(8,128)(2,1)} %copy-done.3, f32[27,8,128]{2,1,0:T(8,128)} %broadcast_in_dim.36.refs_1_.refs_4_), custom_call_target="tpu_custom_call" | custom-call | tf_op jit(solution)/shard_map/pallas_call | solution.py:181
  120.3 2.7 %collective-permute-start.19 = (bf16[64,1024]{1,0:T(8,128)(2,1)S(1)}, bf16[64,1024]{1,0:T(8,128)(2,1)S(1)}, u32[]{:S(2)}, u32[]{:S(2)}) collective-permute-start(bf16[64,1024]{1,0:T(8,128)(2,1)S(1)} %add_convert_fusion.2), channel_id=1, source_target_pairs={{0,1},{1,0},{2,3},{3,2},{4,5},{5,4},{6,7},{7,6},{8,9},{9,8},{10,11... | collective-permute-start | bytes 393224 | tf_op jit(solution)/shard_map/ppermute | solution.py:107
  123.8 9.7 %collective-permute-done.19 = bf16[64,1024]{1,0:T(8,128)(2,1)S(1)} collective-permute-done((bf16[64,1024]{1,0:T(8,128)(2,1)S(1)}, bf16[64,1024]{1,0:T(8,128)(2,1)S(1)}, u32[]{:S(2)}, u32[]{:S(2)}) %collective-permute-start.19) | collective-permute-done | bytes 131104 | tf_op jit(solution)/shard_map/ppermute | solution.py:107
  133.5 1.7 %collective-permute-start.20 = (bf16[64,1024]{1,0:T(8,128)(2,1)S(1)}, bf16[64,1024]{1,0:T(8,128)(2,1)S(1)}, u32[]{:S(2)}, u32[]{:S(2)}) collective-permute-start(bf16[64,1024]{1,0:T(8,128)(2,1)S(1)} %add_convert_fusion.1), channel_id=1, source_target_pairs={{0,2},{1,3},{2,0},{3,1},{4,6},{5,7},{6,4},{7,5},{8,10},{9,11},{10,... | collective-permute-start | bytes 393224 | tf_op jit(solution)/shard_map/ppermute | solution.py:107
  135.9 1.1 copy.38
  137.0 2.5 %reshape.96.refs_3_ = bf16[2,16,16384]{2,1,0:T(8,128)(2,1)} reshape(bf16[32,256,64]{2,1,0:T(8,128)(2,1)S(1)} %copy.38) | data formatting | bytes 2097152 | tf_op jit(solution)/shard_map/reshape | solution.py:311
  139.5 1.2 collective-permute-done.20
  141.7 6.9 %shard_map.97 = bf16[2,16,16384]{2,1,0:T(8,128)(2,1)} custom-call(bf16[1,18,16640]{2,1,0:T(8,128)(2,1)} %collective-permute-done.14.refs_0_, bf16[1,18,16640]{2,1,0:T(8,128)(2,1)} %collective-permute-done.15.refs_1_, f32[2,16,16384]{2,1,0:T(8,128)} %shard_map.96.refs_2_, bf16[2,16,16384]{2,1,0:T(8,128)(2,1)} %reshape.96.refs_3_, ...), custom_call_target="tpu_custom_call" | custom-call | tf_op jit(solution)/shard_map/pallas_call | solution.py:181
  (110 shorter events, 16.7 us)
Async XLA Ops:
  0.6 54.2 %copy-start = (bf16[64,256]{1,0:T(8,128)(2,1)S(1)}, bf16[64,256]{1,0:T(8,128)(2,1)}, u32[]{:S(2)}) copy-start(bf16[64,256]{1,0:T(8,128)(2,1)} %param.9) | copy-start | bytes 98308
  4.8 8.6 %copy-start.5 = (bf16[2,16,16384]{2,1,0:T(8,128)(2,1)S(1)}, bf16[2,16,16384]{2,1,0:T(8,128)(2,1)}, u32[]{:S(2)}) copy-start(bf16[2,16,16384]{2,1,0:T(8,128)(2,1)} %param.7) | copy-start | bytes 3145732
  5.0 18.4 %collective-permute-start = (f32[16,32,128]{2,0,1:T(8,128)S(1)}, f32[16,32,128]{2,0,1:T(8,128)}, u32[]{:S(2)}, u32[]{:S(2)}) collective-permute-start(f32[16,32,128]{2,0,1:T(8,128)S(1)} %fusion.16), channel_id=1, source_target_pairs={{0,16},{8,24},{16,0},{24,8},{1,17},{9,25},{17,1},{25,9},{2,18},{10... | collective-permute-start | bytes 786440 | tf_op jit(solution)/shard_map/ppermute | solution.py:90
  8.7 4.7 %collective-permute-start.2 = (bf16[2,16,128]{2,1,0:T(8,128)(2,1)S(1)}, bf16[2,16,128]{2,1,0:T(8,128)(2,1)S(1)}, u32[]{:S(2)}, u32[]{:S(2)}) collective-permute-start(bf16[2,16,128]{2,1,0:T(8,128)(2,1)S(1)} %get-tuple-element.22), channel_id=1, source_target_pairs={{0,8},{8,16},{16,24},{24,0},{1,9},{9,17},{17,25},{25,1},{2,10},{10... | collective-permute-start | bytes 24584 | tf_op jit(solution)/shard_map/ppermute | solution.py:26
  10.2 3.7 %collective-permute-start.3 = (bf16[2,16,128]{2,1,0:T(8,128)(2,1)S(1)}, bf16[2,16,128]{2,1,0:T(8,128)(2,1)S(1)}, u32[]{:S(2)}, u32[]{:S(2)}) collective-permute-start(bf16[2,16,128]{2,1,0:T(8,128)(2,1)S(1)} %get-tuple-element.21), channel_id=1, source_target_pairs={{8,0},{16,8},{24,16},{0,24},{9,1},{17,9},{25,17},{1,25},{10,2},{18... | collective-permute-start | bytes 24584 | tf_op jit(solution)/shard_map/ppermute | solution.py:27
  14.1 1.4 collective-permute-start.4
  16.3 8.1 %copy-start.2 = (bf16[2,18,16640]{2,1,0:T(8,128)(2,1)}, bf16[2,18,16640]{2,1,0:T(8,128)(2,1)S(1)}, u32[]{:S(2)}) copy-start(bf16[2,18,16640]{2,1,0:T(8,128)(2,1)S(1)} %pad_maximum_fusion.refs_0_) | copy-start | bytes 3594244
  16.4 10.3 %copy-start.7 = (bf16[2,16,16384]{2,1,0:T(8,128)(2,1)S(1)}, bf16[2,16,16384]{2,1,0:T(8,128)(2,1)}, u32[]{:S(2)}) copy-start(bf16[2,16,16384]{2,1,0:T(8,128)(2,1)} %param.13) | copy-start | bytes 3145732
  17.6 25.6 %collective-permute-start.5 = (bf16[1,18,16640]{2,1,0:T(8,128)(2,1)}, bf16[1,18,16640]{2,1,0:T(8,128)(2,1)}, u32[]{:S(2)}, u32[]{:S(2)}) collective-permute-start(bf16[1,18,16640]{2,1,0:T(8,128)(2,1)} %get-tuple-element.18), channel_id=1, source_target_pairs={{0,1},{1,2},{2,3},{4,5},{5,6},{6,7},{8,9},{9,10},{10,11},{12,13},{... | collective-permute-start | bytes 1797128 | tf_op jit(solution)/shard_map/ppermute | solution.py:126
  22.0 21.8 %collective-permute-start.6 = (bf16[1,18,16640]{2,1,0:T(8,128)(2,1)}, bf16[1,18,16640]{2,1,0:T(8,128)(2,1)}, u32[]{:S(2)}, u32[]{:S(2)}) collective-permute-start(bf16[1,18,16640]{2,1,0:T(8,128)(2,1)} %get-tuple-element.17), channel_id=1, source_target_pairs={{1,0},{2,1},{3,2},{5,4},{6,5},{7,6},{9,8},{10,9},{11,10},{13,12},{... | collective-permute-start | bytes 1797128 | tf_op jit(solution)/shard_map/ppermute | solution.py:127
  24.4 2.2 %copy-start.11 = (f32[16,32,128]{2,0,1:T(8,128)}, f32[16,32,128]{2,0,1:T(8,128)S(1)}, u32[]{:S(2)}) copy-start(f32[16,32,128]{2,0,1:T(8,128)S(1)} %fusion.18) | copy-start | bytes 786436
  25.2 16.9 %collective-permute-start.1 = (f32[8,32,128]{2,0,1:T(8,128)}, f32[8,32,128]{2,0,1:T(8,128)}, u32[]{:S(2)}, u32[]{:S(2)}) collective-permute-start(f32[8,32,128]{2,0,1:T(8,128)} %constant_dynamic-slice_fusion.1), channel_id=1, source_target_pairs={{0,8},{8,0},{16,24},{24,16},{1,9},{9,1},{17,25},{25,17},{2,10},{10... | collective-permute-start | bytes 393224 | tf_op jit(solution)/shard_map/ppermute | solution.py:90
  29.1 1.6 %copy-start.6 = (bf16[32,64,64]{2,1,0:T(8,128)(2,1)S(1)}, bf16[32,64,64]{2,1,0:T(8,128)(2,1)}, u32[]{:S(2)}) copy-start(bf16[32,64,64]{2,1,0:T(8,128)(2,1)} %param.12) | copy-start | bytes 786436
  29.2 1.8 %copy-start.14 = (bf16[27,64]{1,0:T(8,128)(2,1)S(1)}, bf16[27,64]{1,0:T(8,128)(2,1)}, u32[]{:S(2)}) copy-start(bf16[27,64]{1,0:T(8,128)(2,1)} %param.8) | copy-start | bytes 10372
  32.2 9.9 %copy-start.12 = (f32[16,32,128]{2,0,1:T(8,128)S(1)}, f32[16,32,128]{2,0,1:T(8,128)}, u32[]{:S(2)}) copy-start(f32[16,32,128]{2,0,1:T(8,128)} %copy-done.11) | copy-start | bytes 786436
  50.3 9.1 %collective-permute-start.7 = (bf16[8,32,128]{2,1,0:T(8,128)(2,1)S(1)}, bf16[8,32,128]{2,1,0:T(8,128)(2,1)S(1)}, u32[]{:S(2)}, u32[]{:S(2)}) collective-permute-start(bf16[8,32,128]{2,1,0:T(8,128)(2,1)S(1)} %convolution_convert_fusion.2), channel_id=1, source_target_pairs={{0,8},{8,0},{16,24},{24,16},{1,9},{9,1},{17,25},{25,17},{2,10},{10... | collective-permute-start | bytes 196616 | tf_op jit(solution)/shard_map/ppermute | solution.py:68
  54.9 1.2 copy-start.15
  56.1 3.3 %copy-start.4 = (f32[8192,256]{1,0:T(8,128)}, f32[8192,256]{1,0:T(8,128)S(1)}, u32[]{:S(2)}) copy-start(f32[8192,256]{1,0:T(8,128)S(1)} %fusion.106) | copy-start | bytes 25165828
  59.4 5.8 %copy-start.8 = (bf16[32,256,64]{1,2,0:T(8,128)(2,1)S(1)}, bf16[32,256,64]{1,2,0:T(8,128)(2,1)}, u32[]{:S(2)}) copy-start(bf16[32,256,64]{1,2,0:T(8,128)(2,1)} %copy.30) | copy-start | bytes 3145732
  59.4 5.0 %collective-permute-start.8 = (bf16[16,32,128]{2,1,0:T(8,128)(2,1)S(1)}, bf16[16,32,128]{2,1,0:T(8,128)(2,1)S(1)}, u32[]{:S(2)}, u32[]{:S(2)}) collective-permute-start(bf16[16,32,128]{2,1,0:T(8,128)(2,1)S(1)} %pad_maximum_fusion.3), channel_id=1, source_target_pairs={{0,16},{8,24},{16,0},{24,8},{1,17},{9,25},{17,1},{25,9},{2,18},{10... | collective-permute-start | bytes 393224 | tf_op jit(solution)/shard_map/ppermute | solution.py:68
  69.4 6.4 %collective-permute-start.9 = (f32[16,32,128]{2,0,1:T(8,128)S(1)}, f32[16,32,128]{2,0,1:T(8,128)S(1)}, u32[]{:S(2)}, u32[]{:S(2)}) collective-permute-start(f32[16,32,128]{2,0,1:T(8,128)S(1)} %fusion.13), channel_id=1, source_target_pairs={{0,16},{8,24},{16,0},{24,8},{1,17},{9,25},{17,1},{25,9},{2,18},{10... | collective-permute-start | bytes 786440 | tf_op jit(solution)/shard_map/ppermute | solution.py:90
  76.0 1.3 copy-start.13
  76.7 15.0 %collective-permute-start.10 = (f32[8,32,128]{2,0,1:T(8,128)}, f32[8,32,128]{2,0,1:T(8,128)}, u32[]{:S(2)}, u32[]{:S(2)}) collective-permute-start(f32[8,32,128]{2,0,1:T(8,128)} %constant_dynamic-slice_fusion), channel_id=1, source_target_pairs={{0,8},{8,0},{16,24},{24,16},{1,9},{9,1},{17,25},{25,17},{2,10},{10... | collective-permute-start | bytes 393224 | tf_op jit(solution)/shard_map/ppermute | solution.py:90
  77.3 7.9 %copy-start.9 = (bf16[32,256,64]{1,2,0:T(8,128)(2,1)S(1)}, bf16[32,256,64]{1,2,0:T(8,128)(2,1)}, u32[]{:S(2)}) copy-start(bf16[32,256,64]{1,2,0:T(8,128)(2,1)} %get-tuple-element.14) | copy-start | bytes 3145732
  86.2 2.5 %copy-start.10 = (bf16[8192,64]{0,1:T(8,128)(2,1)S(1)}, bf16[8192,64]{0,1:T(8,128)(2,1)}, u32[]{:S(2)}) copy-start(bf16[8192,64]{0,1:T(8,128)(2,1)} %convolution_convert_fusion) | copy-start | bytes 3145732
  93.6 4.8 %collective-permute-start.11 = (bf16[2,16,128]{2,1,0:T(8,128)(2,1)S(1)}, bf16[2,16,128]{2,1,0:T(8,128)(2,1)S(1)}, u32[]{:S(2)}, u32[]{:S(2)}) collective-permute-start(bf16[2,16,128]{2,1,0:T(8,128)(2,1)S(1)} %get-tuple-element.20), channel_id=1, source_target_pairs={{0,8},{8,16},{16,24},{24,0},{1,9},{9,17},{17,25},{25,1},{2,10},{10... | collective-permute-start | bytes 24584 | tf_op jit(solution)/shard_map/ppermute | solution.py:26
  95.1 4.9 %collective-permute-start.16 = (bf16[8,32,128]{2,1,0:T(8,128)(2,1)S(1)}, bf16[8,32,128]{2,1,0:T(8,128)(2,1)S(1)}, u32[]{:S(2)}, u32[]{:S(2)}) collective-permute-start(bf16[8,32,128]{2,1,0:T(8,128)(2,1)S(1)} %convolution_convert_fusion.1), channel_id=1, source_target_pairs={{0,8},{8,0},{16,24},{24,16},{1,9},{9,1},{17,25},{25,17},{2,10},{10... | collective-permute-start | bytes 196616 | tf_op jit(solution)/shard_map/ppermute | solution.py:68
  96.1 3.7 %collective-permute-start.12 = (bf16[2,16,128]{2,1,0:T(8,128)(2,1)S(1)}, bf16[2,16,128]{2,1,0:T(8,128)(2,1)S(1)}, u32[]{:S(2)}, u32[]{:S(2)}) collective-permute-start(bf16[2,16,128]{2,1,0:T(8,128)(2,1)S(1)} %get-tuple-element.19), channel_id=1, source_target_pairs={{8,0},{16,8},{24,16},{0,24},{9,1},{17,9},{25,17},{1,25},{10,2},{18... | collective-permute-start | bytes 24584 | tf_op jit(solution)/shard_map/ppermute | solution.py:27
  98.3 22.0 %collective-permute-start.18 = (bf16[64,1024]{1,0:T(8,128)(2,1)S(1)}, bf16[64,1024]{1,0:T(8,128)(2,1)S(1)}, u32[]{:S(2)}, u32[]{:S(2)}) collective-permute-start(bf16[64,1024]{1,0:T(8,128)(2,1)S(1)} %convert_element_type.143), channel_id=1, source_target_pairs={{0,4},{4,0},{1,5},{5,1},{2,6},{6,2},{3,7},{7,3},{8,12},{12,8},{9,1... | collective-permute-start | bytes 393224 | tf_op jit(solution)/shard_map/ppermute | solution.py:107
  99.9 1.5 collective-permute-start.13
  100.0 23.0 %collective-permute-start.17 = (bf16[16,32,128]{2,1,0:T(8,128)(2,1)S(1)}, bf16[16,32,128]{2,1,0:T(8,128)(2,1)S(1)}, u32[]{:S(2)}, u32[]{:S(2)}) collective-permute-start(bf16[16,32,128]{2,1,0:T(8,128)(2,1)S(1)} %pad_maximum_fusion.4), channel_id=1, source_target_pairs={{0,16},{8,24},{16,0},{24,8},{1,17},{9,25},{17,1},{25,9},{2,18},{10... | collective-permute-start | bytes 393224 | tf_op jit(solution)/shard_map/ppermute | solution.py:68
  102.2 8.7 %copy-start.3 = (bf16[2,18,16640]{2,1,0:T(8,128)(2,1)}, bf16[2,18,16640]{2,1,0:T(8,128)(2,1)S(1)}, u32[]{:S(2)}) copy-start(bf16[2,18,16640]{2,1,0:T(8,128)(2,1)S(1)} %pad_maximum_fusion.1.refs_0_) | copy-start | bytes 3594244
  103.6 38.1 %collective-permute-start.14 = (bf16[1,18,16640]{2,1,0:T(8,128)(2,1)}, bf16[1,18,16640]{2,1,0:T(8,128)(2,1)}, u32[]{:S(2)}, u32[]{:S(2)}) collective-permute-start(bf16[1,18,16640]{2,1,0:T(8,128)(2,1)} %get-tuple-element.16), channel_id=1, source_target_pairs={{0,1},{1,2},{2,3},{4,5},{5,6},{6,7},{8,9},{9,10},{10,11},{12,13},{... | collective-permute-start | bytes 1797128 | tf_op jit(solution)/shard_map/ppermute | solution.py:126
  109.0 32.7 %collective-permute-start.15 = (bf16[1,18,16640]{2,1,0:T(8,128)(2,1)}, bf16[1,18,16640]{2,1,0:T(8,128)(2,1)}, u32[]{:S(2)}, u32[]{:S(2)}) collective-permute-start(bf16[1,18,16640]{2,1,0:T(8,128)(2,1)} %get-tuple-element.15), channel_id=1, source_target_pairs={{1,0},{2,1},{3,2},{5,4},{6,5},{7,6},{9,8},{10,9},{11,10},{13,12},{... | collective-permute-start | bytes 1797128 | tf_op jit(solution)/shard_map/ppermute | solution.py:127
  120.3 13.2 %collective-permute-start.19 = (bf16[64,1024]{1,0:T(8,128)(2,1)S(1)}, bf16[64,1024]{1,0:T(8,128)(2,1)S(1)}, u32[]{:S(2)}, u32[]{:S(2)}) collective-permute-start(bf16[64,1024]{1,0:T(8,128)(2,1)S(1)} %add_convert_fusion.2), channel_id=1, source_target_pairs={{0,1},{1,0},{2,3},{3,2},{4,5},{5,4},{6,7},{7,6},{8,9},{9,8},{10,11... | collective-permute-start | bytes 393224 | tf_op jit(solution)/shard_map/ppermute | solution.py:107
  133.5 7.2 %collective-permute-start.20 = (bf16[64,1024]{1,0:T(8,128)(2,1)S(1)}, bf16[64,1024]{1,0:T(8,128)(2,1)S(1)}, u32[]{:S(2)}, u32[]{:S(2)}) collective-permute-start(bf16[64,1024]{1,0:T(8,128)(2,1)S(1)} %add_convert_fusion.1), channel_id=1, source_target_pairs={{0,2},{1,3},{2,0},{3,1},{4,6},{5,7},{6,4},{7,5},{8,10},{9,11},{10,... | collective-permute-start | bytes 393224 | tf_op jit(solution)/shard_map/ppermute | solution.py:107
  140.7 7.9 %copy-start.1 = (bf16[64,256]{1,0:T(8,128)(2,1)S(1)}, bf16[64,256]{1,0:T(8,128)(2,1)}, u32[]{:S(2)}) copy-start(bf16[64,256]{1,0:T(8,128)(2,1)} %param.9) | copy-start | bytes 98308

commit v26 on v22

--- a/solution.py
+++ b/solution.py
@@ -198,7 +198,8 @@
         tuple((0, plane + step_z - 1, step_z) for step_z in range(3) if 0 <= plane + step_z - 1 < planes)
         for plane in range(planes)
     )
-    local = stencil_call(local_plan, (inner,), (), gains, y_cells, lanes, channels, jnp.bfloat16)
+    local_dtype = jnp.bfloat16 if flipped else jnp.float32
+    local = stencil_call(local_plan, (inner,), (), gains, y_cells, lanes, channels, local_dtype)
     rim_plan = tuple(
         ((((0, 0, 0),) if plane == 0 else ()) + (((1, 0, 2),) if plane == planes - 1 else ()))
         for plane in range(planes)

time: 149 us -> 149 us (level)
  transfers between devices with their start and end apart: 21 -> 21, of which waited for: 9 -> 10; matrix products, arithmetic and copies ran while one was open for 30% -> 30% of each run, Pallas kernels for 12% -> 13%
where the time goes in v26:
time: 149 us
  starting transfers between devices  35.3 us (24%)
  Pallas kernels  32.4 us (22%)
  local copies, waits for them, and re-layouts  29.9 us (20%)
  waiting for transfers between devices  23.4 us (16%)
  matrix products  19.6 us (13%)
  other arithmetic  7.28 us (5%)
    pallas_call x4, Pallas kernels, stencil_call(): pl.pallas_call(kernel, out_shape=jax.ShapeDtypeStruct((len(plan), y_cells...  32.4 us
    ppermute x3, waiting for transfers between devices, butterfly_sum(): lax.ppermute(value, axis, [(i, i ^ step) for i in range(size)])  10.9 us
    ppermute x2, starting transfers between devices, spatial_rims(): below = lax.ppermute(inner[-1:], 'gz', up)  9.83 us
    dot_general x1, matrix products, per_device(): jnp.dot(grad_hidden, expand_weight.T, preferred_element_type=jnp.float32)  7.88 us
    ppermute x4, starting transfers between devices, ring_reduce_scatter(): lax.ppermute(send, axis, [(i, i ^ step) for i in range(size)])  6.66 us
    ppermute x4, starting transfers between devices, ring_gather(): lax.ppermute(block, axis, [(i, i ^ step) for i in range(size)])  5.36 us
    ppermute x3, starting transfers between devices, butterfly_sum(): lax.ppermute(value, axis, [(i, i ^ step) for i in range(size)])  4.55 us
    ppermute x4, waiting for transfers between devices, ring_reduce_scatter(): lax.ppermute(send, axis, [(i, i ^ step) for i in range(size)])  3.69 us
  transfers between devices with their start and end apart: 21, of which 10 were waited for; matrix products, arithmetic and copies ran while one was open for 30% of the time, Pallas kernels for 13%

profile of v26, /device:TPU:0, one launch (start us, length us, event | category | flops | bytes accessed | tf_op | source)
XLA Modules:
  0.0 149.0 jit_solution(7891007567351579769)
XLA Ops:
  0.7 3.0 %reshape.89 = bf16[32,256,64]{2,1,0:T(8,128)(2,1)S(1)} reshape(bf16[2,16,16384]{2,1,0:T(8,128)(2,1)} %param.7) | data formatting | bytes 2097152 | tf_op jit(solution)/shard_map/reshape | solution.py:262
  5.0 3.0 %collective-permute-start = (f32[16,32,128]{2,0,1:T(8,128)S(1)}, f32[16,32,128]{2,0,1:T(8,128)}, u32[]{:S(2)}, u32[]{:S(2)}) collective-permute-start(f32[16,32,128]{2,0,1:T(8,128)S(1)} %fusion.16), channel_id=1, source_target_pairs={{0,16},{8,24},{16,0},{24,8},{1,17},{9,25},{17,1},{25,9},{2,18},{10... | collective-permute-start | bytes 786440 | tf_op jit(solution)/shard_map/ppermute | solution.py:90
  8.7 1.5 %collective-permute-start.2 = (bf16[2,16,128]{2,1,0:T(8,128)(2,1)S(1)}, bf16[2,16,128]{2,1,0:T(8,128)(2,1)S(1)}, u32[]{:S(2)}, u32[]{:S(2)}) collective-permute-start(bf16[2,16,128]{2,1,0:T(8,128)(2,1)S(1)} %get-tuple-element.22), channel_id=1, source_target_pairs={{0,8},{8,16},{16,24},{24,0},{1,9},{9,17},{17,25},{25,1},{2,10},{10... | collective-permute-start | bytes 24584 | tf_op jit(solution)/shard_map/ppermute | solution.py:26
  10.2 1.4 collective-permute-start.3
  11.7 1.7 %collective-permute-done.2 = bf16[2,16,128]{2,1,0:T(8,128)(2,1)S(1)} collective-permute-done((bf16[2,16,128]{2,1,0:T(8,128)(2,1)S(1)}, bf16[2,16,128]{2,1,0:T(8,128)(2,1)S(1)}, u32[]{:S(2)}, u32[]{:S(2)}) %collective-permute-start.2) | collective-permute-done | bytes 8224 | tf_op jit(solution)/shard_map/ppermute | solution.py:26
  14.3 1.2 collective-permute-done.4
  16.4 1.3 fusion.101
  17.6 4.4 %collective-permute-start.5 = (bf16[1,18,16640]{2,1,0:T(8,128)(2,1)}, bf16[1,18,16640]{2,1,0:T(8,128)(2,1)}, u32[]{:S(2)}, u32[]{:S(2)}) collective-permute-start(bf16[1,18,16640]{2,1,0:T(8,128)(2,1)} %get-tuple-element.18), channel_id=1, source_target_pairs={{0,1},{1,2},{2,3},{4,5},{5,6},{6,7},{8,9},{9,10},{10,11},{12,13},{... | collective-permute-start | bytes 1797128 | tf_op jit(solution)/shard_map/ppermute | solution.py:126
  22.0 1.3 collective-permute-start.6
  23.3 1.1 fusion.18
  25.2 1.5 collective-permute-start.1
  26.7 2.5 %reshape.93 = bf16[32,256,64]{2,1,0:T(8,128)(2,1)S(1)} reshape(bf16[2,16,16384]{2,1,0:T(8,128)(2,1)S(1)} %copy-done.7) | data formatting | bytes 2097152 | tf_op jit(solution)/shard_map/reshape | solution.py:282
  29.2 1.6 %copy.30 = bf16[32,256,64]{1,2,0:T(8,128)(2,1)} copy(bf16[32,256,64]{2,1,0:T(8,128)(2,1)S(1)} %reshape.93) | data formatting | bytes 2097152 | tf_op jit(solution)/shard_map/optimization_barrier | solution.py:282
  31.0 1.1 fusion.20
  32.8 9.6 %shard_map.94.refs_2_ = f32[2,16,16384]{2,1,0:T(8,128)} custom-call(bf16[2,18,16640]{2,1,0:T(8,128)(2,1)} %copy-done.2, f32[27,8,128]{2,1,0:T(8,128)} %broadcast_in_dim.18.refs_1_.refs_3_), custom_call_target="tpu_custom_call" | custom-call | tf_op jit(solution)/shard_map/pallas_call | solution.py:181
  43.8 6.7 %shard_map.95 = bf16[2,16,16384]{2,1,0:T(8,128)(2,1)} custom-call(bf16[1,18,16640]{2,1,0:T(8,128)(2,1)} %collective-permute-done.5.refs_0_, bf16[1,18,16640]{2,1,0:T(8,128)(2,1)} %collective-permute-done.6.refs_1_, f32[2,16,16384]{2,1,0:T(8,128)} %shard_map.94.refs_2_, f32[27,8,128]{2,1,0:T(8,128)} %broadcast_in_dim.18.refs_1_.refs_3_), custom_call_target="tpu_custom_call" | custom-call | tf_op jit(solution)/shard_map/pallas_call | solution.py:181
  50.6 1.5 collective-permute-start.7
  52.0 3.0 %reshape.90 = bf16[8192,64]{1,0:T(8,128)(2,1)S(1)} reshape(bf16[2,16,16384]{2,1,0:T(8,128)(2,1)} %shard_map.95) | data formatting | bytes 2097152 | tf_op jit(solution)/shard_map/reshape | solution.py:271
  55.1 1.2 fusion.106
  56.4 2.8 %fusion.5 = f32[8192,64]{0,1:T(8,128)S(1)} fusion(bf16[256,64]{0,1:T(8,128)(2,1)S(1)} %copy-done.15, f32[8192,256]{1,0:T(8,128)S(1)} %fusion.106), kind=kOutput, calls=%fused_computation.10 | convolution fusion | flops 278921216 | bytes 10518528 | tf_op jit(solution)/shard_map/dot_general | solution.py:274
  59.6 1.6 %collective-permute-start.8 = (bf16[16,32,128]{2,1,0:T(8,128)(2,1)S(1)}, bf16[16,32,128]{2,1,0:T(8,128)(2,1)S(1)}, u32[]{:S(2)}, u32[]{:S(2)}) collective-permute-start(bf16[16,32,128]{2,1,0:T(8,128)(2,1)S(1)} %pad_maximum_fusion.3), channel_id=1, source_target_pairs={{0,16},{8,24},{16,0},{24,8},{1,17},{9,25},{17,1},{25,9},{2,18},{10... | collective-permute-start | bytes 393224 | tf_op jit(solution)/shard_map/ppermute | solution.py:68
  61.3 3.4 %collective-permute-done.8 = bf16[16,32,128]{2,1,0:T(8,128)(2,1)S(1)} collective-permute-done((bf16[16,32,128]{2,1,0:T(8,128)(2,1)S(1)}, bf16[16,32,128]{2,1,0:T(8,128)(2,1)S(1)}, u32[]{:S(2)}, u32[]{:S(2)}) %collective-permute-start.8) | collective-permute-done | bytes 131104 | tf_op jit(solution)/shard_map/ppermute | solution.py:68
  65.5 2.7 %fusion.11 = (bf16[32,256,64]{1,2,0:T(8,128)(2,1)S(1)}, bf16[32,256,64]{1,2,0:T(8,128)(2,1)}) fusion(bf16[32,256,64]{1,2,0:T(8,128)(2,1)S(1)} %copy-done.8, f32[256,32,64]{0,2,1:T(8,128)S(1)} %fusion.27, bf16[32,32,64]{2,1,0:T(8,128)(2,1)S(1)} %get-tuple-element.27, f32[32]{0:T(128)S(1)} %get-tuple-element.33, s32[32]{0:T(128)S(1)} %add.135, ...), kind=kOutput, calls=%fused_computation.17 | convolution fusion | flops 41566208 | bytes 7472384 | tf_op jit(solution)/shard_map/krc,xk->rxc/dot_general | solution.py:219
  69.6 1.6 %collective-permute-start.9 = (f32[16,32,128]{2,0,1:T(8,128)S(1)}, f32[16,32,128]{2,0,1:T(8,128)S(1)}, u32[]{:S(2)}, u32[]{:S(2)}) collective-permute-start(f32[16,32,128]{2,0,1:T(8,128)S(1)} %fusion.13), channel_id=1, source_target_pairs={{0,16},{8,24},{16,0},{24,8},{1,17},{9,25},{17,1},{25,9},{2,18},{10... | collective-permute-start | bytes 786440 | tf_op jit(solution)/shard_map/ppermute | solution.py:90
  71.3 1.0 copy.42
  72.4 3.7 %collective-permute-done.9 = f32[16,32,128]{2,0,1:T(8,128)S(1)} collective-permute-done((f32[16,32,128]{2,0,1:T(8,128)S(1)}, f32[16,32,128]{2,0,1:T(8,128)S(1)}, u32[]{:S(2)}, u32[]{:S(2)}) %collective-permute-start.9) | collective-permute-done | bytes 262176 | tf_op jit(solution)/shard_map/ppermute | solution.py:90
  77.5 7.9 %convolution_convert_fusion = bf16[8192,64]{0,1:T(8,128)(2,1)} fusion(bf16[64,256]{1,0:T(8,128)(2,1)S(1)} %copy-done, bf16[8192,64]{0,1:T(8,128)(2,1)} %bitcast.54, bf16[256,64]{0,1:T(8,128)(2,1)} %param.10, f32[8192,256]{1,0:T(8,128)} %copy-done.4), kind=kOutput, calls=%fused_computation.3 | convolution fusion | flops 558366720 | bytes 10551296 | tf_op jit(solution)/shard_map/dot_general | solution.py:291
  85.4 1.1 copy.29
  86.5 2.5 %reshape.92 = bf16[2,16,16384]{2,1,0:T(8,128)(2,1)} reshape(bf16[32,256,64]{2,1,0:T(8,128)(2,1)S(1)} %copy.29) | data formatting | bytes 2097152 | tf_op jit(solution)/shard_map/reshape | solution.py:280
  89.0 1.1 copy.35
  90.0 1.9 %reshape.95 = bf16[2,16,16384]{2,1,0:T(8,128)(2,1)S(1)} reshape(bf16[8192,64]{1,0:T(8,128)(2,1)S(1)} %copy.35) | data formatting | bytes 2097152 | tf_op jit(solution)/shard_map/reshape | solution.py:294
  92.0 1.0 add_convert_fusion.3
  93.8 1.5 %collective-permute-start.11 = (bf16[2,16,128]{2,1,0:T(8,128)(2,1)S(1)}, bf16[2,16,128]{2,1,0:T(8,128)(2,1)S(1)}, u32[]{:S(2)}, u32[]{:S(2)}) collective-permute-start(bf16[2,16,128]{2,1,0:T(8,128)(2,1)S(1)} %get-tuple-element.20), channel_id=1, source_target_pairs={{0,8},{8,16},{16,24},{24,0},{1,9},{9,17},{17,25},{25,1},{2,10},{10... | collective-permute-start | bytes 24584 | tf_op jit(solution)/shard_map/ppermute | solution.py:26
  95.3 1.3 collective-permute-start.16
  96.6 1.7 %collective-permute-start.12 = (bf16[2,16,128]{2,1,0:T(8,128)(2,1)S(1)}, bf16[2,16,128]{2,1,0:T(8,128)(2,1)S(1)}, u32[]{:S(2)}, u32[]{:S(2)}) collective-permute-start(bf16[2,16,128]{2,1,0:T(8,128)(2,1)S(1)} %get-tuple-element.19), channel_id=1, source_target_pairs={{8,0},{16,8},{24,16},{0,24},{9,1},{17,9},{25,17},{1,25},{10,2},{18... | collective-permute-start | bytes 24584 | tf_op jit(solution)/shard_map/ppermute | solution.py:27
  98.7 1.5 %collective-permute-done.12 = bf16[2,16,128]{2,1,0:T(8,128)(2,1)S(1)} collective-permute-done((bf16[2,16,128]{2,1,0:T(8,128)(2,1)S(1)}, bf16[2,16,128]{2,1,0:T(8,128)(2,1)S(1)}, u32[]{:S(2)}, u32[]{:S(2)}) %collective-permute-start.12) | collective-permute-done | bytes 8224 | tf_op jit(solution)/shard_map/ppermute | solution.py:27
  100.6 1.0 collective-permute-start.17
  102.7 1.4 fusion.100
  104.1 5.4 %collective-permute-start.14 = (bf16[1,18,16640]{2,1,0:T(8,128)(2,1)}, bf16[1,18,16640]{2,1,0:T(8,128)(2,1)}, u32[]{:S(2)}, u32[]{:S(2)}) collective-permute-start(bf16[1,18,16640]{2,1,0:T(8,128)(2,1)} %get-tuple-element.16), channel_id=1, source_target_pairs={{0,1},{1,2},{2,3},{4,5},{5,6},{6,7},{8,9},{9,10},{10,11},{12,13},{... | collective-permute-start | bytes 1797128 | tf_op jit(solution)/shard_map/ppermute | solution.py:126
  109.5 1.3 collective-permute-start.15
  111.5 9.2 %shard_map.96.refs_2_ = bf16[2,16,16384]{2,1,0:T(8,128)(2,1)} custom-call(bf16[2,18,16640]{2,1,0:T(8,128)(2,1)} %copy-done.3, f32[27,8,128]{2,1,0:T(8,128)} %broadcast_in_dim.36.refs_1_.refs_4_), custom_call_target="tpu_custom_call" | custom-call | tf_op jit(solution)/shard_map/pallas_call | solution.py:181
  120.8 2.7 %collective-permute-start.19 = (bf16[64,1024]{1,0:T(8,128)(2,1)S(1)}, bf16[64,1024]{1,0:T(8,128)(2,1)S(1)}, u32[]{:S(2)}, u32[]{:S(2)}) collective-permute-start(bf16[64,1024]{1,0:T(8,128)(2,1)S(1)} %add_convert_fusion.2), channel_id=1, source_target_pairs={{0,1},{1,0},{2,3},{3,2},{4,5},{5,4},{6,7},{7,6},{8,9},{9,8},{10,11... | collective-permute-start | bytes 393224 | tf_op jit(solution)/shard_map/ppermute | solution.py:107
  124.3 9.7 %collective-permute-done.19 = bf16[64,1024]{1,0:T(8,128)(2,1)S(1)} collective-permute-done((bf16[64,1024]{1,0:T(8,128)(2,1)S(1)}, bf16[64,1024]{1,0:T(8,128)(2,1)S(1)}, u32[]{:S(2)}, u32[]{:S(2)}) %collective-permute-start.19) | collective-permute-done | bytes 131104 | tf_op jit(solution)/shard_map/ppermute | solution.py:107
  134.0 1.8 %collective-permute-start.20 = (bf16[64,1024]{1,0:T(8,128)(2,1)S(1)}, bf16[64,1024]{1,0:T(8,128)(2,1)S(1)}, u32[]{:S(2)}, u32[]{:S(2)}) collective-permute-start(bf16[64,1024]{1,0:T(8,128)(2,1)S(1)} %add_convert_fusion.1), channel_id=1, source_target_pairs={{0,2},{1,3},{2,0},{3,1},{4,6},{5,7},{6,4},{7,5},{8,10},{9,11},{10,... | collective-permute-start | bytes 393224 | tf_op jit(solution)/shard_map/ppermute | solution.py:107
  136.4 1.1 copy.38
  137.5 2.5 %reshape.96.refs_3_ = bf16[2,16,16384]{2,1,0:T(8,128)(2,1)} reshape(bf16[32,256,64]{2,1,0:T(8,128)(2,1)S(1)} %copy.38) | data formatting | bytes 2097152 | tf_op jit(solution)/shard_map/reshape | solution.py:312
  140.0 1.2 collective-permute-done.20
  142.2 6.8 %shard_map.97 = bf16[2,16,16384]{2,1,0:T(8,128)(2,1)} custom-call(bf16[1,18,16640]{2,1,0:T(8,128)(2,1)} %collective-permute-done.14.refs_0_, bf16[1,18,16640]{2,1,0:T(8,128)(2,1)} %collective-permute-done.15.refs_1_, bf16[2,16,16384]{2,1,0:T(8,128)(2,1)} %shard_map.96.refs_2_, bf16[2,16,16384]{2,1,0:T(8,128)(2,1)} %reshape.96.refs_3_, ...), custom_call_target="tpu_custom_call" | custom-call | tf_op jit(solution)/shard_map/pallas_call | solution.py:181
  (110 shorter events, 16.7 us)
Async XLA Ops:
  0.6 54.5 %copy-start = (bf16[64,256]{1,0:T(8,128)(2,1)S(1)}, bf16[64,256]{1,0:T(8,128)(2,1)}, u32[]{:S(2)}) copy-start(bf16[64,256]{1,0:T(8,128)(2,1)} %param.9) | copy-start | bytes 98308
  4.8 8.6 %copy-start.5 = (bf16[2,16,16384]{2,1,0:T(8,128)(2,1)S(1)}, bf16[2,16,16384]{2,1,0:T(8,128)(2,1)}, u32[]{:S(2)}) copy-start(bf16[2,16,16384]{2,1,0:T(8,128)(2,1)} %param.7) | copy-start | bytes 3145732
  5.0 18.4 %collective-permute-start = (f32[16,32,128]{2,0,1:T(8,128)S(1)}, f32[16,32,128]{2,0,1:T(8,128)}, u32[]{:S(2)}, u32[]{:S(2)}) collective-permute-start(f32[16,32,128]{2,0,1:T(8,128)S(1)} %fusion.16), channel_id=1, source_target_pairs={{0,16},{8,24},{16,0},{24,8},{1,17},{9,25},{17,1},{25,9},{2,18},{10... | collective-permute-start | bytes 786440 | tf_op jit(solution)/shard_map/ppermute | solution.py:90
  8.7 4.7 %collective-permute-start.2 = (bf16[2,16,128]{2,1,0:T(8,128)(2,1)S(1)}, bf16[2,16,128]{2,1,0:T(8,128)(2,1)S(1)}, u32[]{:S(2)}, u32[]{:S(2)}) collective-permute-start(bf16[2,16,128]{2,1,0:T(8,128)(2,1)S(1)} %get-tuple-element.22), channel_id=1, source_target_pairs={{0,8},{8,16},{16,24},{24,0},{1,9},{9,17},{17,25},{25,1},{2,10},{10... | collective-permute-start | bytes 24584 | tf_op jit(solution)/shard_map/ppermute | solution.py:26
  10.2 3.7 %collective-permute-start.3 = (bf16[2,16,128]{2,1,0:T(8,128)(2,1)S(1)}, bf16[2,16,128]{2,1,0:T(8,128)(2,1)S(1)}, u32[]{:S(2)}, u32[]{:S(2)}) collective-permute-start(bf16[2,16,128]{2,1,0:T(8,128)(2,1)S(1)} %get-tuple-element.21), channel_id=1, source_target_pairs={{8,0},{16,8},{24,16},{0,24},{9,1},{17,9},{25,17},{1,25},{10,2},{18... | collective-permute-start | bytes 24584 | tf_op jit(solution)/shard_map/ppermute | solution.py:27
  14.1 1.4 collective-permute-start.4
  16.3 8.1 %copy-start.2 = (bf16[2,18,16640]{2,1,0:T(8,128)(2,1)}, bf16[2,18,16640]{2,1,0:T(8,128)(2,1)S(1)}, u32[]{:S(2)}) copy-start(bf16[2,18,16640]{2,1,0:T(8,128)(2,1)S(1)} %pad_maximum_fusion.refs_0_) | copy-start | bytes 3594244
  16.4 10.3 %copy-start.7 = (bf16[2,16,16384]{2,1,0:T(8,128)(2,1)S(1)}, bf16[2,16,16384]{2,1,0:T(8,128)(2,1)}, u32[]{:S(2)}) copy-start(bf16[2,16,16384]{2,1,0:T(8,128)(2,1)} %param.13) | copy-start | bytes 3145732
  17.6 25.9 %collective-permute-start.5 = (bf16[1,18,16640]{2,1,0:T(8,128)(2,1)}, bf16[1,18,16640]{2,1,0:T(8,128)(2,1)}, u32[]{:S(2)}, u32[]{:S(2)}) collective-permute-start(bf16[1,18,16640]{2,1,0:T(8,128)(2,1)} %get-tuple-element.18), channel_id=1, source_target_pairs={{0,1},{1,2},{2,3},{4,5},{5,6},{6,7},{8,9},{9,10},{10,11},{12,13},{... | collective-permute-start | bytes 1797128 | tf_op jit(solution)/shard_map/ppermute | solution.py:126
  22.0 21.8 %collective-permute-start.6 = (bf16[1,18,16640]{2,1,0:T(8,128)(2,1)}, bf16[1,18,16640]{2,1,0:T(8,128)(2,1)}, u32[]{:S(2)}, u32[]{:S(2)}) collective-permute-start(bf16[1,18,16640]{2,1,0:T(8,128)(2,1)} %get-tuple-element.17), channel_id=1, source_target_pairs={{1,0},{2,1},{3,2},{5,4},{6,5},{7,6},{9,8},{10,9},{11,10},{13,12},{... | collective-permute-start | bytes 1797128 | tf_op jit(solution)/shard_map/ppermute | solution.py:127
  24.4 2.2 %copy-start.11 = (f32[16,32,128]{2,0,1:T(8,128)}, f32[16,32,128]{2,0,1:T(8,128)S(1)}, u32[]{:S(2)}) copy-start(f32[16,32,128]{2,0,1:T(8,128)S(1)} %fusion.18) | copy-start | bytes 786436
  25.2 17.2 %collective-permute-start.1 = (f32[8,32,128]{2,0,1:T(8,128)}, f32[8,32,128]{2,0,1:T(8,128)}, u32[]{:S(2)}, u32[]{:S(2)}) collective-permute-start(f32[8,32,128]{2,0,1:T(8,128)} %constant_dynamic-slice_fusion.1), channel_id=1, source_target_pairs={{0,8},{8,0},{16,24},{24,16},{1,9},{9,1},{17,25},{25,17},{2,10},{10... | collective-permute-start | bytes 393224 | tf_op jit(solution)/shard_map/ppermute | solution.py:90
  29.1 1.6 %copy-start.6 = (bf16[32,64,64]{2,1,0:T(8,128)(2,1)S(1)}, bf16[32,64,64]{2,1,0:T(8,128)(2,1)}, u32[]{:S(2)}) copy-start(bf16[32,64,64]{2,1,0:T(8,128)(2,1)} %param.12) | copy-start | bytes 786436
  29.2 1.8 %copy-start.14 = (bf16[27,64]{1,0:T(8,128)(2,1)S(1)}, bf16[27,64]{1,0:T(8,128)(2,1)}, u32[]{:S(2)}) copy-start(bf16[27,64]{1,0:T(8,128)(2,1)} %param.8) | copy-start | bytes 10372
  32.2 10.2 %copy-start.12 = (f32[16,32,128]{2,0,1:T(8,128)S(1)}, f32[16,32,128]{2,0,1:T(8,128)}, u32[]{:S(2)}) copy-start(f32[16,32,128]{2,0,1:T(8,128)} %copy-done.11) | copy-start | bytes 786436
  50.6 9.1 %collective-permute-start.7 = (bf16[8,32,128]{2,1,0:T(8,128)(2,1)S(1)}, bf16[8,32,128]{2,1,0:T(8,128)(2,1)S(1)}, u32[]{:S(2)}, u32[]{:S(2)}) collective-permute-start(bf16[8,32,128]{2,1,0:T(8,128)(2,1)S(1)} %convolution_convert_fusion.2), channel_id=1, source_target_pairs={{0,8},{8,0},{16,24},{24,16},{1,9},{9,1},{17,25},{25,17},{2,10},{10... | collective-permute-start | bytes 196616 | tf_op jit(solution)/shard_map/ppermute | solution.py:68
  55.1 1.2 copy-start.15
  56.3 3.3 %copy-start.4 = (f32[8192,256]{1,0:T(8,128)}, f32[8192,256]{1,0:T(8,128)S(1)}, u32[]{:S(2)}) copy-start(f32[8192,256]{1,0:T(8,128)S(1)} %fusion.106) | copy-start | bytes 25165828
  59.6 5.8 %copy-start.8 = (bf16[32,256,64]{1,2,0:T(8,128)(2,1)S(1)}, bf16[32,256,64]{1,2,0:T(8,128)(2,1)}, u32[]{:S(2)}) copy-start(bf16[32,256,64]{1,2,0:T(8,128)(2,1)} %copy.30) | copy-start | bytes 3145732
  59.6 5.0 %collective-permute-start.8 = (bf16[16,32,128]{2,1,0:T(8,128)(2,1)S(1)}, bf16[16,32,128]{2,1,0:T(8,128)(2,1)S(1)}, u32[]{:S(2)}, u32[]{:S(2)}) collective-permute-start(bf16[16,32,128]{2,1,0:T(8,128)(2,1)S(1)} %pad_maximum_fusion.3), channel_id=1, source_target_pairs={{0,16},{8,24},{16,0},{24,8},{1,17},{9,25},{17,1},{25,9},{2,18},{10... | collective-permute-start | bytes 393224 | tf_op jit(solution)/shard_map/ppermute | solution.py:68
  69.6 6.4 %collective-permute-start.9 = (f32[16,32,128]{2,0,1:T(8,128)S(1)}, f32[16,32,128]{2,0,1:T(8,128)S(1)}, u32[]{:S(2)}, u32[]{:S(2)}) collective-permute-start(f32[16,32,128]{2,0,1:T(8,128)S(1)} %fusion.13), channel_id=1, source_target_pairs={{0,16},{8,24},{16,0},{24,8},{1,17},{9,25},{17,1},{25,9},{2,18},{10... | collective-permute-start | bytes 786440 | tf_op jit(solution)/shard_map/ppermute | solution.py:90
  76.2 1.3 copy-start.13
  77.0 15.0 %collective-permute-start.10 = (f32[8,32,128]{2,0,1:T(8,128)}, f32[8,32,128]{2,0,1:T(8,128)}, u32[]{:S(2)}, u32[]{:S(2)}) collective-permute-start(f32[8,32,128]{2,0,1:T(8,128)} %constant_dynamic-slice_fusion), channel_id=1, source_target_pairs={{0,8},{8,0},{16,24},{24,16},{1,9},{9,1},{17,25},{25,17},{2,10},{10... | collective-permute-start | bytes 393224 | tf_op jit(solution)/shard_map/ppermute | solution.py:90
  77.5 7.9 %copy-start.9 = (bf16[32,256,64]{1,2,0:T(8,128)(2,1)S(1)}, bf16[32,256,64]{1,2,0:T(8,128)(2,1)}, u32[]{:S(2)}) copy-start(bf16[32,256,64]{1,2,0:T(8,128)(2,1)} %get-tuple-element.14) | copy-start | bytes 3145732
  86.5 2.5 %copy-start.10 = (bf16[8192,64]{0,1:T(8,128)(2,1)S(1)}, bf16[8192,64]{0,1:T(8,128)(2,1)}, u32[]{:S(2)}) copy-start(bf16[8192,64]{0,1:T(8,128)(2,1)} %convolution_convert_fusion) | copy-start | bytes 3145732
  93.8 4.8 %collective-permute-start.11 = (bf16[2,16,128]{2,1,0:T(8,128)(2,1)S(1)}, bf16[2,16,128]{2,1,0:T(8,128)(2,1)S(1)}, u32[]{:S(2)}, u32[]{:S(2)}) collective-permute-start(bf16[2,16,128]{2,1,0:T(8,128)(2,1)S(1)} %get-tuple-element.20), channel_id=1, source_target_pairs={{0,8},{8,16},{16,24},{24,0},{1,9},{9,17},{17,25},{25,1},{2,10},{10... | collective-permute-start | bytes 24584 | tf_op jit(solution)/shard_map/ppermute | solution.py:26
  95.3 5.2 %collective-permute-start.16 = (bf16[8,32,128]{2,1,0:T(8,128)(2,1)S(1)}, bf16[8,32,128]{2,1,0:T(8,128)(2,1)S(1)}, u32[]{:S(2)}, u32[]{:S(2)}) collective-permute-start(bf16[8,32,128]{2,1,0:T(8,128)(2,1)S(1)} %convolution_convert_fusion.1), channel_id=1, source_target_pairs={{0,8},{8,0},{16,24},{24,16},{1,9},{9,1},{17,25},{25,17},{2,10},{10... | collective-permute-start | bytes 196616 | tf_op jit(solution)/shard_map/ppermute | solution.py:68
  96.6 3.7 %collective-permute-start.12 = (bf16[2,16,128]{2,1,0:T(8,128)(2,1)S(1)}, bf16[2,16,128]{2,1,0:T(8,128)(2,1)S(1)}, u32[]{:S(2)}, u32[]{:S(2)}) collective-permute-start(bf16[2,16,128]{2,1,0:T(8,128)(2,1)S(1)} %get-tuple-element.19), channel_id=1, source_target_pairs={{8,0},{16,8},{24,16},{0,24},{9,1},{17,9},{25,17},{1,25},{10,2},{18... | collective-permute-start | bytes 24584 | tf_op jit(solution)/shard_map/ppermute | solution.py:27
  98.5 22.2 %collective-permute-start.18 = (bf16[64,1024]{1,0:T(8,128)(2,1)S(1)}, bf16[64,1024]{1,0:T(8,128)(2,1)S(1)}, u32[]{:S(2)}, u32[]{:S(2)}) collective-permute-start(bf16[64,1024]{1,0:T(8,128)(2,1)S(1)} %convert_element_type.143), channel_id=1, source_target_pairs={{0,4},{4,0},{1,5},{5,1},{2,6},{6,2},{3,7},{7,3},{8,12},{12,8},{9,1... | collective-permute-start | bytes 393224 | tf_op jit(solution)/shard_map/ppermute | solution.py:107
  100.5 1.4 collective-permute-start.13
  100.6 22.9 %collective-permute-start.17 = (bf16[16,32,128]{2,1,0:T(8,128)(2,1)S(1)}, bf16[16,32,128]{2,1,0:T(8,128)(2,1)S(1)}, u32[]{:S(2)}, u32[]{:S(2)}) collective-permute-start(bf16[16,32,128]{2,1,0:T(8,128)(2,1)S(1)} %pad_maximum_fusion.4), channel_id=1, source_target_pairs={{0,16},{8,24},{16,0},{24,8},{1,17},{9,25},{17,1},{25,9},{2,18},{10... | collective-permute-start | bytes 393224 | tf_op jit(solution)/shard_map/ppermute | solution.py:68
  102.7 8.8 %copy-start.3 = (bf16[2,18,16640]{2,1,0:T(8,128)(2,1)}, bf16[2,18,16640]{2,1,0:T(8,128)(2,1)S(1)}, u32[]{:S(2)}) copy-start(bf16[2,18,16640]{2,1,0:T(8,128)(2,1)S(1)} %pad_maximum_fusion.1.refs_0_) | copy-start | bytes 3594244
  104.1 38.1 %collective-permute-start.14 = (bf16[1,18,16640]{2,1,0:T(8,128)(2,1)}, bf16[1,18,16640]{2,1,0:T(8,128)(2,1)}, u32[]{:S(2)}, u32[]{:S(2)}) collective-permute-start(bf16[1,18,16640]{2,1,0:T(8,128)(2,1)} %get-tuple-element.16), channel_id=1, source_target_pairs={{0,1},{1,2},{2,3},{4,5},{5,6},{6,7},{8,9},{9,10},{10,11},{12,13},{... | collective-permute-start | bytes 1797128 | tf_op jit(solution)/shard_map/ppermute | solution.py:126
  109.5 32.7 %collective-permute-start.15 = (bf16[1,18,16640]{2,1,0:T(8,128)(2,1)}, bf16[1,18,16640]{2,1,0:T(8,128)(2,1)}, u32[]{:S(2)}, u32[]{:S(2)}) collective-permute-start(bf16[1,18,16640]{2,1,0:T(8,128)(2,1)} %get-tuple-element.15), channel_id=1, source_target_pairs={{1,0},{2,1},{3,2},{5,4},{6,5},{7,6},{9,8},{10,9},{11,10},{13,12},{... | collective-permute-start | bytes 1797128 | tf_op jit(solution)/shard_map/ppermute | solution.py:127
  120.8 13.2 %collective-permute-start.19 = (bf16[64,1024]{1,0:T(8,128)(2,1)S(1)}, bf16[64,1024]{1,0:T(8,128)(2,1)S(1)}, u32[]{:S(2)}, u32[]{:S(2)}) collective-permute-start(bf16[64,1024]{1,0:T(8,128)(2,1)S(1)} %add_convert_fusion.2), channel_id=1, source_target_pairs={{0,1},{1,0},{2,3},{3,2},{4,5},{5,4},{6,7},{7,6},{8,9},{9,8},{10,11... | collective-permute-start | bytes 393224 | tf_op jit(solution)/shard_map/ppermute | solution.py:107
  134.0 7.2 %collective-permute-start.20 = (bf16[64,1024]{1,0:T(8,128)(2,1)S(1)}, bf16[64,1024]{1,0:T(8,128)(2,1)S(1)}, u32[]{:S(2)}, u32[]{:S(2)}) collective-permute-start(bf16[64,1024]{1,0:T(8,128)(2,1)S(1)} %add_convert_fusion.1), channel_id=1, source_target_pairs={{0,2},{1,3},{2,0},{3,1},{4,6},{5,7},{6,4},{7,5},{8,10},{9,11},{10,... | collective-permute-start | bytes 393224 | tf_op jit(solution)/shard_map/ppermute | solution.py:107
  141.2 7.8 %copy-start.1 = (bf16[64,256]{1,0:T(8,128)(2,1)S(1)}, bf16[64,256]{1,0:T(8,128)(2,1)}, u32[]{:S(2)}) copy-start(bf16[64,256]{1,0:T(8,128)(2,1)} %param.9) | copy-start | bytes 98308

commit v27 on v26

--- a/solution.py
+++ b/solution.py
@@ -172,7 +172,7 @@
 
 
 def stencil_call(plan, inputs, accs, gains, y_cells, lanes, channels, out_dtype):
-    chunk = min(1024, lanes)
+    chunk = min(2048, lanes)
     rows = 8 if y_cells % 8 == 0 else y_cells
     kernel = functools.partial(
         stencil_kernel, chunk, 2 * channels, y_cells, rows, plan, len(inputs), len(accs)

time: 149 us -> 149 us (level)
  transfers between devices with their start and end apart: 21 -> 21, of which waited for: 10 -> 9; matrix products, arithmetic and copies ran while one was open for 30% -> 30% of each run, Pallas kernels for 13% -> 12%
where the time goes in v27:
time: 149 us; the launch traced here: 148 us
  starting transfers between devices  35.5 us (24%)
  Pallas kernels  31.3 us (21%)
  local copies, waits for them, and re-layouts  29.9 us (20%)
  waiting for transfers between devices  23.5 us (16%)
  matrix products  19.6 us (13%)
  other arithmetic  7.28 us (5%)
    pallas_call x4, Pallas kernels, stencil_call(): pl.pallas_call(kernel, out_shape=jax.ShapeDtypeStruct((len(plan), y_cells...  31.3 us
    ppermute x3, waiting for transfers between devices, butterfly_sum(): lax.ppermute(value, axis, [(i, i ^ step) for i in range(size)])  11.2 us
    ppermute x2, starting transfers between devices, spatial_rims(): below = lax.ppermute(inner[-1:], 'gz', up)  9.76 us
    dot_general x1, matrix products, per_device(): jnp.dot(grad_hidden, expand_weight.T, preferred_element_type=jnp.float32)  7.88 us
    ppermute x4, starting transfers between devices, ring_reduce_scatter(): lax.ppermute(send, axis, [(i, i ^ step) for i in range(size)])  6.66 us
    ppermute x4, starting transfers between devices, ring_gather(): lax.ppermute(block, axis, [(i, i ^ step) for i in range(size)])  5.36 us
    ppermute x3, starting transfers between devices, butterfly_sum(): lax.ppermute(value, axis, [(i, i ^ step) for i in range(size)])  4.56 us
    ppermute x4, waiting for transfers between devices, ring_reduce_scatter(): lax.ppermute(send, axis, [(i, i ^ step) for i in range(size)])  3.69 us
  transfers between devices with their start and end apart: 21, of which 9 were waited for; matrix products, arithmetic and copies ran while one was open for 30% of the time, Pallas kernels for 12%

profile of v27, /device:TPU:0, one launch (start us, length us, event | category | flops | bytes accessed | tf_op | source)
XLA Modules:
  0.0 148.3 jit_solution(16467836977215599386)
XLA Ops:
  0.7 3.0 %reshape.89 = bf16[32,256,64]{2,1,0:T(8,128)(2,1)S(1)} reshape(bf16[2,16,16384]{2,1,0:T(8,128)(2,1)} %param.7) | data formatting | bytes 2097152 | tf_op jit(solution)/shard_map/reshape | solution.py:262
  5.0 3.0 %collective-permute-start = (f32[16,32,128]{2,0,1:T(8,128)S(1)}, f32[16,32,128]{2,0,1:T(8,128)}, u32[]{:S(2)}, u32[]{:S(2)}) collective-permute-start(f32[16,32,128]{2,0,1:T(8,128)S(1)} %fusion.16), channel_id=1, source_target_pairs={{0,16},{8,24},{16,0},{24,8},{1,17},{9,25},{17,1},{25,9},{2,18},{10... | collective-permute-start | bytes 786440 | tf_op jit(solution)/shard_map/ppermute | solution.py:90
  8.7 1.5 %collective-permute-start.2 = (bf16[2,16,128]{2,1,0:T(8,128)(2,1)S(1)}, bf16[2,16,128]{2,1,0:T(8,128)(2,1)S(1)}, u32[]{:S(2)}, u32[]{:S(2)}) collective-permute-start(bf16[2,16,128]{2,1,0:T(8,128)(2,1)S(1)} %get-tuple-element.22), channel_id=1, source_target_pairs={{0,8},{8,16},{16,24},{24,0},{1,9},{9,17},{17,25},{25,1},{2,10},{10... | collective-permute-start | bytes 24584 | tf_op jit(solution)/shard_map/ppermute | solution.py:26
  10.2 1.4 collective-permute-start.3
  11.7 1.7 %collective-permute-done.2 = bf16[2,16,128]{2,1,0:T(8,128)(2,1)S(1)} collective-permute-done((bf16[2,16,128]{2,1,0:T(8,128)(2,1)S(1)}, bf16[2,16,128]{2,1,0:T(8,128)(2,1)S(1)}, u32[]{:S(2)}, u32[]{:S(2)}) %collective-permute-start.2) | collective-permute-done | bytes 8224 | tf_op jit(solution)/shard_map/ppermute | solution.py:26
  14.3 1.2 collective-permute-done.4
  16.4 1.3 fusion.101
  17.6 4.4 %collective-permute-start.5 = (bf16[1,18,16640]{2,1,0:T(8,128)(2,1)}, bf16[1,18,16640]{2,1,0:T(8,128)(2,1)}, u32[]{:S(2)}, u32[]{:S(2)}) collective-permute-start(bf16[1,18,16640]{2,1,0:T(8,128)(2,1)} %get-tuple-element.18), channel_id=1, source_target_pairs={{0,1},{1,2},{2,3},{4,5},{5,6},{6,7},{8,9},{9,10},{10,11},{12,13},{... | collective-permute-start | bytes 1797128 | tf_op jit(solution)/shard_map/ppermute | solution.py:126
  22.0 1.3 collective-permute-start.6
  23.3 1.1 fusion.18
  25.2 1.5 %collective-permute-start.1 = (f32[8,32,128]{2,0,1:T(8,128)}, f32[8,32,128]{2,0,1:T(8,128)}, u32[]{:S(2)}, u32[]{:S(2)}) collective-permute-start(f32[8,32,128]{2,0,1:T(8,128)} %constant_dynamic-slice_fusion.1), channel_id=1, source_target_pairs={{0,8},{8,0},{16,24},{24,16},{1,9},{9,1},{17,25},{25,17},{2,10},{10... | collective-permute-start | bytes 393224 | tf_op jit(solution)/shard_map/ppermute | solution.py:90
  26.7 2.5 %reshape.93 = bf16[32,256,64]{2,1,0:T(8,128)(2,1)S(1)} reshape(bf16[2,16,16384]{2,1,0:T(8,128)(2,1)S(1)} %copy-done.7) | data formatting | bytes 2097152 | tf_op jit(solution)/shard_map/reshape | solution.py:282
  29.2 1.6 %copy.30 = bf16[32,256,64]{1,2,0:T(8,128)(2,1)} copy(bf16[32,256,64]{2,1,0:T(8,128)(2,1)S(1)} %reshape.93) | data formatting | bytes 2097152 | tf_op jit(solution)/shard_map/optimization_barrier | solution.py:282
  31.0 1.1 fusion.20
  32.8 9.3 %shard_map.94.refs_2_ = f32[2,16,16384]{2,1,0:T(8,128)} custom-call(bf16[2,18,16640]{2,1,0:T(8,128)(2,1)} %copy-done.2, f32[27,8,128]{2,1,0:T(8,128)} %broadcast_in_dim.18.refs_1_.refs_3_), custom_call_target="tpu_custom_call" | custom-call | tf_op jit(solution)/shard_map/pallas_call | solution.py:181
  43.8 6.5 %shard_map.95 = bf16[2,16,16384]{2,1,0:T(8,128)(2,1)} custom-call(bf16[1,18,16640]{2,1,0:T(8,128)(2,1)} %collective-permute-done.5.refs_0_, bf16[1,18,16640]{2,1,0:T(8,128)(2,1)} %collective-permute-done.6.refs_1_, f32[2,16,16384]{2,1,0:T(8,128)} %shard_map.94.refs_2_, f32[27,8,128]{2,1,0:T(8,128)} %broadcast_in_dim.18.refs_1_.refs_3_), custom_call_target="tpu_custom_call" | custom-call | tf_op jit(solution)/shard_map/pallas_call | solution.py:181
  50.3 1.5 %collective-permute-start.7 = (bf16[8,32,128]{2,1,0:T(8,128)(2,1)S(1)}, bf16[8,32,128]{2,1,0:T(8,128)(2,1)S(1)}, u32[]{:S(2)}, u32[]{:S(2)}) collective-permute-start(bf16[8,32,128]{2,1,0:T(8,128)(2,1)S(1)} %convolution_convert_fusion.2), channel_id=1, source_target_pairs={{0,8},{8,0},{16,24},{24,16},{1,9},{9,1},{17,25},{25,17},{2,10},{10... | collective-permute-start | bytes 196616 | tf_op jit(solution)/shard_map/ppermute | solution.py:68
  51.8 3.0 %reshape.90 = bf16[8192,64]{1,0:T(8,128)(2,1)S(1)} reshape(bf16[2,16,16384]{2,1,0:T(8,128)(2,1)} %shard_map.95) | data formatting | bytes 2097152 | tf_op jit(solution)/shard_map/reshape | solution.py:271
  54.9 1.2 fusion.106
  56.1 2.8 %fusion.5 = f32[8192,64]{0,1:T(8,128)S(1)} fusion(bf16[256,64]{0,1:T(8,128)(2,1)S(1)} %copy-done.15, f32[8192,256]{1,0:T(8,128)S(1)} %fusion.106), kind=kOutput, calls=%fused_computation.10 | convolution fusion | flops 278921216 | bytes 10518528 | tf_op jit(solution)/shard_map/dot_general | solution.py:274
  59.4 1.6 %collective-permute-start.8 = (bf16[16,32,128]{2,1,0:T(8,128)(2,1)S(1)}, bf16[16,32,128]{2,1,0:T(8,128)(2,1)S(1)}, u32[]{:S(2)}, u32[]{:S(2)}) collective-permute-start(bf16[16,32,128]{2,1,0:T(8,128)(2,1)S(1)} %pad_maximum_fusion.3), channel_id=1, source_target_pairs={{0,16},{8,24},{16,0},{24,8},{1,17},{9,25},{17,1},{25,9},{2,18},{10... | collective-permute-start | bytes 393224 | tf_op jit(solution)/shard_map/ppermute | solution.py:68
  61.0 3.4 %collective-permute-done.8 = bf16[16,32,128]{2,1,0:T(8,128)(2,1)S(1)} collective-permute-done((bf16[16,32,128]{2,1,0:T(8,128)(2,1)S(1)}, bf16[16,32,128]{2,1,0:T(8,128)(2,1)S(1)}, u32[]{:S(2)}, u32[]{:S(2)}) %collective-permute-start.8) | collective-permute-done | bytes 131104 | tf_op jit(solution)/shard_map/ppermute | solution.py:68
  65.2 2.7 %fusion.11 = (bf16[32,256,64]{1,2,0:T(8,128)(2,1)S(1)}, bf16[32,256,64]{1,2,0:T(8,128)(2,1)}) fusion(bf16[32,256,64]{1,2,0:T(8,128)(2,1)S(1)} %copy-done.8, f32[256,32,64]{0,2,1:T(8,128)S(1)} %fusion.27, bf16[32,32,64]{2,1,0:T(8,128)(2,1)S(1)} %get-tuple-element.27, f32[32]{0:T(128)S(1)} %get-tuple-element.33, s32[32]{0:T(128)S(1)} %add.135, ...), kind=kOutput, calls=%fused_computation.17 | convolution fusion | flops 41566208 | bytes 7472384 | tf_op jit(solution)/shard_map/krc,xk->rxc/dot_general | solution.py:219
  69.4 1.6 %collective-permute-start.9 = (f32[16,32,128]{2,0,1:T(8,128)S(1)}, f32[16,32,128]{2,0,1:T(8,128)S(1)}, u32[]{:S(2)}, u32[]{:S(2)}) collective-permute-start(f32[16,32,128]{2,0,1:T(8,128)S(1)} %fusion.13), channel_id=1, source_target_pairs={{0,16},{8,24},{16,0},{24,8},{1,17},{9,25},{17,1},{25,9},{2,18},{10... | collective-permute-start | bytes 786440 | tf_op jit(solution)/shard_map/ppermute | solution.py:90
  71.1 1.0 copy.42
  72.2 3.7 %collective-permute-done.9 = f32[16,32,128]{2,0,1:T(8,128)S(1)} collective-permute-done((f32[16,32,128]{2,0,1:T(8,128)S(1)}, f32[16,32,128]{2,0,1:T(8,128)S(1)}, u32[]{:S(2)}, u32[]{:S(2)}) %collective-permute-start.9) | collective-permute-done | bytes 262176 | tf_op jit(solution)/shard_map/ppermute | solution.py:90
  77.3 7.9 %convolution_convert_fusion = bf16[8192,64]{0,1:T(8,128)(2,1)} fusion(bf16[64,256]{1,0:T(8,128)(2,1)S(1)} %copy-done, bf16[8192,64]{0,1:T(8,128)(2,1)} %bitcast.54, bf16[256,64]{0,1:T(8,128)(2,1)} %param.10, f32[8192,256]{1,0:T(8,128)} %copy-done.4), kind=kOutput, calls=%fused_computation.3 | convolution fusion | flops 558366720 | bytes 10551296 | tf_op jit(solution)/shard_map/dot_general | solution.py:291
  85.2 1.1 copy.29
  86.3 2.5 %reshape.92 = bf16[2,16,16384]{2,1,0:T(8,128)(2,1)} reshape(bf16[32,256,64]{2,1,0:T(8,128)(2,1)S(1)} %copy.29) | data formatting | bytes 2097152 | tf_op jit(solution)/shard_map/reshape | solution.py:280
  88.7 1.1 copy.35
  89.8 1.9 %reshape.95 = bf16[2,16,16384]{2,1,0:T(8,128)(2,1)S(1)} reshape(bf16[8192,64]{1,0:T(8,128)(2,1)S(1)} %copy.35) | data formatting | bytes 2097152 | tf_op jit(solution)/shard_map/reshape | solution.py:294
  91.7 1.0 add_convert_fusion.3
  93.6 1.5 %collective-permute-start.11 = (bf16[2,16,128]{2,1,0:T(8,128)(2,1)S(1)}, bf16[2,16,128]{2,1,0:T(8,128)(2,1)S(1)}, u32[]{:S(2)}, u32[]{:S(2)}) collective-permute-start(bf16[2,16,128]{2,1,0:T(8,128)(2,1)S(1)} %get-tuple-element.20), channel_id=1, source_target_pairs={{0,8},{8,16},{16,24},{24,0},{1,9},{9,17},{17,25},{25,1},{2,10},{10... | collective-permute-start | bytes 24584 | tf_op jit(solution)/shard_map/ppermute | solution.py:26
  95.1 1.0 collective-permute-start.16
  96.1 2.0 %collective-permute-start.12 = (bf16[2,16,128]{2,1,0:T(8,128)(2,1)S(1)}, bf16[2,16,128]{2,1,0:T(8,128)(2,1)S(1)}, u32[]{:S(2)}, u32[]{:S(2)}) collective-permute-start(bf16[2,16,128]{2,1,0:T(8,128)(2,1)S(1)} %get-tuple-element.19), channel_id=1, source_target_pairs={{8,0},{16,8},{24,16},{0,24},{9,1},{17,9},{25,17},{1,25},{10,2},{18... | collective-permute-start | bytes 24584 | tf_op jit(solution)/shard_map/ppermute | solution.py:27
  98.5 1.3 collective-permute-done.12
  100.0 1.3 collective-permute-start.17
  102.2 1.4 fusion.100
  103.6 5.4 %collective-permute-start.14 = (bf16[1,18,16640]{2,1,0:T(8,128)(2,1)}, bf16[1,18,16640]{2,1,0:T(8,128)(2,1)}, u32[]{:S(2)}, u32[]{:S(2)}) collective-permute-start(bf16[1,18,16640]{2,1,0:T(8,128)(2,1)} %get-tuple-element.16), channel_id=1, source_target_pairs={{0,1},{1,2},{2,3},{4,5},{5,6},{6,7},{8,9},{9,10},{10,11},{12,13},{... | collective-permute-start | bytes 1797128 | tf_op jit(solution)/shard_map/ppermute | solution.py:126
  109.0 1.3 collective-permute-start.15
  110.9 8.9 %shard_map.96.refs_2_ = bf16[2,16,16384]{2,1,0:T(8,128)(2,1)} custom-call(bf16[2,18,16640]{2,1,0:T(8,128)(2,1)} %copy-done.3, f32[27,8,128]{2,1,0:T(8,128)} %broadcast_in_dim.36.refs_1_.refs_4_), custom_call_target="tpu_custom_call" | custom-call | tf_op jit(solution)/shard_map/pallas_call | solution.py:181
  119.9 2.7 %collective-permute-start.19 = (bf16[64,1024]{1,0:T(8,128)(2,1)S(1)}, bf16[64,1024]{1,0:T(8,128)(2,1)S(1)}, u32[]{:S(2)}, u32[]{:S(2)}) collective-permute-start(bf16[64,1024]{1,0:T(8,128)(2,1)S(1)} %add_convert_fusion.2), channel_id=1, source_target_pairs={{0,1},{1,0},{2,3},{3,2},{4,5},{5,4},{6,7},{7,6},{8,9},{9,8},{10,11... | collective-permute-start | bytes 393224 | tf_op jit(solution)/shard_map/ppermute | solution.py:107
  123.4 10.1 %collective-permute-done.19 = bf16[64,1024]{1,0:T(8,128)(2,1)S(1)} collective-permute-done((bf16[64,1024]{1,0:T(8,128)(2,1)S(1)}, bf16[64,1024]{1,0:T(8,128)(2,1)S(1)}, u32[]{:S(2)}, u32[]{:S(2)}) %collective-permute-start.19) | collective-permute-done | bytes 131104 | tf_op jit(solution)/shard_map/ppermute | solution.py:107
  133.5 1.8 %collective-permute-start.20 = (bf16[64,1024]{1,0:T(8,128)(2,1)S(1)}, bf16[64,1024]{1,0:T(8,128)(2,1)S(1)}, u32[]{:S(2)}, u32[]{:S(2)}) collective-permute-start(bf16[64,1024]{1,0:T(8,128)(2,1)S(1)} %add_convert_fusion.1), channel_id=1, source_target_pairs={{0,2},{1,3},{2,0},{3,1},{4,6},{5,7},{6,4},{7,5},{8,10},{9,11},{10,... | collective-permute-start | bytes 393224 | tf_op jit(solution)/shard_map/ppermute | solution.py:107
  135.9 1.1 copy.38
  137.0 2.5 %reshape.96.refs_3_ = bf16[2,16,16384]{2,1,0:T(8,128)(2,1)} reshape(bf16[32,256,64]{2,1,0:T(8,128)(2,1)S(1)} %copy.38) | data formatting | bytes 2097152 | tf_op jit(solution)/shard_map/reshape | solution.py:312
  139.5 1.1 collective-permute-done.20
  141.6 6.6 %shard_map.97 = bf16[2,16,16384]{2,1,0:T(8,128)(2,1)} custom-call(bf16[1,18,16640]{2,1,0:T(8,128)(2,1)} %collective-permute-done.14.refs_0_, bf16[1,18,16640]{2,1,0:T(8,128)(2,1)} %collective-permute-done.15.refs_1_, bf16[2,16,16384]{2,1,0:T(8,128)(2,1)} %shard_map.96.refs_2_, bf16[2,16,16384]{2,1,0:T(8,128)(2,1)} %reshape.96.refs_3_, ...), custom_call_target="tpu_custom_call" | custom-call | tf_op jit(solution)/shard_map/pallas_call | solution.py:181
  (110 shorter events, 16.7 us)
Async XLA Ops:
  0.6 54.2 %copy-start = (bf16[64,256]{1,0:T(8,128)(2,1)S(1)}, bf16[64,256]{1,0:T(8,128)(2,1)}, u32[]{:S(2)}) copy-start(bf16[64,256]{1,0:T(8,128)(2,1)} %param.9) | copy-start | bytes 98308
  4.8 8.6 %copy-start.5 = (bf16[2,16,16384]{2,1,0:T(8,128)(2,1)S(1)}, bf16[2,16,16384]{2,1,0:T(8,128)(2,1)}, u32[]{:S(2)}) copy-start(bf16[2,16,16384]{2,1,0:T(8,128)(2,1)} %param.7) | copy-start | bytes 3145732
  5.0 18.4 %collective-permute-start = (f32[16,32,128]{2,0,1:T(8,128)S(1)}, f32[16,32,128]{2,0,1:T(8,128)}, u32[]{:S(2)}, u32[]{:S(2)}) collective-permute-start(f32[16,32,128]{2,0,1:T(8,128)S(1)} %fusion.16), channel_id=1, source_target_pairs={{0,16},{8,24},{16,0},{24,8},{1,17},{9,25},{17,1},{25,9},{2,18},{10... | collective-permute-start | bytes 786440 | tf_op jit(solution)/shard_map/ppermute | solution.py:90
  8.7 4.7 %collective-permute-start.2 = (bf16[2,16,128]{2,1,0:T(8,128)(2,1)S(1)}, bf16[2,16,128]{2,1,0:T(8,128)(2,1)S(1)}, u32[]{:S(2)}, u32[]{:S(2)}) collective-permute-start(bf16[2,16,128]{2,1,0:T(8,128)(2,1)S(1)} %get-tuple-element.22), channel_id=1, source_target_pairs={{0,8},{8,16},{16,24},{24,0},{1,9},{9,17},{17,25},{25,1},{2,10},{10... | collective-permute-start | bytes 24584 | tf_op jit(solution)/shard_map/ppermute | solution.py:26
  10.2 3.7 %collective-permute-start.3 = (bf16[2,16,128]{2,1,0:T(8,128)(2,1)S(1)}, bf16[2,16,128]{2,1,0:T(8,128)(2,1)S(1)}, u32[]{:S(2)}, u32[]{:S(2)}) collective-permute-start(bf16[2,16,128]{2,1,0:T(8,128)(2,1)S(1)} %get-tuple-element.21), channel_id=1, source_target_pairs={{8,0},{16,8},{24,16},{0,24},{9,1},{17,9},{25,17},{1,25},{10,2},{18... | collective-permute-start | bytes 24584 | tf_op jit(solution)/shard_map/ppermute | solution.py:27
  14.1 1.4 collective-permute-start.4
  16.3 8.1 %copy-start.2 = (bf16[2,18,16640]{2,1,0:T(8,128)(2,1)}, bf16[2,18,16640]{2,1,0:T(8,128)(2,1)S(1)}, u32[]{:S(2)}) copy-start(bf16[2,18,16640]{2,1,0:T(8,128)(2,1)S(1)} %pad_maximum_fusion.refs_0_) | copy-start | bytes 3594244
  16.4 10.3 %copy-start.7 = (bf16[2,16,16384]{2,1,0:T(8,128)(2,1)S(1)}, bf16[2,16,16384]{2,1,0:T(8,128)(2,1)}, u32[]{:S(2)}) copy-start(bf16[2,16,16384]{2,1,0:T(8,128)(2,1)} %param.13) | copy-start | bytes 3145732
  17.6 25.6 %collective-permute-start.5 = (bf16[1,18,16640]{2,1,0:T(8,128)(2,1)}, bf16[1,18,16640]{2,1,0:T(8,128)(2,1)}, u32[]{:S(2)}, u32[]{:S(2)}) collective-permute-start(bf16[1,18,16640]{2,1,0:T(8,128)(2,1)} %get-tuple-element.18), channel_id=1, source_target_pairs={{0,1},{1,2},{2,3},{4,5},{5,6},{6,7},{8,9},{9,10},{10,11},{12,13},{... | collective-permute-start | bytes 1797128 | tf_op jit(solution)/shard_map/ppermute | solution.py:126
  22.0 21.8 %collective-permute-start.6 = (bf16[1,18,16640]{2,1,0:T(8,128)(2,1)}, bf16[1,18,16640]{2,1,0:T(8,128)(2,1)}, u32[]{:S(2)}, u32[]{:S(2)}) collective-permute-start(bf16[1,18,16640]{2,1,0:T(8,128)(2,1)} %get-tuple-element.17), channel_id=1, source_target_pairs={{1,0},{2,1},{3,2},{5,4},{6,5},{7,6},{9,8},{10,9},{11,10},{13,12},{... | collective-permute-start | bytes 1797128 | tf_op jit(solution)/shard_map/ppermute | solution.py:127
  24.4 2.2 %copy-start.11 = (f32[16,32,128]{2,0,1:T(8,128)}, f32[16,32,128]{2,0,1:T(8,128)S(1)}, u32[]{:S(2)}) copy-start(f32[16,32,128]{2,0,1:T(8,128)S(1)} %fusion.18) | copy-start | bytes 786436
  25.2 16.9 %collective-permute-start.1 = (f32[8,32,128]{2,0,1:T(8,128)}, f32[8,32,128]{2,0,1:T(8,128)}, u32[]{:S(2)}, u32[]{:S(2)}) collective-permute-start(f32[8,32,128]{2,0,1:T(8,128)} %constant_dynamic-slice_fusion.1), channel_id=1, source_target_pairs={{0,8},{8,0},{16,24},{24,16},{1,9},{9,1},{17,25},{25,17},{2,10},{10... | collective-permute-start | bytes 393224 | tf_op jit(solution)/shard_map/ppermute | solution.py:90
  29.1 1.6 %copy-start.6 = (bf16[32,64,64]{2,1,0:T(8,128)(2,1)S(1)}, bf16[32,64,64]{2,1,0:T(8,128)(2,1)}, u32[]{:S(2)}) copy-start(bf16[32,64,64]{2,1,0:T(8,128)(2,1)} %param.12) | copy-start | bytes 786436
  29.2 1.8 %copy-start.14 = (bf16[27,64]{1,0:T(8,128)(2,1)S(1)}, bf16[27,64]{1,0:T(8,128)(2,1)}, u32[]{:S(2)}) copy-start(bf16[27,64]{1,0:T(8,128)(2,1)} %param.8) | copy-start | bytes 10372
  32.2 9.9 %copy-start.12 = (f32[16,32,128]{2,0,1:T(8,128)S(1)}, f32[16,32,128]{2,0,1:T(8,128)}, u32[]{:S(2)}) copy-start(f32[16,32,128]{2,0,1:T(8,128)} %copy-done.11) | copy-start | bytes 786436
  50.3 9.1 %collective-permute-start.7 = (bf16[8,32,128]{2,1,0:T(8,128)(2,1)S(1)}, bf16[8,32,128]{2,1,0:T(8,128)(2,1)S(1)}, u32[]{:S(2)}, u32[]{:S(2)}) collective-permute-start(bf16[8,32,128]{2,1,0:T(8,128)(2,1)S(1)} %convolution_convert_fusion.2), channel_id=1, source_target_pairs={{0,8},{8,0},{16,24},{24,16},{1,9},{9,1},{17,25},{25,17},{2,10},{10... | collective-permute-start | bytes 196616 | tf_op jit(solution)/shard_map/ppermute | solution.py:68
  54.9 1.2 copy-start.15
  56.1 3.3 %copy-start.4 = (f32[8192,256]{1,0:T(8,128)}, f32[8192,256]{1,0:T(8,128)S(1)}, u32[]{:S(2)}) copy-start(f32[8192,256]{1,0:T(8,128)S(1)} %fusion.106) | copy-start | bytes 25165828
  59.4 5.8 %copy-start.8 = (bf16[32,256,64]{1,2,0:T(8,128)(2,1)S(1)}, bf16[32,256,64]{1,2,0:T(8,128)(2,1)}, u32[]{:S(2)}) copy-start(bf16[32,256,64]{1,2,0:T(8,128)(2,1)} %copy.30) | copy-start | bytes 3145732
  59.4 5.0 %collective-permute-start.8 = (bf16[16,32,128]{2,1,0:T(8,128)(2,1)S(1)}, bf16[16,32,128]{2,1,0:T(8,128)(2,1)S(1)}, u32[]{:S(2)}, u32[]{:S(2)}) collective-permute-start(bf16[16,32,128]{2,1,0:T(8,128)(2,1)S(1)} %pad_maximum_fusion.3), channel_id=1, source_target_pairs={{0,16},{8,24},{16,0},{24,8},{1,17},{9,25},{17,1},{25,9},{2,18},{10... | collective-permute-start | bytes 393224 | tf_op jit(solution)/shard_map/ppermute | solution.py:68
  69.4 6.4 %collective-permute-start.9 = (f32[16,32,128]{2,0,1:T(8,128)S(1)}, f32[16,32,128]{2,0,1:T(8,128)S(1)}, u32[]{:S(2)}, u32[]{:S(2)}) collective-permute-start(f32[16,32,128]{2,0,1:T(8,128)S(1)} %fusion.13), channel_id=1, source_target_pairs={{0,16},{8,24},{16,0},{24,8},{1,17},{9,25},{17,1},{25,9},{2,18},{10... | collective-permute-start | bytes 786440 | tf_op jit(solution)/shard_map/ppermute | solution.py:90
  76.0 1.3 copy-start.13
  76.7 15.0 %collective-permute-start.10 = (f32[8,32,128]{2,0,1:T(8,128)}, f32[8,32,128]{2,0,1:T(8,128)}, u32[]{:S(2)}, u32[]{:S(2)}) collective-permute-start(f32[8,32,128]{2,0,1:T(8,128)} %constant_dynamic-slice_fusion), channel_id=1, source_target_pairs={{0,8},{8,0},{16,24},{24,16},{1,9},{9,1},{17,25},{25,17},{2,10},{10... | collective-permute-start | bytes 393224 | tf_op jit(solution)/shard_map/ppermute | solution.py:90
  77.3 7.9 %copy-start.9 = (bf16[32,256,64]{1,2,0:T(8,128)(2,1)S(1)}, bf16[32,256,64]{1,2,0:T(8,128)(2,1)}, u32[]{:S(2)}) copy-start(bf16[32,256,64]{1,2,0:T(8,128)(2,1)} %get-tuple-element.14) | copy-start | bytes 3145732
  86.2 2.5 %copy-start.10 = (bf16[8192,64]{0,1:T(8,128)(2,1)S(1)}, bf16[8192,64]{0,1:T(8,128)(2,1)}, u32[]{:S(2)}) copy-start(bf16[8192,64]{0,1:T(8,128)(2,1)} %convolution_convert_fusion) | copy-start | bytes 3145732
  93.6 4.8 %collective-permute-start.11 = (bf16[2,16,128]{2,1,0:T(8,128)(2,1)S(1)}, bf16[2,16,128]{2,1,0:T(8,128)(2,1)S(1)}, u32[]{:S(2)}, u32[]{:S(2)}) collective-permute-start(bf16[2,16,128]{2,1,0:T(8,128)(2,1)S(1)} %get-tuple-element.20), channel_id=1, source_target_pairs={{0,8},{8,16},{16,24},{24,0},{1,9},{9,17},{17,25},{25,1},{2,10},{10... | collective-permute-start | bytes 24584 | tf_op jit(solution)/shard_map/ppermute | solution.py:26
  95.1 4.9 %collective-permute-start.16 = (bf16[8,32,128]{2,1,0:T(8,128)(2,1)S(1)}, bf16[8,32,128]{2,1,0:T(8,128)(2,1)S(1)}, u32[]{:S(2)}, u32[]{:S(2)}) collective-permute-start(bf16[8,32,128]{2,1,0:T(8,128)(2,1)S(1)} %convolution_convert_fusion.1), channel_id=1, source_target_pairs={{0,8},{8,0},{16,24},{24,16},{1,9},{9,1},{17,25},{25,17},{2,10},{10... | collective-permute-start | bytes 196616 | tf_op jit(solution)/shard_map/ppermute | solution.py:68
  96.1 3.7 %collective-permute-start.12 = (bf16[2,16,128]{2,1,0:T(8,128)(2,1)S(1)}, bf16[2,16,128]{2,1,0:T(8,128)(2,1)S(1)}, u32[]{:S(2)}, u32[]{:S(2)}) collective-permute-start(bf16[2,16,128]{2,1,0:T(8,128)(2,1)S(1)} %get-tuple-element.19), channel_id=1, source_target_pairs={{8,0},{16,8},{24,16},{0,24},{9,1},{17,9},{25,17},{1,25},{10,2},{18... | collective-permute-start | bytes 24584 | tf_op jit(solution)/shard_map/ppermute | solution.py:27
  98.3 21.6 %collective-permute-start.18 = (bf16[64,1024]{1,0:T(8,128)(2,1)S(1)}, bf16[64,1024]{1,0:T(8,128)(2,1)S(1)}, u32[]{:S(2)}, u32[]{:S(2)}) collective-permute-start(bf16[64,1024]{1,0:T(8,128)(2,1)S(1)} %convert_element_type.143), channel_id=1, source_target_pairs={{0,4},{4,0},{1,5},{5,1},{2,6},{6,2},{3,7},{7,3},{8,12},{12,8},{9,1... | collective-permute-start | bytes 393224 | tf_op jit(solution)/shard_map/ppermute | solution.py:107
  99.9 1.5 collective-permute-start.13
  100.0 22.5 %collective-permute-start.17 = (bf16[16,32,128]{2,1,0:T(8,128)(2,1)S(1)}, bf16[16,32,128]{2,1,0:T(8,128)(2,1)S(1)}, u32[]{:S(2)}, u32[]{:S(2)}) collective-permute-start(bf16[16,32,128]{2,1,0:T(8,128)(2,1)S(1)} %pad_maximum_fusion.4), channel_id=1, source_target_pairs={{0,16},{8,24},{16,0},{24,8},{1,17},{9,25},{17,1},{25,9},{2,18},{10... | collective-permute-start | bytes 393224 | tf_op jit(solution)/shard_map/ppermute | solution.py:68
  102.2 8.7 %copy-start.3 = (bf16[2,18,16640]{2,1,0:T(8,128)(2,1)}, bf16[2,18,16640]{2,1,0:T(8,128)(2,1)S(1)}, u32[]{:S(2)}) copy-start(bf16[2,18,16640]{2,1,0:T(8,128)(2,1)S(1)} %pad_maximum_fusion.1.refs_0_) | copy-start | bytes 3594244
  103.6 38.0 %collective-permute-start.14 = (bf16[1,18,16640]{2,1,0:T(8,128)(2,1)}, bf16[1,18,16640]{2,1,0:T(8,128)(2,1)}, u32[]{:S(2)}, u32[]{:S(2)}) collective-permute-start(bf16[1,18,16640]{2,1,0:T(8,128)(2,1)} %get-tuple-element.16), channel_id=1, source_target_pairs={{0,1},{1,2},{2,3},{4,5},{5,6},{6,7},{8,9},{9,10},{10,11},{12,13},{... | collective-permute-start | bytes 1797128 | tf_op jit(solution)/shard_map/ppermute | solution.py:126
  109.0 32.7 %collective-permute-start.15 = (bf16[1,18,16640]{2,1,0:T(8,128)(2,1)}, bf16[1,18,16640]{2,1,0:T(8,128)(2,1)}, u32[]{:S(2)}, u32[]{:S(2)}) collective-permute-start(bf16[1,18,16640]{2,1,0:T(8,128)(2,1)} %get-tuple-element.15), channel_id=1, source_target_pairs={{1,0},{2,1},{3,2},{5,4},{6,5},{7,6},{9,8},{10,9},{11,10},{13,12},{... | collective-permute-start | bytes 1797128 | tf_op jit(solution)/shard_map/ppermute | solution.py:127
  119.9 13.6 %collective-permute-start.19 = (bf16[64,1024]{1,0:T(8,128)(2,1)S(1)}, bf16[64,1024]{1,0:T(8,128)(2,1)S(1)}, u32[]{:S(2)}, u32[]{:S(2)}) collective-permute-start(bf16[64,1024]{1,0:T(8,128)(2,1)S(1)} %add_convert_fusion.2), channel_id=1, source_target_pairs={{0,1},{1,0},{2,3},{3,2},{4,5},{5,4},{6,7},{7,6},{8,9},{9,8},{10,11... | collective-permute-start | bytes 393224 | tf_op jit(solution)/shard_map/ppermute | solution.py:107
  133.5 7.2 %collective-permute-start.20 = (bf16[64,1024]{1,0:T(8,128)(2,1)S(1)}, bf16[64,1024]{1,0:T(8,128)(2,1)S(1)}, u32[]{:S(2)}, u32[]{:S(2)}) collective-permute-start(bf16[64,1024]{1,0:T(8,128)(2,1)S(1)} %add_convert_fusion.1), channel_id=1, source_target_pairs={{0,2},{1,3},{2,0},{3,1},{4,6},{5,7},{6,4},{7,5},{8,10},{9,11},{10,... | collective-permute-start | bytes 393224 | tf_op jit(solution)/shard_map/ppermute | solution.py:107
  140.7 7.6 %copy-start.1 = (bf16[64,256]{1,0:T(8,128)(2,1)S(1)}, bf16[64,256]{1,0:T(8,128)(2,1)}, u32[]{:S(2)}) copy-start(bf16[64,256]{1,0:T(8,128)(2,1)} %param.9) | copy-start | bytes 98308
